TPU v7x, 32 devices: a whole 2x2x4 slice. The times are simulated.
32 devices in a mesh: slab: 2 (over y), frame: 4 (over z), coil: 4 (over x, core).
Axes of the slice: x: 2, y: 2, z: 4, core: 2. Of those that a mesh axis runs over, the one named last changes fastest.
Arguments:
- factors: float32 [4, 16, 256, 256], P('slab', None, 'coil', 'frame'), parts along dimension 0, may hold values from -3 to 3
- temporal: float32 [4, 4, 16], P('slab'), parts along dimension 0, may hold values from -3 to 3
- maps: bfloat16 [32, 512, 512], P('coil', 'slab'), parts along dimension 1, may hold values from -1 to 1
- kdata: bfloat16 [4, 32, 512, 512], P('frame', 'coil', 'slab'), parts along dimension 2, may hold values from -1.5 to 1.5
- masks: int32 [4, 32, 512], P('frame', 'coil', 'slab'), parts along dimension 2, may hold values 0 or 1
Outputs:
- new_factors: float32 [4, 16, 256, 256], P('slab', None, 'coil', 'frame'), parts along dimension 0
There are 2 independent parts, one for each index of `slab`. A program takes and returns all parts, laid end to end along the dimension named above; each array names one. Nothing has to cross between parts.
All inputs are finite; a program needn't handle non-finite values. No bound on the sum of `masks` on one device may be relied on, other than what follows from the above.
Results may differ from a plain program's by a relative error of at most 0.0085.
Values may be sent and summed in bfloat16 or wider, within the bound.
No kernel may reach another device: no remote copies, remote signals or barrier semaphores. Data moves between devices by JAX's collectives and lax.ppermute only.
A program may use at most 64 MiB of HBM per device.

v0:
```python
import math

import jax
import jax.numpy as jnp
from jax import lax
from jax.sharding import PartitionSpec as P


def dft_parts(length):
    index = jnp.arange(length, dtype=jnp.int32)
    phase = index[:, None] * index[None, :] % length
    angle = 2.0 * math.pi / length * phase.astype(jnp.float32)
    scale = 1.0 / math.sqrt(length)
    return (
        (jnp.cos(angle) * scale).astype(jnp.bfloat16),
        (-jnp.sin(angle) * scale).astype(jnp.bfloat16),
    )


def rotate_plus(values, half_width):
    return jnp.concatenate([-values[..., half_width:], values[..., :half_width]], axis=-1)


def rotate_minus(values, half_width):
    return jnp.concatenate([values[..., half_width:], -values[..., :half_width]], axis=-1)


def sens_times(sens, values, half_width):
    sens_re = sens[..., :half_width].astype(jnp.float32)
    sens_im = sens[..., half_width:].astype(jnp.float32)
    value_re = values[..., :half_width].astype(jnp.float32)
    value_im = values[..., half_width:].astype(jnp.float32)
    return jnp.concatenate(
        [sens_re * value_re - sens_im * value_im, sens_re * value_im + sens_im * value_re], axis=-1
    )


def conj_sens_times(sens, values, half_width):
    sens_re = sens[..., :half_width].astype(jnp.float32)
    sens_im = sens[..., half_width:].astype(jnp.float32)
    value_re = values[..., :half_width]
    value_im = values[..., half_width:]
    return jnp.concatenate(
        [sens_re * value_re + sens_im * value_im, sens_re * value_im - sens_im * value_re], axis=-1
    )


def precise(form, first, second):
    return jnp.einsum(form, first, second, precision=lax.Precision.HIGHEST)


def on_device(factors, temporal, maps, kdata, masks):
    width_x = maps.shape[2] // 2
    width_y = maps.shape[1]
    rows_own = factors.shape[2]
    table_x_re, table_x_im = dft_parts(width_x)
    table_y_re, table_y_im = dft_parts(width_y)
    forward_x = jnp.concatenate(
        [
            jnp.concatenate([table_x_re, table_x_im], axis=1),
            jnp.concatenate([-table_x_im, table_x_re], axis=1),
        ],
        axis=0,
    )
    adjoint_x = jnp.concatenate(
        [
            jnp.concatenate([table_x_re, -table_x_im], axis=1),
            jnp.concatenate([table_x_im, table_x_re], axis=1),
        ],
        axis=0,
    )
    wide_y = jnp.concatenate([table_y_re, table_y_im], axis=1)
    left_re = factors[0]
    left_im = factors[1]
    time_re = temporal[0]
    time_im = temporal[1]
    image_re = precise("tr,ryx->tyx", time_re, left_re) - precise("tr,ryx->tyx", time_im, left_im)
    image_im = precise("tr,ryx->tyx", time_im, left_re) + precise("tr,ryx->tyx", time_re, left_im)
    images = jnp.stack([image_re, image_im], axis=2).astype(jnp.bfloat16)
    own_frame = lax.all_to_all(images, "frame", split_axis=0, concat_axis=3, tiled=True)
    own_rows = own_frame.reshape(own_frame.shape[1], 2 * width_x)
    sens = maps
    coil_image = sens_times(
        sens, lax.all_gather(own_rows, "coil", axis=0, tiled=True)[None], width_x
    ).astype(jnp.bfloat16)
    half_k = jnp.einsum(
        "cyn,nm->cym", coil_image, forward_x, preferred_element_type=jnp.float32
    ).astype(jnp.bfloat16)
    stacked = jnp.concatenate([half_k, rotate_plus(half_k, width_x)], axis=1)
    kspace = jnp.einsum("kj,cjn->ckn", wide_y, stacked, preferred_element_type=jnp.float32)
    sampled = masks[0].astype(jnp.float32)[:, :, None]
    residual = (sampled * (kspace - kdata[0].astype(jnp.float32))).astype(jnp.bfloat16)
    resid_stack = jnp.concatenate([residual, rotate_minus(residual, width_x)], axis=1)
    back_half = jnp.einsum(
        "kj,cjn->ckn", wide_y, resid_stack, preferred_element_type=jnp.float32
    ).astype(jnp.bfloat16)
    coil_back = jnp.einsum("cyn,nm->cym", back_half, adjoint_x, preferred_element_type=jnp.float32)
    sens = maps
    combined = lax.psum(
        jnp.sum(conj_sens_times(sens, coil_back, width_x), axis=0).astype(jnp.bfloat16), "coil"
    ).astype(jnp.float32)
    own_share = lax.dynamic_slice_in_dim(combined, lax.axis_index("coil") * rows_own, rows_own, 0)
    returned = lax.all_to_all(
        own_share.reshape(1, rows_own, 2, width_x).astype(jnp.bfloat16),
        "frame",
        split_axis=3,
        concat_axis=0,
        tiled=True,
    ).astype(jnp.float32)
    back_re = returned[:, :, 0]
    back_im = returned[:, :, 1]
    grad_re = precise("tr,tyx->ryx", time_re, back_re) + precise("tr,tyx->ryx", time_im, back_im)
    grad_im = precise("tr,tyx->ryx", time_re, back_im) - precise("tr,tyx->ryx", time_im, back_re)
    return factors - 0.5 * jnp.stack([grad_re, grad_im])


def solution(mesh):
    placed = (
        P("slab", None, "coil", "frame"),
        P("slab", None, None),
        P("coil", "slab", None),
        P("frame", "coil", "slab", None),
        P("frame", "coil", "slab"),
    )
    return jax.shard_map(
        on_device,
        mesh=mesh,
        in_specs=placed,
        out_specs=P("slab", None, "coil", "frame"),
        check_vma=False,
    )
```

profile of v0, /device:TPU:0, one launch (start us, length us, event | category | flops | bytes accessed | tf_op | source)
XLA Modules:
  0.0 103.2 jit_solution(2421429024773020784)
XLA Ops:
  6.5 1.8 %copy.40 = f32[2,16,64,64]{3,1,2,0:T(8,128)S(1)} copy(f32[2,16,64,64]{3,2,1,0:T(8,128)} %param.5) | data formatting | bytes 1048576 | tf_op args[0]
  10.1 0.8 reshape.35
  10.9 6.3 %all-to-all-start = ((bf16[4,2,4096]{2,1,0:T(2,128)(2,1)}), bf16[4,2,4096]{2,1,0:T(2,128)(2,1)S(1)}, u32[]{:S(2)}, u32[]{:S(2)}) async-start(bf16[4,2,4096]{2,1,0:T(2,128)(2,1)} %reshape.35), calls=%async_computation | async-start | bytes 131072 | tf_op jit(solution)/shard_map/all_to_all | solution.py:80
  17.2 1.1 %multiply_convert_fusion = (bf16[256,256]{1,0:T(8,128)(2,1)S(1)}, bf16[256,256]{1,0:T(8,128)(2,1)S(1)}) fusion(), kind=kLoop, calls=%fused_computation.75 | loop fusion | flops 1245184 | bytes 262144 | tf_op jit(solution)/shard_map/convert_element_type | solution.py:16
  18.4 2.4 %copy.36 = bf16[1,8,256,512]{2,3,1,0:T(8,128)(2,1)} copy(bf16[1,8,256,512]{3,2,1,0:T(8,128)(2,1)S(1)} %copy-done.2) | data formatting | bytes 4194304 | tf_op args[3]
  20.8 1.0 fusion.65
  21.8 1.2 %all-to-all-done = bf16[4,2,4096]{2,1,0:T(2,128)(2,1)S(1)} async-done(((bf16[4,2,4096]{2,1,0:T(2,128)(2,1)}), bf16[4,2,4096]{2,1,0:T(2,128)(2,1)S(1)}, u32[]{:S(2)}, u32[]{:S(2)}) %all-to-all-start) | async-done | bytes 65568 | tf_op jit(solution)/shard_map/all_to_all | solution.py:80
  23.4 6.0 %all_gather.3 = bf16[256,512]{1,0:T(8,128)(2,1)S(1)} all-gather(bf16[64,512]{1,0:T(8,128)(2,1)S(1)} %reshape.26), channel_id=1, replica_groups=mesh['slab'=2,'frame'=4,'coil'=4] {'coil'}, dimensions={0}, use_global_device_ids=true | all-gather | bytes 327680 | tf_op jit(solution)/shard_map/all_gather | solution.py:84
  29.4 0.8 fusion.17
  30.2 1.3 %fusion.29 = bf16[8,256,512]{2,1,0:T(8,128)(2,1)S(1)} fusion(bf16[8,256,256]{2,1,0:T(8,128)(2,1)S(1)} %get-tuple-element.8, bf16[8,256,256]{2,1,0:T(8,128)(2,1)S(1)} %get-tuple-element.7, bf16[256,256]{1,0:T(8,128)(2,1)S(1)} %get-tuple-element.16, bf16[256,256]{1,0:T(8,128)(2,1)S(1)} %fusion.65, bf16[256,256]{1,0:T(8,128)(2,1)S(1)} %get-tuple-element.15), kind=kOutput, calls=%fused_computation.37 | convolution fusion | flops 1081081856 | bytes 4587520 | tf_op jit(solution)/shard_map/cyn,nm->cym/dot_general | solution.py:86
  31.6 1.4 %copy-done.3 = bf16[1,8,256,512]{2,3,1,0:T(8,128)(2,1)S(1)} copy-done((bf16[1,8,256,512]{2,3,1,0:T(8,128)(2,1)S(1)}, bf16[1,8,256,512]{2,3,1,0:T(8,128)(2,1)}, u32[]{:S(2)}) %copy-start.3) | copy-done | bytes 2097176
  33.1 1.6 %fusion.13 = bf16[8,256,512]{1,2,0:T(8,128)(2,1)S(1)} fusion(bf16[8,256,256]{2,1,0:T(8,128)(2,1)S(1)} %get-tuple-element.12, bf16[8,256,256]{2,1,0:T(8,128)(2,1)S(1)} %get-tuple-element.11, bf16[8,256,512]{2,1,0:T(8,128)(2,1)S(1)} %fusion.29, bf16[1,8,256,512]{2,3,1,0:T(8,128)(2,1)S(1)} %copy-done.3, f32[8,256]{1,0:T(8,128)S(1)} %convert_bitcast_fusion, ...), kind=kOutput, calls=%fused_computation.15 | convolution fusion | flops 1091043328 | bytes 8658944 | tf_op jit(solution)/shard_map/kj,cjn->ckn/dot_general | solution.py:90
  34.6 1.2 %fusion.86 = (bf16[8,256,256]{1,2,0:T(8,128)(2,1)S(1)}, bf16[8,256,256]{1,2,0:T(8,128)(2,1)}) fusion(bf16[8,256,512]{1,2,0:T(8,128)(2,1)S(1)} %fusion.13), kind=kLoop, calls=%fused_computation.111 | loop fusion | flops 524288 | bytes 4194304 | tf_op jit(solution)/shard_map/slice | solution.py:25
  36.3 8.3 %fusion.26 = f32[8,256,512]{2,1,0:T(8,128)} fusion(bf16[8,256,256]{1,2,0:T(8,128)(2,1)} %get-tuple-element.10, bf16[8,256,256]{1,2,0:T(8,128)(2,1)S(1)} %get-tuple-element.9, bf16[8,256,512]{1,2,0:T(8,128)(2,1)} %copy-done.4, bf16[256,256]{1,0:T(8,128)(2,1)S(1)} %get-tuple-element.16, bf16[256,256]{1,0:T(8,128)(2,1)S(1)} %get-tuple-element.15, ...), kind=kOutput, calls=%fused_computation.34 | convolution fusion | flops 2163736576 | bytes 8781824 | tf_op jit(solution)/shard_map/cyn,nm->cym/dot_general | solution.py:97
  44.6 2.9 %fusion.20 = (f32[8,256,256]{2,1,0:T(8,128)S(1)}, f32[8,256,256]{2,1,0:T(8,128)S(1)}) fusion(f32[8,256,512]{2,1,0:T(8,128)} %fusion.26, bf16[8,256,512]{2,1,0:T(8,128)(2,1)S(1)} %copy-done), kind=kLoop, calls=%fused_computation.28 | loop fusion | flops 4194304 | bytes 10485760 | tf_op jit(solution)/shard_map/add | solution.py:44
  47.5 1.0 maximum_reduce_fusion
  48.5 32.4 %all-reduce.2.cloned.1.call-done = bf16[256,512]{1,0:T(8,128)(2,1)} async-done(((bf16[256,512]{1,0:T(8,128)(2,1)}), bf16[256,512]{1,0:T(8,128)(2,1)}) %all-reduce.2.cloned.1.call-update) | async-done | bytes 262160 | tf_op jit(solution)/shard_map/psum | solution.py:99
  80.9 0.8 convert_convert_fusion
  82.1 10.3 %all_to_all.33 = bf16[4,2,4096]{2,1,0:T(2,128)(2,1)S(1)} all-to-all(bf16[4,2,4096]{2,1,0:T(2,128)(2,1)S(1)} %reshape.37), channel_id=1, replica_groups=mesh['slab'=2,'frame'=4,'coil'=4] {'frame'}, dimensions={0} | all-to-all | bytes 131072 | tf_op jit(solution)/shard_map/all_to_all | solution.py:103
  92.7 0.4 fusion.63
  93.5 0.4 fusion.37
  94.0 0.4 fusion.36
  94.4 0.7 fusion.42
  95.1 1.3 %copy.41 = f32[2,16,64,64]{3,2,1,0:T(8,128)} copy(f32[2,16,64,64]{3,1,2,0:T(8,128)S(1)} %fusion.42) | data formatting | bytes 1048576 | tf_op jit(solution)/shard_map/sub | solution.py:114
  (34 shorter events, 3.7 us)
Async XLA Ops:
  6.5 1.9 %copy-start.5 = (f32[2,4,16]{2,1,0:T(4,128)S(1)}, f32[2,4,16]{2,1,0:T(4,128)}, u32[]{:S(2)}) copy-start(f32[2,4,16]{2,1,0:T(4,128)} %param.6) | copy-start | bytes 1540
  8.4 9.9 %copy-start.2 = (bf16[1,8,256,512]{3,2,1,0:T(8,128)(2,1)S(1)}, bf16[1,8,256,512]{3,2,1,0:T(8,128)(2,1)}, u32[]{:S(2)}) copy-start(bf16[1,8,256,512]{3,2,1,0:T(8,128)(2,1)} %param.8) | copy-start | bytes 6291460
  10.9 12.1 %all-to-all-start = ((bf16[4,2,4096]{2,1,0:T(2,128)(2,1)}), bf16[4,2,4096]{2,1,0:T(2,128)(2,1)S(1)}, u32[]{:S(2)}, u32[]{:S(2)}) async-start(bf16[4,2,4096]{2,1,0:T(2,128)(2,1)} %reshape.35), calls=%async_computation | async-start | bytes 131072 | tf_op jit(solution)/shard_map/all_to_all | solution.py:80
  17.2 63.7 %all-reduce.2.cloned.1.call-start = ((), (), s32[]{:S(2)}) async-start(), calls=%async_computation.2 | async-start | bytes 524288 | tf_op jit(solution)/shard_map/psum | solution.py:99
  18.3 2.4 %copy-start.6 = (s32[1,8,256]{2,1,0:T(8,128)S(1)}, s32[1,8,256]{2,1,0:T(8,128)}, u32[]{:S(2)}) copy-start(s32[1,8,256]{2,1,0:T(8,128)} %param.9) | copy-start | bytes 24580
  20.8 8.6 %copy-start = (bf16[8,256,512]{2,1,0:T(8,128)(2,1)S(1)}, bf16[8,256,512]{2,1,0:T(8,128)(2,1)}, u32[]{:S(2)}) copy-start(bf16[8,256,512]{2,1,0:T(8,128)(2,1)} %param.7) | copy-start | bytes 6291460
  31.5 1.6 %copy-start.3 = (bf16[1,8,256,512]{2,3,1,0:T(8,128)(2,1)S(1)}, bf16[1,8,256,512]{2,3,1,0:T(8,128)(2,1)}, u32[]{:S(2)}) copy-start(bf16[1,8,256,512]{2,3,1,0:T(8,128)(2,1)} %copy.36) | copy-start | bytes 6291460
  34.6 1.6 %copy-start.4 = (bf16[8,256,512]{1,2,0:T(8,128)(2,1)}, bf16[8,256,512]{1,2,0:T(8,128)(2,1)S(1)}, u32[]{:S(2)}) copy-start(bf16[8,256,512]{1,2,0:T(8,128)(2,1)S(1)} %fusion.13) | copy-start | bytes 6291460
  81.9 12.5 %copy-start.1 = (f32[2,16,64,64]{3,2,1,0:T(8,128)S(1)}, f32[2,16,64,64]{3,2,1,0:T(8,128)}, u32[]{:S(2)}) copy-start(f32[2,16,64,64]{3,2,1,0:T(8,128)} %param.5) | copy-start | bytes 1572868
Sparse Core Ops, SparseCore 0:
  48.6 32.2 all-reduce.1
where the time goes:
time: 104 us; the launch traced here: 103 us
  waiting for transfers between devices  33.6 us (32%)
  blocking collectives  16.2 us (16%)
  matrix products  14.3 us (14%)
  between operations  13.7 us (13%)
  other arithmetic  9.76 us (9%)
  local copies, waits for them, and re-layouts  9.24 us (9%)
  starting transfers between devices  6.32 us (6%)
    psum x1, waiting for transfers between devices, on_device(): lax.psum(jnp.sum(conj_sens_times(sens, coil_back, width_x), axis=0).astyp...  32.4 us
    all_to_all x1, blocking collectives, on_device(): lax.all_to_all(own_share.reshape(1, rows_own, 2, width_x).astype(jnp.bflo...  10.3 us
    dot_general x1, matrix products, on_device(): jnp.einsum('cyn,nm->cym', back_half, adjoint_x, preferred_element_type=jn...  8.28 us
    unnamed x20, local copies, waits for them, and re-layouts  7.37 us
    all_to_all x1, starting transfers between devices, on_device(): lax.all_to_all(images, 'frame', split_axis=0, concat_axis=3, tiled=True)  6.32 us
    all_gather x1, blocking collectives, on_device(): lax.all_gather(own_rows, 'coil', axis=0, tiled=True)[None]  5.97 us
    dot_general x8, matrix products, precise(): return jnp.einsum(form, first, second, precision=lax.Precision.HIGHEST)  3.21 us
    add x1, other arithmetic, conj_sens_times(): sens_re * value_re + sens_im * value_im  2.93 us
  transfers between devices with their start and end apart: 2, of which 2 were waited for; matrix products, arithmetic and copies ran while one was open for 4% of the time, Pallas kernels for 0%

commit v1 on v0

--- a/solution.py
+++ b/solution.py
@@ -49,6 +49,52 @@
     return jnp.einsum(form, first, second, precision=lax.Precision.HIGHEST)
 
 
+PERMUTE_LIMIT = 8
+
+
+def shifted(count, step):
+    return [(source, (source + step) % count) for source in range(count)]
+
+
+def by_sender(pieces, count, me):
+    ring = jnp.stack([pieces[0]] + pieces[1:][::-1])
+    doubled = jnp.concatenate([ring, ring], axis=0)
+    return lax.dynamic_slice_in_dim(doubled, (count - me) % count, count, 0)
+
+
+def gather_blocks(value, axis):
+    count = lax.axis_size(axis)
+    if count > PERMUTE_LIMIT:
+        return lax.all_gather(value, axis)
+    me = lax.axis_index(axis)
+    pieces = [value] + [lax.ppermute(value, axis, shifted(count, step)) for step in range(1, count)]
+    return by_sender(pieces, count, me)
+
+
+def exchange_blocks(blocks, axis):
+    count = lax.axis_size(axis)
+    if count > PERMUTE_LIMIT:
+        return lax.all_to_all(blocks, axis, 0, 0, tiled=True)
+    me = lax.axis_index(axis)
+    pieces = [lax.dynamic_index_in_dim(blocks, me, 0, keepdims=False)]
+    for step in range(1, count):
+        outgoing = lax.dynamic_index_in_dim(blocks, (me + step) % count, 0, keepdims=False)
+        pieces.append(lax.ppermute(outgoing, axis, shifted(count, step)))
+    return by_sender(pieces, count, me)
+
+
+def reduce_blocks(blocks, axis):
+    count = lax.axis_size(axis)
+    if count > PERMUTE_LIMIT:
+        return lax.psum_scatter(blocks.astype(jnp.bfloat16), axis, scatter_dimension=0).astype(jnp.float32)
+    me = lax.axis_index(axis)
+    total = lax.dynamic_index_in_dim(blocks, me, 0, keepdims=False)
+    for step in range(1, count):
+        outgoing = lax.dynamic_index_in_dim(blocks, (me + step) % count, 0, keepdims=False)
+        total = total + lax.ppermute(outgoing.astype(jnp.bfloat16), axis, shifted(count, step)).astype(jnp.float32)
+    return total
+
+
 def on_device(factors, temporal, maps, kdata, masks):
     width_x = maps.shape[2] // 2
     width_y = maps.shape[1]
@@ -77,12 +123,13 @@
     image_re = precise("tr,ryx->tyx", time_re, left_re) - precise("tr,ryx->tyx", time_im, left_im)
     image_im = precise("tr,ryx->tyx", time_im, left_re) + precise("tr,ryx->tyx", time_re, left_im)
     images = jnp.stack([image_re, image_im], axis=2).astype(jnp.bfloat16)
-    own_frame = lax.all_to_all(images, "frame", split_axis=0, concat_axis=3, tiled=True)
-    own_rows = own_frame.reshape(own_frame.shape[1], 2 * width_x)
+    frames_here = images.shape[0]
+    width_own = images.shape[3]
+    pieces_x = exchange_blocks(images, "frame")
+    own_rows = jnp.transpose(pieces_x, (1, 2, 0, 3)).reshape(rows_own, 2 * width_x)
+    full_image = gather_blocks(own_rows, "coil").reshape(width_y, 2 * width_x)
     sens = maps
-    coil_image = sens_times(
-        sens, lax.all_gather(own_rows, "coil", axis=0, tiled=True)[None], width_x
-    ).astype(jnp.bfloat16)
+    coil_image = sens_times(sens, full_image[None], width_x).astype(jnp.bfloat16)
     half_k = jnp.einsum(
         "cyn,nm->cym", coil_image, forward_x, preferred_element_type=jnp.float32
     ).astype(jnp.bfloat16)
@@ -96,17 +143,13 @@
     ).astype(jnp.bfloat16)
     coil_back = jnp.einsum("cyn,nm->cym", back_half, adjoint_x, preferred_element_type=jnp.float32)
     sens = maps
-    combined = lax.psum(
-        jnp.sum(conj_sens_times(sens, coil_back, width_x), axis=0).astype(jnp.bfloat16), "coil"
-    ).astype(jnp.float32)
-    own_share = lax.dynamic_slice_in_dim(combined, lax.axis_index("coil") * rows_own, rows_own, 0)
-    returned = lax.all_to_all(
-        own_share.reshape(1, rows_own, 2, width_x).astype(jnp.bfloat16),
-        "frame",
-        split_axis=3,
-        concat_axis=0,
-        tiled=True,
-    ).astype(jnp.float32)
+    combined = jnp.sum(conj_sens_times(sens, coil_back, width_x), axis=0)
+    groups = width_y // rows_own
+    own_share = reduce_blocks(combined.reshape(groups, rows_own, 2 * width_x), "coil")
+    outgoing = jnp.transpose(
+        own_share.reshape(rows_own, 2, frames_here, width_own), (2, 0, 1, 3)
+    ).astype(jnp.bfloat16)
+    returned = exchange_blocks(outgoing, "frame").astype(jnp.float32)
     back_re = returned[:, :, 0]
     back_im = returned[:, :, 1]
     grad_re = precise("tr,tyx->ryx", time_re, back_re) + precise("tr,tyx->ryx", time_im, back_im)

time: 104 us -> 60.5 us (0.58)
  waiting for transfers between devices: 33.6 us -> 12.3 us
  blocking collectives: 16.2 us -> 0 us
  between operations: 13.7 us -> 0.51 us
  starting transfers between devices: 6.32 us -> 14.4 us
  other arithmetic: 9.76 us -> 8.43 us
  local copies, waits for them, and re-layouts: 9.24 us -> 10.4 us
    psum x1 -> x0, waiting for transfers between devices: 32.4 us -> none  [on_device(): lax.psum(jnp.sum(conj_sens_times(sens, coil_back, width_x), axis=0).astyp...]
    ppermute x0 -> x12, starting transfers between devices: none -> 14.4 us  [the longest x6 10.2 us: exchange_blocks(): pieces.append(lax.ppermute(outgoing, axis, shifted(count, step)))]
    ppermute x0 -> x12, waiting for transfers between devices: none -> 12.3 us  [the longest x6 5.56 us: exchange_blocks(): pieces.append(lax.ppermute(outgoing, axis, shifted(count, step)))]
    all_to_all x1 -> x0, blocking collectives: 10.3 us -> none  [on_device(): lax.all_to_all(own_share.reshape(1, rows_own, 2, width_x).astype(jnp.bflo...]
    all_to_all x1 -> x0, starting transfers between devices: 6.32 us -> none  [on_device(): lax.all_to_all(images, 'frame', split_axis=0, concat_axis=3, tiled=True)]
    all_gather x1 -> x0, blocking collectives: 5.97 us -> none  [on_device(): lax.all_gather(own_rows, 'coil', axis=0, tiled=True)[None]]
    concatenate x0 -> x3, local copies, waits for them, and re-layouts: none -> 1.68 us  [by_sender(): doubled = jnp.concatenate([ring, ring], axis=0)]
    all_to_all x1 -> x0, waiting for transfers between devices: 1.21 us -> none  [on_device(): lax.all_to_all(images, 'frame', split_axis=0, concat_axis=3, tiled=True)]
  transfers between devices with their start and end apart: 2 -> 12, of which waited for: 2 -> 8; matrix products, arithmetic and copies ran while one was open for 4% -> 8% of each run, Pallas kernels for 0% -> 0%
where the time goes in v1:
time: 60.5 us; the launch traced here: 60.3 us
  starting transfers between devices  14.4 us (24%)
  matrix products  14.3 us (24%)
  waiting for transfers between devices  12.3 us (20%)
  local copies, waits for them, and re-layouts  10.4 us (17%)
  other arithmetic  8.43 us (14%)
    ppermute x6, starting transfers between devices, exchange_blocks(): pieces.append(lax.ppermute(outgoing, axis, shifted(count, step)))  10.2 us
    dot_general x1, matrix products, on_device(): jnp.einsum('cyn,nm->cym', back_half, adjoint_x, preferred_element_type=jn...  8.26 us
    unnamed x26, local copies, waits for them, and re-layouts  6.19 us
    ppermute x6, waiting for transfers between devices, exchange_blocks(): pieces.append(lax.ppermute(outgoing, axis, shifted(count, step)))  5.56 us
    ppermute x3, waiting for transfers between devices, gather_blocks(): lax.ppermute(value, axis, shifted(count, step))  4.09 us
    dot_general x8, matrix products, precise(): return jnp.einsum(form, first, second, precision=lax.Precision.HIGHEST)  3.2 us
    add x1, other arithmetic, conj_sens_times(): sens_re * value_re + sens_im * value_im  2.83 us
    ppermute x3, waiting for transfers between devices, reduce_blocks(): lax.ppermute(outgoing.astype(jnp.bfloat16), axis, shifted(count, step))  2.66 us
  transfers between devices with their start and end apart: 12, of which 8 were waited for; matrix products, arithmetic and copies ran while one was open for 8% of the time, Pallas kernels for 0%

profile of v1, /device:TPU:0, one launch (start us, length us, event | category | flops | bytes accessed | tf_op | source)
XLA Modules:
  0.0 60.3 jit_solution(7217638050965617454)
XLA Ops:
  0.0 1.8 %copy.60 = f32[2,16,64,64]{3,1,2,0:T(8,128)S(1)} copy(f32[2,16,64,64]{3,2,1,0:T(8,128)} %param.5) | data formatting | bytes 1048576 | tf_op args[0]
  3.9 5.1 %collective-permute-start = (bf16[64,2,64]{2,0,1:T(8,128)(2,1)S(1)}, bf16[64,2,64]{2,0,1:T(8,128)(2,1)S(1)}, u32[]{:S(2)}, u32[]{:S(2)}) collective-permute-start(bf16[64,2,64]{2,0,1:T(8,128)(2,1)S(1)} %bitcast.137), channel_id=1, source_target_pairs={{0,12},{4,0},{8,4},{12,8},{1,13},{5,1},{9,5},{13,9},{2,14},{6,2},{... | collective-permute-start | bytes 49160 | tf_op jit(solution)/shard_map/ppermute | solution.py:82
  9.0 1.0 %collective-permute-start.2 = (bf16[64,2,64]{2,0,1:T(8,128)(2,1)S(1)}, bf16[64,2,64]{2,0,1:T(8,128)(2,1)S(1)}, u32[]{:S(2)}, u32[]{:S(2)}) collective-permute-start(bf16[64,2,64]{2,0,1:T(8,128)(2,1)S(1)} %bitcast.141), channel_id=1, source_target_pairs={{0,4},{4,8},{8,12},{12,0},{1,5},{5,9},{9,13},{13,1},{2,6},{6,10},{... | collective-permute-start | bytes 49160 | tf_op jit(solution)/shard_map/ppermute | solution.py:82
  10.0 1.1 %multiply_convert_fusion = (bf16[256,256]{1,0:T(8,128)(2,1)S(1)}, bf16[256,256]{1,0:T(8,128)(2,1)S(1)}) fusion(), kind=kLoop, calls=%fused_computation.75 | loop fusion | flops 1245184 | bytes 262144 | tf_op jit(solution)/shard_map/convert_element_type | solution.py:16
  11.2 1.0 %fusion.73 = bf16[256,256]{1,0:T(8,128)(2,1)S(1)} fusion(), kind=kLoop, calls=%fused_computation.115 | loop fusion | flops 1310720 | bytes 131072 | tf_op jit(solution)/shard_map/neg | solution.py:107
  12.2 2.4 %copy.46 = bf16[1,8,256,512]{2,3,1,0:T(8,128)(2,1)} copy(bf16[1,8,256,512]{3,2,1,0:T(8,128)(2,1)S(1)} %copy-done.2) | data formatting | bytes 4194304 | tf_op args[3]
  16.3 1.5 %collective-permute-start.4 = (bf16[64,512]{1,0:T(8,128)(2,1)S(1)}, bf16[64,512]{1,0:T(8,128)(2,1)S(1)}, u32[]{:S(2)}, u32[]{:S(2)}) collective-permute-start(bf16[64,512]{1,0:T(8,128)(2,1)S(1)} %reshape.26), channel_id=1, source_target_pairs={{0,2},{1,3},{2,0},{3,1},{4,6},{5,7},{6,4},{7,5},{8,10},{9,11},{10,... | collective-permute-start | bytes 196616 | tf_op jit(solution)/shard_map/ppermute | solution.py:70
  18.2 3.6 %collective-permute-done.4 = bf16[64,512]{1,0:T(8,128)(2,1)S(1)} collective-permute-done((bf16[64,512]{1,0:T(8,128)(2,1)S(1)}, bf16[64,512]{1,0:T(8,128)(2,1)S(1)}, u32[]{:S(2)}, u32[]{:S(2)}) %collective-permute-start.4) | collective-permute-done | bytes 65568 | tf_op jit(solution)/shard_map/ppermute | solution.py:70
  22.9 1.3 %fusion.29 = bf16[8,256,512]{2,1,0:T(8,128)(2,1)S(1)} fusion(bf16[8,256,256]{2,1,0:T(8,128)(2,1)S(1)} %get-tuple-element.8, bf16[8,256,256]{2,1,0:T(8,128)(2,1)S(1)} %get-tuple-element.7, bf16[256,256]{1,0:T(8,128)(2,1)S(1)} %get-tuple-element.27, bf16[256,256]{1,0:T(8,128)(2,1)S(1)} %fusion.73, bf16[256,256]{1,0:T(8,128)(2,1)S(1)} %get-tuple-element.26), kind=kOutput, calls=%fused_computation.37 | convolution fusion | flops 1081081856 | bytes 4587520 | tf_op jit(solution)/shard_map/cyn,nm->cym/dot_general | solution.py:133
  24.4 1.4 %copy-done.3 = bf16[1,8,256,512]{2,3,1,0:T(8,128)(2,1)S(1)} copy-done((bf16[1,8,256,512]{2,3,1,0:T(8,128)(2,1)S(1)}, bf16[1,8,256,512]{2,3,1,0:T(8,128)(2,1)}, u32[]{:S(2)}) %copy-start.3) | copy-done | bytes 2097176
  25.8 1.6 %fusion.13 = bf16[8,256,512]{1,2,0:T(8,128)(2,1)S(1)} fusion(bf16[8,256,256]{2,1,0:T(8,128)(2,1)S(1)} %get-tuple-element.12, bf16[8,256,256]{2,1,0:T(8,128)(2,1)S(1)} %get-tuple-element.11, bf16[8,256,512]{2,1,0:T(8,128)(2,1)S(1)} %fusion.29, bf16[1,8,256,512]{2,3,1,0:T(8,128)(2,1)S(1)} %copy-done.3, f32[8,256]{1,0:T(8,128)S(1)} %convert_bitcast_fusion, ...), kind=kOutput, calls=%fused_computation.15 | convolution fusion | flops 1091043328 | bytes 8658944 | tf_op jit(solution)/shard_map/kj,cjn->ckn/dot_general | solution.py:137
  27.4 1.2 %fusion.100 = (bf16[8,256,256]{1,2,0:T(8,128)(2,1)S(1)}, bf16[8,256,256]{1,2,0:T(8,128)(2,1)}) fusion(bf16[8,256,512]{1,2,0:T(8,128)(2,1)S(1)} %fusion.13), kind=kLoop, calls=%fused_computation.156 | loop fusion | flops 524288 | bytes 4194304 | tf_op jit(solution)/shard_map/slice | solution.py:25
  29.0 8.3 %fusion.26 = f32[8,256,512]{2,1,0:T(8,128)} fusion(bf16[8,256,256]{1,2,0:T(8,128)(2,1)} %get-tuple-element.10, bf16[8,256,256]{1,2,0:T(8,128)(2,1)S(1)} %get-tuple-element.9, bf16[8,256,512]{1,2,0:T(8,128)(2,1)} %copy-done.4, bf16[256,256]{1,0:T(8,128)(2,1)S(1)} %get-tuple-element.27, bf16[256,256]{1,0:T(8,128)(2,1)S(1)} %get-tuple-element.26, ...), kind=kOutput, calls=%fused_computation.34 | convolution fusion | flops 2163736576 | bytes 8781824 | tf_op jit(solution)/shard_map/cyn,nm->cym/dot_general | solution.py:144
  37.3 2.8 %fusion.20 = (f32[8,256,256]{2,1,0:T(8,128)S(1)}, f32[8,256,256]{2,1,0:T(8,128)S(1)}) fusion(f32[8,256,512]{2,1,0:T(8,128)} %fusion.26, bf16[8,256,512]{2,1,0:T(8,128)(2,1)S(1)} %copy-done), kind=kLoop, calls=%fused_computation.28 | loop fusion | flops 4194304 | bytes 10485760 | tf_op jit(solution)/shard_map/add | solution.py:44
  40.5 0.9 %collective-permute-start.7 = (bf16[64,512]{1,0:T(8,128)(2,1)S(1)}, bf16[64,512]{1,0:T(8,128)(2,1)S(1)}, u32[]{:S(2)}, u32[]{:S(2)}) collective-permute-start(bf16[64,512]{1,0:T(8,128)(2,1)S(1)} %get-tuple-element.15), channel_id=1, source_target_pairs={{0,2},{1,3},{2,0},{3,1},{4,6},{5,7},{6,4},{7,5},{8,10},{9,11},{10,... | collective-permute-start | bytes 196616 | tf_op jit(solution)/shard_map/ppermute | solution.py:94
  41.4 1.4 %collective-permute-start.8 = (bf16[64,512]{1,0:T(8,128)(2,1)S(1)}, bf16[64,512]{1,0:T(8,128)(2,1)S(1)}, u32[]{:S(2)}, u32[]{:S(2)}) collective-permute-start(bf16[64,512]{1,0:T(8,128)(2,1)S(1)} %get-tuple-element.14), channel_id=1, source_target_pairs={{0,3},{1,0},{2,1},{3,2},{4,7},{5,4},{6,5},{7,6},{8,11},{9,8},{10,9... | collective-permute-start | bytes 196616 | tf_op jit(solution)/shard_map/ppermute | solution.py:94
  42.8 1.4 %collective-permute-done.6 = bf16[64,512]{1,0:T(8,128)(2,1)S(1)} collective-permute-done((bf16[64,512]{1,0:T(8,128)(2,1)S(1)}, bf16[64,512]{1,0:T(8,128)(2,1)S(1)}, u32[]{:S(2)}, u32[]{:S(2)}) %collective-permute-start.6) | collective-permute-done | bytes 65568 | tf_op jit(solution)/shard_map/ppermute | solution.py:94
  44.3 1.2 %collective-permute-done.7 = bf16[64,512]{1,0:T(8,128)(2,1)S(1)} collective-permute-done((bf16[64,512]{1,0:T(8,128)(2,1)S(1)}, bf16[64,512]{1,0:T(8,128)(2,1)S(1)}, u32[]{:S(2)}, u32[]{:S(2)}) %collective-permute-start.7) | collective-permute-done | bytes 65568 | tf_op jit(solution)/shard_map/ppermute | solution.py:94
  46.0 2.9 %collective-permute-start.9 = (bf16[64,2,64]{2,0,1:T(8,128)(2,1)S(1)}, bf16[64,2,64]{2,0,1:T(8,128)(2,1)S(1)}, u32[]{:S(2)}, u32[]{:S(2)}) collective-permute-start(bf16[64,2,64]{2,0,1:T(8,128)(2,1)S(1)} %bitcast.143), channel_id=1, source_target_pairs={{0,12},{4,0},{8,4},{12,8},{1,13},{5,1},{9,5},{13,9},{2,14},{6,2},{... | collective-permute-start | bytes 49160 | tf_op jit(solution)/shard_map/ppermute | solution.py:82
  48.9 1.1 %collective-permute-start.10 = (bf16[64,2,64]{2,0,1:T(8,128)(2,1)S(1)}, bf16[64,2,64]{2,0,1:T(8,128)(2,1)S(1)}, u32[]{:S(2)}, u32[]{:S(2)}) collective-permute-start(bf16[64,2,64]{2,0,1:T(8,128)(2,1)S(1)} %bitcast.145), channel_id=1, source_target_pairs={{0,8},{4,12},{8,0},{12,4},{1,9},{5,13},{9,1},{13,5},{2,10},{6,14},... | collective-permute-start | bytes 49160 | tf_op jit(solution)/shard_map/ppermute | solution.py:82
  50.7 3.1 %collective-permute-done.10 = bf16[64,2,64]{2,0,1:T(8,128)(2,1)S(1)} collective-permute-done((bf16[64,2,64]{2,0,1:T(8,128)(2,1)S(1)}, bf16[64,2,64]{2,0,1:T(8,128)(2,1)S(1)}, u32[]{:S(2)}, u32[]{:S(2)}) %collective-permute-start.10) | collective-permute-done | bytes 16416 | tf_op jit(solution)/shard_map/ppermute | solution.py:82
  53.8 2.0 %collective-permute-done.11 = bf16[64,2,64]{2,0,1:T(8,128)(2,1)S(1)} collective-permute-done((bf16[64,2,64]{2,0,1:T(8,128)(2,1)S(1)}, bf16[64,2,64]{2,0,1:T(8,128)(2,1)S(1)}, u32[]{:S(2)}, u32[]{:S(2)}) %collective-permute-start.11) | collective-permute-done | bytes 16416 | tf_op jit(solution)/shard_map/ppermute | solution.py:82
  55.8 0.8 %concatenate.64 = bf16[8,64,2,64]{3,0,1,2:T(8,128)(2,1)S(1)} concatenate(bf16[1,64,2,64]{3,0,1,2:T(2,128)(2,1)S(1)} %copy.52, bf16[1,64,2,64]{3,0,1,2:T(2,128)(2,1)S(1)} %copy.53, bf16[1,64,2,64]{3,0,1,2:T(2,128)(2,1)S(1)} %copy.54, bf16[1,64,2,64]{3,0,1,2:T(2,128)(2,1)S(1)} %copy.55, bf16[1,64,2,64]{3,0,1,2:T(2,128)(2,1)S(1)} %copy.52, bf16[1,64,2,64]{3,0,1,2:T(2,128)(2,1)S(1)} %copy.53, ...), dimensions={0} | concatenate | bytes 262144 | tf_op jit(solution)/shard_map/concatenate | solution.py:61
  59.1 1.3 %copy.61 = f32[2,16,64,64]{3,2,1,0:T(8,128)} copy(f32[2,16,64,64]{3,1,2,0:T(8,128)S(1)} %fusion.42) | data formatting | bytes 1048576 | tf_op jit(solution)/shard_map/sub | solution.py:157
  (72 shorter events, 9.5 us)
Async XLA Ops:
  0.0 1.9 %copy-start.5 = (f32[2,4,16]{2,1,0:T(4,128)S(1)}, f32[2,4,16]{2,1,0:T(4,128)}, u32[]{:S(2)}) copy-start(f32[2,4,16]{2,1,0:T(4,128)} %param.6) | copy-start | bytes 1540
  1.9 9.3 %copy-start.6 = (s32[1,8,256]{2,1,0:T(8,128)S(1)}, s32[1,8,256]{2,1,0:T(8,128)}, u32[]{:S(2)}) copy-start(s32[1,8,256]{2,1,0:T(8,128)} %param.9) | copy-start | bytes 24580
  1.9 10.3 %copy-start.2 = (bf16[1,8,256,512]{3,2,1,0:T(8,128)(2,1)S(1)}, bf16[1,8,256,512]{3,2,1,0:T(8,128)(2,1)}, u32[]{:S(2)}) copy-start(bf16[1,8,256,512]{3,2,1,0:T(8,128)(2,1)} %param.8) | copy-start | bytes 6291460
  3.9 10.7 %collective-permute-start = (bf16[64,2,64]{2,0,1:T(8,128)(2,1)S(1)}, bf16[64,2,64]{2,0,1:T(8,128)(2,1)S(1)}, u32[]{:S(2)}, u32[]{:S(2)}) collective-permute-start(bf16[64,2,64]{2,0,1:T(8,128)(2,1)S(1)} %bitcast.137), channel_id=1, source_target_pairs={{0,12},{4,0},{8,4},{12,8},{1,13},{5,1},{9,5},{13,9},{2,14},{6,2},{... | collective-permute-start | bytes 49160 | tf_op jit(solution)/shard_map/ppermute | solution.py:82
  9.0 5.7 %collective-permute-start.1 = (bf16[64,2,64]{2,0,1:T(8,128)(2,1)S(1)}, bf16[64,2,64]{2,0,1:T(8,128)(2,1)S(1)}, u32[]{:S(2)}, u32[]{:S(2)}) collective-permute-start(bf16[64,2,64]{2,0,1:T(8,128)(2,1)S(1)} %bitcast.139), channel_id=1, source_target_pairs={{0,8},{4,12},{8,0},{12,4},{1,9},{5,13},{9,1},{13,5},{2,10},{6,14},... | collective-permute-start | bytes 49160 | tf_op jit(solution)/shard_map/ppermute | solution.py:82
  9.0 5.8 %collective-permute-start.2 = (bf16[64,2,64]{2,0,1:T(8,128)(2,1)S(1)}, bf16[64,2,64]{2,0,1:T(8,128)(2,1)S(1)}, u32[]{:S(2)}, u32[]{:S(2)}) collective-permute-start(bf16[64,2,64]{2,0,1:T(8,128)(2,1)S(1)} %bitcast.141), channel_id=1, source_target_pairs={{0,4},{4,8},{8,12},{12,0},{1,5},{5,9},{9,13},{13,1},{2,6},{6,10},{... | collective-permute-start | bytes 49160 | tf_op jit(solution)/shard_map/ppermute | solution.py:82
  14.7 7.4 %copy-start = (bf16[8,256,512]{2,1,0:T(8,128)(2,1)S(1)}, bf16[8,256,512]{2,1,0:T(8,128)(2,1)}, u32[]{:S(2)}) copy-start(bf16[8,256,512]{2,1,0:T(8,128)(2,1)} %param.7) | copy-start | bytes 6291460
  16.1 2.0 %collective-permute-start.3 = (bf16[64,512]{1,0:T(8,128)(2,1)S(1)}, bf16[64,512]{1,0:T(8,128)(2,1)S(1)}, u32[]{:S(2)}, u32[]{:S(2)}) collective-permute-start(bf16[64,512]{1,0:T(8,128)(2,1)S(1)} %reshape.26), channel_id=1, source_target_pairs={{0,3},{1,0},{2,1},{3,2},{4,7},{5,4},{6,5},{7,6},{8,11},{9,8},{10,9... | collective-permute-start | bytes 196616 | tf_op jit(solution)/shard_map/ppermute | solution.py:70
  16.3 5.6 %collective-permute-start.4 = (bf16[64,512]{1,0:T(8,128)(2,1)S(1)}, bf16[64,512]{1,0:T(8,128)(2,1)S(1)}, u32[]{:S(2)}, u32[]{:S(2)}) collective-permute-start(bf16[64,512]{1,0:T(8,128)(2,1)S(1)} %reshape.26), channel_id=1, source_target_pairs={{0,2},{1,3},{2,0},{3,1},{4,6},{5,7},{6,4},{7,5},{8,10},{9,11},{10,... | collective-permute-start | bytes 196616 | tf_op jit(solution)/shard_map/ppermute | solution.py:70
  17.7 4.3 %collective-permute-start.5 = (bf16[64,512]{1,0:T(8,128)(2,1)S(1)}, bf16[64,512]{1,0:T(8,128)(2,1)S(1)}, u32[]{:S(2)}, u32[]{:S(2)}) collective-permute-start(bf16[64,512]{1,0:T(8,128)(2,1)S(1)} %reshape.26), channel_id=1, source_target_pairs={{0,1},{1,2},{2,3},{3,0},{4,5},{5,6},{6,7},{7,4},{8,9},{9,10},{10,1... | collective-permute-start | bytes 196616 | tf_op jit(solution)/shard_map/ppermute | solution.py:70
  24.2 1.6 %copy-start.3 = (bf16[1,8,256,512]{2,3,1,0:T(8,128)(2,1)S(1)}, bf16[1,8,256,512]{2,3,1,0:T(8,128)(2,1)}, u32[]{:S(2)}) copy-start(bf16[1,8,256,512]{2,3,1,0:T(8,128)(2,1)} %copy.46) | copy-start | bytes 6291460
  27.4 1.7 %copy-start.4 = (bf16[8,256,512]{1,2,0:T(8,128)(2,1)}, bf16[8,256,512]{1,2,0:T(8,128)(2,1)S(1)}, u32[]{:S(2)}) copy-start(bf16[8,256,512]{1,2,0:T(8,128)(2,1)S(1)} %fusion.13) | copy-start | bytes 6291460
  40.4 3.8 %collective-permute-start.6 = (bf16[64,512]{1,0:T(8,128)(2,1)S(1)}, bf16[64,512]{1,0:T(8,128)(2,1)S(1)}, u32[]{:S(2)}, u32[]{:S(2)}) collective-permute-start(bf16[64,512]{1,0:T(8,128)(2,1)S(1)} %get-tuple-element.13), channel_id=1, source_target_pairs={{0,1},{1,2},{2,3},{3,0},{4,5},{5,6},{6,7},{7,4},{8,9},{9,10},{10,1... | collective-permute-start | bytes 196616 | tf_op jit(solution)/shard_map/ppermute | solution.py:94
  40.5 5.0 %collective-permute-start.7 = (bf16[64,512]{1,0:T(8,128)(2,1)S(1)}, bf16[64,512]{1,0:T(8,128)(2,1)S(1)}, u32[]{:S(2)}, u32[]{:S(2)}) collective-permute-start(bf16[64,512]{1,0:T(8,128)(2,1)S(1)} %get-tuple-element.15), channel_id=1, source_target_pairs={{0,2},{1,3},{2,0},{3,1},{4,6},{5,7},{6,4},{7,5},{8,10},{9,11},{10,... | collective-permute-start | bytes 196616 | tf_op jit(solution)/shard_map/ppermute | solution.py:94
  41.4 4.0 %collective-permute-start.8 = (bf16[64,512]{1,0:T(8,128)(2,1)S(1)}, bf16[64,512]{1,0:T(8,128)(2,1)S(1)}, u32[]{:S(2)}, u32[]{:S(2)}) collective-permute-start(bf16[64,512]{1,0:T(8,128)(2,1)S(1)} %get-tuple-element.14), channel_id=1, source_target_pairs={{0,3},{1,0},{2,1},{3,2},{4,7},{5,4},{6,5},{7,6},{8,11},{9,8},{10,9... | collective-permute-start | bytes 196616 | tf_op jit(solution)/shard_map/ppermute | solution.py:94
  46.0 4.7 %collective-permute-start.9 = (bf16[64,2,64]{2,0,1:T(8,128)(2,1)S(1)}, bf16[64,2,64]{2,0,1:T(8,128)(2,1)S(1)}, u32[]{:S(2)}, u32[]{:S(2)}) collective-permute-start(bf16[64,2,64]{2,0,1:T(8,128)(2,1)S(1)} %bitcast.143), channel_id=1, source_target_pairs={{0,12},{4,0},{8,4},{12,8},{1,13},{5,1},{9,5},{13,9},{2,14},{6,2},{... | collective-permute-start | bytes 49160 | tf_op jit(solution)/shard_map/ppermute | solution.py:82
  48.9 4.9 %collective-permute-start.10 = (bf16[64,2,64]{2,0,1:T(8,128)(2,1)S(1)}, bf16[64,2,64]{2,0,1:T(8,128)(2,1)S(1)}, u32[]{:S(2)}, u32[]{:S(2)}) collective-permute-start(bf16[64,2,64]{2,0,1:T(8,128)(2,1)S(1)} %bitcast.145), channel_id=1, source_target_pairs={{0,8},{4,12},{8,0},{12,4},{1,9},{5,13},{9,1},{13,5},{2,10},{6,14},... | collective-permute-start | bytes 49160 | tf_op jit(solution)/shard_map/ppermute | solution.py:82
  50.0 5.8 %collective-permute-start.11 = (bf16[64,2,64]{2,0,1:T(8,128)(2,1)S(1)}, bf16[64,2,64]{2,0,1:T(8,128)(2,1)S(1)}, u32[]{:S(2)}, u32[]{:S(2)}) collective-permute-start(bf16[64,2,64]{2,0,1:T(8,128)(2,1)S(1)} %bitcast.147), channel_id=1, source_target_pairs={{0,4},{4,8},{8,12},{12,0},{1,5},{5,9},{9,13},{13,1},{2,6},{6,10},{... | collective-permute-start | bytes 49160 | tf_op jit(solution)/shard_map/ppermute | solution.py:82
  55.8 2.6 %copy-start.1 = (f32[2,16,64,64]{3,2,1,0:T(8,128)S(1)}, f32[2,16,64,64]{3,2,1,0:T(8,128)}, u32[]{:S(2)}) copy-start(f32[2,16,64,64]{3,2,1,0:T(8,128)} %param.5) | copy-start | bytes 1572868

commit v2 on v1

--- a/solution.py
+++ b/solution.py
@@ -93,6 +93,54 @@
         outgoing = lax.dynamic_index_in_dim(blocks, (me + step) % count, 0, keepdims=False)
         total = total + lax.ppermute(outgoing.astype(jnp.bfloat16), axis, shifted(count, step)).astype(jnp.float32)
     return total
+
+
+def shifted_pair(frames, groups, step_f, step_c):
+    pairs = []
+    for frame in range(frames):
+        for group in range(groups):
+            target = ((frame + step_f) % frames) * groups + (group + step_c) % groups
+            pairs.append((frame * groups + group, target))
+    return pairs
+
+
+def spread_image(images, frames, groups):
+    me_f = lax.axis_index("frame")
+    me_c = lax.axis_index("coil")
+    outgoing = {}
+    by_x = []
+    for step_f in range(frames):
+        block = lax.dynamic_index_in_dim(images, (me_f + step_f) % frames, 0, keepdims=False)
+        pieces = []
+        for step_c in range(groups):
+            if step_f == 0 and step_c == 0:
+                pieces.append(block)
+            else:
+                pieces.append(lax.ppermute(block, ("frame", "coil"), shifted_pair(frames, groups, step_f, step_c)))
+        by_x.append(by_sender(pieces, groups, me_c))
+    return by_sender(by_x, frames, me_f)
+
+
+def collect_image(blocks, frames, groups):
+    me_f = lax.axis_index("frame")
+    me_c = lax.axis_index("coil")
+    sums = []
+    for step_f in range(frames):
+        total = None
+        for step_c in range(groups):
+            block = lax.dynamic_index_in_dim(
+                lax.dynamic_index_in_dim(blocks, (me_c + step_c) % groups, 0, keepdims=False),
+                (me_f + step_f) % frames, 0, keepdims=False,
+            )
+            if step_f == 0 and step_c == 0:
+                term = block
+            else:
+                term = lax.ppermute(
+                    block.astype(jnp.bfloat16), ("frame", "coil"), shifted_pair(frames, groups, step_f, step_c)
+                ).astype(jnp.float32)
+            total = term if total is None else total + term
+        sums.append(total)
+    return by_sender(sums, frames, me_f)
 
 
 def on_device(factors, temporal, maps, kdata, masks):
@@ -125,9 +173,16 @@
     images = jnp.stack([image_re, image_im], axis=2).astype(jnp.bfloat16)
     frames_here = images.shape[0]
     width_own = images.shape[3]
-    pieces_x = exchange_blocks(images, "frame")
-    own_rows = jnp.transpose(pieces_x, (1, 2, 0, 3)).reshape(rows_own, 2 * width_x)
-    full_image = gather_blocks(own_rows, "coil").reshape(width_y, 2 * width_x)
+    frames = lax.axis_size("frame")
+    groups = lax.axis_size("coil")
+    direct = frames * groups <= 2 * PERMUTE_LIMIT
+    if direct:
+        blocks = spread_image(images, frames, groups)
+        full_image = jnp.transpose(blocks, (1, 2, 3, 0, 4)).reshape(width_y, 2 * width_x)
+    else:
+        pieces_x = exchange_blocks(images, "frame")
+        own_rows = jnp.transpose(pieces_x, (1, 2, 0, 3)).reshape(rows_own, 2 * width_x)
+        full_image = gather_blocks(own_rows, "coil").reshape(width_y, 2 * width_x)
     sens = maps
     coil_image = sens_times(sens, full_image[None], width_x).astype(jnp.bfloat16)
     half_k = jnp.einsum(
@@ -144,12 +199,17 @@
     coil_back = jnp.einsum("cyn,nm->cym", back_half, adjoint_x, preferred_element_type=jnp.float32)
     sens = maps
     combined = jnp.sum(conj_sens_times(sens, coil_back, width_x), axis=0)
-    groups = width_y // rows_own
-    own_share = reduce_blocks(combined.reshape(groups, rows_own, 2 * width_x), "coil")
-    outgoing = jnp.transpose(
-        own_share.reshape(rows_own, 2, frames_here, width_own), (2, 0, 1, 3)
-    ).astype(jnp.bfloat16)
-    returned = exchange_blocks(outgoing, "frame").astype(jnp.float32)
+    if direct:
+        blocks = jnp.transpose(
+            combined.reshape(groups, rows_own, 2, frames, width_own), (0, 3, 1, 2, 4)
+        )
+        returned = collect_image(blocks, frames, groups)
+    else:
+        own_share = reduce_blocks(combined.reshape(groups, rows_own, 2 * width_x), "coil")
+        outgoing = jnp.transpose(
+            own_share.reshape(rows_own, 2, frames_here, width_own), (2, 0, 1, 3)
+        ).astype(jnp.bfloat16)
+        returned = exchange_blocks(outgoing, "frame").astype(jnp.float32)
     back_re = returned[:, :, 0]
     back_im = returned[:, :, 1]
     grad_re = precise("tr,tyx->ryx", time_re, back_re) + precise("tr,tyx->ryx", time_im, back_im)

time: 60.5 us -> 94.4 us (1.56)
  starting transfers between devices: 14.4 us -> 45.1 us
  local copies, waits for them, and re-layouts: 10.4 us -> 13.2 us
  waiting for transfers between devices: 12.3 us -> 11.2 us
    ppermute x12 -> x30, starting transfers between devices: 14.4 us -> 45.1 us  [the longest x15 24.3 us: spread_image(): lax.ppermute(block, ('frame', 'coil'), shifted_pair(frames, groups, step_...]
    another operation x5 -> x3, local copies, waits for them, and re-layouts: 0.31 us -> 1.58 us
    unnamed x26 -> x63, local copies, waits for them, and re-layouts: 6.19 us -> 7.38 us
    ppermute x12 -> x30, waiting for transfers between devices: 12.3 us -> 11.2 us  [the longest x15 9.43 us: spread_image(): lax.ppermute(block, ('frame', 'coil'), shifted_pair(frames, groups, step_...]
  transfers between devices with their start and end apart: 12 -> 30, of which waited for: 8 -> 9; matrix products, arithmetic and copies ran while one was open for 8% -> 6% of each run, Pallas kernels for 0% -> 0%
where the time goes in v2:
time: 94.4 us; the launch traced here: 93.9 us
  starting transfers between devices  45.1 us (48%)
  matrix products  15.2 us (16%)
  local copies, waits for them, and re-layouts  13.2 us (14%)
  waiting for transfers between devices  11.2 us (12%)
  other arithmetic  8.47 us (9%)
    ppermute x15, starting transfers between devices, spread_image(): lax.ppermute(block, ('frame', 'coil'), shifted_pair(frames, groups, step_...  24.3 us
    ppermute x15, starting transfers between devices, collect_image(): lax.ppermute(block.astype(jnp.bfloat16), ('frame', 'coil'), shifted_pair(...  20.8 us
    ppermute x15, waiting for transfers between devices, spread_image(): lax.ppermute(block, ('frame', 'coil'), shifted_pair(frames, groups, step_...  9.43 us
    dot_general x1, matrix products, on_device(): jnp.einsum('cyn,nm->cym', back_half, adjoint_x, preferred_element_type=jn...  8.31 us
    unnamed x63, local copies, waits for them, and re-layouts  7.38 us
    dot_general x8, matrix products, precise(): return jnp.einsum(form, first, second, precision=lax.Precision.HIGHEST)  4 us
    add x1, other arithmetic, conj_sens_times(): sens_re * value_re + sens_im * value_im  2.83 us
  transfers between devices with their start and end apart: 30, of which 9 were waited for; matrix products, arithmetic and copies ran while one was open for 6% of the time, Pallas kernels for 0%

profile of v2, /device:TPU:0, one launch (start us, length us, event | category | flops | bytes accessed | tf_op | source)
XLA Modules:
  0.0 93.9 jit_solution(11453168405824024351)
XLA Ops:
  0.0 1.8 %copy.76 = f32[2,16,64,64]{3,1,2,0:T(8,128)S(1)} copy(f32[2,16,64,64]{3,2,1,0:T(8,128)} %param.5) | data formatting | bytes 1048576 | tf_op args[0]
  3.9 3.1 %collective-permute-start.11 = (bf16[64,2,64]{2,0,1:T(8,128)(2,1)S(1)}, bf16[64,2,64]{2,0,1:T(8,128)(2,1)S(1)}, u32[]{:S(2)}, u32[]{:S(2)}) collective-permute-start(bf16[64,2,64]{2,0,1:T(8,128)(2,1)S(1)} %bitcast.207), channel_id=1, source_target_pairs={{0,4},{1,5},{2,6},{3,7},{4,8},{5,9},{6,10},{7,11},{8,12},{9,13},{1... | collective-permute-start | bytes 49160 | tf_op jit(solution)/shard_map/ppermute | solution.py:119
  7.0 1.7 %collective-permute-start.12 = (bf16[64,2,64]{2,0,1:T(8,128)(2,1)S(1)}, bf16[64,2,64]{2,0,1:T(8,128)(2,1)S(1)}, u32[]{:S(2)}, u32[]{:S(2)}) collective-permute-start(bf16[64,2,64]{2,0,1:T(8,128)(2,1)S(1)} %bitcast.208), channel_id=1, source_target_pairs={{0,7},{1,4},{2,5},{3,6},{4,11},{5,8},{6,9},{7,10},{8,15},{9,12},{1... | collective-permute-start | bytes 49160 | tf_op jit(solution)/shard_map/ppermute | solution.py:119
  12.6 2.4 %copy.58 = bf16[1,8,256,512]{2,3,1,0:T(8,128)(2,1)} copy(bf16[1,8,256,512]{3,2,1,0:T(8,128)(2,1)S(1)} %copy-done.2) | data formatting | bytes 4194304 | tf_op args[3]
  15.0 2.5 %collective-permute-start.13 = (bf16[64,2,64]{2,0,1:T(8,128)(2,1)S(1)}, bf16[64,2,64]{2,0,1:T(8,128)(2,1)S(1)}, u32[]{:S(2)}, u32[]{:S(2)}) collective-permute-start(bf16[64,2,64]{2,0,1:T(8,128)(2,1)S(1)} %bitcast.209), channel_id=1, source_target_pairs={{0,6},{1,7},{2,4},{3,5},{4,10},{5,11},{6,8},{7,9},{8,14},{9,15},{1... | collective-permute-start | bytes 49160 | tf_op jit(solution)/shard_map/ppermute | solution.py:119
  18.0 2.6 %collective-permute-start.7 = (bf16[64,2,64]{2,0,1:T(8,128)(2,1)S(1)}, bf16[64,2,64]{2,0,1:T(8,128)(2,1)S(1)}, u32[]{:S(2)}, u32[]{:S(2)}) collective-permute-start(bf16[64,2,64]{2,0,1:T(8,128)(2,1)S(1)} %bitcast.222), channel_id=1, source_target_pairs={{0,8},{1,9},{2,10},{3,11},{4,12},{5,13},{6,14},{7,15},{8,0},{9,1},... | collective-permute-start | bytes 49160 | tf_op jit(solution)/shard_map/ppermute | solution.py:119
  22.4 1.7 %collective-permute-done.7 = bf16[64,2,64]{2,0,1:T(8,128)(2,1)S(1)} collective-permute-done((bf16[64,2,64]{2,0,1:T(8,128)(2,1)S(1)}, bf16[64,2,64]{2,0,1:T(8,128)(2,1)S(1)}, u32[]{:S(2)}, u32[]{:S(2)}) %collective-permute-start.7) | collective-permute-done | bytes 16416 | tf_op jit(solution)/shard_map/ppermute | solution.py:119
  24.1 2.2 %collective-permute-start.9 = (bf16[64,2,64]{2,0,1:T(8,128)(2,1)S(1)}, bf16[64,2,64]{2,0,1:T(8,128)(2,1)S(1)}, u32[]{:S(2)}, u32[]{:S(2)}) collective-permute-start(bf16[64,2,64]{2,0,1:T(8,128)(2,1)S(1)} %bitcast.224), channel_id=1, source_target_pairs={{0,10},{1,11},{2,8},{3,9},{4,14},{5,15},{6,12},{7,13},{8,2},{9,3},... | collective-permute-start | bytes 49160 | tf_op jit(solution)/shard_map/ppermute | solution.py:119
  27.0 3.0 %collective-permute-done.9 = bf16[64,2,64]{2,0,1:T(8,128)(2,1)S(1)} collective-permute-done((bf16[64,2,64]{2,0,1:T(8,128)(2,1)S(1)}, bf16[64,2,64]{2,0,1:T(8,128)(2,1)S(1)}, u32[]{:S(2)}, u32[]{:S(2)}) %collective-permute-start.9) | collective-permute-done | bytes 16416 | tf_op jit(solution)/shard_map/ppermute | solution.py:119
  29.9 2.4 %collective-permute-start.3 = (bf16[64,2,64]{2,0,1:T(8,128)(2,1)S(1)}, bf16[64,2,64]{2,0,1:T(8,128)(2,1)S(1)}, u32[]{:S(2)}, u32[]{:S(2)}) collective-permute-start(bf16[64,2,64]{2,0,1:T(8,128)(2,1)S(1)} %bitcast.217), channel_id=1, source_target_pairs={{0,12},{1,13},{2,14},{3,15},{4,0},{5,1},{6,2},{7,3},{8,4},{9,5},{1... | collective-permute-start | bytes 49160 | tf_op jit(solution)/shard_map/ppermute | solution.py:119
  34.1 5.2 %collective-permute-start.5 = (bf16[64,2,64]{2,0,1:T(8,128)(2,1)S(1)}, bf16[64,2,64]{2,0,1:T(8,128)(2,1)S(1)}, u32[]{:S(2)}, u32[]{:S(2)}) collective-permute-start(bf16[64,2,64]{2,0,1:T(8,128)(2,1)S(1)} %bitcast.219), channel_id=1, source_target_pairs={{0,14},{1,15},{2,12},{3,13},{4,2},{5,3},{6,0},{7,1},{8,6},{9,7},{1... | collective-permute-start | bytes 49160 | tf_op jit(solution)/shard_map/ppermute | solution.py:119
  40.9 2.6 %collective-permute-done.6 = bf16[64,2,64]{2,0,1:T(8,128)(2,1)S(1)} collective-permute-done((bf16[64,2,64]{2,0,1:T(8,128)(2,1)S(1)}, bf16[64,2,64]{2,0,1:T(8,128)(2,1)S(1)}, u32[]{:S(2)}, u32[]{:S(2)}) %collective-permute-start.6) | collective-permute-done | bytes 16416 | tf_op jit(solution)/shard_map/ppermute | solution.py:119
  49.2 1.6 %fusion.13 = bf16[8,256,512]{1,2,0:T(8,128)(2,1)S(1)} fusion(bf16[8,256,256]{2,1,0:T(8,128)(2,1)S(1)} %get-tuple-element.12, bf16[8,256,256]{2,1,0:T(8,128)(2,1)S(1)} %get-tuple-element.11, bf16[8,256,512]{2,1,0:T(8,128)(2,1)S(1)} %fusion.29, bf16[1,8,256,512]{2,3,1,0:T(8,128)(2,1)S(1)} %copy-done.3, f32[8,256]{1,0:T(8,128)S(1)} %convert_bitcast_fusion, ...), kind=kOutput, calls=%fused_computation.15 | convolution fusion | flops 1091043328 | bytes 8658944 | tf_op jit(solution)/shard_map/kj,cjn->ckn/dot_general | solution.py:192
  52.4 8.3 %fusion.26 = f32[8,256,512]{2,1,0:T(8,128)} fusion(bf16[8,256,256]{1,2,0:T(8,128)(2,1)} %get-tuple-element.10, bf16[8,256,256]{1,2,0:T(8,128)(2,1)S(1)} %get-tuple-element.9, bf16[8,256,512]{1,2,0:T(8,128)(2,1)} %copy-done.4, bf16[256,256]{1,0:T(8,128)(2,1)S(1)} %get-tuple-element.35, bf16[256,256]{1,0:T(8,128)(2,1)S(1)} %get-tuple-element.34, ...), kind=kOutput, calls=%fused_computation.34 | convolution fusion | flops 2163736576 | bytes 8781824 | tf_op jit(solution)/shard_map/cyn,nm->cym/dot_general | solution.py:199
  60.7 2.8 %fusion.20 = (f32[8,256,256]{2,1,0:T(8,128)S(1)}, f32[8,256,256]{2,1,0:T(8,128)S(1)}) fusion(f32[8,256,512]{2,1,0:T(8,128)} %fusion.26, bf16[8,256,512]{2,1,0:T(8,128)(2,1)S(1)} %copy-done), kind=kLoop, calls=%fused_computation.28 | loop fusion | flops 4194304 | bytes 10485760 | tf_op jit(solution)/shard_map/add | solution.py:44
  65.8 2.1 %collective-permute-start.28 = (bf16[64,2,64]{2,0,1:T(8,128)(2,1)S(1)}, bf16[64,2,64]{2,0,1:T(8,128)(2,1)S(1)}, u32[]{:S(2)}, u32[]{:S(2)}) collective-permute-start(bf16[64,2,64]{2,0,1:T(8,128)(2,1)S(1)} %bitcast.237), channel_id=1, source_target_pairs={{0,6},{1,7},{2,4},{3,5},{4,10},{5,11},{6,8},{7,9},{8,14},{9,15},{1... | collective-permute-start | bytes 49160 | tf_op jit(solution)/shard_map/ppermute | solution.py:138
  67.8 3.2 %collective-permute-start.29 = (bf16[64,2,64]{2,0,1:T(8,128)(2,1)S(1)}, bf16[64,2,64]{2,0,1:T(8,128)(2,1)S(1)}, u32[]{:S(2)}, u32[]{:S(2)}) collective-permute-start(bf16[64,2,64]{2,0,1:T(8,128)(2,1)S(1)} %bitcast.236), channel_id=1, source_target_pairs={{0,7},{1,4},{2,5},{3,6},{4,11},{5,8},{6,9},{7,10},{8,15},{9,12},{1... | collective-permute-start | bytes 49160 | tf_op jit(solution)/shard_map/ppermute | solution.py:138
  72.7 2.7 %collective-permute-start.24 = (bf16[64,2,64]{2,0,1:T(8,128)(2,1)S(1)}, bf16[64,2,64]{2,0,1:T(8,128)(2,1)S(1)}, u32[]{:S(2)}, u32[]{:S(2)}) collective-permute-start(bf16[64,2,64]{2,0,1:T(8,128)(2,1)S(1)} %bitcast.233), channel_id=1, source_target_pairs={{0,10},{1,11},{2,8},{3,9},{4,14},{5,15},{6,12},{7,13},{8,2},{9,3},... | collective-permute-start | bytes 49160 | tf_op jit(solution)/shard_map/ppermute | solution.py:138
  75.4 3.2 %collective-permute-start.25 = (bf16[64,2,64]{2,0,1:T(8,128)(2,1)S(1)}, bf16[64,2,64]{2,0,1:T(8,128)(2,1)S(1)}, u32[]{:S(2)}, u32[]{:S(2)}) collective-permute-start(bf16[64,2,64]{2,0,1:T(8,128)(2,1)S(1)} %bitcast.232), channel_id=1, source_target_pairs={{0,11},{1,8},{2,9},{3,10},{4,15},{5,12},{6,13},{7,14},{8,3},{9,0},... | collective-permute-start | bytes 49160 | tf_op jit(solution)/shard_map/ppermute | solution.py:138
  78.6 1.5 %collective-permute-start.18 = (bf16[64,2,64]{2,0,1:T(8,128)(2,1)S(1)}, bf16[64,2,64]{2,0,1:T(8,128)(2,1)S(1)}, u32[]{:S(2)}, u32[]{:S(2)}) collective-permute-start(bf16[64,2,64]{2,0,1:T(8,128)(2,1)S(1)} %bitcast.231), channel_id=1, source_target_pairs={{0,12},{1,13},{2,14},{3,15},{4,0},{5,1},{6,2},{7,3},{8,4},{9,5},{1... | collective-permute-start | bytes 49160 | tf_op jit(solution)/shard_map/ppermute | solution.py:138
  80.1 1.6 %collective-permute-start.20 = (bf16[64,2,64]{2,0,1:T(8,128)(2,1)S(1)}, bf16[64,2,64]{2,0,1:T(8,128)(2,1)S(1)}, u32[]{:S(2)}, u32[]{:S(2)}) collective-permute-start(bf16[64,2,64]{2,0,1:T(8,128)(2,1)S(1)} %bitcast.229), channel_id=1, source_target_pairs={{0,14},{1,15},{2,12},{3,13},{4,2},{5,3},{6,0},{7,1},{8,6},{9,7},{1... | collective-permute-start | bytes 49160 | tf_op jit(solution)/shard_map/ppermute | solution.py:138
  81.7 2.2 %collective-permute-start.21 = (bf16[64,2,64]{2,0,1:T(8,128)(2,1)S(1)}, bf16[64,2,64]{2,0,1:T(8,128)(2,1)S(1)}, u32[]{:S(2)}, u32[]{:S(2)}) collective-permute-start(bf16[64,2,64]{2,0,1:T(8,128)(2,1)S(1)} %bitcast.228), channel_id=1, source_target_pairs={{0,15},{1,12},{2,13},{3,14},{4,3},{5,0},{6,1},{7,2},{8,7},{9,4},{1... | collective-permute-start | bytes 49160 | tf_op jit(solution)/shard_map/ppermute | solution.py:138
  83.9 1.6 %collective-permute-start.16 = (bf16[64,2,64]{2,0,1:T(8,128)(2,1)S(1)}, bf16[64,2,64]{2,0,1:T(8,128)(2,1)S(1)}, u32[]{:S(2)}, u32[]{:S(2)}) collective-permute-start(bf16[64,2,64]{2,0,1:T(8,128)(2,1)S(1)} %bitcast.226), channel_id=1, source_target_pairs={{0,2},{1,3},{2,0},{3,1},{4,6},{5,7},{6,4},{7,5},{8,10},{9,11},{10,... | collective-permute-start | bytes 49160 | tf_op jit(solution)/shard_map/ppermute | solution.py:138
  85.5 1.5 %collective-permute-start.17 = (bf16[64,2,64]{2,0,1:T(8,128)(2,1)S(1)}, bf16[64,2,64]{2,0,1:T(8,128)(2,1)S(1)}, u32[]{:S(2)}, u32[]{:S(2)}) collective-permute-start(bf16[64,2,64]{2,0,1:T(8,128)(2,1)S(1)} %bitcast.221), channel_id=1, source_target_pairs={{0,3},{1,0},{2,1},{3,2},{4,7},{5,4},{6,5},{7,6},{8,11},{9,8},{10,9... | collective-permute-start | bytes 49160 | tf_op jit(solution)/shard_map/ppermute | solution.py:138
  (142 shorter events, 29.8 us)
Async XLA Ops:
  3.9 17.7 %collective-permute-start.11 = (bf16[64,2,64]{2,0,1:T(8,128)(2,1)S(1)}, bf16[64,2,64]{2,0,1:T(8,128)(2,1)S(1)}, u32[]{:S(2)}, u32[]{:S(2)}) collective-permute-start(bf16[64,2,64]{2,0,1:T(8,128)(2,1)S(1)} %bitcast.207), channel_id=1, source_target_pairs={{0,4},{1,5},{2,6},{3,7},{4,8},{5,9},{6,10},{7,11},{8,12},{9,13},{1... | collective-permute-start | bytes 49160 | tf_op jit(solution)/shard_map/ppermute | solution.py:119
  7.0 36.7 %collective-permute-start.12 = (bf16[64,2,64]{2,0,1:T(8,128)(2,1)S(1)}, bf16[64,2,64]{2,0,1:T(8,128)(2,1)S(1)}, u32[]{:S(2)}, u32[]{:S(2)}) collective-permute-start(bf16[64,2,64]{2,0,1:T(8,128)(2,1)S(1)} %bitcast.208), channel_id=1, source_target_pairs={{0,7},{1,4},{2,5},{3,6},{4,11},{5,8},{6,9},{7,10},{8,15},{9,12},{1... | collective-permute-start | bytes 49160 | tf_op jit(solution)/shard_map/ppermute | solution.py:119
  8.6 6.4 %collective-permute-start = (bf16[64,2,64]{2,0,1:T(8,128)(2,1)S(1)}, bf16[64,2,64]{2,0,1:T(8,128)(2,1)S(1)}, u32[]{:S(2)}, u32[]{:S(2)}) collective-permute-start(bf16[64,2,64]{2,0,1:T(8,128)(2,1)S(1)} %bitcast.211), channel_id=1, source_target_pairs={{0,3},{1,0},{2,1},{3,2},{4,7},{5,4},{6,5},{7,6},{8,11},{9,8},{10,9... | collective-permute-start | bytes 49160 | tf_op jit(solution)/shard_map/ppermute | solution.py:119
  9.8 7.8 %collective-permute-start.1 = (bf16[64,2,64]{2,0,1:T(8,128)(2,1)S(1)}, bf16[64,2,64]{2,0,1:T(8,128)(2,1)S(1)}, u32[]{:S(2)}, u32[]{:S(2)}) collective-permute-start(bf16[64,2,64]{2,0,1:T(8,128)(2,1)S(1)} %bitcast.212), channel_id=1, source_target_pairs={{0,2},{1,3},{2,0},{3,1},{4,6},{5,7},{6,4},{7,5},{8,10},{9,11},{10,... | collective-permute-start | bytes 49160 | tf_op jit(solution)/shard_map/ppermute | solution.py:119
  10.3 7.7 %collective-permute-start.2 = (bf16[64,2,64]{2,0,1:T(8,128)(2,1)S(1)}, bf16[64,2,64]{2,0,1:T(8,128)(2,1)S(1)}, u32[]{:S(2)}, u32[]{:S(2)}) collective-permute-start(bf16[64,2,64]{2,0,1:T(8,128)(2,1)S(1)} %bitcast.213), channel_id=1, source_target_pairs={{0,1},{1,2},{2,3},{3,0},{4,5},{5,6},{6,7},{7,4},{8,9},{9,10},{10,1... | collective-permute-start | bytes 49160 | tf_op jit(solution)/shard_map/ppermute | solution.py:119
  15.0 28.7 %collective-permute-start.13 = (bf16[64,2,64]{2,0,1:T(8,128)(2,1)S(1)}, bf16[64,2,64]{2,0,1:T(8,128)(2,1)S(1)}, u32[]{:S(2)}, u32[]{:S(2)}) collective-permute-start(bf16[64,2,64]{2,0,1:T(8,128)(2,1)S(1)} %bitcast.209), channel_id=1, source_target_pairs={{0,6},{1,7},{2,4},{3,5},{4,10},{5,11},{6,8},{7,9},{8,14},{9,15},{1... | collective-permute-start | bytes 49160 | tf_op jit(solution)/shard_map/ppermute | solution.py:119
  17.6 26.2 %collective-permute-start.14 = (bf16[64,2,64]{2,0,1:T(8,128)(2,1)S(1)}, bf16[64,2,64]{2,0,1:T(8,128)(2,1)S(1)}, u32[]{:S(2)}, u32[]{:S(2)}) collective-permute-start(bf16[64,2,64]{2,0,1:T(8,128)(2,1)S(1)} %bitcast.210), channel_id=1, source_target_pairs={{0,5},{1,6},{2,7},{3,4},{4,9},{5,10},{6,11},{7,8},{8,13},{9,14},{1... | collective-permute-start | bytes 49160 | tf_op jit(solution)/shard_map/ppermute | solution.py:119
  18.0 6.2 %collective-permute-start.7 = (bf16[64,2,64]{2,0,1:T(8,128)(2,1)S(1)}, bf16[64,2,64]{2,0,1:T(8,128)(2,1)S(1)}, u32[]{:S(2)}, u32[]{:S(2)}) collective-permute-start(bf16[64,2,64]{2,0,1:T(8,128)(2,1)S(1)} %bitcast.222), channel_id=1, source_target_pairs={{0,8},{1,9},{2,10},{3,11},{4,12},{5,13},{6,14},{7,15},{8,0},{9,1},... | collective-permute-start | bytes 49160 | tf_op jit(solution)/shard_map/ppermute | solution.py:119
  24.1 5.8 %collective-permute-start.9 = (bf16[64,2,64]{2,0,1:T(8,128)(2,1)S(1)}, bf16[64,2,64]{2,0,1:T(8,128)(2,1)S(1)}, u32[]{:S(2)}, u32[]{:S(2)}) collective-permute-start(bf16[64,2,64]{2,0,1:T(8,128)(2,1)S(1)} %bitcast.224), channel_id=1, source_target_pairs={{0,10},{1,11},{2,8},{3,9},{4,14},{5,15},{6,12},{7,13},{8,2},{9,3},... | collective-permute-start | bytes 49160 | tf_op jit(solution)/shard_map/ppermute | solution.py:119
  26.3 6.0 %collective-permute-start.10 = (bf16[64,2,64]{2,0,1:T(8,128)(2,1)S(1)}, bf16[64,2,64]{2,0,1:T(8,128)(2,1)S(1)}, u32[]{:S(2)}, u32[]{:S(2)}) collective-permute-start(bf16[64,2,64]{2,0,1:T(8,128)(2,1)S(1)} %bitcast.225), channel_id=1, source_target_pairs={{0,9},{1,10},{2,11},{3,8},{4,13},{5,14},{6,15},{7,12},{8,1},{9,2},... | collective-permute-start | bytes 49160 | tf_op jit(solution)/shard_map/ppermute | solution.py:119
  32.3 7.0 %collective-permute-start.4 = (bf16[64,2,64]{2,0,1:T(8,128)(2,1)S(1)}, bf16[64,2,64]{2,0,1:T(8,128)(2,1)S(1)}, u32[]{:S(2)}, u32[]{:S(2)}) collective-permute-start(bf16[64,2,64]{2,0,1:T(8,128)(2,1)S(1)} %bitcast.218), channel_id=1, source_target_pairs={{0,15},{1,12},{2,13},{3,14},{4,3},{5,0},{6,1},{7,2},{8,7},{9,4},{1... | collective-permute-start | bytes 49160 | tf_op jit(solution)/shard_map/ppermute | solution.py:119
  34.1 6.8 %collective-permute-start.5 = (bf16[64,2,64]{2,0,1:T(8,128)(2,1)S(1)}, bf16[64,2,64]{2,0,1:T(8,128)(2,1)S(1)}, u32[]{:S(2)}, u32[]{:S(2)}) collective-permute-start(bf16[64,2,64]{2,0,1:T(8,128)(2,1)S(1)} %bitcast.219), channel_id=1, source_target_pairs={{0,14},{1,15},{2,12},{3,13},{4,2},{5,3},{6,0},{7,1},{8,6},{9,7},{1... | collective-permute-start | bytes 49160 | tf_op jit(solution)/shard_map/ppermute | solution.py:119
  65.6 5.9 %collective-permute-start.26 = (bf16[64,2,64]{2,0,1:T(8,128)(2,1)S(1)}, bf16[64,2,64]{2,0,1:T(8,128)(2,1)S(1)}, u32[]{:S(2)}, u32[]{:S(2)}) collective-permute-start(bf16[64,2,64]{2,0,1:T(8,128)(2,1)S(1)} %bitcast.239), channel_id=1, source_target_pairs={{0,4},{1,5},{2,6},{3,7},{4,8},{5,9},{6,10},{7,11},{8,12},{9,13},{1... | collective-permute-start | bytes 49160 | tf_op jit(solution)/shard_map/ppermute | solution.py:138
  65.7 7.0 %collective-permute-start.27 = (bf16[64,2,64]{2,0,1:T(8,128)(2,1)S(1)}, bf16[64,2,64]{2,0,1:T(8,128)(2,1)S(1)}, u32[]{:S(2)}, u32[]{:S(2)}) collective-permute-start(bf16[64,2,64]{2,0,1:T(8,128)(2,1)S(1)} %bitcast.238), channel_id=1, source_target_pairs={{0,5},{1,6},{2,7},{3,4},{4,9},{5,10},{6,11},{7,8},{8,13},{9,14},{1... | collective-permute-start | bytes 49160 | tf_op jit(solution)/shard_map/ppermute | solution.py:138
  65.8 9.6 %collective-permute-start.28 = (bf16[64,2,64]{2,0,1:T(8,128)(2,1)S(1)}, bf16[64,2,64]{2,0,1:T(8,128)(2,1)S(1)}, u32[]{:S(2)}, u32[]{:S(2)}) collective-permute-start(bf16[64,2,64]{2,0,1:T(8,128)(2,1)S(1)} %bitcast.237), channel_id=1, source_target_pairs={{0,6},{1,7},{2,4},{3,5},{4,10},{5,11},{6,8},{7,9},{8,14},{9,15},{1... | collective-permute-start | bytes 49160 | tf_op jit(solution)/shard_map/ppermute | solution.py:138
  67.8 10.7 %collective-permute-start.29 = (bf16[64,2,64]{2,0,1:T(8,128)(2,1)S(1)}, bf16[64,2,64]{2,0,1:T(8,128)(2,1)S(1)}, u32[]{:S(2)}, u32[]{:S(2)}) collective-permute-start(bf16[64,2,64]{2,0,1:T(8,128)(2,1)S(1)} %bitcast.236), channel_id=1, source_target_pairs={{0,7},{1,4},{2,5},{3,6},{4,11},{5,8},{6,9},{7,10},{8,15},{9,12},{1... | collective-permute-start | bytes 49160 | tf_op jit(solution)/shard_map/ppermute | solution.py:138
  71.1 8.9 %collective-permute-start.22 = (bf16[64,2,64]{2,0,1:T(8,128)(2,1)S(1)}, bf16[64,2,64]{2,0,1:T(8,128)(2,1)S(1)}, u32[]{:S(2)}, u32[]{:S(2)}) collective-permute-start(bf16[64,2,64]{2,0,1:T(8,128)(2,1)S(1)} %bitcast.235), channel_id=1, source_target_pairs={{0,8},{1,9},{2,10},{3,11},{4,12},{5,13},{6,14},{7,15},{8,0},{9,1},... | collective-permute-start | bytes 49160 | tf_op jit(solution)/shard_map/ppermute | solution.py:138
  71.5 8.6 %collective-permute-start.23 = (bf16[64,2,64]{2,0,1:T(8,128)(2,1)S(1)}, bf16[64,2,64]{2,0,1:T(8,128)(2,1)S(1)}, u32[]{:S(2)}, u32[]{:S(2)}) collective-permute-start(bf16[64,2,64]{2,0,1:T(8,128)(2,1)S(1)} %bitcast.234), channel_id=1, source_target_pairs={{0,9},{1,10},{2,11},{3,8},{4,13},{5,14},{6,15},{7,12},{8,1},{9,2},... | collective-permute-start | bytes 49160 | tf_op jit(solution)/shard_map/ppermute | solution.py:138
  72.7 9.0 %collective-permute-start.24 = (bf16[64,2,64]{2,0,1:T(8,128)(2,1)S(1)}, bf16[64,2,64]{2,0,1:T(8,128)(2,1)S(1)}, u32[]{:S(2)}, u32[]{:S(2)}) collective-permute-start(bf16[64,2,64]{2,0,1:T(8,128)(2,1)S(1)} %bitcast.233), channel_id=1, source_target_pairs={{0,10},{1,11},{2,8},{3,9},{4,14},{5,15},{6,12},{7,13},{8,2},{9,3},... | collective-permute-start | bytes 49160 | tf_op jit(solution)/shard_map/ppermute | solution.py:138
  75.4 8.5 %collective-permute-start.25 = (bf16[64,2,64]{2,0,1:T(8,128)(2,1)S(1)}, bf16[64,2,64]{2,0,1:T(8,128)(2,1)S(1)}, u32[]{:S(2)}, u32[]{:S(2)}) collective-permute-start(bf16[64,2,64]{2,0,1:T(8,128)(2,1)S(1)} %bitcast.232), channel_id=1, source_target_pairs={{0,11},{1,8},{2,9},{3,10},{4,15},{5,12},{6,13},{7,14},{8,3},{9,0},... | collective-permute-start | bytes 49160 | tf_op jit(solution)/shard_map/ppermute | solution.py:138
  78.6 5.4 %collective-permute-start.18 = (bf16[64,2,64]{2,0,1:T(8,128)(2,1)S(1)}, bf16[64,2,64]{2,0,1:T(8,128)(2,1)S(1)}, u32[]{:S(2)}, u32[]{:S(2)}) collective-permute-start(bf16[64,2,64]{2,0,1:T(8,128)(2,1)S(1)} %bitcast.231), channel_id=1, source_target_pairs={{0,12},{1,13},{2,14},{3,15},{4,0},{5,1},{6,2},{7,3},{8,4},{9,5},{1... | collective-permute-start | bytes 49160 | tf_op jit(solution)/shard_map/ppermute | solution.py:138
  80.1 5.5 %collective-permute-start.19 = (bf16[64,2,64]{2,0,1:T(8,128)(2,1)S(1)}, bf16[64,2,64]{2,0,1:T(8,128)(2,1)S(1)}, u32[]{:S(2)}, u32[]{:S(2)}) collective-permute-start(bf16[64,2,64]{2,0,1:T(8,128)(2,1)S(1)} %bitcast.230), channel_id=1, source_target_pairs={{0,13},{1,14},{2,15},{3,12},{4,1},{5,2},{6,3},{7,0},{8,5},{9,6},{1... | collective-permute-start | bytes 49160 | tf_op jit(solution)/shard_map/ppermute | solution.py:138
  80.1 6.8 %collective-permute-start.20 = (bf16[64,2,64]{2,0,1:T(8,128)(2,1)S(1)}, bf16[64,2,64]{2,0,1:T(8,128)(2,1)S(1)}, u32[]{:S(2)}, u32[]{:S(2)}) collective-permute-start(bf16[64,2,64]{2,0,1:T(8,128)(2,1)S(1)} %bitcast.229), channel_id=1, source_target_pairs={{0,14},{1,15},{2,12},{3,13},{4,2},{5,3},{6,0},{7,1},{8,6},{9,7},{1... | collective-permute-start | bytes 49160 | tf_op jit(solution)/shard_map/ppermute | solution.py:138
  81.7 5.3 %collective-permute-start.21 = (bf16[64,2,64]{2,0,1:T(8,128)(2,1)S(1)}, bf16[64,2,64]{2,0,1:T(8,128)(2,1)S(1)}, u32[]{:S(2)}, u32[]{:S(2)}) collective-permute-start(bf16[64,2,64]{2,0,1:T(8,128)(2,1)S(1)} %bitcast.228), channel_id=1, source_target_pairs={{0,15},{1,12},{2,13},{3,14},{4,3},{5,0},{6,1},{7,2},{8,7},{9,4},{1... | collective-permute-start | bytes 49160 | tf_op jit(solution)/shard_map/ppermute | solution.py:138
  (13 other events, 53.0 us)

commit v3 on v1

--- a/solution.py
+++ b/solution.py
@@ -120,8 +120,12 @@
     left_im = factors[1]
     time_re = temporal[0]
     time_im = temporal[1]
-    image_re = precise("tr,ryx->tyx", time_re, left_re) - precise("tr,ryx->tyx", time_im, left_im)
-    image_im = precise("tr,ryx->tyx", time_im, left_re) + precise("tr,ryx->tyx", time_re, left_im)
+    image_re = jnp.sum(
+        time_re[:, :, None, None] * left_re[None] - time_im[:, :, None, None] * left_im[None], axis=1
+    )
+    image_im = jnp.sum(
+        time_im[:, :, None, None] * left_re[None] + time_re[:, :, None, None] * left_im[None], axis=1
+    )
     images = jnp.stack([image_re, image_im], axis=2).astype(jnp.bfloat16)
     frames_here = images.shape[0]
     width_own = images.shape[3]
@@ -152,8 +156,12 @@
     returned = exchange_blocks(outgoing, "frame").astype(jnp.float32)
     back_re = returned[:, :, 0]
     back_im = returned[:, :, 1]
-    grad_re = precise("tr,tyx->ryx", time_re, back_re) + precise("tr,tyx->ryx", time_im, back_im)
-    grad_im = precise("tr,tyx->ryx", time_re, back_im) - precise("tr,tyx->ryx", time_im, back_re)
+    grad_re = jnp.sum(
+        time_re[:, :, None, None] * back_re[:, None] + time_im[:, :, None, None] * back_im[:, None], axis=0
+    )
+    grad_im = jnp.sum(
+        time_re[:, :, None, None] * back_im[:, None] - time_im[:, :, None, None] * back_re[:, None], axis=0
+    )
     return factors - 0.5 * jnp.stack([grad_re, grad_im])
 
 

time: 60.5 us -> 56.4 us (0.932)
  matrix products: 14.3 us -> 11.1 us
  local copies, waits for them, and re-layouts: 10.4 us -> 7.7 us
  other arithmetic: 8.43 us -> 10.1 us
    dot_general x8 -> x0, matrix products: 3.2 us -> none  [precise(): return jnp.einsum(form, first, second, precision=lax.Precision.HIGHEST)]
    mul x0 -> x3, local copies, waits for them, and re-layouts: none -> 2.14 us  [the longest x1 1.27 us: on_device(): time_re[:, :, None, None] * left_re[None]]
    concatenate x3, local copies, waits for them, and re-layouts: 1.68 us -> 0.03 us  [by_sender(): doubled = jnp.concatenate([ring, ring], axis=0)]
    reduce_sum x0 -> x2, other arithmetic: none -> 1.63 us  [the longest x1 0.89 us: on_device(): jnp.sum(time_re[:, :, None, None] * left_re[None] - time_im[:, :, None, N...]
    unnamed x26 -> x36, local copies, waits for them, and re-layouts: 6.19 us -> 4.63 us
    sub x1 -> x0, local copies, waits for them, and re-layouts: 1.28 us -> none  [on_device(): return factors - 0.5 * jnp.stack([grad_re, grad_im])]
where the time goes in v3:
time: 56.4 us; the launch traced here: 56.2 us
  starting transfers between devices  14.4 us (26%)
  waiting for transfers between devices  12.5 us (22%)
  matrix products  11.1 us (20%)
  other arithmetic  10.1 us (18%)
  local copies, waits for them, and re-layouts  7.7 us (14%)
    ppermute x6, starting transfers between devices, exchange_blocks(): pieces.append(lax.ppermute(outgoing, axis, shifted(count, step)))  10.2 us
    dot_general x1, matrix products, on_device(): jnp.einsum('cyn,nm->cym', back_half, adjoint_x, preferred_element_type=jn...  8.27 us
    ppermute x6, waiting for transfers between devices, exchange_blocks(): pieces.append(lax.ppermute(outgoing, axis, shifted(count, step)))  5.71 us
    unnamed x36, local copies, waits for them, and re-layouts  4.63 us
    ppermute x3, waiting for transfers between devices, gather_blocks(): lax.ppermute(value, axis, shifted(count, step))  4.09 us
    add x1, other arithmetic, conj_sens_times(): sens_re * value_re + sens_im * value_im  2.83 us
    ppermute x3, waiting for transfers between devices, reduce_blocks(): lax.ppermute(outgoing.astype(jnp.bfloat16), axis, shifted(count, step))  2.66 us
    ppermute x3, starting transfers between devices, reduce_blocks(): lax.ppermute(outgoing.astype(jnp.bfloat16), axis, shifted(count, step))  2.38 us
  transfers between devices with their start and end apart: 12, of which 8 were waited for; matrix products, arithmetic and copies ran while one was open for 8% of the time, Pallas kernels for 0%

profile of v3, /device:TPU:0, one launch (start us, length us, event | category | flops | bytes accessed | tf_op | source)
XLA Modules:
  0.0 56.2 jit_solution(16905890878795992495)
XLA Ops:
  0.9 1.3 %slice_bitcast_fusion.1 = (f32[16,64,64]{2,1,0:T(8,128)S(1)}, f32[16,64,64]{2,1,0:T(8,128)S(1)}) fusion(f32[2,16,64,64]{3,2,1,0:T(8,128)} %param.5), kind=kLoop, calls=%fused_computation.59 | loop fusion | bytes 1048576 | tf_op jit(solution)/shard_map/mul | solution.py:124
  2.1 0.9 %subtract_reduce_fusion.1 = (bf16[4,64,64]{2,1,0:T(8,128)(2,1)S(1)}, bf16[4,64,64]{2,1,0:T(8,128)(2,1)S(1)}) fusion(f32[16,64,64]{2,1,0:T(8,128)S(1)} %get-tuple-element.18, f32[4,16]{1,0:T(4,128)S(1)} %get-tuple-element.35, f32[16,64,64]{2,1,0:T(8,128)S(1)} %get-tuple-element.17, f32[4,16]{1,0:T(4,128)S(1)} %get-tuple-element.34), kind=kLoop, calls=%fused_computation.40 | loop fusion | flops 2064384 | bytes 590336 | tf_op jit(solution)/shard_map/reduce_sum | solution.py:123
  3.1 5.1 %collective-permute-start = (bf16[64,2,64]{2,0,1:T(8,128)(2,1)S(1)}, bf16[64,2,64]{2,0,1:T(8,128)(2,1)S(1)}, u32[]{:S(2)}, u32[]{:S(2)}) collective-permute-start(bf16[64,2,64]{2,0,1:T(8,128)(2,1)S(1)} %get-tuple-element.32), channel_id=1, source_target_pairs={{0,12},{4,0},{8,4},{12,8},{1,13},{5,1},{9,5},{13,9},{2,14},{6,2},{... | collective-permute-start | bytes 49160 | tf_op jit(solution)/shard_map/ppermute | solution.py:82
  8.2 1.0 %collective-permute-start.2 = (bf16[64,2,64]{2,0,1:T(8,128)(2,1)S(1)}, bf16[64,2,64]{2,0,1:T(8,128)(2,1)S(1)}, u32[]{:S(2)}, u32[]{:S(2)}) collective-permute-start(bf16[64,2,64]{2,0,1:T(8,128)(2,1)S(1)} %get-tuple-element.30), channel_id=1, source_target_pairs={{0,4},{4,8},{8,12},{12,0},{1,5},{5,9},{9,13},{13,1},{2,6},{6,10},{... | collective-permute-start | bytes 49160 | tf_op jit(solution)/shard_map/ppermute | solution.py:82
  9.2 1.1 %multiply_convert_fusion = (bf16[256,256]{1,0:T(8,128)(2,1)S(1)}, bf16[256,256]{1,0:T(8,128)(2,1)S(1)}) fusion(), kind=kLoop, calls=%fused_computation.67 | loop fusion | flops 1245184 | bytes 262144 | tf_op jit(solution)/shard_map/convert_element_type | solution.py:16
  10.3 1.0 %fusion.61 = bf16[256,256]{1,0:T(8,128)(2,1)S(1)} fusion(), kind=kLoop, calls=%fused_computation.124 | loop fusion | flops 1310720 | bytes 131072 | tf_op jit(solution)/shard_map/neg | solution.py:107
  11.4 2.4 %copy.28 = bf16[1,8,256,512]{2,3,1,0:T(8,128)(2,1)} copy(bf16[1,8,256,512]{3,2,1,0:T(8,128)(2,1)S(1)} %copy-done.2) | data formatting | bytes 4194304 | tf_op args[3]
  14.6 1.5 %collective-permute-start.4 = (bf16[64,512]{1,0:T(8,128)(2,1)S(1)}, bf16[64,512]{1,0:T(8,128)(2,1)S(1)}, u32[]{:S(2)}, u32[]{:S(2)}) collective-permute-start(bf16[64,512]{1,0:T(8,128)(2,1)S(1)} %reshape.30), channel_id=1, source_target_pairs={{0,2},{1,3},{2,0},{3,1},{4,6},{5,7},{6,4},{7,5},{8,10},{9,11},{10,... | collective-permute-start | bytes 196616 | tf_op jit(solution)/shard_map/ppermute | solution.py:70
  16.5 3.7 %collective-permute-done.4 = bf16[64,512]{1,0:T(8,128)(2,1)S(1)} collective-permute-done((bf16[64,512]{1,0:T(8,128)(2,1)S(1)}, bf16[64,512]{1,0:T(8,128)(2,1)S(1)}, u32[]{:S(2)}, u32[]{:S(2)}) %collective-permute-start.4) | collective-permute-done | bytes 65568 | tf_op jit(solution)/shard_map/ppermute | solution.py:70
  21.2 1.3 %fusion.29 = bf16[8,256,512]{2,1,0:T(8,128)(2,1)S(1)} fusion(bf16[8,256,256]{2,1,0:T(8,128)(2,1)S(1)} %get-tuple-element.12, bf16[8,256,256]{2,1,0:T(8,128)(2,1)S(1)} %get-tuple-element.11, bf16[256,256]{1,0:T(8,128)(2,1)S(1)} %get-tuple-element.37, bf16[256,256]{1,0:T(8,128)(2,1)S(1)} %fusion.61, bf16[256,256]{1,0:T(8,128)(2,1)S(1)} %get-tuple-element.36), kind=kOutput, calls=%fused_computation.41 | convolution fusion | flops 1081081856 | bytes 4587520 | tf_op jit(solution)/shard_map/cyn,nm->cym/dot_general | solution.py:137
  22.7 1.4 %copy-done.3 = bf16[1,8,256,512]{2,3,1,0:T(8,128)(2,1)S(1)} copy-done((bf16[1,8,256,512]{2,3,1,0:T(8,128)(2,1)S(1)}, bf16[1,8,256,512]{2,3,1,0:T(8,128)(2,1)}, u32[]{:S(2)}) %copy-start.3) | copy-done | bytes 2097176
  24.1 1.6 %fusion.13 = bf16[8,256,512]{1,2,0:T(8,128)(2,1)S(1)} fusion(bf16[8,256,256]{2,1,0:T(8,128)(2,1)S(1)} %get-tuple-element.16, bf16[8,256,256]{2,1,0:T(8,128)(2,1)S(1)} %get-tuple-element.15, bf16[8,256,512]{2,1,0:T(8,128)(2,1)S(1)} %fusion.29, bf16[1,8,256,512]{2,3,1,0:T(8,128)(2,1)S(1)} %copy-done.3, f32[8,256]{1,0:T(8,128)S(1)} %convert_bitcast_fusion.2, ...), kind=kOutput, calls=%fused_computation.15 | convolution fusion | flops 1091043328 | bytes 8658944 | tf_op jit(solution)/shard_map/kj,cjn->ckn/dot_general | solution.py:141
  25.7 1.1 %fusion.73 = (bf16[8,256,256]{1,2,0:T(8,128)(2,1)S(1)}, bf16[8,256,256]{1,2,0:T(8,128)(2,1)}) fusion(bf16[8,256,512]{1,2,0:T(8,128)(2,1)S(1)} %fusion.13), kind=kLoop, calls=%fused_computation.146 | loop fusion | flops 524288 | bytes 4194304 | tf_op jit(solution)/shard_map/slice | solution.py:25
  27.4 8.3 %fusion.26 = f32[8,256,512]{2,1,0:T(8,128)} fusion(bf16[8,256,256]{1,2,0:T(8,128)(2,1)} %get-tuple-element.14, bf16[8,256,256]{1,2,0:T(8,128)(2,1)S(1)} %get-tuple-element.13, bf16[8,256,512]{1,2,0:T(8,128)(2,1)} %copy-done.4, bf16[256,256]{1,0:T(8,128)(2,1)S(1)} %get-tuple-element.37, bf16[256,256]{1,0:T(8,128)(2,1)S(1)} %get-tuple-element.36, ...), kind=kOutput, calls=%fused_computation.34 | convolution fusion | flops 2163736576 | bytes 8781824 | tf_op jit(solution)/shard_map/cyn,nm->cym/dot_general | solution.py:148
  35.6 2.8 %fusion.20 = (f32[8,256,256]{2,1,0:T(8,128)S(1)}, f32[8,256,256]{2,1,0:T(8,128)S(1)}) fusion(f32[8,256,512]{2,1,0:T(8,128)} %fusion.26, bf16[8,256,512]{2,1,0:T(8,128)(2,1)S(1)} %copy-done), kind=kLoop, calls=%fused_computation.28 | loop fusion | flops 4194304 | bytes 10485760 | tf_op jit(solution)/shard_map/add | solution.py:44
  38.9 0.9 %collective-permute-start.7 = (bf16[64,512]{1,0:T(8,128)(2,1)S(1)}, bf16[64,512]{1,0:T(8,128)(2,1)S(1)}, u32[]{:S(2)}, u32[]{:S(2)}) collective-permute-start(bf16[64,512]{1,0:T(8,128)(2,1)S(1)} %get-tuple-element.21), channel_id=1, source_target_pairs={{0,2},{1,3},{2,0},{3,1},{4,6},{5,7},{6,4},{7,5},{8,10},{9,11},{10,... | collective-permute-start | bytes 196616 | tf_op jit(solution)/shard_map/ppermute | solution.py:94
  39.8 1.4 %collective-permute-start.8 = (bf16[64,512]{1,0:T(8,128)(2,1)S(1)}, bf16[64,512]{1,0:T(8,128)(2,1)S(1)}, u32[]{:S(2)}, u32[]{:S(2)}) collective-permute-start(bf16[64,512]{1,0:T(8,128)(2,1)S(1)} %get-tuple-element.20), channel_id=1, source_target_pairs={{0,3},{1,0},{2,1},{3,2},{4,7},{5,4},{6,5},{7,6},{8,11},{9,8},{10,9... | collective-permute-start | bytes 196616 | tf_op jit(solution)/shard_map/ppermute | solution.py:94
  41.2 1.4 %collective-permute-done.6 = bf16[64,512]{1,0:T(8,128)(2,1)S(1)} collective-permute-done((bf16[64,512]{1,0:T(8,128)(2,1)S(1)}, bf16[64,512]{1,0:T(8,128)(2,1)S(1)}, u32[]{:S(2)}, u32[]{:S(2)}) %collective-permute-start.6) | collective-permute-done | bytes 65568 | tf_op jit(solution)/shard_map/ppermute | solution.py:94
  42.6 1.2 %collective-permute-done.7 = bf16[64,512]{1,0:T(8,128)(2,1)S(1)} collective-permute-done((bf16[64,512]{1,0:T(8,128)(2,1)S(1)}, bf16[64,512]{1,0:T(8,128)(2,1)S(1)}, u32[]{:S(2)}, u32[]{:S(2)}) %collective-permute-start.7) | collective-permute-done | bytes 65568 | tf_op jit(solution)/shard_map/ppermute | solution.py:94
  44.3 2.9 %collective-permute-start.9 = (bf16[64,2,64]{2,0,1:T(8,128)(2,1)S(1)}, bf16[64,2,64]{2,0,1:T(8,128)(2,1)S(1)}, u32[]{:S(2)}, u32[]{:S(2)}) collective-permute-start(bf16[64,2,64]{2,0,1:T(8,128)(2,1)S(1)} %bitcast.132), channel_id=1, source_target_pairs={{0,12},{4,0},{8,4},{12,8},{1,13},{5,1},{9,5},{13,9},{2,14},{6,2},{... | collective-permute-start | bytes 49160 | tf_op jit(solution)/shard_map/ppermute | solution.py:82
  47.2 1.2 %collective-permute-start.10 = (bf16[64,2,64]{2,0,1:T(8,128)(2,1)S(1)}, bf16[64,2,64]{2,0,1:T(8,128)(2,1)S(1)}, u32[]{:S(2)}, u32[]{:S(2)}) collective-permute-start(bf16[64,2,64]{2,0,1:T(8,128)(2,1)S(1)} %bitcast.133), channel_id=1, source_target_pairs={{0,8},{4,12},{8,0},{12,4},{1,9},{5,13},{9,1},{13,5},{2,10},{6,14},... | collective-permute-start | bytes 49160 | tf_op jit(solution)/shard_map/ppermute | solution.py:82
  49.0 3.1 %collective-permute-done.10 = bf16[64,2,64]{2,0,1:T(8,128)(2,1)S(1)} collective-permute-done((bf16[64,2,64]{2,0,1:T(8,128)(2,1)S(1)}, bf16[64,2,64]{2,0,1:T(8,128)(2,1)S(1)}, u32[]{:S(2)}, u32[]{:S(2)}) %collective-permute-start.10) | collective-permute-done | bytes 16416 | tf_op jit(solution)/shard_map/ppermute | solution.py:82
  52.1 2.1 %collective-permute-done.11 = bf16[64,2,64]{2,0,1:T(8,128)(2,1)S(1)} collective-permute-done((bf16[64,2,64]{2,0,1:T(8,128)(2,1)S(1)}, bf16[64,2,64]{2,0,1:T(8,128)(2,1)S(1)}, u32[]{:S(2)}, u32[]{:S(2)}) %collective-permute-start.11) | collective-permute-done | bytes 16416 | tf_op jit(solution)/shard_map/ppermute | solution.py:82
  55.1 1.1 %fusion.36 = f32[2,16,64,64]{3,2,1,0:T(8,128)} fusion(f32[2,16,64,64]{3,2,1,0:T(8,128)S(1)} %copy-done.1, f32[1,16,64,64]{3,2,1,0:T(8,128)S(1)} %bitcast.124, f32[1,16,64,64]{3,2,1,0:T(8,128)S(1)} %bitcast.123), kind=kLoop, calls=%fused_computation.45 | loop fusion | flops 393216 | bytes 1572864 | tf_op jit(solution)/shard_map/sub | solution.py:165
  (72 shorter events, 6.0 us)
Async XLA Ops:
  0.0 10.3 %copy-start.7 = (s32[1,8,256]{2,1,0:T(8,128)S(1)}, s32[1,8,256]{2,1,0:T(8,128)}, u32[]{:S(2)}) copy-start(s32[1,8,256]{2,1,0:T(8,128)} %param.9) | copy-start | bytes 24580
  0.0 11.4 %copy-start.2 = (bf16[1,8,256,512]{3,2,1,0:T(8,128)(2,1)S(1)}, bf16[1,8,256,512]{3,2,1,0:T(8,128)(2,1)}, u32[]{:S(2)}) copy-start(bf16[1,8,256,512]{3,2,1,0:T(8,128)(2,1)} %param.8) | copy-start | bytes 6291460
  3.1 10.8 %collective-permute-start = (bf16[64,2,64]{2,0,1:T(8,128)(2,1)S(1)}, bf16[64,2,64]{2,0,1:T(8,128)(2,1)S(1)}, u32[]{:S(2)}, u32[]{:S(2)}) collective-permute-start(bf16[64,2,64]{2,0,1:T(8,128)(2,1)S(1)} %get-tuple-element.32), channel_id=1, source_target_pairs={{0,12},{4,0},{8,4},{12,8},{1,13},{5,1},{9,5},{13,9},{2,14},{6,2},{... | collective-permute-start | bytes 49160 | tf_op jit(solution)/shard_map/ppermute | solution.py:82
  8.2 5.7 %collective-permute-start.1 = (bf16[64,2,64]{2,0,1:T(8,128)(2,1)S(1)}, bf16[64,2,64]{2,0,1:T(8,128)(2,1)S(1)}, u32[]{:S(2)}, u32[]{:S(2)}) collective-permute-start(bf16[64,2,64]{2,0,1:T(8,128)(2,1)S(1)} %get-tuple-element.33), channel_id=1, source_target_pairs={{0,8},{4,12},{8,0},{12,4},{1,9},{5,13},{9,1},{13,5},{2,10},{6,14},... | collective-permute-start | bytes 49160 | tf_op jit(solution)/shard_map/ppermute | solution.py:82
  8.2 5.7 %collective-permute-start.2 = (bf16[64,2,64]{2,0,1:T(8,128)(2,1)S(1)}, bf16[64,2,64]{2,0,1:T(8,128)(2,1)S(1)}, u32[]{:S(2)}, u32[]{:S(2)}) collective-permute-start(bf16[64,2,64]{2,0,1:T(8,128)(2,1)S(1)} %get-tuple-element.30), channel_id=1, source_target_pairs={{0,4},{4,8},{8,12},{12,0},{1,5},{5,9},{9,13},{13,1},{2,6},{6,10},{... | collective-permute-start | bytes 49160 | tf_op jit(solution)/shard_map/ppermute | solution.py:82
  11.3 9.9 %copy-start.5 = (bf16[256,256]{1,0:T(8,128)(2,1)}, bf16[256,256]{1,0:T(8,128)(2,1)S(1)}, u32[]{:S(2)}) copy-start(bf16[256,256]{1,0:T(8,128)(2,1)S(1)} %fusion.61) | copy-start | bytes 393220
  13.8 6.6 %copy-start = (bf16[8,256,512]{2,1,0:T(8,128)(2,1)S(1)}, bf16[8,256,512]{2,1,0:T(8,128)(2,1)}, u32[]{:S(2)}) copy-start(bf16[8,256,512]{2,1,0:T(8,128)(2,1)} %param.7) | copy-start | bytes 6291460
  14.4 2.0 %collective-permute-start.3 = (bf16[64,512]{1,0:T(8,128)(2,1)S(1)}, bf16[64,512]{1,0:T(8,128)(2,1)S(1)}, u32[]{:S(2)}, u32[]{:S(2)}) collective-permute-start(bf16[64,512]{1,0:T(8,128)(2,1)S(1)} %reshape.30), channel_id=1, source_target_pairs={{0,3},{1,0},{2,1},{3,2},{4,7},{5,4},{6,5},{7,6},{8,11},{9,8},{10,9... | collective-permute-start | bytes 196616 | tf_op jit(solution)/shard_map/ppermute | solution.py:70
  14.6 5.6 %collective-permute-start.4 = (bf16[64,512]{1,0:T(8,128)(2,1)S(1)}, bf16[64,512]{1,0:T(8,128)(2,1)S(1)}, u32[]{:S(2)}, u32[]{:S(2)}) collective-permute-start(bf16[64,512]{1,0:T(8,128)(2,1)S(1)} %reshape.30), channel_id=1, source_target_pairs={{0,2},{1,3},{2,0},{3,1},{4,6},{5,7},{6,4},{7,5},{8,10},{9,11},{10,... | collective-permute-start | bytes 196616 | tf_op jit(solution)/shard_map/ppermute | solution.py:70
  16.0 4.3 %collective-permute-start.5 = (bf16[64,512]{1,0:T(8,128)(2,1)S(1)}, bf16[64,512]{1,0:T(8,128)(2,1)S(1)}, u32[]{:S(2)}, u32[]{:S(2)}) collective-permute-start(bf16[64,512]{1,0:T(8,128)(2,1)S(1)} %reshape.30), channel_id=1, source_target_pairs={{0,1},{1,2},{2,3},{3,0},{4,5},{5,6},{6,7},{7,4},{8,9},{9,10},{10,1... | collective-permute-start | bytes 196616 | tf_op jit(solution)/shard_map/ppermute | solution.py:70
  22.5 1.6 %copy-start.3 = (bf16[1,8,256,512]{2,3,1,0:T(8,128)(2,1)S(1)}, bf16[1,8,256,512]{2,3,1,0:T(8,128)(2,1)}, u32[]{:S(2)}) copy-start(bf16[1,8,256,512]{2,3,1,0:T(8,128)(2,1)} %copy.28) | copy-start | bytes 6291460
  25.7 1.7 %copy-start.4 = (bf16[8,256,512]{1,2,0:T(8,128)(2,1)}, bf16[8,256,512]{1,2,0:T(8,128)(2,1)S(1)}, u32[]{:S(2)}) copy-start(bf16[8,256,512]{1,2,0:T(8,128)(2,1)S(1)} %fusion.13) | copy-start | bytes 6291460
  25.7 1.7 %copy-start.6 = (bf16[256,256]{1,0:T(8,128)(2,1)S(1)}, bf16[256,256]{1,0:T(8,128)(2,1)}, u32[]{:S(2)}) copy-start(bf16[256,256]{1,0:T(8,128)(2,1)} %copy-done.5) | copy-start | bytes 393220
  38.8 3.8 %collective-permute-start.6 = (bf16[64,512]{1,0:T(8,128)(2,1)S(1)}, bf16[64,512]{1,0:T(8,128)(2,1)S(1)}, u32[]{:S(2)}, u32[]{:S(2)}) collective-permute-start(bf16[64,512]{1,0:T(8,128)(2,1)S(1)} %get-tuple-element.19), channel_id=1, source_target_pairs={{0,1},{1,2},{2,3},{3,0},{4,5},{5,6},{6,7},{7,4},{8,9},{9,10},{10,1... | collective-permute-start | bytes 196616 | tf_op jit(solution)/shard_map/ppermute | solution.py:94
  38.9 5.0 %collective-permute-start.7 = (bf16[64,512]{1,0:T(8,128)(2,1)S(1)}, bf16[64,512]{1,0:T(8,128)(2,1)S(1)}, u32[]{:S(2)}, u32[]{:S(2)}) collective-permute-start(bf16[64,512]{1,0:T(8,128)(2,1)S(1)} %get-tuple-element.21), channel_id=1, source_target_pairs={{0,2},{1,3},{2,0},{3,1},{4,6},{5,7},{6,4},{7,5},{8,10},{9,11},{10,... | collective-permute-start | bytes 196616 | tf_op jit(solution)/shard_map/ppermute | solution.py:94
  39.8 4.1 %collective-permute-start.8 = (bf16[64,512]{1,0:T(8,128)(2,1)S(1)}, bf16[64,512]{1,0:T(8,128)(2,1)S(1)}, u32[]{:S(2)}, u32[]{:S(2)}) collective-permute-start(bf16[64,512]{1,0:T(8,128)(2,1)S(1)} %get-tuple-element.20), channel_id=1, source_target_pairs={{0,3},{1,0},{2,1},{3,2},{4,7},{5,4},{6,5},{7,6},{8,11},{9,8},{10,9... | collective-permute-start | bytes 196616 | tf_op jit(solution)/shard_map/ppermute | solution.py:94
  41.2 13.9 %copy-start.1 = (f32[2,16,64,64]{3,2,1,0:T(8,128)S(1)}, f32[2,16,64,64]{3,2,1,0:T(8,128)}, u32[]{:S(2)}) copy-start(f32[2,16,64,64]{3,2,1,0:T(8,128)} %param.5) | copy-start | bytes 1572868
  44.3 4.7 %collective-permute-start.9 = (bf16[64,2,64]{2,0,1:T(8,128)(2,1)S(1)}, bf16[64,2,64]{2,0,1:T(8,128)(2,1)S(1)}, u32[]{:S(2)}, u32[]{:S(2)}) collective-permute-start(bf16[64,2,64]{2,0,1:T(8,128)(2,1)S(1)} %bitcast.132), channel_id=1, source_target_pairs={{0,12},{4,0},{8,4},{12,8},{1,13},{5,1},{9,5},{13,9},{2,14},{6,2},{... | collective-permute-start | bytes 49160 | tf_op jit(solution)/shard_map/ppermute | solution.py:82
  47.2 4.9 %collective-permute-start.10 = (bf16[64,2,64]{2,0,1:T(8,128)(2,1)S(1)}, bf16[64,2,64]{2,0,1:T(8,128)(2,1)S(1)}, u32[]{:S(2)}, u32[]{:S(2)}) collective-permute-start(bf16[64,2,64]{2,0,1:T(8,128)(2,1)S(1)} %bitcast.133), channel_id=1, source_target_pairs={{0,8},{4,12},{8,0},{12,4},{1,9},{5,13},{9,1},{13,5},{2,10},{6,14},... | collective-permute-start | bytes 49160 | tf_op jit(solution)/shard_map/ppermute | solution.py:82
  48.4 5.8 %collective-permute-start.11 = (bf16[64,2,64]{2,0,1:T(8,128)(2,1)S(1)}, bf16[64,2,64]{2,0,1:T(8,128)(2,1)S(1)}, u32[]{:S(2)}, u32[]{:S(2)}) collective-permute-start(bf16[64,2,64]{2,0,1:T(8,128)(2,1)S(1)} %bitcast.134), channel_id=1, source_target_pairs={{0,4},{4,8},{8,12},{12,0},{1,5},{5,9},{9,13},{13,1},{2,6},{6,10},{... | collective-permute-start | bytes 49160 | tf_op jit(solution)/shard_map/ppermute | solution.py:82

commit v4 on v3

--- a/solution.py
+++ b/solution.py
@@ -3,6 +3,8 @@
 import jax
 import jax.numpy as jnp
 from jax import lax
+from jax.experimental import pallas as pl
+from jax.experimental.pallas import tpu as pltpu
 from jax.sharding import PartitionSpec as P
 
 
@@ -93,6 +95,80 @@
         outgoing = lax.dynamic_index_in_dim(blocks, (me + step) % count, 0, keepdims=False)
         total = total + lax.ppermute(outgoing.astype(jnp.bfloat16), axis, shifted(count, step)).astype(jnp.float32)
     return total
+
+
+def swap_halves(values, half_width, negate_first):
+    low = values[:, :half_width]
+    high = values[:, half_width:]
+    if negate_first:
+        return jnp.concatenate([-high, low], axis=1)
+    return jnp.concatenate([high, -low], axis=1)
+
+
+def coil_chain_kernel(image_ref, sens_ref, measured_ref, sampled_ref, forward_ref, adjoint_ref,
+                      table_re_ref, table_im_ref, out_ref):
+    half_width = image_ref.shape[1] // 2
+    sens = sens_ref[0].astype(jnp.float32)
+    sens_re = sens[:, :half_width]
+    sens_im = sens[:, half_width:]
+    image = image_ref[...].astype(jnp.float32)
+    image_re = image[:, :half_width]
+    image_im = image[:, half_width:]
+    coil = jnp.concatenate(
+        [sens_re * image_re - sens_im * image_im, sens_re * image_im + sens_im * image_re], axis=1
+    ).astype(jnp.bfloat16)
+    half_k = jnp.dot(coil, forward_ref[...], preferred_element_type=jnp.float32).astype(jnp.bfloat16)
+    table_re = table_re_ref[...]
+    table_im = table_im_ref[...]
+    kspace = jnp.dot(table_re, half_k, preferred_element_type=jnp.float32) + jnp.dot(
+        table_im, swap_halves(half_k, half_width, True), preferred_element_type=jnp.float32
+    )
+    residual = (sampled_ref[0] * (kspace - measured_ref[0].astype(jnp.float32))).astype(jnp.bfloat16)
+    back_half = (
+        jnp.dot(table_re, residual, preferred_element_type=jnp.float32)
+        + jnp.dot(table_im, swap_halves(residual, half_width, False), preferred_element_type=jnp.float32)
+    ).astype(jnp.bfloat16)
+    coil_back = jnp.dot(back_half, adjoint_ref[...], preferred_element_type=jnp.float32)
+    back_re = coil_back[:, :half_width]
+    back_im = coil_back[:, half_width:]
+    term = jnp.concatenate(
+        [sens_re * back_re + sens_im * back_im, sens_re * back_im - sens_im * back_re], axis=1
+    )
+
+    @pl.when(pl.program_id(0) == 0)
+    def _():
+        out_ref[...] = term
+
+    @pl.when(pl.program_id(0) > 0)
+    def _():
+        out_ref[...] += term
+
+
+def coil_chain(image, sens, measured, sampled, forward_x, adjoint_x, table_y_re, table_y_im):
+    coils, rows, width = sens.shape
+    whole = lambda c: (0, 0)
+    per_coil = lambda c: (c, 0, 0)
+    flops = coils * 8 * rows * width * width
+    return pl.pallas_call(
+        coil_chain_kernel,
+        out_shape=jax.ShapeDtypeStruct((rows, width), jnp.float32),
+        grid=(coils,),
+        in_specs=[
+            pl.BlockSpec((rows, width), whole),
+            pl.BlockSpec((1, rows, width), per_coil),
+            pl.BlockSpec((1, rows, width), per_coil),
+            pl.BlockSpec((1, rows, 1), per_coil),
+            pl.BlockSpec((width, width), whole),
+            pl.BlockSpec((width, width), whole),
+            pl.BlockSpec((rows, rows), whole),
+            pl.BlockSpec((rows, rows), whole),
+        ],
+        out_specs=pl.BlockSpec((rows, width), whole),
+        compiler_params=pltpu.CompilerParams(dimension_semantics=("arbitrary",)),
+        cost_estimate=pl.CostEstimate(
+            flops=flops, transcendentals=0, bytes_accessed=2 * 2 * coils * rows * width + 4 * rows * width
+        ),
+    )(image, sens, measured, sampled, forward_x, adjoint_x, table_y_re, table_y_im)
 
 
 def on_device(factors, temporal, maps, kdata, masks):
@@ -132,22 +208,8 @@
     pieces_x = exchange_blocks(images, "frame")
     own_rows = jnp.transpose(pieces_x, (1, 2, 0, 3)).reshape(rows_own, 2 * width_x)
     full_image = gather_blocks(own_rows, "coil").reshape(width_y, 2 * width_x)
-    sens = maps
-    coil_image = sens_times(sens, full_image[None], width_x).astype(jnp.bfloat16)
-    half_k = jnp.einsum(
-        "cyn,nm->cym", coil_image, forward_x, preferred_element_type=jnp.float32
-    ).astype(jnp.bfloat16)
-    stacked = jnp.concatenate([half_k, rotate_plus(half_k, width_x)], axis=1)
-    kspace = jnp.einsum("kj,cjn->ckn", wide_y, stacked, preferred_element_type=jnp.float32)
     sampled = masks[0].astype(jnp.float32)[:, :, None]
-    residual = (sampled * (kspace - kdata[0].astype(jnp.float32))).astype(jnp.bfloat16)
-    resid_stack = jnp.concatenate([residual, rotate_minus(residual, width_x)], axis=1)
-    back_half = jnp.einsum(
-        "kj,cjn->ckn", wide_y, resid_stack, preferred_element_type=jnp.float32
-    ).astype(jnp.bfloat16)
-    coil_back = jnp.einsum("cyn,nm->cym", back_half, adjoint_x, preferred_element_type=jnp.float32)
-    sens = maps
-    combined = jnp.sum(conj_sens_times(sens, coil_back, width_x), axis=0)
+    combined = coil_chain(full_image, maps, kdata[0], sampled, forward_x, adjoint_x, table_y_re, table_y_im)
     groups = width_y // rows_own
     own_share = reduce_blocks(combined.reshape(groups, rows_own, 2 * width_x), "coil")
     outgoing = jnp.transpose(

time: 56.4 us -> 52.2 us (0.926)
  Pallas kernels: 0 us -> 11.6 us
  matrix products: 11.1 us -> 0 us
  other arithmetic: 10.1 us -> 6.96 us
  local copies, waits for them, and re-layouts: 7.7 us -> 6.19 us
    pallas_call x0 -> x1, Pallas kernels: none -> 11.6 us  [coil_chain(): pl.pallas_call(coil_chain_kernel, out_shape=jax.ShapeDtypeStruct((rows, w...]
    dot_general x3 -> x0, matrix products: 11.1 us -> none  [the longest x1 8.27 us: on_device(): jnp.einsum('cyn,nm->cym', back_half, adjoint_x, preferred_element_type=jn...]
    unnamed x36 -> x27, local copies, waits for them, and re-layouts: 4.63 us -> 0.18 us
    add x1 -> x0, other arithmetic: 2.83 us -> none  [conj_sens_times(): sens_re * value_re + sens_im * value_im]
    convert_element_type x0 -> x1, local copies, waits for them, and re-layouts: none -> 1.34 us  [on_device(): sampled = masks[0].astype(jnp.float32)[:, :, None]]
    slice x1 -> x0, other arithmetic: 1.11 us -> none  [rotate_minus(): values[..., half_width:]]
    concatenate x0 -> x1, other arithmetic: none -> 1.06 us  [on_device(): jnp.concatenate([jnp.concatenate([table_x_re, -table_x_im], axis=1), jnp....]
    convert_element_type x1, local copies, waits for them, and re-layouts: 0.04 us -> 1.05 us  [reduce_blocks(): outgoing.astype(jnp.bfloat16)]
  transfers between devices with their start and end apart: 12 -> 12, of which waited for: 8 -> 9; matrix products, arithmetic and copies ran while one was open for 8% -> 9% of each run, Pallas kernels for 0% -> 0%
where the time goes in v4:
time: 52.2 us; the launch traced here: 51.9 us
  starting transfers between devices  14.3 us (27%)
  waiting for transfers between devices  12.5 us (24%)
  Pallas kernels  11.6 us (22%)
  other arithmetic  6.96 us (13%)
  local copies, waits for them, and re-layouts  6.19 us (12%)
    pallas_call x1, Pallas kernels, coil_chain(): pl.pallas_call(coil_chain_kernel, out_shape=jax.ShapeDtypeStruct((rows, w...  11.6 us
    ppermute x6, starting transfers between devices, exchange_blocks(): pieces.append(lax.ppermute(outgoing, axis, shifted(count, step)))  10.2 us
    ppermute x6, waiting for transfers between devices, exchange_blocks(): pieces.append(lax.ppermute(outgoing, axis, shifted(count, step)))  5.79 us
    ppermute x3, waiting for transfers between devices, gather_blocks(): lax.ppermute(value, axis, shifted(count, step))  4.09 us
    ppermute x3, waiting for transfers between devices, reduce_blocks(): lax.ppermute(outgoing.astype(jnp.bfloat16), axis, shifted(count, step))  2.65 us
    ppermute x3, starting transfers between devices, reduce_blocks(): lax.ppermute(outgoing.astype(jnp.bfloat16), axis, shifted(count, step))  2.39 us
    ppermute x3, starting transfers between devices, gather_blocks(): lax.ppermute(value, axis, shifted(count, step))  1.78 us
    convert_element_type x1, local copies, waits for them, and re-layouts, on_device(): sampled = masks[0].astype(jnp.float32)[:, :, None]  1.34 us
  transfers between devices with their start and end apart: 12, of which 9 were waited for; matrix products, arithmetic and copies ran while one was open for 9% of the time, Pallas kernels for 0%

profile of v4, /device:TPU:0, one launch (start us, length us, event | category | flops | bytes accessed | tf_op | source)
XLA Modules:
  0.0 51.9 jit_solution(9070800771381002727)
XLA Ops:
  0.7 1.3 %slice_bitcast_fusion.1 = (f32[16,64,64]{2,1,0:T(8,128)S(1)}, f32[16,64,64]{2,1,0:T(8,128)S(1)}) fusion(f32[2,16,64,64]{3,2,1,0:T(8,128)} %param.5), kind=kLoop, calls=%fused_computation.13 | loop fusion | bytes 1048576 | tf_op jit(solution)/shard_map/mul | solution.py:200
  2.0 0.9 %subtract_reduce_fusion.1 = (bf16[4,64,64]{2,1,0:T(8,128)(2,1)S(1)}, bf16[4,64,64]{2,1,0:T(8,128)(2,1)S(1)}) fusion(f32[16,64,64]{2,1,0:T(8,128)S(1)} %get-tuple-element.10, f32[4,16]{1,0:T(4,128)S(1)} %get-tuple-element.27, f32[16,64,64]{2,1,0:T(8,128)S(1)} %get-tuple-element.9, f32[4,16]{1,0:T(4,128)S(1)} %get-tuple-element.26), kind=kLoop, calls=%fused_computation.3 | loop fusion | flops 2064384 | bytes 590336 | tf_op jit(solution)/shard_map/reduce_sum | solution.py:199
  3.0 5.1 %collective-permute-start = (bf16[64,2,64]{2,0,1:T(8,128)(2,1)S(1)}, bf16[64,2,64]{2,0,1:T(8,128)(2,1)S(1)}, u32[]{:S(2)}, u32[]{:S(2)}) collective-permute-start(bf16[64,2,64]{2,0,1:T(8,128)(2,1)S(1)} %get-tuple-element.24), channel_id=1, source_target_pairs={{0,12},{4,0},{8,4},{12,8},{1,13},{5,1},{9,5},{13,9},{2,14},{6,2},{... | collective-permute-start | bytes 49160 | tf_op jit(solution)/shard_map/ppermute | solution.py:84
  8.1 1.0 %collective-permute-start.2 = (bf16[64,2,64]{2,0,1:T(8,128)(2,1)S(1)}, bf16[64,2,64]{2,0,1:T(8,128)(2,1)S(1)}, u32[]{:S(2)}, u32[]{:S(2)}) collective-permute-start(bf16[64,2,64]{2,0,1:T(8,128)(2,1)S(1)} %get-tuple-element.22), channel_id=1, source_target_pairs={{0,4},{4,8},{8,12},{12,0},{1,5},{5,9},{9,13},{13,1},{2,6},{6,10},{... | collective-permute-start | bytes 49160 | tf_op jit(solution)/shard_map/ppermute | solution.py:84
  9.1 1.1 %multiply_convert_fusion = (bf16[256,256]{1,0:T(8,128)(2,1)S(1)}, bf16[256,256]{1,0:T(8,128)(2,1)S(1)}) fusion(), kind=kLoop, calls=%fused_computation.20 | loop fusion | flops 1245184 | bytes 262144 | tf_op jit(solution)/shard_map/convert_element_type | solution.py:18
  10.2 1.0 %fusion.15 = bf16[256,256]{1,0:T(8,128)(2,1)S(1)} fusion(), kind=kLoop, calls=%fused_computation.73 | loop fusion | flops 1310720 | bytes 131072 | tf_op jit(solution)/shard_map/neg | solution.py:183
  11.2 1.1 %fusion.2 = (bf16[512,512]{1,0:T(8,128)(2,1)}, bf16[512,512]{1,0:T(8,128)(2,1)}) fusion(bf16[256,256]{1,0:T(8,128)(2,1)S(1)} %get-tuple-element.29.table_re_ref, bf16[256,256]{1,0:T(8,128)(2,1)S(1)} %get-tuple-element.28.table_im_ref, bf16[256,256]{1,0:T(8,128)(2,1)S(1)} %fusion.15), kind=kLoop, calls=%fused_computation.11 | loop fusion | flops 3670016 | bytes 1441792 | tf_op jit(solution)/shard_map/concatenate | solution.py:187
  12.3 1.3 %copy.22.sampled_ref = f32[8,256,1]{2,1,0:T(8,128)} copy(f32[8,256,1]{1,0,2:T(8,128)S(1)} %convert_bitcast_fusion.2) | data formatting | bytes 16384 | tf_op jit(solution)/shard_map/convert_element_type | solution.py:211
  14.4 1.6 %collective-permute-start.4 = (bf16[64,512]{1,0:T(8,128)(2,1)S(1)}, bf16[64,512]{1,0:T(8,128)(2,1)S(1)}, u32[]{:S(2)}, u32[]{:S(2)}) collective-permute-start(bf16[64,512]{1,0:T(8,128)(2,1)S(1)} %reshape.36), channel_id=1, source_target_pairs={{0,2},{1,3},{2,0},{3,1},{4,6},{5,7},{6,4},{7,5},{8,10},{9,11},{10,... | collective-permute-start | bytes 196616 | tf_op jit(solution)/shard_map/ppermute | solution.py:72
  16.3 3.7 %collective-permute-done.4 = bf16[64,512]{1,0:T(8,128)(2,1)S(1)} collective-permute-done((bf16[64,512]{1,0:T(8,128)(2,1)S(1)}, bf16[64,512]{1,0:T(8,128)(2,1)S(1)}, u32[]{:S(2)}, u32[]{:S(2)}) %collective-permute-start.4) | collective-permute-done | bytes 65568 | tf_op jit(solution)/shard_map/ppermute | solution.py:72
  20.2 0.7 %constant_dynamic-slice_fusion.4 = bf16[4,64,512]{2,1,0:T(8,128)(2,1)} fusion(bf16[8,64,512]{2,1,0:T(8,128)(2,1)S(1)} %bitcast_dynamic-update-slice_fusion.1, s32[]{:T(128)S(6)} %select_n.116), kind=kLoop, calls=%fused_computation.89 | loop fusion | bytes 524292 | tf_op jit(solution)/shard_map/dynamic_slice | solution.py:64
  21.0 11.6 %shard_map.55 = f32[256,512]{1,0:T(8,128)} custom-call(bf16[256,512]{1,0:T(8,128)(2,1)} %bitcast.98, bf16[8,256,512]{2,1,0:T(8,128)(2,1)} %sens_ref.1, bf16[8,256,512]{2,1,0:T(8,128)(2,1)} %bitcast.104, f32[8,256,1]{2,1,0:T(8,128)} %copy.22.sampled_ref, bf16[512,512]{1,0:T(8,128)(2,1)} %get-tuple-element.15.forward_ref, ...), custom_call_target="tpu_custom_call" | custom-call | flops 4294967296 | bytes 4718592 | tf_op jit(solution)/shard_map/pallas_call | solution.py:152
  32.6 1.1 %fusion.12 = (bf16[64,512]{1,0:T(8,128)(2,1)S(1)}, bf16[64,512]{1,0:T(8,128)(2,1)S(1)}, bf16[64,512]{1,0:T(8,128)(2,1)S(1)}) fusion(f32[4,64,512]{2,1,0:T(8,128)} %bitcast.99, s32[]{:T(128)S(6)} %select_n.120, s32[]{:T(128)S(6)} %select_n.124, s32[]{:T(128)S(6)} %select_n.122), kind=kLoop, calls=%fused_computation.44 | loop fusion | bytes 393228 | tf_op jit(solution)/shard_map/convert_element_type | solution.py:96
  33.8 0.9 %collective-permute-start.7 = (bf16[64,512]{1,0:T(8,128)(2,1)S(1)}, bf16[64,512]{1,0:T(8,128)(2,1)S(1)}, u32[]{:S(2)}, u32[]{:S(2)}) collective-permute-start(bf16[64,512]{1,0:T(8,128)(2,1)S(1)} %get-tuple-element.13), channel_id=1, source_target_pairs={{0,2},{1,3},{2,0},{3,1},{4,6},{5,7},{6,4},{7,5},{8,10},{9,11},{10,... | collective-permute-start | bytes 196616 | tf_op jit(solution)/shard_map/ppermute | solution.py:96
  34.7 1.4 %collective-permute-start.8 = (bf16[64,512]{1,0:T(8,128)(2,1)S(1)}, bf16[64,512]{1,0:T(8,128)(2,1)S(1)}, u32[]{:S(2)}, u32[]{:S(2)}) collective-permute-start(bf16[64,512]{1,0:T(8,128)(2,1)S(1)} %get-tuple-element.12), channel_id=1, source_target_pairs={{0,3},{1,0},{2,1},{3,2},{4,7},{5,4},{6,5},{7,6},{8,11},{9,8},{10,9... | collective-permute-start | bytes 196616 | tf_op jit(solution)/shard_map/ppermute | solution.py:96
  36.1 1.4 %collective-permute-done.6 = bf16[64,512]{1,0:T(8,128)(2,1)S(1)} collective-permute-done((bf16[64,512]{1,0:T(8,128)(2,1)S(1)}, bf16[64,512]{1,0:T(8,128)(2,1)S(1)}, u32[]{:S(2)}, u32[]{:S(2)}) %collective-permute-start.6) | collective-permute-done | bytes 65568 | tf_op jit(solution)/shard_map/ppermute | solution.py:96
  37.5 1.2 %collective-permute-done.7 = bf16[64,512]{1,0:T(8,128)(2,1)S(1)} collective-permute-done((bf16[64,512]{1,0:T(8,128)(2,1)S(1)}, bf16[64,512]{1,0:T(8,128)(2,1)S(1)}, u32[]{:S(2)}, u32[]{:S(2)}) %collective-permute-start.7) | collective-permute-done | bytes 65568 | tf_op jit(solution)/shard_map/ppermute | solution.py:96
  38.7 0.9 %fusion.11 = bf16[64,512]{1,0:T(8,128)(2,1)S(1)} fusion(bf16[64,512]{1,0:T(8,128)(2,1)S(1)} %collective-permute-done.8, bf16[64,512]{1,0:T(8,128)(2,1)S(1)} %collective-permute-done.7, bf16[64,512]{1,0:T(8,128)(2,1)S(1)} %collective-permute-done.6, f32[4,64,512]{2,1,0:T(8,128)} %bitcast.100, s32[]{:T(128)S(6)} %select_n.118), kind=kLoop, calls=%fused_computation.38 | loop fusion | flops 229376 | bytes 393220 | tf_op jit(solution)/shard_map/convert_element_type | solution.py:217
  40.1 2.8 %collective-permute-start.9 = (bf16[64,2,64]{2,0,1:T(8,128)(2,1)S(1)}, bf16[64,2,64]{2,0,1:T(8,128)(2,1)S(1)}, u32[]{:S(2)}, u32[]{:S(2)}) collective-permute-start(bf16[64,2,64]{2,0,1:T(8,128)(2,1)S(1)} %bitcast.101), channel_id=1, source_target_pairs={{0,12},{4,0},{8,4},{12,8},{1,13},{5,1},{9,5},{13,9},{2,14},{6,2},{... | collective-permute-start | bytes 49160 | tf_op jit(solution)/shard_map/ppermute | solution.py:84
  42.9 1.2 %collective-permute-start.10 = (bf16[64,2,64]{2,0,1:T(8,128)(2,1)S(1)}, bf16[64,2,64]{2,0,1:T(8,128)(2,1)S(1)}, u32[]{:S(2)}, u32[]{:S(2)}) collective-permute-start(bf16[64,2,64]{2,0,1:T(8,128)(2,1)S(1)} %bitcast.102), channel_id=1, source_target_pairs={{0,8},{4,12},{8,0},{12,4},{1,9},{5,13},{9,1},{13,5},{2,10},{6,14},... | collective-permute-start | bytes 49160 | tf_op jit(solution)/shard_map/ppermute | solution.py:84
  44.8 3.1 %collective-permute-done.10 = bf16[64,2,64]{2,0,1:T(8,128)(2,1)S(1)} collective-permute-done((bf16[64,2,64]{2,0,1:T(8,128)(2,1)S(1)}, bf16[64,2,64]{2,0,1:T(8,128)(2,1)S(1)}, u32[]{:S(2)}, u32[]{:S(2)}) %collective-permute-start.10) | collective-permute-done | bytes 16416 | tf_op jit(solution)/shard_map/ppermute | solution.py:84
  47.8 2.1 %collective-permute-done.11 = bf16[64,2,64]{2,0,1:T(8,128)(2,1)S(1)} collective-permute-done((bf16[64,2,64]{2,0,1:T(8,128)(2,1)S(1)}, bf16[64,2,64]{2,0,1:T(8,128)(2,1)S(1)}, u32[]{:S(2)}, u32[]{:S(2)}) %collective-permute-start.11) | collective-permute-done | bytes 16416 | tf_op jit(solution)/shard_map/ppermute | solution.py:84
  50.0 0.7 %add_reduce_fusion = (f32[16,64,64]{2,1,0:T(8,128)S(1)}, f32[16,64,64]{2,1,0:T(8,128)S(1)}) fusion(f32[4,64,64]{2,1,0:T(8,128)S(1)} %get-tuple-element.17, f32[4,64,64]{2,1,0:T(8,128)S(1)} %get-tuple-element.16, f32[4,16]{1,0:T(4,128)S(1)} %get-tuple-element.27, f32[4,16]{1,0:T(4,128)S(1)} %get-tuple-element.26), kind=kLoop, calls=%fused_computation.1 | loop fusion | flops 1966080 | bytes 655872 | tf_op jit(solution)/shard_map/reduce_sum | solution.py:221
  50.8 1.1 %fusion = f32[2,16,64,64]{3,2,1,0:T(8,128)} fusion(f32[2,16,64,64]{3,2,1,0:T(8,128)S(1)} %copy-done, f32[1,16,64,64]{3,2,1,0:T(8,128)S(1)} %bitcast.93, f32[1,16,64,64]{3,2,1,0:T(8,128)S(1)} %bitcast.92), kind=kLoop, calls=%fused_computation.5 | loop fusion | flops 393216 | bytes 1572864 | tf_op jit(solution)/shard_map/sub | solution.py:227
  (57 shorter events, 3.2 us)
Async XLA Ops:
  0.0 11.2 %copy-start.3 = (s32[1,8,256]{2,1,0:T(8,128)S(1)}, s32[1,8,256]{2,1,0:T(8,128)}, u32[]{:S(2)}) copy-start(s32[1,8,256]{2,1,0:T(8,128)} %param.9) | copy-start | bytes 24580
  3.0 10.7 %collective-permute-start = (bf16[64,2,64]{2,0,1:T(8,128)(2,1)S(1)}, bf16[64,2,64]{2,0,1:T(8,128)(2,1)S(1)}, u32[]{:S(2)}, u32[]{:S(2)}) collective-permute-start(bf16[64,2,64]{2,0,1:T(8,128)(2,1)S(1)} %get-tuple-element.24), channel_id=1, source_target_pairs={{0,12},{4,0},{8,4},{12,8},{1,13},{5,1},{9,5},{13,9},{2,14},{6,2},{... | collective-permute-start | bytes 49160 | tf_op jit(solution)/shard_map/ppermute | solution.py:84
  8.1 5.6 %collective-permute-start.1 = (bf16[64,2,64]{2,0,1:T(8,128)(2,1)S(1)}, bf16[64,2,64]{2,0,1:T(8,128)(2,1)S(1)}, u32[]{:S(2)}, u32[]{:S(2)}) collective-permute-start(bf16[64,2,64]{2,0,1:T(8,128)(2,1)S(1)} %get-tuple-element.25), channel_id=1, source_target_pairs={{0,8},{4,12},{8,0},{12,4},{1,9},{5,13},{9,1},{13,5},{2,10},{6,14},... | collective-permute-start | bytes 49160 | tf_op jit(solution)/shard_map/ppermute | solution.py:84
  8.1 5.7 %collective-permute-start.2 = (bf16[64,2,64]{2,0,1:T(8,128)(2,1)S(1)}, bf16[64,2,64]{2,0,1:T(8,128)(2,1)S(1)}, u32[]{:S(2)}, u32[]{:S(2)}) collective-permute-start(bf16[64,2,64]{2,0,1:T(8,128)(2,1)S(1)} %get-tuple-element.22), channel_id=1, source_target_pairs={{0,4},{4,8},{8,12},{12,0},{1,5},{5,9},{9,13},{13,1},{2,6},{6,10},{... | collective-permute-start | bytes 49160 | tf_op jit(solution)/shard_map/ppermute | solution.py:84
  10.2 4.1 %copy-start.1 = (bf16[256,256]{1,0:T(8,128)(2,1)}, bf16[256,256]{1,0:T(8,128)(2,1)S(1)}, u32[]{:S(2)}) copy-start(bf16[256,256]{1,0:T(8,128)(2,1)S(1)} %get-tuple-element.28.table_im_ref) | copy-start | bytes 393220
  10.2 4.1 %copy-start.2 = (bf16[256,256]{1,0:T(8,128)(2,1)}, bf16[256,256]{1,0:T(8,128)(2,1)S(1)}, u32[]{:S(2)}) copy-start(bf16[256,256]{1,0:T(8,128)(2,1)S(1)} %get-tuple-element.29.table_re_ref) | copy-start | bytes 393220
  14.3 2.0 %collective-permute-start.3 = (bf16[64,512]{1,0:T(8,128)(2,1)S(1)}, bf16[64,512]{1,0:T(8,128)(2,1)S(1)}, u32[]{:S(2)}, u32[]{:S(2)}) collective-permute-start(bf16[64,512]{1,0:T(8,128)(2,1)S(1)} %reshape.36), channel_id=1, source_target_pairs={{0,3},{1,0},{2,1},{3,2},{4,7},{5,4},{6,5},{7,6},{8,11},{9,8},{10,9... | collective-permute-start | bytes 196616 | tf_op jit(solution)/shard_map/ppermute | solution.py:72
  14.4 5.6 %collective-permute-start.4 = (bf16[64,512]{1,0:T(8,128)(2,1)S(1)}, bf16[64,512]{1,0:T(8,128)(2,1)S(1)}, u32[]{:S(2)}, u32[]{:S(2)}) collective-permute-start(bf16[64,512]{1,0:T(8,128)(2,1)S(1)} %reshape.36), channel_id=1, source_target_pairs={{0,2},{1,3},{2,0},{3,1},{4,6},{5,7},{6,4},{7,5},{8,10},{9,11},{10,... | collective-permute-start | bytes 196616 | tf_op jit(solution)/shard_map/ppermute | solution.py:72
  15.9 4.3 %collective-permute-start.5 = (bf16[64,512]{1,0:T(8,128)(2,1)S(1)}, bf16[64,512]{1,0:T(8,128)(2,1)S(1)}, u32[]{:S(2)}, u32[]{:S(2)}) collective-permute-start(bf16[64,512]{1,0:T(8,128)(2,1)S(1)} %reshape.36), channel_id=1, source_target_pairs={{0,1},{1,2},{2,3},{3,0},{4,5},{5,6},{6,7},{7,4},{8,9},{9,10},{10,1... | collective-permute-start | bytes 196616 | tf_op jit(solution)/shard_map/ppermute | solution.py:72
  33.7 3.8 %collective-permute-start.6 = (bf16[64,512]{1,0:T(8,128)(2,1)S(1)}, bf16[64,512]{1,0:T(8,128)(2,1)S(1)}, u32[]{:S(2)}, u32[]{:S(2)}) collective-permute-start(bf16[64,512]{1,0:T(8,128)(2,1)S(1)} %get-tuple-element.11), channel_id=1, source_target_pairs={{0,1},{1,2},{2,3},{3,0},{4,5},{5,6},{6,7},{7,4},{8,9},{9,10},{10,1... | collective-permute-start | bytes 196616 | tf_op jit(solution)/shard_map/ppermute | solution.py:96
  33.8 5.0 %collective-permute-start.7 = (bf16[64,512]{1,0:T(8,128)(2,1)S(1)}, bf16[64,512]{1,0:T(8,128)(2,1)S(1)}, u32[]{:S(2)}, u32[]{:S(2)}) collective-permute-start(bf16[64,512]{1,0:T(8,128)(2,1)S(1)} %get-tuple-element.13), channel_id=1, source_target_pairs={{0,2},{1,3},{2,0},{3,1},{4,6},{5,7},{6,4},{7,5},{8,10},{9,11},{10,... | collective-permute-start | bytes 196616 | tf_op jit(solution)/shard_map/ppermute | solution.py:96
  34.7 4.0 %collective-permute-start.8 = (bf16[64,512]{1,0:T(8,128)(2,1)S(1)}, bf16[64,512]{1,0:T(8,128)(2,1)S(1)}, u32[]{:S(2)}, u32[]{:S(2)}) collective-permute-start(bf16[64,512]{1,0:T(8,128)(2,1)S(1)} %get-tuple-element.12), channel_id=1, source_target_pairs={{0,3},{1,0},{2,1},{3,2},{4,7},{5,4},{6,5},{7,6},{8,11},{9,8},{10,9... | collective-permute-start | bytes 196616 | tf_op jit(solution)/shard_map/ppermute | solution.py:96
  36.1 14.7 %copy-start = (f32[2,16,64,64]{3,2,1,0:T(8,128)S(1)}, f32[2,16,64,64]{3,2,1,0:T(8,128)}, u32[]{:S(2)}) copy-start(f32[2,16,64,64]{3,2,1,0:T(8,128)} %param.5) | copy-start | bytes 1572868
  40.1 4.6 %collective-permute-start.9 = (bf16[64,2,64]{2,0,1:T(8,128)(2,1)S(1)}, bf16[64,2,64]{2,0,1:T(8,128)(2,1)S(1)}, u32[]{:S(2)}, u32[]{:S(2)}) collective-permute-start(bf16[64,2,64]{2,0,1:T(8,128)(2,1)S(1)} %bitcast.101), channel_id=1, source_target_pairs={{0,12},{4,0},{8,4},{12,8},{1,13},{5,1},{9,5},{13,9},{2,14},{6,2},{... | collective-permute-start | bytes 49160 | tf_op jit(solution)/shard_map/ppermute | solution.py:84
  42.9 4.9 %collective-permute-start.10 = (bf16[64,2,64]{2,0,1:T(8,128)(2,1)S(1)}, bf16[64,2,64]{2,0,1:T(8,128)(2,1)S(1)}, u32[]{:S(2)}, u32[]{:S(2)}) collective-permute-start(bf16[64,2,64]{2,0,1:T(8,128)(2,1)S(1)} %bitcast.102), channel_id=1, source_target_pairs={{0,8},{4,12},{8,0},{12,4},{1,9},{5,13},{9,1},{13,5},{2,10},{6,14},... | collective-permute-start | bytes 49160 | tf_op jit(solution)/shard_map/ppermute | solution.py:84
  44.1 5.8 %collective-permute-start.11 = (bf16[64,2,64]{2,0,1:T(8,128)(2,1)S(1)}, bf16[64,2,64]{2,0,1:T(8,128)(2,1)S(1)}, u32[]{:S(2)}, u32[]{:S(2)}) collective-permute-start(bf16[64,2,64]{2,0,1:T(8,128)(2,1)S(1)} %bitcast.103), channel_id=1, source_target_pairs={{0,4},{4,8},{8,12},{12,0},{1,5},{5,9},{9,13},{13,1},{2,6},{6,10},{... | collective-permute-start | bytes 49160 | tf_op jit(solution)/shard_map/ppermute | solution.py:84

commit v5 on v4

--- a/solution.py
+++ b/solution.py
@@ -54,12 +54,23 @@
 PERMUTE_LIMIT = 8
 
 
-def shifted(count, step):
+def paired(count, step):
+    if count & (count - 1) == 0:
+        return [(source, source ^ step) for source in range(count)]
     return [(source, (source + step) % count) for source in range(count)]
 
 
+def partner(count, me, step):
+    if count & (count - 1) == 0:
+        return me ^ step
+    return (me + step) % count
+
+
 def by_sender(pieces, count, me):
-    ring = jnp.stack([pieces[0]] + pieces[1:][::-1])
+    stacked = jnp.stack(pieces)
+    if count & (count - 1) == 0:
+        return jnp.take(stacked, me ^ jnp.arange(count), axis=0)
+    ring = jnp.concatenate([stacked[:1], stacked[1:][::-1]], axis=0)
     doubled = jnp.concatenate([ring, ring], axis=0)
     return lax.dynamic_slice_in_dim(doubled, (count - me) % count, count, 0)
 
@@ -69,7 +80,7 @@
     if count > PERMUTE_LIMIT:
         return lax.all_gather(value, axis)
     me = lax.axis_index(axis)
-    pieces = [value] + [lax.ppermute(value, axis, shifted(count, step)) for step in range(1, count)]
+    pieces = [value] + [lax.ppermute(value, axis, paired(count, step)) for step in range(1, count)]
     return by_sender(pieces, count, me)
 
 
@@ -80,8 +91,8 @@
     me = lax.axis_index(axis)
     pieces = [lax.dynamic_index_in_dim(blocks, me, 0, keepdims=False)]
     for step in range(1, count):
-        outgoing = lax.dynamic_index_in_dim(blocks, (me + step) % count, 0, keepdims=False)
-        pieces.append(lax.ppermute(outgoing, axis, shifted(count, step)))
+        outgoing = lax.dynamic_index_in_dim(blocks, partner(count, me, step), 0, keepdims=False)
+        pieces.append(lax.ppermute(outgoing, axis, paired(count, step)))
     return by_sender(pieces, count, me)
 
 
@@ -92,8 +103,8 @@
     me = lax.axis_index(axis)
     total = lax.dynamic_index_in_dim(blocks, me, 0, keepdims=False)
     for step in range(1, count):
-        outgoing = lax.dynamic_index_in_dim(blocks, (me + step) % count, 0, keepdims=False)
-        total = total + lax.ppermute(outgoing.astype(jnp.bfloat16), axis, shifted(count, step)).astype(jnp.float32)
+        outgoing = lax.dynamic_index_in_dim(blocks, partner(count, me, step), 0, keepdims=False)
+        total = total + lax.ppermute(outgoing.astype(jnp.bfloat16), axis, paired(count, step)).astype(jnp.float32)
     return total
 
 

time: 52.2 us -> 54.7 us (1.048)
  other arithmetic: 6.96 us -> 8.04 us
  local copies, waits for them, and re-layouts: 6.19 us -> 7.11 us
  waiting for transfers between devices: 12.5 us -> 13.2 us
    gather x0 -> x3, local copies, waits for them, and re-layouts: none -> 1.71 us  [by_sender(): return jnp.take(stacked, me ^ jnp.arange(count), axis=0)]
    select_n x0 -> x3, other arithmetic: none -> 0.83 us  [by_sender(): return jnp.take(stacked, me ^ jnp.arange(count), axis=0)]
    dynamic_slice x1 -> x0, local copies, waits for them, and re-layouts: 0.74 us -> none  [by_sender(): return lax.dynamic_slice_in_dim(doubled, (count - me) % count, count, 0)]
    ppermute x12, waiting for transfers between devices: 12.5 us -> 13.2 us  [the longest x6 5.48 us: exchange_blocks(): pieces.append(lax.ppermute(outgoing, axis, paired(count, step)))]
  transfers between devices with their start and end apart: 12 -> 12, of which waited for: 9 -> 6; matrix products, arithmetic and copies ran while one was open for 9% -> 9% of each run, Pallas kernels for 0% -> 0%
where the time goes in v5:
time: 54.7 us; the launch traced here: 54.5 us
  starting transfers between devices  14.2 us (26%)
  waiting for transfers between devices  13.2 us (24%)
  Pallas kernels  11.6 us (21%)
  other arithmetic  8.04 us (15%)
  local copies, waits for them, and re-layouts  7.11 us (13%)
    pallas_call x1, Pallas kernels, coil_chain(): pl.pallas_call(coil_chain_kernel, out_shape=jax.ShapeDtypeStruct((rows, w...  11.6 us
    ppermute x6, starting transfers between devices, exchange_blocks(): pieces.append(lax.ppermute(outgoing, axis, paired(count, step)))  10.3 us
    ppermute x6, waiting for transfers between devices, exchange_blocks(): pieces.append(lax.ppermute(outgoing, axis, paired(count, step)))  5.48 us
    ppermute x3, waiting for transfers between devices, reduce_blocks(): lax.ppermute(outgoing.astype(jnp.bfloat16), axis, paired(count, step))  4.03 us
    ppermute x3, waiting for transfers between devices, gather_blocks(): lax.ppermute(value, axis, paired(count, step))  3.73 us
    ppermute x3, starting transfers between devices, gather_blocks(): lax.ppermute(value, axis, paired(count, step))  1.93 us
    ppermute x3, starting transfers between devices, reduce_blocks(): lax.ppermute(outgoing.astype(jnp.bfloat16), axis, paired(count, step))  1.93 us
    gather x3, local copies, waits for them, and re-layouts, by_sender(): return jnp.take(stacked, me ^ jnp.arange(count), axis=0)  1.71 us
  transfers between devices with their start and end apart: 12, of which 6 were waited for; matrix products, arithmetic and copies ran while one was open for 9% of the time, Pallas kernels for 0%

profile of v5, /device:TPU:0, one launch (start us, length us, event | category | flops | bytes accessed | tf_op | source)
XLA Modules:
  0.0 54.5 jit_solution(17355669054622229666)
XLA Ops:
  0.0 0.7 %slice_bitcast_fusion.5 = (f32[4,16]{1,0:T(4,128)S(1)}, f32[4,16]{1,0:T(4,128)S(1)}) fusion(f32[2,4,16]{2,1,0:T(4,128)} %param.8), kind=kLoop, calls=%fused_computation.79 | loop fusion | bytes 1024 | tf_op jit(solution)/shard_map/mul | solution.py:233
  0.7 1.3 %slice_bitcast_fusion.1 = (f32[16,64,64]{2,1,0:T(8,128)S(1)}, f32[16,64,64]{2,1,0:T(8,128)S(1)}) fusion(f32[2,16,64,64]{3,2,1,0:T(8,128)} %param.7), kind=kLoop, calls=%fused_computation.16 | loop fusion | bytes 1048576 | tf_op jit(solution)/shard_map/mul | solution.py:211
  2.0 0.9 %add_reduce_fusion.1 = (bf16[4,64,64]{2,1,0:T(8,128)(2,1)S(1)}, bf16[4,64,64]{2,1,0:T(8,128)(2,1)S(1)}) fusion(f32[16,64,64]{2,1,0:T(8,128)S(1)} %get-tuple-element.11, f32[4,16]{1,0:T(4,128)S(1)} %get-tuple-element.28, f32[16,64,64]{2,1,0:T(8,128)S(1)} %get-tuple-element.10, f32[4,16]{1,0:T(4,128)S(1)} %get-tuple-element.27), kind=kLoop, calls=%fused_computation.5 | loop fusion | flops 2064384 | bytes 590336 | tf_op jit(solution)/shard_map/reduce_sum | solution.py:213
  3.0 5.1 %collective-permute-start.2 = (bf16[64,2,64]{2,0,1:T(8,128)(2,1)S(1)}, bf16[64,2,64]{2,0,1:T(8,128)(2,1)S(1)}, u32[]{:S(2)}, u32[]{:S(2)}) collective-permute-start(bf16[64,2,64]{2,0,1:T(8,128)(2,1)S(1)} %get-tuple-element.26), channel_id=1, source_target_pairs={{0,12},{4,8},{8,4},{12,0},{1,13},{5,9},{9,5},{13,1},{2,14},{6,10},... | collective-permute-start | bytes 49160 | tf_op jit(solution)/shard_map/ppermute | solution.py:95
  8.7 1.1 %multiply_convert_fusion = (bf16[256,256]{1,0:T(8,128)(2,1)S(1)}, bf16[256,256]{1,0:T(8,128)(2,1)S(1)}) fusion(), kind=kLoop, calls=%fused_computation.25 | loop fusion | flops 1245184 | bytes 262144 | tf_op jit(solution)/shard_map/convert_element_type | solution.py:18
  9.9 1.0 %fusion.15 = bf16[256,256]{1,0:T(8,128)(2,1)S(1)} fusion(), kind=kLoop, calls=%fused_computation.56 | loop fusion | flops 1310720 | bytes 131072 | tf_op jit(solution)/shard_map/neg | solution.py:194
  10.9 1.1 %fusion.2 = (bf16[512,512]{1,0:T(8,128)(2,1)}, bf16[512,512]{1,0:T(8,128)(2,1)}) fusion(bf16[256,256]{1,0:T(8,128)(2,1)S(1)} %get-tuple-element.32.table_re_ref, bf16[256,256]{1,0:T(8,128)(2,1)S(1)} %get-tuple-element.31.table_im_ref, bf16[256,256]{1,0:T(8,128)(2,1)S(1)} %fusion.15), kind=kLoop, calls=%fused_computation.14 | loop fusion | flops 3670016 | bytes 1441792 | tf_op jit(solution)/shard_map/concatenate | solution.py:198
  12.1 1.3 %copy.18.sampled_ref = f32[8,256,1]{2,1,0:T(8,128)} copy(f32[8,256,1]{1,0,2:T(8,128)S(1)} %convert_bitcast_fusion.2) | data formatting | bytes 16384 | tf_op jit(solution)/shard_map/convert_element_type | solution.py:222
  14.5 1.7 %collective-permute-start.4 = (bf16[64,512]{1,0:T(8,128)(2,1)S(1)}, bf16[64,512]{1,0:T(8,128)(2,1)S(1)}, u32[]{:S(2)}, u32[]{:S(2)}) collective-permute-start(bf16[64,512]{1,0:T(8,128)(2,1)S(1)} %reshape.62), channel_id=1, source_target_pairs={{0,2},{1,3},{2,0},{3,1},{4,6},{5,7},{6,4},{7,5},{8,10},{9,11},{10,... | collective-permute-start | bytes 196616 | tf_op jit(solution)/shard_map/ppermute | solution.py:83
  16.5 2.5 %collective-permute-done.4 = bf16[64,512]{1,0:T(8,128)(2,1)S(1)} collective-permute-done((bf16[64,512]{1,0:T(8,128)(2,1)S(1)}, bf16[64,512]{1,0:T(8,128)(2,1)S(1)}, u32[]{:S(2)}, u32[]{:S(2)}) %collective-permute-start.4) | collective-permute-done | bytes 65568 | tf_op jit(solution)/shard_map/ppermute | solution.py:83
  19.0 1.2 %collective-permute-done.5 = bf16[64,512]{1,0:T(8,128)(2,1)S(1)} collective-permute-done((bf16[64,512]{1,0:T(8,128)(2,1)S(1)}, bf16[64,512]{1,0:T(8,128)(2,1)S(1)}, u32[]{:S(2)}, u32[]{:S(2)}) %collective-permute-start.5) | collective-permute-done | bytes 65568 | tf_op jit(solution)/shard_map/ppermute | solution.py:83
  20.9 0.8 %bitcast_select_fusion.image_ref = bf16[256,512]{1,0:T(8,128)(2,1)} fusion(bf16[4,64,512]{2,1,0:T(8,128)(2,1)S(1)} %gather_fusion, pred[256]{0:T(512)(128)(4,1)S(1)} %broadcast_in_dim.29), kind=kLoop, calls=%fused_computation.24 | loop fusion | flops 131072 | bytes 524544 | tf_op jit(solution)/shard_map/jit(_take)/select_n | solution.py:72
  21.7 11.6 %shard_map.55 = f32[256,512]{1,0:T(8,128)} custom-call(bf16[256,512]{1,0:T(8,128)(2,1)} %bitcast_select_fusion.image_ref, bf16[8,256,512]{2,1,0:T(8,128)(2,1)} %sens_ref.1, bf16[8,256,512]{2,1,0:T(8,128)(2,1)} %bitcast.90, f32[8,256,1]{2,1,0:T(8,128)} %copy.18.sampled_ref, bf16[512,512]{1,0:T(8,128)(2,1)} %get-tuple-element.16.forward_ref, ...), custom_call_target="tpu_custom_call" | custom-call | flops 4294967296 | bytes 4718592 | tf_op jit(solution)/shard_map/pallas_call | solution.py:163
  33.4 1.1 %fusion.12 = (bf16[64,512]{1,0:T(8,128)(2,1)S(1)}, bf16[64,512]{1,0:T(8,128)(2,1)S(1)}, bf16[64,512]{1,0:T(8,128)(2,1)S(1)}) fusion(f32[4,64,512]{2,1,0:T(8,128)} %bitcast.75, s32[]{:T(128)S(6)} %select_n.93, s32[]{:T(128)S(6)} %select_n.95, s32[]{:T(128)S(6)} %select_n.94), kind=kLoop, calls=%fused_computation.51 | loop fusion | bytes 393228 | tf_op jit(solution)/shard_map/convert_element_type | solution.py:107
  34.7 1.5 %collective-permute-start.7 = (bf16[64,512]{1,0:T(8,128)(2,1)S(1)}, bf16[64,512]{1,0:T(8,128)(2,1)S(1)}, u32[]{:S(2)}, u32[]{:S(2)}) collective-permute-start(bf16[64,512]{1,0:T(8,128)(2,1)S(1)} %get-tuple-element.14), channel_id=1, source_target_pairs={{0,2},{1,3},{2,0},{3,1},{4,6},{5,7},{6,4},{7,5},{8,10},{9,11},{10,... | collective-permute-start | bytes 196616 | tf_op jit(solution)/shard_map/ppermute | solution.py:107
  36.4 2.6 %collective-permute-done.7 = bf16[64,512]{1,0:T(8,128)(2,1)S(1)} collective-permute-done((bf16[64,512]{1,0:T(8,128)(2,1)S(1)}, bf16[64,512]{1,0:T(8,128)(2,1)S(1)}, u32[]{:S(2)}, u32[]{:S(2)}) %collective-permute-start.7) | collective-permute-done | bytes 65568 | tf_op jit(solution)/shard_map/ppermute | solution.py:107
  39.0 1.4 %collective-permute-done.8 = bf16[64,512]{1,0:T(8,128)(2,1)S(1)} collective-permute-done((bf16[64,512]{1,0:T(8,128)(2,1)S(1)}, bf16[64,512]{1,0:T(8,128)(2,1)S(1)}, u32[]{:S(2)}, u32[]{:S(2)}) %collective-permute-start.8) | collective-permute-done | bytes 65568 | tf_op jit(solution)/shard_map/ppermute | solution.py:107
  40.4 0.9 %fusion.11 = bf16[64,512]{1,0:T(8,128)(2,1)S(1)} fusion(bf16[64,512]{1,0:T(8,128)(2,1)S(1)} %collective-permute-done.8, bf16[64,512]{1,0:T(8,128)(2,1)S(1)} %collective-permute-done.7, bf16[64,512]{1,0:T(8,128)(2,1)S(1)} %collective-permute-done.6, f32[4,64,512]{2,1,0:T(8,128)} %bitcast.76, s32[]{:T(128)S(6)} %select_n.92), kind=kLoop, calls=%fused_computation.45 | loop fusion | flops 229376 | bytes 393220 | tf_op jit(solution)/shard_map/convert_element_type | solution.py:228
  41.8 1.3 %collective-permute-start.9 = (bf16[64,2,64]{2,0,1:T(8,128)(2,1)S(1)}, bf16[64,2,64]{2,0,1:T(8,128)(2,1)S(1)}, u32[]{:S(2)}, u32[]{:S(2)}) collective-permute-start(bf16[64,2,64]{2,0,1:T(8,128)(2,1)S(1)} %bitcast.81), channel_id=1, source_target_pairs={{0,4},{4,0},{8,12},{12,8},{1,5},{5,1},{9,13},{13,9},{2,6},{6,2},{1... | collective-permute-start | bytes 49160 | tf_op jit(solution)/shard_map/ppermute | solution.py:95
  43.1 2.9 %collective-permute-start.10 = (bf16[64,2,64]{2,0,1:T(8,128)(2,1)S(1)}, bf16[64,2,64]{2,0,1:T(8,128)(2,1)S(1)}, u32[]{:S(2)}, u32[]{:S(2)}) collective-permute-start(bf16[64,2,64]{2,0,1:T(8,128)(2,1)S(1)} %bitcast.82), channel_id=1, source_target_pairs={{0,8},{4,12},{8,0},{12,4},{1,9},{5,13},{9,1},{13,5},{2,10},{6,14},... | collective-permute-start | bytes 49160 | tf_op jit(solution)/shard_map/ppermute | solution.py:95
  46.4 2.0 %collective-permute-done.10 = bf16[64,2,64]{2,0,1:T(8,128)(2,1)S(1)} collective-permute-done((bf16[64,2,64]{2,0,1:T(8,128)(2,1)S(1)}, bf16[64,2,64]{2,0,1:T(8,128)(2,1)S(1)}, u32[]{:S(2)}, u32[]{:S(2)}) %collective-permute-start.10) | collective-permute-done | bytes 16416 | tf_op jit(solution)/shard_map/ppermute | solution.py:95
  48.4 3.4 %collective-permute-done.11 = bf16[64,2,64]{2,0,1:T(8,128)(2,1)S(1)} collective-permute-done((bf16[64,2,64]{2,0,1:T(8,128)(2,1)S(1)}, bf16[64,2,64]{2,0,1:T(8,128)(2,1)S(1)}, u32[]{:S(2)}, u32[]{:S(2)}) %collective-permute-start.11) | collective-permute-done | bytes 16416 | tf_op jit(solution)/shard_map/ppermute | solution.py:95
  52.6 0.7 %add_reduce_fusion = (f32[16,64,64]{2,1,0:T(8,128)S(1)}, f32[16,64,64]{2,1,0:T(8,128)S(1)}) fusion(f32[4,64,64]{2,1,0:T(8,128)S(1)} %get-tuple-element.18, f32[4,64,64]{2,1,0:T(8,128)S(1)} %get-tuple-element.17, f32[4,16]{1,0:T(4,128)S(1)} %get-tuple-element.28, f32[4,16]{1,0:T(4,128)S(1)} %get-tuple-element.27), kind=kLoop, calls=%fused_computation.4 | loop fusion | flops 1966080 | bytes 655872 | tf_op jit(solution)/shard_map/reduce_sum | solution.py:232
  53.3 1.1 %fusion = f32[2,16,64,64]{3,2,1,0:T(8,128)} fusion(f32[2,16,64,64]{3,2,1,0:T(8,128)S(1)} %copy-done, f32[1,16,64,64]{3,2,1,0:T(8,128)S(1)} %bitcast.72, f32[1,16,64,64]{3,2,1,0:T(8,128)S(1)} %bitcast.71), kind=kLoop, calls=%fused_computation.8 | loop fusion | flops 393216 | bytes 1572864 | tf_op jit(solution)/shard_map/sub | solution.py:238
  (48 shorter events, 4.7 us)
Async XLA Ops:
  0.0 10.9 %copy-start.3 = (s32[1,8,256]{2,1,0:T(8,128)S(1)}, s32[1,8,256]{2,1,0:T(8,128)}, u32[]{:S(2)}) copy-start(s32[1,8,256]{2,1,0:T(8,128)} %param.11) | copy-start | bytes 24580
  3.0 10.5 %collective-permute-start.2 = (bf16[64,2,64]{2,0,1:T(8,128)(2,1)S(1)}, bf16[64,2,64]{2,0,1:T(8,128)(2,1)S(1)}, u32[]{:S(2)}, u32[]{:S(2)}) collective-permute-start(bf16[64,2,64]{2,0,1:T(8,128)(2,1)S(1)} %get-tuple-element.26), channel_id=1, source_target_pairs={{0,12},{4,8},{8,4},{12,0},{1,13},{5,9},{9,5},{13,1},{2,14},{6,10},... | collective-permute-start | bytes 49160 | tf_op jit(solution)/shard_map/ppermute | solution.py:95
  8.1 5.4 %collective-permute-start = (bf16[64,2,64]{2,0,1:T(8,128)(2,1)S(1)}, bf16[64,2,64]{2,0,1:T(8,128)(2,1)S(1)}, u32[]{:S(2)}, u32[]{:S(2)}) collective-permute-start(bf16[64,2,64]{2,0,1:T(8,128)(2,1)S(1)} %get-tuple-element.24), channel_id=1, source_target_pairs={{0,4},{4,0},{8,12},{12,8},{1,5},{5,1},{9,13},{13,9},{2,6},{6,2},{1... | collective-permute-start | bytes 49160 | tf_op jit(solution)/shard_map/ppermute | solution.py:95
  8.1 5.4 %collective-permute-start.1 = (bf16[64,2,64]{2,0,1:T(8,128)(2,1)S(1)}, bf16[64,2,64]{2,0,1:T(8,128)(2,1)S(1)}, u32[]{:S(2)}, u32[]{:S(2)}) collective-permute-start(bf16[64,2,64]{2,0,1:T(8,128)(2,1)S(1)} %get-tuple-element.25), channel_id=1, source_target_pairs={{0,8},{4,12},{8,0},{12,4},{1,9},{5,13},{9,1},{13,5},{2,10},{6,14},... | collective-permute-start | bytes 49160 | tf_op jit(solution)/shard_map/ppermute | solution.py:95
  9.8 10.5 %copy-start.1 = (bf16[256,256]{1,0:T(8,128)(2,1)}, bf16[256,256]{1,0:T(8,128)(2,1)S(1)}, u32[]{:S(2)}) copy-start(bf16[256,256]{1,0:T(8,128)(2,1)S(1)} %get-tuple-element.31.table_im_ref) | copy-start | bytes 393220
  9.8 10.5 %copy-start.2 = (bf16[256,256]{1,0:T(8,128)(2,1)}, bf16[256,256]{1,0:T(8,128)(2,1)S(1)}, u32[]{:S(2)}) copy-start(bf16[256,256]{1,0:T(8,128)(2,1)S(1)} %get-tuple-element.32.table_re_ref) | copy-start | bytes 393220
  14.4 2.1 %collective-permute-start.3 = (bf16[64,512]{1,0:T(8,128)(2,1)S(1)}, bf16[64,512]{1,0:T(8,128)(2,1)S(1)}, u32[]{:S(2)}, u32[]{:S(2)}) collective-permute-start(bf16[64,512]{1,0:T(8,128)(2,1)S(1)} %reshape.62), channel_id=1, source_target_pairs={{0,1},{1,0},{2,3},{3,2},{4,5},{5,4},{6,7},{7,6},{8,9},{9,8},{10,11... | collective-permute-start | bytes 196616 | tf_op jit(solution)/shard_map/ppermute | solution.py:83
  14.5 4.5 %collective-permute-start.4 = (bf16[64,512]{1,0:T(8,128)(2,1)S(1)}, bf16[64,512]{1,0:T(8,128)(2,1)S(1)}, u32[]{:S(2)}, u32[]{:S(2)}) collective-permute-start(bf16[64,512]{1,0:T(8,128)(2,1)S(1)} %reshape.62), channel_id=1, source_target_pairs={{0,2},{1,3},{2,0},{3,1},{4,6},{5,7},{6,4},{7,5},{8,10},{9,11},{10,... | collective-permute-start | bytes 196616 | tf_op jit(solution)/shard_map/ppermute | solution.py:83
  16.2 4.0 %collective-permute-start.5 = (bf16[64,512]{1,0:T(8,128)(2,1)S(1)}, bf16[64,512]{1,0:T(8,128)(2,1)S(1)}, u32[]{:S(2)}, u32[]{:S(2)}) collective-permute-start(bf16[64,512]{1,0:T(8,128)(2,1)S(1)} %reshape.62), channel_id=1, source_target_pairs={{0,3},{1,2},{2,1},{3,0},{4,7},{5,6},{6,5},{7,4},{8,11},{9,10},{10,... | collective-permute-start | bytes 196616 | tf_op jit(solution)/shard_map/ppermute | solution.py:83
  34.4 1.9 %collective-permute-start.6 = (bf16[64,512]{1,0:T(8,128)(2,1)S(1)}, bf16[64,512]{1,0:T(8,128)(2,1)S(1)}, u32[]{:S(2)}, u32[]{:S(2)}) collective-permute-start(bf16[64,512]{1,0:T(8,128)(2,1)S(1)} %get-tuple-element.12), channel_id=1, source_target_pairs={{0,1},{1,0},{2,3},{3,2},{4,5},{5,4},{6,7},{7,6},{8,9},{9,8},{10,11... | collective-permute-start | bytes 196616 | tf_op jit(solution)/shard_map/ppermute | solution.py:107
  34.7 4.3 %collective-permute-start.7 = (bf16[64,512]{1,0:T(8,128)(2,1)S(1)}, bf16[64,512]{1,0:T(8,128)(2,1)S(1)}, u32[]{:S(2)}, u32[]{:S(2)}) collective-permute-start(bf16[64,512]{1,0:T(8,128)(2,1)S(1)} %get-tuple-element.14), channel_id=1, source_target_pairs={{0,2},{1,3},{2,0},{3,1},{4,6},{5,7},{6,4},{7,5},{8,10},{9,11},{10,... | collective-permute-start | bytes 196616 | tf_op jit(solution)/shard_map/ppermute | solution.py:107
  36.1 4.3 %collective-permute-start.8 = (bf16[64,512]{1,0:T(8,128)(2,1)S(1)}, bf16[64,512]{1,0:T(8,128)(2,1)S(1)}, u32[]{:S(2)}, u32[]{:S(2)}) collective-permute-start(bf16[64,512]{1,0:T(8,128)(2,1)S(1)} %get-tuple-element.13), channel_id=1, source_target_pairs={{0,3},{1,2},{2,1},{3,0},{4,7},{5,6},{6,5},{7,4},{8,11},{9,10},{10,... | collective-permute-start | bytes 196616 | tf_op jit(solution)/shard_map/ppermute | solution.py:107
  36.3 17.0 %copy-start = (f32[2,16,64,64]{3,2,1,0:T(8,128)S(1)}, f32[2,16,64,64]{3,2,1,0:T(8,128)}, u32[]{:S(2)}) copy-start(f32[2,16,64,64]{3,2,1,0:T(8,128)} %param.7) | copy-start | bytes 1572868
  41.8 4.6 %collective-permute-start.9 = (bf16[64,2,64]{2,0,1:T(8,128)(2,1)S(1)}, bf16[64,2,64]{2,0,1:T(8,128)(2,1)S(1)}, u32[]{:S(2)}, u32[]{:S(2)}) collective-permute-start(bf16[64,2,64]{2,0,1:T(8,128)(2,1)S(1)} %bitcast.81), channel_id=1, source_target_pairs={{0,4},{4,0},{8,12},{12,8},{1,5},{5,1},{9,13},{13,9},{2,6},{6,2},{1... | collective-permute-start | bytes 49160 | tf_op jit(solution)/shard_map/ppermute | solution.py:95
  43.1 5.3 %collective-permute-start.10 = (bf16[64,2,64]{2,0,1:T(8,128)(2,1)S(1)}, bf16[64,2,64]{2,0,1:T(8,128)(2,1)S(1)}, u32[]{:S(2)}, u32[]{:S(2)}) collective-permute-start(bf16[64,2,64]{2,0,1:T(8,128)(2,1)S(1)} %bitcast.82), channel_id=1, source_target_pairs={{0,8},{4,12},{8,0},{12,4},{1,9},{5,13},{9,1},{13,5},{2,10},{6,14},... | collective-permute-start | bytes 49160 | tf_op jit(solution)/shard_map/ppermute | solution.py:95
  46.1 5.8 %collective-permute-start.11 = (bf16[64,2,64]{2,0,1:T(8,128)(2,1)S(1)}, bf16[64,2,64]{2,0,1:T(8,128)(2,1)S(1)}, u32[]{:S(2)}, u32[]{:S(2)}) collective-permute-start(bf16[64,2,64]{2,0,1:T(8,128)(2,1)S(1)} %bitcast.83), channel_id=1, source_target_pairs={{0,12},{4,8},{8,4},{12,0},{1,13},{5,9},{9,5},{13,1},{2,14},{6,10},... | collective-permute-start | bytes 49160 | tf_op jit(solution)/shard_map/ppermute | solution.py:95

commit v6 on v4

--- a/solution.py
+++ b/solution.py
@@ -1,6 +1,8 @@
 import math
 
 import jax
+import ml_dtypes
+import numpy as np
 import jax.numpy as jnp
 from jax import lax
 from jax.experimental import pallas as pl
@@ -9,14 +11,13 @@
 
 
 def dft_parts(length):
-    index = jnp.arange(length, dtype=jnp.int32)
-    phase = index[:, None] * index[None, :] % length
-    angle = 2.0 * math.pi / length * phase.astype(jnp.float32)
-    scale = 1.0 / math.sqrt(length)
-    return (
-        (jnp.cos(angle) * scale).astype(jnp.bfloat16),
-        (-jnp.sin(angle) * scale).astype(jnp.bfloat16),
-    )
+    index = np.arange(length, dtype=np.int64)
+    phase = (index[:, None] * index[None, :]) % length
+    angle = np.float32(2.0 * math.pi / length) * phase.astype(np.float32)
+    scale = np.float32(1.0 / math.sqrt(length))
+    real = (np.cos(angle.astype(np.float64)).astype(np.float32) * scale).astype(ml_dtypes.bfloat16)
+    imag = (-np.sin(angle.astype(np.float64)).astype(np.float32) * scale).astype(ml_dtypes.bfloat16)
+    return real, imag
 
 
 def rotate_plus(values, half_width):
@@ -105,9 +106,28 @@
     return jnp.concatenate([high, -low], axis=1)
 
 
-def coil_chain_kernel(image_ref, sens_ref, measured_ref, sampled_ref, forward_ref, adjoint_ref,
-                      table_re_ref, table_im_ref, out_ref):
+def coil_chain_kernel(*refs):
+    groups = len(refs) - 12
+    pieces = refs[:groups]
+    place_ref, sens_ref, measured_ref, sampled_ref, forward_ref, adjoint_ref, table_re_ref, table_im_ref = refs[
+        groups:groups + 8
+    ]
+    own_ref, send_ref = refs[groups + 8:groups + 10]
+    image_ref, total_ref = refs[groups + 10:]
+    rows = pieces[0].shape[0]
     half_width = image_ref.shape[1] // 2
+    me = place_ref[0]
+    step = pl.program_id(0)
+
+    @pl.when(step == 0)
+    def _():
+        for block in range(groups):
+            source = (me - block + groups) % groups
+            value = pieces[0][...]
+            for other in range(1, groups):
+                value = jnp.where(source == other, pieces[other][...], value)
+            image_ref[block * rows:(block + 1) * rows, :] = value
+
     sens = sens_ref[0].astype(jnp.float32)
     sens_re = sens[:, :half_width]
     sens_im = sens[:, half_width:]
@@ -123,10 +143,11 @@
     kspace = jnp.dot(table_re, half_k, preferred_element_type=jnp.float32) + jnp.dot(
         table_im, swap_halves(half_k, half_width, True), preferred_element_type=jnp.float32
     )
-    residual = (sampled_ref[0] * (kspace - measured_ref[0].astype(jnp.float32))).astype(jnp.bfloat16)
+    residual = (kspace - measured_ref[0].astype(jnp.float32)).astype(jnp.bfloat16)
+    sampled = sampled_ref[0].astype(jnp.bfloat16)
     back_half = (
-        jnp.dot(table_re, residual, preferred_element_type=jnp.float32)
-        + jnp.dot(table_im, swap_halves(residual, half_width, False), preferred_element_type=jnp.float32)
+        jnp.dot(table_re * sampled, residual, preferred_element_type=jnp.float32)
+        + jnp.dot(table_im * sampled, swap_halves(residual, half_width, False), preferred_element_type=jnp.float32)
     ).astype(jnp.bfloat16)
     coil_back = jnp.dot(back_half, adjoint_ref[...], preferred_element_type=jnp.float32)
     back_re = coil_back[:, :half_width]
@@ -135,40 +156,58 @@
         [sens_re * back_re + sens_im * back_im, sens_re * back_im - sens_im * back_re], axis=1
     )
 
-    @pl.when(pl.program_id(0) == 0)
-    def _():
-        out_ref[...] = term
-
-    @pl.when(pl.program_id(0) > 0)
-    def _():
-        out_ref[...] += term
-
-
-def coil_chain(image, sens, measured, sampled, forward_x, adjoint_x, table_y_re, table_y_im):
-    coils, rows, width = sens.shape
+    @pl.when(step == 0)
+    def _():
+        total_ref[...] = term
+
+    @pl.when(step > 0)
+    def _():
+        total_ref[...] += term
+
+    @pl.when(step == pl.num_programs(0) - 1)
+    def _():
+        start = pl.multiple_of(me * rows, rows)
+        own_ref[...] = total_ref[pl.ds(start, rows), :]
+        for shift in range(1, groups):
+            start = pl.multiple_of(((me + shift) % groups) * rows, rows)
+            send_ref[shift - 1] = total_ref[pl.ds(start, rows), :].astype(jnp.bfloat16)
+
+
+def coil_chain(pieces, place, sens, measured, sampled, forward_x, adjoint_x, table_y_re, table_y_im):
+    coils, height, width = sens.shape
+    groups = len(pieces)
+    rows = pieces[0].shape[0]
     whole = lambda c: (0, 0)
     per_coil = lambda c: (c, 0, 0)
-    flops = coils * 8 * rows * width * width
+    flops = coils * 8 * height * width * width
     return pl.pallas_call(
         coil_chain_kernel,
-        out_shape=jax.ShapeDtypeStruct((rows, width), jnp.float32),
+        out_shape=(
+            jax.ShapeDtypeStruct((rows, width), jnp.float32),
+            jax.ShapeDtypeStruct((groups - 1, rows, width), jnp.bfloat16),
+        ),
         grid=(coils,),
-        in_specs=[
-            pl.BlockSpec((rows, width), whole),
-            pl.BlockSpec((1, rows, width), per_coil),
-            pl.BlockSpec((1, rows, width), per_coil),
-            pl.BlockSpec((1, rows, 1), per_coil),
+        in_specs=[pl.BlockSpec((rows, width), whole)] * groups
+        + [
+            pl.BlockSpec(memory_space=pltpu.SMEM),
+            pl.BlockSpec((1, height, width), per_coil),
+            pl.BlockSpec((1, height, width), per_coil),
+            pl.BlockSpec((1, 1, height), per_coil),
             pl.BlockSpec((width, width), whole),
             pl.BlockSpec((width, width), whole),
-            pl.BlockSpec((rows, rows), whole),
-            pl.BlockSpec((rows, rows), whole),
+            pl.BlockSpec((height, height), whole),
+            pl.BlockSpec((height, height), whole),
         ],
-        out_specs=pl.BlockSpec((rows, width), whole),
+        out_specs=(
+            pl.BlockSpec((rows, width), whole),
+            pl.BlockSpec((groups - 1, rows, width), lambda c: (0, 0, 0)),
+        ),
+        scratch_shapes=[pltpu.VMEM((height, width), jnp.bfloat16), pltpu.VMEM((height, width), jnp.float32)],
         compiler_params=pltpu.CompilerParams(dimension_semantics=("arbitrary",)),
         cost_estimate=pl.CostEstimate(
-            flops=flops, transcendentals=0, bytes_accessed=2 * 2 * coils * rows * width + 4 * rows * width
+            flops=flops, transcendentals=0, bytes_accessed=2 * 2 * coils * height * width + 4 * height * width
         ),
-    )(image, sens, measured, sampled, forward_x, adjoint_x, table_y_re, table_y_im)
+    )(*pieces, place, sens, measured, sampled, forward_x, adjoint_x, table_y_re, table_y_im)
 
 
 def on_device(factors, temporal, maps, kdata, masks):
@@ -177,54 +216,44 @@
     rows_own = factors.shape[2]
     table_x_re, table_x_im = dft_parts(width_x)
     table_y_re, table_y_im = dft_parts(width_y)
-    forward_x = jnp.concatenate(
-        [
-            jnp.concatenate([table_x_re, table_x_im], axis=1),
-            jnp.concatenate([-table_x_im, table_x_re], axis=1),
-        ],
-        axis=0,
-    )
-    adjoint_x = jnp.concatenate(
-        [
-            jnp.concatenate([table_x_re, -table_x_im], axis=1),
-            jnp.concatenate([table_x_im, table_x_re], axis=1),
-        ],
-        axis=0,
-    )
-    wide_y = jnp.concatenate([table_y_re, table_y_im], axis=1)
-    left_re = factors[0]
-    left_im = factors[1]
+    forward_x = jnp.asarray(np.block([[table_x_re, table_x_im], [-table_x_im, table_x_re]]))
+    adjoint_x = jnp.asarray(np.block([[table_x_re, -table_x_im], [table_x_im, table_x_re]]))
+    table_y_re = jnp.asarray(table_y_re)
+    table_y_im = jnp.asarray(table_y_im)
     time_re = temporal[0]
     time_im = temporal[1]
-    image_re = jnp.sum(
-        time_re[:, :, None, None] * left_re[None] - time_im[:, :, None, None] * left_im[None], axis=1
-    )
-    image_im = jnp.sum(
-        time_im[:, :, None, None] * left_re[None] + time_re[:, :, None, None] * left_im[None], axis=1
-    )
-    images = jnp.stack([image_re, image_im], axis=2).astype(jnp.bfloat16)
+    mixing = jnp.stack(
+        [jnp.stack([time_re, -time_im], axis=1), jnp.stack([time_im, time_re], axis=1)], axis=1
+    )
+    images = jnp.sum(
+        mixing[:, :, :, :, None, None] * factors[None, None], axis=(2, 3)
+    ).astype(jnp.bfloat16)
     frames_here = images.shape[0]
     width_own = images.shape[3]
     pieces_x = exchange_blocks(images, "frame")
-    own_rows = jnp.transpose(pieces_x, (1, 2, 0, 3)).reshape(rows_own, 2 * width_x)
-    full_image = gather_blocks(own_rows, "coil").reshape(width_y, 2 * width_x)
-    sampled = masks[0].astype(jnp.float32)[:, :, None]
-    combined = coil_chain(full_image, maps, kdata[0], sampled, forward_x, adjoint_x, table_y_re, table_y_im)
-    groups = width_y // rows_own
-    own_share = reduce_blocks(combined.reshape(groups, rows_own, 2 * width_x), "coil")
+    own_rows = jnp.transpose(pieces_x, (2, 1, 0, 3)).reshape(rows_own, 2 * width_x)
+    groups = lax.axis_size("coil")
+    me_c = lax.axis_index("coil")
+    pieces = [own_rows] + [lax.ppermute(own_rows, "coil", shifted(groups, step)) for step in range(1, groups)]
+    sampled = masks[0].astype(jnp.float32)[:, None, :]
+    place = jnp.reshape(me_c, (1,)).astype(jnp.int32)
+    own_total, outgoing = coil_chain(
+        pieces, place, maps, kdata[0], sampled, forward_x, adjoint_x, table_y_re, table_y_im
+    )
+    own_share = own_total
+    for step in range(1, groups):
+        own_share = own_share + lax.ppermute(outgoing[step - 1], "coil", shifted(groups, step)).astype(jnp.float32)
     outgoing = jnp.transpose(
         own_share.reshape(rows_own, 2, frames_here, width_own), (2, 0, 1, 3)
     ).astype(jnp.bfloat16)
     returned = exchange_blocks(outgoing, "frame").astype(jnp.float32)
-    back_re = returned[:, :, 0]
-    back_im = returned[:, :, 1]
-    grad_re = jnp.sum(
-        time_re[:, :, None, None] * back_re[:, None] + time_im[:, :, None, None] * back_im[:, None], axis=0
-    )
-    grad_im = jnp.sum(
-        time_re[:, :, None, None] * back_im[:, None] - time_im[:, :, None, None] * back_re[:, None], axis=0
-    )
-    return factors - 0.5 * jnp.stack([grad_re, grad_im])
+    weights = jnp.stack(
+        [jnp.stack([time_re.T, time_im.T], axis=2), jnp.stack([-time_im.T, time_re.T], axis=2)], axis=0
+    )
+    gradient = jnp.sum(
+        weights[:, :, :, None, :, None] * returned[None, None], axis=(2, 4)
+    )
+    return factors - 0.5 * gradient
 
 
 def solution(mesh):

time: 52.2 us -> 52.3 us (level)
  local copies, waits for them, and re-layouts: 6.19 us -> 3.96 us
  starting transfers between devices: 14.3 us -> 15.3 us
  other arithmetic: 6.96 us -> 7.83 us
    convert_element_type x2 -> x0, local copies, waits for them, and re-layouts: 2.4 us -> none  [the longest x1 1.34 us: on_device(): sampled = masks[0].astype(jnp.float32)[:, :, None]]
    reduce_sum x2, other arithmetic: 1.63 us -> 3.65 us  [the longest x1 2.29 us: on_device(): jnp.sum(mixing[:, :, :, :, None, None] * factors[None, None], axis=(2, 3))]
    mul x3 -> x0, local copies, waits for them, and re-layouts: 2 us -> none  [the longest x1 1.27 us: on_device(): time_re[:, :, None, None] * left_re[None]]
    unnamed x27, local copies, waits for them, and re-layouts: 0.18 us -> 1.4 us
    concatenate x1 -> x0, other arithmetic: 1.06 us -> none  [on_device(): jnp.concatenate([jnp.concatenate([table_x_re, -table_x_im], axis=1), jnp....]
    squeeze x0 -> x2, local copies, waits for them, and re-layouts: none -> 1.03 us  [the longest x1 1 us: on_device(): outgoing[step - 1]]
    dynamic_slice x1 -> x0, local copies, waits for them, and re-layouts: 0.74 us -> none  [by_sender(): return lax.dynamic_slice_in_dim(doubled, (count - me) % count, count, 0)]
    ppermute x6, starting transfers between devices: 10.2 us -> 10.9 us  [exchange_blocks(): pieces.append(lax.ppermute(outgoing, axis, shifted(count, step)))]
  transfers between devices with their start and end apart: 12 -> 12, of which waited for: 9 -> 9; matrix products, arithmetic and copies ran while one was open for 9% -> 4% of each run, Pallas kernels for 0% -> 0%
where the time goes in v6:
time: 52.3 us; the launch traced here: 52 us
  starting transfers between devices  15.3 us (29%)
  waiting for transfers between devices  13 us (25%)
  Pallas kernels  11.7 us (22%)
  other arithmetic  7.83 us (15%)
  local copies, waits for them, and re-layouts  3.96 us (8%)
    pallas_call x1, Pallas kernels, coil_chain(): pl.pallas_call(coil_chain_kernel, out_shape=(jax.ShapeDtypeStruct((rows,...  11.7 us
    ppermute x6, starting transfers between devices, exchange_blocks(): pieces.append(lax.ppermute(outgoing, axis, shifted(count, step)))  10.9 us
    ppermute x6, waiting for transfers between devices, exchange_blocks(): pieces.append(lax.ppermute(outgoing, axis, shifted(count, step)))  5.63 us
    ppermute x3, waiting for transfers between devices, on_device(): lax.ppermute(own_rows, 'coil', shifted(groups, step))  4.1 us
    ppermute x3, waiting for transfers between devices, on_device(): lax.ppermute(outgoing[step - 1], 'coil', shifted(groups, step))  3.25 us
    ppermute x3, starting transfers between devices, on_device(): lax.ppermute(outgoing[step - 1], 'coil', shifted(groups, step))  2.66 us
    reduce_sum x1, other arithmetic, on_device(): jnp.sum(mixing[:, :, :, :, None, None] * factors[None, None], axis=(2, 3))  2.29 us
    ppermute x3, starting transfers between devices, on_device(): lax.ppermute(own_rows, 'coil', shifted(groups, step))  1.78 us
  transfers between devices with their start and end apart: 12, of which 9 were waited for; matrix products, arithmetic and copies ran while one was open for 4% of the time, Pallas kernels for 0%

profile of v6, /device:TPU:0, one launch (start us, length us, event | category | flops | bytes accessed | tf_op | source)
XLA Modules:
  0.0 52.0 jit_solution(8250289384335267416)
XLA Ops:
  0.0 0.7 %fusion.1 = f32[4,1,16]{2,0,1:T(4,128)S(1)} fusion(f32[2,4,16]{2,1,0:T(4,128)} %param.10), kind=kLoop, calls=%fused_computation.51 | loop fusion | flops 64 | bytes 512 | tf_op jit(solution)/shard_map/neg | solution.py:226
  0.7 0.7 %slice_bitcast_fusion.5 = (f32[16,4,1]{0,1,2:T(4,128)S(1)}, f32[4,1,16]{2,0,1:T(4,128)S(1)}, f32[4,1,16]{2,0,1:T(4,128)S(1)}, f32[16,4,1]{0,1,2:T(4,128)S(1)}) fusion(f32[2,4,16]{2,1,0:T(4,128)} %param.10), kind=kLoop, calls=%fused_computation.49 | loop fusion | bytes 1536 | tf_op jit(solution)/shard_map/stack | solution.py:251
  1.4 2.3 %multiply_reduce_fusion.1 = bf16[4,2,64,64]{3,2,1,0:T(8,128)(2,1)S(1)} fusion(f32[2,16,64,64]{3,2,1,0:T(8,128)} %param.9, f32[4,1,2,16]{3,2,0,1:T(2,128)S(1)} %get-tuple-element.28, f32[4,1,2,16]{3,2,0,1:T(2,128)S(1)} %get-tuple-element.29), kind=kLoop, calls=%fused_computation.1 | loop fusion | flops 2064640 | bytes 590848 | tf_op jit(solution)/shard_map/reduce_sum | solution.py:228
  3.7 3.1 %collective-permute-start.2 = (bf16[2,64,64]{2,1,0:T(8,128)(2,1)S(1)}, bf16[2,64,64]{2,1,0:T(8,128)(2,1)S(1)}, u32[]{:S(2)}, u32[]{:S(2)}) collective-permute-start(bf16[2,64,64]{2,1,0:T(8,128)(2,1)S(1)} %get-tuple-element.16), channel_id=1, source_target_pairs={{0,4},{4,8},{8,12},{12,0},{1,5},{5,9},{9,13},{13,1},{2,6},{6,10},{... | collective-permute-start | bytes 49160 | tf_op jit(solution)/shard_map/ppermute | solution.py:85
  6.8 2.6 %collective-permute-start.1 = (bf16[2,64,64]{2,1,0:T(8,128)(2,1)S(1)}, bf16[2,64,64]{2,1,0:T(8,128)(2,1)S(1)}, u32[]{:S(2)}, u32[]{:S(2)}) collective-permute-start(bf16[2,64,64]{2,1,0:T(8,128)(2,1)S(1)} %get-tuple-element.17), channel_id=1, source_target_pairs={{0,8},{4,12},{8,0},{12,4},{1,9},{5,13},{9,1},{13,5},{2,10},{6,14},... | collective-permute-start | bytes 49160 | tf_op jit(solution)/shard_map/ppermute | solution.py:85
  9.4 1.3 %collective-permute-start = (bf16[2,64,64]{2,1,0:T(8,128)(2,1)S(1)}, bf16[2,64,64]{2,1,0:T(8,128)(2,1)S(1)}, u32[]{:S(2)}, u32[]{:S(2)}) collective-permute-start(bf16[2,64,64]{2,1,0:T(8,128)(2,1)S(1)} %get-tuple-element.18), channel_id=1, source_target_pairs={{0,12},{4,0},{8,4},{12,8},{1,13},{5,1},{9,5},{13,9},{2,14},{6,2},{... | collective-permute-start | bytes 49160 | tf_op jit(solution)/shard_map/ppermute | solution.py:85
  10.7 0.7 %fusion = f32[16,4,1]{0,1,2:T(4,128)S(1)} fusion(f32[2,4,16]{2,1,0:T(4,128)} %param.10), kind=kLoop, calls=%fused_computation.46 | loop fusion | flops 64 | bytes 512 | tf_op jit(solution)/shard_map/stack | solution.py:251
  11.4 0.7 %convert_element_type.44 = f32[1,8,256]{2,1,0:T(8,128)S(1)} convert(s32[1,8,256]{2,1,0:T(8,128)} %param.13) | non-fusion elementwise | flops 2048 | bytes 16384 | tf_op jit(solution)/shard_map/convert_element_type | solution.py:238
  13.8 1.6 %collective-permute-start.4 = (bf16[64,512]{1,0:T(8,128)(2,1)S(1)}, bf16[64,512]{1,0:T(8,128)(2,1)S(1)}, u32[]{:S(2)}, u32[]{:S(2)}) collective-permute-start(bf16[64,512]{1,0:T(8,128)(2,1)S(1)} %reshape.40.refs_0_), channel_id=1, source_target_pairs={{0,2},{1,3},{2,0},{3,1},{4,6},{5,7},{6,4},{7,5},{8,10},{9,11},{10,... | collective-permute-start | bytes 196616 | tf_op jit(solution)/shard_map/ppermute | solution.py:237
  15.7 3.7 %collective-permute-done.4.refs_2_ = bf16[64,512]{1,0:T(8,128)(2,1)S(1)} collective-permute-done((bf16[64,512]{1,0:T(8,128)(2,1)S(1)}, bf16[64,512]{1,0:T(8,128)(2,1)S(1)}, u32[]{:S(2)}, u32[]{:S(2)}) %collective-permute-start.4) | collective-permute-done | bytes 65568 | tf_op jit(solution)/shard_map/ppermute | solution.py:237
  20.2 11.7 %shard_map.91 = (f32[64,512]{1,0:T(8,128)}, bf16[3,64,512]{2,1,0:T(8,128)(2,1)}) custom-call(bf16[64,512]{1,0:T(8,128)(2,1)} %copy-done.1, bf16[64,512]{1,0:T(8,128)(2,1)} %copy-done.4, bf16[64,512]{1,0:T(8,128)(2,1)} %copy-done.3, bf16[64,512]{1,0:T(8,128)(2,1)} %copy-done.2, s32[1]{0:T(128)} %bitcast.23.refs_4_, bf16[8,256,512]{2,1,0:T(8,128)(2,1)} %refs_5_.1, ...), custom_call_target="tpu_custom_call" | custom-call | flops 4294967296 | bytes 4718592 | tf_op jit(solution)/shard_map/pallas_call | solution.py:183
  32.0 1.0 %slice_bitcast_fusion.2 = (bf16[64,512]{1,0:T(8,128)(2,1)S(1)}, bf16[64,512]{1,0:T(8,128)(2,1)S(1)}, bf16[64,512]{1,0:T(8,128)(2,1)S(1)}) fusion(bf16[3,64,512]{2,1,0:T(8,128)(2,1)} %get-tuple-element.8), kind=kLoop, calls=%fused_computation.8 | loop fusion | bytes 393216 | tf_op jit(solution)/shard_map/squeeze | solution.py:245
  33.0 1.7 %collective-permute-start.8 = (bf16[64,512]{1,0:T(8,128)(2,1)S(1)}, bf16[64,512]{1,0:T(8,128)(2,1)S(1)}, u32[]{:S(2)}, u32[]{:S(2)}) collective-permute-start(bf16[64,512]{1,0:T(8,128)(2,1)S(1)} %get-tuple-element.10), channel_id=1, source_target_pairs={{0,3},{1,0},{2,1},{3,2},{4,7},{5,4},{6,5},{7,6},{8,11},{9,8},{10,9... | collective-permute-start | bytes 196616 | tf_op jit(solution)/shard_map/ppermute | solution.py:245
  34.8 0.9 %collective-permute-start.7 = (bf16[64,512]{1,0:T(8,128)(2,1)S(1)}, bf16[64,512]{1,0:T(8,128)(2,1)S(1)}, u32[]{:S(2)}, u32[]{:S(2)}) collective-permute-start(bf16[64,512]{1,0:T(8,128)(2,1)S(1)} %get-tuple-element.11), channel_id=1, source_target_pairs={{0,2},{1,3},{2,0},{3,1},{4,6},{5,7},{6,4},{7,5},{8,10},{9,11},{10,... | collective-permute-start | bytes 196616 | tf_op jit(solution)/shard_map/ppermute | solution.py:245
  35.8 0.9 %collective-permute-done.6 = bf16[64,512]{1,0:T(8,128)(2,1)S(1)} collective-permute-done((bf16[64,512]{1,0:T(8,128)(2,1)S(1)}, bf16[64,512]{1,0:T(8,128)(2,1)S(1)}, u32[]{:S(2)}, u32[]{:S(2)}) %collective-permute-start.6) | collective-permute-done | bytes 65568 | tf_op jit(solution)/shard_map/ppermute | solution.py:245
  36.7 2.3 %collective-permute-done.7 = bf16[64,512]{1,0:T(8,128)(2,1)S(1)} collective-permute-done((bf16[64,512]{1,0:T(8,128)(2,1)S(1)}, bf16[64,512]{1,0:T(8,128)(2,1)S(1)}, u32[]{:S(2)}, u32[]{:S(2)}) %collective-permute-start.7) | collective-permute-done | bytes 65568 | tf_op jit(solution)/shard_map/ppermute | solution.py:245
  39.0 0.9 %add_convert_fusion = bf16[64,512]{1,0:T(8,128)(2,1)S(1)} fusion(bf16[64,512]{1,0:T(8,128)(2,1)S(1)} %collective-permute-done.8, bf16[64,512]{1,0:T(8,128)(2,1)S(1)} %collective-permute-done.7, f32[64,512]{1,0:T(8,128)} %get-tuple-element.7, bf16[64,512]{1,0:T(8,128)(2,1)S(1)} %collective-permute-done.6), kind=kLoop, calls=%fused_computation.4 | loop fusion | flops 229376 | bytes 393216 | tf_op jit(solution)/shard_map/convert_element_type | solution.py:248
  40.4 3.2 %collective-permute-start.9 = (bf16[64,2,64]{2,0,1:T(8,128)(2,1)S(1)}, bf16[64,2,64]{2,0,1:T(8,128)(2,1)S(1)}, u32[]{:S(2)}, u32[]{:S(2)}) collective-permute-start(bf16[64,2,64]{2,0,1:T(8,128)(2,1)S(1)} %bitcast.85), channel_id=1, source_target_pairs={{0,12},{4,0},{8,4},{12,8},{1,13},{5,1},{9,5},{13,9},{2,14},{6,2},{... | collective-permute-start | bytes 49160 | tf_op jit(solution)/shard_map/ppermute | solution.py:85
  43.7 0.6 %collective-permute-start.11 = (bf16[64,2,64]{2,0,1:T(8,128)(2,1)S(1)}, bf16[64,2,64]{2,0,1:T(8,128)(2,1)S(1)}, u32[]{:S(2)}, u32[]{:S(2)}) collective-permute-start(bf16[64,2,64]{2,0,1:T(8,128)(2,1)S(1)} %bitcast.83), channel_id=1, source_target_pairs={{0,4},{4,8},{8,12},{12,0},{1,5},{5,9},{9,13},{13,1},{2,6},{6,10},{... | collective-permute-start | bytes 49160 | tf_op jit(solution)/shard_map/ppermute | solution.py:85
  44.3 0.9 %collective-permute-done.9 = bf16[64,2,64]{2,0,1:T(8,128)(2,1)S(1)} collective-permute-done((bf16[64,2,64]{2,0,1:T(8,128)(2,1)S(1)}, bf16[64,2,64]{2,0,1:T(8,128)(2,1)S(1)}, u32[]{:S(2)}, u32[]{:S(2)}) %collective-permute-start.9) | collective-permute-done | bytes 16416 | tf_op jit(solution)/shard_map/ppermute | solution.py:85
  45.3 3.2 %collective-permute-done.10 = bf16[64,2,64]{2,0,1:T(8,128)(2,1)S(1)} collective-permute-done((bf16[64,2,64]{2,0,1:T(8,128)(2,1)S(1)}, bf16[64,2,64]{2,0,1:T(8,128)(2,1)S(1)}, u32[]{:S(2)}, u32[]{:S(2)}) %collective-permute-start.10) | collective-permute-done | bytes 16416 | tf_op jit(solution)/shard_map/ppermute | solution.py:85
  48.5 0.9 %collective-permute-done.11 = bf16[64,2,64]{2,0,1:T(8,128)(2,1)S(1)} collective-permute-done((bf16[64,2,64]{2,0,1:T(8,128)(2,1)S(1)}, bf16[64,2,64]{2,0,1:T(8,128)(2,1)S(1)}, u32[]{:S(2)}, u32[]{:S(2)}) %collective-permute-start.11) | collective-permute-done | bytes 16416 | tf_op jit(solution)/shard_map/ppermute | solution.py:85
  49.5 1.4 %multiply_reduce_fusion = f32[2,16,64,64]{3,2,1,0:T(8,128)S(1)} fusion(f32[4,64,2,64]{3,1,2,0:T(8,128)S(1)} %dynamic-slice_convert_fusion, f32[2,16,4,2]{3,2,1,0:T(4,128)S(1)} %copy.26), kind=kLoop, calls=%fused_computation | loop fusion | flops 1966080 | bytes 656384 | tf_op jit(solution)/shard_map/reduce_sum | solution.py:253
  50.9 1.1 %multiply_subtract_fusion = f32[2,16,64,64]{3,2,1,0:T(8,128)} fusion(f32[2,16,64,64]{3,2,1,0:T(8,128)S(1)} %copy-done, f32[2,16,64,64]{3,2,1,0:T(8,128)S(1)} %multiply_reduce_fusion), kind=kLoop, calls=%fused_computation.2 | loop fusion | flops 262144 | bytes 1572864 | tf_op jit(solution)/shard_map/sub | solution.py:256
  (51 shorter events, 3.5 us)
Async XLA Ops:
  3.7 9.6 %collective-permute-start.2 = (bf16[2,64,64]{2,1,0:T(8,128)(2,1)S(1)}, bf16[2,64,64]{2,1,0:T(8,128)(2,1)S(1)}, u32[]{:S(2)}, u32[]{:S(2)}) collective-permute-start(bf16[2,64,64]{2,1,0:T(8,128)(2,1)S(1)} %get-tuple-element.16), channel_id=1, source_target_pairs={{0,4},{4,8},{8,12},{12,0},{1,5},{5,9},{9,13},{13,1},{2,6},{6,10},{... | collective-permute-start | bytes 49160 | tf_op jit(solution)/shard_map/ppermute | solution.py:85
  6.8 6.5 %collective-permute-start.1 = (bf16[2,64,64]{2,1,0:T(8,128)(2,1)S(1)}, bf16[2,64,64]{2,1,0:T(8,128)(2,1)S(1)}, u32[]{:S(2)}, u32[]{:S(2)}) collective-permute-start(bf16[2,64,64]{2,1,0:T(8,128)(2,1)S(1)} %get-tuple-element.17), channel_id=1, source_target_pairs={{0,8},{4,12},{8,0},{12,4},{1,9},{5,13},{9,1},{13,5},{2,10},{6,14},... | collective-permute-start | bytes 49160 | tf_op jit(solution)/shard_map/ppermute | solution.py:85
  9.4 3.9 %collective-permute-start = (bf16[2,64,64]{2,1,0:T(8,128)(2,1)S(1)}, bf16[2,64,64]{2,1,0:T(8,128)(2,1)S(1)}, u32[]{:S(2)}, u32[]{:S(2)}) collective-permute-start(bf16[2,64,64]{2,1,0:T(8,128)(2,1)S(1)} %get-tuple-element.18), channel_id=1, source_target_pairs={{0,12},{4,0},{8,4},{12,8},{1,13},{5,1},{9,5},{13,9},{2,14},{6,2},{... | collective-permute-start | bytes 49160 | tf_op jit(solution)/shard_map/ppermute | solution.py:85
  13.7 5.9 %copy-start.1 = (bf16[64,512]{1,0:T(8,128)(2,1)}, bf16[64,512]{1,0:T(8,128)(2,1)S(1)}, u32[]{:S(2)}) copy-start(bf16[64,512]{1,0:T(8,128)(2,1)S(1)} %reshape.40.refs_0_) | copy-start | bytes 196612
  13.7 2.0 %collective-permute-start.5 = (bf16[64,512]{1,0:T(8,128)(2,1)S(1)}, bf16[64,512]{1,0:T(8,128)(2,1)S(1)}, u32[]{:S(2)}, u32[]{:S(2)}) collective-permute-start(bf16[64,512]{1,0:T(8,128)(2,1)S(1)} %reshape.40.refs_0_), channel_id=1, source_target_pairs={{0,3},{1,0},{2,1},{3,2},{4,7},{5,4},{6,5},{7,6},{8,11},{9,8},{10,9... | collective-permute-start | bytes 196616 | tf_op jit(solution)/shard_map/ppermute | solution.py:237
  13.8 5.6 %collective-permute-start.4 = (bf16[64,512]{1,0:T(8,128)(2,1)S(1)}, bf16[64,512]{1,0:T(8,128)(2,1)S(1)}, u32[]{:S(2)}, u32[]{:S(2)}) collective-permute-start(bf16[64,512]{1,0:T(8,128)(2,1)S(1)} %reshape.40.refs_0_), channel_id=1, source_target_pairs={{0,2},{1,3},{2,0},{3,1},{4,6},{5,7},{6,4},{7,5},{8,10},{9,11},{10,... | collective-permute-start | bytes 196616 | tf_op jit(solution)/shard_map/ppermute | solution.py:237
  15.3 4.3 %collective-permute-start.3 = (bf16[64,512]{1,0:T(8,128)(2,1)S(1)}, bf16[64,512]{1,0:T(8,128)(2,1)S(1)}, u32[]{:S(2)}, u32[]{:S(2)}) collective-permute-start(bf16[64,512]{1,0:T(8,128)(2,1)S(1)} %reshape.40.refs_0_), channel_id=1, source_target_pairs={{0,1},{1,2},{2,3},{3,0},{4,5},{5,6},{6,7},{7,4},{8,9},{9,10},{10,1... | collective-permute-start | bytes 196616 | tf_op jit(solution)/shard_map/ppermute | solution.py:237
  15.7 3.9 %copy-start.2 = (bf16[64,512]{1,0:T(8,128)(2,1)}, bf16[64,512]{1,0:T(8,128)(2,1)S(1)}, u32[]{:S(2)}) copy-start(bf16[64,512]{1,0:T(8,128)(2,1)S(1)} %collective-permute-done.5.refs_3_) | copy-start | bytes 196612
  19.4 0.6 %copy-start.3 = (bf16[64,512]{1,0:T(8,128)(2,1)}, bf16[64,512]{1,0:T(8,128)(2,1)S(1)}, u32[]{:S(2)}) copy-start(bf16[64,512]{1,0:T(8,128)(2,1)S(1)} %collective-permute-done.4.refs_2_) | copy-start | bytes 196612
  19.6 0.6 %copy-start.4 = (bf16[64,512]{1,0:T(8,128)(2,1)}, bf16[64,512]{1,0:T(8,128)(2,1)S(1)}, u32[]{:S(2)}) copy-start(bf16[64,512]{1,0:T(8,128)(2,1)S(1)} %collective-permute-done.3.refs_1_) | copy-start | bytes 196612
  32.0 18.9 %copy-start = (f32[2,16,64,64]{3,2,1,0:T(8,128)S(1)}, f32[2,16,64,64]{3,2,1,0:T(8,128)}, u32[]{:S(2)}) copy-start(f32[2,16,64,64]{3,2,1,0:T(8,128)} %param.9) | copy-start | bytes 1572868
  33.0 3.7 %collective-permute-start.6 = (bf16[64,512]{1,0:T(8,128)(2,1)S(1)}, bf16[64,512]{1,0:T(8,128)(2,1)S(1)}, u32[]{:S(2)}, u32[]{:S(2)}) collective-permute-start(bf16[64,512]{1,0:T(8,128)(2,1)S(1)} %get-tuple-element.9), channel_id=1, source_target_pairs={{0,1},{1,2},{2,3},{3,0},{4,5},{5,6},{6,7},{7,4},{8,9},{9,10},{10,1... | collective-permute-start | bytes 196616 | tf_op jit(solution)/shard_map/ppermute | solution.py:245
  33.0 3.7 %collective-permute-start.8 = (bf16[64,512]{1,0:T(8,128)(2,1)S(1)}, bf16[64,512]{1,0:T(8,128)(2,1)S(1)}, u32[]{:S(2)}, u32[]{:S(2)}) collective-permute-start(bf16[64,512]{1,0:T(8,128)(2,1)S(1)} %get-tuple-element.10), channel_id=1, source_target_pairs={{0,3},{1,0},{2,1},{3,2},{4,7},{5,4},{6,5},{7,6},{8,11},{9,8},{10,9... | collective-permute-start | bytes 196616 | tf_op jit(solution)/shard_map/ppermute | solution.py:245
  34.8 4.3 %collective-permute-start.7 = (bf16[64,512]{1,0:T(8,128)(2,1)S(1)}, bf16[64,512]{1,0:T(8,128)(2,1)S(1)}, u32[]{:S(2)}, u32[]{:S(2)}) collective-permute-start(bf16[64,512]{1,0:T(8,128)(2,1)S(1)} %get-tuple-element.11), channel_id=1, source_target_pairs={{0,2},{1,3},{2,0},{3,1},{4,6},{5,7},{6,4},{7,5},{8,10},{9,11},{10,... | collective-permute-start | bytes 196616 | tf_op jit(solution)/shard_map/ppermute | solution.py:245
  40.4 4.8 %collective-permute-start.9 = (bf16[64,2,64]{2,0,1:T(8,128)(2,1)S(1)}, bf16[64,2,64]{2,0,1:T(8,128)(2,1)S(1)}, u32[]{:S(2)}, u32[]{:S(2)}) collective-permute-start(bf16[64,2,64]{2,0,1:T(8,128)(2,1)S(1)} %bitcast.85), channel_id=1, source_target_pairs={{0,12},{4,0},{8,4},{12,8},{1,13},{5,1},{9,5},{13,9},{2,14},{6,2},{... | collective-permute-start | bytes 49160 | tf_op jit(solution)/shard_map/ppermute | solution.py:85
  43.7 4.8 %collective-permute-start.10 = (bf16[64,2,64]{2,0,1:T(8,128)(2,1)S(1)}, bf16[64,2,64]{2,0,1:T(8,128)(2,1)S(1)}, u32[]{:S(2)}, u32[]{:S(2)}) collective-permute-start(bf16[64,2,64]{2,0,1:T(8,128)(2,1)S(1)} %bitcast.84), channel_id=1, source_target_pairs={{0,8},{4,12},{8,0},{12,4},{1,9},{5,13},{9,1},{13,5},{2,10},{6,14},... | collective-permute-start | bytes 49160 | tf_op jit(solution)/shard_map/ppermute | solution.py:85
  43.7 5.7 %collective-permute-start.11 = (bf16[64,2,64]{2,0,1:T(8,128)(2,1)S(1)}, bf16[64,2,64]{2,0,1:T(8,128)(2,1)S(1)}, u32[]{:S(2)}, u32[]{:S(2)}) collective-permute-start(bf16[64,2,64]{2,0,1:T(8,128)(2,1)S(1)} %bitcast.83), channel_id=1, source_target_pairs={{0,4},{4,8},{8,12},{12,0},{1,5},{5,9},{9,13},{13,1},{2,6},{6,10},{... | collective-permute-start | bytes 49160 | tf_op jit(solution)/shard_map/ppermute | solution.py:85

commit v7 on v6

--- a/solution.py
+++ b/solution.py
@@ -230,23 +230,33 @@
     ).astype(jnp.bfloat16)
     frames_here = images.shape[0]
     width_own = images.shape[3]
-    pieces_x = exchange_blocks(images, "frame")
-    own_rows = jnp.transpose(pieces_x, (2, 1, 0, 3)).reshape(rows_own, 2 * width_x)
     groups = lax.axis_size("coil")
+    frames = lax.axis_size("frame")
     me_c = lax.axis_index("coil")
-    pieces = [own_rows] + [lax.ppermute(own_rows, "coil", shifted(groups, step)) for step in range(1, groups)]
+    spread = jnp.broadcast_to(images[:, None], (frames, groups) + images.shape[1:]).reshape(
+        (frames * groups,) + images.shape[1:]
+    )
+    arrived = lax.all_to_all(spread, ("frame", "coil"), 0, 0, tiled=True)
+    full_rows = jnp.transpose(arrived.reshape((frames, groups) + images.shape[1:]), (1, 3, 2, 0, 4))
+    full_rows = full_rows.reshape(groups, rows_own, 2 * width_x)
+    pieces = [lax.dynamic_index_in_dim(full_rows, (me_c - step) % groups, 0, keepdims=False) for step in range(groups)]
     sampled = masks[0].astype(jnp.float32)[:, None, :]
     place = jnp.reshape(me_c, (1,)).astype(jnp.int32)
     own_total, outgoing = coil_chain(
         pieces, place, maps, kdata[0], sampled, forward_x, adjoint_x, table_y_re, table_y_im
     )
-    own_share = own_total
+    total_rows = [None] * groups
+    total_rows[0] = own_total
     for step in range(1, groups):
-        own_share = own_share + lax.ppermute(outgoing[step - 1], "coil", shifted(groups, step)).astype(jnp.float32)
-    outgoing = jnp.transpose(
-        own_share.reshape(rows_own, 2, frames_here, width_own), (2, 0, 1, 3)
-    ).astype(jnp.bfloat16)
-    returned = exchange_blocks(outgoing, "frame").astype(jnp.float32)
+        total_rows[step] = outgoing[step - 1].astype(jnp.float32)
+    ordered = jnp.take(jnp.stack(total_rows), (jnp.arange(groups) - me_c) % groups, axis=0)
+    terms = jnp.transpose(
+        ordered.reshape(groups, rows_own, 2, frames, width_own), (3, 0, 1, 2, 4)
+    ).reshape((frames * groups, rows_own, 2, width_own))
+    received = lax.all_to_all(terms.astype(jnp.bfloat16), ("frame", "coil"), 0, 0, tiled=True)
+    returned = jnp.sum(
+        received.reshape((frames, groups, rows_own, 2, width_own)).astype(jnp.float32), axis=1
+    )
     weights = jnp.stack(
         [jnp.stack([time_re.T, time_im.T], axis=2), jnp.stack([-time_im.T, time_re.T], axis=2)], axis=0
     )

time: 52.3 us -> 57 us (1.090)
  waiting for transfers between devices: 13 us -> 19.1 us
  starting transfers between devices: 15.3 us -> 10.9 us
  local copies, waits for them, and re-layouts: 3.96 us -> 7.67 us
  other arithmetic: 7.83 us -> 6.81 us
    all_to_all x0 -> x2, waiting for transfers between devices: none -> 19.1 us  [the longest x1 9.83 us: on_device(): lax.all_to_all(terms.astype(jnp.bfloat16), ('frame', 'coil'), 0, 0, tiled...]
    ppermute x12 -> x0, starting transfers between devices: 15.3 us -> none  [the longest x6 10.9 us: exchange_blocks(): pieces.append(lax.ppermute(outgoing, axis, shifted(count, step)))]
    ppermute x12 -> x0, waiting for transfers between devices: 13 us -> none  [the longest x6 5.63 us: exchange_blocks(): pieces.append(lax.ppermute(outgoing, axis, shifted(count, step)))]
    all_to_all x0 -> x2, starting transfers between devices: none -> 10.9 us  [the longest x1 7.36 us: on_device(): arrived = lax.all_to_all(spread, ('frame', 'coil'), 0, 0, tiled=True)]
    unnamed x27 -> x11, local copies, waits for them, and re-layouts: 1.4 us -> 3.52 us
    another operation x0 -> x1, other arithmetic: none -> 0.95 us  [on_device(): jnp.stack(total_rows)]
    slice x0 -> x1, local copies, waits for them, and re-layouts: none -> 0.92 us  [on_device(): total_rows[step] = outgoing[step - 1].astype(jnp.float32)]
    gather x0 -> x2, local copies, waits for them, and re-layouts: none -> 0.83 us  [on_device(): jnp.take(jnp.stack(total_rows), (jnp.arange(groups) - me_c) % groups, axi...]
  transfers between devices with their start and end apart: 12 -> 2, of which waited for: 9 -> 2; matrix products, arithmetic and copies ran while one was open for 4% -> 1% of each run, Pallas kernels for 0% -> 0%
where the time goes in v7:
time: 57 us; the launch traced here: 56.5 us
  waiting for transfers between devices  19.1 us (34%)
  Pallas kernels  11.7 us (21%)
  starting transfers between devices  10.9 us (19%)
  local copies, waits for them, and re-layouts  7.67 us (13%)
  other arithmetic  6.81 us (12%)
    pallas_call x1, Pallas kernels, coil_chain(): pl.pallas_call(coil_chain_kernel, out_shape=(jax.ShapeDtypeStruct((rows,...  11.7 us
    all_to_all x1, waiting for transfers between devices, on_device(): lax.all_to_all(terms.astype(jnp.bfloat16), ('frame', 'coil'), 0, 0, tiled...  9.83 us
    all_to_all x1, waiting for transfers between devices, on_device(): arrived = lax.all_to_all(spread, ('frame', 'coil'), 0, 0, tiled=True)  9.3 us
    all_to_all x1, starting transfers between devices, on_device(): arrived = lax.all_to_all(spread, ('frame', 'coil'), 0, 0, tiled=True)  7.36 us
    all_to_all x1, starting transfers between devices, on_device(): lax.all_to_all(terms.astype(jnp.bfloat16), ('frame', 'coil'), 0, 0, tiled...  3.53 us
    unnamed x11, local copies, waits for them, and re-layouts  3.52 us
    reduce_sum x1, other arithmetic, on_device(): jnp.sum(mixing[:, :, :, :, None, None] * factors[None, None], axis=(2, 3))  2.29 us
    reduce_sum x1, other arithmetic, on_device(): jnp.sum(weights[:, :, :, None, :, None] * returned[None, None], axis=(2, 4))  1.36 us
  transfers between devices with their start and end apart: 2, of which 2 were waited for; matrix products, arithmetic and copies ran while one was open for 1% of the time, Pallas kernels for 0%

profile of v7, /device:TPU:0, one launch (start us, length us, event | category | flops | bytes accessed | tf_op | source)
XLA Modules:
  0.0 56.5 jit_solution(1008456723336871076)
XLA Ops:
  0.0 0.7 %fusion.5 = f32[4,1,16]{2,0,1:T(4,128)S(1)} fusion(f32[2,4,16]{2,1,0:T(4,128)} %param.10), kind=kLoop, calls=%fused_computation.43 | loop fusion | flops 64 | bytes 512 | tf_op jit(solution)/shard_map/neg | solution.py:226
  0.7 0.7 %slice_bitcast_fusion.2 = (f32[16,4,1]{0,1,2:T(4,128)S(1)}, f32[4,1,16]{2,0,1:T(4,128)S(1)}, f32[4,1,16]{2,0,1:T(4,128)S(1)}, f32[16,4,1]{0,1,2:T(4,128)S(1)}) fusion(f32[2,4,16]{2,1,0:T(4,128)} %param.10), kind=kLoop, calls=%fused_computation.38 | loop fusion | bytes 1536 | tf_op jit(solution)/shard_map/stack | solution.py:261
  1.4 2.3 %multiply_reduce_fusion.1 = bf16[4,2,64,64]{3,2,1,0:T(8,128)(2,1)S(1)} fusion(f32[2,16,64,64]{3,2,1,0:T(8,128)} %param.9, f32[4,1,2,16]{3,2,0,1:T(2,128)S(1)} %get-tuple-element.24, f32[4,1,2,16]{3,2,0,1:T(2,128)S(1)} %get-tuple-element.25), kind=kLoop, calls=%fused_computation.2 | loop fusion | flops 2064640 | bytes 590848 | tf_op jit(solution)/shard_map/reduce_sum | solution.py:228
  3.8 1.1 %reshape.114 = bf16[16,2,4096]{2,1,0:T(2,128)(2,1)} reshape(bf16[16,2,64,64]{3,2,1,0:T(8,128)(2,1)S(1)} %bitcast.60) | data formatting | bytes 524288
  4.9 7.4 %all-to-all-start = ((bf16[16,2,4096]{2,1,0:T(2,128)(2,1)}), bf16[16,2,4096]{2,1,0:T(2,128)(2,1)S(1)}, u32[]{:S(2)}, u32[]{:S(2)}) async-start(bf16[16,2,4096]{2,1,0:T(2,128)(2,1)} %reshape.114), calls=%async_computation | async-start | bytes 524288 | tf_op jit(solution)/shard_map/all_to_all | solution.py:239
  12.4 0.6 %copy.52 = f32[1,8,256]{2,0,1:T(1,128)} copy(f32[1,8,256]{2,1,0:T(8,128)S(1)} %convert_element_type.59) | data formatting | bytes 16384
  13.1 9.3 %all-to-all-done = bf16[16,2,4096]{2,1,0:T(2,128)(2,1)S(1)} async-done(((bf16[16,2,4096]{2,1,0:T(2,128)(2,1)}), bf16[16,2,4096]{2,1,0:T(2,128)(2,1)S(1)}, u32[]{:S(2)}, u32[]{:S(2)}) %all-to-all-start) | async-done | bytes 262176 | tf_op jit(solution)/shard_map/all_to_all | solution.py:239
  22.4 0.3 reshape.115
  22.7 0.4 copy.40
  23.1 0.3 reshape.103
  23.4 0.7 %dynamic-slice_bitcast_fusion = (bf16[64,512]{1,0:T(8,128)(2,1)}, bf16[64,512]{1,0:T(8,128)(2,1)}, bf16[64,512]{1,0:T(8,128)(2,1)}, bf16[64,512]{1,0:T(8,128)(2,1)}) fusion(bf16[4,64,512]{2,1,0:T(8,128)(2,1)S(1)} %reshape.103, s32[]{:T(128)S(6)} %select_n.79, s32[]{:T(128)S(6)} %select_n.77, s32[]{:T(128)S(6)} %select_n.75, s32[]{:T(128)S(6)} %select_n.73), kind=kLoop, calls=%fused_computation.11 | loop fusion | bytes 524304 | tf_op jit(solution)/shard_map/jit(dynamic_index_in_dim)/squeeze | solution.py:242
  24.2 11.7 %shard_map.91 = (f32[64,512]{1,0:T(8,128)}, bf16[3,64,512]{2,1,0:T(8,128)(2,1)}) custom-call(bf16[64,512]{1,0:T(8,128)(2,1)} %get-tuple-element.12.refs_0_, bf16[64,512]{1,0:T(8,128)(2,1)} %get-tuple-element.11.refs_1_, bf16[64,512]{1,0:T(8,128)(2,1)} %get-tuple-element.10.refs_2_, bf16[64,512]{1,0:T(8,128)(2,1)} %get-tuple-element.9.refs_3_, ...), custom_call_target="tpu_custom_call" | custom-call | flops 4294967296 | bytes 4718592 | tf_op jit(solution)/shard_map/pallas_call | solution.py:183
  35.9 0.9 %fusion.6 = (bf16[1,64,512]{2,1,0:T(8,128)(2,1)S(1)}, bf16[1,64,512]{2,1,0:T(8,128)(2,1)S(1)}, bf16[1,64,512]{2,1,0:T(8,128)(2,1)S(1)}) fusion(bf16[3,64,512]{2,1,0:T(8,128)(2,1)} %get-tuple-element.8), kind=kLoop, calls=%fused_computation.44 | loop fusion | bytes 393216 | tf_op jit(solution)/shard_map/slice | solution.py:251
  36.8 0.9 %pad_maximum_fusion = bf16[4,64,512]{2,1,0:T(8,128)(2,1)S(1)} fusion(bf16[1,64,512]{2,1,0:T(8,128)(2,1)S(1)} %get-tuple-element.14, bf16[1,64,512]{2,1,0:T(8,128)(2,1)S(1)} %get-tuple-element.15, bf16[1,64,512]{2,1,0:T(8,128)(2,1)S(1)} %get-tuple-element.13, f32[1,64,512]{2,1,0:T(8,128)} %bitcast.63), kind=kLoop, calls=%fused_computation.7 | loop fusion | flops 393216 | bytes 589824 | tf_op jit(solution)/shard_map/stack | solution.py:252
  37.8 0.6 gather_fusion
  38.3 0.3 gather.7
  38.6 0.2 fusion
  38.9 1.1 %reshape.116 = bf16[16,2,4096]{2,1,0:T(2,128)(2,1)} reshape(bf16[16,2,64,64]{3,2,1,0:T(8,128)(2,1)S(1)} %bitcast.61) | data formatting | bytes 524288
  40.0 3.5 %all-to-all-start.1 = ((bf16[16,2,4096]{2,1,0:T(2,128)(2,1)}), bf16[16,2,4096]{2,1,0:T(2,128)(2,1)S(1)}, u32[]{:S(2)}, u32[]{:S(2)}) async-start(bf16[16,2,4096]{2,1,0:T(2,128)(2,1)} %reshape.116), calls=%async_computation.1 | async-start | bytes 524288 | tf_op jit(solution)/shard_map/all_to_all | solution.py:256
  43.6 0.1 copy.36
  43.7 9.8 %all-to-all-done.1 = bf16[16,2,4096]{2,1,0:T(2,128)(2,1)S(1)} async-done(((bf16[16,2,4096]{2,1,0:T(2,128)(2,1)}), bf16[16,2,4096]{2,1,0:T(2,128)(2,1)S(1)}, u32[]{:S(2)}, u32[]{:S(2)}) %all-to-all-start.1) | async-done | bytes 262176 | tf_op jit(solution)/shard_map/all_to_all | solution.py:256
  53.5 0.3 reshape.117
  54.0 1.4 %multiply_reduce_fusion = f32[2,16,64,64]{3,2,1,0:T(8,128)S(1)} fusion(f32[4,64,2,64]{3,1,2,0:T(8,128)S(1)} %convert_reduce_fusion, f32[2,16,4,2]{3,2,1,0:T(4,128)S(1)} %copy.36), kind=kLoop, calls=%fused_computation.1 | loop fusion | flops 1966080 | bytes 656384 | tf_op jit(solution)/shard_map/reduce_sum | solution.py:263
  55.4 1.1 %multiply_subtract_fusion = f32[2,16,64,64]{3,2,1,0:T(8,128)} fusion(f32[2,16,64,64]{3,2,1,0:T(8,128)S(1)} %copy-done, f32[2,16,64,64]{3,2,1,0:T(8,128)S(1)} %multiply_reduce_fusion), kind=kLoop, calls=%fused_computation.6 | loop fusion | flops 262144 | bytes 1572864 | tf_op jit(solution)/shard_map/sub | solution.py:266
  (17 shorter events, 0.3 us)
Async XLA Ops:
  0.0 12.4 %copy-start.2 = (s32[1,8,256]{2,1,0:T(8,128)S(1)}, s32[1,8,256]{2,1,0:T(8,128)}, u32[]{:S(2)}) copy-start(s32[1,8,256]{2,1,0:T(8,128)} %param.13) | copy-start | bytes 24580
  4.9 17.4 %all-to-all-start = ((bf16[16,2,4096]{2,1,0:T(2,128)(2,1)}), bf16[16,2,4096]{2,1,0:T(2,128)(2,1)S(1)}, u32[]{:S(2)}, u32[]{:S(2)}) async-start(bf16[16,2,4096]{2,1,0:T(2,128)(2,1)} %reshape.114), calls=%async_computation | async-start | bytes 524288 | tf_op jit(solution)/shard_map/all_to_all | solution.py:239
  36.8 6.7 %copy-start.1 = (f32[2,4,16]{2,1,0:T(4,128)S(1)}, f32[2,4,16]{2,1,0:T(4,128)}, u32[]{:S(2)}) copy-start(f32[2,4,16]{2,1,0:T(4,128)} %param.10) | copy-start | bytes 1540
  38.8 16.5 %copy-start = (f32[2,16,64,64]{3,2,1,0:T(8,128)S(1)}, f32[2,16,64,64]{3,2,1,0:T(8,128)}, u32[]{:S(2)}) copy-start(f32[2,16,64,64]{3,2,1,0:T(8,128)} %param.9) | copy-start | bytes 1572868
  40.0 13.5 %all-to-all-start.1 = ((bf16[16,2,4096]{2,1,0:T(2,128)(2,1)}), bf16[16,2,4096]{2,1,0:T(2,128)(2,1)S(1)}, u32[]{:S(2)}, u32[]{:S(2)}) async-start(bf16[16,2,4096]{2,1,0:T(2,128)(2,1)} %reshape.116), calls=%async_computation.1 | async-start | bytes 524288 | tf_op jit(solution)/shard_map/all_to_all | solution.py:256

commit v8 on v6

--- a/solution.py
+++ b/solution.py
@@ -107,15 +107,14 @@
 
 
 def coil_chain_kernel(*refs):
-    groups = len(refs) - 12
+    groups = len(refs) - 13
     pieces = refs[:groups]
-    place_ref, sens_ref, measured_ref, sampled_ref, forward_ref, adjoint_ref, table_re_ref, table_im_ref = refs[
-        groups:groups + 8
-    ]
-    own_ref, send_ref = refs[groups + 8:groups + 10]
-    image_ref, total_ref = refs[groups + 10:]
+    place_ref, sens_ref, measured_ref, sampled_ref, forward_ref, adjoint_ref, table_ref = refs[groups:groups + 7]
+    own_ref, send_ref = refs[groups + 7:groups + 9]
+    image_re_ref, image_im_ref, total_re_ref, total_im_ref = refs[groups + 9:]
     rows = pieces[0].shape[0]
-    half_width = image_ref.shape[1] // 2
+    half_width = image_re_ref.shape[1]
+    height = image_re_ref.shape[0]
     me = place_ref[0]
     step = pl.program_id(0)
 
@@ -126,54 +125,65 @@
             value = pieces[0][...]
             for other in range(1, groups):
                 value = jnp.where(source == other, pieces[other][...], value)
-            image_ref[block * rows:(block + 1) * rows, :] = value
-
-    sens = sens_ref[0].astype(jnp.float32)
-    sens_re = sens[:, :half_width]
-    sens_im = sens[:, half_width:]
-    image = image_ref[...].astype(jnp.float32)
-    image_re = image[:, :half_width]
-    image_im = image[:, half_width:]
-    coil = jnp.concatenate(
-        [sens_re * image_re - sens_im * image_im, sens_re * image_im + sens_im * image_re], axis=1
+            value = value.astype(jnp.float32)
+            image_re_ref[block * rows:(block + 1) * rows, :] = value[:, :half_width]
+            image_im_ref[block * rows:(block + 1) * rows, :] = value[:, half_width:]
+
+    sens_re = sens_ref[0, :, :half_width].astype(jnp.float32)
+    sens_im = sens_ref[0, :, half_width:].astype(jnp.float32)
+    image_re = image_re_ref[...]
+    image_im = image_im_ref[...]
+    coil_re = (sens_re * image_re - sens_im * image_im).astype(jnp.bfloat16)
+    coil_im = (sens_re * image_im + sens_im * image_re).astype(jnp.bfloat16)
+    half_k = (
+        jnp.dot(coil_re, forward_ref[:half_width, :], preferred_element_type=jnp.float32)
+        + jnp.dot(coil_im, forward_ref[half_width:, :], preferred_element_type=jnp.float32)
     ).astype(jnp.bfloat16)
-    half_k = jnp.dot(coil, forward_ref[...], preferred_element_type=jnp.float32).astype(jnp.bfloat16)
-    table_re = table_re_ref[...]
-    table_im = table_im_ref[...]
-    kspace = jnp.dot(table_re, half_k, preferred_element_type=jnp.float32) + jnp.dot(
-        table_im, swap_halves(half_k, half_width, True), preferred_element_type=jnp.float32
-    )
-    residual = (kspace - measured_ref[0].astype(jnp.float32)).astype(jnp.bfloat16)
-    sampled = sampled_ref[0].astype(jnp.bfloat16)
-    back_half = (
-        jnp.dot(table_re * sampled, residual, preferred_element_type=jnp.float32)
-        + jnp.dot(table_im * sampled, swap_halves(residual, half_width, False), preferred_element_type=jnp.float32)
-    ).astype(jnp.bfloat16)
-    coil_back = jnp.dot(back_half, adjoint_ref[...], preferred_element_type=jnp.float32)
-    back_re = coil_back[:, :half_width]
-    back_im = coil_back[:, half_width:]
-    term = jnp.concatenate(
-        [sens_re * back_re + sens_im * back_im, sens_re * back_im - sens_im * back_re], axis=1
-    )
+    table = table_ref[...]
+    parts = jnp.dot(table, half_k, preferred_element_type=jnp.float32)
+    kspace_re = parts[:height, :half_width] - parts[height:, half_width:]
+    kspace_im = parts[:height, half_width:] + parts[height:, :half_width]
+    residual = jnp.concatenate(
+        [
+            (kspace_re - measured_ref[0, :, :half_width].astype(jnp.float32)).astype(jnp.bfloat16),
+            (kspace_im - measured_ref[0, :, half_width:].astype(jnp.float32)).astype(jnp.bfloat16),
+        ],
+        axis=1,
+    )
+    masked = table * sampled_ref[0].astype(jnp.bfloat16)
+    parts = jnp.dot(masked, residual, preferred_element_type=jnp.float32)
+    back_re = (parts[:height, :half_width] + parts[height:, half_width:]).astype(jnp.bfloat16)
+    back_im = (parts[:height, half_width:] - parts[height:, :half_width]).astype(jnp.bfloat16)
+    coil_back = jnp.dot(back_re, adjoint_ref[:half_width, :], preferred_element_type=jnp.float32) + jnp.dot(
+        back_im, adjoint_ref[half_width:, :], preferred_element_type=jnp.float32
+    )
+    cb_re = coil_back[:, :half_width]
+    cb_im = coil_back[:, half_width:]
+    term_re = sens_re * cb_re + sens_im * cb_im
+    term_im = sens_re * cb_im - sens_im * cb_re
 
     @pl.when(step == 0)
     def _():
-        total_ref[...] = term
+        total_re_ref[...] = term_re
+        total_im_ref[...] = term_im
 
     @pl.when(step > 0)
     def _():
-        total_ref[...] += term
+        total_re_ref[...] += term_re
+        total_im_ref[...] += term_im
 
     @pl.when(step == pl.num_programs(0) - 1)
     def _():
         start = pl.multiple_of(me * rows, rows)
-        own_ref[...] = total_ref[pl.ds(start, rows), :]
+        own_ref[:, :half_width] = total_re_ref[pl.ds(start, rows), :]
+        own_ref[:, half_width:] = total_im_ref[pl.ds(start, rows), :]
         for shift in range(1, groups):
             start = pl.multiple_of(((me + shift) % groups) * rows, rows)
-            send_ref[shift - 1] = total_ref[pl.ds(start, rows), :].astype(jnp.bfloat16)
-
-
-def coil_chain(pieces, place, sens, measured, sampled, forward_x, adjoint_x, table_y_re, table_y_im):
+            send_ref[shift - 1, :, :half_width] = total_re_ref[pl.ds(start, rows), :].astype(jnp.bfloat16)
+            send_ref[shift - 1, :, half_width:] = total_im_ref[pl.ds(start, rows), :].astype(jnp.bfloat16)
+
+
+def coil_chain(pieces, place, sens, measured, sampled, forward_x, adjoint_x, table_y):
     coils, height, width = sens.shape
     groups = len(pieces)
     rows = pieces[0].shape[0]
@@ -195,19 +205,18 @@
             pl.BlockSpec((1, 1, height), per_coil),
             pl.BlockSpec((width, width), whole),
             pl.BlockSpec((width, width), whole),
-            pl.BlockSpec((height, height), whole),
-            pl.BlockSpec((height, height), whole),
+            pl.BlockSpec((2 * height, height), whole),
         ],
         out_specs=(
             pl.BlockSpec((rows, width), whole),
             pl.BlockSpec((groups - 1, rows, width), lambda c: (0, 0, 0)),
         ),
-        scratch_shapes=[pltpu.VMEM((height, width), jnp.bfloat16), pltpu.VMEM((height, width), jnp.float32)],
+        scratch_shapes=[pltpu.VMEM((height, width // 2), jnp.float32)] * 4,
         compiler_params=pltpu.CompilerParams(dimension_semantics=("arbitrary",)),
         cost_estimate=pl.CostEstimate(
             flops=flops, transcendentals=0, bytes_accessed=2 * 2 * coils * height * width + 4 * height * width
         ),
-    )(*pieces, place, sens, measured, sampled, forward_x, adjoint_x, table_y_re, table_y_im)
+    )(*pieces, place, sens, measured, sampled, forward_x, adjoint_x, table_y)
 
 
 def on_device(factors, temporal, maps, kdata, masks):
@@ -218,8 +227,7 @@
     table_y_re, table_y_im = dft_parts(width_y)
     forward_x = jnp.asarray(np.block([[table_x_re, table_x_im], [-table_x_im, table_x_re]]))
     adjoint_x = jnp.asarray(np.block([[table_x_re, -table_x_im], [table_x_im, table_x_re]]))
-    table_y_re = jnp.asarray(table_y_re)
-    table_y_im = jnp.asarray(table_y_im)
+    table_y = jnp.asarray(np.concatenate([table_y_re, table_y_im], axis=0))
     time_re = temporal[0]
     time_im = temporal[1]
     mixing = jnp.stack(
@@ -238,7 +246,7 @@
     sampled = masks[0].astype(jnp.float32)[:, None, :]
     place = jnp.reshape(me_c, (1,)).astype(jnp.int32)
     own_total, outgoing = coil_chain(
-        pieces, place, maps, kdata[0], sampled, forward_x, adjoint_x, table_y_re, table_y_im
+        pieces, place, maps, kdata[0], sampled, forward_x, adjoint_x, table_y
     )
     own_share = own_total
     for step in range(1, groups):

time: 52.3 us -> 53.6 us (1.025)
  Pallas kernels: 11.7 us -> 13 us
    pallas_call x1, Pallas kernels: 11.7 us -> 13 us  [coil_chain(): pl.pallas_call(coil_chain_kernel, out_shape=(jax.ShapeDtypeStruct((rows,...]
where the time goes in v8:
time: 53.6 us; the launch traced here: 53.3 us
  starting transfers between devices  15.3 us (29%)
  waiting for transfers between devices  13 us (24%)
  Pallas kernels  13 us (24%)
  other arithmetic  7.83 us (15%)
  local copies, waits for them, and re-layouts  3.96 us (7%)
    pallas_call x1, Pallas kernels, coil_chain(): pl.pallas_call(coil_chain_kernel, out_shape=(jax.ShapeDtypeStruct((rows,...  13 us
    ppermute x6, starting transfers between devices, exchange_blocks(): pieces.append(lax.ppermute(outgoing, axis, shifted(count, step)))  10.9 us
    ppermute x6, waiting for transfers between devices, exchange_blocks(): pieces.append(lax.ppermute(outgoing, axis, shifted(count, step)))  5.63 us
    ppermute x3, waiting for transfers between devices, on_device(): lax.ppermute(own_rows, 'coil', shifted(groups, step))  4.1 us
    ppermute x3, waiting for transfers between devices, on_device(): lax.ppermute(outgoing[step - 1], 'coil', shifted(groups, step))  3.24 us
    ppermute x3, starting transfers between devices, on_device(): lax.ppermute(outgoing[step - 1], 'coil', shifted(groups, step))  2.67 us
    reduce_sum x1, other arithmetic, on_device(): jnp.sum(mixing[:, :, :, :, None, None] * factors[None, None], axis=(2, 3))  2.29 us
    ppermute x3, starting transfers between devices, on_device(): lax.ppermute(own_rows, 'coil', shifted(groups, step))  1.78 us
  transfers between devices with their start and end apart: 12, of which 9 were waited for; matrix products, arithmetic and copies ran while one was open for 4% of the time, Pallas kernels for 0%

profile of v8, /device:TPU:0, one launch (start us, length us, event | category | flops | bytes accessed | tf_op | source)
XLA Modules:
  0.0 53.3 jit_solution(14169654357893219315)
XLA Ops:
  0.0 0.7 %fusion.1 = f32[4,1,16]{2,0,1:T(4,128)S(1)} fusion(f32[2,4,16]{2,1,0:T(4,128)} %param.9), kind=kLoop, calls=%fused_computation.51 | loop fusion | flops 64 | bytes 512 | tf_op jit(solution)/shard_map/neg | solution.py:234
  0.7 0.7 %slice_bitcast_fusion.5 = (f32[16,4,1]{0,1,2:T(4,128)S(1)}, f32[4,1,16]{2,0,1:T(4,128)S(1)}, f32[4,1,16]{2,0,1:T(4,128)S(1)}, f32[16,4,1]{0,1,2:T(4,128)S(1)}) fusion(f32[2,4,16]{2,1,0:T(4,128)} %param.9), kind=kLoop, calls=%fused_computation.49 | loop fusion | bytes 1536 | tf_op jit(solution)/shard_map/stack | solution.py:259
  1.4 2.3 %multiply_reduce_fusion.1 = bf16[4,2,64,64]{3,2,1,0:T(8,128)(2,1)S(1)} fusion(f32[2,16,64,64]{3,2,1,0:T(8,128)} %param.8, f32[4,1,2,16]{3,2,0,1:T(2,128)S(1)} %get-tuple-element.28, f32[4,1,2,16]{3,2,0,1:T(2,128)S(1)} %get-tuple-element.29), kind=kLoop, calls=%fused_computation.1 | loop fusion | flops 2064640 | bytes 590848 | tf_op jit(solution)/shard_map/reduce_sum | solution.py:236
  3.7 3.1 %collective-permute-start.2 = (bf16[2,64,64]{2,1,0:T(8,128)(2,1)S(1)}, bf16[2,64,64]{2,1,0:T(8,128)(2,1)S(1)}, u32[]{:S(2)}, u32[]{:S(2)}) collective-permute-start(bf16[2,64,64]{2,1,0:T(8,128)(2,1)S(1)} %get-tuple-element.16), channel_id=1, source_target_pairs={{0,4},{4,8},{8,12},{12,0},{1,5},{5,9},{9,13},{13,1},{2,6},{6,10},{... | collective-permute-start | bytes 49160 | tf_op jit(solution)/shard_map/ppermute | solution.py:85
  6.8 2.6 %collective-permute-start.1 = (bf16[2,64,64]{2,1,0:T(8,128)(2,1)S(1)}, bf16[2,64,64]{2,1,0:T(8,128)(2,1)S(1)}, u32[]{:S(2)}, u32[]{:S(2)}) collective-permute-start(bf16[2,64,64]{2,1,0:T(8,128)(2,1)S(1)} %get-tuple-element.17), channel_id=1, source_target_pairs={{0,8},{4,12},{8,0},{12,4},{1,9},{5,13},{9,1},{13,5},{2,10},{6,14},... | collective-permute-start | bytes 49160 | tf_op jit(solution)/shard_map/ppermute | solution.py:85
  9.4 1.3 %collective-permute-start = (bf16[2,64,64]{2,1,0:T(8,128)(2,1)S(1)}, bf16[2,64,64]{2,1,0:T(8,128)(2,1)S(1)}, u32[]{:S(2)}, u32[]{:S(2)}) collective-permute-start(bf16[2,64,64]{2,1,0:T(8,128)(2,1)S(1)} %get-tuple-element.18), channel_id=1, source_target_pairs={{0,12},{4,0},{8,4},{12,8},{1,13},{5,1},{9,5},{13,9},{2,14},{6,2},{... | collective-permute-start | bytes 49160 | tf_op jit(solution)/shard_map/ppermute | solution.py:85
  10.7 0.7 %fusion = f32[16,4,1]{0,1,2:T(4,128)S(1)} fusion(f32[2,4,16]{2,1,0:T(4,128)} %param.9), kind=kLoop, calls=%fused_computation.46 | loop fusion | flops 64 | bytes 512 | tf_op jit(solution)/shard_map/stack | solution.py:259
  11.4 0.7 %convert_element_type.44 = f32[1,8,256]{2,1,0:T(8,128)S(1)} convert(s32[1,8,256]{2,1,0:T(8,128)} %param.12) | non-fusion elementwise | flops 2048 | bytes 16384 | tf_op jit(solution)/shard_map/convert_element_type | solution.py:246
  13.8 1.6 %collective-permute-start.4 = (bf16[64,512]{1,0:T(8,128)(2,1)S(1)}, bf16[64,512]{1,0:T(8,128)(2,1)S(1)}, u32[]{:S(2)}, u32[]{:S(2)}) collective-permute-start(bf16[64,512]{1,0:T(8,128)(2,1)S(1)} %reshape.40.refs_0_), channel_id=1, source_target_pairs={{0,2},{1,3},{2,0},{3,1},{4,6},{5,7},{6,4},{7,5},{8,10},{9,11},{10,... | collective-permute-start | bytes 196616 | tf_op jit(solution)/shard_map/ppermute | solution.py:245
  15.7 3.7 %collective-permute-done.4.refs_2_ = bf16[64,512]{1,0:T(8,128)(2,1)S(1)} collective-permute-done((bf16[64,512]{1,0:T(8,128)(2,1)S(1)}, bf16[64,512]{1,0:T(8,128)(2,1)S(1)}, u32[]{:S(2)}, u32[]{:S(2)}) %collective-permute-start.4) | collective-permute-done | bytes 65568 | tf_op jit(solution)/shard_map/ppermute | solution.py:245
  20.2 13.0 %shard_map.82 = (f32[64,512]{1,0:T(8,128)}, bf16[3,64,512]{2,1,0:T(8,128)(2,1)}) custom-call(bf16[64,512]{1,0:T(8,128)(2,1)} %copy-done.1, bf16[64,512]{1,0:T(8,128)(2,1)} %copy-done.4, bf16[64,512]{1,0:T(8,128)(2,1)} %copy-done.3, bf16[64,512]{1,0:T(8,128)(2,1)} %copy-done.2, s32[1]{0:T(128)} %bitcast.23.refs_4_, bf16[8,256,512]{2,1,0:T(8,128)(2,1)} %refs_5_.1, ...), custom_call_target="tpu_custom_call" | custom-call | flops 4294967296 | bytes 4718592 | tf_op jit(solution)/shard_map/pallas_call | solution.py:193
  33.3 1.0 %slice_bitcast_fusion.2 = (bf16[64,512]{1,0:T(8,128)(2,1)S(1)}, bf16[64,512]{1,0:T(8,128)(2,1)S(1)}, bf16[64,512]{1,0:T(8,128)(2,1)S(1)}) fusion(bf16[3,64,512]{2,1,0:T(8,128)(2,1)} %get-tuple-element.8), kind=kLoop, calls=%fused_computation.8 | loop fusion | bytes 393216 | tf_op jit(solution)/shard_map/squeeze | solution.py:253
  34.3 1.7 %collective-permute-start.8 = (bf16[64,512]{1,0:T(8,128)(2,1)S(1)}, bf16[64,512]{1,0:T(8,128)(2,1)S(1)}, u32[]{:S(2)}, u32[]{:S(2)}) collective-permute-start(bf16[64,512]{1,0:T(8,128)(2,1)S(1)} %get-tuple-element.10), channel_id=1, source_target_pairs={{0,3},{1,0},{2,1},{3,2},{4,7},{5,4},{6,5},{7,6},{8,11},{9,8},{10,9... | collective-permute-start | bytes 196616 | tf_op jit(solution)/shard_map/ppermute | solution.py:253
  36.1 0.9 %collective-permute-start.7 = (bf16[64,512]{1,0:T(8,128)(2,1)S(1)}, bf16[64,512]{1,0:T(8,128)(2,1)S(1)}, u32[]{:S(2)}, u32[]{:S(2)}) collective-permute-start(bf16[64,512]{1,0:T(8,128)(2,1)S(1)} %get-tuple-element.11), channel_id=1, source_target_pairs={{0,2},{1,3},{2,0},{3,1},{4,6},{5,7},{6,4},{7,5},{8,10},{9,11},{10,... | collective-permute-start | bytes 196616 | tf_op jit(solution)/shard_map/ppermute | solution.py:253
  37.1 0.9 %collective-permute-done.6 = bf16[64,512]{1,0:T(8,128)(2,1)S(1)} collective-permute-done((bf16[64,512]{1,0:T(8,128)(2,1)S(1)}, bf16[64,512]{1,0:T(8,128)(2,1)S(1)}, u32[]{:S(2)}, u32[]{:S(2)}) %collective-permute-start.6) | collective-permute-done | bytes 65568 | tf_op jit(solution)/shard_map/ppermute | solution.py:253
  38.0 2.3 %collective-permute-done.7 = bf16[64,512]{1,0:T(8,128)(2,1)S(1)} collective-permute-done((bf16[64,512]{1,0:T(8,128)(2,1)S(1)}, bf16[64,512]{1,0:T(8,128)(2,1)S(1)}, u32[]{:S(2)}, u32[]{:S(2)}) %collective-permute-start.7) | collective-permute-done | bytes 65568 | tf_op jit(solution)/shard_map/ppermute | solution.py:253
  40.3 0.9 %add_convert_fusion = bf16[64,512]{1,0:T(8,128)(2,1)S(1)} fusion(bf16[64,512]{1,0:T(8,128)(2,1)S(1)} %collective-permute-done.8, bf16[64,512]{1,0:T(8,128)(2,1)S(1)} %collective-permute-done.7, f32[64,512]{1,0:T(8,128)} %get-tuple-element.7, bf16[64,512]{1,0:T(8,128)(2,1)S(1)} %collective-permute-done.6), kind=kLoop, calls=%fused_computation.4 | loop fusion | flops 229376 | bytes 393216 | tf_op jit(solution)/shard_map/convert_element_type | solution.py:256
  41.7 3.2 %collective-permute-start.9 = (bf16[64,2,64]{2,0,1:T(8,128)(2,1)S(1)}, bf16[64,2,64]{2,0,1:T(8,128)(2,1)S(1)}, u32[]{:S(2)}, u32[]{:S(2)}) collective-permute-start(bf16[64,2,64]{2,0,1:T(8,128)(2,1)S(1)} %bitcast.85), channel_id=1, source_target_pairs={{0,12},{4,0},{8,4},{12,8},{1,13},{5,1},{9,5},{13,9},{2,14},{6,2},{... | collective-permute-start | bytes 49160 | tf_op jit(solution)/shard_map/ppermute | solution.py:85
  45.0 0.6 %collective-permute-start.11 = (bf16[64,2,64]{2,0,1:T(8,128)(2,1)S(1)}, bf16[64,2,64]{2,0,1:T(8,128)(2,1)S(1)}, u32[]{:S(2)}, u32[]{:S(2)}) collective-permute-start(bf16[64,2,64]{2,0,1:T(8,128)(2,1)S(1)} %bitcast.83), channel_id=1, source_target_pairs={{0,4},{4,8},{8,12},{12,0},{1,5},{5,9},{9,13},{13,1},{2,6},{6,10},{... | collective-permute-start | bytes 49160 | tf_op jit(solution)/shard_map/ppermute | solution.py:85
  45.6 0.9 %collective-permute-done.9 = bf16[64,2,64]{2,0,1:T(8,128)(2,1)S(1)} collective-permute-done((bf16[64,2,64]{2,0,1:T(8,128)(2,1)S(1)}, bf16[64,2,64]{2,0,1:T(8,128)(2,1)S(1)}, u32[]{:S(2)}, u32[]{:S(2)}) %collective-permute-start.9) | collective-permute-done | bytes 16416 | tf_op jit(solution)/shard_map/ppermute | solution.py:85
  46.6 3.2 %collective-permute-done.10 = bf16[64,2,64]{2,0,1:T(8,128)(2,1)S(1)} collective-permute-done((bf16[64,2,64]{2,0,1:T(8,128)(2,1)S(1)}, bf16[64,2,64]{2,0,1:T(8,128)(2,1)S(1)}, u32[]{:S(2)}, u32[]{:S(2)}) %collective-permute-start.10) | collective-permute-done | bytes 16416 | tf_op jit(solution)/shard_map/ppermute | solution.py:85
  49.8 0.9 %collective-permute-done.11 = bf16[64,2,64]{2,0,1:T(8,128)(2,1)S(1)} collective-permute-done((bf16[64,2,64]{2,0,1:T(8,128)(2,1)S(1)}, bf16[64,2,64]{2,0,1:T(8,128)(2,1)S(1)}, u32[]{:S(2)}, u32[]{:S(2)}) %collective-permute-start.11) | collective-permute-done | bytes 16416 | tf_op jit(solution)/shard_map/ppermute | solution.py:85
  50.8 1.4 %multiply_reduce_fusion = f32[2,16,64,64]{3,2,1,0:T(8,128)S(1)} fusion(f32[4,64,2,64]{3,1,2,0:T(8,128)S(1)} %dynamic-slice_convert_fusion, f32[2,16,4,2]{3,2,1,0:T(4,128)S(1)} %copy.25), kind=kLoop, calls=%fused_computation | loop fusion | flops 1966080 | bytes 656384 | tf_op jit(solution)/shard_map/reduce_sum | solution.py:261
  52.2 1.1 %multiply_subtract_fusion = f32[2,16,64,64]{3,2,1,0:T(8,128)} fusion(f32[2,16,64,64]{3,2,1,0:T(8,128)S(1)} %copy-done, f32[2,16,64,64]{3,2,1,0:T(8,128)S(1)} %multiply_reduce_fusion), kind=kLoop, calls=%fused_computation.2 | loop fusion | flops 262144 | bytes 1572864 | tf_op jit(solution)/shard_map/sub | solution.py:264
  (51 shorter events, 3.5 us)
Async XLA Ops:
  3.7 9.6 %collective-permute-start.2 = (bf16[2,64,64]{2,1,0:T(8,128)(2,1)S(1)}, bf16[2,64,64]{2,1,0:T(8,128)(2,1)S(1)}, u32[]{:S(2)}, u32[]{:S(2)}) collective-permute-start(bf16[2,64,64]{2,1,0:T(8,128)(2,1)S(1)} %get-tuple-element.16), channel_id=1, source_target_pairs={{0,4},{4,8},{8,12},{12,0},{1,5},{5,9},{9,13},{13,1},{2,6},{6,10},{... | collective-permute-start | bytes 49160 | tf_op jit(solution)/shard_map/ppermute | solution.py:85
  6.8 6.5 %collective-permute-start.1 = (bf16[2,64,64]{2,1,0:T(8,128)(2,1)S(1)}, bf16[2,64,64]{2,1,0:T(8,128)(2,1)S(1)}, u32[]{:S(2)}, u32[]{:S(2)}) collective-permute-start(bf16[2,64,64]{2,1,0:T(8,128)(2,1)S(1)} %get-tuple-element.17), channel_id=1, source_target_pairs={{0,8},{4,12},{8,0},{12,4},{1,9},{5,13},{9,1},{13,5},{2,10},{6,14},... | collective-permute-start | bytes 49160 | tf_op jit(solution)/shard_map/ppermute | solution.py:85
  9.4 3.9 %collective-permute-start = (bf16[2,64,64]{2,1,0:T(8,128)(2,1)S(1)}, bf16[2,64,64]{2,1,0:T(8,128)(2,1)S(1)}, u32[]{:S(2)}, u32[]{:S(2)}) collective-permute-start(bf16[2,64,64]{2,1,0:T(8,128)(2,1)S(1)} %get-tuple-element.18), channel_id=1, source_target_pairs={{0,12},{4,0},{8,4},{12,8},{1,13},{5,1},{9,5},{13,9},{2,14},{6,2},{... | collective-permute-start | bytes 49160 | tf_op jit(solution)/shard_map/ppermute | solution.py:85
  13.7 5.9 %copy-start.1 = (bf16[64,512]{1,0:T(8,128)(2,1)}, bf16[64,512]{1,0:T(8,128)(2,1)S(1)}, u32[]{:S(2)}) copy-start(bf16[64,512]{1,0:T(8,128)(2,1)S(1)} %reshape.40.refs_0_) | copy-start | bytes 196612
  13.7 2.0 %collective-permute-start.5 = (bf16[64,512]{1,0:T(8,128)(2,1)S(1)}, bf16[64,512]{1,0:T(8,128)(2,1)S(1)}, u32[]{:S(2)}, u32[]{:S(2)}) collective-permute-start(bf16[64,512]{1,0:T(8,128)(2,1)S(1)} %reshape.40.refs_0_), channel_id=1, source_target_pairs={{0,3},{1,0},{2,1},{3,2},{4,7},{5,4},{6,5},{7,6},{8,11},{9,8},{10,9... | collective-permute-start | bytes 196616 | tf_op jit(solution)/shard_map/ppermute | solution.py:245
  13.8 5.6 %collective-permute-start.4 = (bf16[64,512]{1,0:T(8,128)(2,1)S(1)}, bf16[64,512]{1,0:T(8,128)(2,1)S(1)}, u32[]{:S(2)}, u32[]{:S(2)}) collective-permute-start(bf16[64,512]{1,0:T(8,128)(2,1)S(1)} %reshape.40.refs_0_), channel_id=1, source_target_pairs={{0,2},{1,3},{2,0},{3,1},{4,6},{5,7},{6,4},{7,5},{8,10},{9,11},{10,... | collective-permute-start | bytes 196616 | tf_op jit(solution)/shard_map/ppermute | solution.py:245
  15.3 4.3 %collective-permute-start.3 = (bf16[64,512]{1,0:T(8,128)(2,1)S(1)}, bf16[64,512]{1,0:T(8,128)(2,1)S(1)}, u32[]{:S(2)}, u32[]{:S(2)}) collective-permute-start(bf16[64,512]{1,0:T(8,128)(2,1)S(1)} %reshape.40.refs_0_), channel_id=1, source_target_pairs={{0,1},{1,2},{2,3},{3,0},{4,5},{5,6},{6,7},{7,4},{8,9},{9,10},{10,1... | collective-permute-start | bytes 196616 | tf_op jit(solution)/shard_map/ppermute | solution.py:245
  15.7 3.9 %copy-start.2 = (bf16[64,512]{1,0:T(8,128)(2,1)}, bf16[64,512]{1,0:T(8,128)(2,1)S(1)}, u32[]{:S(2)}) copy-start(bf16[64,512]{1,0:T(8,128)(2,1)S(1)} %collective-permute-done.5.refs_3_) | copy-start | bytes 196612
  19.4 0.6 %copy-start.3 = (bf16[64,512]{1,0:T(8,128)(2,1)}, bf16[64,512]{1,0:T(8,128)(2,1)S(1)}, u32[]{:S(2)}) copy-start(bf16[64,512]{1,0:T(8,128)(2,1)S(1)} %collective-permute-done.4.refs_2_) | copy-start | bytes 196612
  19.6 0.6 %copy-start.4 = (bf16[64,512]{1,0:T(8,128)(2,1)}, bf16[64,512]{1,0:T(8,128)(2,1)S(1)}, u32[]{:S(2)}) copy-start(bf16[64,512]{1,0:T(8,128)(2,1)S(1)} %collective-permute-done.3.refs_1_) | copy-start | bytes 196612
  33.3 18.9 %copy-start = (f32[2,16,64,64]{3,2,1,0:T(8,128)S(1)}, f32[2,16,64,64]{3,2,1,0:T(8,128)}, u32[]{:S(2)}) copy-start(f32[2,16,64,64]{3,2,1,0:T(8,128)} %param.8) | copy-start | bytes 1572868
  34.3 3.7 %collective-permute-start.6 = (bf16[64,512]{1,0:T(8,128)(2,1)S(1)}, bf16[64,512]{1,0:T(8,128)(2,1)S(1)}, u32[]{:S(2)}, u32[]{:S(2)}) collective-permute-start(bf16[64,512]{1,0:T(8,128)(2,1)S(1)} %get-tuple-element.9), channel_id=1, source_target_pairs={{0,1},{1,2},{2,3},{3,0},{4,5},{5,6},{6,7},{7,4},{8,9},{9,10},{10,1... | collective-permute-start | bytes 196616 | tf_op jit(solution)/shard_map/ppermute | solution.py:253
  34.3 3.7 %collective-permute-start.8 = (bf16[64,512]{1,0:T(8,128)(2,1)S(1)}, bf16[64,512]{1,0:T(8,128)(2,1)S(1)}, u32[]{:S(2)}, u32[]{:S(2)}) collective-permute-start(bf16[64,512]{1,0:T(8,128)(2,1)S(1)} %get-tuple-element.10), channel_id=1, source_target_pairs={{0,3},{1,0},{2,1},{3,2},{4,7},{5,4},{6,5},{7,6},{8,11},{9,8},{10,9... | collective-permute-start | bytes 196616 | tf_op jit(solution)/shard_map/ppermute | solution.py:253
  36.1 4.3 %collective-permute-start.7 = (bf16[64,512]{1,0:T(8,128)(2,1)S(1)}, bf16[64,512]{1,0:T(8,128)(2,1)S(1)}, u32[]{:S(2)}, u32[]{:S(2)}) collective-permute-start(bf16[64,512]{1,0:T(8,128)(2,1)S(1)} %get-tuple-element.11), channel_id=1, source_target_pairs={{0,2},{1,3},{2,0},{3,1},{4,6},{5,7},{6,4},{7,5},{8,10},{9,11},{10,... | collective-permute-start | bytes 196616 | tf_op jit(solution)/shard_map/ppermute | solution.py:253
  41.7 4.8 %collective-permute-start.9 = (bf16[64,2,64]{2,0,1:T(8,128)(2,1)S(1)}, bf16[64,2,64]{2,0,1:T(8,128)(2,1)S(1)}, u32[]{:S(2)}, u32[]{:S(2)}) collective-permute-start(bf16[64,2,64]{2,0,1:T(8,128)(2,1)S(1)} %bitcast.85), channel_id=1, source_target_pairs={{0,12},{4,0},{8,4},{12,8},{1,13},{5,1},{9,5},{13,9},{2,14},{6,2},{... | collective-permute-start | bytes 49160 | tf_op jit(solution)/shard_map/ppermute | solution.py:85
  45.0 4.8 %collective-permute-start.10 = (bf16[64,2,64]{2,0,1:T(8,128)(2,1)S(1)}, bf16[64,2,64]{2,0,1:T(8,128)(2,1)S(1)}, u32[]{:S(2)}, u32[]{:S(2)}) collective-permute-start(bf16[64,2,64]{2,0,1:T(8,128)(2,1)S(1)} %bitcast.84), channel_id=1, source_target_pairs={{0,8},{4,12},{8,0},{12,4},{1,9},{5,13},{9,1},{13,5},{2,10},{6,14},... | collective-permute-start | bytes 49160 | tf_op jit(solution)/shard_map/ppermute | solution.py:85
  45.0 5.7 %collective-permute-start.11 = (bf16[64,2,64]{2,0,1:T(8,128)(2,1)S(1)}, bf16[64,2,64]{2,0,1:T(8,128)(2,1)S(1)}, u32[]{:S(2)}, u32[]{:S(2)}) collective-permute-start(bf16[64,2,64]{2,0,1:T(8,128)(2,1)S(1)} %bitcast.83), channel_id=1, source_target_pairs={{0,4},{4,8},{8,12},{12,0},{1,5},{5,9},{9,13},{13,1},{2,6},{6,10},{... | collective-permute-start | bytes 49160 | tf_op jit(solution)/shard_map/ppermute | solution.py:85

commit v9 on v6

--- a/solution.py
+++ b/solution.py
@@ -104,6 +104,40 @@
     if negate_first:
         return jnp.concatenate([-high, low], axis=1)
     return jnp.concatenate([high, -low], axis=1)
+
+
+def coil_term(coil_index, image_ref, sens_ref, measured_ref, sampled_ref, forward_ref, adjoint_ref,
+              table_re_ref, table_im_ref):
+    half_width = image_ref.shape[1] // 2
+    sens = sens_ref[coil_index].astype(jnp.float32)
+    sens_re = sens[:, :half_width]
+    sens_im = sens[:, half_width:]
+    image = image_ref[...].astype(jnp.float32)
+    image_re = image[:, :half_width]
+    image_im = image[:, half_width:]
+    coil = jnp.concatenate(
+        [sens_re * image_re - sens_im * image_im, sens_re * image_im + sens_im * image_re], axis=1
+    ).astype(jnp.bfloat16)
+    half_k = jnp.dot(coil, forward_ref[...], preferred_element_type=jnp.float32).astype(jnp.bfloat16)
+    table_re = table_re_ref[...]
+    table_im = table_im_ref[...]
+    kspace = jnp.dot(table_re, half_k, preferred_element_type=jnp.float32) + jnp.dot(
+        table_im, swap_halves(half_k, half_width, True), preferred_element_type=jnp.float32
+    )
+    residual = (kspace - measured_ref[coil_index].astype(jnp.float32)).astype(jnp.bfloat16)
+    sampled = sampled_ref[coil_index].astype(jnp.bfloat16)
+    back_half = (
+        jnp.dot(table_re * sampled, residual, preferred_element_type=jnp.float32)
+        + jnp.dot(table_im * sampled, swap_halves(residual, half_width, False), preferred_element_type=jnp.float32)
+    ).astype(jnp.bfloat16)
+    coil_back = jnp.dot(back_half, adjoint_ref[...], preferred_element_type=jnp.float32)
+    back_re = coil_back[:, :half_width]
+    back_im = coil_back[:, half_width:]
+    term = jnp.concatenate(
+        [sens_re * back_re + sens_im * back_im, sens_re * back_im - sens_im * back_re], axis=1
+    )
+
+    return term
 
 
 def coil_chain_kernel(*refs):
@@ -128,33 +162,11 @@
                 value = jnp.where(source == other, pieces[other][...], value)
             image_ref[block * rows:(block + 1) * rows, :] = value
 
-    sens = sens_ref[0].astype(jnp.float32)
-    sens_re = sens[:, :half_width]
-    sens_im = sens[:, half_width:]
-    image = image_ref[...].astype(jnp.float32)
-    image_re = image[:, :half_width]
-    image_im = image[:, half_width:]
-    coil = jnp.concatenate(
-        [sens_re * image_re - sens_im * image_im, sens_re * image_im + sens_im * image_re], axis=1
-    ).astype(jnp.bfloat16)
-    half_k = jnp.dot(coil, forward_ref[...], preferred_element_type=jnp.float32).astype(jnp.bfloat16)
-    table_re = table_re_ref[...]
-    table_im = table_im_ref[...]
-    kspace = jnp.dot(table_re, half_k, preferred_element_type=jnp.float32) + jnp.dot(
-        table_im, swap_halves(half_k, half_width, True), preferred_element_type=jnp.float32
-    )
-    residual = (kspace - measured_ref[0].astype(jnp.float32)).astype(jnp.bfloat16)
-    sampled = sampled_ref[0].astype(jnp.bfloat16)
-    back_half = (
-        jnp.dot(table_re * sampled, residual, preferred_element_type=jnp.float32)
-        + jnp.dot(table_im * sampled, swap_halves(residual, half_width, False), preferred_element_type=jnp.float32)
-    ).astype(jnp.bfloat16)
-    coil_back = jnp.dot(back_half, adjoint_ref[...], preferred_element_type=jnp.float32)
-    back_re = coil_back[:, :half_width]
-    back_im = coil_back[:, half_width:]
-    term = jnp.concatenate(
-        [sens_re * back_re + sens_im * back_im, sens_re * back_im - sens_im * back_re], axis=1
-    )
+    term = None
+    for coil_index in range(sens_ref.shape[0]):
+        one = coil_term(coil_index, image_ref, sens_ref, measured_ref, sampled_ref, forward_ref, adjoint_ref,
+                        table_re_ref, table_im_ref)
+        term = one if term is None else term + one
 
     @pl.when(step == 0)
     def _():
@@ -179,6 +191,7 @@
     rows = pieces[0].shape[0]
     whole = lambda c: (0, 0)
     per_coil = lambda c: (c, 0, 0)
+    step_coils = 2 if coils % 2 == 0 else 1
     flops = coils * 8 * height * width * width
     return pl.pallas_call(
         coil_chain_kernel,
@@ -186,13 +199,13 @@
             jax.ShapeDtypeStruct((rows, width), jnp.float32),
             jax.ShapeDtypeStruct((groups - 1, rows, width), jnp.bfloat16),
         ),
-        grid=(coils,),
+        grid=(coils // step_coils,),
         in_specs=[pl.BlockSpec((rows, width), whole)] * groups
         + [
             pl.BlockSpec(memory_space=pltpu.SMEM),
-            pl.BlockSpec((1, height, width), per_coil),
-            pl.BlockSpec((1, height, width), per_coil),
-            pl.BlockSpec((1, 1, height), per_coil),
+            pl.BlockSpec((step_coils, height, width), per_coil),
+            pl.BlockSpec((step_coils, height, width), per_coil),
+            pl.BlockSpec((step_coils, 1, height), per_coil),
             pl.BlockSpec((width, width), whole),
             pl.BlockSpec((width, width), whole),
             pl.BlockSpec((height, height), whole),

time: 52.3 us -> 51.4 us (0.983)
  Pallas kernels: 11.7 us -> 10.9 us
    pallas_call x1, Pallas kernels: 11.7 us -> 10.9 us  [coil_chain(): pl.pallas_call(coil_chain_kernel, out_shape=(jax.ShapeDtypeStruct((rows,...]
where the time goes in v9:
time: 51.4 us; the launch traced here: 51.1 us
  starting transfers between devices  15.3 us (30%)
  waiting for transfers between devices  13 us (25%)
  Pallas kernels  10.9 us (21%)
  other arithmetic  7.83 us (15%)
  local copies, waits for them, and re-layouts  3.96 us (8%)
    pallas_call x1, Pallas kernels, coil_chain(): pl.pallas_call(coil_chain_kernel, out_shape=(jax.ShapeDtypeStruct((rows,...  10.9 us
    ppermute x6, starting transfers between devices, exchange_blocks(): pieces.append(lax.ppermute(outgoing, axis, shifted(count, step)))  10.9 us
    ppermute x6, waiting for transfers between devices, exchange_blocks(): pieces.append(lax.ppermute(outgoing, axis, shifted(count, step)))  5.63 us
    ppermute x3, waiting for transfers between devices, on_device(): lax.ppermute(own_rows, 'coil', shifted(groups, step))  4.1 us
    ppermute x3, waiting for transfers between devices, on_device(): lax.ppermute(outgoing[step - 1], 'coil', shifted(groups, step))  3.25 us
    ppermute x3, starting transfers between devices, on_device(): lax.ppermute(outgoing[step - 1], 'coil', shifted(groups, step))  2.66 us
    reduce_sum x1, other arithmetic, on_device(): jnp.sum(mixing[:, :, :, :, None, None] * factors[None, None], axis=(2, 3))  2.29 us
    ppermute x3, starting transfers between devices, on_device(): lax.ppermute(own_rows, 'coil', shifted(groups, step))  1.78 us
  transfers between devices with their start and end apart: 12, of which 9 were waited for; matrix products, arithmetic and copies ran while one was open for 4% of the time, Pallas kernels for 0%

profile of v9, /device:TPU:0, one launch (start us, length us, event | category | flops | bytes accessed | tf_op | source)
XLA Modules:
  0.0 51.1 jit_solution(11443787707122739381)
XLA Ops:
  0.0 0.7 %fusion.1 = f32[4,1,16]{2,0,1:T(4,128)S(1)} fusion(f32[2,4,16]{2,1,0:T(4,128)} %param.10), kind=kLoop, calls=%fused_computation.51 | loop fusion | flops 64 | bytes 512 | tf_op jit(solution)/shard_map/neg | solution.py:239
  0.7 0.7 %slice_bitcast_fusion.5 = (f32[16,4,1]{0,1,2:T(4,128)S(1)}, f32[4,1,16]{2,0,1:T(4,128)S(1)}, f32[4,1,16]{2,0,1:T(4,128)S(1)}, f32[16,4,1]{0,1,2:T(4,128)S(1)}) fusion(f32[2,4,16]{2,1,0:T(4,128)} %param.10), kind=kLoop, calls=%fused_computation.49 | loop fusion | bytes 1536 | tf_op jit(solution)/shard_map/stack | solution.py:264
  1.4 2.3 %multiply_reduce_fusion.1 = bf16[4,2,64,64]{3,2,1,0:T(8,128)(2,1)S(1)} fusion(f32[2,16,64,64]{3,2,1,0:T(8,128)} %param.9, f32[4,1,2,16]{3,2,0,1:T(2,128)S(1)} %get-tuple-element.28, f32[4,1,2,16]{3,2,0,1:T(2,128)S(1)} %get-tuple-element.29), kind=kLoop, calls=%fused_computation.1 | loop fusion | flops 2064640 | bytes 590848 | tf_op jit(solution)/shard_map/reduce_sum | solution.py:241
  3.7 3.1 %collective-permute-start.2 = (bf16[2,64,64]{2,1,0:T(8,128)(2,1)S(1)}, bf16[2,64,64]{2,1,0:T(8,128)(2,1)S(1)}, u32[]{:S(2)}, u32[]{:S(2)}) collective-permute-start(bf16[2,64,64]{2,1,0:T(8,128)(2,1)S(1)} %get-tuple-element.16), channel_id=1, source_target_pairs={{0,4},{4,8},{8,12},{12,0},{1,5},{5,9},{9,13},{13,1},{2,6},{6,10},{... | collective-permute-start | bytes 49160 | tf_op jit(solution)/shard_map/ppermute | solution.py:85
  6.8 2.6 %collective-permute-start.1 = (bf16[2,64,64]{2,1,0:T(8,128)(2,1)S(1)}, bf16[2,64,64]{2,1,0:T(8,128)(2,1)S(1)}, u32[]{:S(2)}, u32[]{:S(2)}) collective-permute-start(bf16[2,64,64]{2,1,0:T(8,128)(2,1)S(1)} %get-tuple-element.17), channel_id=1, source_target_pairs={{0,8},{4,12},{8,0},{12,4},{1,9},{5,13},{9,1},{13,5},{2,10},{6,14},... | collective-permute-start | bytes 49160 | tf_op jit(solution)/shard_map/ppermute | solution.py:85
  9.4 1.3 %collective-permute-start = (bf16[2,64,64]{2,1,0:T(8,128)(2,1)S(1)}, bf16[2,64,64]{2,1,0:T(8,128)(2,1)S(1)}, u32[]{:S(2)}, u32[]{:S(2)}) collective-permute-start(bf16[2,64,64]{2,1,0:T(8,128)(2,1)S(1)} %get-tuple-element.18), channel_id=1, source_target_pairs={{0,12},{4,0},{8,4},{12,8},{1,13},{5,1},{9,5},{13,9},{2,14},{6,2},{... | collective-permute-start | bytes 49160 | tf_op jit(solution)/shard_map/ppermute | solution.py:85
  10.7 0.7 %fusion = f32[16,4,1]{0,1,2:T(4,128)S(1)} fusion(f32[2,4,16]{2,1,0:T(4,128)} %param.10), kind=kLoop, calls=%fused_computation.46 | loop fusion | flops 64 | bytes 512 | tf_op jit(solution)/shard_map/stack | solution.py:264
  11.4 0.7 %convert_element_type.44 = f32[1,8,256]{2,1,0:T(8,128)S(1)} convert(s32[1,8,256]{2,1,0:T(8,128)} %param.13) | non-fusion elementwise | flops 2048 | bytes 16384 | tf_op jit(solution)/shard_map/convert_element_type | solution.py:251
  13.8 1.6 %collective-permute-start.4 = (bf16[64,512]{1,0:T(8,128)(2,1)S(1)}, bf16[64,512]{1,0:T(8,128)(2,1)S(1)}, u32[]{:S(2)}, u32[]{:S(2)}) collective-permute-start(bf16[64,512]{1,0:T(8,128)(2,1)S(1)} %reshape.40.refs_0_), channel_id=1, source_target_pairs={{0,2},{1,3},{2,0},{3,1},{4,6},{5,7},{6,4},{7,5},{8,10},{9,11},{10,... | collective-permute-start | bytes 196616 | tf_op jit(solution)/shard_map/ppermute | solution.py:250
  15.7 3.7 %collective-permute-done.4.refs_2_ = bf16[64,512]{1,0:T(8,128)(2,1)S(1)} collective-permute-done((bf16[64,512]{1,0:T(8,128)(2,1)S(1)}, bf16[64,512]{1,0:T(8,128)(2,1)S(1)}, u32[]{:S(2)}, u32[]{:S(2)}) %collective-permute-start.4) | collective-permute-done | bytes 65568 | tf_op jit(solution)/shard_map/ppermute | solution.py:250
  20.2 10.9 %shard_map.91 = (f32[64,512]{1,0:T(8,128)}, bf16[3,64,512]{2,1,0:T(8,128)(2,1)}) custom-call(bf16[64,512]{1,0:T(8,128)(2,1)} %copy-done.1, bf16[64,512]{1,0:T(8,128)(2,1)} %copy-done.4, bf16[64,512]{1,0:T(8,128)(2,1)} %copy-done.3, bf16[64,512]{1,0:T(8,128)(2,1)} %copy-done.2, s32[1]{0:T(128)} %bitcast.23.refs_4_, bf16[8,256,512]{2,1,0:T(8,128)(2,1)} %refs_5_.1, ...), custom_call_target="tpu_custom_call" | custom-call | flops 4294967296 | bytes 4718592 | tf_op jit(solution)/shard_map/pallas_call | solution.py:196
  31.1 1.0 %slice_bitcast_fusion.2 = (bf16[64,512]{1,0:T(8,128)(2,1)S(1)}, bf16[64,512]{1,0:T(8,128)(2,1)S(1)}, bf16[64,512]{1,0:T(8,128)(2,1)S(1)}) fusion(bf16[3,64,512]{2,1,0:T(8,128)(2,1)} %get-tuple-element.8), kind=kLoop, calls=%fused_computation.8 | loop fusion | bytes 393216 | tf_op jit(solution)/shard_map/squeeze | solution.py:258
  32.2 1.7 %collective-permute-start.8 = (bf16[64,512]{1,0:T(8,128)(2,1)S(1)}, bf16[64,512]{1,0:T(8,128)(2,1)S(1)}, u32[]{:S(2)}, u32[]{:S(2)}) collective-permute-start(bf16[64,512]{1,0:T(8,128)(2,1)S(1)} %get-tuple-element.10), channel_id=1, source_target_pairs={{0,3},{1,0},{2,1},{3,2},{4,7},{5,4},{6,5},{7,6},{8,11},{9,8},{10,9... | collective-permute-start | bytes 196616 | tf_op jit(solution)/shard_map/ppermute | solution.py:258
  33.9 0.9 %collective-permute-start.7 = (bf16[64,512]{1,0:T(8,128)(2,1)S(1)}, bf16[64,512]{1,0:T(8,128)(2,1)S(1)}, u32[]{:S(2)}, u32[]{:S(2)}) collective-permute-start(bf16[64,512]{1,0:T(8,128)(2,1)S(1)} %get-tuple-element.11), channel_id=1, source_target_pairs={{0,2},{1,3},{2,0},{3,1},{4,6},{5,7},{6,4},{7,5},{8,10},{9,11},{10,... | collective-permute-start | bytes 196616 | tf_op jit(solution)/shard_map/ppermute | solution.py:258
  34.9 0.9 %collective-permute-done.6 = bf16[64,512]{1,0:T(8,128)(2,1)S(1)} collective-permute-done((bf16[64,512]{1,0:T(8,128)(2,1)S(1)}, bf16[64,512]{1,0:T(8,128)(2,1)S(1)}, u32[]{:S(2)}, u32[]{:S(2)}) %collective-permute-start.6) | collective-permute-done | bytes 65568 | tf_op jit(solution)/shard_map/ppermute | solution.py:258
  35.9 2.3 %collective-permute-done.7 = bf16[64,512]{1,0:T(8,128)(2,1)S(1)} collective-permute-done((bf16[64,512]{1,0:T(8,128)(2,1)S(1)}, bf16[64,512]{1,0:T(8,128)(2,1)S(1)}, u32[]{:S(2)}, u32[]{:S(2)}) %collective-permute-start.7) | collective-permute-done | bytes 65568 | tf_op jit(solution)/shard_map/ppermute | solution.py:258
  38.2 0.9 %add_convert_fusion = bf16[64,512]{1,0:T(8,128)(2,1)S(1)} fusion(bf16[64,512]{1,0:T(8,128)(2,1)S(1)} %collective-permute-done.8, bf16[64,512]{1,0:T(8,128)(2,1)S(1)} %collective-permute-done.7, f32[64,512]{1,0:T(8,128)} %get-tuple-element.7, bf16[64,512]{1,0:T(8,128)(2,1)S(1)} %collective-permute-done.6), kind=kLoop, calls=%fused_computation.4 | loop fusion | flops 229376 | bytes 393216 | tf_op jit(solution)/shard_map/convert_element_type | solution.py:261
  39.6 3.2 %collective-permute-start.9 = (bf16[64,2,64]{2,0,1:T(8,128)(2,1)S(1)}, bf16[64,2,64]{2,0,1:T(8,128)(2,1)S(1)}, u32[]{:S(2)}, u32[]{:S(2)}) collective-permute-start(bf16[64,2,64]{2,0,1:T(8,128)(2,1)S(1)} %bitcast.85), channel_id=1, source_target_pairs={{0,12},{4,0},{8,4},{12,8},{1,13},{5,1},{9,5},{13,9},{2,14},{6,2},{... | collective-permute-start | bytes 49160 | tf_op jit(solution)/shard_map/ppermute | solution.py:85
  42.8 0.6 %collective-permute-start.11 = (bf16[64,2,64]{2,0,1:T(8,128)(2,1)S(1)}, bf16[64,2,64]{2,0,1:T(8,128)(2,1)S(1)}, u32[]{:S(2)}, u32[]{:S(2)}) collective-permute-start(bf16[64,2,64]{2,0,1:T(8,128)(2,1)S(1)} %bitcast.83), channel_id=1, source_target_pairs={{0,4},{4,8},{8,12},{12,0},{1,5},{5,9},{9,13},{13,1},{2,6},{6,10},{... | collective-permute-start | bytes 49160 | tf_op jit(solution)/shard_map/ppermute | solution.py:85
  43.4 0.9 %collective-permute-done.9 = bf16[64,2,64]{2,0,1:T(8,128)(2,1)S(1)} collective-permute-done((bf16[64,2,64]{2,0,1:T(8,128)(2,1)S(1)}, bf16[64,2,64]{2,0,1:T(8,128)(2,1)S(1)}, u32[]{:S(2)}, u32[]{:S(2)}) %collective-permute-start.9) | collective-permute-done | bytes 16416 | tf_op jit(solution)/shard_map/ppermute | solution.py:85
  44.4 3.2 %collective-permute-done.10 = bf16[64,2,64]{2,0,1:T(8,128)(2,1)S(1)} collective-permute-done((bf16[64,2,64]{2,0,1:T(8,128)(2,1)S(1)}, bf16[64,2,64]{2,0,1:T(8,128)(2,1)S(1)}, u32[]{:S(2)}, u32[]{:S(2)}) %collective-permute-start.10) | collective-permute-done | bytes 16416 | tf_op jit(solution)/shard_map/ppermute | solution.py:85
  47.6 0.9 %collective-permute-done.11 = bf16[64,2,64]{2,0,1:T(8,128)(2,1)S(1)} collective-permute-done((bf16[64,2,64]{2,0,1:T(8,128)(2,1)S(1)}, bf16[64,2,64]{2,0,1:T(8,128)(2,1)S(1)}, u32[]{:S(2)}, u32[]{:S(2)}) %collective-permute-start.11) | collective-permute-done | bytes 16416 | tf_op jit(solution)/shard_map/ppermute | solution.py:85
  48.6 1.4 %multiply_reduce_fusion = f32[2,16,64,64]{3,2,1,0:T(8,128)S(1)} fusion(f32[4,64,2,64]{3,1,2,0:T(8,128)S(1)} %dynamic-slice_convert_fusion, f32[2,16,4,2]{3,2,1,0:T(4,128)S(1)} %copy.26), kind=kLoop, calls=%fused_computation | loop fusion | flops 1966080 | bytes 656384 | tf_op jit(solution)/shard_map/reduce_sum | solution.py:266
  50.0 1.1 %multiply_subtract_fusion = f32[2,16,64,64]{3,2,1,0:T(8,128)} fusion(f32[2,16,64,64]{3,2,1,0:T(8,128)S(1)} %copy-done, f32[2,16,64,64]{3,2,1,0:T(8,128)S(1)} %multiply_reduce_fusion), kind=kLoop, calls=%fused_computation.2 | loop fusion | flops 262144 | bytes 1572864 | tf_op jit(solution)/shard_map/sub | solution.py:269
  (51 shorter events, 3.5 us)
Async XLA Ops:
  3.7 9.6 %collective-permute-start.2 = (bf16[2,64,64]{2,1,0:T(8,128)(2,1)S(1)}, bf16[2,64,64]{2,1,0:T(8,128)(2,1)S(1)}, u32[]{:S(2)}, u32[]{:S(2)}) collective-permute-start(bf16[2,64,64]{2,1,0:T(8,128)(2,1)S(1)} %get-tuple-element.16), channel_id=1, source_target_pairs={{0,4},{4,8},{8,12},{12,0},{1,5},{5,9},{9,13},{13,1},{2,6},{6,10},{... | collective-permute-start | bytes 49160 | tf_op jit(solution)/shard_map/ppermute | solution.py:85
  6.8 6.5 %collective-permute-start.1 = (bf16[2,64,64]{2,1,0:T(8,128)(2,1)S(1)}, bf16[2,64,64]{2,1,0:T(8,128)(2,1)S(1)}, u32[]{:S(2)}, u32[]{:S(2)}) collective-permute-start(bf16[2,64,64]{2,1,0:T(8,128)(2,1)S(1)} %get-tuple-element.17), channel_id=1, source_target_pairs={{0,8},{4,12},{8,0},{12,4},{1,9},{5,13},{9,1},{13,5},{2,10},{6,14},... | collective-permute-start | bytes 49160 | tf_op jit(solution)/shard_map/ppermute | solution.py:85
  9.4 3.9 %collective-permute-start = (bf16[2,64,64]{2,1,0:T(8,128)(2,1)S(1)}, bf16[2,64,64]{2,1,0:T(8,128)(2,1)S(1)}, u32[]{:S(2)}, u32[]{:S(2)}) collective-permute-start(bf16[2,64,64]{2,1,0:T(8,128)(2,1)S(1)} %get-tuple-element.18), channel_id=1, source_target_pairs={{0,12},{4,0},{8,4},{12,8},{1,13},{5,1},{9,5},{13,9},{2,14},{6,2},{... | collective-permute-start | bytes 49160 | tf_op jit(solution)/shard_map/ppermute | solution.py:85
  13.7 5.9 %copy-start.1 = (bf16[64,512]{1,0:T(8,128)(2,1)}, bf16[64,512]{1,0:T(8,128)(2,1)S(1)}, u32[]{:S(2)}) copy-start(bf16[64,512]{1,0:T(8,128)(2,1)S(1)} %reshape.40.refs_0_) | copy-start | bytes 196612
  13.7 2.0 %collective-permute-start.5 = (bf16[64,512]{1,0:T(8,128)(2,1)S(1)}, bf16[64,512]{1,0:T(8,128)(2,1)S(1)}, u32[]{:S(2)}, u32[]{:S(2)}) collective-permute-start(bf16[64,512]{1,0:T(8,128)(2,1)S(1)} %reshape.40.refs_0_), channel_id=1, source_target_pairs={{0,3},{1,0},{2,1},{3,2},{4,7},{5,4},{6,5},{7,6},{8,11},{9,8},{10,9... | collective-permute-start | bytes 196616 | tf_op jit(solution)/shard_map/ppermute | solution.py:250
  13.8 5.6 %collective-permute-start.4 = (bf16[64,512]{1,0:T(8,128)(2,1)S(1)}, bf16[64,512]{1,0:T(8,128)(2,1)S(1)}, u32[]{:S(2)}, u32[]{:S(2)}) collective-permute-start(bf16[64,512]{1,0:T(8,128)(2,1)S(1)} %reshape.40.refs_0_), channel_id=1, source_target_pairs={{0,2},{1,3},{2,0},{3,1},{4,6},{5,7},{6,4},{7,5},{8,10},{9,11},{10,... | collective-permute-start | bytes 196616 | tf_op jit(solution)/shard_map/ppermute | solution.py:250
  15.3 4.3 %collective-permute-start.3 = (bf16[64,512]{1,0:T(8,128)(2,1)S(1)}, bf16[64,512]{1,0:T(8,128)(2,1)S(1)}, u32[]{:S(2)}, u32[]{:S(2)}) collective-permute-start(bf16[64,512]{1,0:T(8,128)(2,1)S(1)} %reshape.40.refs_0_), channel_id=1, source_target_pairs={{0,1},{1,2},{2,3},{3,0},{4,5},{5,6},{6,7},{7,4},{8,9},{9,10},{10,1... | collective-permute-start | bytes 196616 | tf_op jit(solution)/shard_map/ppermute | solution.py:250
  15.7 3.9 %copy-start.2 = (bf16[64,512]{1,0:T(8,128)(2,1)}, bf16[64,512]{1,0:T(8,128)(2,1)S(1)}, u32[]{:S(2)}) copy-start(bf16[64,512]{1,0:T(8,128)(2,1)S(1)} %collective-permute-done.5.refs_3_) | copy-start | bytes 196612
  19.4 0.6 %copy-start.3 = (bf16[64,512]{1,0:T(8,128)(2,1)}, bf16[64,512]{1,0:T(8,128)(2,1)S(1)}, u32[]{:S(2)}) copy-start(bf16[64,512]{1,0:T(8,128)(2,1)S(1)} %collective-permute-done.4.refs_2_) | copy-start | bytes 196612
  19.6 0.6 %copy-start.4 = (bf16[64,512]{1,0:T(8,128)(2,1)}, bf16[64,512]{1,0:T(8,128)(2,1)S(1)}, u32[]{:S(2)}) copy-start(bf16[64,512]{1,0:T(8,128)(2,1)S(1)} %collective-permute-done.3.refs_1_) | copy-start | bytes 196612
  31.1 18.9 %copy-start = (f32[2,16,64,64]{3,2,1,0:T(8,128)S(1)}, f32[2,16,64,64]{3,2,1,0:T(8,128)}, u32[]{:S(2)}) copy-start(f32[2,16,64,64]{3,2,1,0:T(8,128)} %param.9) | copy-start | bytes 1572868
  32.1 3.7 %collective-permute-start.6 = (bf16[64,512]{1,0:T(8,128)(2,1)S(1)}, bf16[64,512]{1,0:T(8,128)(2,1)S(1)}, u32[]{:S(2)}, u32[]{:S(2)}) collective-permute-start(bf16[64,512]{1,0:T(8,128)(2,1)S(1)} %get-tuple-element.9), channel_id=1, source_target_pairs={{0,1},{1,2},{2,3},{3,0},{4,5},{5,6},{6,7},{7,4},{8,9},{9,10},{10,1... | collective-permute-start | bytes 196616 | tf_op jit(solution)/shard_map/ppermute | solution.py:258
  32.2 3.7 %collective-permute-start.8 = (bf16[64,512]{1,0:T(8,128)(2,1)S(1)}, bf16[64,512]{1,0:T(8,128)(2,1)S(1)}, u32[]{:S(2)}, u32[]{:S(2)}) collective-permute-start(bf16[64,512]{1,0:T(8,128)(2,1)S(1)} %get-tuple-element.10), channel_id=1, source_target_pairs={{0,3},{1,0},{2,1},{3,2},{4,7},{5,4},{6,5},{7,6},{8,11},{9,8},{10,9... | collective-permute-start | bytes 196616 | tf_op jit(solution)/shard_map/ppermute | solution.py:258
  33.9 4.3 %collective-permute-start.7 = (bf16[64,512]{1,0:T(8,128)(2,1)S(1)}, bf16[64,512]{1,0:T(8,128)(2,1)S(1)}, u32[]{:S(2)}, u32[]{:S(2)}) collective-permute-start(bf16[64,512]{1,0:T(8,128)(2,1)S(1)} %get-tuple-element.11), channel_id=1, source_target_pairs={{0,2},{1,3},{2,0},{3,1},{4,6},{5,7},{6,4},{7,5},{8,10},{9,11},{10,... | collective-permute-start | bytes 196616 | tf_op jit(solution)/shard_map/ppermute | solution.py:258
  39.6 4.8 %collective-permute-start.9 = (bf16[64,2,64]{2,0,1:T(8,128)(2,1)S(1)}, bf16[64,2,64]{2,0,1:T(8,128)(2,1)S(1)}, u32[]{:S(2)}, u32[]{:S(2)}) collective-permute-start(bf16[64,2,64]{2,0,1:T(8,128)(2,1)S(1)} %bitcast.85), channel_id=1, source_target_pairs={{0,12},{4,0},{8,4},{12,8},{1,13},{5,1},{9,5},{13,9},{2,14},{6,2},{... | collective-permute-start | bytes 49160 | tf_op jit(solution)/shard_map/ppermute | solution.py:85
  42.8 4.8 %collective-permute-start.10 = (bf16[64,2,64]{2,0,1:T(8,128)(2,1)S(1)}, bf16[64,2,64]{2,0,1:T(8,128)(2,1)S(1)}, u32[]{:S(2)}, u32[]{:S(2)}) collective-permute-start(bf16[64,2,64]{2,0,1:T(8,128)(2,1)S(1)} %bitcast.84), channel_id=1, source_target_pairs={{0,8},{4,12},{8,0},{12,4},{1,9},{5,13},{9,1},{13,5},{2,10},{6,14},... | collective-permute-start | bytes 49160 | tf_op jit(solution)/shard_map/ppermute | solution.py:85
  42.8 5.7 %collective-permute-start.11 = (bf16[64,2,64]{2,0,1:T(8,128)(2,1)S(1)}, bf16[64,2,64]{2,0,1:T(8,128)(2,1)S(1)}, u32[]{:S(2)}, u32[]{:S(2)}) collective-permute-start(bf16[64,2,64]{2,0,1:T(8,128)(2,1)S(1)} %bitcast.83), channel_id=1, source_target_pairs={{0,4},{4,8},{8,12},{12,0},{1,5},{5,9},{9,13},{13,1},{2,6},{6,10},{... | collective-permute-start | bytes 49160 | tf_op jit(solution)/shard_map/ppermute | solution.py:85

commit v10 on v9

--- a/solution.py
+++ b/solution.py
@@ -140,28 +140,9 @@
     return term
 
 
-def coil_chain_kernel(*refs):
-    groups = len(refs) - 12
-    pieces = refs[:groups]
-    place_ref, sens_ref, measured_ref, sampled_ref, forward_ref, adjoint_ref, table_re_ref, table_im_ref = refs[
-        groups:groups + 8
-    ]
-    own_ref, send_ref = refs[groups + 8:groups + 10]
-    image_ref, total_ref = refs[groups + 10:]
-    rows = pieces[0].shape[0]
-    half_width = image_ref.shape[1] // 2
-    me = place_ref[0]
+def coil_chain_kernel(image_ref, sens_ref, measured_ref, sampled_ref, forward_ref, adjoint_ref,
+                      table_re_ref, table_im_ref, total_ref):
     step = pl.program_id(0)
-
-    @pl.when(step == 0)
-    def _():
-        for block in range(groups):
-            source = (me - block + groups) % groups
-            value = pieces[0][...]
-            for other in range(1, groups):
-                value = jnp.where(source == other, pieces[other][...], value)
-            image_ref[block * rows:(block + 1) * rows, :] = value
-
     term = None
     for coil_index in range(sens_ref.shape[0]):
         one = coil_term(coil_index, image_ref, sens_ref, measured_ref, sampled_ref, forward_ref, adjoint_ref,
@@ -176,33 +157,19 @@
     def _():
         total_ref[...] += term
 
-    @pl.when(step == pl.num_programs(0) - 1)
-    def _():
-        start = pl.multiple_of(me * rows, rows)
-        own_ref[...] = total_ref[pl.ds(start, rows), :]
-        for shift in range(1, groups):
-            start = pl.multiple_of(((me + shift) % groups) * rows, rows)
-            send_ref[shift - 1] = total_ref[pl.ds(start, rows), :].astype(jnp.bfloat16)
-
-
-def coil_chain(pieces, place, sens, measured, sampled, forward_x, adjoint_x, table_y_re, table_y_im):
+
+def coil_chain(image, sens, measured, sampled, forward_x, adjoint_x, table_y_re, table_y_im):
     coils, height, width = sens.shape
-    groups = len(pieces)
-    rows = pieces[0].shape[0]
     whole = lambda c: (0, 0)
     per_coil = lambda c: (c, 0, 0)
     step_coils = 2 if coils % 2 == 0 else 1
     flops = coils * 8 * height * width * width
     return pl.pallas_call(
         coil_chain_kernel,
-        out_shape=(
-            jax.ShapeDtypeStruct((rows, width), jnp.float32),
-            jax.ShapeDtypeStruct((groups - 1, rows, width), jnp.bfloat16),
-        ),
+        out_shape=jax.ShapeDtypeStruct((height, width), jnp.float32),
         grid=(coils // step_coils,),
-        in_specs=[pl.BlockSpec((rows, width), whole)] * groups
-        + [
-            pl.BlockSpec(memory_space=pltpu.SMEM),
+        in_specs=[
+            pl.BlockSpec((height, width), whole),
             pl.BlockSpec((step_coils, height, width), per_coil),
             pl.BlockSpec((step_coils, height, width), per_coil),
             pl.BlockSpec((step_coils, 1, height), per_coil),
@@ -211,16 +178,41 @@
             pl.BlockSpec((height, height), whole),
             pl.BlockSpec((height, height), whole),
         ],
-        out_specs=(
-            pl.BlockSpec((rows, width), whole),
-            pl.BlockSpec((groups - 1, rows, width), lambda c: (0, 0, 0)),
-        ),
-        scratch_shapes=[pltpu.VMEM((height, width), jnp.bfloat16), pltpu.VMEM((height, width), jnp.float32)],
+        out_specs=pl.BlockSpec((height, width), whole),
         compiler_params=pltpu.CompilerParams(dimension_semantics=("arbitrary",)),
         cost_estimate=pl.CostEstimate(
             flops=flops, transcendentals=0, bytes_accessed=2 * 2 * coils * height * width + 4 * height * width
         ),
-    )(*pieces, place, sens, measured, sampled, forward_x, adjoint_x, table_y_re, table_y_im)
+    )(image, sens, measured, sampled, forward_x, adjoint_x, table_y_re, table_y_im)
+
+
+def doubling_gather(value, axis):
+    count = lax.axis_size(axis)
+    me = lax.axis_index(axis)
+    span = 1
+    while span < count:
+        other = lax.ppermute(value, axis, [(i, i ^ span) for i in range(count)])
+        upper = (me & span) != 0
+        value = jnp.concatenate([jnp.where(upper, other, value), jnp.where(upper, value, other)], axis=0)
+        span *= 2
+    return value
+
+
+def halving_reduce(total, axis):
+    count = lax.axis_size(axis)
+    me = lax.axis_index(axis)
+    span = count // 2
+    while span >= 1:
+        size = total.shape[0] // 2
+        low = total[:size]
+        high = total[size:]
+        upper = (me & span) != 0
+        keep = jnp.where(upper, high, low)
+        give = jnp.where(upper, low, high)
+        other = lax.ppermute(give.astype(jnp.bfloat16), axis, [(i, i ^ span) for i in range(count)])
+        total = keep + other.astype(jnp.float32)
+        span //= 2
+    return total
 
 
 def on_device(factors, temporal, maps, kdata, masks):
@@ -246,16 +238,16 @@
     pieces_x = exchange_blocks(images, "frame")
     own_rows = jnp.transpose(pieces_x, (2, 1, 0, 3)).reshape(rows_own, 2 * width_x)
     groups = lax.axis_size("coil")
-    me_c = lax.axis_index("coil")
-    pieces = [own_rows] + [lax.ppermute(own_rows, "coil", shifted(groups, step)) for step in range(1, groups)]
     sampled = masks[0].astype(jnp.float32)[:, None, :]
-    place = jnp.reshape(me_c, (1,)).astype(jnp.int32)
-    own_total, outgoing = coil_chain(
-        pieces, place, maps, kdata[0], sampled, forward_x, adjoint_x, table_y_re, table_y_im
-    )
-    own_share = own_total
-    for step in range(1, groups):
-        own_share = own_share + lax.ppermute(outgoing[step - 1], "coil", shifted(groups, step)).astype(jnp.float32)
+    if groups & (groups - 1) == 0:
+        full_image = doubling_gather(own_rows, "coil")
+    else:
+        full_image = gather_blocks(own_rows, "coil").reshape(width_y, 2 * width_x)
+    combined = coil_chain(full_image, maps, kdata[0], sampled, forward_x, adjoint_x, table_y_re, table_y_im)
+    if groups & (groups - 1) == 0:
+        own_share = halving_reduce(combined, "coil")
+    else:
+        own_share = reduce_blocks(combined.reshape(groups, rows_own, 2 * width_x), "coil")
     outgoing = jnp.transpose(
         own_share.reshape(rows_own, 2, frames_here, width_own), (2, 0, 1, 3)
     ).astype(jnp.bfloat16)

time: 51.4 us -> 54.1 us (1.053)
  waiting for transfers between devices: 13 us -> 19 us
  starting transfers between devices: 15.3 us -> 13 us
  local copies, waits for them, and re-layouts: 3.96 us -> 2.33 us
  other arithmetic: 7.83 us -> 8.5 us
    ppermute x6, waiting for transfers between devices: 5.63 us -> 9.72 us  [exchange_blocks(): pieces.append(lax.ppermute(outgoing, axis, shifted(count, step)))]
    ppermute x6 -> x4, waiting for transfers between devices: 7.35 us -> 9.24 us  [the longest x2 4.69 us: doubling_gather(): other = lax.ppermute(value, axis, [(i, i ^ span) for i in range(count)])]
    ppermute x6 -> x4, starting transfers between devices: 4.44 us -> 3.27 us  [the longest x2 1.64 us: halving_reduce(): lax.ppermute(give.astype(jnp.bfloat16), axis, [(i, i ^ span) for i in ran...]
    ppermute x6, starting transfers between devices: 10.9 us -> 9.77 us  [exchange_blocks(): pieces.append(lax.ppermute(outgoing, axis, shifted(count, step)))]
    add x0 -> x1, other arithmetic: none -> 1.09 us  [halving_reduce(): total = keep + other.astype(jnp.float32)]
    convert_element_type x0 -> x2, other arithmetic: none -> 1.07 us  [halving_reduce(): give.astype(jnp.bfloat16)]
    squeeze x1 -> x0, local copies, waits for them, and re-layouts: 1 us -> none  [on_device(): outgoing[step - 1]]
    convert_element_type x1, other arithmetic: 0.94 us -> 0.02 us  [on_device(): outgoing = jnp.transpose(own_share.reshape(rows_own, 2, frames_here, widt...]
  transfers between devices with their start and end apart: 12 -> 10, of which waited for: 9 -> 10; matrix products, arithmetic and copies ran while one was open for 4% -> 1% of each run, Pallas kernels for 0% -> 0%
where the time goes in v10:
time: 54.1 us; the launch traced here: 53.8 us
  waiting for transfers between devices  19 us (35%)
  starting transfers between devices  13 us (24%)
  Pallas kernels  10.8 us (20%)
  other arithmetic  8.5 us (16%)
  local copies, waits for them, and re-layouts  2.33 us (4%)
    pallas_call x1, Pallas kernels, coil_chain(): pl.pallas_call(coil_chain_kernel, out_shape=jax.ShapeDtypeStruct((height,...  10.8 us
    ppermute x6, starting transfers between devices, exchange_blocks(): pieces.append(lax.ppermute(outgoing, axis, shifted(count, step)))  9.77 us
    ppermute x6, waiting for transfers between devices, exchange_blocks(): pieces.append(lax.ppermute(outgoing, axis, shifted(count, step)))  9.72 us
    ppermute x2, waiting for transfers between devices, doubling_gather(): other = lax.ppermute(value, axis, [(i, i ^ span) for i in range(count)])  4.69 us
    ppermute x2, waiting for transfers between devices, halving_reduce(): lax.ppermute(give.astype(jnp.bfloat16), axis, [(i, i ^ span) for i in ran...  4.54 us
    reduce_sum x1, other arithmetic, on_device(): jnp.sum(mixing[:, :, :, :, None, None] * factors[None, None], axis=(2, 3))  2.29 us
    ppermute x2, starting transfers between devices, halving_reduce(): lax.ppermute(give.astype(jnp.bfloat16), axis, [(i, i ^ span) for i in ran...  1.64 us
    ppermute x2, starting transfers between devices, doubling_gather(): other = lax.ppermute(value, axis, [(i, i ^ span) for i in range(count)])  1.63 us
  transfers between devices with their start and end apart: 10, of which 10 were waited for; matrix products, arithmetic and copies ran while one was open for 1% of the time, Pallas kernels for 0%

profile of v10, /device:TPU:0, one launch (start us, length us, event | category | flops | bytes accessed | tf_op | source)
XLA Modules:
  0.0 53.8 jit_solution(5249475055075355803)
XLA Ops:
  0.0 0.7 %fusion.1 = f32[4,1,16]{2,0,1:T(4,128)S(1)} fusion(f32[2,4,16]{2,1,0:T(4,128)} %param.10), kind=kLoop, calls=%fused_computation.57 | loop fusion | flops 64 | bytes 512 | tf_op jit(solution)/shard_map/neg | solution.py:231
  0.7 0.7 %slice_bitcast_fusion.2 = (f32[16,4,1]{0,1,2:T(4,128)S(1)}, f32[4,1,16]{2,0,1:T(4,128)S(1)}, f32[4,1,16]{2,0,1:T(4,128)S(1)}, f32[16,4,1]{0,1,2:T(4,128)S(1)}) fusion(f32[2,4,16]{2,1,0:T(4,128)} %param.10), kind=kLoop, calls=%fused_computation.55 | loop fusion | bytes 1536 | tf_op jit(solution)/shard_map/stack | solution.py:256
  1.4 2.3 %multiply_reduce_fusion.1 = bf16[4,2,64,64]{3,2,1,0:T(8,128)(2,1)S(1)} fusion(f32[2,16,64,64]{3,2,1,0:T(8,128)} %param.9, f32[4,1,2,16]{3,2,0,1:T(2,128)S(1)} %get-tuple-element.25, f32[4,1,2,16]{3,2,0,1:T(2,128)S(1)} %get-tuple-element.26), kind=kLoop, calls=%fused_computation.1 | loop fusion | flops 2064640 | bytes 590848 | tf_op jit(solution)/shard_map/reduce_sum | solution.py:233
  3.7 5.1 %collective-permute-start = (bf16[2,64,64]{2,1,0:T(8,128)(2,1)S(1)}, bf16[2,64,64]{2,1,0:T(8,128)(2,1)S(1)}, u32[]{:S(2)}, u32[]{:S(2)}) collective-permute-start(bf16[2,64,64]{2,1,0:T(8,128)(2,1)S(1)} %get-tuple-element.15), channel_id=1, source_target_pairs={{0,12},{4,0},{8,4},{12,8},{1,13},{5,1},{9,5},{13,9},{2,14},{6,2},{... | collective-permute-start | bytes 49160 | tf_op jit(solution)/shard_map/ppermute | solution.py:85
  8.8 1.0 %collective-permute-start.1 = (bf16[2,64,64]{2,1,0:T(8,128)(2,1)S(1)}, bf16[2,64,64]{2,1,0:T(8,128)(2,1)S(1)}, u32[]{:S(2)}, u32[]{:S(2)}) collective-permute-start(bf16[2,64,64]{2,1,0:T(8,128)(2,1)S(1)} %get-tuple-element.14), channel_id=1, source_target_pairs={{0,8},{4,12},{8,0},{12,4},{1,9},{5,13},{9,1},{13,5},{2,10},{6,14},... | collective-permute-start | bytes 49160 | tf_op jit(solution)/shard_map/ppermute | solution.py:85
  10.5 3.4 %collective-permute-done.1 = bf16[2,64,64]{2,1,0:T(8,128)(2,1)S(1)} collective-permute-done((bf16[2,64,64]{2,1,0:T(8,128)(2,1)S(1)}, bf16[2,64,64]{2,1,0:T(8,128)(2,1)S(1)}, u32[]{:S(2)}, u32[]{:S(2)}) %collective-permute-start.1) | collective-permute-done | bytes 16416 | tf_op jit(solution)/shard_map/ppermute | solution.py:85
  13.9 0.7 %collective-permute-done.2 = bf16[2,64,64]{2,1,0:T(8,128)(2,1)S(1)} collective-permute-done((bf16[2,64,64]{2,1,0:T(8,128)(2,1)S(1)}, bf16[2,64,64]{2,1,0:T(8,128)(2,1)S(1)}, u32[]{:S(2)}, u32[]{:S(2)}) %collective-permute-start.2) | collective-permute-done | bytes 16416 | tf_op jit(solution)/shard_map/ppermute | solution.py:85
  15.0 1.2 %collective-permute-done.3 = bf16[64,512]{1,0:T(8,128)(2,1)S(1)} collective-permute-done((bf16[64,512]{1,0:T(8,128)(2,1)S(1)}, bf16[64,512]{1,0:T(8,128)(2,1)S(1)}, u32[]{:S(2)}, u32[]{:S(2)}) %collective-permute-start.3) | collective-permute-done | bytes 65568 | tf_op jit(solution)/shard_map/ppermute | solution.py:194
  16.3 1.6 %collective-permute-start.4 = (bf16[128,512]{1,0:T(8,128)(2,1)S(1)}, bf16[128,512]{1,0:T(8,128)(2,1)S(1)}, u32[]{:S(2)}, u32[]{:S(2)}) collective-permute-start(bf16[128,512]{1,0:T(8,128)(2,1)S(1)} %pad_maximum_fusion.1), channel_id=1, source_target_pairs={{0,2},{1,3},{2,0},{3,1},{4,6},{5,7},{6,4},{7,5},{8,10},{9,11},{10,... | collective-permute-start | bytes 393224 | tf_op jit(solution)/shard_map/ppermute | solution.py:194
  18.4 3.5 %collective-permute-done.4 = bf16[128,512]{1,0:T(8,128)(2,1)S(1)} collective-permute-done((bf16[128,512]{1,0:T(8,128)(2,1)S(1)}, bf16[128,512]{1,0:T(8,128)(2,1)S(1)}, u32[]{:S(2)}, u32[]{:S(2)}) %collective-permute-start.4) | collective-permute-done | bytes 131104 | tf_op jit(solution)/shard_map/ppermute | solution.py:194
  21.9 0.7 %pad_maximum_fusion.image_ref = bf16[256,512]{1,0:T(8,128)(2,1)} fusion(bf16[128,512]{1,0:T(8,128)(2,1)S(1)} %get-tuple-element.6, bf16[128,512]{1,0:T(8,128)(2,1)S(1)} %get-tuple-element.5), kind=kLoop, calls=%fused_computation.3 | loop fusion | flops 524288 | bytes 524288 | tf_op jit(solution)/shard_map/concatenate | solution.py:196
  22.7 10.8 %shard_map.91 = f32[256,512]{1,0:T(8,128)} custom-call(bf16[256,512]{1,0:T(8,128)(2,1)} %pad_maximum_fusion.image_ref, bf16[8,256,512]{2,1,0:T(8,128)(2,1)} %sens_ref.1, bf16[8,256,512]{2,1,0:T(8,128)(2,1)} %bitcast.80, f32[8,1,256]{2,1,0:T(1,128)} %bitcast.79, bf16[512,512]{1,0:T(8,128)(2,1)} %constant.80.clone.forward_ref, ...), custom_call_target="tpu_custom_call" | custom-call | flops 4294967296 | bytes 4718592 | tf_op jit(solution)/shard_map/pallas_call | solution.py:167
  33.5 1.1 %select_convert_fusion = bf16[128,512]{1,0:T(8,128)(2,1)S(1)} fusion(f32[256,512]{1,0:T(8,128)} %shard_map.91, pred[]{:T(512)S(6)} %ne.35), kind=kLoop, calls=%fused_computation.5 | loop fusion | flops 65536 | bytes 393217 | tf_op jit(solution)/shard_map/convert_element_type | solution.py:212
  34.5 1.6 %collective-permute-start.5 = (bf16[128,512]{1,0:T(8,128)(2,1)S(1)}, bf16[128,512]{1,0:T(8,128)(2,1)S(1)}, u32[]{:S(2)}, u32[]{:S(2)}) collective-permute-start(bf16[128,512]{1,0:T(8,128)(2,1)S(1)} %select_convert_fusion), channel_id=1, source_target_pairs={{0,2},{1,3},{2,0},{3,1},{4,6},{5,7},{6,4},{7,5},{8,10},{9,11},{10,... | collective-permute-start | bytes 393224 | tf_op jit(solution)/shard_map/ppermute | solution.py:212
  36.1 3.4 %collective-permute-done.5 = bf16[128,512]{1,0:T(8,128)(2,1)S(1)} collective-permute-done((bf16[128,512]{1,0:T(8,128)(2,1)S(1)}, bf16[128,512]{1,0:T(8,128)(2,1)S(1)}, u32[]{:S(2)}, u32[]{:S(2)}) %collective-permute-start.5) | collective-permute-done | bytes 131104 | tf_op jit(solution)/shard_map/ppermute | solution.py:212
  39.6 1.1 %convert_add_fusion = f32[128,512]{1,0:T(8,128)S(1)} fusion(bf16[128,512]{1,0:T(8,128)(2,1)S(1)} %collective-permute-done.5, f32[256,512]{1,0:T(8,128)} %shard_map.91, pred[]{:T(512)S(6)} %ne.35), kind=kLoop, calls=%fused_computation.4 | loop fusion | flops 196608 | bytes 917505 | tf_op jit(solution)/shard_map/add | solution.py:213
  40.9 1.1 %collective-permute-done.6 = bf16[64,512]{1,0:T(8,128)(2,1)S(1)} collective-permute-done((bf16[64,512]{1,0:T(8,128)(2,1)S(1)}, bf16[64,512]{1,0:T(8,128)(2,1)S(1)}, u32[]{:S(2)}, u32[]{:S(2)}) %collective-permute-start.6) | collective-permute-done | bytes 65568 | tf_op jit(solution)/shard_map/ppermute | solution.py:212
  42.5 3.0 %collective-permute-start.7 = (bf16[64,2,64]{2,0,1:T(8,128)(2,1)S(1)}, bf16[64,2,64]{2,0,1:T(8,128)(2,1)S(1)}, u32[]{:S(2)}, u32[]{:S(2)}) collective-permute-start(bf16[64,2,64]{2,0,1:T(8,128)(2,1)S(1)} %bitcast.78), channel_id=1, source_target_pairs={{0,12},{4,0},{8,4},{12,8},{1,13},{5,1},{9,5},{13,9},{2,14},{6,2},{... | collective-permute-start | bytes 49160 | tf_op jit(solution)/shard_map/ppermute | solution.py:85
  45.5 0.6 %collective-permute-start.9 = (bf16[64,2,64]{2,0,1:T(8,128)(2,1)S(1)}, bf16[64,2,64]{2,0,1:T(8,128)(2,1)S(1)}, u32[]{:S(2)}, u32[]{:S(2)}) collective-permute-start(bf16[64,2,64]{2,0,1:T(8,128)(2,1)S(1)} %bitcast.76), channel_id=1, source_target_pairs={{0,4},{4,8},{8,12},{12,0},{1,5},{5,9},{9,13},{13,1},{2,6},{6,10},{... | collective-permute-start | bytes 49160 | tf_op jit(solution)/shard_map/ppermute | solution.py:85
  46.2 1.0 %collective-permute-done.7 = bf16[64,2,64]{2,0,1:T(8,128)(2,1)S(1)} collective-permute-done((bf16[64,2,64]{2,0,1:T(8,128)(2,1)S(1)}, bf16[64,2,64]{2,0,1:T(8,128)(2,1)S(1)}, u32[]{:S(2)}, u32[]{:S(2)}) %collective-permute-start.7) | collective-permute-done | bytes 16416 | tf_op jit(solution)/shard_map/ppermute | solution.py:85
  47.2 3.3 %collective-permute-done.8 = bf16[64,2,64]{2,0,1:T(8,128)(2,1)S(1)} collective-permute-done((bf16[64,2,64]{2,0,1:T(8,128)(2,1)S(1)}, bf16[64,2,64]{2,0,1:T(8,128)(2,1)S(1)}, u32[]{:S(2)}, u32[]{:S(2)}) %collective-permute-start.8) | collective-permute-done | bytes 16416 | tf_op jit(solution)/shard_map/ppermute | solution.py:85
  50.5 0.7 %collective-permute-done.9 = bf16[64,2,64]{2,0,1:T(8,128)(2,1)S(1)} collective-permute-done((bf16[64,2,64]{2,0,1:T(8,128)(2,1)S(1)}, bf16[64,2,64]{2,0,1:T(8,128)(2,1)S(1)}, u32[]{:S(2)}, u32[]{:S(2)}) %collective-permute-start.9) | collective-permute-done | bytes 16416 | tf_op jit(solution)/shard_map/ppermute | solution.py:85
  51.3 1.4 %multiply_reduce_fusion = f32[2,16,64,64]{3,2,1,0:T(8,128)S(1)} fusion(f32[4,64,2,64]{3,1,2,0:T(8,128)S(1)} %dynamic-slice_convert_fusion, f32[2,16,4,2]{3,2,1,0:T(4,128)S(1)} %copy.26), kind=kLoop, calls=%fused_computation | loop fusion | flops 1966080 | bytes 656384 | tf_op jit(solution)/shard_map/reduce_sum | solution.py:258
  52.7 1.1 %multiply_subtract_fusion = f32[2,16,64,64]{3,2,1,0:T(8,128)} fusion(f32[2,16,64,64]{3,2,1,0:T(8,128)S(1)} %copy-done, f32[2,16,64,64]{3,2,1,0:T(8,128)S(1)} %multiply_reduce_fusion), kind=kLoop, calls=%fused_computation.2 | loop fusion | flops 262144 | bytes 1572864 | tf_op jit(solution)/shard_map/sub | solution.py:261
  (49 shorter events, 2.5 us)
Async XLA Ops:
  0.0 17.8 %copy-start.2 = (s32[1,8,256]{2,1,0:T(8,128)S(1)}, s32[1,8,256]{2,1,0:T(8,128)}, u32[]{:S(2)}) copy-start(s32[1,8,256]{2,1,0:T(8,128)} %param.13) | copy-start | bytes 24580
  3.7 6.7 %collective-permute-start = (bf16[2,64,64]{2,1,0:T(8,128)(2,1)S(1)}, bf16[2,64,64]{2,1,0:T(8,128)(2,1)S(1)}, u32[]{:S(2)}, u32[]{:S(2)}) collective-permute-start(bf16[2,64,64]{2,1,0:T(8,128)(2,1)S(1)} %get-tuple-element.15), channel_id=1, source_target_pairs={{0,12},{4,0},{8,4},{12,8},{1,13},{5,1},{9,5},{13,9},{2,14},{6,2},{... | collective-permute-start | bytes 49160 | tf_op jit(solution)/shard_map/ppermute | solution.py:85
  8.8 5.7 %collective-permute-start.2 = (bf16[2,64,64]{2,1,0:T(8,128)(2,1)S(1)}, bf16[2,64,64]{2,1,0:T(8,128)(2,1)S(1)}, u32[]{:S(2)}, u32[]{:S(2)}) collective-permute-start(bf16[2,64,64]{2,1,0:T(8,128)(2,1)S(1)} %get-tuple-element.13), channel_id=1, source_target_pairs={{0,4},{4,8},{8,12},{12,0},{1,5},{5,9},{9,13},{13,1},{2,6},{6,10},{... | collective-permute-start | bytes 49160 | tf_op jit(solution)/shard_map/ppermute | solution.py:85
  8.8 5.0 %collective-permute-start.1 = (bf16[2,64,64]{2,1,0:T(8,128)(2,1)S(1)}, bf16[2,64,64]{2,1,0:T(8,128)(2,1)S(1)}, u32[]{:S(2)}, u32[]{:S(2)}) collective-permute-start(bf16[2,64,64]{2,1,0:T(8,128)(2,1)S(1)} %get-tuple-element.14), channel_id=1, source_target_pairs={{0,8},{4,12},{8,0},{12,4},{1,9},{5,13},{9,1},{13,5},{2,10},{6,14},... | collective-permute-start | bytes 49160 | tf_op jit(solution)/shard_map/ppermute | solution.py:85
  14.9 1.3 %collective-permute-start.3 = (bf16[64,512]{1,0:T(8,128)(2,1)S(1)}, bf16[64,512]{1,0:T(8,128)(2,1)S(1)}, u32[]{:S(2)}, u32[]{:S(2)}) collective-permute-start(bf16[64,512]{1,0:T(8,128)(2,1)S(1)} %reshape.37), channel_id=1, source_target_pairs={{0,1},{1,0},{2,3},{3,2},{4,5},{5,4},{6,7},{7,6},{8,9},{9,8},{10,11... | collective-permute-start | bytes 196616 | tf_op jit(solution)/shard_map/ppermute | solution.py:194
  16.3 5.6 %collective-permute-start.4 = (bf16[128,512]{1,0:T(8,128)(2,1)S(1)}, bf16[128,512]{1,0:T(8,128)(2,1)S(1)}, u32[]{:S(2)}, u32[]{:S(2)}) collective-permute-start(bf16[128,512]{1,0:T(8,128)(2,1)S(1)} %pad_maximum_fusion.1), channel_id=1, source_target_pairs={{0,2},{1,3},{2,0},{3,1},{4,6},{5,7},{6,4},{7,5},{8,10},{9,11},{10,... | collective-permute-start | bytes 393224 | tf_op jit(solution)/shard_map/ppermute | solution.py:194
  22.7 13.4 %copy-start.1 = (f32[2,4,16]{2,1,0:T(4,128)S(1)}, f32[2,4,16]{2,1,0:T(4,128)}, u32[]{:S(2)}) copy-start(f32[2,4,16]{2,1,0:T(4,128)} %param.10) | copy-start | bytes 1540
  34.5 5.0 %collective-permute-start.5 = (bf16[128,512]{1,0:T(8,128)(2,1)S(1)}, bf16[128,512]{1,0:T(8,128)(2,1)S(1)}, u32[]{:S(2)}, u32[]{:S(2)}) collective-permute-start(bf16[128,512]{1,0:T(8,128)(2,1)S(1)} %select_convert_fusion), channel_id=1, source_target_pairs={{0,2},{1,3},{2,0},{3,1},{4,6},{5,7},{6,4},{7,5},{8,10},{9,11},{10,... | collective-permute-start | bytes 393224 | tf_op jit(solution)/shard_map/ppermute | solution.py:212
  40.6 12.1 %copy-start = (f32[2,16,64,64]{3,2,1,0:T(8,128)S(1)}, f32[2,16,64,64]{3,2,1,0:T(8,128)}, u32[]{:S(2)}) copy-start(f32[2,16,64,64]{3,2,1,0:T(8,128)} %param.9) | copy-start | bytes 1572868
  40.7 1.3 %collective-permute-start.6 = (bf16[64,512]{1,0:T(8,128)(2,1)S(1)}, bf16[64,512]{1,0:T(8,128)(2,1)S(1)}, u32[]{:S(2)}, u32[]{:S(2)}) collective-permute-start(bf16[64,512]{1,0:T(8,128)(2,1)S(1)} %select_convert_fusion.1), channel_id=1, source_target_pairs={{0,1},{1,0},{2,3},{3,2},{4,5},{5,4},{6,7},{7,6},{8,9},{9,8},{10,11... | collective-permute-start | bytes 196616 | tf_op jit(solution)/shard_map/ppermute | solution.py:212
  42.5 4.7 %collective-permute-start.7 = (bf16[64,2,64]{2,0,1:T(8,128)(2,1)S(1)}, bf16[64,2,64]{2,0,1:T(8,128)(2,1)S(1)}, u32[]{:S(2)}, u32[]{:S(2)}) collective-permute-start(bf16[64,2,64]{2,0,1:T(8,128)(2,1)S(1)} %bitcast.78), channel_id=1, source_target_pairs={{0,12},{4,0},{8,4},{12,8},{1,13},{5,1},{9,5},{13,9},{2,14},{6,2},{... | collective-permute-start | bytes 49160 | tf_op jit(solution)/shard_map/ppermute | solution.py:85
  45.5 5.0 %collective-permute-start.8 = (bf16[64,2,64]{2,0,1:T(8,128)(2,1)S(1)}, bf16[64,2,64]{2,0,1:T(8,128)(2,1)S(1)}, u32[]{:S(2)}, u32[]{:S(2)}) collective-permute-start(bf16[64,2,64]{2,0,1:T(8,128)(2,1)S(1)} %bitcast.77), channel_id=1, source_target_pairs={{0,8},{4,12},{8,0},{12,4},{1,9},{5,13},{9,1},{13,5},{2,10},{6,14},... | collective-permute-start | bytes 49160 | tf_op jit(solution)/shard_map/ppermute | solution.py:85
  45.5 5.7 %collective-permute-start.9 = (bf16[64,2,64]{2,0,1:T(8,128)(2,1)S(1)}, bf16[64,2,64]{2,0,1:T(8,128)(2,1)S(1)}, u32[]{:S(2)}, u32[]{:S(2)}) collective-permute-start(bf16[64,2,64]{2,0,1:T(8,128)(2,1)S(1)} %bitcast.76), channel_id=1, source_target_pairs={{0,4},{4,8},{8,12},{12,0},{1,5},{5,9},{9,13},{13,1},{2,6},{6,10},{... | collective-permute-start | bytes 49160 | tf_op jit(solution)/shard_map/ppermute | solution.py:85

commit v11 on v9

--- a/solution.py
+++ b/solution.py
@@ -238,9 +238,14 @@
     mixing = jnp.stack(
         [jnp.stack([time_re, -time_im], axis=1), jnp.stack([time_im, time_re], axis=1)], axis=1
     )
-    images = jnp.sum(
-        mixing[:, :, :, :, None, None] * factors[None, None], axis=(2, 3)
-    ).astype(jnp.bfloat16)
+    parts, ranks, rows_here, cols_here = factors.shape
+    frames_all = mixing.shape[0]
+    images = jnp.dot(
+        mixing.reshape(frames_all * 2, parts * ranks),
+        factors.reshape(parts * ranks, rows_here * cols_here),
+        precision=lax.Precision.HIGHEST,
+        preferred_element_type=jnp.float32,
+    ).reshape(frames_all, 2, rows_here, cols_here).astype(jnp.bfloat16)
     frames_here = images.shape[0]
     width_own = images.shape[3]
     pieces_x = exchange_blocks(images, "frame")
@@ -257,15 +262,18 @@
     for step in range(1, groups):
         own_share = own_share + lax.ppermute(outgoing[step - 1], "coil", shifted(groups, step)).astype(jnp.float32)
     outgoing = jnp.transpose(
-        own_share.reshape(rows_own, 2, frames_here, width_own), (2, 0, 1, 3)
+        own_share.reshape(rows_own, 2, frames_here, width_own), (2, 1, 0, 3)
     ).astype(jnp.bfloat16)
     returned = exchange_blocks(outgoing, "frame").astype(jnp.float32)
     weights = jnp.stack(
         [jnp.stack([time_re.T, time_im.T], axis=2), jnp.stack([-time_im.T, time_re.T], axis=2)], axis=0
     )
-    gradient = jnp.sum(
-        weights[:, :, :, None, :, None] * returned[None, None], axis=(2, 4)
-    )
+    gradient = jnp.dot(
+        weights.reshape(parts * ranks, frames_all * 2),
+        returned.reshape(frames_all * 2, rows_here * cols_here),
+        precision=lax.Precision.HIGHEST,
+        preferred_element_type=jnp.float32,
+    ).reshape(factors.shape)
     return factors - 0.5 * gradient
 
 

time: 51.4 us -> 53.1 us (1.033)
  other arithmetic: 7.83 us -> 1.64 us
  local copies, waits for them, and re-layouts: 3.96 us -> 8.85 us
  matrix products: 0 us -> 2.33 us
  waiting for transfers between devices: 13 us -> 15.3 us
  starting transfers between devices: 15.3 us -> 13.7 us
    reduce_sum x2 -> x0, other arithmetic: 3.65 us -> none  [the longest x1 2.29 us: on_device(): jnp.sum(mixing[:, :, :, :, None, None] * factors[None, None], axis=(2, 3))]
    ppermute x6, waiting for transfers between devices: 5.63 us -> 8.39 us  [exchange_blocks(): pieces.append(lax.ppermute(outgoing, axis, shifted(count, step)))]
    dot_general x0 -> x2, matrix products: none -> 2.33 us  [the longest x1 1.2 us: on_device(): jnp.dot(mixing.reshape(frames_all * 2, parts * ranks), factors.reshape(pa...]
    reshape x0 -> x2, local copies, waits for them, and re-layouts: none -> 1.76 us  [the longest x1 1.58 us: on_device(): factors.reshape(parts * ranks, rows_here * cols_here)]
    ppermute x6, starting transfers between devices: 10.9 us -> 9.23 us  [exchange_blocks(): pieces.append(lax.ppermute(outgoing, axis, shifted(count, step)))]
    sub x0 -> x1, local copies, waits for them, and re-layouts: none -> 1.28 us  [on_device(): return factors - 0.5 * gradient]
    sub x1 -> x0, other arithmetic: 1.13 us -> none  [on_device(): return factors - 0.5 * gradient]
    concatenate x2, local copies, waits for them, and re-layouts: 0.02 us -> 0.85 us  [by_sender(): doubled = jnp.concatenate([ring, ring], axis=0)]
  transfers between devices with their start and end apart: 12 -> 12, of which waited for: 9 -> 10; matrix products, arithmetic and copies ran while one was open for 4% -> 1% of each run, Pallas kernels for 0% -> 0%
where the time goes in v11:
time: 53.1 us; the launch traced here: 52.8 us
  waiting for transfers between devices  15.3 us (29%)
  starting transfers between devices  13.7 us (26%)
  Pallas kernels  10.9 us (21%)
  local copies, waits for them, and re-layouts  8.85 us (17%)
  matrix products  2.33 us (4%)
  other arithmetic  1.64 us (3%)
    pallas_call x1, Pallas kernels, coil_chain(): pl.pallas_call(coil_chain_kernel, out_shape=(jax.ShapeDtypeStruct((rows,...  10.9 us
    ppermute x6, starting transfers between devices, exchange_blocks(): pieces.append(lax.ppermute(outgoing, axis, shifted(count, step)))  9.23 us
    ppermute x6, waiting for transfers between devices, exchange_blocks(): pieces.append(lax.ppermute(outgoing, axis, shifted(count, step)))  8.39 us
    ppermute x3, waiting for transfers between devices, on_device(): lax.ppermute(own_rows, 'coil', shifted(groups, step))  3.48 us
    ppermute x3, waiting for transfers between devices, on_device(): lax.ppermute(outgoing[step - 1], 'coil', shifted(groups, step))  3.38 us
    ppermute x3, starting transfers between devices, on_device(): lax.ppermute(outgoing[step - 1], 'coil', shifted(groups, step))  2.65 us
    ppermute x3, starting transfers between devices, on_device(): lax.ppermute(own_rows, 'coil', shifted(groups, step))  1.78 us
    reshape x1, local copies, waits for them, and re-layouts, on_device(): factors.reshape(parts * ranks, rows_here * cols_here)  1.58 us
  transfers between devices with their start and end apart: 12, of which 10 were waited for; matrix products, arithmetic and copies ran while one was open for 1% of the time, Pallas kernels for 0%

profile of v11, /device:TPU:0, one launch (start us, length us, event | category | flops | bytes accessed | tf_op | source)
XLA Modules:
  0.0 52.8 jit_solution(12239799514634703967)
XLA Ops:
  0.0 0.7 %fusion.12 = f32[4,1,16]{2,0,1:T(4,128)S(1)} fusion(f32[2,4,16]{2,1,0:T(4,128)} %param.10), kind=kLoop, calls=%fused_computation.55 | loop fusion | flops 64 | bytes 512 | tf_op jit(solution)/shard_map/neg | solution.py:239
  0.7 0.7 %slice_bitcast_fusion.5 = (f32[16,4,1]{0,1,2:T(4,128)S(1)}, f32[4,1,16]{2,0,1:T(4,128)S(1)}, f32[4,1,16]{2,0,1:T(4,128)S(1)}, f32[16,4,1]{0,1,2:T(4,128)S(1)}) fusion(f32[2,4,16]{2,1,0:T(4,128)} %param.10), kind=kLoop, calls=%fused_computation.51 | loop fusion | bytes 1536 | tf_op jit(solution)/shard_map/stack | solution.py:269
  1.6 1.6 %reshape.53 = f32[32,4096]{1,0:T(8,128)S(1)} reshape(f32[2,16,64,64]{3,2,1,0:T(8,128)} %param.9) | data formatting | bytes 1048576 | tf_op jit(solution)/shard_map/reshape | solution.py:245
  3.6 1.2 %convolution_convert_fusion = bf16[4,2,64,64]{3,0,2,1:T(4,128)(2,1)S(1)} fusion(f32[64,64,32]{1,0,2:T(8,128)S(1)} %dot_general.15, f32[4,1,32]{2,0,1:T(4,128)S(1)} %stack.74, f32[4,1,32]{2,0,1:T(4,128)S(1)} %stack.72), kind=kOutput, calls=%fused_computation.2 | convolution fusion | flops 12615936 | bytes 590848 | tf_op jit(solution)/shard_map/dot_general | solution.py:243
  5.1 5.1 %collective-permute-start = (bf16[2,64,64]{2,1,0:T(8,128)(2,1)S(1)}, bf16[2,64,64]{2,1,0:T(8,128)(2,1)S(1)}, u32[]{:S(2)}, u32[]{:S(2)}) collective-permute-start(bf16[2,64,64]{2,1,0:T(8,128)(2,1)S(1)} %bitcast.108), channel_id=1, source_target_pairs={{0,12},{4,0},{8,4},{12,8},{1,13},{5,1},{9,5},{13,9},{2,14},{6,2},{... | collective-permute-start | bytes 49160 | tf_op jit(solution)/shard_map/ppermute | solution.py:85
  10.3 1.0 %collective-permute-start.2 = (bf16[2,64,64]{2,1,0:T(8,128)(2,1)S(1)}, bf16[2,64,64]{2,1,0:T(8,128)(2,1)S(1)}, u32[]{:S(2)}, u32[]{:S(2)}) collective-permute-start(bf16[2,64,64]{2,1,0:T(8,128)(2,1)S(1)} %bitcast.112), channel_id=1, source_target_pairs={{0,4},{4,8},{8,12},{12,0},{1,5},{5,9},{9,13},{13,1},{2,6},{6,10},{... | collective-permute-start | bytes 49160 | tf_op jit(solution)/shard_map/ppermute | solution.py:85
  11.9 3.2 %collective-permute-done.1 = bf16[2,64,64]{2,1,0:T(8,128)(2,1)S(1)} collective-permute-done((bf16[2,64,64]{2,1,0:T(8,128)(2,1)S(1)}, bf16[2,64,64]{2,1,0:T(8,128)(2,1)S(1)}, u32[]{:S(2)}, u32[]{:S(2)}) %collective-permute-start.1) | collective-permute-done | bytes 16416 | tf_op jit(solution)/shard_map/ppermute | solution.py:85
  15.1 0.9 %collective-permute-done.2 = bf16[2,64,64]{2,1,0:T(8,128)(2,1)S(1)} collective-permute-done((bf16[2,64,64]{2,1,0:T(8,128)(2,1)S(1)}, bf16[2,64,64]{2,1,0:T(8,128)(2,1)S(1)}, u32[]{:S(2)}, u32[]{:S(2)}) %collective-permute-start.2) | collective-permute-done | bytes 16416 | tf_op jit(solution)/shard_map/ppermute | solution.py:85
  16.1 0.8 %concatenate.10 = bf16[8,2,64,64]{3,0,2,1:T(8,128)(2,1)S(1)} concatenate(bf16[1,2,64,64]{3,0,2,1:T(2,128)(2,1)S(1)} %get-tuple-element.19, bf16[1,2,64,64]{3,0,2,1:T(2,128)(2,1)S(1)} %copy.26, bf16[1,2,64,64]{3,0,2,1:T(2,128)(2,1)S(1)} %copy.27, bf16[1,2,64,64]{3,0,2,1:T(2,128)(2,1)S(1)} %copy.28, bf16[1,2,64,64]{3,0,2,1:T(2,128)(2,1)S(1)} %get-tuple-element.19, ...), dimensions={0} | concatenate | bytes 262144 | tf_op jit(solution)/shard_map/concatenate | solution.py:64
  17.3 1.6 %collective-permute-start.4 = (bf16[64,512]{1,0:T(8,128)(2,1)S(1)}, bf16[64,512]{1,0:T(8,128)(2,1)S(1)}, u32[]{:S(2)}, u32[]{:S(2)}) collective-permute-start(bf16[64,512]{1,0:T(8,128)(2,1)S(1)} %reshape.54.refs_0_), channel_id=1, source_target_pairs={{0,2},{1,3},{2,0},{3,1},{4,6},{5,7},{6,4},{7,5},{8,10},{9,11},{10,... | collective-permute-start | bytes 196616 | tf_op jit(solution)/shard_map/ppermute | solution.py:255
  19.6 3.3 %collective-permute-done.4.refs_2_ = bf16[64,512]{1,0:T(8,128)(2,1)S(1)} collective-permute-done((bf16[64,512]{1,0:T(8,128)(2,1)S(1)}, bf16[64,512]{1,0:T(8,128)(2,1)S(1)}, u32[]{:S(2)}, u32[]{:S(2)}) %collective-permute-start.4) | collective-permute-done | bytes 65568 | tf_op jit(solution)/shard_map/ppermute | solution.py:255
  23.7 10.9 %shard_map.91 = (f32[64,512]{1,0:T(8,128)}, bf16[3,64,512]{2,1,0:T(8,128)(2,1)}) custom-call(bf16[64,512]{1,0:T(8,128)(2,1)} %copy-done.1, bf16[64,512]{1,0:T(8,128)(2,1)} %copy-done.6, bf16[64,512]{1,0:T(8,128)(2,1)} %copy-done.5, bf16[64,512]{1,0:T(8,128)(2,1)} %copy-done.4, s32[1]{0:T(128)} %bitcast.24.refs_4_, bf16[8,256,512]{2,1,0:T(8,128)(2,1)} %refs_5_.1, ...), custom_call_target="tpu_custom_call" | custom-call | flops 4294967296 | bytes 4718592 | tf_op jit(solution)/shard_map/pallas_call | solution.py:196
  34.6 1.0 %slice_bitcast_fusion.2 = (bf16[64,512]{1,0:T(8,128)(2,1)S(1)}, bf16[64,512]{1,0:T(8,128)(2,1)S(1)}, bf16[64,512]{1,0:T(8,128)(2,1)S(1)}) fusion(bf16[3,64,512]{2,1,0:T(8,128)(2,1)} %get-tuple-element.8), kind=kLoop, calls=%fused_computation.11 | loop fusion | bytes 393216 | tf_op jit(solution)/shard_map/squeeze | solution.py:263
  35.7 1.7 %collective-permute-start.8 = (bf16[64,512]{1,0:T(8,128)(2,1)S(1)}, bf16[64,512]{1,0:T(8,128)(2,1)S(1)}, u32[]{:S(2)}, u32[]{:S(2)}) collective-permute-start(bf16[64,512]{1,0:T(8,128)(2,1)S(1)} %get-tuple-element.10), channel_id=1, source_target_pairs={{0,3},{1,0},{2,1},{3,2},{4,7},{5,4},{6,5},{7,6},{8,11},{9,8},{10,9... | collective-permute-start | bytes 196616 | tf_op jit(solution)/shard_map/ppermute | solution.py:263
  37.4 0.9 %collective-permute-start.7 = (bf16[64,512]{1,0:T(8,128)(2,1)S(1)}, bf16[64,512]{1,0:T(8,128)(2,1)S(1)}, u32[]{:S(2)}, u32[]{:S(2)}) collective-permute-start(bf16[64,512]{1,0:T(8,128)(2,1)S(1)} %get-tuple-element.11), channel_id=1, source_target_pairs={{0,2},{1,3},{2,0},{3,1},{4,6},{5,7},{6,4},{7,5},{8,10},{9,11},{10,... | collective-permute-start | bytes 196616 | tf_op jit(solution)/shard_map/ppermute | solution.py:263
  38.3 1.1 %collective-permute-done.6 = bf16[64,512]{1,0:T(8,128)(2,1)S(1)} collective-permute-done((bf16[64,512]{1,0:T(8,128)(2,1)S(1)}, bf16[64,512]{1,0:T(8,128)(2,1)S(1)}, u32[]{:S(2)}, u32[]{:S(2)}) %collective-permute-start.6) | collective-permute-done | bytes 65568 | tf_op jit(solution)/shard_map/ppermute | solution.py:263
  39.3 2.3 %collective-permute-done.7 = bf16[64,512]{1,0:T(8,128)(2,1)S(1)} collective-permute-done((bf16[64,512]{1,0:T(8,128)(2,1)S(1)}, bf16[64,512]{1,0:T(8,128)(2,1)S(1)}, u32[]{:S(2)}, u32[]{:S(2)}) %collective-permute-start.7) | collective-permute-done | bytes 65568 | tf_op jit(solution)/shard_map/ppermute | solution.py:263
  41.7 0.9 %add_convert_fusion = bf16[64,512]{1,0:T(8,128)(2,1)S(1)} fusion(bf16[64,512]{1,0:T(8,128)(2,1)S(1)} %collective-permute-done.8, bf16[64,512]{1,0:T(8,128)(2,1)S(1)} %collective-permute-done.7, f32[64,512]{1,0:T(8,128)} %get-tuple-element.7, bf16[64,512]{1,0:T(8,128)(2,1)S(1)} %collective-permute-done.6), kind=kLoop, calls=%fused_computation.7 | loop fusion | flops 229376 | bytes 393216 | tf_op jit(solution)/shard_map/convert_element_type | solution.py:266
  44.2 1.9 %collective-permute-start.11 = (bf16[2,64,64]{2,1,0:T(8,128)(2,1)S(1)}, bf16[2,64,64]{2,1,0:T(8,128)(2,1)S(1)}, u32[]{:S(2)}, u32[]{:S(2)}) collective-permute-start(bf16[2,64,64]{2,1,0:T(8,128)(2,1)S(1)} %bitcast.114), channel_id=1, source_target_pairs={{0,4},{4,8},{8,12},{12,0},{1,5},{5,9},{9,13},{13,1},{2,6},{6,10},{... | collective-permute-start | bytes 49160 | tf_op jit(solution)/shard_map/ppermute | solution.py:85
  46.2 0.8 %collective-permute-done.9 = bf16[2,64,64]{2,1,0:T(8,128)(2,1)S(1)} collective-permute-done((bf16[2,64,64]{2,1,0:T(8,128)(2,1)S(1)}, bf16[2,64,64]{2,1,0:T(8,128)(2,1)S(1)}, u32[]{:S(2)}, u32[]{:S(2)}) %collective-permute-start.9) | collective-permute-done | bytes 16416 | tf_op jit(solution)/shard_map/ppermute | solution.py:85
  47.0 1.4 %collective-permute-done.10 = bf16[2,64,64]{2,1,0:T(8,128)(2,1)S(1)} collective-permute-done((bf16[2,64,64]{2,1,0:T(8,128)(2,1)S(1)}, bf16[2,64,64]{2,1,0:T(8,128)(2,1)S(1)}, u32[]{:S(2)}, u32[]{:S(2)}) %collective-permute-start.10) | collective-permute-done | bytes 16416 | tf_op jit(solution)/shard_map/ppermute | solution.py:85
  48.4 1.5 %collective-permute-done.11 = bf16[2,64,64]{2,1,0:T(8,128)(2,1)S(1)} collective-permute-done((bf16[2,64,64]{2,1,0:T(8,128)(2,1)S(1)}, bf16[2,64,64]{2,1,0:T(8,128)(2,1)S(1)}, u32[]{:S(2)}, u32[]{:S(2)}) %collective-permute-start.11) | collective-permute-done | bytes 16416 | tf_op jit(solution)/shard_map/ppermute | solution.py:85
  50.4 1.1 %fusion = f32[2,16,64,64]{3,1,2,0:T(8,128)S(1)} fusion(f32[2,16,64,64]{3,2,1,0:T(8,128)S(1)} %copy-done, bf16[64,64,8]{1,0,2:T(8,128)(2,1)S(1)} %dot_general.18, f32[1,16,8]{1,2,0:T(8,128)S(1)} %bitcast.118, f32[1,16,8]{1,2,0:T(8,128)S(1)} %bitcast.117), kind=kOutput, calls=%fused_computation.1 | convolution fusion | flops 12845312 | bytes 1115136 | tf_op jit(solution)/shard_map/dot_general | solution.py:271
  51.6 1.3 %copy.40 = f32[2,16,64,64]{3,2,1,0:T(8,128)} copy(f32[2,16,64,64]{3,1,2,0:T(8,128)S(1)} %fusion) | data formatting | bytes 1048576 | tf_op jit(solution)/shard_map/sub | solution.py:277
  (62 shorter events, 5.7 us)
Async XLA Ops:
  3.6 15.4 %copy-start.2 = (f32[2,4,16]{2,1,0:T(4,128)S(1)}, f32[2,4,16]{2,1,0:T(4,128)}, u32[]{:S(2)}) copy-start(f32[2,4,16]{2,1,0:T(4,128)} %param.10) | copy-start | bytes 1540
  3.6 15.4 %copy-start.3 = (s32[1,8,256]{2,1,0:T(8,128)S(1)}, s32[1,8,256]{2,1,0:T(8,128)}, u32[]{:S(2)}) copy-start(s32[1,8,256]{2,1,0:T(8,128)} %param.13) | copy-start | bytes 24580
  5.1 6.7 %collective-permute-start = (bf16[2,64,64]{2,1,0:T(8,128)(2,1)S(1)}, bf16[2,64,64]{2,1,0:T(8,128)(2,1)S(1)}, u32[]{:S(2)}, u32[]{:S(2)}) collective-permute-start(bf16[2,64,64]{2,1,0:T(8,128)(2,1)S(1)} %bitcast.108), channel_id=1, source_target_pairs={{0,12},{4,0},{8,4},{12,8},{1,13},{5,1},{9,5},{13,9},{2,14},{6,2},{... | collective-permute-start | bytes 49160 | tf_op jit(solution)/shard_map/ppermute | solution.py:85
  10.2 4.8 %collective-permute-start.1 = (bf16[2,64,64]{2,1,0:T(8,128)(2,1)S(1)}, bf16[2,64,64]{2,1,0:T(8,128)(2,1)S(1)}, u32[]{:S(2)}, u32[]{:S(2)}) collective-permute-start(bf16[2,64,64]{2,1,0:T(8,128)(2,1)S(1)} %bitcast.110), channel_id=1, source_target_pairs={{0,8},{4,12},{8,0},{12,4},{1,9},{5,13},{9,1},{13,5},{2,10},{6,14},... | collective-permute-start | bytes 49160 | tf_op jit(solution)/shard_map/ppermute | solution.py:85
  10.3 5.8 %collective-permute-start.2 = (bf16[2,64,64]{2,1,0:T(8,128)(2,1)S(1)}, bf16[2,64,64]{2,1,0:T(8,128)(2,1)S(1)}, u32[]{:S(2)}, u32[]{:S(2)}) collective-permute-start(bf16[2,64,64]{2,1,0:T(8,128)(2,1)S(1)} %bitcast.112), channel_id=1, source_target_pairs={{0,4},{4,8},{8,12},{12,0},{1,5},{5,9},{9,13},{13,1},{2,6},{6,10},{... | collective-permute-start | bytes 49160 | tf_op jit(solution)/shard_map/ppermute | solution.py:85
  17.2 5.9 %copy-start.1 = (bf16[64,512]{1,0:T(8,128)(2,1)}, bf16[64,512]{1,0:T(8,128)(2,1)S(1)}, u32[]{:S(2)}) copy-start(bf16[64,512]{1,0:T(8,128)(2,1)S(1)} %reshape.54.refs_0_) | copy-start | bytes 196612
  17.2 2.4 %collective-permute-start.5 = (bf16[64,512]{1,0:T(8,128)(2,1)S(1)}, bf16[64,512]{1,0:T(8,128)(2,1)S(1)}, u32[]{:S(2)}, u32[]{:S(2)}) collective-permute-start(bf16[64,512]{1,0:T(8,128)(2,1)S(1)} %reshape.54.refs_0_), channel_id=1, source_target_pairs={{0,3},{1,0},{2,1},{3,2},{4,7},{5,4},{6,5},{7,6},{8,11},{9,8},{10,9... | collective-permute-start | bytes 196616 | tf_op jit(solution)/shard_map/ppermute | solution.py:255
  17.3 5.6 %collective-permute-start.4 = (bf16[64,512]{1,0:T(8,128)(2,1)S(1)}, bf16[64,512]{1,0:T(8,128)(2,1)S(1)}, u32[]{:S(2)}, u32[]{:S(2)}) collective-permute-start(bf16[64,512]{1,0:T(8,128)(2,1)S(1)} %reshape.54.refs_0_), channel_id=1, source_target_pairs={{0,2},{1,3},{2,0},{3,1},{4,6},{5,7},{6,4},{7,5},{8,10},{9,11},{10,... | collective-permute-start | bytes 196616 | tf_op jit(solution)/shard_map/ppermute | solution.py:255
  18.8 4.3 %collective-permute-start.3 = (bf16[64,512]{1,0:T(8,128)(2,1)S(1)}, bf16[64,512]{1,0:T(8,128)(2,1)S(1)}, u32[]{:S(2)}, u32[]{:S(2)}) collective-permute-start(bf16[64,512]{1,0:T(8,128)(2,1)S(1)} %reshape.54.refs_0_), channel_id=1, source_target_pairs={{0,1},{1,2},{2,3},{3,0},{4,5},{5,6},{6,7},{7,4},{8,9},{9,10},{10,1... | collective-permute-start | bytes 196616 | tf_op jit(solution)/shard_map/ppermute | solution.py:255
  19.6 3.5 %copy-start.4 = (bf16[64,512]{1,0:T(8,128)(2,1)}, bf16[64,512]{1,0:T(8,128)(2,1)S(1)}, u32[]{:S(2)}) copy-start(bf16[64,512]{1,0:T(8,128)(2,1)S(1)} %collective-permute-done.5.refs_3_) | copy-start | bytes 196612
  22.9 0.6 %copy-start.5 = (bf16[64,512]{1,0:T(8,128)(2,1)}, bf16[64,512]{1,0:T(8,128)(2,1)S(1)}, u32[]{:S(2)}) copy-start(bf16[64,512]{1,0:T(8,128)(2,1)S(1)} %collective-permute-done.4.refs_2_) | copy-start | bytes 196612
  23.1 0.6 %copy-start.6 = (bf16[64,512]{1,0:T(8,128)(2,1)}, bf16[64,512]{1,0:T(8,128)(2,1)S(1)}, u32[]{:S(2)}) copy-start(bf16[64,512]{1,0:T(8,128)(2,1)S(1)} %collective-permute-done.3.refs_1_) | copy-start | bytes 196612
  34.6 15.8 %copy-start = (f32[2,16,64,64]{3,2,1,0:T(8,128)S(1)}, f32[2,16,64,64]{3,2,1,0:T(8,128)}, u32[]{:S(2)}) copy-start(f32[2,16,64,64]{3,2,1,0:T(8,128)} %param.9) | copy-start | bytes 1572868
  35.6 3.7 %collective-permute-start.6 = (bf16[64,512]{1,0:T(8,128)(2,1)S(1)}, bf16[64,512]{1,0:T(8,128)(2,1)S(1)}, u32[]{:S(2)}, u32[]{:S(2)}) collective-permute-start(bf16[64,512]{1,0:T(8,128)(2,1)S(1)} %get-tuple-element.9), channel_id=1, source_target_pairs={{0,1},{1,2},{2,3},{3,0},{4,5},{5,6},{6,7},{7,4},{8,9},{9,10},{10,1... | collective-permute-start | bytes 196616 | tf_op jit(solution)/shard_map/ppermute | solution.py:263
  35.7 3.7 %collective-permute-start.8 = (bf16[64,512]{1,0:T(8,128)(2,1)S(1)}, bf16[64,512]{1,0:T(8,128)(2,1)S(1)}, u32[]{:S(2)}, u32[]{:S(2)}) collective-permute-start(bf16[64,512]{1,0:T(8,128)(2,1)S(1)} %get-tuple-element.10), channel_id=1, source_target_pairs={{0,3},{1,0},{2,1},{3,2},{4,7},{5,4},{6,5},{7,6},{8,11},{9,8},{10,9... | collective-permute-start | bytes 196616 | tf_op jit(solution)/shard_map/ppermute | solution.py:263
  37.4 4.3 %collective-permute-start.7 = (bf16[64,512]{1,0:T(8,128)(2,1)S(1)}, bf16[64,512]{1,0:T(8,128)(2,1)S(1)}, u32[]{:S(2)}, u32[]{:S(2)}) collective-permute-start(bf16[64,512]{1,0:T(8,128)(2,1)S(1)} %get-tuple-element.11), channel_id=1, source_target_pairs={{0,2},{1,3},{2,0},{3,1},{4,6},{5,7},{6,4},{7,5},{8,10},{9,11},{10,... | collective-permute-start | bytes 196616 | tf_op jit(solution)/shard_map/ppermute | solution.py:263
  43.1 4.0 %collective-permute-start.9 = (bf16[2,64,64]{2,1,0:T(8,128)(2,1)S(1)}, bf16[2,64,64]{2,1,0:T(8,128)(2,1)S(1)}, u32[]{:S(2)}, u32[]{:S(2)}) collective-permute-start(bf16[2,64,64]{2,1,0:T(8,128)(2,1)S(1)} %bitcast.116), channel_id=1, source_target_pairs={{0,12},{4,0},{8,4},{12,8},{1,13},{5,1},{9,5},{13,9},{2,14},{6,2},{... | collective-permute-start | bytes 49160 | tf_op jit(solution)/shard_map/ppermute | solution.py:85
  43.6 4.8 %collective-permute-start.10 = (bf16[2,64,64]{2,1,0:T(8,128)(2,1)S(1)}, bf16[2,64,64]{2,1,0:T(8,128)(2,1)S(1)}, u32[]{:S(2)}, u32[]{:S(2)}) collective-permute-start(bf16[2,64,64]{2,1,0:T(8,128)(2,1)S(1)} %bitcast.115), channel_id=1, source_target_pairs={{0,8},{4,12},{8,0},{12,4},{1,9},{5,13},{9,1},{13,5},{2,10},{6,14},... | collective-permute-start | bytes 49160 | tf_op jit(solution)/shard_map/ppermute | solution.py:85
  44.2 5.7 %collective-permute-start.11 = (bf16[2,64,64]{2,1,0:T(8,128)(2,1)S(1)}, bf16[2,64,64]{2,1,0:T(8,128)(2,1)S(1)}, u32[]{:S(2)}, u32[]{:S(2)}) collective-permute-start(bf16[2,64,64]{2,1,0:T(8,128)(2,1)S(1)} %bitcast.114), channel_id=1, source_target_pairs={{0,4},{4,8},{8,12},{12,0},{1,5},{5,9},{9,13},{13,1},{2,6},{6,10},{... | collective-permute-start | bytes 49160 | tf_op jit(solution)/shard_map/ppermute | solution.py:85

commit v12 on v9

--- a/solution.py
+++ b/solution.py
@@ -223,6 +223,65 @@
     )(*pieces, place, sens, measured, sampled, forward_x, adjoint_x, table_y_re, table_y_im)
 
 
+def images_kernel(weight_ref, factors_ref, out_ref):
+    parts, ranks = factors_ref.shape[:2]
+
+    def one_frame(frame, carry):
+        for part_out in range(2):
+            total = None
+            for part in range(parts):
+                for rank in range(ranks):
+                    weight = weight_ref[((frame * 2 + part_out) * parts + part) * ranks + rank]
+                    term = weight * factors_ref[part, rank]
+                    total = term if total is None else total + term
+            out_ref[frame, part_out] = total.astype(out_ref.dtype)
+        return carry
+
+    lax.fori_loop(0, out_ref.shape[0], one_frame, 0)
+
+
+def make_images(weights, factors):
+    parts, ranks, rows, cols = factors.shape
+    frames = weights.shape[0] // (2 * parts * ranks)
+    return pl.pallas_call(
+        images_kernel,
+        out_shape=jax.ShapeDtypeStruct((frames, 2, rows, cols), jnp.bfloat16),
+        in_specs=[pl.BlockSpec(memory_space=pltpu.SMEM), pl.BlockSpec(memory_space=pltpu.VMEM)],
+        out_specs=pl.BlockSpec(memory_space=pltpu.VMEM),
+    )(weights, factors)
+
+
+def step_kernel(weight_ref, back_ref, factors_ref, out_ref):
+    parts, ranks = factors_ref.shape[:2]
+    frames = back_ref.shape[0]
+    for part in range(parts):
+        for rank in range(ranks):
+            base = (part * ranks + rank) * frames * 2
+
+            def one_frame(frame, total):
+                for part_in in range(2):
+                    total = total + weight_ref[base + frame * 2 + part_in] * back_ref[frame, part_in].astype(jnp.float32)
+                return total
+
+            total = lax.fori_loop(
+                0, frames, one_frame, jnp.zeros(factors_ref.shape[2:], jnp.float32), unroll=frames <= 8
+            )
+            out_ref[part, rank] = factors_ref[part, rank] - 0.5 * total
+
+
+def take_step(weights, back, factors):
+    return pl.pallas_call(
+        step_kernel,
+        out_shape=jax.ShapeDtypeStruct(factors.shape, jnp.float32),
+        in_specs=[
+            pl.BlockSpec(memory_space=pltpu.SMEM),
+            pl.BlockSpec(memory_space=pltpu.VMEM),
+            pl.BlockSpec(memory_space=pltpu.VMEM),
+        ],
+        out_specs=pl.BlockSpec(memory_space=pltpu.VMEM),
+    )(weights, back, factors)
+
+
 def on_device(factors, temporal, maps, kdata, masks):
     width_x = maps.shape[2] // 2
     width_y = maps.shape[1]
@@ -238,9 +297,7 @@
     mixing = jnp.stack(
         [jnp.stack([time_re, -time_im], axis=1), jnp.stack([time_im, time_re], axis=1)], axis=1
     )
-    images = jnp.sum(
-        mixing[:, :, :, :, None, None] * factors[None, None], axis=(2, 3)
-    ).astype(jnp.bfloat16)
+    images = make_images(mixing.reshape(-1), factors)
     frames_here = images.shape[0]
     width_own = images.shape[3]
     pieces_x = exchange_blocks(images, "frame")
@@ -257,16 +314,13 @@
     for step in range(1, groups):
         own_share = own_share + lax.ppermute(outgoing[step - 1], "coil", shifted(groups, step)).astype(jnp.float32)
     outgoing = jnp.transpose(
-        own_share.reshape(rows_own, 2, frames_here, width_own), (2, 0, 1, 3)
+        own_share.reshape(rows_own, 2, frames_here, width_own), (2, 1, 0, 3)
     ).astype(jnp.bfloat16)
-    returned = exchange_blocks(outgoing, "frame").astype(jnp.float32)
+    returned = exchange_blocks(outgoing, "frame")
     weights = jnp.stack(
         [jnp.stack([time_re.T, time_im.T], axis=2), jnp.stack([-time_im.T, time_re.T], axis=2)], axis=0
     )
-    gradient = jnp.sum(
-        weights[:, :, :, None, :, None] * returned[None, None], axis=(2, 4)
-    )
-    return factors - 0.5 * gradient
+    return take_step(weights.reshape(-1), returned, factors)
 
 
 def solution(mesh):

time: 51.4 us -> 55.3 us (1.076)
  Pallas kernels: 10.9 us -> 16.6 us
  other arithmetic: 7.83 us -> 3.03 us
  local copies, waits for them, and re-layouts: 3.96 us -> 7.49 us
  waiting for transfers between devices: 13 us -> 12.2 us
    pallas_call x0 -> x2, Pallas kernels: none -> 5.71 us  [the longest x1 3.15 us: take_step(): pl.pallas_call(step_kernel, out_shape=jax.ShapeDtypeStruct(factors.shape,...]
    reduce_sum x2 -> x0, other arithmetic: 3.65 us -> none  [the longest x1 2.29 us: on_device(): jnp.sum(mixing[:, :, :, :, None, None] * factors[None, None], axis=(2, 3))]
    reshape x0 -> x2, local copies, waits for them, and re-layouts: none -> 1.41 us  [the longest x1 0.74 us: on_device(): return take_step(weights.reshape(-1), returned, factors)]
    sub x1 -> x0, other arithmetic: 1.13 us -> none  [on_device(): return factors - 0.5 * gradient]
    squeeze x1, local copies, waits for them, and re-layouts: 0.02 us -> 0.82 us  [exchange_blocks(): lax.dynamic_index_in_dim(blocks, (me + step) % count, 0, keepdims=False)]
    unnamed x27 -> x25, local copies, waits for them, and re-layouts: 1.4 us -> 2.14 us
    ppermute x3, waiting for transfers between devices: 3.25 us -> 2.52 us  [on_device(): lax.ppermute(outgoing[step - 1], 'coil', shifted(groups, step))]
    squeeze x0 -> x1, local copies, waits for them, and re-layouts: none -> 0.7 us  [on_device(): time_im = temporal[1]]
  transfers between devices with their start and end apart: 12 -> 12, of which waited for: 9 -> 9; matrix products, arithmetic and copies ran while one was open for 4% -> 5% of each run, Pallas kernels for 0% -> 0%
where the time goes in v12:
time: 55.3 us; the launch traced here: 54.8 us
  Pallas kernels  16.6 us (30%)
  starting transfers between devices  15.3 us (28%)
  waiting for transfers between devices  12.2 us (22%)
  local copies, waits for them, and re-layouts  7.49 us (14%)
  other arithmetic  3.03 us (5%)
    pallas_call x1, Pallas kernels, coil_chain(): pl.pallas_call(coil_chain_kernel, out_shape=(jax.ShapeDtypeStruct((rows,...  10.9 us
    ppermute x6, starting transfers between devices, exchange_blocks(): pieces.append(lax.ppermute(outgoing, axis, shifted(count, step)))  10.9 us
    ppermute x6, waiting for transfers between devices, exchange_blocks(): pieces.append(lax.ppermute(outgoing, axis, shifted(count, step)))  5.63 us
    ppermute x3, waiting for transfers between devices, on_device(): lax.ppermute(own_rows, 'coil', shifted(groups, step))  4.1 us
    pallas_call x1, Pallas kernels, take_step(): pl.pallas_call(step_kernel, out_shape=jax.ShapeDtypeStruct(factors.shape,...  3.15 us
    ppermute x3, starting transfers between devices, on_device(): lax.ppermute(outgoing[step - 1], 'coil', shifted(groups, step))  2.66 us
    pallas_call x1, Pallas kernels, make_images(): pl.pallas_call(images_kernel, out_shape=jax.ShapeDtypeStruct((frames, 2,...  2.56 us
    ppermute x3, waiting for transfers between devices, on_device(): lax.ppermute(outgoing[step - 1], 'coil', shifted(groups, step))  2.52 us
  transfers between devices with their start and end apart: 12, of which 9 were waited for; matrix products, arithmetic and copies ran while one was open for 5% of the time, Pallas kernels for 0%

profile of v12, /device:TPU:0, one launch (start us, length us, event | category | flops | bytes accessed | tf_op | source)
XLA Modules:
  0.0 54.8 jit_solution(8938569450477537160)
XLA Ops:
  0.0 0.7 %fusion.1 = f32[4,1,16]{2,0,1:T(4,128)S(1)} fusion(f32[2,4,16]{2,1,0:T(4,128)} %param.10), kind=kLoop, calls=%fused_computation.48 | loop fusion | flops 64 | bytes 512 | tf_op jit(solution)/shard_map/neg | solution.py:298
  0.7 0.7 %slice_bitcast_fusion.6 = (f32[4,1,16]{2,0,1:T(4,128)S(1)}, f32[16,4,1]{0,1,2:T(4,128)S(1)}, f32[4,1,16]{2,0,1:T(4,128)S(1)}, f32[16,4,1]{0,1,2:T(4,128)S(1)}) fusion(f32[2,4,16]{2,1,0:T(4,128)} %param.10), kind=kLoop, calls=%fused_computation.47 | loop fusion | bytes 1536 | tf_op jit(solution)/shard_map/squeeze | solution.py:296
  2.1 2.6 %shard_map.91 = bf16[4,2,64,64]{3,2,1,0:T(8,128)(2,1)} custom-call(f32[256]{0:T(256)} %reshape.36.weight_ref, f32[2,16,64,64]{3,2,1,0:T(8,128)} %factors_ref.3), custom_call_target="tpu_custom_call" | custom-call | tf_op jit(solution)/shard_map/pallas_call | solution.py:246
  4.7 0.8 %dynamic-slice_bitcast_fusion.1 = (bf16[2,64,64]{2,1,0:T(8,128)(2,1)S(1)}, bf16[8,2,64,64]{3,2,1,0:T(8,128)(2,1)S(1)}, bf16[2,64,64]{2,1,0:T(8,128)(2,1)S(1)}, bf16[2,64,64]{2,1,0:T(8,128)(2,1)S(1)}) fusion(bf16[4,2,64,64]{3,2,1,0:T(8,128)(2,1)} %shard_map.91, s32[]{:T(128)S(6)} %select_n.54, s32[]{:T(128)S(6)} %select_n.48, s32[]{:T(128)S(6)} %select_n.52, ...), kind=kLoop, calls=%fused_computation.25 | loop fusion | bytes 196624 | tf_op jit(solution)/shard_map/jit(dynamic_index_in_dim)/squeeze | solution.py:84
  5.5 3.1 %collective-permute-start.2 = (bf16[2,64,64]{2,1,0:T(8,128)(2,1)S(1)}, bf16[2,64,64]{2,1,0:T(8,128)(2,1)S(1)}, u32[]{:S(2)}, u32[]{:S(2)}) collective-permute-start(bf16[2,64,64]{2,1,0:T(8,128)(2,1)S(1)} %get-tuple-element.16), channel_id=1, source_target_pairs={{0,4},{4,8},{8,12},{12,0},{1,5},{5,9},{9,13},{13,1},{2,6},{6,10},{... | collective-permute-start | bytes 49160 | tf_op jit(solution)/shard_map/ppermute | solution.py:85
  8.5 2.6 %collective-permute-start.1 = (bf16[2,64,64]{2,1,0:T(8,128)(2,1)S(1)}, bf16[2,64,64]{2,1,0:T(8,128)(2,1)S(1)}, u32[]{:S(2)}, u32[]{:S(2)}) collective-permute-start(bf16[2,64,64]{2,1,0:T(8,128)(2,1)S(1)} %get-tuple-element.18), channel_id=1, source_target_pairs={{0,8},{4,12},{8,0},{12,4},{1,9},{5,13},{9,1},{13,5},{2,10},{6,14},... | collective-permute-start | bytes 49160 | tf_op jit(solution)/shard_map/ppermute | solution.py:85
  11.1 1.3 %collective-permute-start = (bf16[2,64,64]{2,1,0:T(8,128)(2,1)S(1)}, bf16[2,64,64]{2,1,0:T(8,128)(2,1)S(1)}, u32[]{:S(2)}, u32[]{:S(2)}) collective-permute-start(bf16[2,64,64]{2,1,0:T(8,128)(2,1)S(1)} %get-tuple-element.19), channel_id=1, source_target_pairs={{0,12},{4,0},{8,4},{12,8},{1,13},{5,1},{9,5},{13,9},{2,14},{6,2},{... | collective-permute-start | bytes 49160 | tf_op jit(solution)/shard_map/ppermute | solution.py:85
  12.5 0.7 %fusion = f32[16,4,1]{0,1,2:T(4,128)S(1)} fusion(f32[2,4,16]{2,1,0:T(4,128)} %param.10), kind=kLoop, calls=%fused_computation.43 | loop fusion | flops 64 | bytes 512 | tf_op jit(solution)/shard_map/stack | solution.py:321
  13.2 0.7 %convert_element_type.36 = f32[1,8,256]{2,1,0:T(8,128)S(1)} convert(s32[1,8,256]{2,1,0:T(8,128)} %param.13) | non-fusion elementwise | flops 2048 | bytes 16384 | tf_op jit(solution)/shard_map/convert_element_type | solution.py:308
  15.1 0.8 %constant_dynamic-update-slice_fusion.3 = bf16[8,2,64,64]{3,2,1,0:T(8,128)(2,1)S(1)} fusion(bf16[8,2,64,64]{3,2,1,0:T(8,128)(2,1)S(1)} %constant_dynamic-update-slice_fusion.4, bf16[4,2,64,64]{3,2,1,0:T(8,128)(2,1)} %shard_map.91, s32[]{:T(128)S(6)} %select_n.48), kind=kLoop, calls=%fused_computation.8 | loop fusion | bytes 49156
  16.3 1.6 %collective-permute-start.4 = (bf16[64,512]{1,0:T(8,128)(2,1)S(1)}, bf16[64,512]{1,0:T(8,128)(2,1)S(1)}, u32[]{:S(2)}, u32[]{:S(2)}) collective-permute-start(bf16[64,512]{1,0:T(8,128)(2,1)S(1)} %reshape.37.refs_0_), channel_id=1, source_target_pairs={{0,2},{1,3},{2,0},{3,1},{4,6},{5,7},{6,4},{7,5},{8,10},{9,11},{10,... | collective-permute-start | bytes 196616 | tf_op jit(solution)/shard_map/ppermute | solution.py:307
  18.2 3.7 %collective-permute-done.4.refs_2_ = bf16[64,512]{1,0:T(8,128)(2,1)S(1)} collective-permute-done((bf16[64,512]{1,0:T(8,128)(2,1)S(1)}, bf16[64,512]{1,0:T(8,128)(2,1)S(1)}, u32[]{:S(2)}, u32[]{:S(2)}) %collective-permute-start.4) | collective-permute-done | bytes 65568 | tf_op jit(solution)/shard_map/ppermute | solution.py:307
  22.7 10.9 %shard_map.92 = (f32[64,512]{1,0:T(8,128)}, bf16[3,64,512]{2,1,0:T(8,128)(2,1)}) custom-call(bf16[64,512]{1,0:T(8,128)(2,1)} %copy-done, bf16[64,512]{1,0:T(8,128)(2,1)} %copy-done.3, bf16[64,512]{1,0:T(8,128)(2,1)} %copy-done.2, bf16[64,512]{1,0:T(8,128)(2,1)} %copy-done.1, s32[1]{0:T(128)} %bitcast.23.refs_4_, bf16[8,256,512]{2,1,0:T(8,128)(2,1)} %refs_5_.1, ...), custom_call_target="tpu_custom_call" | custom-call | flops 4294967296 | bytes 4718592 | tf_op jit(solution)/shard_map/pallas_call | solution.py:196
  33.6 0.9 %slice_bitcast_fusion.2 = (bf16[64,512]{1,0:T(8,128)(2,1)S(1)}, bf16[64,512]{1,0:T(8,128)(2,1)S(1)}, bf16[64,512]{1,0:T(8,128)(2,1)S(1)}) fusion(bf16[3,64,512]{2,1,0:T(8,128)(2,1)} %get-tuple-element.8), kind=kLoop, calls=%fused_computation.4 | loop fusion | bytes 393216 | tf_op jit(solution)/shard_map/squeeze | solution.py:315
  34.6 1.7 %collective-permute-start.8 = (bf16[64,512]{1,0:T(8,128)(2,1)S(1)}, bf16[64,512]{1,0:T(8,128)(2,1)S(1)}, u32[]{:S(2)}, u32[]{:S(2)}) collective-permute-start(bf16[64,512]{1,0:T(8,128)(2,1)S(1)} %get-tuple-element.10), channel_id=1, source_target_pairs={{0,3},{1,0},{2,1},{3,2},{4,7},{5,4},{6,5},{7,6},{8,11},{9,8},{10,9... | collective-permute-start | bytes 196616 | tf_op jit(solution)/shard_map/ppermute | solution.py:315
  36.3 0.9 %collective-permute-start.7 = (bf16[64,512]{1,0:T(8,128)(2,1)S(1)}, bf16[64,512]{1,0:T(8,128)(2,1)S(1)}, u32[]{:S(2)}, u32[]{:S(2)}) collective-permute-start(bf16[64,512]{1,0:T(8,128)(2,1)S(1)} %get-tuple-element.11), channel_id=1, source_target_pairs={{0,2},{1,3},{2,0},{3,1},{4,6},{5,7},{6,4},{7,5},{8,10},{9,11},{10,... | collective-permute-start | bytes 196616 | tf_op jit(solution)/shard_map/ppermute | solution.py:315
  37.3 0.7 %reshape.35.weight_ref = f32[256]{0:T(256)} reshape(f32[2,16,4,2]{3,2,1,0:T(4,128)S(1)} %copy.14) | data formatting | bytes 2048 | tf_op jit(solution)/shard_map/reshape | solution.py:323
  38.2 2.3 %collective-permute-done.7 = bf16[64,512]{1,0:T(8,128)(2,1)S(1)} collective-permute-done((bf16[64,512]{1,0:T(8,128)(2,1)S(1)}, bf16[64,512]{1,0:T(8,128)(2,1)S(1)}, u32[]{:S(2)}, u32[]{:S(2)}) %collective-permute-start.7) | collective-permute-done | bytes 65568 | tf_op jit(solution)/shard_map/ppermute | solution.py:315
  40.6 0.9 %add_convert_fusion = bf16[64,512]{1,0:T(8,128)(2,1)S(1)} fusion(bf16[64,512]{1,0:T(8,128)(2,1)S(1)} %collective-permute-done.8, bf16[64,512]{1,0:T(8,128)(2,1)S(1)} %collective-permute-done.7, f32[64,512]{1,0:T(8,128)} %get-tuple-element.7, bf16[64,512]{1,0:T(8,128)(2,1)S(1)} %collective-permute-done.6), kind=kLoop, calls=%fused_computation | loop fusion | flops 229376 | bytes 393216 | tf_op jit(solution)/shard_map/convert_element_type | solution.py:318
  42.0 3.2 %collective-permute-start.9 = (bf16[2,64,64]{2,1,0:T(8,128)(2,1)S(1)}, bf16[2,64,64]{2,1,0:T(8,128)(2,1)S(1)}, u32[]{:S(2)}, u32[]{:S(2)}) collective-permute-start(bf16[2,64,64]{2,1,0:T(8,128)(2,1)S(1)} %bitcast.91), channel_id=1, source_target_pairs={{0,12},{4,0},{8,4},{12,8},{1,13},{5,1},{9,5},{13,9},{2,14},{6,2},{... | collective-permute-start | bytes 49160 | tf_op jit(solution)/shard_map/ppermute | solution.py:85
  45.8 0.9 %collective-permute-done.9 = bf16[2,64,64]{2,1,0:T(8,128)(2,1)S(1)} collective-permute-done((bf16[2,64,64]{2,1,0:T(8,128)(2,1)S(1)}, bf16[2,64,64]{2,1,0:T(8,128)(2,1)S(1)}, u32[]{:S(2)}, u32[]{:S(2)}) %collective-permute-start.9) | collective-permute-done | bytes 16416 | tf_op jit(solution)/shard_map/ppermute | solution.py:85
  46.8 3.2 %collective-permute-done.10 = bf16[2,64,64]{2,1,0:T(8,128)(2,1)S(1)} collective-permute-done((bf16[2,64,64]{2,1,0:T(8,128)(2,1)S(1)}, bf16[2,64,64]{2,1,0:T(8,128)(2,1)S(1)}, u32[]{:S(2)}, u32[]{:S(2)}) %collective-permute-start.10) | collective-permute-done | bytes 16416 | tf_op jit(solution)/shard_map/ppermute | solution.py:85
  50.0 0.9 %collective-permute-done.11 = bf16[2,64,64]{2,1,0:T(8,128)(2,1)S(1)} collective-permute-done((bf16[2,64,64]{2,1,0:T(8,128)(2,1)S(1)}, bf16[2,64,64]{2,1,0:T(8,128)(2,1)S(1)}, u32[]{:S(2)}, u32[]{:S(2)}) %collective-permute-start.11) | collective-permute-done | bytes 16416 | tf_op jit(solution)/shard_map/ppermute | solution.py:85
  51.6 3.2 %shard_map.93 = f32[2,16,64,64]{3,2,1,0:T(8,128)} custom-call(f32[256]{0:T(256)} %reshape.35.weight_ref, bf16[4,2,64,64]{3,2,1,0:T(8,128)(2,1)} %constant_dynamic-slice_fusion.back_ref, f32[2,16,64,64]{3,2,1,0:T(8,128)} %factors_ref.3), custom_call_target="tpu_custom_call" | custom-call | tf_op jit(solution)/shard_map/pallas_call | solution.py:273
  (52 shorter events, 5.6 us)
Async XLA Ops:
  5.5 9.6 %collective-permute-start.2 = (bf16[2,64,64]{2,1,0:T(8,128)(2,1)S(1)}, bf16[2,64,64]{2,1,0:T(8,128)(2,1)S(1)}, u32[]{:S(2)}, u32[]{:S(2)}) collective-permute-start(bf16[2,64,64]{2,1,0:T(8,128)(2,1)S(1)} %get-tuple-element.16), channel_id=1, source_target_pairs={{0,4},{4,8},{8,12},{12,0},{1,5},{5,9},{9,13},{13,1},{2,6},{6,10},{... | collective-permute-start | bytes 49160 | tf_op jit(solution)/shard_map/ppermute | solution.py:85
  8.5 6.5 %collective-permute-start.1 = (bf16[2,64,64]{2,1,0:T(8,128)(2,1)S(1)}, bf16[2,64,64]{2,1,0:T(8,128)(2,1)S(1)}, u32[]{:S(2)}, u32[]{:S(2)}) collective-permute-start(bf16[2,64,64]{2,1,0:T(8,128)(2,1)S(1)} %get-tuple-element.18), channel_id=1, source_target_pairs={{0,8},{4,12},{8,0},{12,4},{1,9},{5,13},{9,1},{13,5},{2,10},{6,14},... | collective-permute-start | bytes 49160 | tf_op jit(solution)/shard_map/ppermute | solution.py:85
  11.1 3.9 %collective-permute-start = (bf16[2,64,64]{2,1,0:T(8,128)(2,1)S(1)}, bf16[2,64,64]{2,1,0:T(8,128)(2,1)S(1)}, u32[]{:S(2)}, u32[]{:S(2)}) collective-permute-start(bf16[2,64,64]{2,1,0:T(8,128)(2,1)S(1)} %get-tuple-element.19), channel_id=1, source_target_pairs={{0,12},{4,0},{8,4},{12,8},{1,13},{5,1},{9,5},{13,9},{2,14},{6,2},{... | collective-permute-start | bytes 49160 | tf_op jit(solution)/shard_map/ppermute | solution.py:85
  16.2 5.9 %copy-start = (bf16[64,512]{1,0:T(8,128)(2,1)}, bf16[64,512]{1,0:T(8,128)(2,1)S(1)}, u32[]{:S(2)}) copy-start(bf16[64,512]{1,0:T(8,128)(2,1)S(1)} %reshape.37.refs_0_) | copy-start | bytes 196612
  16.2 2.0 %collective-permute-start.5 = (bf16[64,512]{1,0:T(8,128)(2,1)S(1)}, bf16[64,512]{1,0:T(8,128)(2,1)S(1)}, u32[]{:S(2)}, u32[]{:S(2)}) collective-permute-start(bf16[64,512]{1,0:T(8,128)(2,1)S(1)} %reshape.37.refs_0_), channel_id=1, source_target_pairs={{0,3},{1,0},{2,1},{3,2},{4,7},{5,4},{6,5},{7,6},{8,11},{9,8},{10,9... | collective-permute-start | bytes 196616 | tf_op jit(solution)/shard_map/ppermute | solution.py:307
  16.3 5.6 %collective-permute-start.4 = (bf16[64,512]{1,0:T(8,128)(2,1)S(1)}, bf16[64,512]{1,0:T(8,128)(2,1)S(1)}, u32[]{:S(2)}, u32[]{:S(2)}) collective-permute-start(bf16[64,512]{1,0:T(8,128)(2,1)S(1)} %reshape.37.refs_0_), channel_id=1, source_target_pairs={{0,2},{1,3},{2,0},{3,1},{4,6},{5,7},{6,4},{7,5},{8,10},{9,11},{10,... | collective-permute-start | bytes 196616 | tf_op jit(solution)/shard_map/ppermute | solution.py:307
  17.8 4.3 %collective-permute-start.3 = (bf16[64,512]{1,0:T(8,128)(2,1)S(1)}, bf16[64,512]{1,0:T(8,128)(2,1)S(1)}, u32[]{:S(2)}, u32[]{:S(2)}) collective-permute-start(bf16[64,512]{1,0:T(8,128)(2,1)S(1)} %reshape.37.refs_0_), channel_id=1, source_target_pairs={{0,1},{1,2},{2,3},{3,0},{4,5},{5,6},{6,7},{7,4},{8,9},{9,10},{10,1... | collective-permute-start | bytes 196616 | tf_op jit(solution)/shard_map/ppermute | solution.py:307
  18.2 3.9 %copy-start.1 = (bf16[64,512]{1,0:T(8,128)(2,1)}, bf16[64,512]{1,0:T(8,128)(2,1)S(1)}, u32[]{:S(2)}) copy-start(bf16[64,512]{1,0:T(8,128)(2,1)S(1)} %collective-permute-done.5.refs_3_) | copy-start | bytes 196612
  21.9 0.6 %copy-start.2 = (bf16[64,512]{1,0:T(8,128)(2,1)}, bf16[64,512]{1,0:T(8,128)(2,1)S(1)}, u32[]{:S(2)}) copy-start(bf16[64,512]{1,0:T(8,128)(2,1)S(1)} %collective-permute-done.4.refs_2_) | copy-start | bytes 196612
  22.1 0.6 %copy-start.3 = (bf16[64,512]{1,0:T(8,128)(2,1)}, bf16[64,512]{1,0:T(8,128)(2,1)S(1)}, u32[]{:S(2)}) copy-start(bf16[64,512]{1,0:T(8,128)(2,1)S(1)} %collective-permute-done.3.refs_1_) | copy-start | bytes 196612
  34.5 3.7 %collective-permute-start.6 = (bf16[64,512]{1,0:T(8,128)(2,1)S(1)}, bf16[64,512]{1,0:T(8,128)(2,1)S(1)}, u32[]{:S(2)}, u32[]{:S(2)}) collective-permute-start(bf16[64,512]{1,0:T(8,128)(2,1)S(1)} %get-tuple-element.9), channel_id=1, source_target_pairs={{0,1},{1,2},{2,3},{3,0},{4,5},{5,6},{6,7},{7,4},{8,9},{9,10},{10,1... | collective-permute-start | bytes 196616 | tf_op jit(solution)/shard_map/ppermute | solution.py:315
  34.6 3.7 %collective-permute-start.8 = (bf16[64,512]{1,0:T(8,128)(2,1)S(1)}, bf16[64,512]{1,0:T(8,128)(2,1)S(1)}, u32[]{:S(2)}, u32[]{:S(2)}) collective-permute-start(bf16[64,512]{1,0:T(8,128)(2,1)S(1)} %get-tuple-element.10), channel_id=1, source_target_pairs={{0,3},{1,0},{2,1},{3,2},{4,7},{5,4},{6,5},{7,6},{8,11},{9,8},{10,9... | collective-permute-start | bytes 196616 | tf_op jit(solution)/shard_map/ppermute | solution.py:315
  36.3 4.3 %collective-permute-start.7 = (bf16[64,512]{1,0:T(8,128)(2,1)S(1)}, bf16[64,512]{1,0:T(8,128)(2,1)S(1)}, u32[]{:S(2)}, u32[]{:S(2)}) collective-permute-start(bf16[64,512]{1,0:T(8,128)(2,1)S(1)} %get-tuple-element.11), channel_id=1, source_target_pairs={{0,2},{1,3},{2,0},{3,1},{4,6},{5,7},{6,4},{7,5},{8,10},{9,11},{10,... | collective-permute-start | bytes 196616 | tf_op jit(solution)/shard_map/ppermute | solution.py:315
  42.0 4.8 %collective-permute-start.9 = (bf16[2,64,64]{2,1,0:T(8,128)(2,1)S(1)}, bf16[2,64,64]{2,1,0:T(8,128)(2,1)S(1)}, u32[]{:S(2)}, u32[]{:S(2)}) collective-permute-start(bf16[2,64,64]{2,1,0:T(8,128)(2,1)S(1)} %bitcast.91), channel_id=1, source_target_pairs={{0,12},{4,0},{8,4},{12,8},{1,13},{5,1},{9,5},{13,9},{2,14},{6,2},{... | collective-permute-start | bytes 49160 | tf_op jit(solution)/shard_map/ppermute | solution.py:85
  45.2 4.8 %collective-permute-start.10 = (bf16[2,64,64]{2,1,0:T(8,128)(2,1)S(1)}, bf16[2,64,64]{2,1,0:T(8,128)(2,1)S(1)}, u32[]{:S(2)}, u32[]{:S(2)}) collective-permute-start(bf16[2,64,64]{2,1,0:T(8,128)(2,1)S(1)} %bitcast.90), channel_id=1, source_target_pairs={{0,8},{4,12},{8,0},{12,4},{1,9},{5,13},{9,1},{13,5},{2,10},{6,14},... | collective-permute-start | bytes 49160 | tf_op jit(solution)/shard_map/ppermute | solution.py:85
  45.2 5.7 %collective-permute-start.11 = (bf16[2,64,64]{2,1,0:T(8,128)(2,1)S(1)}, bf16[2,64,64]{2,1,0:T(8,128)(2,1)S(1)}, u32[]{:S(2)}, u32[]{:S(2)}) collective-permute-start(bf16[2,64,64]{2,1,0:T(8,128)(2,1)S(1)} %bitcast.89), channel_id=1, source_target_pairs={{0,4},{4,8},{8,12},{12,0},{1,5},{5,9},{9,13},{13,1},{2,6},{6,10},{... | collective-permute-start | bytes 49160 | tf_op jit(solution)/shard_map/ppermute | solution.py:85

commit v13 on v9

--- a/solution.py
+++ b/solution.py
@@ -141,13 +141,14 @@
 
 
 def coil_chain_kernel(*refs):
-    groups = len(refs) - 12
+    groups = (len(refs) - 9) // 2
     pieces = refs[:groups]
     place_ref, sens_ref, measured_ref, sampled_ref, forward_ref, adjoint_ref, table_re_ref, table_im_ref = refs[
         groups:groups + 8
     ]
-    own_ref, send_ref = refs[groups + 8:groups + 10]
-    image_ref, total_ref = refs[groups + 10:]
+    own_ref = refs[groups + 8]
+    send_refs = refs[groups + 9:2 * groups + 8]
+    image_ref, total_ref = refs[2 * groups + 8:]
     rows = pieces[0].shape[0]
     half_width = image_ref.shape[1] // 2
     me = place_ref[0]
@@ -182,7 +183,7 @@
         own_ref[...] = total_ref[pl.ds(start, rows), :]
         for shift in range(1, groups):
             start = pl.multiple_of(((me + shift) % groups) * rows, rows)
-            send_ref[shift - 1] = total_ref[pl.ds(start, rows), :].astype(jnp.bfloat16)
+            send_refs[shift - 1][...] = total_ref[pl.ds(start, rows), :].astype(jnp.bfloat16)
 
 
 def coil_chain(pieces, place, sens, measured, sampled, forward_x, adjoint_x, table_y_re, table_y_im):
@@ -195,10 +196,8 @@
     flops = coils * 8 * height * width * width
     return pl.pallas_call(
         coil_chain_kernel,
-        out_shape=(
-            jax.ShapeDtypeStruct((rows, width), jnp.float32),
-            jax.ShapeDtypeStruct((groups - 1, rows, width), jnp.bfloat16),
-        ),
+        out_shape=(jax.ShapeDtypeStruct((rows, width), jnp.float32),)
+        + (jax.ShapeDtypeStruct((rows, width), jnp.bfloat16),) * (groups - 1),
         grid=(coils // step_coils,),
         in_specs=[pl.BlockSpec((rows, width), whole)] * groups
         + [
@@ -211,10 +210,7 @@
             pl.BlockSpec((height, height), whole),
             pl.BlockSpec((height, height), whole),
         ],
-        out_specs=(
-            pl.BlockSpec((rows, width), whole),
-            pl.BlockSpec((groups - 1, rows, width), lambda c: (0, 0, 0)),
-        ),
+        out_specs=(pl.BlockSpec((rows, width), whole),) * groups,
         scratch_shapes=[pltpu.VMEM((height, width), jnp.bfloat16), pltpu.VMEM((height, width), jnp.float32)],
         compiler_params=pltpu.CompilerParams(dimension_semantics=("arbitrary",)),
         cost_estimate=pl.CostEstimate(
@@ -238,9 +234,13 @@
     mixing = jnp.stack(
         [jnp.stack([time_re, -time_im], axis=1), jnp.stack([time_im, time_re], axis=1)], axis=1
     )
-    images = jnp.sum(
-        mixing[:, :, :, :, None, None] * factors[None, None], axis=(2, 3)
-    ).astype(jnp.bfloat16)
+    parts, ranks = factors.shape[:2]
+    images = None
+    for part in range(parts):
+        for rank in range(ranks):
+            term = mixing[:, :, part, rank, None, None] * factors[part, rank][None, None]
+            images = term if images is None else images + term
+    images = images.astype(jnp.bfloat16)
     frames_here = images.shape[0]
     width_own = images.shape[3]
     pieces_x = exchange_blocks(images, "frame")
@@ -250,7 +250,7 @@
     pieces = [own_rows] + [lax.ppermute(own_rows, "coil", shifted(groups, step)) for step in range(1, groups)]
     sampled = masks[0].astype(jnp.float32)[:, None, :]
     place = jnp.reshape(me_c, (1,)).astype(jnp.int32)
-    own_total, outgoing = coil_chain(
+    own_total, *outgoing = coil_chain(
         pieces, place, maps, kdata[0], sampled, forward_x, adjoint_x, table_y_re, table_y_im
     )
     own_share = own_total
@@ -263,9 +263,11 @@
     weights = jnp.stack(
         [jnp.stack([time_re.T, time_im.T], axis=2), jnp.stack([-time_im.T, time_re.T], axis=2)], axis=0
     )
-    gradient = jnp.sum(
-        weights[:, :, :, None, :, None] * returned[None, None], axis=(2, 4)
-    )
+    gradient = None
+    for frame in range(returned.shape[0]):
+        for part_in in range(2):
+            term = weights[:, :, frame, part_in, None, None] * returned[frame, :, part_in][None, None]
+            gradient = term if gradient is None else gradient + term
     return factors - 0.5 * gradient
 
 

time: 51.4 us -> 53.4 us (1.039)
  local copies, waits for them, and re-layouts: 3.96 us -> 8.45 us
  other arithmetic: 7.83 us -> 4.52 us
  waiting for transfers between devices: 13 us -> 14 us
    mul x0 -> x35, local copies, waits for them, and re-layouts: none -> 5.6 us  [the longest x34 5.58 us: on_device(): mixing[:, :, part, rank, None, None] * factors[part, rank][None, None]]
    reduce_sum x2 -> x0, other arithmetic: 3.65 us -> none  [the longest x1 2.29 us: on_device(): jnp.sum(mixing[:, :, :, :, None, None] * factors[None, None], axis=(2, 3))]
    ppermute x6, waiting for transfers between devices: 5.63 us -> 6.99 us  [exchange_blocks(): pieces.append(lax.ppermute(outgoing, axis, shifted(count, step)))]
    squeeze x1 -> x0, local copies, waits for them, and re-layouts: 1 us -> none  [on_device(): outgoing[step - 1]]
    convert_element_type x1, other arithmetic: 0.7 us -> 0.01 us  [on_device(): sampled = masks[0].astype(jnp.float32)[:, None, :]]
    another operation x1, other arithmetic: 0.68 us -> 0.01 us  [on_device(): jnp.stack([-time_im.T, time_re.T], axis=2)]
    convert_element_type x0 -> x1, other arithmetic: none -> 0.66 us  [on_device(): images = images.astype(jnp.bfloat16)]
    sub x1, other arithmetic: 1.13 us -> 1.68 us  [on_device(): return factors - 0.5 * gradient]
  transfers between devices with their start and end apart: 12 -> 12, of which waited for: 9 -> 9; matrix products, arithmetic and copies ran while one was open for 4% -> 1% of each run, Pallas kernels for 0% -> 0%
where the time goes in v13:
time: 53.4 us; the launch traced here: 53.1 us
  starting transfers between devices  15 us (28%)
  waiting for transfers between devices  14 us (26%)
  Pallas kernels  10.9 us (20%)
  local copies, waits for them, and re-layouts  8.45 us (16%)
  other arithmetic  4.52 us (8%)
    pallas_call x1, Pallas kernels, coil_chain(): pl.pallas_call(coil_chain_kernel, out_shape=(jax.ShapeDtypeStruct((rows,...  10.9 us
    ppermute x6, starting transfers between devices, exchange_blocks(): pieces.append(lax.ppermute(outgoing, axis, shifted(count, step)))  10.9 us
    ppermute x6, waiting for transfers between devices, exchange_blocks(): pieces.append(lax.ppermute(outgoing, axis, shifted(count, step)))  6.99 us
    mul x34, local copies, waits for them, and re-layouts, on_device(): mixing[:, :, part, rank, None, None] * factors[part, rank][None, None]  5.58 us
    ppermute x3, waiting for transfers between devices, on_device(): lax.ppermute(own_rows, 'coil', shifted(groups, step))  4.1 us
    ppermute x3, waiting for transfers between devices, on_device(): lax.ppermute(outgoing[step - 1], 'coil', shifted(groups, step))  2.87 us
    ppermute x3, starting transfers between devices, on_device(): lax.ppermute(outgoing[step - 1], 'coil', shifted(groups, step))  2.36 us
    ppermute x3, starting transfers between devices, on_device(): lax.ppermute(own_rows, 'coil', shifted(groups, step))  1.78 us
  transfers between devices with their start and end apart: 12, of which 9 were waited for; matrix products, arithmetic and copies ran while one was open for 1% of the time, Pallas kernels for 0%

profile of v13, /device:TPU:0, one launch (start us, length us, event | category | flops | bytes accessed | tf_op | source)
XLA Modules:
  0.0 53.1 jit_solution(4404392875419717060)
XLA Ops:
  0.0 0.7 %fusion.39 = f32[4,1,16]{2,0,1:T(4,128)S(1)} fusion(f32[2,4,16]{2,1,0:T(4,128)} %param.10), kind=kLoop, calls=%fused_computation.201 | loop fusion | flops 64 | bytes 512 | tf_op jit(solution)/shard_map/neg | solution.py:235
  0.7 0.7 %slice_bitcast_fusion.42 = (f32[16,4,1]{0,1,2:T(4,128)S(1)}, f32[4,1,16]{2,0,1:T(4,128)S(1)}, f32[4,1,16]{2,0,1:T(4,128)S(1)}, f32[16,4,1]{0,1,2:T(4,128)S(1)}) fusion(f32[2,4,16]{2,1,0:T(4,128)} %param.10), kind=kLoop, calls=%fused_computation.191 | loop fusion | bytes 1536 | tf_op jit(solution)/shard_map/stack | solution.py:264
  2.0 1.0 %slice_bitcast_fusion.38 = (f32[64,64]{1,0:T(8,128)S(1)}, f32[64,64]{1,0:T(8,128)S(1)}, f32[64,64]{1,0:T(8,128)S(1)}, f32[64,64]{1,0:T(8,128)S(1)}, f32[64,64]{1...) fusion(f32[2,16,64,64]{3,2,1,0:T(8,128)} %param.9), kind=kLoop, calls=%fused_computation.66 | loop fusion | bytes 425984 | tf_op jit(solution)/shard_map/mul | solution.py:241
  3.0 1.1 %slice_bitcast_fusion.39 = (f32[64,64]{1,0:T(8,128)S(1)}, f32[64,64]{1,0:T(8,128)S(1)}, f32[64,64]{1,0:T(8,128)S(1)}, f32[64,64]{1,0:T(8,128)S(1)}, f32[64,64]{1...) fusion(f32[2,16,64,64]{3,2,1,0:T(8,128)} %param.9), kind=kLoop, calls=%fused_computation.67 | loop fusion | bytes 622592 | tf_op jit(solution)/shard_map/mul | solution.py:241
  7.6 0.7 %add_convert_fusion = bf16[4,2,64,64]{3,2,1,0:T(8,128)(2,1)S(1)} fusion(f32[64,64]{1,0:T(8,128)S(1)} %get-tuple-element.44, f32[4,2]{1,0:T(4,128)S(1)} %bitcast.203, f32[64,64]{1,0:T(8,128)S(1)} %get-tuple-element.14, f32[4,2]{1,0:T(4,128)S(1)} %bitcast.204, f32[64,64]{1,0:T(8,128)S(1)} %get-tuple-element.15, f32[4,2]{1,0:T(4,128)S(1)} %bitcast.202, ...), kind=kLoop, calls=%fused_computation.1 | loop fusion | flops 2097152 | bytes 590848 | tf_op jit(solution)/shard_map/convert_element_type | solution.py:243
  8.3 3.1 %collective-permute-start.2 = (bf16[2,64,64]{2,1,0:T(8,128)(2,1)S(1)}, bf16[2,64,64]{2,1,0:T(8,128)(2,1)S(1)}, u32[]{:S(2)}, u32[]{:S(2)}) collective-permute-start(bf16[2,64,64]{2,1,0:T(8,128)(2,1)S(1)} %get-tuple-element.57), channel_id=1, source_target_pairs={{0,4},{4,8},{8,12},{12,0},{1,5},{5,9},{9,13},{13,1},{2,6},{6,10},{... | collective-permute-start | bytes 49160 | tf_op jit(solution)/shard_map/ppermute | solution.py:85
  11.3 2.6 %collective-permute-start.1 = (bf16[2,64,64]{2,1,0:T(8,128)(2,1)S(1)}, bf16[2,64,64]{2,1,0:T(8,128)(2,1)S(1)}, u32[]{:S(2)}, u32[]{:S(2)}) collective-permute-start(bf16[2,64,64]{2,1,0:T(8,128)(2,1)S(1)} %get-tuple-element.59), channel_id=1, source_target_pairs={{0,8},{4,12},{8,0},{12,4},{1,9},{5,13},{9,1},{13,5},{2,10},{6,14},... | collective-permute-start | bytes 49160 | tf_op jit(solution)/shard_map/ppermute | solution.py:85
  13.9 1.3 %collective-permute-start = (bf16[2,64,64]{2,1,0:T(8,128)(2,1)S(1)}, bf16[2,64,64]{2,1,0:T(8,128)(2,1)S(1)}, u32[]{:S(2)}, u32[]{:S(2)}) collective-permute-start(bf16[2,64,64]{2,1,0:T(8,128)(2,1)S(1)} %get-tuple-element.60), channel_id=1, source_target_pairs={{0,12},{4,0},{8,4},{12,8},{1,13},{5,1},{9,5},{13,9},{2,14},{6,2},{... | collective-permute-start | bytes 49160 | tf_op jit(solution)/shard_map/ppermute | solution.py:85
  15.3 0.6 %copy.104 = f32[1,8,256]{2,0,1:T(1,128)} copy(f32[1,8,256]{2,1,0:T(8,128)S(1)} %convert_element_type.44) | data formatting | bytes 16384
  15.9 1.9 %collective-permute-done = bf16[2,64,64]{2,1,0:T(8,128)(2,1)S(1)} collective-permute-done((bf16[2,64,64]{2,1,0:T(8,128)(2,1)S(1)}, bf16[2,64,64]{2,1,0:T(8,128)(2,1)S(1)}, u32[]{:S(2)}, u32[]{:S(2)}) %collective-permute-start) | collective-permute-done | bytes 16416 | tf_op jit(solution)/shard_map/ppermute | solution.py:85
  18.3 1.6 %collective-permute-start.4 = (bf16[64,512]{1,0:T(8,128)(2,1)S(1)}, bf16[64,512]{1,0:T(8,128)(2,1)S(1)}, u32[]{:S(2)}, u32[]{:S(2)}) collective-permute-start(bf16[64,512]{1,0:T(8,128)(2,1)S(1)} %reshape.44.refs_0_), channel_id=1, source_target_pairs={{0,2},{1,3},{2,0},{3,1},{4,6},{5,7},{6,4},{7,5},{8,10},{9,11},{10,... | collective-permute-start | bytes 196616 | tf_op jit(solution)/shard_map/ppermute | solution.py:250
  20.2 3.7 %collective-permute-done.4.refs_2_ = bf16[64,512]{1,0:T(8,128)(2,1)S(1)} collective-permute-done((bf16[64,512]{1,0:T(8,128)(2,1)S(1)}, bf16[64,512]{1,0:T(8,128)(2,1)S(1)}, u32[]{:S(2)}, u32[]{:S(2)}) %collective-permute-start.4) | collective-permute-done | bytes 65568 | tf_op jit(solution)/shard_map/ppermute | solution.py:250
  24.8 10.9 %shard_map.91 = (f32[64,512]{1,0:T(8,128)}, bf16[64,512]{1,0:T(8,128)(2,1)}, bf16[64,512]{1,0:T(8,128)(2,1)}, bf16[64,512]{1,0:T(8,128)(2,1)}) custom-call(bf16[64,512]{1,0:T(8,128)(2,1)} %copy-done.1, bf16[64,512]{1,0:T(8,128)(2,1)} %copy-done.6, bf16[64,512]{1,0:T(8,128)(2,1)} %copy-done.5, bf16[64,512]{1,0:T(8,128)(2,1)} %copy-done.4, s32[1]{0:T(128)} %bitcast.88.refs_4_, ...), custom_call_target="tpu_custom_call" | custom-call | flops 4294967296 | bytes 4718592 | tf_op jit(solution)/shard_map/pallas_call | solution.py:197
  35.7 0.9 %collective-permute-start.7 = (bf16[64,512]{1,0:T(8,128)(2,1)}, bf16[64,512]{1,0:T(8,128)(2,1)S(1)}, u32[]{:S(2)}, u32[]{:S(2)}) collective-permute-start(bf16[64,512]{1,0:T(8,128)(2,1)} %get-tuple-element.11), channel_id=1, source_target_pairs={{0,2},{1,3},{2,0},{3,1},{4,6},{5,7},{6,4},{7,5},{8,10},{9,11},{10,... | collective-permute-start | bytes 196616 | tf_op jit(solution)/shard_map/ppermute | solution.py:258
  36.6 1.4 %collective-permute-start.8 = (bf16[64,512]{1,0:T(8,128)(2,1)}, bf16[64,512]{1,0:T(8,128)(2,1)S(1)}, u32[]{:S(2)}, u32[]{:S(2)}) collective-permute-start(bf16[64,512]{1,0:T(8,128)(2,1)} %get-tuple-element.12), channel_id=1, source_target_pairs={{0,3},{1,0},{2,1},{3,2},{4,7},{5,4},{6,5},{7,6},{8,11},{9,8},{10,9... | collective-permute-start | bytes 196616 | tf_op jit(solution)/shard_map/ppermute | solution.py:258
  38.0 1.7 %collective-permute-done.6 = bf16[64,512]{1,0:T(8,128)(2,1)S(1)} collective-permute-done((bf16[64,512]{1,0:T(8,128)(2,1)}, bf16[64,512]{1,0:T(8,128)(2,1)S(1)}, u32[]{:S(2)}, u32[]{:S(2)}) %collective-permute-start.6) | collective-permute-done | bytes 65568 | tf_op jit(solution)/shard_map/ppermute | solution.py:258
  39.7 1.2 %collective-permute-done.7 = bf16[64,512]{1,0:T(8,128)(2,1)S(1)} collective-permute-done((bf16[64,512]{1,0:T(8,128)(2,1)}, bf16[64,512]{1,0:T(8,128)(2,1)S(1)}, u32[]{:S(2)}, u32[]{:S(2)}) %collective-permute-start.7) | collective-permute-done | bytes 65568 | tf_op jit(solution)/shard_map/ppermute | solution.py:258
  40.9 0.9 %add_convert_fusion.1 = bf16[64,512]{1,0:T(8,128)(2,1)S(1)} fusion(bf16[64,512]{1,0:T(8,128)(2,1)S(1)} %collective-permute-done.8, bf16[64,512]{1,0:T(8,128)(2,1)S(1)} %collective-permute-done.7, f32[64,512]{1,0:T(8,128)} %get-tuple-element.9, bf16[64,512]{1,0:T(8,128)(2,1)S(1)} %collective-permute-done.6), kind=kLoop, calls=%fused_computation.3 | loop fusion | flops 229376 | bytes 393216 | tf_op jit(solution)/shard_map/convert_element_type | solution.py:261
  42.3 3.2 %collective-permute-start.9 = (bf16[64,2,64]{2,0,1:T(8,128)(2,1)S(1)}, bf16[64,2,64]{2,0,1:T(8,128)(2,1)S(1)}, u32[]{:S(2)}, u32[]{:S(2)}) collective-permute-start(bf16[64,2,64]{2,0,1:T(8,128)(2,1)S(1)} %bitcast.199), channel_id=1, source_target_pairs={{0,12},{4,0},{8,4},{12,8},{1,13},{5,1},{9,5},{13,9},{2,14},{6,2},{... | collective-permute-start | bytes 49160 | tf_op jit(solution)/shard_map/ppermute | solution.py:85
  45.5 0.6 %collective-permute-start.11 = (bf16[64,2,64]{2,0,1:T(8,128)(2,1)S(1)}, bf16[64,2,64]{2,0,1:T(8,128)(2,1)S(1)}, u32[]{:S(2)}, u32[]{:S(2)}) collective-permute-start(bf16[64,2,64]{2,0,1:T(8,128)(2,1)S(1)} %bitcast.197), channel_id=1, source_target_pairs={{0,4},{4,8},{8,12},{12,0},{1,5},{5,9},{9,13},{13,1},{2,6},{6,10},{... | collective-permute-start | bytes 49160 | tf_op jit(solution)/shard_map/ppermute | solution.py:85
  46.2 1.0 %collective-permute-done.9 = bf16[64,2,64]{2,0,1:T(8,128)(2,1)S(1)} collective-permute-done((bf16[64,2,64]{2,0,1:T(8,128)(2,1)S(1)}, bf16[64,2,64]{2,0,1:T(8,128)(2,1)S(1)}, u32[]{:S(2)}, u32[]{:S(2)}) %collective-permute-start.9) | collective-permute-done | bytes 16416 | tf_op jit(solution)/shard_map/ppermute | solution.py:85
  47.2 3.1 %collective-permute-done.10 = bf16[64,2,64]{2,0,1:T(8,128)(2,1)S(1)} collective-permute-done((bf16[64,2,64]{2,0,1:T(8,128)(2,1)S(1)}, bf16[64,2,64]{2,0,1:T(8,128)(2,1)S(1)}, u32[]{:S(2)}, u32[]{:S(2)}) %collective-permute-start.10) | collective-permute-done | bytes 16416 | tf_op jit(solution)/shard_map/ppermute | solution.py:85
  50.3 0.9 %collective-permute-done.11 = bf16[64,2,64]{2,0,1:T(8,128)(2,1)S(1)} collective-permute-done((bf16[64,2,64]{2,0,1:T(8,128)(2,1)S(1)}, bf16[64,2,64]{2,0,1:T(8,128)(2,1)S(1)}, u32[]{:S(2)}, u32[]{:S(2)}) %collective-permute-start.11) | collective-permute-done | bytes 16416 | tf_op jit(solution)/shard_map/ppermute | solution.py:85
  51.4 1.7 %multiply_subtract_fusion = f32[2,16,64,64]{3,2,1,0:T(8,128)} fusion(f32[2,16,64,64]{3,2,1,0:T(8,128)S(1)} %copy-done, f32[64,64]{1,0:T(8,128)S(1)} %get-tuple-element.46, f32[2,16]{1,0:T(2,128)S(1)} %bitcast.239, f32[64,64]{1,0:T(8,128)S(1)} %get-tuple-element.47, f32[2,16]{1,0:T(2,128)S(1)} %bitcast.240, f32[64,64]{1,0:T(8,128)S(1)} %get-tuple-element.48, ...), kind=kLoop, calls=%fused_computation | loop fusion | flops 2228224 | bytes 1180672 | tf_op jit(solution)/shard_map/sub | solution.py:271
  (91 shorter events, 6.2 us)
Async XLA Ops:
  1.4 13.9 %copy-start.2 = (f32[2,4,16]{2,1,0:T(4,128)S(1)}, f32[2,4,16]{2,1,0:T(4,128)}, u32[]{:S(2)}) copy-start(f32[2,4,16]{2,1,0:T(4,128)} %param.10) | copy-start | bytes 1540
  1.4 13.9 %copy-start.3 = (s32[1,8,256]{2,1,0:T(8,128)S(1)}, s32[1,8,256]{2,1,0:T(8,128)}, u32[]{:S(2)}) copy-start(s32[1,8,256]{2,1,0:T(8,128)} %param.13) | copy-start | bytes 24580
  8.3 9.6 %collective-permute-start.2 = (bf16[2,64,64]{2,1,0:T(8,128)(2,1)S(1)}, bf16[2,64,64]{2,1,0:T(8,128)(2,1)S(1)}, u32[]{:S(2)}, u32[]{:S(2)}) collective-permute-start(bf16[2,64,64]{2,1,0:T(8,128)(2,1)S(1)} %get-tuple-element.57), channel_id=1, source_target_pairs={{0,4},{4,8},{8,12},{12,0},{1,5},{5,9},{9,13},{13,1},{2,6},{6,10},{... | collective-permute-start | bytes 49160 | tf_op jit(solution)/shard_map/ppermute | solution.py:85
  11.3 6.5 %collective-permute-start.1 = (bf16[2,64,64]{2,1,0:T(8,128)(2,1)S(1)}, bf16[2,64,64]{2,1,0:T(8,128)(2,1)S(1)}, u32[]{:S(2)}, u32[]{:S(2)}) collective-permute-start(bf16[2,64,64]{2,1,0:T(8,128)(2,1)S(1)} %get-tuple-element.59), channel_id=1, source_target_pairs={{0,8},{4,12},{8,0},{12,4},{1,9},{5,13},{9,1},{13,5},{2,10},{6,14},... | collective-permute-start | bytes 49160 | tf_op jit(solution)/shard_map/ppermute | solution.py:85
  13.9 3.9 %collective-permute-start = (bf16[2,64,64]{2,1,0:T(8,128)(2,1)S(1)}, bf16[2,64,64]{2,1,0:T(8,128)(2,1)S(1)}, u32[]{:S(2)}, u32[]{:S(2)}) collective-permute-start(bf16[2,64,64]{2,1,0:T(8,128)(2,1)S(1)} %get-tuple-element.60), channel_id=1, source_target_pairs={{0,12},{4,0},{8,4},{12,8},{1,13},{5,1},{9,5},{13,9},{2,14},{6,2},{... | collective-permute-start | bytes 49160 | tf_op jit(solution)/shard_map/ppermute | solution.py:85
  18.3 5.9 %copy-start.1 = (bf16[64,512]{1,0:T(8,128)(2,1)}, bf16[64,512]{1,0:T(8,128)(2,1)S(1)}, u32[]{:S(2)}) copy-start(bf16[64,512]{1,0:T(8,128)(2,1)S(1)} %reshape.44.refs_0_) | copy-start | bytes 196612
  18.3 2.0 %collective-permute-start.5 = (bf16[64,512]{1,0:T(8,128)(2,1)S(1)}, bf16[64,512]{1,0:T(8,128)(2,1)S(1)}, u32[]{:S(2)}, u32[]{:S(2)}) collective-permute-start(bf16[64,512]{1,0:T(8,128)(2,1)S(1)} %reshape.44.refs_0_), channel_id=1, source_target_pairs={{0,3},{1,0},{2,1},{3,2},{4,7},{5,4},{6,5},{7,6},{8,11},{9,8},{10,9... | collective-permute-start | bytes 196616 | tf_op jit(solution)/shard_map/ppermute | solution.py:250
  18.3 5.6 %collective-permute-start.4 = (bf16[64,512]{1,0:T(8,128)(2,1)S(1)}, bf16[64,512]{1,0:T(8,128)(2,1)S(1)}, u32[]{:S(2)}, u32[]{:S(2)}) collective-permute-start(bf16[64,512]{1,0:T(8,128)(2,1)S(1)} %reshape.44.refs_0_), channel_id=1, source_target_pairs={{0,2},{1,3},{2,0},{3,1},{4,6},{5,7},{6,4},{7,5},{8,10},{9,11},{10,... | collective-permute-start | bytes 196616 | tf_op jit(solution)/shard_map/ppermute | solution.py:250
  19.9 4.3 %collective-permute-start.3 = (bf16[64,512]{1,0:T(8,128)(2,1)S(1)}, bf16[64,512]{1,0:T(8,128)(2,1)S(1)}, u32[]{:S(2)}, u32[]{:S(2)}) collective-permute-start(bf16[64,512]{1,0:T(8,128)(2,1)S(1)} %reshape.44.refs_0_), channel_id=1, source_target_pairs={{0,1},{1,2},{2,3},{3,0},{4,5},{5,6},{6,7},{7,4},{8,9},{9,10},{10,1... | collective-permute-start | bytes 196616 | tf_op jit(solution)/shard_map/ppermute | solution.py:250
  20.2 3.9 %copy-start.4 = (bf16[64,512]{1,0:T(8,128)(2,1)}, bf16[64,512]{1,0:T(8,128)(2,1)S(1)}, u32[]{:S(2)}) copy-start(bf16[64,512]{1,0:T(8,128)(2,1)S(1)} %collective-permute-done.5.refs_3_) | copy-start | bytes 196612
  24.0 0.6 %copy-start.5 = (bf16[64,512]{1,0:T(8,128)(2,1)}, bf16[64,512]{1,0:T(8,128)(2,1)S(1)}, u32[]{:S(2)}) copy-start(bf16[64,512]{1,0:T(8,128)(2,1)S(1)} %collective-permute-done.4.refs_2_) | copy-start | bytes 196612
  24.2 0.6 %copy-start.6 = (bf16[64,512]{1,0:T(8,128)(2,1)}, bf16[64,512]{1,0:T(8,128)(2,1)S(1)}, u32[]{:S(2)}) copy-start(bf16[64,512]{1,0:T(8,128)(2,1)S(1)} %collective-permute-done.3.refs_1_) | copy-start | bytes 196612
  35.7 15.7 %copy-start = (f32[2,16,64,64]{3,2,1,0:T(8,128)S(1)}, f32[2,16,64,64]{3,2,1,0:T(8,128)}, u32[]{:S(2)}) copy-start(f32[2,16,64,64]{3,2,1,0:T(8,128)} %param.9) | copy-start | bytes 1572868
  35.7 4.0 %collective-permute-start.6 = (bf16[64,512]{1,0:T(8,128)(2,1)}, bf16[64,512]{1,0:T(8,128)(2,1)S(1)}, u32[]{:S(2)}, u32[]{:S(2)}) collective-permute-start(bf16[64,512]{1,0:T(8,128)(2,1)} %get-tuple-element.10), channel_id=1, source_target_pairs={{0,1},{1,2},{2,3},{3,0},{4,5},{5,6},{6,7},{7,4},{8,9},{9,10},{10,1... | collective-permute-start | bytes 196616 | tf_op jit(solution)/shard_map/ppermute | solution.py:258
  35.7 5.2 %collective-permute-start.7 = (bf16[64,512]{1,0:T(8,128)(2,1)}, bf16[64,512]{1,0:T(8,128)(2,1)S(1)}, u32[]{:S(2)}, u32[]{:S(2)}) collective-permute-start(bf16[64,512]{1,0:T(8,128)(2,1)} %get-tuple-element.11), channel_id=1, source_target_pairs={{0,2},{1,3},{2,0},{3,1},{4,6},{5,7},{6,4},{7,5},{8,10},{9,11},{10,... | collective-permute-start | bytes 196616 | tf_op jit(solution)/shard_map/ppermute | solution.py:258
  36.6 4.3 %collective-permute-start.8 = (bf16[64,512]{1,0:T(8,128)(2,1)}, bf16[64,512]{1,0:T(8,128)(2,1)S(1)}, u32[]{:S(2)}, u32[]{:S(2)}) collective-permute-start(bf16[64,512]{1,0:T(8,128)(2,1)} %get-tuple-element.12), channel_id=1, source_target_pairs={{0,3},{1,0},{2,1},{3,2},{4,7},{5,4},{6,5},{7,6},{8,11},{9,8},{10,9... | collective-permute-start | bytes 196616 | tf_op jit(solution)/shard_map/ppermute | solution.py:258
  42.3 4.9 %collective-permute-start.9 = (bf16[64,2,64]{2,0,1:T(8,128)(2,1)S(1)}, bf16[64,2,64]{2,0,1:T(8,128)(2,1)S(1)}, u32[]{:S(2)}, u32[]{:S(2)}) collective-permute-start(bf16[64,2,64]{2,0,1:T(8,128)(2,1)S(1)} %bitcast.199), channel_id=1, source_target_pairs={{0,12},{4,0},{8,4},{12,8},{1,13},{5,1},{9,5},{13,9},{2,14},{6,2},{... | collective-permute-start | bytes 49160 | tf_op jit(solution)/shard_map/ppermute | solution.py:85
  45.5 4.8 %collective-permute-start.10 = (bf16[64,2,64]{2,0,1:T(8,128)(2,1)S(1)}, bf16[64,2,64]{2,0,1:T(8,128)(2,1)S(1)}, u32[]{:S(2)}, u32[]{:S(2)}) collective-permute-start(bf16[64,2,64]{2,0,1:T(8,128)(2,1)S(1)} %bitcast.198), channel_id=1, source_target_pairs={{0,8},{4,12},{8,0},{12,4},{1,9},{5,13},{9,1},{13,5},{2,10},{6,14},... | collective-permute-start | bytes 49160 | tf_op jit(solution)/shard_map/ppermute | solution.py:85
  45.5 5.7 %collective-permute-start.11 = (bf16[64,2,64]{2,0,1:T(8,128)(2,1)S(1)}, bf16[64,2,64]{2,0,1:T(8,128)(2,1)S(1)}, u32[]{:S(2)}, u32[]{:S(2)}) collective-permute-start(bf16[64,2,64]{2,0,1:T(8,128)(2,1)S(1)} %bitcast.197), channel_id=1, source_target_pairs={{0,4},{4,8},{8,12},{12,0},{1,5},{5,9},{9,13},{13,1},{2,6},{6,10},{... | collective-permute-start | bytes 49160 | tf_op jit(solution)/shard_map/ppermute | solution.py:85

commit v14 on v13

--- a/solution.py
+++ b/solution.py
@@ -234,13 +234,9 @@
     mixing = jnp.stack(
         [jnp.stack([time_re, -time_im], axis=1), jnp.stack([time_im, time_re], axis=1)], axis=1
     )
-    parts, ranks = factors.shape[:2]
-    images = None
-    for part in range(parts):
-        for rank in range(ranks):
-            term = mixing[:, :, part, rank, None, None] * factors[part, rank][None, None]
-            images = term if images is None else images + term
-    images = images.astype(jnp.bfloat16)
+    images = jnp.sum(
+        mixing[:, :, :, :, None, None] * factors[None, None], axis=(2, 3)
+    ).astype(jnp.bfloat16)
     frames_here = images.shape[0]
     width_own = images.shape[3]
     pieces_x = exchange_blocks(images, "frame")

time: 53.4 us -> 48.8 us (0.914)
  local copies, waits for them, and re-layouts: 8.45 us -> 2.84 us
  other arithmetic: 4.52 us -> 7.02 us
  waiting for transfers between devices: 14 us -> 12.6 us
    mul x34 -> x0, local copies, waits for them, and re-layouts: 5.58 us -> none  [on_device(): mixing[:, :, part, rank, None, None] * factors[part, rank][None, None]]
    reduce_sum x0 -> x1, other arithmetic: none -> 2.29 us  [on_device(): jnp.sum(mixing[:, :, :, :, None, None] * factors[None, None], axis=(2, 3))]
    ppermute x6, waiting for transfers between devices: 6.99 us -> 5.63 us  [exchange_blocks(): pieces.append(lax.ppermute(outgoing, axis, shifted(count, step)))]
    convert_element_type x1, other arithmetic: 0.01 us -> 0.7 us  [on_device(): sampled = masks[0].astype(jnp.float32)[:, None, :]]
    another operation x1, other arithmetic: 0.01 us -> 0.68 us  [on_device(): jnp.stack([-time_im.T, time_re.T], axis=2)]
    convert_element_type x1 -> x0, other arithmetic: 0.66 us -> none  [on_device(): images = images.astype(jnp.bfloat16)]
    unnamed x31 -> x27, local copies, waits for them, and re-layouts: 1.42 us -> 1.4 us
  transfers between devices with their start and end apart: 12 -> 12, of which waited for: 9 -> 9; matrix products, arithmetic and copies ran while one was open for 1% -> 4% of each run, Pallas kernels for 0% -> 0%
where the time goes in v14:
time: 48.8 us; the launch traced here: 48.5 us
  starting transfers between devices  15 us (31%)
  waiting for transfers between devices  12.6 us (26%)
  Pallas kernels  10.8 us (22%)
  other arithmetic  7.02 us (14%)
  local copies, waits for them, and re-layouts  2.84 us (6%)
    ppermute x6, starting transfers between devices, exchange_blocks(): pieces.append(lax.ppermute(outgoing, axis, shifted(count, step)))  10.9 us
    pallas_call x1, Pallas kernels, coil_chain(): pl.pallas_call(coil_chain_kernel, out_shape=(jax.ShapeDtypeStruct((rows,...  10.8 us
    ppermute x6, waiting for transfers between devices, exchange_blocks(): pieces.append(lax.ppermute(outgoing, axis, shifted(count, step)))  5.63 us
    ppermute x3, waiting for transfers between devices, on_device(): lax.ppermute(own_rows, 'coil', shifted(groups, step))  4.1 us
    ppermute x3, waiting for transfers between devices, on_device(): lax.ppermute(outgoing[step - 1], 'coil', shifted(groups, step))  2.85 us
    ppermute x3, starting transfers between devices, on_device(): lax.ppermute(outgoing[step - 1], 'coil', shifted(groups, step))  2.38 us
    reduce_sum x1, other arithmetic, on_device(): jnp.sum(mixing[:, :, :, :, None, None] * factors[None, None], axis=(2, 3))  2.29 us
    ppermute x3, starting transfers between devices, on_device(): lax.ppermute(own_rows, 'coil', shifted(groups, step))  1.78 us
  transfers between devices with their start and end apart: 12, of which 9 were waited for; matrix products, arithmetic and copies ran while one was open for 4% of the time, Pallas kernels for 0%

profile of v14, /device:TPU:0, one launch (start us, length us, event | category | flops | bytes accessed | tf_op | source)
XLA Modules:
  0.0 48.5 jit_solution(747877751636504376)
XLA Ops:
  0.0 0.7 %fusion.8 = f32[4,1,16]{2,0,1:T(4,128)S(1)} fusion(f32[2,4,16]{2,1,0:T(4,128)} %param.10), kind=kLoop, calls=%fused_computation.76 | loop fusion | flops 64 | bytes 512 | tf_op jit(solution)/shard_map/neg | solution.py:235
  0.7 0.7 %slice_bitcast_fusion.10 = (f32[16,4,1]{0,1,2:T(4,128)S(1)}, f32[4,1,16]{2,0,1:T(4,128)S(1)}, f32[4,1,16]{2,0,1:T(4,128)S(1)}, f32[16,4,1]{0,1,2:T(4,128)S(1)}) fusion(f32[2,4,16]{2,1,0:T(4,128)} %param.10), kind=kLoop, calls=%fused_computation.66 | loop fusion | bytes 1536 | tf_op jit(solution)/shard_map/stack | solution.py:260
  1.4 2.3 %multiply_reduce_fusion = bf16[4,2,64,64]{3,2,1,0:T(8,128)(2,1)S(1)} fusion(f32[2,16,64,64]{3,2,1,0:T(8,128)} %param.9, f32[4,1,2,16]{3,2,0,1:T(2,128)S(1)} %get-tuple-element.45, f32[4,1,2,16]{3,2,0,1:T(2,128)S(1)} %get-tuple-element.46), kind=kLoop, calls=%fused_computation | loop fusion | flops 2064640 | bytes 590848 | tf_op jit(solution)/shard_map/reduce_sum | solution.py:237
  3.7 3.1 %collective-permute-start.2 = (bf16[2,64,64]{2,1,0:T(8,128)(2,1)S(1)}, bf16[2,64,64]{2,1,0:T(8,128)(2,1)S(1)}, u32[]{:S(2)}, u32[]{:S(2)}) collective-permute-start(bf16[2,64,64]{2,1,0:T(8,128)(2,1)S(1)} %get-tuple-element.25), channel_id=1, source_target_pairs={{0,4},{4,8},{8,12},{12,0},{1,5},{5,9},{9,13},{13,1},{2,6},{6,10},{... | collective-permute-start | bytes 49160 | tf_op jit(solution)/shard_map/ppermute | solution.py:85
  6.8 2.6 %collective-permute-start.1 = (bf16[2,64,64]{2,1,0:T(8,128)(2,1)S(1)}, bf16[2,64,64]{2,1,0:T(8,128)(2,1)S(1)}, u32[]{:S(2)}, u32[]{:S(2)}) collective-permute-start(bf16[2,64,64]{2,1,0:T(8,128)(2,1)S(1)} %get-tuple-element.26), channel_id=1, source_target_pairs={{0,8},{4,12},{8,0},{12,4},{1,9},{5,13},{9,1},{13,5},{2,10},{6,14},... | collective-permute-start | bytes 49160 | tf_op jit(solution)/shard_map/ppermute | solution.py:85
  9.4 1.3 %collective-permute-start = (bf16[2,64,64]{2,1,0:T(8,128)(2,1)S(1)}, bf16[2,64,64]{2,1,0:T(8,128)(2,1)S(1)}, u32[]{:S(2)}, u32[]{:S(2)}) collective-permute-start(bf16[2,64,64]{2,1,0:T(8,128)(2,1)S(1)} %get-tuple-element.27), channel_id=1, source_target_pairs={{0,12},{4,0},{8,4},{12,8},{1,13},{5,1},{9,5},{13,9},{2,14},{6,2},{... | collective-permute-start | bytes 49160 | tf_op jit(solution)/shard_map/ppermute | solution.py:85
  10.7 0.7 %fusion = f32[16,4,1]{0,1,2:T(4,128)S(1)} fusion(f32[2,4,16]{2,1,0:T(4,128)} %param.10), kind=kLoop, calls=%fused_computation.63 | loop fusion | flops 64 | bytes 512 | tf_op jit(solution)/shard_map/stack | solution.py:260
  11.4 0.7 %convert_element_type.44 = f32[1,8,256]{2,1,0:T(8,128)S(1)} convert(s32[1,8,256]{2,1,0:T(8,128)} %param.13) | non-fusion elementwise | flops 2048 | bytes 16384 | tf_op jit(solution)/shard_map/convert_element_type | solution.py:247
  12.1 0.6 %copy.53 = f32[1,8,256]{2,0,1:T(1,128)} copy(f32[1,8,256]{2,1,0:T(8,128)S(1)} %convert_element_type.44) | data formatting | bytes 16384
  12.7 0.6 %collective-permute-done = bf16[2,64,64]{2,1,0:T(8,128)(2,1)S(1)} collective-permute-done((bf16[2,64,64]{2,1,0:T(8,128)(2,1)S(1)}, bf16[2,64,64]{2,1,0:T(8,128)(2,1)S(1)}, u32[]{:S(2)}, u32[]{:S(2)}) %collective-permute-start) | collective-permute-done | bytes 16416 | tf_op jit(solution)/shard_map/ppermute | solution.py:85
  13.8 1.6 %collective-permute-start.4 = (bf16[64,512]{1,0:T(8,128)(2,1)S(1)}, bf16[64,512]{1,0:T(8,128)(2,1)S(1)}, u32[]{:S(2)}, u32[]{:S(2)}) collective-permute-start(bf16[64,512]{1,0:T(8,128)(2,1)S(1)} %reshape.46.refs_0_), channel_id=1, source_target_pairs={{0,2},{1,3},{2,0},{3,1},{4,6},{5,7},{6,4},{7,5},{8,10},{9,11},{10,... | collective-permute-start | bytes 196616 | tf_op jit(solution)/shard_map/ppermute | solution.py:246
  15.7 3.7 %collective-permute-done.4.refs_2_ = bf16[64,512]{1,0:T(8,128)(2,1)S(1)} collective-permute-done((bf16[64,512]{1,0:T(8,128)(2,1)S(1)}, bf16[64,512]{1,0:T(8,128)(2,1)S(1)}, u32[]{:S(2)}, u32[]{:S(2)}) %collective-permute-start.4) | collective-permute-done | bytes 65568 | tf_op jit(solution)/shard_map/ppermute | solution.py:246
  20.2 10.8 %shard_map.91 = (f32[64,512]{1,0:T(8,128)}, bf16[64,512]{1,0:T(8,128)(2,1)}, bf16[64,512]{1,0:T(8,128)(2,1)}, bf16[64,512]{1,0:T(8,128)(2,1)}) custom-call(bf16[64,512]{1,0:T(8,128)(2,1)} %copy-done.1, bf16[64,512]{1,0:T(8,128)(2,1)} %copy-done.4, bf16[64,512]{1,0:T(8,128)(2,1)} %copy-done.3, bf16[64,512]{1,0:T(8,128)(2,1)} %copy-done.2, s32[1]{0:T(128)} %bitcast.24.refs_4_, ...), custom_call_target="tpu_custom_call" | custom-call | flops 4294967296 | bytes 4718592 | tf_op jit(solution)/shard_map/pallas_call | solution.py:197
  31.1 0.9 %collective-permute-start.7 = (bf16[64,512]{1,0:T(8,128)(2,1)}, bf16[64,512]{1,0:T(8,128)(2,1)S(1)}, u32[]{:S(2)}, u32[]{:S(2)}) collective-permute-start(bf16[64,512]{1,0:T(8,128)(2,1)} %get-tuple-element.11), channel_id=1, source_target_pairs={{0,2},{1,3},{2,0},{3,1},{4,6},{5,7},{6,4},{7,5},{8,10},{9,11},{10,... | collective-permute-start | bytes 196616 | tf_op jit(solution)/shard_map/ppermute | solution.py:254
  32.1 1.4 %collective-permute-start.8 = (bf16[64,512]{1,0:T(8,128)(2,1)}, bf16[64,512]{1,0:T(8,128)(2,1)S(1)}, u32[]{:S(2)}, u32[]{:S(2)}) collective-permute-start(bf16[64,512]{1,0:T(8,128)(2,1)} %get-tuple-element.12), channel_id=1, source_target_pairs={{0,3},{1,0},{2,1},{3,2},{4,7},{5,4},{6,5},{7,6},{8,11},{9,8},{10,9... | collective-permute-start | bytes 196616 | tf_op jit(solution)/shard_map/ppermute | solution.py:254
  33.5 1.6 %collective-permute-done.6 = bf16[64,512]{1,0:T(8,128)(2,1)S(1)} collective-permute-done((bf16[64,512]{1,0:T(8,128)(2,1)}, bf16[64,512]{1,0:T(8,128)(2,1)S(1)}, u32[]{:S(2)}, u32[]{:S(2)}) %collective-permute-start.6) | collective-permute-done | bytes 65568 | tf_op jit(solution)/shard_map/ppermute | solution.py:254
  35.1 1.2 %collective-permute-done.7 = bf16[64,512]{1,0:T(8,128)(2,1)S(1)} collective-permute-done((bf16[64,512]{1,0:T(8,128)(2,1)}, bf16[64,512]{1,0:T(8,128)(2,1)S(1)}, u32[]{:S(2)}, u32[]{:S(2)}) %collective-permute-start.7) | collective-permute-done | bytes 65568 | tf_op jit(solution)/shard_map/ppermute | solution.py:254
  36.3 0.9 %add_convert_fusion = bf16[64,512]{1,0:T(8,128)(2,1)S(1)} fusion(bf16[64,512]{1,0:T(8,128)(2,1)S(1)} %collective-permute-done.8, bf16[64,512]{1,0:T(8,128)(2,1)S(1)} %collective-permute-done.7, f32[64,512]{1,0:T(8,128)} %get-tuple-element.9, bf16[64,512]{1,0:T(8,128)(2,1)S(1)} %collective-permute-done.6), kind=kLoop, calls=%fused_computation.3 | loop fusion | flops 229376 | bytes 393216 | tf_op jit(solution)/shard_map/convert_element_type | solution.py:257
  37.8 3.2 %collective-permute-start.9 = (bf16[64,2,64]{2,0,1:T(8,128)(2,1)S(1)}, bf16[64,2,64]{2,0,1:T(8,128)(2,1)S(1)}, u32[]{:S(2)}, u32[]{:S(2)}) collective-permute-start(bf16[64,2,64]{2,0,1:T(8,128)(2,1)S(1)} %bitcast.103), channel_id=1, source_target_pairs={{0,12},{4,0},{8,4},{12,8},{1,13},{5,1},{9,5},{13,9},{2,14},{6,2},{... | collective-permute-start | bytes 49160 | tf_op jit(solution)/shard_map/ppermute | solution.py:85
  41.0 0.6 %collective-permute-start.11 = (bf16[64,2,64]{2,0,1:T(8,128)(2,1)S(1)}, bf16[64,2,64]{2,0,1:T(8,128)(2,1)S(1)}, u32[]{:S(2)}, u32[]{:S(2)}) collective-permute-start(bf16[64,2,64]{2,0,1:T(8,128)(2,1)S(1)} %bitcast.101), channel_id=1, source_target_pairs={{0,4},{4,8},{8,12},{12,0},{1,5},{5,9},{9,13},{13,1},{2,6},{6,10},{... | collective-permute-start | bytes 49160 | tf_op jit(solution)/shard_map/ppermute | solution.py:85
  41.6 1.0 %collective-permute-done.9 = bf16[64,2,64]{2,0,1:T(8,128)(2,1)S(1)} collective-permute-done((bf16[64,2,64]{2,0,1:T(8,128)(2,1)S(1)}, bf16[64,2,64]{2,0,1:T(8,128)(2,1)S(1)}, u32[]{:S(2)}, u32[]{:S(2)}) %collective-permute-start.9) | collective-permute-done | bytes 16416 | tf_op jit(solution)/shard_map/ppermute | solution.py:85
  42.6 3.1 %collective-permute-done.10 = bf16[64,2,64]{2,0,1:T(8,128)(2,1)S(1)} collective-permute-done((bf16[64,2,64]{2,0,1:T(8,128)(2,1)S(1)}, bf16[64,2,64]{2,0,1:T(8,128)(2,1)S(1)}, u32[]{:S(2)}, u32[]{:S(2)}) %collective-permute-start.10) | collective-permute-done | bytes 16416 | tf_op jit(solution)/shard_map/ppermute | solution.py:85
  45.8 0.9 %collective-permute-done.11 = bf16[64,2,64]{2,0,1:T(8,128)(2,1)S(1)} collective-permute-done((bf16[64,2,64]{2,0,1:T(8,128)(2,1)S(1)}, bf16[64,2,64]{2,0,1:T(8,128)(2,1)S(1)}, u32[]{:S(2)}, u32[]{:S(2)}) %collective-permute-start.11) | collective-permute-done | bytes 16416 | tf_op jit(solution)/shard_map/ppermute | solution.py:85
  46.8 1.7 %multiply_subtract_fusion = f32[2,16,64,64]{3,2,1,0:T(8,128)} fusion(f32[2,16,64,64]{3,2,1,0:T(8,128)S(1)} %copy-done, f32[64,64]{1,0:T(8,128)S(1)} %get-tuple-element.14, f32[2,16]{1,0:T(2,128)S(1)} %bitcast.111, f32[64,64]{1,0:T(8,128)S(1)} %get-tuple-element.15, f32[2,16]{1,0:T(2,128)S(1)} %bitcast.112, f32[64,64]{1,0:T(8,128)S(1)} %get-tuple-element.16, ...), kind=kLoop, calls=%fused_computation.1 | loop fusion | flops 2228224 | bytes 1180672 | tf_op jit(solution)/shard_map/sub | solution.py:267
  (49 shorter events, 2.2 us)
Async XLA Ops:
  3.7 9.6 %collective-permute-start.2 = (bf16[2,64,64]{2,1,0:T(8,128)(2,1)S(1)}, bf16[2,64,64]{2,1,0:T(8,128)(2,1)S(1)}, u32[]{:S(2)}, u32[]{:S(2)}) collective-permute-start(bf16[2,64,64]{2,1,0:T(8,128)(2,1)S(1)} %get-tuple-element.25), channel_id=1, source_target_pairs={{0,4},{4,8},{8,12},{12,0},{1,5},{5,9},{9,13},{13,1},{2,6},{6,10},{... | collective-permute-start | bytes 49160 | tf_op jit(solution)/shard_map/ppermute | solution.py:85
  6.8 6.5 %collective-permute-start.1 = (bf16[2,64,64]{2,1,0:T(8,128)(2,1)S(1)}, bf16[2,64,64]{2,1,0:T(8,128)(2,1)S(1)}, u32[]{:S(2)}, u32[]{:S(2)}) collective-permute-start(bf16[2,64,64]{2,1,0:T(8,128)(2,1)S(1)} %get-tuple-element.26), channel_id=1, source_target_pairs={{0,8},{4,12},{8,0},{12,4},{1,9},{5,13},{9,1},{13,5},{2,10},{6,14},... | collective-permute-start | bytes 49160 | tf_op jit(solution)/shard_map/ppermute | solution.py:85
  9.4 3.9 %collective-permute-start = (bf16[2,64,64]{2,1,0:T(8,128)(2,1)S(1)}, bf16[2,64,64]{2,1,0:T(8,128)(2,1)S(1)}, u32[]{:S(2)}, u32[]{:S(2)}) collective-permute-start(bf16[2,64,64]{2,1,0:T(8,128)(2,1)S(1)} %get-tuple-element.27), channel_id=1, source_target_pairs={{0,12},{4,0},{8,4},{12,8},{1,13},{5,1},{9,5},{13,9},{2,14},{6,2},{... | collective-permute-start | bytes 49160 | tf_op jit(solution)/shard_map/ppermute | solution.py:85
  13.7 5.9 %copy-start.1 = (bf16[64,512]{1,0:T(8,128)(2,1)}, bf16[64,512]{1,0:T(8,128)(2,1)S(1)}, u32[]{:S(2)}) copy-start(bf16[64,512]{1,0:T(8,128)(2,1)S(1)} %reshape.46.refs_0_) | copy-start | bytes 196612
  13.7 2.0 %collective-permute-start.5 = (bf16[64,512]{1,0:T(8,128)(2,1)S(1)}, bf16[64,512]{1,0:T(8,128)(2,1)S(1)}, u32[]{:S(2)}, u32[]{:S(2)}) collective-permute-start(bf16[64,512]{1,0:T(8,128)(2,1)S(1)} %reshape.46.refs_0_), channel_id=1, source_target_pairs={{0,3},{1,0},{2,1},{3,2},{4,7},{5,4},{6,5},{7,6},{8,11},{9,8},{10,9... | collective-permute-start | bytes 196616 | tf_op jit(solution)/shard_map/ppermute | solution.py:246
  13.8 5.6 %collective-permute-start.4 = (bf16[64,512]{1,0:T(8,128)(2,1)S(1)}, bf16[64,512]{1,0:T(8,128)(2,1)S(1)}, u32[]{:S(2)}, u32[]{:S(2)}) collective-permute-start(bf16[64,512]{1,0:T(8,128)(2,1)S(1)} %reshape.46.refs_0_), channel_id=1, source_target_pairs={{0,2},{1,3},{2,0},{3,1},{4,6},{5,7},{6,4},{7,5},{8,10},{9,11},{10,... | collective-permute-start | bytes 196616 | tf_op jit(solution)/shard_map/ppermute | solution.py:246
  15.3 4.3 %collective-permute-start.3 = (bf16[64,512]{1,0:T(8,128)(2,1)S(1)}, bf16[64,512]{1,0:T(8,128)(2,1)S(1)}, u32[]{:S(2)}, u32[]{:S(2)}) collective-permute-start(bf16[64,512]{1,0:T(8,128)(2,1)S(1)} %reshape.46.refs_0_), channel_id=1, source_target_pairs={{0,1},{1,2},{2,3},{3,0},{4,5},{5,6},{6,7},{7,4},{8,9},{9,10},{10,1... | collective-permute-start | bytes 196616 | tf_op jit(solution)/shard_map/ppermute | solution.py:246
  15.7 3.9 %copy-start.2 = (bf16[64,512]{1,0:T(8,128)(2,1)}, bf16[64,512]{1,0:T(8,128)(2,1)S(1)}, u32[]{:S(2)}) copy-start(bf16[64,512]{1,0:T(8,128)(2,1)S(1)} %collective-permute-done.5.refs_3_) | copy-start | bytes 196612
  19.4 0.6 %copy-start.3 = (bf16[64,512]{1,0:T(8,128)(2,1)}, bf16[64,512]{1,0:T(8,128)(2,1)S(1)}, u32[]{:S(2)}) copy-start(bf16[64,512]{1,0:T(8,128)(2,1)S(1)} %collective-permute-done.4.refs_2_) | copy-start | bytes 196612
  19.6 0.6 %copy-start.4 = (bf16[64,512]{1,0:T(8,128)(2,1)}, bf16[64,512]{1,0:T(8,128)(2,1)S(1)}, u32[]{:S(2)}) copy-start(bf16[64,512]{1,0:T(8,128)(2,1)S(1)} %collective-permute-done.3.refs_1_) | copy-start | bytes 196612
  31.1 15.7 %copy-start = (f32[2,16,64,64]{3,2,1,0:T(8,128)S(1)}, f32[2,16,64,64]{3,2,1,0:T(8,128)}, u32[]{:S(2)}) copy-start(f32[2,16,64,64]{3,2,1,0:T(8,128)} %param.9) | copy-start | bytes 1572868
  31.1 4.0 %collective-permute-start.6 = (bf16[64,512]{1,0:T(8,128)(2,1)}, bf16[64,512]{1,0:T(8,128)(2,1)S(1)}, u32[]{:S(2)}, u32[]{:S(2)}) collective-permute-start(bf16[64,512]{1,0:T(8,128)(2,1)} %get-tuple-element.10), channel_id=1, source_target_pairs={{0,1},{1,2},{2,3},{3,0},{4,5},{5,6},{6,7},{7,4},{8,9},{9,10},{10,1... | collective-permute-start | bytes 196616 | tf_op jit(solution)/shard_map/ppermute | solution.py:254
  31.1 5.2 %collective-permute-start.7 = (bf16[64,512]{1,0:T(8,128)(2,1)}, bf16[64,512]{1,0:T(8,128)(2,1)S(1)}, u32[]{:S(2)}, u32[]{:S(2)}) collective-permute-start(bf16[64,512]{1,0:T(8,128)(2,1)} %get-tuple-element.11), channel_id=1, source_target_pairs={{0,2},{1,3},{2,0},{3,1},{4,6},{5,7},{6,4},{7,5},{8,10},{9,11},{10,... | collective-permute-start | bytes 196616 | tf_op jit(solution)/shard_map/ppermute | solution.py:254
  32.1 4.3 %collective-permute-start.8 = (bf16[64,512]{1,0:T(8,128)(2,1)}, bf16[64,512]{1,0:T(8,128)(2,1)S(1)}, u32[]{:S(2)}, u32[]{:S(2)}) collective-permute-start(bf16[64,512]{1,0:T(8,128)(2,1)} %get-tuple-element.12), channel_id=1, source_target_pairs={{0,3},{1,0},{2,1},{3,2},{4,7},{5,4},{6,5},{7,6},{8,11},{9,8},{10,9... | collective-permute-start | bytes 196616 | tf_op jit(solution)/shard_map/ppermute | solution.py:254
  37.8 4.9 %collective-permute-start.9 = (bf16[64,2,64]{2,0,1:T(8,128)(2,1)S(1)}, bf16[64,2,64]{2,0,1:T(8,128)(2,1)S(1)}, u32[]{:S(2)}, u32[]{:S(2)}) collective-permute-start(bf16[64,2,64]{2,0,1:T(8,128)(2,1)S(1)} %bitcast.103), channel_id=1, source_target_pairs={{0,12},{4,0},{8,4},{12,8},{1,13},{5,1},{9,5},{13,9},{2,14},{6,2},{... | collective-permute-start | bytes 49160 | tf_op jit(solution)/shard_map/ppermute | solution.py:85
  40.9 4.8 %collective-permute-start.10 = (bf16[64,2,64]{2,0,1:T(8,128)(2,1)S(1)}, bf16[64,2,64]{2,0,1:T(8,128)(2,1)S(1)}, u32[]{:S(2)}, u32[]{:S(2)}) collective-permute-start(bf16[64,2,64]{2,0,1:T(8,128)(2,1)S(1)} %bitcast.102), channel_id=1, source_target_pairs={{0,8},{4,12},{8,0},{12,4},{1,9},{5,13},{9,1},{13,5},{2,10},{6,14},... | collective-permute-start | bytes 49160 | tf_op jit(solution)/shard_map/ppermute | solution.py:85
  41.0 5.7 %collective-permute-start.11 = (bf16[64,2,64]{2,0,1:T(8,128)(2,1)S(1)}, bf16[64,2,64]{2,0,1:T(8,128)(2,1)S(1)}, u32[]{:S(2)}, u32[]{:S(2)}) collective-permute-start(bf16[64,2,64]{2,0,1:T(8,128)(2,1)S(1)} %bitcast.101), channel_id=1, source_target_pairs={{0,4},{4,8},{8,12},{12,0},{1,5},{5,9},{9,13},{13,1},{2,6},{6,10},{... | collective-permute-start | bytes 49160 | tf_op jit(solution)/shard_map/ppermute | solution.py:85

commit v15 on v14

--- a/solution.py
+++ b/solution.py
@@ -192,7 +192,7 @@
     rows = pieces[0].shape[0]
     whole = lambda c: (0, 0)
     per_coil = lambda c: (c, 0, 0)
-    step_coils = 2 if coils % 2 == 0 else 1
+    step_coils = 4 if coils % 4 == 0 else (2 if coils % 2 == 0 else 1)
     flops = coils * 8 * height * width * width
     return pl.pallas_call(
         coil_chain_kernel,

time: 48.8 us -> 48.9 us (level)
  no operation moved by 1% of the time
where the time goes in v15:
time: 48.9 us; the launch traced here: 48.6 us
  starting transfers between devices  15 us (31%)
  waiting for transfers between devices  12.6 us (26%)
  Pallas kernels  10.9 us (22%)
  other arithmetic  7.02 us (14%)
  local copies, waits for them, and re-layouts  2.84 us (6%)
    pallas_call x1, Pallas kernels, coil_chain(): pl.pallas_call(coil_chain_kernel, out_shape=(jax.ShapeDtypeStruct((rows,...  10.9 us
    ppermute x6, starting transfers between devices, exchange_blocks(): pieces.append(lax.ppermute(outgoing, axis, shifted(count, step)))  10.9 us
    ppermute x6, waiting for transfers between devices, exchange_blocks(): pieces.append(lax.ppermute(outgoing, axis, shifted(count, step)))  5.63 us
    ppermute x3, waiting for transfers between devices, on_device(): lax.ppermute(own_rows, 'coil', shifted(groups, step))  4.1 us
    ppermute x3, waiting for transfers between devices, on_device(): lax.ppermute(outgoing[step - 1], 'coil', shifted(groups, step))  2.86 us
    ppermute x3, starting transfers between devices, on_device(): lax.ppermute(outgoing[step - 1], 'coil', shifted(groups, step))  2.37 us
    reduce_sum x1, other arithmetic, on_device(): jnp.sum(mixing[:, :, :, :, None, None] * factors[None, None], axis=(2, 3))  2.29 us
    ppermute x3, starting transfers between devices, on_device(): lax.ppermute(own_rows, 'coil', shifted(groups, step))  1.78 us
  transfers between devices with their start and end apart: 12, of which 9 were waited for; matrix products, arithmetic and copies ran while one was open for 4% of the time, Pallas kernels for 0%

profile of v15, /device:TPU:0, one launch (start us, length us, event | category | flops | bytes accessed | tf_op | source)
XLA Modules:
  0.0 48.6 jit_solution(13779836546436140938)
XLA Ops:
  0.0 0.7 %fusion.8 = f32[4,1,16]{2,0,1:T(4,128)S(1)} fusion(f32[2,4,16]{2,1,0:T(4,128)} %param.10), kind=kLoop, calls=%fused_computation.76 | loop fusion | flops 64 | bytes 512 | tf_op jit(solution)/shard_map/neg | solution.py:235
  0.7 0.7 %slice_bitcast_fusion.10 = (f32[16,4,1]{0,1,2:T(4,128)S(1)}, f32[4,1,16]{2,0,1:T(4,128)S(1)}, f32[4,1,16]{2,0,1:T(4,128)S(1)}, f32[16,4,1]{0,1,2:T(4,128)S(1)}) fusion(f32[2,4,16]{2,1,0:T(4,128)} %param.10), kind=kLoop, calls=%fused_computation.66 | loop fusion | bytes 1536 | tf_op jit(solution)/shard_map/stack | solution.py:260
  1.4 2.3 %multiply_reduce_fusion = bf16[4,2,64,64]{3,2,1,0:T(8,128)(2,1)S(1)} fusion(f32[2,16,64,64]{3,2,1,0:T(8,128)} %param.9, f32[4,1,2,16]{3,2,0,1:T(2,128)S(1)} %get-tuple-element.45, f32[4,1,2,16]{3,2,0,1:T(2,128)S(1)} %get-tuple-element.46), kind=kLoop, calls=%fused_computation | loop fusion | flops 2064640 | bytes 590848 | tf_op jit(solution)/shard_map/reduce_sum | solution.py:237
  3.7 3.1 %collective-permute-start.2 = (bf16[2,64,64]{2,1,0:T(8,128)(2,1)S(1)}, bf16[2,64,64]{2,1,0:T(8,128)(2,1)S(1)}, u32[]{:S(2)}, u32[]{:S(2)}) collective-permute-start(bf16[2,64,64]{2,1,0:T(8,128)(2,1)S(1)} %get-tuple-element.25), channel_id=1, source_target_pairs={{0,4},{4,8},{8,12},{12,0},{1,5},{5,9},{9,13},{13,1},{2,6},{6,10},{... | collective-permute-start | bytes 49160 | tf_op jit(solution)/shard_map/ppermute | solution.py:85
  6.8 2.6 %collective-permute-start.1 = (bf16[2,64,64]{2,1,0:T(8,128)(2,1)S(1)}, bf16[2,64,64]{2,1,0:T(8,128)(2,1)S(1)}, u32[]{:S(2)}, u32[]{:S(2)}) collective-permute-start(bf16[2,64,64]{2,1,0:T(8,128)(2,1)S(1)} %get-tuple-element.26), channel_id=1, source_target_pairs={{0,8},{4,12},{8,0},{12,4},{1,9},{5,13},{9,1},{13,5},{2,10},{6,14},... | collective-permute-start | bytes 49160 | tf_op jit(solution)/shard_map/ppermute | solution.py:85
  9.4 1.3 %collective-permute-start = (bf16[2,64,64]{2,1,0:T(8,128)(2,1)S(1)}, bf16[2,64,64]{2,1,0:T(8,128)(2,1)S(1)}, u32[]{:S(2)}, u32[]{:S(2)}) collective-permute-start(bf16[2,64,64]{2,1,0:T(8,128)(2,1)S(1)} %get-tuple-element.27), channel_id=1, source_target_pairs={{0,12},{4,0},{8,4},{12,8},{1,13},{5,1},{9,5},{13,9},{2,14},{6,2},{... | collective-permute-start | bytes 49160 | tf_op jit(solution)/shard_map/ppermute | solution.py:85
  10.7 0.7 %fusion = f32[16,4,1]{0,1,2:T(4,128)S(1)} fusion(f32[2,4,16]{2,1,0:T(4,128)} %param.10), kind=kLoop, calls=%fused_computation.63 | loop fusion | flops 64 | bytes 512 | tf_op jit(solution)/shard_map/stack | solution.py:260
  11.4 0.7 %convert_element_type.44 = f32[1,8,256]{2,1,0:T(8,128)S(1)} convert(s32[1,8,256]{2,1,0:T(8,128)} %param.13) | non-fusion elementwise | flops 2048 | bytes 16384 | tf_op jit(solution)/shard_map/convert_element_type | solution.py:247
  12.1 0.6 %copy.53 = f32[1,8,256]{2,0,1:T(1,128)} copy(f32[1,8,256]{2,1,0:T(8,128)S(1)} %convert_element_type.44) | data formatting | bytes 16384
  12.7 0.6 %collective-permute-done = bf16[2,64,64]{2,1,0:T(8,128)(2,1)S(1)} collective-permute-done((bf16[2,64,64]{2,1,0:T(8,128)(2,1)S(1)}, bf16[2,64,64]{2,1,0:T(8,128)(2,1)S(1)}, u32[]{:S(2)}, u32[]{:S(2)}) %collective-permute-start) | collective-permute-done | bytes 16416 | tf_op jit(solution)/shard_map/ppermute | solution.py:85
  13.8 1.6 %collective-permute-start.4 = (bf16[64,512]{1,0:T(8,128)(2,1)S(1)}, bf16[64,512]{1,0:T(8,128)(2,1)S(1)}, u32[]{:S(2)}, u32[]{:S(2)}) collective-permute-start(bf16[64,512]{1,0:T(8,128)(2,1)S(1)} %reshape.46.refs_0_), channel_id=1, source_target_pairs={{0,2},{1,3},{2,0},{3,1},{4,6},{5,7},{6,4},{7,5},{8,10},{9,11},{10,... | collective-permute-start | bytes 196616 | tf_op jit(solution)/shard_map/ppermute | solution.py:246
  15.7 3.7 %collective-permute-done.4.refs_2_ = bf16[64,512]{1,0:T(8,128)(2,1)S(1)} collective-permute-done((bf16[64,512]{1,0:T(8,128)(2,1)S(1)}, bf16[64,512]{1,0:T(8,128)(2,1)S(1)}, u32[]{:S(2)}, u32[]{:S(2)}) %collective-permute-start.4) | collective-permute-done | bytes 65568 | tf_op jit(solution)/shard_map/ppermute | solution.py:246
  20.2 10.9 %shard_map.91 = (f32[64,512]{1,0:T(8,128)}, bf16[64,512]{1,0:T(8,128)(2,1)}, bf16[64,512]{1,0:T(8,128)(2,1)}, bf16[64,512]{1,0:T(8,128)(2,1)}) custom-call(bf16[64,512]{1,0:T(8,128)(2,1)} %copy-done.1, bf16[64,512]{1,0:T(8,128)(2,1)} %copy-done.4, bf16[64,512]{1,0:T(8,128)(2,1)} %copy-done.3, bf16[64,512]{1,0:T(8,128)(2,1)} %copy-done.2, s32[1]{0:T(128)} %bitcast.24.refs_4_, ...), custom_call_target="tpu_custom_call" | custom-call | flops 4294967296 | bytes 4718592 | tf_op jit(solution)/shard_map/pallas_call | solution.py:197
  31.2 0.9 %collective-permute-start.7 = (bf16[64,512]{1,0:T(8,128)(2,1)}, bf16[64,512]{1,0:T(8,128)(2,1)S(1)}, u32[]{:S(2)}, u32[]{:S(2)}) collective-permute-start(bf16[64,512]{1,0:T(8,128)(2,1)} %get-tuple-element.11), channel_id=1, source_target_pairs={{0,2},{1,3},{2,0},{3,1},{4,6},{5,7},{6,4},{7,5},{8,10},{9,11},{10,... | collective-permute-start | bytes 196616 | tf_op jit(solution)/shard_map/ppermute | solution.py:254
  32.2 1.4 %collective-permute-start.8 = (bf16[64,512]{1,0:T(8,128)(2,1)}, bf16[64,512]{1,0:T(8,128)(2,1)S(1)}, u32[]{:S(2)}, u32[]{:S(2)}) collective-permute-start(bf16[64,512]{1,0:T(8,128)(2,1)} %get-tuple-element.12), channel_id=1, source_target_pairs={{0,3},{1,0},{2,1},{3,2},{4,7},{5,4},{6,5},{7,6},{8,11},{9,8},{10,9... | collective-permute-start | bytes 196616 | tf_op jit(solution)/shard_map/ppermute | solution.py:254
  33.6 1.6 %collective-permute-done.6 = bf16[64,512]{1,0:T(8,128)(2,1)S(1)} collective-permute-done((bf16[64,512]{1,0:T(8,128)(2,1)}, bf16[64,512]{1,0:T(8,128)(2,1)S(1)}, u32[]{:S(2)}, u32[]{:S(2)}) %collective-permute-start.6) | collective-permute-done | bytes 65568 | tf_op jit(solution)/shard_map/ppermute | solution.py:254
  35.2 1.2 %collective-permute-done.7 = bf16[64,512]{1,0:T(8,128)(2,1)S(1)} collective-permute-done((bf16[64,512]{1,0:T(8,128)(2,1)}, bf16[64,512]{1,0:T(8,128)(2,1)S(1)}, u32[]{:S(2)}, u32[]{:S(2)}) %collective-permute-start.7) | collective-permute-done | bytes 65568 | tf_op jit(solution)/shard_map/ppermute | solution.py:254
  36.4 0.9 %add_convert_fusion = bf16[64,512]{1,0:T(8,128)(2,1)S(1)} fusion(bf16[64,512]{1,0:T(8,128)(2,1)S(1)} %collective-permute-done.8, bf16[64,512]{1,0:T(8,128)(2,1)S(1)} %collective-permute-done.7, f32[64,512]{1,0:T(8,128)} %get-tuple-element.9, bf16[64,512]{1,0:T(8,128)(2,1)S(1)} %collective-permute-done.6), kind=kLoop, calls=%fused_computation.3 | loop fusion | flops 229376 | bytes 393216 | tf_op jit(solution)/shard_map/convert_element_type | solution.py:257
  37.8 3.2 %collective-permute-start.9 = (bf16[64,2,64]{2,0,1:T(8,128)(2,1)S(1)}, bf16[64,2,64]{2,0,1:T(8,128)(2,1)S(1)}, u32[]{:S(2)}, u32[]{:S(2)}) collective-permute-start(bf16[64,2,64]{2,0,1:T(8,128)(2,1)S(1)} %bitcast.103), channel_id=1, source_target_pairs={{0,12},{4,0},{8,4},{12,8},{1,13},{5,1},{9,5},{13,9},{2,14},{6,2},{... | collective-permute-start | bytes 49160 | tf_op jit(solution)/shard_map/ppermute | solution.py:85
  41.0 0.6 %collective-permute-start.11 = (bf16[64,2,64]{2,0,1:T(8,128)(2,1)S(1)}, bf16[64,2,64]{2,0,1:T(8,128)(2,1)S(1)}, u32[]{:S(2)}, u32[]{:S(2)}) collective-permute-start(bf16[64,2,64]{2,0,1:T(8,128)(2,1)S(1)} %bitcast.101), channel_id=1, source_target_pairs={{0,4},{4,8},{8,12},{12,0},{1,5},{5,9},{9,13},{13,1},{2,6},{6,10},{... | collective-permute-start | bytes 49160 | tf_op jit(solution)/shard_map/ppermute | solution.py:85
  41.7 1.0 %collective-permute-done.9 = bf16[64,2,64]{2,0,1:T(8,128)(2,1)S(1)} collective-permute-done((bf16[64,2,64]{2,0,1:T(8,128)(2,1)S(1)}, bf16[64,2,64]{2,0,1:T(8,128)(2,1)S(1)}, u32[]{:S(2)}, u32[]{:S(2)}) %collective-permute-start.9) | collective-permute-done | bytes 16416 | tf_op jit(solution)/shard_map/ppermute | solution.py:85
  42.7 3.1 %collective-permute-done.10 = bf16[64,2,64]{2,0,1:T(8,128)(2,1)S(1)} collective-permute-done((bf16[64,2,64]{2,0,1:T(8,128)(2,1)S(1)}, bf16[64,2,64]{2,0,1:T(8,128)(2,1)S(1)}, u32[]{:S(2)}, u32[]{:S(2)}) %collective-permute-start.10) | collective-permute-done | bytes 16416 | tf_op jit(solution)/shard_map/ppermute | solution.py:85
  45.9 0.9 %collective-permute-done.11 = bf16[64,2,64]{2,0,1:T(8,128)(2,1)S(1)} collective-permute-done((bf16[64,2,64]{2,0,1:T(8,128)(2,1)S(1)}, bf16[64,2,64]{2,0,1:T(8,128)(2,1)S(1)}, u32[]{:S(2)}, u32[]{:S(2)}) %collective-permute-start.11) | collective-permute-done | bytes 16416 | tf_op jit(solution)/shard_map/ppermute | solution.py:85
  46.9 1.7 %multiply_subtract_fusion = f32[2,16,64,64]{3,2,1,0:T(8,128)} fusion(f32[2,16,64,64]{3,2,1,0:T(8,128)S(1)} %copy-done, f32[64,64]{1,0:T(8,128)S(1)} %get-tuple-element.14, f32[2,16]{1,0:T(2,128)S(1)} %bitcast.111, f32[64,64]{1,0:T(8,128)S(1)} %get-tuple-element.15, f32[2,16]{1,0:T(2,128)S(1)} %bitcast.112, f32[64,64]{1,0:T(8,128)S(1)} %get-tuple-element.16, ...), kind=kLoop, calls=%fused_computation.1 | loop fusion | flops 2228224 | bytes 1180672 | tf_op jit(solution)/shard_map/sub | solution.py:267
  (49 shorter events, 2.2 us)
Async XLA Ops:
  3.7 9.6 %collective-permute-start.2 = (bf16[2,64,64]{2,1,0:T(8,128)(2,1)S(1)}, bf16[2,64,64]{2,1,0:T(8,128)(2,1)S(1)}, u32[]{:S(2)}, u32[]{:S(2)}) collective-permute-start(bf16[2,64,64]{2,1,0:T(8,128)(2,1)S(1)} %get-tuple-element.25), channel_id=1, source_target_pairs={{0,4},{4,8},{8,12},{12,0},{1,5},{5,9},{9,13},{13,1},{2,6},{6,10},{... | collective-permute-start | bytes 49160 | tf_op jit(solution)/shard_map/ppermute | solution.py:85
  6.8 6.5 %collective-permute-start.1 = (bf16[2,64,64]{2,1,0:T(8,128)(2,1)S(1)}, bf16[2,64,64]{2,1,0:T(8,128)(2,1)S(1)}, u32[]{:S(2)}, u32[]{:S(2)}) collective-permute-start(bf16[2,64,64]{2,1,0:T(8,128)(2,1)S(1)} %get-tuple-element.26), channel_id=1, source_target_pairs={{0,8},{4,12},{8,0},{12,4},{1,9},{5,13},{9,1},{13,5},{2,10},{6,14},... | collective-permute-start | bytes 49160 | tf_op jit(solution)/shard_map/ppermute | solution.py:85
  9.4 3.9 %collective-permute-start = (bf16[2,64,64]{2,1,0:T(8,128)(2,1)S(1)}, bf16[2,64,64]{2,1,0:T(8,128)(2,1)S(1)}, u32[]{:S(2)}, u32[]{:S(2)}) collective-permute-start(bf16[2,64,64]{2,1,0:T(8,128)(2,1)S(1)} %get-tuple-element.27), channel_id=1, source_target_pairs={{0,12},{4,0},{8,4},{12,8},{1,13},{5,1},{9,5},{13,9},{2,14},{6,2},{... | collective-permute-start | bytes 49160 | tf_op jit(solution)/shard_map/ppermute | solution.py:85
  13.7 5.9 %copy-start.1 = (bf16[64,512]{1,0:T(8,128)(2,1)}, bf16[64,512]{1,0:T(8,128)(2,1)S(1)}, u32[]{:S(2)}) copy-start(bf16[64,512]{1,0:T(8,128)(2,1)S(1)} %reshape.46.refs_0_) | copy-start | bytes 196612
  13.7 2.0 %collective-permute-start.5 = (bf16[64,512]{1,0:T(8,128)(2,1)S(1)}, bf16[64,512]{1,0:T(8,128)(2,1)S(1)}, u32[]{:S(2)}, u32[]{:S(2)}) collective-permute-start(bf16[64,512]{1,0:T(8,128)(2,1)S(1)} %reshape.46.refs_0_), channel_id=1, source_target_pairs={{0,3},{1,0},{2,1},{3,2},{4,7},{5,4},{6,5},{7,6},{8,11},{9,8},{10,9... | collective-permute-start | bytes 196616 | tf_op jit(solution)/shard_map/ppermute | solution.py:246
  13.8 5.6 %collective-permute-start.4 = (bf16[64,512]{1,0:T(8,128)(2,1)S(1)}, bf16[64,512]{1,0:T(8,128)(2,1)S(1)}, u32[]{:S(2)}, u32[]{:S(2)}) collective-permute-start(bf16[64,512]{1,0:T(8,128)(2,1)S(1)} %reshape.46.refs_0_), channel_id=1, source_target_pairs={{0,2},{1,3},{2,0},{3,1},{4,6},{5,7},{6,4},{7,5},{8,10},{9,11},{10,... | collective-permute-start | bytes 196616 | tf_op jit(solution)/shard_map/ppermute | solution.py:246
  15.3 4.3 %collective-permute-start.3 = (bf16[64,512]{1,0:T(8,128)(2,1)S(1)}, bf16[64,512]{1,0:T(8,128)(2,1)S(1)}, u32[]{:S(2)}, u32[]{:S(2)}) collective-permute-start(bf16[64,512]{1,0:T(8,128)(2,1)S(1)} %reshape.46.refs_0_), channel_id=1, source_target_pairs={{0,1},{1,2},{2,3},{3,0},{4,5},{5,6},{6,7},{7,4},{8,9},{9,10},{10,1... | collective-permute-start | bytes 196616 | tf_op jit(solution)/shard_map/ppermute | solution.py:246
  15.7 3.9 %copy-start.2 = (bf16[64,512]{1,0:T(8,128)(2,1)}, bf16[64,512]{1,0:T(8,128)(2,1)S(1)}, u32[]{:S(2)}) copy-start(bf16[64,512]{1,0:T(8,128)(2,1)S(1)} %collective-permute-done.5.refs_3_) | copy-start | bytes 196612
  19.4 0.6 %copy-start.3 = (bf16[64,512]{1,0:T(8,128)(2,1)}, bf16[64,512]{1,0:T(8,128)(2,1)S(1)}, u32[]{:S(2)}) copy-start(bf16[64,512]{1,0:T(8,128)(2,1)S(1)} %collective-permute-done.4.refs_2_) | copy-start | bytes 196612
  19.6 0.6 %copy-start.4 = (bf16[64,512]{1,0:T(8,128)(2,1)}, bf16[64,512]{1,0:T(8,128)(2,1)S(1)}, u32[]{:S(2)}) copy-start(bf16[64,512]{1,0:T(8,128)(2,1)S(1)} %collective-permute-done.3.refs_1_) | copy-start | bytes 196612
  31.2 15.7 %copy-start = (f32[2,16,64,64]{3,2,1,0:T(8,128)S(1)}, f32[2,16,64,64]{3,2,1,0:T(8,128)}, u32[]{:S(2)}) copy-start(f32[2,16,64,64]{3,2,1,0:T(8,128)} %param.9) | copy-start | bytes 1572868
  31.2 4.0 %collective-permute-start.6 = (bf16[64,512]{1,0:T(8,128)(2,1)}, bf16[64,512]{1,0:T(8,128)(2,1)S(1)}, u32[]{:S(2)}, u32[]{:S(2)}) collective-permute-start(bf16[64,512]{1,0:T(8,128)(2,1)} %get-tuple-element.10), channel_id=1, source_target_pairs={{0,1},{1,2},{2,3},{3,0},{4,5},{5,6},{6,7},{7,4},{8,9},{9,10},{10,1... | collective-permute-start | bytes 196616 | tf_op jit(solution)/shard_map/ppermute | solution.py:254
  31.2 5.2 %collective-permute-start.7 = (bf16[64,512]{1,0:T(8,128)(2,1)}, bf16[64,512]{1,0:T(8,128)(2,1)S(1)}, u32[]{:S(2)}, u32[]{:S(2)}) collective-permute-start(bf16[64,512]{1,0:T(8,128)(2,1)} %get-tuple-element.11), channel_id=1, source_target_pairs={{0,2},{1,3},{2,0},{3,1},{4,6},{5,7},{6,4},{7,5},{8,10},{9,11},{10,... | collective-permute-start | bytes 196616 | tf_op jit(solution)/shard_map/ppermute | solution.py:254
  32.2 4.3 %collective-permute-start.8 = (bf16[64,512]{1,0:T(8,128)(2,1)}, bf16[64,512]{1,0:T(8,128)(2,1)S(1)}, u32[]{:S(2)}, u32[]{:S(2)}) collective-permute-start(bf16[64,512]{1,0:T(8,128)(2,1)} %get-tuple-element.12), channel_id=1, source_target_pairs={{0,3},{1,0},{2,1},{3,2},{4,7},{5,4},{6,5},{7,6},{8,11},{9,8},{10,9... | collective-permute-start | bytes 196616 | tf_op jit(solution)/shard_map/ppermute | solution.py:254
  37.8 4.9 %collective-permute-start.9 = (bf16[64,2,64]{2,0,1:T(8,128)(2,1)S(1)}, bf16[64,2,64]{2,0,1:T(8,128)(2,1)S(1)}, u32[]{:S(2)}, u32[]{:S(2)}) collective-permute-start(bf16[64,2,64]{2,0,1:T(8,128)(2,1)S(1)} %bitcast.103), channel_id=1, source_target_pairs={{0,12},{4,0},{8,4},{12,8},{1,13},{5,1},{9,5},{13,9},{2,14},{6,2},{... | collective-permute-start | bytes 49160 | tf_op jit(solution)/shard_map/ppermute | solution.py:85
  41.0 4.8 %collective-permute-start.10 = (bf16[64,2,64]{2,0,1:T(8,128)(2,1)S(1)}, bf16[64,2,64]{2,0,1:T(8,128)(2,1)S(1)}, u32[]{:S(2)}, u32[]{:S(2)}) collective-permute-start(bf16[64,2,64]{2,0,1:T(8,128)(2,1)S(1)} %bitcast.102), channel_id=1, source_target_pairs={{0,8},{4,12},{8,0},{12,4},{1,9},{5,13},{9,1},{13,5},{2,10},{6,14},... | collective-permute-start | bytes 49160 | tf_op jit(solution)/shard_map/ppermute | solution.py:85
  41.0 5.7 %collective-permute-start.11 = (bf16[64,2,64]{2,0,1:T(8,128)(2,1)S(1)}, bf16[64,2,64]{2,0,1:T(8,128)(2,1)S(1)}, u32[]{:S(2)}, u32[]{:S(2)}) collective-permute-start(bf16[64,2,64]{2,0,1:T(8,128)(2,1)S(1)} %bitcast.101), channel_id=1, source_target_pairs={{0,4},{4,8},{8,12},{12,0},{1,5},{5,9},{9,13},{13,1},{2,6},{6,10},{... | collective-permute-start | bytes 49160 | tf_op jit(solution)/shard_map/ppermute | solution.py:85

commit v16 on v14

--- a/solution.py
+++ b/solution.py
@@ -106,38 +106,49 @@
     return jnp.concatenate([high, -low], axis=1)
 
 
-def coil_term(coil_index, image_ref, sens_ref, measured_ref, sampled_ref, forward_ref, adjoint_ref,
-              table_re_ref, table_im_ref):
-    half_width = image_ref.shape[1] // 2
-    sens = sens_ref[coil_index].astype(jnp.float32)
-    sens_re = sens[:, :half_width]
-    sens_im = sens[:, half_width:]
-    image = image_ref[...].astype(jnp.float32)
-    image_re = image[:, :half_width]
-    image_im = image[:, half_width:]
+def coil_terms(image_ref, sens_ref, measured_ref, sampled_ref, forward_ref, adjoint_ref, table_re_ref, table_im_ref):
+    coils, height, width = sens_ref.shape
+    half_width = width // 2
+    sens = sens_ref[...].astype(jnp.float32)
+    sens_re = sens[:, :, :half_width]
+    sens_im = sens[:, :, half_width:]
+    image = image_ref[...].astype(jnp.float32)[None]
+    image_re = image[:, :, :half_width]
+    image_im = image[:, :, half_width:]
     coil = jnp.concatenate(
-        [sens_re * image_re - sens_im * image_im, sens_re * image_im + sens_im * image_re], axis=1
-    ).astype(jnp.bfloat16)
-    half_k = jnp.dot(coil, forward_ref[...], preferred_element_type=jnp.float32).astype(jnp.bfloat16)
+        [sens_re * image_re - sens_im * image_im, sens_re * image_im + sens_im * image_re], axis=2
+    ).astype(jnp.bfloat16)
+    half_k = jnp.dot(
+        coil.reshape(coils * height, width), forward_ref[...], preferred_element_type=jnp.float32
+    ).astype(jnp.bfloat16)
     table_re = table_re_ref[...]
     table_im = table_im_ref[...]
-    kspace = jnp.dot(table_re, half_k, preferred_element_type=jnp.float32) + jnp.dot(
-        table_im, swap_halves(half_k, half_width, True), preferred_element_type=jnp.float32
-    )
-    residual = (kspace - measured_ref[coil_index].astype(jnp.float32)).astype(jnp.bfloat16)
-    sampled = sampled_ref[coil_index].astype(jnp.bfloat16)
-    back_half = (
-        jnp.dot(table_re * sampled, residual, preferred_element_type=jnp.float32)
-        + jnp.dot(table_im * sampled, swap_halves(residual, half_width, False), preferred_element_type=jnp.float32)
-    ).astype(jnp.bfloat16)
-    coil_back = jnp.dot(back_half, adjoint_ref[...], preferred_element_type=jnp.float32)
-    back_re = coil_back[:, :half_width]
-    back_im = coil_back[:, half_width:]
+    backs = []
+    for coil_index in range(coils):
+        one = half_k[coil_index * height:(coil_index + 1) * height]
+        kspace = jnp.dot(table_re, one, preferred_element_type=jnp.float32) + jnp.dot(
+            table_im, swap_halves(one, half_width, True), preferred_element_type=jnp.float32
+        )
+        residual = (kspace - measured_ref[coil_index].astype(jnp.float32)).astype(jnp.bfloat16)
+        sampled = sampled_ref[coil_index].astype(jnp.bfloat16)
+        backs.append(
+            (
+                jnp.dot(table_re * sampled, residual, preferred_element_type=jnp.float32)
+                + jnp.dot(
+                    table_im * sampled, swap_halves(residual, half_width, False), preferred_element_type=jnp.float32
+                )
+            ).astype(jnp.bfloat16)
+        )
+    back_half = jnp.concatenate(backs, axis=0)
+    coil_back = jnp.dot(back_half, adjoint_ref[...], preferred_element_type=jnp.float32).reshape(
+        coils, height, width
+    )
+    back_re = coil_back[:, :, :half_width]
+    back_im = coil_back[:, :, half_width:]
     term = jnp.concatenate(
-        [sens_re * back_re + sens_im * back_im, sens_re * back_im - sens_im * back_re], axis=1
-    )
-
-    return term
+        [sens_re * back_re + sens_im * back_im, sens_re * back_im - sens_im * back_re], axis=2
+    )
+    return jnp.sum(term, axis=0)
 
 
 def coil_chain_kernel(*refs):
@@ -163,11 +174,8 @@
                 value = jnp.where(source == other, pieces[other][...], value)
             image_ref[block * rows:(block + 1) * rows, :] = value
 
-    term = None
-    for coil_index in range(sens_ref.shape[0]):
-        one = coil_term(coil_index, image_ref, sens_ref, measured_ref, sampled_ref, forward_ref, adjoint_ref,
-                        table_re_ref, table_im_ref)
-        term = one if term is None else term + one
+    term = coil_terms(image_ref, sens_ref, measured_ref, sampled_ref, forward_ref, adjoint_ref,
+                      table_re_ref, table_im_ref)
 
     @pl.when(step == 0)
     def _():

time: 48.8 us -> 47.4 us (0.971)
  Pallas kernels: 10.8 us -> 9.5 us
    pallas_call x1, Pallas kernels: 10.8 us -> 9.5 us  [coil_chain(): pl.pallas_call(coil_chain_kernel, out_shape=(jax.ShapeDtypeStruct((rows,...]
where the time goes in v16:
time: 47.4 us; the launch traced here: 47.1 us
  starting transfers between devices  15 us (32%)
  waiting for transfers between devices  12.6 us (27%)
  Pallas kernels  9.5 us (20%)
  other arithmetic  7.02 us (15%)
  local copies, waits for them, and re-layouts  2.84 us (6%)
    ppermute x6, starting transfers between devices, exchange_blocks(): pieces.append(lax.ppermute(outgoing, axis, shifted(count, step)))  10.9 us
    pallas_call x1, Pallas kernels, coil_chain(): pl.pallas_call(coil_chain_kernel, out_shape=(jax.ShapeDtypeStruct((rows,...  9.5 us
    ppermute x6, waiting for transfers between devices, exchange_blocks(): pieces.append(lax.ppermute(outgoing, axis, shifted(count, step)))  5.63 us
    ppermute x3, waiting for transfers between devices, on_device(): lax.ppermute(own_rows, 'coil', shifted(groups, step))  4.1 us
    ppermute x3, waiting for transfers between devices, on_device(): lax.ppermute(outgoing[step - 1], 'coil', shifted(groups, step))  2.86 us
    ppermute x3, starting transfers between devices, on_device(): lax.ppermute(outgoing[step - 1], 'coil', shifted(groups, step))  2.38 us
    reduce_sum x1, other arithmetic, on_device(): jnp.sum(mixing[:, :, :, :, None, None] * factors[None, None], axis=(2, 3))  2.29 us
    ppermute x3, starting transfers between devices, on_device(): lax.ppermute(own_rows, 'coil', shifted(groups, step))  1.78 us
  transfers between devices with their start and end apart: 12, of which 9 were waited for; matrix products, arithmetic and copies ran while one was open for 4% of the time, Pallas kernels for 0%

profile of v16, /device:TPU:0, one launch (start us, length us, event | category | flops | bytes accessed | tf_op | source)
XLA Modules:
  0.0 47.1 jit_solution(14190175126198658832)
XLA Ops:
  0.0 0.7 %fusion.8 = f32[4,1,16]{2,0,1:T(4,128)S(1)} fusion(f32[2,4,16]{2,1,0:T(4,128)} %param.10), kind=kLoop, calls=%fused_computation.76 | loop fusion | flops 64 | bytes 512 | tf_op jit(solution)/shard_map/neg | solution.py:243
  0.7 0.7 %slice_bitcast_fusion.10 = (f32[16,4,1]{0,1,2:T(4,128)S(1)}, f32[4,1,16]{2,0,1:T(4,128)S(1)}, f32[4,1,16]{2,0,1:T(4,128)S(1)}, f32[16,4,1]{0,1,2:T(4,128)S(1)}) fusion(f32[2,4,16]{2,1,0:T(4,128)} %param.10), kind=kLoop, calls=%fused_computation.66 | loop fusion | bytes 1536 | tf_op jit(solution)/shard_map/stack | solution.py:268
  1.4 2.3 %multiply_reduce_fusion = bf16[4,2,64,64]{3,2,1,0:T(8,128)(2,1)S(1)} fusion(f32[2,16,64,64]{3,2,1,0:T(8,128)} %param.9, f32[4,1,2,16]{3,2,0,1:T(2,128)S(1)} %get-tuple-element.45, f32[4,1,2,16]{3,2,0,1:T(2,128)S(1)} %get-tuple-element.46), kind=kLoop, calls=%fused_computation | loop fusion | flops 2064640 | bytes 590848 | tf_op jit(solution)/shard_map/reduce_sum | solution.py:245
  3.7 3.1 %collective-permute-start.2 = (bf16[2,64,64]{2,1,0:T(8,128)(2,1)S(1)}, bf16[2,64,64]{2,1,0:T(8,128)(2,1)S(1)}, u32[]{:S(2)}, u32[]{:S(2)}) collective-permute-start(bf16[2,64,64]{2,1,0:T(8,128)(2,1)S(1)} %get-tuple-element.25), channel_id=1, source_target_pairs={{0,4},{4,8},{8,12},{12,0},{1,5},{5,9},{9,13},{13,1},{2,6},{6,10},{... | collective-permute-start | bytes 49160 | tf_op jit(solution)/shard_map/ppermute | solution.py:85
  6.8 2.6 %collective-permute-start.1 = (bf16[2,64,64]{2,1,0:T(8,128)(2,1)S(1)}, bf16[2,64,64]{2,1,0:T(8,128)(2,1)S(1)}, u32[]{:S(2)}, u32[]{:S(2)}) collective-permute-start(bf16[2,64,64]{2,1,0:T(8,128)(2,1)S(1)} %get-tuple-element.26), channel_id=1, source_target_pairs={{0,8},{4,12},{8,0},{12,4},{1,9},{5,13},{9,1},{13,5},{2,10},{6,14},... | collective-permute-start | bytes 49160 | tf_op jit(solution)/shard_map/ppermute | solution.py:85
  9.4 1.3 %collective-permute-start = (bf16[2,64,64]{2,1,0:T(8,128)(2,1)S(1)}, bf16[2,64,64]{2,1,0:T(8,128)(2,1)S(1)}, u32[]{:S(2)}, u32[]{:S(2)}) collective-permute-start(bf16[2,64,64]{2,1,0:T(8,128)(2,1)S(1)} %get-tuple-element.27), channel_id=1, source_target_pairs={{0,12},{4,0},{8,4},{12,8},{1,13},{5,1},{9,5},{13,9},{2,14},{6,2},{... | collective-permute-start | bytes 49160 | tf_op jit(solution)/shard_map/ppermute | solution.py:85
  10.7 0.7 %fusion = f32[16,4,1]{0,1,2:T(4,128)S(1)} fusion(f32[2,4,16]{2,1,0:T(4,128)} %param.10), kind=kLoop, calls=%fused_computation.63 | loop fusion | flops 64 | bytes 512 | tf_op jit(solution)/shard_map/stack | solution.py:268
  11.4 0.7 %convert_element_type.44 = f32[1,8,256]{2,1,0:T(8,128)S(1)} convert(s32[1,8,256]{2,1,0:T(8,128)} %param.13) | non-fusion elementwise | flops 2048 | bytes 16384 | tf_op jit(solution)/shard_map/convert_element_type | solution.py:255
  12.1 0.6 %copy.53 = f32[1,8,256]{2,0,1:T(1,128)} copy(f32[1,8,256]{2,1,0:T(8,128)S(1)} %convert_element_type.44) | data formatting | bytes 16384
  12.7 0.6 %collective-permute-done = bf16[2,64,64]{2,1,0:T(8,128)(2,1)S(1)} collective-permute-done((bf16[2,64,64]{2,1,0:T(8,128)(2,1)S(1)}, bf16[2,64,64]{2,1,0:T(8,128)(2,1)S(1)}, u32[]{:S(2)}, u32[]{:S(2)}) %collective-permute-start) | collective-permute-done | bytes 16416 | tf_op jit(solution)/shard_map/ppermute | solution.py:85
  13.8 1.6 %collective-permute-start.4 = (bf16[64,512]{1,0:T(8,128)(2,1)S(1)}, bf16[64,512]{1,0:T(8,128)(2,1)S(1)}, u32[]{:S(2)}, u32[]{:S(2)}) collective-permute-start(bf16[64,512]{1,0:T(8,128)(2,1)S(1)} %reshape.46.refs_0_), channel_id=1, source_target_pairs={{0,2},{1,3},{2,0},{3,1},{4,6},{5,7},{6,4},{7,5},{8,10},{9,11},{10,... | collective-permute-start | bytes 196616 | tf_op jit(solution)/shard_map/ppermute | solution.py:254
  15.7 3.7 %collective-permute-done.4.refs_2_ = bf16[64,512]{1,0:T(8,128)(2,1)S(1)} collective-permute-done((bf16[64,512]{1,0:T(8,128)(2,1)S(1)}, bf16[64,512]{1,0:T(8,128)(2,1)S(1)}, u32[]{:S(2)}, u32[]{:S(2)}) %collective-permute-start.4) | collective-permute-done | bytes 65568 | tf_op jit(solution)/shard_map/ppermute | solution.py:254
  20.2 9.5 %shard_map.91 = (f32[64,512]{1,0:T(8,128)}, bf16[64,512]{1,0:T(8,128)(2,1)}, bf16[64,512]{1,0:T(8,128)(2,1)}, bf16[64,512]{1,0:T(8,128)(2,1)}) custom-call(bf16[64,512]{1,0:T(8,128)(2,1)} %copy-done.1, bf16[64,512]{1,0:T(8,128)(2,1)} %copy-done.4, bf16[64,512]{1,0:T(8,128)(2,1)} %copy-done.3, bf16[64,512]{1,0:T(8,128)(2,1)} %copy-done.2, s32[1]{0:T(128)} %bitcast.24.refs_4_, ...), custom_call_target="tpu_custom_call" | custom-call | flops 4294967296 | bytes 4718592 | tf_op jit(solution)/shard_map/pallas_call | solution.py:205
  29.8 0.9 %collective-permute-start.7 = (bf16[64,512]{1,0:T(8,128)(2,1)}, bf16[64,512]{1,0:T(8,128)(2,1)S(1)}, u32[]{:S(2)}, u32[]{:S(2)}) collective-permute-start(bf16[64,512]{1,0:T(8,128)(2,1)} %get-tuple-element.11), channel_id=1, source_target_pairs={{0,2},{1,3},{2,0},{3,1},{4,6},{5,7},{6,4},{7,5},{8,10},{9,11},{10,... | collective-permute-start | bytes 196616 | tf_op jit(solution)/shard_map/ppermute | solution.py:262
  30.7 1.4 %collective-permute-start.8 = (bf16[64,512]{1,0:T(8,128)(2,1)}, bf16[64,512]{1,0:T(8,128)(2,1)S(1)}, u32[]{:S(2)}, u32[]{:S(2)}) collective-permute-start(bf16[64,512]{1,0:T(8,128)(2,1)} %get-tuple-element.12), channel_id=1, source_target_pairs={{0,3},{1,0},{2,1},{3,2},{4,7},{5,4},{6,5},{7,6},{8,11},{9,8},{10,9... | collective-permute-start | bytes 196616 | tf_op jit(solution)/shard_map/ppermute | solution.py:262
  32.1 1.6 %collective-permute-done.6 = bf16[64,512]{1,0:T(8,128)(2,1)S(1)} collective-permute-done((bf16[64,512]{1,0:T(8,128)(2,1)}, bf16[64,512]{1,0:T(8,128)(2,1)S(1)}, u32[]{:S(2)}, u32[]{:S(2)}) %collective-permute-start.6) | collective-permute-done | bytes 65568 | tf_op jit(solution)/shard_map/ppermute | solution.py:262
  33.8 1.2 %collective-permute-done.7 = bf16[64,512]{1,0:T(8,128)(2,1)S(1)} collective-permute-done((bf16[64,512]{1,0:T(8,128)(2,1)}, bf16[64,512]{1,0:T(8,128)(2,1)S(1)}, u32[]{:S(2)}, u32[]{:S(2)}) %collective-permute-start.7) | collective-permute-done | bytes 65568 | tf_op jit(solution)/shard_map/ppermute | solution.py:262
  35.0 0.9 %add_convert_fusion = bf16[64,512]{1,0:T(8,128)(2,1)S(1)} fusion(bf16[64,512]{1,0:T(8,128)(2,1)S(1)} %collective-permute-done.8, bf16[64,512]{1,0:T(8,128)(2,1)S(1)} %collective-permute-done.7, f32[64,512]{1,0:T(8,128)} %get-tuple-element.9, bf16[64,512]{1,0:T(8,128)(2,1)S(1)} %collective-permute-done.6), kind=kLoop, calls=%fused_computation.3 | loop fusion | flops 229376 | bytes 393216 | tf_op jit(solution)/shard_map/convert_element_type | solution.py:265
  36.4 3.2 %collective-permute-start.9 = (bf16[64,2,64]{2,0,1:T(8,128)(2,1)S(1)}, bf16[64,2,64]{2,0,1:T(8,128)(2,1)S(1)}, u32[]{:S(2)}, u32[]{:S(2)}) collective-permute-start(bf16[64,2,64]{2,0,1:T(8,128)(2,1)S(1)} %bitcast.103), channel_id=1, source_target_pairs={{0,12},{4,0},{8,4},{12,8},{1,13},{5,1},{9,5},{13,9},{2,14},{6,2},{... | collective-permute-start | bytes 49160 | tf_op jit(solution)/shard_map/ppermute | solution.py:85
  39.6 0.6 %collective-permute-start.11 = (bf16[64,2,64]{2,0,1:T(8,128)(2,1)S(1)}, bf16[64,2,64]{2,0,1:T(8,128)(2,1)S(1)}, u32[]{:S(2)}, u32[]{:S(2)}) collective-permute-start(bf16[64,2,64]{2,0,1:T(8,128)(2,1)S(1)} %bitcast.101), channel_id=1, source_target_pairs={{0,4},{4,8},{8,12},{12,0},{1,5},{5,9},{9,13},{13,1},{2,6},{6,10},{... | collective-permute-start | bytes 49160 | tf_op jit(solution)/shard_map/ppermute | solution.py:85
  40.3 1.0 %collective-permute-done.9 = bf16[64,2,64]{2,0,1:T(8,128)(2,1)S(1)} collective-permute-done((bf16[64,2,64]{2,0,1:T(8,128)(2,1)S(1)}, bf16[64,2,64]{2,0,1:T(8,128)(2,1)S(1)}, u32[]{:S(2)}, u32[]{:S(2)}) %collective-permute-start.9) | collective-permute-done | bytes 16416 | tf_op jit(solution)/shard_map/ppermute | solution.py:85
  41.3 3.1 %collective-permute-done.10 = bf16[64,2,64]{2,0,1:T(8,128)(2,1)S(1)} collective-permute-done((bf16[64,2,64]{2,0,1:T(8,128)(2,1)S(1)}, bf16[64,2,64]{2,0,1:T(8,128)(2,1)S(1)}, u32[]{:S(2)}, u32[]{:S(2)}) %collective-permute-start.10) | collective-permute-done | bytes 16416 | tf_op jit(solution)/shard_map/ppermute | solution.py:85
  44.4 0.9 %collective-permute-done.11 = bf16[64,2,64]{2,0,1:T(8,128)(2,1)S(1)} collective-permute-done((bf16[64,2,64]{2,0,1:T(8,128)(2,1)S(1)}, bf16[64,2,64]{2,0,1:T(8,128)(2,1)S(1)}, u32[]{:S(2)}, u32[]{:S(2)}) %collective-permute-start.11) | collective-permute-done | bytes 16416 | tf_op jit(solution)/shard_map/ppermute | solution.py:85
  45.5 1.7 %multiply_subtract_fusion = f32[2,16,64,64]{3,2,1,0:T(8,128)} fusion(f32[2,16,64,64]{3,2,1,0:T(8,128)S(1)} %copy-done, f32[64,64]{1,0:T(8,128)S(1)} %get-tuple-element.14, f32[2,16]{1,0:T(2,128)S(1)} %bitcast.111, f32[64,64]{1,0:T(8,128)S(1)} %get-tuple-element.15, f32[2,16]{1,0:T(2,128)S(1)} %bitcast.112, f32[64,64]{1,0:T(8,128)S(1)} %get-tuple-element.16, ...), kind=kLoop, calls=%fused_computation.1 | loop fusion | flops 2228224 | bytes 1180672 | tf_op jit(solution)/shard_map/sub | solution.py:275
  (49 shorter events, 2.2 us)
Async XLA Ops:
  3.7 9.6 %collective-permute-start.2 = (bf16[2,64,64]{2,1,0:T(8,128)(2,1)S(1)}, bf16[2,64,64]{2,1,0:T(8,128)(2,1)S(1)}, u32[]{:S(2)}, u32[]{:S(2)}) collective-permute-start(bf16[2,64,64]{2,1,0:T(8,128)(2,1)S(1)} %get-tuple-element.25), channel_id=1, source_target_pairs={{0,4},{4,8},{8,12},{12,0},{1,5},{5,9},{9,13},{13,1},{2,6},{6,10},{... | collective-permute-start | bytes 49160 | tf_op jit(solution)/shard_map/ppermute | solution.py:85
  6.8 6.5 %collective-permute-start.1 = (bf16[2,64,64]{2,1,0:T(8,128)(2,1)S(1)}, bf16[2,64,64]{2,1,0:T(8,128)(2,1)S(1)}, u32[]{:S(2)}, u32[]{:S(2)}) collective-permute-start(bf16[2,64,64]{2,1,0:T(8,128)(2,1)S(1)} %get-tuple-element.26), channel_id=1, source_target_pairs={{0,8},{4,12},{8,0},{12,4},{1,9},{5,13},{9,1},{13,5},{2,10},{6,14},... | collective-permute-start | bytes 49160 | tf_op jit(solution)/shard_map/ppermute | solution.py:85
  9.4 3.9 %collective-permute-start = (bf16[2,64,64]{2,1,0:T(8,128)(2,1)S(1)}, bf16[2,64,64]{2,1,0:T(8,128)(2,1)S(1)}, u32[]{:S(2)}, u32[]{:S(2)}) collective-permute-start(bf16[2,64,64]{2,1,0:T(8,128)(2,1)S(1)} %get-tuple-element.27), channel_id=1, source_target_pairs={{0,12},{4,0},{8,4},{12,8},{1,13},{5,1},{9,5},{13,9},{2,14},{6,2},{... | collective-permute-start | bytes 49160 | tf_op jit(solution)/shard_map/ppermute | solution.py:85
  13.7 5.9 %copy-start.1 = (bf16[64,512]{1,0:T(8,128)(2,1)}, bf16[64,512]{1,0:T(8,128)(2,1)S(1)}, u32[]{:S(2)}) copy-start(bf16[64,512]{1,0:T(8,128)(2,1)S(1)} %reshape.46.refs_0_) | copy-start | bytes 196612
  13.7 2.0 %collective-permute-start.5 = (bf16[64,512]{1,0:T(8,128)(2,1)S(1)}, bf16[64,512]{1,0:T(8,128)(2,1)S(1)}, u32[]{:S(2)}, u32[]{:S(2)}) collective-permute-start(bf16[64,512]{1,0:T(8,128)(2,1)S(1)} %reshape.46.refs_0_), channel_id=1, source_target_pairs={{0,3},{1,0},{2,1},{3,2},{4,7},{5,4},{6,5},{7,6},{8,11},{9,8},{10,9... | collective-permute-start | bytes 196616 | tf_op jit(solution)/shard_map/ppermute | solution.py:254
  13.8 5.6 %collective-permute-start.4 = (bf16[64,512]{1,0:T(8,128)(2,1)S(1)}, bf16[64,512]{1,0:T(8,128)(2,1)S(1)}, u32[]{:S(2)}, u32[]{:S(2)}) collective-permute-start(bf16[64,512]{1,0:T(8,128)(2,1)S(1)} %reshape.46.refs_0_), channel_id=1, source_target_pairs={{0,2},{1,3},{2,0},{3,1},{4,6},{5,7},{6,4},{7,5},{8,10},{9,11},{10,... | collective-permute-start | bytes 196616 | tf_op jit(solution)/shard_map/ppermute | solution.py:254
  15.3 4.3 %collective-permute-start.3 = (bf16[64,512]{1,0:T(8,128)(2,1)S(1)}, bf16[64,512]{1,0:T(8,128)(2,1)S(1)}, u32[]{:S(2)}, u32[]{:S(2)}) collective-permute-start(bf16[64,512]{1,0:T(8,128)(2,1)S(1)} %reshape.46.refs_0_), channel_id=1, source_target_pairs={{0,1},{1,2},{2,3},{3,0},{4,5},{5,6},{6,7},{7,4},{8,9},{9,10},{10,1... | collective-permute-start | bytes 196616 | tf_op jit(solution)/shard_map/ppermute | solution.py:254
  15.7 3.9 %copy-start.2 = (bf16[64,512]{1,0:T(8,128)(2,1)}, bf16[64,512]{1,0:T(8,128)(2,1)S(1)}, u32[]{:S(2)}) copy-start(bf16[64,512]{1,0:T(8,128)(2,1)S(1)} %collective-permute-done.5.refs_3_) | copy-start | bytes 196612
  19.4 0.6 %copy-start.3 = (bf16[64,512]{1,0:T(8,128)(2,1)}, bf16[64,512]{1,0:T(8,128)(2,1)S(1)}, u32[]{:S(2)}) copy-start(bf16[64,512]{1,0:T(8,128)(2,1)S(1)} %collective-permute-done.4.refs_2_) | copy-start | bytes 196612
  19.6 0.6 %copy-start.4 = (bf16[64,512]{1,0:T(8,128)(2,1)}, bf16[64,512]{1,0:T(8,128)(2,1)S(1)}, u32[]{:S(2)}) copy-start(bf16[64,512]{1,0:T(8,128)(2,1)S(1)} %collective-permute-done.3.refs_1_) | copy-start | bytes 196612
  29.7 15.7 %copy-start = (f32[2,16,64,64]{3,2,1,0:T(8,128)S(1)}, f32[2,16,64,64]{3,2,1,0:T(8,128)}, u32[]{:S(2)}) copy-start(f32[2,16,64,64]{3,2,1,0:T(8,128)} %param.9) | copy-start | bytes 1572868
  29.7 4.0 %collective-permute-start.6 = (bf16[64,512]{1,0:T(8,128)(2,1)}, bf16[64,512]{1,0:T(8,128)(2,1)S(1)}, u32[]{:S(2)}, u32[]{:S(2)}) collective-permute-start(bf16[64,512]{1,0:T(8,128)(2,1)} %get-tuple-element.10), channel_id=1, source_target_pairs={{0,1},{1,2},{2,3},{3,0},{4,5},{5,6},{6,7},{7,4},{8,9},{9,10},{10,1... | collective-permute-start | bytes 196616 | tf_op jit(solution)/shard_map/ppermute | solution.py:262
  29.8 5.2 %collective-permute-start.7 = (bf16[64,512]{1,0:T(8,128)(2,1)}, bf16[64,512]{1,0:T(8,128)(2,1)S(1)}, u32[]{:S(2)}, u32[]{:S(2)}) collective-permute-start(bf16[64,512]{1,0:T(8,128)(2,1)} %get-tuple-element.11), channel_id=1, source_target_pairs={{0,2},{1,3},{2,0},{3,1},{4,6},{5,7},{6,4},{7,5},{8,10},{9,11},{10,... | collective-permute-start | bytes 196616 | tf_op jit(solution)/shard_map/ppermute | solution.py:262
  30.7 4.3 %collective-permute-start.8 = (bf16[64,512]{1,0:T(8,128)(2,1)}, bf16[64,512]{1,0:T(8,128)(2,1)S(1)}, u32[]{:S(2)}, u32[]{:S(2)}) collective-permute-start(bf16[64,512]{1,0:T(8,128)(2,1)} %get-tuple-element.12), channel_id=1, source_target_pairs={{0,3},{1,0},{2,1},{3,2},{4,7},{5,4},{6,5},{7,6},{8,11},{9,8},{10,9... | collective-permute-start | bytes 196616 | tf_op jit(solution)/shard_map/ppermute | solution.py:262
  36.4 4.9 %collective-permute-start.9 = (bf16[64,2,64]{2,0,1:T(8,128)(2,1)S(1)}, bf16[64,2,64]{2,0,1:T(8,128)(2,1)S(1)}, u32[]{:S(2)}, u32[]{:S(2)}) collective-permute-start(bf16[64,2,64]{2,0,1:T(8,128)(2,1)S(1)} %bitcast.103), channel_id=1, source_target_pairs={{0,12},{4,0},{8,4},{12,8},{1,13},{5,1},{9,5},{13,9},{2,14},{6,2},{... | collective-permute-start | bytes 49160 | tf_op jit(solution)/shard_map/ppermute | solution.py:85
  39.6 4.8 %collective-permute-start.10 = (bf16[64,2,64]{2,0,1:T(8,128)(2,1)S(1)}, bf16[64,2,64]{2,0,1:T(8,128)(2,1)S(1)}, u32[]{:S(2)}, u32[]{:S(2)}) collective-permute-start(bf16[64,2,64]{2,0,1:T(8,128)(2,1)S(1)} %bitcast.102), channel_id=1, source_target_pairs={{0,8},{4,12},{8,0},{12,4},{1,9},{5,13},{9,1},{13,5},{2,10},{6,14},... | collective-permute-start | bytes 49160 | tf_op jit(solution)/shard_map/ppermute | solution.py:85
  39.6 5.7 %collective-permute-start.11 = (bf16[64,2,64]{2,0,1:T(8,128)(2,1)S(1)}, bf16[64,2,64]{2,0,1:T(8,128)(2,1)S(1)}, u32[]{:S(2)}, u32[]{:S(2)}) collective-permute-start(bf16[64,2,64]{2,0,1:T(8,128)(2,1)S(1)} %bitcast.101), channel_id=1, source_target_pairs={{0,4},{4,8},{8,12},{12,0},{1,5},{5,9},{9,13},{13,1},{2,6},{6,10},{... | collective-permute-start | bytes 49160 | tf_op jit(solution)/shard_map/ppermute | solution.py:85

commit v17 on v16

--- a/solution.py
+++ b/solution.py
@@ -200,7 +200,7 @@
     rows = pieces[0].shape[0]
     whole = lambda c: (0, 0)
     per_coil = lambda c: (c, 0, 0)
-    step_coils = 2 if coils % 2 == 0 else 1
+    step_coils = 4 if coils % 4 == 0 else (2 if coils % 2 == 0 else 1)
     flops = coils * 8 * height * width * width
     return pl.pallas_call(
         coil_chain_kernel,

time: 47.4 us -> 47 us (level)
  no operation moved by 1% of the time
where the time goes in v17:
time: 47 us; the launch traced here: 46.7 us
  starting transfers between devices  15 us (32%)
  waiting for transfers between devices  12.6 us (27%)
  Pallas kernels  9.08 us (19%)
  other arithmetic  7.02 us (15%)
  local copies, waits for them, and re-layouts  2.84 us (6%)
    ppermute x6, starting transfers between devices, exchange_blocks(): pieces.append(lax.ppermute(outgoing, axis, shifted(count, step)))  10.9 us
    pallas_call x1, Pallas kernels, coil_chain(): pl.pallas_call(coil_chain_kernel, out_shape=(jax.ShapeDtypeStruct((rows,...  9.08 us
    ppermute x6, waiting for transfers between devices, exchange_blocks(): pieces.append(lax.ppermute(outgoing, axis, shifted(count, step)))  5.63 us
    ppermute x3, waiting for transfers between devices, on_device(): lax.ppermute(own_rows, 'coil', shifted(groups, step))  4.1 us
    ppermute x3, waiting for transfers between devices, on_device(): lax.ppermute(outgoing[step - 1], 'coil', shifted(groups, step))  2.86 us
    ppermute x3, starting transfers between devices, on_device(): lax.ppermute(outgoing[step - 1], 'coil', shifted(groups, step))  2.37 us
    reduce_sum x1, other arithmetic, on_device(): jnp.sum(mixing[:, :, :, :, None, None] * factors[None, None], axis=(2, 3))  2.29 us
    ppermute x3, starting transfers between devices, on_device(): lax.ppermute(own_rows, 'coil', shifted(groups, step))  1.78 us
  transfers between devices with their start and end apart: 12, of which 9 were waited for; matrix products, arithmetic and copies ran while one was open for 4% of the time, Pallas kernels for 0%

profile of v17, /device:TPU:0, one launch (start us, length us, event | category | flops | bytes accessed | tf_op | source)
XLA Modules:
  0.0 46.7 jit_solution(7588378119764557411)
XLA Ops:
  0.0 0.7 %fusion.8 = f32[4,1,16]{2,0,1:T(4,128)S(1)} fusion(f32[2,4,16]{2,1,0:T(4,128)} %param.10), kind=kLoop, calls=%fused_computation.76 | loop fusion | flops 64 | bytes 512 | tf_op jit(solution)/shard_map/neg | solution.py:243
  0.7 0.7 %slice_bitcast_fusion.10 = (f32[16,4,1]{0,1,2:T(4,128)S(1)}, f32[4,1,16]{2,0,1:T(4,128)S(1)}, f32[4,1,16]{2,0,1:T(4,128)S(1)}, f32[16,4,1]{0,1,2:T(4,128)S(1)}) fusion(f32[2,4,16]{2,1,0:T(4,128)} %param.10), kind=kLoop, calls=%fused_computation.66 | loop fusion | bytes 1536 | tf_op jit(solution)/shard_map/stack | solution.py:268
  1.4 2.3 %multiply_reduce_fusion = bf16[4,2,64,64]{3,2,1,0:T(8,128)(2,1)S(1)} fusion(f32[2,16,64,64]{3,2,1,0:T(8,128)} %param.9, f32[4,1,2,16]{3,2,0,1:T(2,128)S(1)} %get-tuple-element.45, f32[4,1,2,16]{3,2,0,1:T(2,128)S(1)} %get-tuple-element.46), kind=kLoop, calls=%fused_computation | loop fusion | flops 2064640 | bytes 590848 | tf_op jit(solution)/shard_map/reduce_sum | solution.py:245
  3.7 3.1 %collective-permute-start.2 = (bf16[2,64,64]{2,1,0:T(8,128)(2,1)S(1)}, bf16[2,64,64]{2,1,0:T(8,128)(2,1)S(1)}, u32[]{:S(2)}, u32[]{:S(2)}) collective-permute-start(bf16[2,64,64]{2,1,0:T(8,128)(2,1)S(1)} %get-tuple-element.25), channel_id=1, source_target_pairs={{0,4},{4,8},{8,12},{12,0},{1,5},{5,9},{9,13},{13,1},{2,6},{6,10},{... | collective-permute-start | bytes 49160 | tf_op jit(solution)/shard_map/ppermute | solution.py:85
  6.8 2.6 %collective-permute-start.1 = (bf16[2,64,64]{2,1,0:T(8,128)(2,1)S(1)}, bf16[2,64,64]{2,1,0:T(8,128)(2,1)S(1)}, u32[]{:S(2)}, u32[]{:S(2)}) collective-permute-start(bf16[2,64,64]{2,1,0:T(8,128)(2,1)S(1)} %get-tuple-element.26), channel_id=1, source_target_pairs={{0,8},{4,12},{8,0},{12,4},{1,9},{5,13},{9,1},{13,5},{2,10},{6,14},... | collective-permute-start | bytes 49160 | tf_op jit(solution)/shard_map/ppermute | solution.py:85
  9.4 1.3 %collective-permute-start = (bf16[2,64,64]{2,1,0:T(8,128)(2,1)S(1)}, bf16[2,64,64]{2,1,0:T(8,128)(2,1)S(1)}, u32[]{:S(2)}, u32[]{:S(2)}) collective-permute-start(bf16[2,64,64]{2,1,0:T(8,128)(2,1)S(1)} %get-tuple-element.27), channel_id=1, source_target_pairs={{0,12},{4,0},{8,4},{12,8},{1,13},{5,1},{9,5},{13,9},{2,14},{6,2},{... | collective-permute-start | bytes 49160 | tf_op jit(solution)/shard_map/ppermute | solution.py:85
  10.7 0.7 %fusion = f32[16,4,1]{0,1,2:T(4,128)S(1)} fusion(f32[2,4,16]{2,1,0:T(4,128)} %param.10), kind=kLoop, calls=%fused_computation.63 | loop fusion | flops 64 | bytes 512 | tf_op jit(solution)/shard_map/stack | solution.py:268
  11.4 0.7 %convert_element_type.44 = f32[1,8,256]{2,1,0:T(8,128)S(1)} convert(s32[1,8,256]{2,1,0:T(8,128)} %param.13) | non-fusion elementwise | flops 2048 | bytes 16384 | tf_op jit(solution)/shard_map/convert_element_type | solution.py:255
  12.1 0.6 %copy.53 = f32[1,8,256]{2,0,1:T(1,128)} copy(f32[1,8,256]{2,1,0:T(8,128)S(1)} %convert_element_type.44) | data formatting | bytes 16384
  12.7 0.6 %collective-permute-done = bf16[2,64,64]{2,1,0:T(8,128)(2,1)S(1)} collective-permute-done((bf16[2,64,64]{2,1,0:T(8,128)(2,1)S(1)}, bf16[2,64,64]{2,1,0:T(8,128)(2,1)S(1)}, u32[]{:S(2)}, u32[]{:S(2)}) %collective-permute-start) | collective-permute-done | bytes 16416 | tf_op jit(solution)/shard_map/ppermute | solution.py:85
  13.8 1.6 %collective-permute-start.4 = (bf16[64,512]{1,0:T(8,128)(2,1)S(1)}, bf16[64,512]{1,0:T(8,128)(2,1)S(1)}, u32[]{:S(2)}, u32[]{:S(2)}) collective-permute-start(bf16[64,512]{1,0:T(8,128)(2,1)S(1)} %reshape.46.refs_0_), channel_id=1, source_target_pairs={{0,2},{1,3},{2,0},{3,1},{4,6},{5,7},{6,4},{7,5},{8,10},{9,11},{10,... | collective-permute-start | bytes 196616 | tf_op jit(solution)/shard_map/ppermute | solution.py:254
  15.7 3.7 %collective-permute-done.4.refs_2_ = bf16[64,512]{1,0:T(8,128)(2,1)S(1)} collective-permute-done((bf16[64,512]{1,0:T(8,128)(2,1)S(1)}, bf16[64,512]{1,0:T(8,128)(2,1)S(1)}, u32[]{:S(2)}, u32[]{:S(2)}) %collective-permute-start.4) | collective-permute-done | bytes 65568 | tf_op jit(solution)/shard_map/ppermute | solution.py:254
  20.2 9.1 %shard_map.91 = (f32[64,512]{1,0:T(8,128)}, bf16[64,512]{1,0:T(8,128)(2,1)}, bf16[64,512]{1,0:T(8,128)(2,1)}, bf16[64,512]{1,0:T(8,128)(2,1)}) custom-call(bf16[64,512]{1,0:T(8,128)(2,1)} %copy-done.1, bf16[64,512]{1,0:T(8,128)(2,1)} %copy-done.4, bf16[64,512]{1,0:T(8,128)(2,1)} %copy-done.3, bf16[64,512]{1,0:T(8,128)(2,1)} %copy-done.2, s32[1]{0:T(128)} %bitcast.24.refs_4_, ...), custom_call_target="tpu_custom_call" | custom-call | flops 4294967296 | bytes 4718592 | tf_op jit(solution)/shard_map/pallas_call | solution.py:205
  29.4 0.9 %collective-permute-start.7 = (bf16[64,512]{1,0:T(8,128)(2,1)}, bf16[64,512]{1,0:T(8,128)(2,1)S(1)}, u32[]{:S(2)}, u32[]{:S(2)}) collective-permute-start(bf16[64,512]{1,0:T(8,128)(2,1)} %get-tuple-element.11), channel_id=1, source_target_pairs={{0,2},{1,3},{2,0},{3,1},{4,6},{5,7},{6,4},{7,5},{8,10},{9,11},{10,... | collective-permute-start | bytes 196616 | tf_op jit(solution)/shard_map/ppermute | solution.py:262
  30.3 1.4 %collective-permute-start.8 = (bf16[64,512]{1,0:T(8,128)(2,1)}, bf16[64,512]{1,0:T(8,128)(2,1)S(1)}, u32[]{:S(2)}, u32[]{:S(2)}) collective-permute-start(bf16[64,512]{1,0:T(8,128)(2,1)} %get-tuple-element.12), channel_id=1, source_target_pairs={{0,3},{1,0},{2,1},{3,2},{4,7},{5,4},{6,5},{7,6},{8,11},{9,8},{10,9... | collective-permute-start | bytes 196616 | tf_op jit(solution)/shard_map/ppermute | solution.py:262
  31.7 1.6 %collective-permute-done.6 = bf16[64,512]{1,0:T(8,128)(2,1)S(1)} collective-permute-done((bf16[64,512]{1,0:T(8,128)(2,1)}, bf16[64,512]{1,0:T(8,128)(2,1)S(1)}, u32[]{:S(2)}, u32[]{:S(2)}) %collective-permute-start.6) | collective-permute-done | bytes 65568 | tf_op jit(solution)/shard_map/ppermute | solution.py:262
  33.4 1.2 %collective-permute-done.7 = bf16[64,512]{1,0:T(8,128)(2,1)S(1)} collective-permute-done((bf16[64,512]{1,0:T(8,128)(2,1)}, bf16[64,512]{1,0:T(8,128)(2,1)S(1)}, u32[]{:S(2)}, u32[]{:S(2)}) %collective-permute-start.7) | collective-permute-done | bytes 65568 | tf_op jit(solution)/shard_map/ppermute | solution.py:262
  34.6 0.9 %add_convert_fusion = bf16[64,512]{1,0:T(8,128)(2,1)S(1)} fusion(bf16[64,512]{1,0:T(8,128)(2,1)S(1)} %collective-permute-done.8, bf16[64,512]{1,0:T(8,128)(2,1)S(1)} %collective-permute-done.7, f32[64,512]{1,0:T(8,128)} %get-tuple-element.9, bf16[64,512]{1,0:T(8,128)(2,1)S(1)} %collective-permute-done.6), kind=kLoop, calls=%fused_computation.3 | loop fusion | flops 229376 | bytes 393216 | tf_op jit(solution)/shard_map/convert_element_type | solution.py:265
  36.0 3.2 %collective-permute-start.9 = (bf16[64,2,64]{2,0,1:T(8,128)(2,1)S(1)}, bf16[64,2,64]{2,0,1:T(8,128)(2,1)S(1)}, u32[]{:S(2)}, u32[]{:S(2)}) collective-permute-start(bf16[64,2,64]{2,0,1:T(8,128)(2,1)S(1)} %bitcast.103), channel_id=1, source_target_pairs={{0,12},{4,0},{8,4},{12,8},{1,13},{5,1},{9,5},{13,9},{2,14},{6,2},{... | collective-permute-start | bytes 49160 | tf_op jit(solution)/shard_map/ppermute | solution.py:85
  39.2 0.6 %collective-permute-start.11 = (bf16[64,2,64]{2,0,1:T(8,128)(2,1)S(1)}, bf16[64,2,64]{2,0,1:T(8,128)(2,1)S(1)}, u32[]{:S(2)}, u32[]{:S(2)}) collective-permute-start(bf16[64,2,64]{2,0,1:T(8,128)(2,1)S(1)} %bitcast.101), channel_id=1, source_target_pairs={{0,4},{4,8},{8,12},{12,0},{1,5},{5,9},{9,13},{13,1},{2,6},{6,10},{... | collective-permute-start | bytes 49160 | tf_op jit(solution)/shard_map/ppermute | solution.py:85
  39.8 1.0 %collective-permute-done.9 = bf16[64,2,64]{2,0,1:T(8,128)(2,1)S(1)} collective-permute-done((bf16[64,2,64]{2,0,1:T(8,128)(2,1)S(1)}, bf16[64,2,64]{2,0,1:T(8,128)(2,1)S(1)}, u32[]{:S(2)}, u32[]{:S(2)}) %collective-permute-start.9) | collective-permute-done | bytes 16416 | tf_op jit(solution)/shard_map/ppermute | solution.py:85
  40.9 3.1 %collective-permute-done.10 = bf16[64,2,64]{2,0,1:T(8,128)(2,1)S(1)} collective-permute-done((bf16[64,2,64]{2,0,1:T(8,128)(2,1)S(1)}, bf16[64,2,64]{2,0,1:T(8,128)(2,1)S(1)}, u32[]{:S(2)}, u32[]{:S(2)}) %collective-permute-start.10) | collective-permute-done | bytes 16416 | tf_op jit(solution)/shard_map/ppermute | solution.py:85
  44.0 0.9 %collective-permute-done.11 = bf16[64,2,64]{2,0,1:T(8,128)(2,1)S(1)} collective-permute-done((bf16[64,2,64]{2,0,1:T(8,128)(2,1)S(1)}, bf16[64,2,64]{2,0,1:T(8,128)(2,1)S(1)}, u32[]{:S(2)}, u32[]{:S(2)}) %collective-permute-start.11) | collective-permute-done | bytes 16416 | tf_op jit(solution)/shard_map/ppermute | solution.py:85
  45.0 1.7 %multiply_subtract_fusion = f32[2,16,64,64]{3,2,1,0:T(8,128)} fusion(f32[2,16,64,64]{3,2,1,0:T(8,128)S(1)} %copy-done, f32[64,64]{1,0:T(8,128)S(1)} %get-tuple-element.14, f32[2,16]{1,0:T(2,128)S(1)} %bitcast.111, f32[64,64]{1,0:T(8,128)S(1)} %get-tuple-element.15, f32[2,16]{1,0:T(2,128)S(1)} %bitcast.112, f32[64,64]{1,0:T(8,128)S(1)} %get-tuple-element.16, ...), kind=kLoop, calls=%fused_computation.1 | loop fusion | flops 2228224 | bytes 1180672 | tf_op jit(solution)/shard_map/sub | solution.py:275
  (49 shorter events, 2.2 us)
Async XLA Ops:
  3.7 9.6 %collective-permute-start.2 = (bf16[2,64,64]{2,1,0:T(8,128)(2,1)S(1)}, bf16[2,64,64]{2,1,0:T(8,128)(2,1)S(1)}, u32[]{:S(2)}, u32[]{:S(2)}) collective-permute-start(bf16[2,64,64]{2,1,0:T(8,128)(2,1)S(1)} %get-tuple-element.25), channel_id=1, source_target_pairs={{0,4},{4,8},{8,12},{12,0},{1,5},{5,9},{9,13},{13,1},{2,6},{6,10},{... | collective-permute-start | bytes 49160 | tf_op jit(solution)/shard_map/ppermute | solution.py:85
  6.8 6.5 %collective-permute-start.1 = (bf16[2,64,64]{2,1,0:T(8,128)(2,1)S(1)}, bf16[2,64,64]{2,1,0:T(8,128)(2,1)S(1)}, u32[]{:S(2)}, u32[]{:S(2)}) collective-permute-start(bf16[2,64,64]{2,1,0:T(8,128)(2,1)S(1)} %get-tuple-element.26), channel_id=1, source_target_pairs={{0,8},{4,12},{8,0},{12,4},{1,9},{5,13},{9,1},{13,5},{2,10},{6,14},... | collective-permute-start | bytes 49160 | tf_op jit(solution)/shard_map/ppermute | solution.py:85
  9.4 3.9 %collective-permute-start = (bf16[2,64,64]{2,1,0:T(8,128)(2,1)S(1)}, bf16[2,64,64]{2,1,0:T(8,128)(2,1)S(1)}, u32[]{:S(2)}, u32[]{:S(2)}) collective-permute-start(bf16[2,64,64]{2,1,0:T(8,128)(2,1)S(1)} %get-tuple-element.27), channel_id=1, source_target_pairs={{0,12},{4,0},{8,4},{12,8},{1,13},{5,1},{9,5},{13,9},{2,14},{6,2},{... | collective-permute-start | bytes 49160 | tf_op jit(solution)/shard_map/ppermute | solution.py:85
  13.7 5.9 %copy-start.1 = (bf16[64,512]{1,0:T(8,128)(2,1)}, bf16[64,512]{1,0:T(8,128)(2,1)S(1)}, u32[]{:S(2)}) copy-start(bf16[64,512]{1,0:T(8,128)(2,1)S(1)} %reshape.46.refs_0_) | copy-start | bytes 196612
  13.7 2.0 %collective-permute-start.5 = (bf16[64,512]{1,0:T(8,128)(2,1)S(1)}, bf16[64,512]{1,0:T(8,128)(2,1)S(1)}, u32[]{:S(2)}, u32[]{:S(2)}) collective-permute-start(bf16[64,512]{1,0:T(8,128)(2,1)S(1)} %reshape.46.refs_0_), channel_id=1, source_target_pairs={{0,3},{1,0},{2,1},{3,2},{4,7},{5,4},{6,5},{7,6},{8,11},{9,8},{10,9... | collective-permute-start | bytes 196616 | tf_op jit(solution)/shard_map/ppermute | solution.py:254
  13.8 5.6 %collective-permute-start.4 = (bf16[64,512]{1,0:T(8,128)(2,1)S(1)}, bf16[64,512]{1,0:T(8,128)(2,1)S(1)}, u32[]{:S(2)}, u32[]{:S(2)}) collective-permute-start(bf16[64,512]{1,0:T(8,128)(2,1)S(1)} %reshape.46.refs_0_), channel_id=1, source_target_pairs={{0,2},{1,3},{2,0},{3,1},{4,6},{5,7},{6,4},{7,5},{8,10},{9,11},{10,... | collective-permute-start | bytes 196616 | tf_op jit(solution)/shard_map/ppermute | solution.py:254
  15.3 4.3 %collective-permute-start.3 = (bf16[64,512]{1,0:T(8,128)(2,1)S(1)}, bf16[64,512]{1,0:T(8,128)(2,1)S(1)}, u32[]{:S(2)}, u32[]{:S(2)}) collective-permute-start(bf16[64,512]{1,0:T(8,128)(2,1)S(1)} %reshape.46.refs_0_), channel_id=1, source_target_pairs={{0,1},{1,2},{2,3},{3,0},{4,5},{5,6},{6,7},{7,4},{8,9},{9,10},{10,1... | collective-permute-start | bytes 196616 | tf_op jit(solution)/shard_map/ppermute | solution.py:254
  15.7 3.9 %copy-start.2 = (bf16[64,512]{1,0:T(8,128)(2,1)}, bf16[64,512]{1,0:T(8,128)(2,1)S(1)}, u32[]{:S(2)}) copy-start(bf16[64,512]{1,0:T(8,128)(2,1)S(1)} %collective-permute-done.5.refs_3_) | copy-start | bytes 196612
  19.4 0.6 %copy-start.3 = (bf16[64,512]{1,0:T(8,128)(2,1)}, bf16[64,512]{1,0:T(8,128)(2,1)S(1)}, u32[]{:S(2)}) copy-start(bf16[64,512]{1,0:T(8,128)(2,1)S(1)} %collective-permute-done.4.refs_2_) | copy-start | bytes 196612
  19.6 0.6 %copy-start.4 = (bf16[64,512]{1,0:T(8,128)(2,1)}, bf16[64,512]{1,0:T(8,128)(2,1)S(1)}, u32[]{:S(2)}) copy-start(bf16[64,512]{1,0:T(8,128)(2,1)S(1)} %collective-permute-done.3.refs_1_) | copy-start | bytes 196612
  29.3 15.7 %copy-start = (f32[2,16,64,64]{3,2,1,0:T(8,128)S(1)}, f32[2,16,64,64]{3,2,1,0:T(8,128)}, u32[]{:S(2)}) copy-start(f32[2,16,64,64]{3,2,1,0:T(8,128)} %param.9) | copy-start | bytes 1572868
  29.3 4.0 %collective-permute-start.6 = (bf16[64,512]{1,0:T(8,128)(2,1)}, bf16[64,512]{1,0:T(8,128)(2,1)S(1)}, u32[]{:S(2)}, u32[]{:S(2)}) collective-permute-start(bf16[64,512]{1,0:T(8,128)(2,1)} %get-tuple-element.10), channel_id=1, source_target_pairs={{0,1},{1,2},{2,3},{3,0},{4,5},{5,6},{6,7},{7,4},{8,9},{9,10},{10,1... | collective-permute-start | bytes 196616 | tf_op jit(solution)/shard_map/ppermute | solution.py:262
  29.4 5.2 %collective-permute-start.7 = (bf16[64,512]{1,0:T(8,128)(2,1)}, bf16[64,512]{1,0:T(8,128)(2,1)S(1)}, u32[]{:S(2)}, u32[]{:S(2)}) collective-permute-start(bf16[64,512]{1,0:T(8,128)(2,1)} %get-tuple-element.11), channel_id=1, source_target_pairs={{0,2},{1,3},{2,0},{3,1},{4,6},{5,7},{6,4},{7,5},{8,10},{9,11},{10,... | collective-permute-start | bytes 196616 | tf_op jit(solution)/shard_map/ppermute | solution.py:262
  30.3 4.3 %collective-permute-start.8 = (bf16[64,512]{1,0:T(8,128)(2,1)}, bf16[64,512]{1,0:T(8,128)(2,1)S(1)}, u32[]{:S(2)}, u32[]{:S(2)}) collective-permute-start(bf16[64,512]{1,0:T(8,128)(2,1)} %get-tuple-element.12), channel_id=1, source_target_pairs={{0,3},{1,0},{2,1},{3,2},{4,7},{5,4},{6,5},{7,6},{8,11},{9,8},{10,9... | collective-permute-start | bytes 196616 | tf_op jit(solution)/shard_map/ppermute | solution.py:262
  36.0 4.9 %collective-permute-start.9 = (bf16[64,2,64]{2,0,1:T(8,128)(2,1)S(1)}, bf16[64,2,64]{2,0,1:T(8,128)(2,1)S(1)}, u32[]{:S(2)}, u32[]{:S(2)}) collective-permute-start(bf16[64,2,64]{2,0,1:T(8,128)(2,1)S(1)} %bitcast.103), channel_id=1, source_target_pairs={{0,12},{4,0},{8,4},{12,8},{1,13},{5,1},{9,5},{13,9},{2,14},{6,2},{... | collective-permute-start | bytes 49160 | tf_op jit(solution)/shard_map/ppermute | solution.py:85
  39.2 4.8 %collective-permute-start.10 = (bf16[64,2,64]{2,0,1:T(8,128)(2,1)S(1)}, bf16[64,2,64]{2,0,1:T(8,128)(2,1)S(1)}, u32[]{:S(2)}, u32[]{:S(2)}) collective-permute-start(bf16[64,2,64]{2,0,1:T(8,128)(2,1)S(1)} %bitcast.102), channel_id=1, source_target_pairs={{0,8},{4,12},{8,0},{12,4},{1,9},{5,13},{9,1},{13,5},{2,10},{6,14},... | collective-permute-start | bytes 49160 | tf_op jit(solution)/shard_map/ppermute | solution.py:85
  39.2 5.7 %collective-permute-start.11 = (bf16[64,2,64]{2,0,1:T(8,128)(2,1)S(1)}, bf16[64,2,64]{2,0,1:T(8,128)(2,1)S(1)}, u32[]{:S(2)}, u32[]{:S(2)}) collective-permute-start(bf16[64,2,64]{2,0,1:T(8,128)(2,1)S(1)} %bitcast.101), channel_id=1, source_target_pairs={{0,4},{4,8},{8,12},{12,0},{1,5},{5,9},{9,13},{13,1},{2,6},{6,10},{... | collective-permute-start | bytes 49160 | tf_op jit(solution)/shard_map/ppermute | solution.py:85

commit v18 on v17

--- a/solution.py
+++ b/solution.py
@@ -106,7 +106,7 @@
     return jnp.concatenate([high, -low], axis=1)
 
 
-def coil_terms(image_ref, sens_ref, measured_ref, sampled_ref, forward_ref, adjoint_ref, table_re_ref, table_im_ref):
+def coil_terms(image_ref, sens_ref, measured_ref, sampled_ref, forward_ref, adjoint_ref, table_ref):
     coils, height, width = sens_ref.shape
     half_width = width // 2
     sens = sens_ref[...].astype(jnp.float32)
@@ -118,26 +118,30 @@
     coil = jnp.concatenate(
         [sens_re * image_re - sens_im * image_im, sens_re * image_im + sens_im * image_re], axis=2
     ).astype(jnp.bfloat16)
-    half_k = jnp.dot(
-        coil.reshape(coils * height, width), forward_ref[...], preferred_element_type=jnp.float32
-    ).astype(jnp.bfloat16)
-    table_re = table_re_ref[...]
-    table_im = table_im_ref[...]
+    half_k = jnp.dot(coil.reshape(coils * height, width), forward_ref[...], preferred_element_type=jnp.float32)
+    table = table_ref[...]
     backs = []
     for coil_index in range(coils):
-        one = half_k[coil_index * height:(coil_index + 1) * height]
-        kspace = jnp.dot(table_re, one, preferred_element_type=jnp.float32) + jnp.dot(
-            table_im, swap_halves(one, half_width, True), preferred_element_type=jnp.float32
+        one = half_k[coil_index * height:(coil_index + 1) * height].astype(jnp.bfloat16).astype(jnp.float32)
+        turned = jnp.concatenate([one[:, :half_width].T, one[:, half_width:].T], axis=0).astype(jnp.bfloat16)
+        parts = jnp.dot(turned, table, preferred_element_type=jnp.float32)
+        kspace_re = parts[:half_width, :height] - parts[half_width:, height:]
+        kspace_im = parts[:half_width, height:] + parts[half_width:, :height]
+        sampled = sampled_ref[coil_index]
+        residual = jnp.concatenate(
+            [
+                (sampled * (kspace_re - measured_ref[coil_index, 0].astype(jnp.float32))).astype(jnp.bfloat16),
+                (sampled * (kspace_im - measured_ref[coil_index, 1].astype(jnp.float32))).astype(jnp.bfloat16),
+            ],
+            axis=0,
         )
-        residual = (kspace - measured_ref[coil_index].astype(jnp.float32)).astype(jnp.bfloat16)
-        sampled = sampled_ref[coil_index].astype(jnp.bfloat16)
+        parts = jnp.dot(residual, table, preferred_element_type=jnp.float32)
+        back_re = (parts[:half_width, :height] + parts[half_width:, height:]).astype(jnp.bfloat16)
+        back_im = (parts[half_width:, :height] - parts[:half_width, height:]).astype(jnp.bfloat16)
         backs.append(
-            (
-                jnp.dot(table_re * sampled, residual, preferred_element_type=jnp.float32)
-                + jnp.dot(
-                    table_im * sampled, swap_halves(residual, half_width, False), preferred_element_type=jnp.float32
-                )
-            ).astype(jnp.bfloat16)
+            jnp.concatenate([back_re.astype(jnp.float32).T, back_im.astype(jnp.float32).T], axis=1).astype(
+                jnp.bfloat16
+            )
         )
     back_half = jnp.concatenate(backs, axis=0)
     coil_back = jnp.dot(back_half, adjoint_ref[...], preferred_element_type=jnp.float32).reshape(
@@ -152,14 +156,12 @@
 
 
 def coil_chain_kernel(*refs):
-    groups = (len(refs) - 9) // 2
+    groups = (len(refs) - 8) // 2
     pieces = refs[:groups]
-    place_ref, sens_ref, measured_ref, sampled_ref, forward_ref, adjoint_ref, table_re_ref, table_im_ref = refs[
-        groups:groups + 8
-    ]
-    own_ref = refs[groups + 8]
-    send_refs = refs[groups + 9:2 * groups + 8]
-    image_ref, total_ref = refs[2 * groups + 8:]
+    place_ref, sens_ref, measured_ref, sampled_ref, forward_ref, adjoint_ref, table_ref = refs[groups:groups + 7]
+    own_ref = refs[groups + 7]
+    send_refs = refs[groups + 8:2 * groups + 7]
+    image_ref, total_ref = refs[2 * groups + 7:]
     rows = pieces[0].shape[0]
     half_width = image_ref.shape[1] // 2
     me = place_ref[0]
@@ -174,8 +176,7 @@
                 value = jnp.where(source == other, pieces[other][...], value)
             image_ref[block * rows:(block + 1) * rows, :] = value
 
-    term = coil_terms(image_ref, sens_ref, measured_ref, sampled_ref, forward_ref, adjoint_ref,
-                      table_re_ref, table_im_ref)
+    term = coil_terms(image_ref, sens_ref, measured_ref, sampled_ref, forward_ref, adjoint_ref, table_ref)
 
     @pl.when(step == 0)
     def _():
@@ -194,7 +195,7 @@
             send_refs[shift - 1][...] = total_ref[pl.ds(start, rows), :].astype(jnp.bfloat16)
 
 
-def coil_chain(pieces, place, sens, measured, sampled, forward_x, adjoint_x, table_y_re, table_y_im):
+def coil_chain(pieces, place, sens, measured, sampled, forward_x, adjoint_x, table_y):
     coils, height, width = sens.shape
     groups = len(pieces)
     rows = pieces[0].shape[0]
@@ -211,12 +212,11 @@
         + [
             pl.BlockSpec(memory_space=pltpu.SMEM),
             pl.BlockSpec((step_coils, height, width), per_coil),
-            pl.BlockSpec((step_coils, height, width), per_coil),
+            pl.BlockSpec((step_coils, 2, width // 2, height), lambda c: (c, 0, 0, 0)),
             pl.BlockSpec((step_coils, 1, height), per_coil),
             pl.BlockSpec((width, width), whole),
             pl.BlockSpec((width, width), whole),
-            pl.BlockSpec((height, height), whole),
-            pl.BlockSpec((height, height), whole),
+            pl.BlockSpec((height, 2 * height), whole),
         ],
         out_specs=(pl.BlockSpec((rows, width), whole),) * groups,
         scratch_shapes=[pltpu.VMEM((height, width), jnp.bfloat16), pltpu.VMEM((height, width), jnp.float32)],
@@ -224,7 +224,7 @@
         cost_estimate=pl.CostEstimate(
             flops=flops, transcendentals=0, bytes_accessed=2 * 2 * coils * height * width + 4 * height * width
         ),
-    )(*pieces, place, sens, measured, sampled, forward_x, adjoint_x, table_y_re, table_y_im)
+    )(*pieces, place, sens, measured, sampled, forward_x, adjoint_x, table_y)
 
 
 def on_device(factors, temporal, maps, kdata, masks):
@@ -235,8 +235,7 @@
     table_y_re, table_y_im = dft_parts(width_y)
     forward_x = jnp.asarray(np.block([[table_x_re, table_x_im], [-table_x_im, table_x_re]]))
     adjoint_x = jnp.asarray(np.block([[table_x_re, -table_x_im], [table_x_im, table_x_re]]))
-    table_y_re = jnp.asarray(table_y_re)
-    table_y_im = jnp.asarray(table_y_im)
+    table_y = jnp.asarray(np.concatenate([table_y_re, table_y_im], axis=1))
     time_re = temporal[0]
     time_im = temporal[1]
     mixing = jnp.stack(
@@ -254,8 +253,10 @@
     pieces = [own_rows] + [lax.ppermute(own_rows, "coil", shifted(groups, step)) for step in range(1, groups)]
     sampled = masks[0].astype(jnp.float32)[:, None, :]
     place = jnp.reshape(me_c, (1,)).astype(jnp.int32)
+    coils_here = kdata.shape[1]
+    measured = jnp.transpose(kdata[0].reshape(coils_here, width_y, 2, width_x), (0, 2, 3, 1))
     own_total, *outgoing = coil_chain(
-        pieces, place, maps, kdata[0], sampled, forward_x, adjoint_x, table_y_re, table_y_im
+        pieces, place, maps, measured, sampled, forward_x, adjoint_x, table_y
     )
     own_share = own_total
     for step in range(1, groups):

time: 47 us -> 49.1 us (1.045)
  local copies, waits for them, and re-layouts: 2.84 us -> 6.77 us
  waiting for transfers between devices: 12.6 us -> 10.3 us
  starting transfers between devices: 15 us -> 16.4 us
  other arithmetic: 7.02 us -> 6.32 us
    unnamed x27 -> x30, local copies, waits for them, and re-layouts: 1.4 us -> 5.32 us
    ppermute x3, waiting for transfers between devices: 4.1 us -> 1.89 us  [on_device(): lax.ppermute(own_rows, 'coil', shifted(groups, step))]
    ppermute x3, starting transfers between devices: 1.78 us -> 3 us  [on_device(): lax.ppermute(own_rows, 'coil', shifted(groups, step))]
    ppermute x3, starting transfers between devices: 2.37 us -> 3.16 us  [on_device(): lax.ppermute(outgoing[step - 1], 'coil', shifted(groups, step))]
    convert_element_type x1, other arithmetic: 0.7 us -> 0.01 us  [on_device(): sampled = masks[0].astype(jnp.float32)[:, None, :]]
    ppermute x6, starting transfers between devices: 10.9 us -> 10.2 us  [exchange_blocks(): pieces.append(lax.ppermute(outgoing, axis, shifted(count, step)))]
  transfers between devices with their start and end apart: 12 -> 12, of which waited for: 9 -> 8; matrix products, arithmetic and copies ran while one was open for 4% -> 11% of each run, Pallas kernels for 0% -> 0%
where the time goes in v18:
time: 49.1 us; the launch traced here: 48.8 us
  starting transfers between devices  16.4 us (33%)
  waiting for transfers between devices  10.3 us (21%)
  Pallas kernels  8.76 us (18%)
  local copies, waits for them, and re-layouts  6.77 us (14%)
  other arithmetic  6.32 us (13%)
    ppermute x6, starting transfers between devices, exchange_blocks(): pieces.append(lax.ppermute(outgoing, axis, shifted(count, step)))  10.2 us
    pallas_call x1, Pallas kernels, coil_chain(): pl.pallas_call(coil_chain_kernel, out_shape=(jax.ShapeDtypeStruct((rows,...  8.76 us
    ppermute x6, waiting for transfers between devices, exchange_blocks(): pieces.append(lax.ppermute(outgoing, axis, shifted(count, step)))  5.69 us
    unnamed x30, local copies, waits for them, and re-layouts  5.32 us
    ppermute x3, starting transfers between devices, on_device(): lax.ppermute(outgoing[step - 1], 'coil', shifted(groups, step))  3.16 us
    ppermute x3, starting transfers between devices, on_device(): lax.ppermute(own_rows, 'coil', shifted(groups, step))  3 us
    ppermute x3, waiting for transfers between devices, on_device(): lax.ppermute(outgoing[step - 1], 'coil', shifted(groups, step))  2.76 us
    reduce_sum x1, other arithmetic, on_device(): jnp.sum(mixing[:, :, :, :, None, None] * factors[None, None], axis=(2, 3))  2.29 us
  transfers between devices with their start and end apart: 12, of which 8 were waited for; matrix products, arithmetic and copies ran while one was open for 11% of the time, Pallas kernels for 0%

profile of v18, /device:TPU:0, one launch (start us, length us, event | category | flops | bytes accessed | tf_op | source)
XLA Modules:
  0.0 48.8 jit_solution(8595844586180031403)
XLA Ops:
  0.0 0.7 %slice_bitcast_fusion.10 = (f32[16,4,1]{0,1,2:T(4,128)S(1)}, f32[4,1,16]{2,0,1:T(4,128)S(1)}, f32[4,1,16]{2,0,1:T(4,128)S(1)}, f32[16,4,1]{0,1,2:T(4,128)S(1)}) fusion(f32[2,4,16]{2,1,0:T(4,128)} %param.9), kind=kLoop, calls=%fused_computation.66 | loop fusion | bytes 1536 | tf_op jit(solution)/shard_map/stack | solution.py:269
  0.7 0.7 %fusion.8 = f32[4,1,16]{2,0,1:T(4,128)S(1)} fusion(f32[2,4,16]{2,1,0:T(4,128)} %param.9), kind=kLoop, calls=%fused_computation.76 | loop fusion | flops 64 | bytes 512 | tf_op jit(solution)/shard_map/neg | solution.py:242
  1.4 2.3 %multiply_reduce_fusion = bf16[4,2,64,64]{3,2,1,0:T(8,128)(2,1)S(1)} fusion(f32[2,16,64,64]{3,2,1,0:T(8,128)} %param.8, f32[4,1,2,16]{3,2,0,1:T(2,128)S(1)} %get-tuple-element.45, f32[4,1,2,16]{3,2,0,1:T(2,128)S(1)} %get-tuple-element.46), kind=kLoop, calls=%fused_computation | loop fusion | flops 2064640 | bytes 590848 | tf_op jit(solution)/shard_map/reduce_sum | solution.py:244
  3.7 5.1 %collective-permute-start = (bf16[2,64,64]{2,1,0:T(8,128)(2,1)S(1)}, bf16[2,64,64]{2,1,0:T(8,128)(2,1)S(1)}, u32[]{:S(2)}, u32[]{:S(2)}) collective-permute-start(bf16[2,64,64]{2,1,0:T(8,128)(2,1)S(1)} %get-tuple-element.27), channel_id=1, source_target_pairs={{0,12},{4,0},{8,4},{12,8},{1,13},{5,1},{9,5},{13,9},{2,14},{6,2},{... | collective-permute-start | bytes 49160 | tf_op jit(solution)/shard_map/ppermute | solution.py:85
  8.8 1.0 %collective-permute-start.2 = (bf16[2,64,64]{2,1,0:T(8,128)(2,1)S(1)}, bf16[2,64,64]{2,1,0:T(8,128)(2,1)S(1)}, u32[]{:S(2)}, u32[]{:S(2)}) collective-permute-start(bf16[2,64,64]{2,1,0:T(8,128)(2,1)S(1)} %get-tuple-element.25), channel_id=1, source_target_pairs={{0,4},{4,8},{8,12},{12,0},{1,5},{5,9},{9,13},{13,1},{2,6},{6,10},{... | collective-permute-start | bytes 49160 | tf_op jit(solution)/shard_map/ppermute | solution.py:85
  9.8 0.7 %fusion = f32[16,4,1]{0,1,2:T(4,128)S(1)} fusion(f32[2,4,16]{2,1,0:T(4,128)} %param.9), kind=kLoop, calls=%fused_computation.63 | loop fusion | flops 64 | bytes 512 | tf_op jit(solution)/shard_map/stack | solution.py:269
  10.5 3.9 %copy.28 = bf16[1,8,256,512]{2,3,1,0:T(8,128)(2,1)} copy(bf16[1,8,256,512]{3,2,1,0:T(8,128)(2,1)} %param.11) | data formatting | bytes 4194304 | tf_op args[3]
  14.5 0.6 %copy.55 = f32[1,8,256]{2,0,1:T(1,128)} copy(f32[1,8,256]{2,1,0:T(8,128)S(1)} %convert_element_type.44) | data formatting | bytes 16384
  15.5 1.6 %collective-permute-start.4 = (bf16[64,512]{1,0:T(8,128)(2,1)S(1)}, bf16[64,512]{1,0:T(8,128)(2,1)S(1)}, u32[]{:S(2)}, u32[]{:S(2)}) collective-permute-start(bf16[64,512]{1,0:T(8,128)(2,1)S(1)} %reshape.46.refs_0_), channel_id=1, source_target_pairs={{0,2},{1,3},{2,0},{3,1},{4,6},{5,7},{6,4},{7,5},{8,10},{9,11},{10,... | collective-permute-start | bytes 196616 | tf_op jit(solution)/shard_map/ppermute | solution.py:253
  17.1 1.4 %collective-permute-start.5 = (bf16[64,512]{1,0:T(8,128)(2,1)S(1)}, bf16[64,512]{1,0:T(8,128)(2,1)S(1)}, u32[]{:S(2)}, u32[]{:S(2)}) collective-permute-start(bf16[64,512]{1,0:T(8,128)(2,1)S(1)} %reshape.46.refs_0_), channel_id=1, source_target_pairs={{0,3},{1,0},{2,1},{3,2},{4,7},{5,4},{6,5},{7,6},{8,11},{9,8},{10,9... | collective-permute-start | bytes 196616 | tf_op jit(solution)/shard_map/ppermute | solution.py:253
  18.5 0.8 %collective-permute-done.3.refs_1_ = bf16[64,512]{1,0:T(8,128)(2,1)S(1)} collective-permute-done((bf16[64,512]{1,0:T(8,128)(2,1)S(1)}, bf16[64,512]{1,0:T(8,128)(2,1)S(1)}, u32[]{:S(2)}, u32[]{:S(2)}) %collective-permute-start.3) | collective-permute-done | bytes 65568 | tf_op jit(solution)/shard_map/ppermute | solution.py:253
  19.3 0.9 %collective-permute-done.4.refs_2_ = bf16[64,512]{1,0:T(8,128)(2,1)S(1)} collective-permute-done((bf16[64,512]{1,0:T(8,128)(2,1)S(1)}, bf16[64,512]{1,0:T(8,128)(2,1)S(1)}, u32[]{:S(2)}, u32[]{:S(2)}) %collective-permute-start.4) | collective-permute-done | bytes 65568 | tf_op jit(solution)/shard_map/ppermute | solution.py:253
  21.0 8.8 %shard_map.82 = (f32[64,512]{1,0:T(8,128)}, bf16[64,512]{1,0:T(8,128)(2,1)}, bf16[64,512]{1,0:T(8,128)(2,1)}, bf16[64,512]{1,0:T(8,128)(2,1)}) custom-call(bf16[64,512]{1,0:T(8,128)(2,1)} %copy-done.1, bf16[64,512]{1,0:T(8,128)(2,1)} %copy-done.3, bf16[64,512]{1,0:T(8,128)(2,1)} %copy-done.4, bf16[64,512]{1,0:T(8,128)(2,1)} %copy-done.5, s32[1]{0:T(128)} %bitcast.24.refs_4_, ...), custom_call_target="tpu_custom_call" | custom-call | flops 4294967296 | bytes 4718592 | tf_op jit(solution)/shard_map/pallas_call | solution.py:206
  29.8 0.8 %collective-permute-start.6 = (bf16[64,512]{1,0:T(8,128)(2,1)}, bf16[64,512]{1,0:T(8,128)(2,1)S(1)}, u32[]{:S(2)}, u32[]{:S(2)}) collective-permute-start(bf16[64,512]{1,0:T(8,128)(2,1)} %get-tuple-element.10), channel_id=1, source_target_pairs={{0,1},{1,2},{2,3},{3,0},{4,5},{5,6},{6,7},{7,4},{8,9},{9,10},{10,1... | collective-permute-start | bytes 196616 | tf_op jit(solution)/shard_map/ppermute | solution.py:263
  30.6 1.5 %collective-permute-start.7 = (bf16[64,512]{1,0:T(8,128)(2,1)}, bf16[64,512]{1,0:T(8,128)(2,1)S(1)}, u32[]{:S(2)}, u32[]{:S(2)}) collective-permute-start(bf16[64,512]{1,0:T(8,128)(2,1)} %get-tuple-element.11), channel_id=1, source_target_pairs={{0,2},{1,3},{2,0},{3,1},{4,6},{5,7},{6,4},{7,5},{8,10},{9,11},{10,... | collective-permute-start | bytes 196616 | tf_op jit(solution)/shard_map/ppermute | solution.py:263
  32.1 0.9 %collective-permute-start.8 = (bf16[64,512]{1,0:T(8,128)(2,1)}, bf16[64,512]{1,0:T(8,128)(2,1)S(1)}, u32[]{:S(2)}, u32[]{:S(2)}) collective-permute-start(bf16[64,512]{1,0:T(8,128)(2,1)} %get-tuple-element.12), channel_id=1, source_target_pairs={{0,3},{1,0},{2,1},{3,2},{4,7},{5,4},{6,5},{7,6},{8,11},{9,8},{10,9... | collective-permute-start | bytes 196616 | tf_op jit(solution)/shard_map/ppermute | solution.py:263
  33.0 0.9 %collective-permute-done.6 = bf16[64,512]{1,0:T(8,128)(2,1)S(1)} collective-permute-done((bf16[64,512]{1,0:T(8,128)(2,1)}, bf16[64,512]{1,0:T(8,128)(2,1)S(1)}, u32[]{:S(2)}, u32[]{:S(2)}) %collective-permute-start.6) | collective-permute-done | bytes 65568 | tf_op jit(solution)/shard_map/ppermute | solution.py:263
  33.8 1.9 %collective-permute-done.7 = bf16[64,512]{1,0:T(8,128)(2,1)S(1)} collective-permute-done((bf16[64,512]{1,0:T(8,128)(2,1)}, bf16[64,512]{1,0:T(8,128)(2,1)S(1)}, u32[]{:S(2)}, u32[]{:S(2)}) %collective-permute-start.7) | collective-permute-done | bytes 65568 | tf_op jit(solution)/shard_map/ppermute | solution.py:263
  35.7 0.9 %add_convert_fusion = bf16[64,512]{1,0:T(8,128)(2,1)S(1)} fusion(bf16[64,512]{1,0:T(8,128)(2,1)S(1)} %collective-permute-done.8, bf16[64,512]{1,0:T(8,128)(2,1)S(1)} %collective-permute-done.7, f32[64,512]{1,0:T(8,128)} %get-tuple-element.9, bf16[64,512]{1,0:T(8,128)(2,1)S(1)} %collective-permute-done.6), kind=kLoop, calls=%fused_computation.3 | loop fusion | flops 229376 | bytes 393216 | tf_op jit(solution)/shard_map/convert_element_type | solution.py:266
  37.1 2.9 %collective-permute-start.9 = (bf16[64,2,64]{2,0,1:T(8,128)(2,1)S(1)}, bf16[64,2,64]{2,0,1:T(8,128)(2,1)S(1)}, u32[]{:S(2)}, u32[]{:S(2)}) collective-permute-start(bf16[64,2,64]{2,0,1:T(8,128)(2,1)S(1)} %bitcast.104), channel_id=1, source_target_pairs={{0,12},{4,0},{8,4},{12,8},{1,13},{5,1},{9,5},{13,9},{2,14},{6,2},{... | collective-permute-start | bytes 49160 | tf_op jit(solution)/shard_map/ppermute | solution.py:85
  40.0 1.2 %collective-permute-start.10 = (bf16[64,2,64]{2,0,1:T(8,128)(2,1)S(1)}, bf16[64,2,64]{2,0,1:T(8,128)(2,1)S(1)}, u32[]{:S(2)}, u32[]{:S(2)}) collective-permute-start(bf16[64,2,64]{2,0,1:T(8,128)(2,1)S(1)} %bitcast.105), channel_id=1, source_target_pairs={{0,8},{4,12},{8,0},{12,4},{1,9},{5,13},{9,1},{13,5},{2,10},{6,14},... | collective-permute-start | bytes 49160 | tf_op jit(solution)/shard_map/ppermute | solution.py:85
  41.8 3.1 %collective-permute-done.10 = bf16[64,2,64]{2,0,1:T(8,128)(2,1)S(1)} collective-permute-done((bf16[64,2,64]{2,0,1:T(8,128)(2,1)S(1)}, bf16[64,2,64]{2,0,1:T(8,128)(2,1)S(1)}, u32[]{:S(2)}, u32[]{:S(2)}) %collective-permute-start.10) | collective-permute-done | bytes 16416 | tf_op jit(solution)/shard_map/ppermute | solution.py:85
  44.9 2.1 %collective-permute-done.11 = bf16[64,2,64]{2,0,1:T(8,128)(2,1)S(1)} collective-permute-done((bf16[64,2,64]{2,0,1:T(8,128)(2,1)S(1)}, bf16[64,2,64]{2,0,1:T(8,128)(2,1)S(1)}, u32[]{:S(2)}, u32[]{:S(2)}) %collective-permute-start.11) | collective-permute-done | bytes 16416 | tf_op jit(solution)/shard_map/ppermute | solution.py:85
  47.1 1.7 %multiply_subtract_fusion = f32[2,16,64,64]{3,2,1,0:T(8,128)} fusion(f32[2,16,64,64]{3,2,1,0:T(8,128)S(1)} %copy-done, f32[64,64]{1,0:T(8,128)S(1)} %get-tuple-element.14, f32[2,16]{1,0:T(2,128)S(1)} %bitcast.114, f32[64,64]{1,0:T(8,128)S(1)} %get-tuple-element.15, f32[2,16]{1,0:T(2,128)S(1)} %bitcast.115, f32[64,64]{1,0:T(8,128)S(1)} %get-tuple-element.16, ...), kind=kLoop, calls=%fused_computation.1 | loop fusion | flops 2228224 | bytes 1180672 | tf_op jit(solution)/shard_map/sub | solution.py:276
  (52 shorter events, 2.4 us)
Async XLA Ops:
  3.7 11.3 %collective-permute-start = (bf16[2,64,64]{2,1,0:T(8,128)(2,1)S(1)}, bf16[2,64,64]{2,1,0:T(8,128)(2,1)S(1)}, u32[]{:S(2)}, u32[]{:S(2)}) collective-permute-start(bf16[2,64,64]{2,1,0:T(8,128)(2,1)S(1)} %get-tuple-element.27), channel_id=1, source_target_pairs={{0,12},{4,0},{8,4},{12,8},{1,13},{5,1},{9,5},{13,9},{2,14},{6,2},{... | collective-permute-start | bytes 49160 | tf_op jit(solution)/shard_map/ppermute | solution.py:85
  8.8 6.2 %collective-permute-start.1 = (bf16[2,64,64]{2,1,0:T(8,128)(2,1)S(1)}, bf16[2,64,64]{2,1,0:T(8,128)(2,1)S(1)}, u32[]{:S(2)}, u32[]{:S(2)}) collective-permute-start(bf16[2,64,64]{2,1,0:T(8,128)(2,1)S(1)} %get-tuple-element.26), channel_id=1, source_target_pairs={{0,8},{4,12},{8,0},{12,4},{1,9},{5,13},{9,1},{13,5},{2,10},{6,14},... | collective-permute-start | bytes 49160 | tf_op jit(solution)/shard_map/ppermute | solution.py:85
  8.8 6.3 %collective-permute-start.2 = (bf16[2,64,64]{2,1,0:T(8,128)(2,1)S(1)}, bf16[2,64,64]{2,1,0:T(8,128)(2,1)S(1)}, u32[]{:S(2)}, u32[]{:S(2)}) collective-permute-start(bf16[2,64,64]{2,1,0:T(8,128)(2,1)S(1)} %get-tuple-element.25), channel_id=1, source_target_pairs={{0,4},{4,8},{8,12},{12,0},{1,5},{5,9},{9,13},{13,1},{2,6},{6,10},{... | collective-permute-start | bytes 49160 | tf_op jit(solution)/shard_map/ppermute | solution.py:85
  10.5 3.9 %copy-start.2 = (s32[1,8,256]{2,1,0:T(8,128)S(1)}, s32[1,8,256]{2,1,0:T(8,128)}, u32[]{:S(2)}) copy-start(s32[1,8,256]{2,1,0:T(8,128)} %param.12) | copy-start | bytes 24580
  15.5 4.9 %copy-start.1 = (bf16[64,512]{1,0:T(8,128)(2,1)}, bf16[64,512]{1,0:T(8,128)(2,1)S(1)}, u32[]{:S(2)}) copy-start(bf16[64,512]{1,0:T(8,128)(2,1)S(1)} %reshape.46.refs_0_) | copy-start | bytes 196612
  15.5 3.8 %collective-permute-start.3 = (bf16[64,512]{1,0:T(8,128)(2,1)S(1)}, bf16[64,512]{1,0:T(8,128)(2,1)S(1)}, u32[]{:S(2)}, u32[]{:S(2)}) collective-permute-start(bf16[64,512]{1,0:T(8,128)(2,1)S(1)} %reshape.46.refs_0_), channel_id=1, source_target_pairs={{0,1},{1,2},{2,3},{3,0},{4,5},{5,6},{6,7},{7,4},{8,9},{9,10},{10,1... | collective-permute-start | bytes 196616 | tf_op jit(solution)/shard_map/ppermute | solution.py:253
  15.5 4.6 %collective-permute-start.4 = (bf16[64,512]{1,0:T(8,128)(2,1)S(1)}, bf16[64,512]{1,0:T(8,128)(2,1)S(1)}, u32[]{:S(2)}, u32[]{:S(2)}) collective-permute-start(bf16[64,512]{1,0:T(8,128)(2,1)S(1)} %reshape.46.refs_0_), channel_id=1, source_target_pairs={{0,2},{1,3},{2,0},{3,1},{4,6},{5,7},{6,4},{7,5},{8,10},{9,11},{10,... | collective-permute-start | bytes 196616 | tf_op jit(solution)/shard_map/ppermute | solution.py:253
  17.1 3.3 %collective-permute-start.5 = (bf16[64,512]{1,0:T(8,128)(2,1)S(1)}, bf16[64,512]{1,0:T(8,128)(2,1)S(1)}, u32[]{:S(2)}, u32[]{:S(2)}) collective-permute-start(bf16[64,512]{1,0:T(8,128)(2,1)S(1)} %reshape.46.refs_0_), channel_id=1, source_target_pairs={{0,3},{1,0},{2,1},{3,2},{4,7},{5,4},{6,5},{7,6},{8,11},{9,8},{10,9... | collective-permute-start | bytes 196616 | tf_op jit(solution)/shard_map/ppermute | solution.py:253
  19.3 1.1 %copy-start.3 = (bf16[64,512]{1,0:T(8,128)(2,1)}, bf16[64,512]{1,0:T(8,128)(2,1)S(1)}, u32[]{:S(2)}) copy-start(bf16[64,512]{1,0:T(8,128)(2,1)S(1)} %collective-permute-done.3.refs_1_) | copy-start | bytes 196612
  20.2 0.6 %copy-start.4 = (bf16[64,512]{1,0:T(8,128)(2,1)}, bf16[64,512]{1,0:T(8,128)(2,1)S(1)}, u32[]{:S(2)}) copy-start(bf16[64,512]{1,0:T(8,128)(2,1)S(1)} %collective-permute-done.4.refs_2_) | copy-start | bytes 196612
  20.4 0.6 %copy-start.5 = (bf16[64,512]{1,0:T(8,128)(2,1)}, bf16[64,512]{1,0:T(8,128)(2,1)S(1)}, u32[]{:S(2)}) copy-start(bf16[64,512]{1,0:T(8,128)(2,1)S(1)} %collective-permute-done.5.refs_3_) | copy-start | bytes 196612
  29.8 17.3 %copy-start = (f32[2,16,64,64]{3,2,1,0:T(8,128)S(1)}, f32[2,16,64,64]{3,2,1,0:T(8,128)}, u32[]{:S(2)}) copy-start(f32[2,16,64,64]{3,2,1,0:T(8,128)} %param.8) | copy-start | bytes 1572868
  29.8 4.0 %collective-permute-start.6 = (bf16[64,512]{1,0:T(8,128)(2,1)}, bf16[64,512]{1,0:T(8,128)(2,1)S(1)}, u32[]{:S(2)}, u32[]{:S(2)}) collective-permute-start(bf16[64,512]{1,0:T(8,128)(2,1)} %get-tuple-element.10), channel_id=1, source_target_pairs={{0,1},{1,2},{2,3},{3,0},{4,5},{5,6},{6,7},{7,4},{8,9},{9,10},{10,1... | collective-permute-start | bytes 196616 | tf_op jit(solution)/shard_map/ppermute | solution.py:263
  30.6 5.1 %collective-permute-start.7 = (bf16[64,512]{1,0:T(8,128)(2,1)}, bf16[64,512]{1,0:T(8,128)(2,1)S(1)}, u32[]{:S(2)}, u32[]{:S(2)}) collective-permute-start(bf16[64,512]{1,0:T(8,128)(2,1)} %get-tuple-element.11), channel_id=1, source_target_pairs={{0,2},{1,3},{2,0},{3,1},{4,6},{5,7},{6,4},{7,5},{8,10},{9,11},{10,... | collective-permute-start | bytes 196616 | tf_op jit(solution)/shard_map/ppermute | solution.py:263
  32.1 3.7 %collective-permute-start.8 = (bf16[64,512]{1,0:T(8,128)(2,1)}, bf16[64,512]{1,0:T(8,128)(2,1)S(1)}, u32[]{:S(2)}, u32[]{:S(2)}) collective-permute-start(bf16[64,512]{1,0:T(8,128)(2,1)} %get-tuple-element.12), channel_id=1, source_target_pairs={{0,3},{1,0},{2,1},{3,2},{4,7},{5,4},{6,5},{7,6},{8,11},{9,8},{10,9... | collective-permute-start | bytes 196616 | tf_op jit(solution)/shard_map/ppermute | solution.py:263
  37.1 4.6 %collective-permute-start.9 = (bf16[64,2,64]{2,0,1:T(8,128)(2,1)S(1)}, bf16[64,2,64]{2,0,1:T(8,128)(2,1)S(1)}, u32[]{:S(2)}, u32[]{:S(2)}) collective-permute-start(bf16[64,2,64]{2,0,1:T(8,128)(2,1)S(1)} %bitcast.104), channel_id=1, source_target_pairs={{0,12},{4,0},{8,4},{12,8},{1,13},{5,1},{9,5},{13,9},{2,14},{6,2},{... | collective-permute-start | bytes 49160 | tf_op jit(solution)/shard_map/ppermute | solution.py:85
  40.0 4.9 %collective-permute-start.10 = (bf16[64,2,64]{2,0,1:T(8,128)(2,1)S(1)}, bf16[64,2,64]{2,0,1:T(8,128)(2,1)S(1)}, u32[]{:S(2)}, u32[]{:S(2)}) collective-permute-start(bf16[64,2,64]{2,0,1:T(8,128)(2,1)S(1)} %bitcast.105), channel_id=1, source_target_pairs={{0,8},{4,12},{8,0},{12,4},{1,9},{5,13},{9,1},{13,5},{2,10},{6,14},... | collective-permute-start | bytes 49160 | tf_op jit(solution)/shard_map/ppermute | solution.py:85
  41.2 5.8 %collective-permute-start.11 = (bf16[64,2,64]{2,0,1:T(8,128)(2,1)S(1)}, bf16[64,2,64]{2,0,1:T(8,128)(2,1)S(1)}, u32[]{:S(2)}, u32[]{:S(2)}) collective-permute-start(bf16[64,2,64]{2,0,1:T(8,128)(2,1)S(1)} %bitcast.106), channel_id=1, source_target_pairs={{0,4},{4,8},{8,12},{12,0},{1,5},{5,9},{9,13},{13,1},{2,6},{6,10},{... | collective-permute-start | bytes 49160 | tf_op jit(solution)/shard_map/ppermute | solution.py:85

commit v19 on v18

--- a/solution.py
+++ b/solution.py
@@ -128,10 +128,11 @@
         kspace_re = parts[:half_width, :height] - parts[half_width:, height:]
         kspace_im = parts[:half_width, height:] + parts[half_width:, :height]
         sampled = sampled_ref[coil_index]
+        measured = measured_ref[coil_index].astype(jnp.float32)
         residual = jnp.concatenate(
             [
-                (sampled * (kspace_re - measured_ref[coil_index, 0].astype(jnp.float32))).astype(jnp.bfloat16),
-                (sampled * (kspace_im - measured_ref[coil_index, 1].astype(jnp.float32))).astype(jnp.bfloat16),
+                (sampled * (kspace_re - measured[:, :half_width].T)).astype(jnp.bfloat16),
+                (sampled * (kspace_im - measured[:, half_width:].T)).astype(jnp.bfloat16),
             ],
             axis=0,
         )
@@ -212,7 +213,7 @@
         + [
             pl.BlockSpec(memory_space=pltpu.SMEM),
             pl.BlockSpec((step_coils, height, width), per_coil),
-            pl.BlockSpec((step_coils, 2, width // 2, height), lambda c: (c, 0, 0, 0)),
+            pl.BlockSpec((step_coils, height, width), per_coil),
             pl.BlockSpec((step_coils, 1, height), per_coil),
             pl.BlockSpec((width, width), whole),
             pl.BlockSpec((width, width), whole),
@@ -253,8 +254,7 @@
     pieces = [own_rows] + [lax.ppermute(own_rows, "coil", shifted(groups, step)) for step in range(1, groups)]
     sampled = masks[0].astype(jnp.float32)[:, None, :]
     place = jnp.reshape(me_c, (1,)).astype(jnp.int32)
-    coils_here = kdata.shape[1]
-    measured = jnp.transpose(kdata[0].reshape(coils_here, width_y, 2, width_x), (0, 2, 3, 1))
+    measured = kdata[0]
     own_total, *outgoing = coil_chain(
         pieces, place, maps, measured, sampled, forward_x, adjoint_x, table_y
     )

time: 49.1 us -> 46.7 us (0.951)
  local copies, waits for them, and re-layouts: 6.77 us -> 2.84 us
  waiting for transfers between devices: 10.3 us -> 12.6 us
  starting transfers between devices: 16.4 us -> 15 us
  other arithmetic: 6.32 us -> 7.02 us
    unnamed x30 -> x27, local copies, waits for them, and re-layouts: 5.32 us -> 1.4 us
    ppermute x3, waiting for transfers between devices: 1.89 us -> 4.1 us  [on_device(): lax.ppermute(own_rows, 'coil', shifted(groups, step))]
    ppermute x3, starting transfers between devices: 3 us -> 1.78 us  [on_device(): lax.ppermute(own_rows, 'coil', shifted(groups, step))]
    ppermute x3, starting transfers between devices: 3.16 us -> 2.37 us  [on_device(): lax.ppermute(outgoing[step - 1], 'coil', shifted(groups, step))]
    convert_element_type x1, other arithmetic: 0.01 us -> 0.7 us  [on_device(): sampled = masks[0].astype(jnp.float32)[:, None, :]]
    ppermute x6, starting transfers between devices: 10.2 us -> 10.9 us  [exchange_blocks(): pieces.append(lax.ppermute(outgoing, axis, shifted(count, step)))]
  transfers between devices with their start and end apart: 12 -> 12, of which waited for: 8 -> 9; matrix products, arithmetic and copies ran while one was open for 11% -> 4% of each run, Pallas kernels for 0% -> 0%
where the time goes in v19:
time: 46.7 us; the launch traced here: 46.4 us
  starting transfers between devices  15 us (32%)
  waiting for transfers between devices  12.6 us (27%)
  Pallas kernels  8.74 us (19%)
  other arithmetic  7.02 us (15%)
  local copies, waits for them, and re-layouts  2.84 us (6%)
    ppermute x6, starting transfers between devices, exchange_blocks(): pieces.append(lax.ppermute(outgoing, axis, shifted(count, step)))  10.9 us
    pallas_call x1, Pallas kernels, coil_chain(): pl.pallas_call(coil_chain_kernel, out_shape=(jax.ShapeDtypeStruct((rows,...  8.74 us
    ppermute x6, waiting for transfers between devices, exchange_blocks(): pieces.append(lax.ppermute(outgoing, axis, shifted(count, step)))  5.63 us
    ppermute x3, waiting for transfers between devices, on_device(): lax.ppermute(own_rows, 'coil', shifted(groups, step))  4.1 us
    ppermute x3, waiting for transfers between devices, on_device(): lax.ppermute(outgoing[step - 1], 'coil', shifted(groups, step))  2.86 us
    ppermute x3, starting transfers between devices, on_device(): lax.ppermute(outgoing[step - 1], 'coil', shifted(groups, step))  2.37 us
    reduce_sum x1, other arithmetic, on_device(): jnp.sum(mixing[:, :, :, :, None, None] * factors[None, None], axis=(2, 3))  2.29 us
    ppermute x3, starting transfers between devices, on_device(): lax.ppermute(own_rows, 'coil', shifted(groups, step))  1.78 us
  transfers between devices with their start and end apart: 12, of which 9 were waited for; matrix products, arithmetic and copies ran while one was open for 4% of the time, Pallas kernels for 0%

profile of v19, /device:TPU:0, one launch (start us, length us, event | category | flops | bytes accessed | tf_op | source)
XLA Modules:
  0.0 46.4 jit_solution(15695940447747747337)
XLA Ops:
  0.0 0.7 %fusion.8 = f32[4,1,16]{2,0,1:T(4,128)S(1)} fusion(f32[2,4,16]{2,1,0:T(4,128)} %param.9), kind=kLoop, calls=%fused_computation.76 | loop fusion | flops 64 | bytes 512 | tf_op jit(solution)/shard_map/neg | solution.py:243
  0.7 0.7 %slice_bitcast_fusion.10 = (f32[16,4,1]{0,1,2:T(4,128)S(1)}, f32[4,1,16]{2,0,1:T(4,128)S(1)}, f32[4,1,16]{2,0,1:T(4,128)S(1)}, f32[16,4,1]{0,1,2:T(4,128)S(1)}) fusion(f32[2,4,16]{2,1,0:T(4,128)} %param.9), kind=kLoop, calls=%fused_computation.66 | loop fusion | bytes 1536 | tf_op jit(solution)/shard_map/stack | solution.py:269
  1.4 2.3 %multiply_reduce_fusion = bf16[4,2,64,64]{3,2,1,0:T(8,128)(2,1)S(1)} fusion(f32[2,16,64,64]{3,2,1,0:T(8,128)} %param.8, f32[4,1,2,16]{3,2,0,1:T(2,128)S(1)} %get-tuple-element.45, f32[4,1,2,16]{3,2,0,1:T(2,128)S(1)} %get-tuple-element.46), kind=kLoop, calls=%fused_computation | loop fusion | flops 2064640 | bytes 590848 | tf_op jit(solution)/shard_map/reduce_sum | solution.py:245
  3.7 3.1 %collective-permute-start.2 = (bf16[2,64,64]{2,1,0:T(8,128)(2,1)S(1)}, bf16[2,64,64]{2,1,0:T(8,128)(2,1)S(1)}, u32[]{:S(2)}, u32[]{:S(2)}) collective-permute-start(bf16[2,64,64]{2,1,0:T(8,128)(2,1)S(1)} %get-tuple-element.25), channel_id=1, source_target_pairs={{0,4},{4,8},{8,12},{12,0},{1,5},{5,9},{9,13},{13,1},{2,6},{6,10},{... | collective-permute-start | bytes 49160 | tf_op jit(solution)/shard_map/ppermute | solution.py:85
  6.8 2.6 %collective-permute-start.1 = (bf16[2,64,64]{2,1,0:T(8,128)(2,1)S(1)}, bf16[2,64,64]{2,1,0:T(8,128)(2,1)S(1)}, u32[]{:S(2)}, u32[]{:S(2)}) collective-permute-start(bf16[2,64,64]{2,1,0:T(8,128)(2,1)S(1)} %get-tuple-element.26), channel_id=1, source_target_pairs={{0,8},{4,12},{8,0},{12,4},{1,9},{5,13},{9,1},{13,5},{2,10},{6,14},... | collective-permute-start | bytes 49160 | tf_op jit(solution)/shard_map/ppermute | solution.py:85
  9.4 1.3 %collective-permute-start = (bf16[2,64,64]{2,1,0:T(8,128)(2,1)S(1)}, bf16[2,64,64]{2,1,0:T(8,128)(2,1)S(1)}, u32[]{:S(2)}, u32[]{:S(2)}) collective-permute-start(bf16[2,64,64]{2,1,0:T(8,128)(2,1)S(1)} %get-tuple-element.27), channel_id=1, source_target_pairs={{0,12},{4,0},{8,4},{12,8},{1,13},{5,1},{9,5},{13,9},{2,14},{6,2},{... | collective-permute-start | bytes 49160 | tf_op jit(solution)/shard_map/ppermute | solution.py:85
  10.7 0.7 %fusion = f32[16,4,1]{0,1,2:T(4,128)S(1)} fusion(f32[2,4,16]{2,1,0:T(4,128)} %param.9), kind=kLoop, calls=%fused_computation.63 | loop fusion | flops 64 | bytes 512 | tf_op jit(solution)/shard_map/stack | solution.py:269
  11.4 0.7 %convert_element_type.44 = f32[1,8,256]{2,1,0:T(8,128)S(1)} convert(s32[1,8,256]{2,1,0:T(8,128)} %param.12) | non-fusion elementwise | flops 2048 | bytes 16384 | tf_op jit(solution)/shard_map/convert_element_type | solution.py:255
  12.1 0.6 %copy.52 = f32[1,8,256]{2,0,1:T(1,128)} copy(f32[1,8,256]{2,1,0:T(8,128)S(1)} %convert_element_type.44) | data formatting | bytes 16384
  12.7 0.6 %collective-permute-done = bf16[2,64,64]{2,1,0:T(8,128)(2,1)S(1)} collective-permute-done((bf16[2,64,64]{2,1,0:T(8,128)(2,1)S(1)}, bf16[2,64,64]{2,1,0:T(8,128)(2,1)S(1)}, u32[]{:S(2)}, u32[]{:S(2)}) %collective-permute-start) | collective-permute-done | bytes 16416 | tf_op jit(solution)/shard_map/ppermute | solution.py:85
  13.8 1.6 %collective-permute-start.4 = (bf16[64,512]{1,0:T(8,128)(2,1)S(1)}, bf16[64,512]{1,0:T(8,128)(2,1)S(1)}, u32[]{:S(2)}, u32[]{:S(2)}) collective-permute-start(bf16[64,512]{1,0:T(8,128)(2,1)S(1)} %reshape.46.refs_0_), channel_id=1, source_target_pairs={{0,2},{1,3},{2,0},{3,1},{4,6},{5,7},{6,4},{7,5},{8,10},{9,11},{10,... | collective-permute-start | bytes 196616 | tf_op jit(solution)/shard_map/ppermute | solution.py:254
  15.7 3.7 %collective-permute-done.4.refs_2_ = bf16[64,512]{1,0:T(8,128)(2,1)S(1)} collective-permute-done((bf16[64,512]{1,0:T(8,128)(2,1)S(1)}, bf16[64,512]{1,0:T(8,128)(2,1)S(1)}, u32[]{:S(2)}, u32[]{:S(2)}) %collective-permute-start.4) | collective-permute-done | bytes 65568 | tf_op jit(solution)/shard_map/ppermute | solution.py:254
  20.2 8.7 %shard_map.82 = (f32[64,512]{1,0:T(8,128)}, bf16[64,512]{1,0:T(8,128)(2,1)}, bf16[64,512]{1,0:T(8,128)(2,1)}, bf16[64,512]{1,0:T(8,128)(2,1)}) custom-call(bf16[64,512]{1,0:T(8,128)(2,1)} %copy-done.1, bf16[64,512]{1,0:T(8,128)(2,1)} %copy-done.4, bf16[64,512]{1,0:T(8,128)(2,1)} %copy-done.3, bf16[64,512]{1,0:T(8,128)(2,1)} %copy-done.2, s32[1]{0:T(128)} %bitcast.24.refs_4_, ...), custom_call_target="tpu_custom_call" | custom-call | flops 4294967296 | bytes 4718592 | tf_op jit(solution)/shard_map/pallas_call | solution.py:207
  29.0 0.9 %collective-permute-start.7 = (bf16[64,512]{1,0:T(8,128)(2,1)}, bf16[64,512]{1,0:T(8,128)(2,1)S(1)}, u32[]{:S(2)}, u32[]{:S(2)}) collective-permute-start(bf16[64,512]{1,0:T(8,128)(2,1)} %get-tuple-element.11), channel_id=1, source_target_pairs={{0,2},{1,3},{2,0},{3,1},{4,6},{5,7},{6,4},{7,5},{8,10},{9,11},{10,... | collective-permute-start | bytes 196616 | tf_op jit(solution)/shard_map/ppermute | solution.py:263
  30.0 1.4 %collective-permute-start.8 = (bf16[64,512]{1,0:T(8,128)(2,1)}, bf16[64,512]{1,0:T(8,128)(2,1)S(1)}, u32[]{:S(2)}, u32[]{:S(2)}) collective-permute-start(bf16[64,512]{1,0:T(8,128)(2,1)} %get-tuple-element.12), channel_id=1, source_target_pairs={{0,3},{1,0},{2,1},{3,2},{4,7},{5,4},{6,5},{7,6},{8,11},{9,8},{10,9... | collective-permute-start | bytes 196616 | tf_op jit(solution)/shard_map/ppermute | solution.py:263
  31.4 1.6 %collective-permute-done.6 = bf16[64,512]{1,0:T(8,128)(2,1)S(1)} collective-permute-done((bf16[64,512]{1,0:T(8,128)(2,1)}, bf16[64,512]{1,0:T(8,128)(2,1)S(1)}, u32[]{:S(2)}, u32[]{:S(2)}) %collective-permute-start.6) | collective-permute-done | bytes 65568 | tf_op jit(solution)/shard_map/ppermute | solution.py:263
  33.0 1.2 %collective-permute-done.7 = bf16[64,512]{1,0:T(8,128)(2,1)S(1)} collective-permute-done((bf16[64,512]{1,0:T(8,128)(2,1)}, bf16[64,512]{1,0:T(8,128)(2,1)S(1)}, u32[]{:S(2)}, u32[]{:S(2)}) %collective-permute-start.7) | collective-permute-done | bytes 65568 | tf_op jit(solution)/shard_map/ppermute | solution.py:263
  34.2 0.9 %add_convert_fusion = bf16[64,512]{1,0:T(8,128)(2,1)S(1)} fusion(bf16[64,512]{1,0:T(8,128)(2,1)S(1)} %collective-permute-done.8, bf16[64,512]{1,0:T(8,128)(2,1)S(1)} %collective-permute-done.7, f32[64,512]{1,0:T(8,128)} %get-tuple-element.9, bf16[64,512]{1,0:T(8,128)(2,1)S(1)} %collective-permute-done.6), kind=kLoop, calls=%fused_computation.3 | loop fusion | flops 229376 | bytes 393216 | tf_op jit(solution)/shard_map/convert_element_type | solution.py:266
  35.6 3.2 %collective-permute-start.9 = (bf16[64,2,64]{2,0,1:T(8,128)(2,1)S(1)}, bf16[64,2,64]{2,0,1:T(8,128)(2,1)S(1)}, u32[]{:S(2)}, u32[]{:S(2)}) collective-permute-start(bf16[64,2,64]{2,0,1:T(8,128)(2,1)S(1)} %bitcast.103), channel_id=1, source_target_pairs={{0,12},{4,0},{8,4},{12,8},{1,13},{5,1},{9,5},{13,9},{2,14},{6,2},{... | collective-permute-start | bytes 49160 | tf_op jit(solution)/shard_map/ppermute | solution.py:85
  38.9 0.6 %collective-permute-start.11 = (bf16[64,2,64]{2,0,1:T(8,128)(2,1)S(1)}, bf16[64,2,64]{2,0,1:T(8,128)(2,1)S(1)}, u32[]{:S(2)}, u32[]{:S(2)}) collective-permute-start(bf16[64,2,64]{2,0,1:T(8,128)(2,1)S(1)} %bitcast.101), channel_id=1, source_target_pairs={{0,4},{4,8},{8,12},{12,0},{1,5},{5,9},{9,13},{13,1},{2,6},{6,10},{... | collective-permute-start | bytes 49160 | tf_op jit(solution)/shard_map/ppermute | solution.py:85
  39.5 1.0 %collective-permute-done.9 = bf16[64,2,64]{2,0,1:T(8,128)(2,1)S(1)} collective-permute-done((bf16[64,2,64]{2,0,1:T(8,128)(2,1)S(1)}, bf16[64,2,64]{2,0,1:T(8,128)(2,1)S(1)}, u32[]{:S(2)}, u32[]{:S(2)}) %collective-permute-start.9) | collective-permute-done | bytes 16416 | tf_op jit(solution)/shard_map/ppermute | solution.py:85
  40.6 3.1 %collective-permute-done.10 = bf16[64,2,64]{2,0,1:T(8,128)(2,1)S(1)} collective-permute-done((bf16[64,2,64]{2,0,1:T(8,128)(2,1)S(1)}, bf16[64,2,64]{2,0,1:T(8,128)(2,1)S(1)}, u32[]{:S(2)}, u32[]{:S(2)}) %collective-permute-start.10) | collective-permute-done | bytes 16416 | tf_op jit(solution)/shard_map/ppermute | solution.py:85
  43.7 0.9 %collective-permute-done.11 = bf16[64,2,64]{2,0,1:T(8,128)(2,1)S(1)} collective-permute-done((bf16[64,2,64]{2,0,1:T(8,128)(2,1)S(1)}, bf16[64,2,64]{2,0,1:T(8,128)(2,1)S(1)}, u32[]{:S(2)}, u32[]{:S(2)}) %collective-permute-start.11) | collective-permute-done | bytes 16416 | tf_op jit(solution)/shard_map/ppermute | solution.py:85
  44.7 1.7 %multiply_subtract_fusion = f32[2,16,64,64]{3,2,1,0:T(8,128)} fusion(f32[2,16,64,64]{3,2,1,0:T(8,128)S(1)} %copy-done, f32[64,64]{1,0:T(8,128)S(1)} %get-tuple-element.14, f32[2,16]{1,0:T(2,128)S(1)} %bitcast.111, f32[64,64]{1,0:T(8,128)S(1)} %get-tuple-element.15, f32[2,16]{1,0:T(2,128)S(1)} %bitcast.112, f32[64,64]{1,0:T(8,128)S(1)} %get-tuple-element.16, ...), kind=kLoop, calls=%fused_computation.1 | loop fusion | flops 2228224 | bytes 1180672 | tf_op jit(solution)/shard_map/sub | solution.py:276
  (49 shorter events, 2.2 us)
Async XLA Ops:
  3.7 9.6 %collective-permute-start.2 = (bf16[2,64,64]{2,1,0:T(8,128)(2,1)S(1)}, bf16[2,64,64]{2,1,0:T(8,128)(2,1)S(1)}, u32[]{:S(2)}, u32[]{:S(2)}) collective-permute-start(bf16[2,64,64]{2,1,0:T(8,128)(2,1)S(1)} %get-tuple-element.25), channel_id=1, source_target_pairs={{0,4},{4,8},{8,12},{12,0},{1,5},{5,9},{9,13},{13,1},{2,6},{6,10},{... | collective-permute-start | bytes 49160 | tf_op jit(solution)/shard_map/ppermute | solution.py:85
  6.8 6.5 %collective-permute-start.1 = (bf16[2,64,64]{2,1,0:T(8,128)(2,1)S(1)}, bf16[2,64,64]{2,1,0:T(8,128)(2,1)S(1)}, u32[]{:S(2)}, u32[]{:S(2)}) collective-permute-start(bf16[2,64,64]{2,1,0:T(8,128)(2,1)S(1)} %get-tuple-element.26), channel_id=1, source_target_pairs={{0,8},{4,12},{8,0},{12,4},{1,9},{5,13},{9,1},{13,5},{2,10},{6,14},... | collective-permute-start | bytes 49160 | tf_op jit(solution)/shard_map/ppermute | solution.py:85
  9.4 3.9 %collective-permute-start = (bf16[2,64,64]{2,1,0:T(8,128)(2,1)S(1)}, bf16[2,64,64]{2,1,0:T(8,128)(2,1)S(1)}, u32[]{:S(2)}, u32[]{:S(2)}) collective-permute-start(bf16[2,64,64]{2,1,0:T(8,128)(2,1)S(1)} %get-tuple-element.27), channel_id=1, source_target_pairs={{0,12},{4,0},{8,4},{12,8},{1,13},{5,1},{9,5},{13,9},{2,14},{6,2},{... | collective-permute-start | bytes 49160 | tf_op jit(solution)/shard_map/ppermute | solution.py:85
  13.7 5.9 %copy-start.1 = (bf16[64,512]{1,0:T(8,128)(2,1)}, bf16[64,512]{1,0:T(8,128)(2,1)S(1)}, u32[]{:S(2)}) copy-start(bf16[64,512]{1,0:T(8,128)(2,1)S(1)} %reshape.46.refs_0_) | copy-start | bytes 196612
  13.7 2.0 %collective-permute-start.5 = (bf16[64,512]{1,0:T(8,128)(2,1)S(1)}, bf16[64,512]{1,0:T(8,128)(2,1)S(1)}, u32[]{:S(2)}, u32[]{:S(2)}) collective-permute-start(bf16[64,512]{1,0:T(8,128)(2,1)S(1)} %reshape.46.refs_0_), channel_id=1, source_target_pairs={{0,3},{1,0},{2,1},{3,2},{4,7},{5,4},{6,5},{7,6},{8,11},{9,8},{10,9... | collective-permute-start | bytes 196616 | tf_op jit(solution)/shard_map/ppermute | solution.py:254
  13.8 5.6 %collective-permute-start.4 = (bf16[64,512]{1,0:T(8,128)(2,1)S(1)}, bf16[64,512]{1,0:T(8,128)(2,1)S(1)}, u32[]{:S(2)}, u32[]{:S(2)}) collective-permute-start(bf16[64,512]{1,0:T(8,128)(2,1)S(1)} %reshape.46.refs_0_), channel_id=1, source_target_pairs={{0,2},{1,3},{2,0},{3,1},{4,6},{5,7},{6,4},{7,5},{8,10},{9,11},{10,... | collective-permute-start | bytes 196616 | tf_op jit(solution)/shard_map/ppermute | solution.py:254
  15.3 4.3 %collective-permute-start.3 = (bf16[64,512]{1,0:T(8,128)(2,1)S(1)}, bf16[64,512]{1,0:T(8,128)(2,1)S(1)}, u32[]{:S(2)}, u32[]{:S(2)}) collective-permute-start(bf16[64,512]{1,0:T(8,128)(2,1)S(1)} %reshape.46.refs_0_), channel_id=1, source_target_pairs={{0,1},{1,2},{2,3},{3,0},{4,5},{5,6},{6,7},{7,4},{8,9},{9,10},{10,1... | collective-permute-start | bytes 196616 | tf_op jit(solution)/shard_map/ppermute | solution.py:254
  15.7 3.9 %copy-start.2 = (bf16[64,512]{1,0:T(8,128)(2,1)}, bf16[64,512]{1,0:T(8,128)(2,1)S(1)}, u32[]{:S(2)}) copy-start(bf16[64,512]{1,0:T(8,128)(2,1)S(1)} %collective-permute-done.5.refs_3_) | copy-start | bytes 196612
  19.4 0.6 %copy-start.3 = (bf16[64,512]{1,0:T(8,128)(2,1)}, bf16[64,512]{1,0:T(8,128)(2,1)S(1)}, u32[]{:S(2)}) copy-start(bf16[64,512]{1,0:T(8,128)(2,1)S(1)} %collective-permute-done.4.refs_2_) | copy-start | bytes 196612
  19.6 0.6 %copy-start.4 = (bf16[64,512]{1,0:T(8,128)(2,1)}, bf16[64,512]{1,0:T(8,128)(2,1)S(1)}, u32[]{:S(2)}) copy-start(bf16[64,512]{1,0:T(8,128)(2,1)S(1)} %collective-permute-done.3.refs_1_) | copy-start | bytes 196612
  29.0 15.7 %copy-start = (f32[2,16,64,64]{3,2,1,0:T(8,128)S(1)}, f32[2,16,64,64]{3,2,1,0:T(8,128)}, u32[]{:S(2)}) copy-start(f32[2,16,64,64]{3,2,1,0:T(8,128)} %param.8) | copy-start | bytes 1572868
  29.0 4.0 %collective-permute-start.6 = (bf16[64,512]{1,0:T(8,128)(2,1)}, bf16[64,512]{1,0:T(8,128)(2,1)S(1)}, u32[]{:S(2)}, u32[]{:S(2)}) collective-permute-start(bf16[64,512]{1,0:T(8,128)(2,1)} %get-tuple-element.10), channel_id=1, source_target_pairs={{0,1},{1,2},{2,3},{3,0},{4,5},{5,6},{6,7},{7,4},{8,9},{9,10},{10,1... | collective-permute-start | bytes 196616 | tf_op jit(solution)/shard_map/ppermute | solution.py:263
  29.0 5.2 %collective-permute-start.7 = (bf16[64,512]{1,0:T(8,128)(2,1)}, bf16[64,512]{1,0:T(8,128)(2,1)S(1)}, u32[]{:S(2)}, u32[]{:S(2)}) collective-permute-start(bf16[64,512]{1,0:T(8,128)(2,1)} %get-tuple-element.11), channel_id=1, source_target_pairs={{0,2},{1,3},{2,0},{3,1},{4,6},{5,7},{6,4},{7,5},{8,10},{9,11},{10,... | collective-permute-start | bytes 196616 | tf_op jit(solution)/shard_map/ppermute | solution.py:263
  30.0 4.3 %collective-permute-start.8 = (bf16[64,512]{1,0:T(8,128)(2,1)}, bf16[64,512]{1,0:T(8,128)(2,1)S(1)}, u32[]{:S(2)}, u32[]{:S(2)}) collective-permute-start(bf16[64,512]{1,0:T(8,128)(2,1)} %get-tuple-element.12), channel_id=1, source_target_pairs={{0,3},{1,0},{2,1},{3,2},{4,7},{5,4},{6,5},{7,6},{8,11},{9,8},{10,9... | collective-permute-start | bytes 196616 | tf_op jit(solution)/shard_map/ppermute | solution.py:263
  35.6 4.9 %collective-permute-start.9 = (bf16[64,2,64]{2,0,1:T(8,128)(2,1)S(1)}, bf16[64,2,64]{2,0,1:T(8,128)(2,1)S(1)}, u32[]{:S(2)}, u32[]{:S(2)}) collective-permute-start(bf16[64,2,64]{2,0,1:T(8,128)(2,1)S(1)} %bitcast.103), channel_id=1, source_target_pairs={{0,12},{4,0},{8,4},{12,8},{1,13},{5,1},{9,5},{13,9},{2,14},{6,2},{... | collective-permute-start | bytes 49160 | tf_op jit(solution)/shard_map/ppermute | solution.py:85
  38.9 4.8 %collective-permute-start.10 = (bf16[64,2,64]{2,0,1:T(8,128)(2,1)S(1)}, bf16[64,2,64]{2,0,1:T(8,128)(2,1)S(1)}, u32[]{:S(2)}, u32[]{:S(2)}) collective-permute-start(bf16[64,2,64]{2,0,1:T(8,128)(2,1)S(1)} %bitcast.102), channel_id=1, source_target_pairs={{0,8},{4,12},{8,0},{12,4},{1,9},{5,13},{9,1},{13,5},{2,10},{6,14},... | collective-permute-start | bytes 49160 | tf_op jit(solution)/shard_map/ppermute | solution.py:85
  38.9 5.7 %collective-permute-start.11 = (bf16[64,2,64]{2,0,1:T(8,128)(2,1)S(1)}, bf16[64,2,64]{2,0,1:T(8,128)(2,1)S(1)}, u32[]{:S(2)}, u32[]{:S(2)}) collective-permute-start(bf16[64,2,64]{2,0,1:T(8,128)(2,1)S(1)} %bitcast.101), channel_id=1, source_target_pairs={{0,4},{4,8},{8,12},{12,0},{1,5},{5,9},{9,13},{13,1},{2,6},{6,10},{... | collective-permute-start | bytes 49160 | tf_op jit(solution)/shard_map/ppermute | solution.py:85

commit v20 on v19

--- a/solution.py
+++ b/solution.py
@@ -127,7 +127,8 @@
         parts = jnp.dot(turned, table, preferred_element_type=jnp.float32)
         kspace_re = parts[:half_width, :height] - parts[half_width:, height:]
         kspace_im = parts[:half_width, height:] + parts[half_width:, :height]
-        sampled = sampled_ref[coil_index]
+        row = pl.program_id(0) * coils + coil_index
+        sampled = sampled_ref[pl.ds(row, 1), :].astype(jnp.float32)
         measured = measured_ref[coil_index].astype(jnp.float32)
         residual = jnp.concatenate(
             [
@@ -214,7 +215,7 @@
             pl.BlockSpec(memory_space=pltpu.SMEM),
             pl.BlockSpec((step_coils, height, width), per_coil),
             pl.BlockSpec((step_coils, height, width), per_coil),
-            pl.BlockSpec((step_coils, 1, height), per_coil),
+            pl.BlockSpec((coils, height), whole),
             pl.BlockSpec((width, width), whole),
             pl.BlockSpec((width, width), whole),
             pl.BlockSpec((height, 2 * height), whole),
@@ -239,12 +240,12 @@
     table_y = jnp.asarray(np.concatenate([table_y_re, table_y_im], axis=1))
     time_re = temporal[0]
     time_im = temporal[1]
-    mixing = jnp.stack(
-        [jnp.stack([time_re, -time_im], axis=1), jnp.stack([time_im, time_re], axis=1)], axis=1
-    )
+    sign = jnp.asarray(np.array([[1.0, -1.0], [1.0, 1.0]], np.float32))
+    mixing = jnp.stack([temporal, temporal[::-1]]) * sign[:, :, None, None]
     images = jnp.sum(
-        mixing[:, :, :, :, None, None] * factors[None, None], axis=(2, 3)
-    ).astype(jnp.bfloat16)
+        mixing[:, :, :, :, None, None] * factors[None, :, None], axis=(1, 3)
+    )
+    images = jnp.transpose(images, (1, 0, 2, 3)).astype(jnp.bfloat16)
     frames_here = images.shape[0]
     width_own = images.shape[3]
     pieces_x = exchange_blocks(images, "frame")
@@ -252,7 +253,7 @@
     groups = lax.axis_size("coil")
     me_c = lax.axis_index("coil")
     pieces = [own_rows] + [lax.ppermute(own_rows, "coil", shifted(groups, step)) for step in range(1, groups)]
-    sampled = masks[0].astype(jnp.float32)[:, None, :]
+    sampled = masks[0]
     place = jnp.reshape(me_c, (1,)).astype(jnp.int32)
     measured = kdata[0]
     own_total, *outgoing = coil_chain(
@@ -265,8 +266,9 @@
         own_share.reshape(rows_own, 2, frames_here, width_own), (2, 0, 1, 3)
     ).astype(jnp.bfloat16)
     returned = exchange_blocks(outgoing, "frame").astype(jnp.float32)
+    late = lax.optimization_barrier(temporal)
     weights = jnp.stack(
-        [jnp.stack([time_re.T, time_im.T], axis=2), jnp.stack([-time_im.T, time_re.T], axis=2)], axis=0
+        [jnp.stack([late[0].T, late[1].T], axis=2), jnp.stack([-late[1].T, late[0].T], axis=2)], axis=0
     )
     gradient = None
     for frame in range(returned.shape[0]):

time: 46.7 us -> 46.4 us (level)
  other arithmetic: 7.02 us -> 6.34 us
  waiting for transfers between devices: 12.6 us -> 13.2 us
    mul x0 -> x1, other arithmetic: none -> 0.77 us  [on_device(): mixing = jnp.stack([temporal, temporal[::-1]]) * sign[:, :, None, None]]
    convert_element_type x1 -> x0, other arithmetic: 0.7 us -> none  [on_device(): sampled = masks[0].astype(jnp.float32)[:, None, :]]
    neg x1 -> x0, other arithmetic: 0.68 us -> none  [on_device(): -time_im]
    another operation x3, local copies, waits for them, and re-layouts: 0.99 us -> 1.67 us  [the longest x1 0.7 us: on_device(): jnp.stack([late[0].T, late[1].T], axis=2)]
    ppermute x6, waiting for transfers between devices: 5.63 us -> 6.23 us  [exchange_blocks(): pieces.append(lax.ppermute(outgoing, axis, shifted(count, step)))]
    unnamed x27, local copies, waits for them, and re-layouts: 1.4 us -> 0.8 us
  transfers between devices with their start and end apart: 12 -> 12, of which waited for: 9 -> 9; matrix products, arithmetic and copies ran while one was open for 4% -> 3% of each run, Pallas kernels for 0% -> 0%
where the time goes in v20:
time: 46.4 us; the launch traced here: 46.1 us
  starting transfers between devices  15 us (32%)
  waiting for transfers between devices  13.2 us (28%)
  Pallas kernels  8.42 us (18%)
  other arithmetic  6.34 us (14%)
  local copies, waits for them, and re-layouts  2.92 us (6%)
    ppermute x6, starting transfers between devices, exchange_blocks(): pieces.append(lax.ppermute(outgoing, axis, shifted(count, step)))  10.9 us
    pallas_call x1, Pallas kernels, coil_chain(): pl.pallas_call(coil_chain_kernel, out_shape=(jax.ShapeDtypeStruct((rows,...  8.42 us
    ppermute x6, waiting for transfers between devices, exchange_blocks(): pieces.append(lax.ppermute(outgoing, axis, shifted(count, step)))  6.23 us
    ppermute x3, waiting for transfers between devices, on_device(): lax.ppermute(own_rows, 'coil', shifted(groups, step))  4.1 us
    ppermute x3, waiting for transfers between devices, on_device(): lax.ppermute(outgoing[step - 1], 'coil', shifted(groups, step))  2.85 us
    ppermute x3, starting transfers between devices, on_device(): lax.ppermute(outgoing[step - 1], 'coil', shifted(groups, step))  2.38 us
    reduce_sum x1, other arithmetic, on_device(): jnp.sum(mixing[:, :, :, :, None, None] * factors[None, :, None], axis=(1,...  2.23 us
    ppermute x3, starting transfers between devices, on_device(): lax.ppermute(own_rows, 'coil', shifted(groups, step))  1.78 us
  transfers between devices with their start and end apart: 12, of which 9 were waited for; matrix products, arithmetic and copies ran while one was open for 3% of the time, Pallas kernels for 0%

profile of v20, /device:TPU:0, one launch (start us, length us, event | category | flops | bytes accessed | tf_op | source)
XLA Modules:
  0.0 46.1 jit_solution(5020648806017991758)
XLA Ops:
  0.0 0.7 %reverse_bitcast_fusion = f32[1,2,4,16]{3,2,1,0:T(4,128)S(1)} fusion(f32[2,4,16]{2,1,0:T(4,128)} %param.10), kind=kLoop, calls=%fused_computation.53 | loop fusion | bytes 1024 | tf_op jit(solution)/shard_map/stack | solution.py:244
  0.7 0.8 %maximum_multiply_fusion = f32[2,2,4,16]{3,2,1,0:T(4,128)S(1)} fusion(f32[1,2,4,16]{3,2,1,0:T(4,128)S(1)} %reverse_bitcast_fusion, f32[1,2,4,16]{3,2,1,0:T(4,128)} %bitcast.95, f32[2,2]{1,0:T(2,128)} %constant.83.clone), kind=kLoop, calls=%fused_computation.50 | loop fusion | flops 512 | bytes 2064 | tf_op jit(solution)/shard_map/mul | solution.py:244
  1.5 2.2 %multiply_reduce_fusion = bf16[2,4,64,64]{3,2,1,0:T(8,128)(2,1)S(1)} fusion(f32[2,16,64,64]{3,2,1,0:T(8,128)} %param.9, f32[2,2,4,16]{3,2,1,0:T(4,128)S(1)} %maximum_multiply_fusion), kind=kLoop, calls=%fused_computation | loop fusion | flops 2064384 | bytes 590848 | tf_op jit(solution)/shard_map/reduce_sum | solution.py:245
  3.7 3.1 %collective-permute-start.2 = (bf16[2,64,64]{2,1,0:T(8,128)(2,1)S(1)}, bf16[2,64,64]{2,1,0:T(8,128)(2,1)S(1)}, u32[]{:S(2)}, u32[]{:S(2)}) collective-permute-start(bf16[2,64,64]{2,1,0:T(8,128)(2,1)S(1)} %get-tuple-element.25), channel_id=1, source_target_pairs={{0,4},{4,8},{8,12},{12,0},{1,5},{5,9},{9,13},{13,1},{2,6},{6,10},{... | collective-permute-start | bytes 49160 | tf_op jit(solution)/shard_map/ppermute | solution.py:85
  6.8 2.6 %collective-permute-start.1 = (bf16[2,64,64]{2,1,0:T(8,128)(2,1)S(1)}, bf16[2,64,64]{2,1,0:T(8,128)(2,1)S(1)}, u32[]{:S(2)}, u32[]{:S(2)}) collective-permute-start(bf16[2,64,64]{2,1,0:T(8,128)(2,1)S(1)} %get-tuple-element.26), channel_id=1, source_target_pairs={{0,8},{4,12},{8,0},{12,4},{1,9},{5,13},{9,1},{13,5},{2,10},{6,14},... | collective-permute-start | bytes 49160 | tf_op jit(solution)/shard_map/ppermute | solution.py:85
  9.4 1.3 %collective-permute-start = (bf16[2,64,64]{2,1,0:T(8,128)(2,1)S(1)}, bf16[2,64,64]{2,1,0:T(8,128)(2,1)S(1)}, u32[]{:S(2)}, u32[]{:S(2)}) collective-permute-start(bf16[2,64,64]{2,1,0:T(8,128)(2,1)S(1)} %get-tuple-element.27), channel_id=1, source_target_pairs={{0,12},{4,0},{8,4},{12,8},{1,13},{5,1},{9,5},{13,9},{2,14},{6,2},{... | collective-permute-start | bytes 49160 | tf_op jit(solution)/shard_map/ppermute | solution.py:85
  10.7 0.7 %fusion = f32[16,4,1]{0,1,2:T(4,128)S(1)} fusion(f32[2,4,16]{2,1,0:T(4,128)} %param.10), kind=kLoop, calls=%fused_computation.60 | loop fusion | flops 64 | bytes 512 | tf_op jit(solution)/shard_map/stack | solution.py:271
  11.4 0.7 %slice_bitcast_fusion.9 = (f32[16,4,1]{0,1,2:T(4,128)S(1)}, f32[16,4,1]{0,1,2:T(4,128)S(1)}) fusion(f32[2,4,16]{2,1,0:T(4,128)} %param.10), kind=kLoop, calls=%fused_computation.61 | loop fusion | bytes 1024 | tf_op jit(solution)/shard_map/stack | solution.py:271
  12.1 1.2 %collective-permute-done = bf16[2,64,64]{2,1,0:T(8,128)(2,1)S(1)} collective-permute-done((bf16[2,64,64]{2,1,0:T(8,128)(2,1)S(1)}, bf16[2,64,64]{2,1,0:T(8,128)(2,1)S(1)}, u32[]{:S(2)}, u32[]{:S(2)}) %collective-permute-start) | collective-permute-done | bytes 16416 | tf_op jit(solution)/shard_map/ppermute | solution.py:85
  13.8 1.6 %collective-permute-start.4 = (bf16[64,512]{1,0:T(8,128)(2,1)S(1)}, bf16[64,512]{1,0:T(8,128)(2,1)S(1)}, u32[]{:S(2)}, u32[]{:S(2)}) collective-permute-start(bf16[64,512]{1,0:T(8,128)(2,1)S(1)} %reshape.49.refs_0_), channel_id=1, source_target_pairs={{0,2},{1,3},{2,0},{3,1},{4,6},{5,7},{6,4},{7,5},{8,10},{9,11},{10,... | collective-permute-start | bytes 196616 | tf_op jit(solution)/shard_map/ppermute | solution.py:255
  15.7 3.7 %collective-permute-done.4.refs_2_ = bf16[64,512]{1,0:T(8,128)(2,1)S(1)} collective-permute-done((bf16[64,512]{1,0:T(8,128)(2,1)S(1)}, bf16[64,512]{1,0:T(8,128)(2,1)S(1)}, u32[]{:S(2)}, u32[]{:S(2)}) %collective-permute-start.4) | collective-permute-done | bytes 65568 | tf_op jit(solution)/shard_map/ppermute | solution.py:255
  19.6 0.4 copy-done.3
  20.2 8.4 %shard_map.91 = (f32[64,512]{1,0:T(8,128)}, bf16[64,512]{1,0:T(8,128)(2,1)}, bf16[64,512]{1,0:T(8,128)(2,1)}, bf16[64,512]{1,0:T(8,128)(2,1)}) custom-call(bf16[64,512]{1,0:T(8,128)(2,1)} %copy-done.1, bf16[64,512]{1,0:T(8,128)(2,1)} %copy-done.4, bf16[64,512]{1,0:T(8,128)(2,1)} %copy-done.3, bf16[64,512]{1,0:T(8,128)(2,1)} %copy-done.2, s32[1]{0:T(128)} %bitcast.23.refs_4_, ...), custom_call_target="tpu_custom_call" | custom-call | flops 4294967296 | bytes 4718592 | tf_op jit(solution)/shard_map/pallas_call | solution.py:208
  28.7 0.9 %collective-permute-start.7 = (bf16[64,512]{1,0:T(8,128)(2,1)}, bf16[64,512]{1,0:T(8,128)(2,1)S(1)}, u32[]{:S(2)}, u32[]{:S(2)}) collective-permute-start(bf16[64,512]{1,0:T(8,128)(2,1)} %get-tuple-element.11), channel_id=1, source_target_pairs={{0,2},{1,3},{2,0},{3,1},{4,6},{5,7},{6,4},{7,5},{8,10},{9,11},{10,... | collective-permute-start | bytes 196616 | tf_op jit(solution)/shard_map/ppermute | solution.py:264
  29.7 1.4 %collective-permute-start.8 = (bf16[64,512]{1,0:T(8,128)(2,1)}, bf16[64,512]{1,0:T(8,128)(2,1)S(1)}, u32[]{:S(2)}, u32[]{:S(2)}) collective-permute-start(bf16[64,512]{1,0:T(8,128)(2,1)} %get-tuple-element.12), channel_id=1, source_target_pairs={{0,3},{1,0},{2,1},{3,2},{4,7},{5,4},{6,5},{7,6},{8,11},{9,8},{10,9... | collective-permute-start | bytes 196616 | tf_op jit(solution)/shard_map/ppermute | solution.py:264
  31.1 1.6 %collective-permute-done.6 = bf16[64,512]{1,0:T(8,128)(2,1)S(1)} collective-permute-done((bf16[64,512]{1,0:T(8,128)(2,1)}, bf16[64,512]{1,0:T(8,128)(2,1)S(1)}, u32[]{:S(2)}, u32[]{:S(2)}) %collective-permute-start.6) | collective-permute-done | bytes 65568 | tf_op jit(solution)/shard_map/ppermute | solution.py:264
  32.7 1.2 %collective-permute-done.7 = bf16[64,512]{1,0:T(8,128)(2,1)S(1)} collective-permute-done((bf16[64,512]{1,0:T(8,128)(2,1)}, bf16[64,512]{1,0:T(8,128)(2,1)S(1)}, u32[]{:S(2)}, u32[]{:S(2)}) %collective-permute-start.7) | collective-permute-done | bytes 65568 | tf_op jit(solution)/shard_map/ppermute | solution.py:264
  33.9 0.9 %add_convert_fusion = bf16[64,512]{1,0:T(8,128)(2,1)S(1)} fusion(bf16[64,512]{1,0:T(8,128)(2,1)S(1)} %collective-permute-done.8, bf16[64,512]{1,0:T(8,128)(2,1)S(1)} %collective-permute-done.7, f32[64,512]{1,0:T(8,128)} %get-tuple-element.9, bf16[64,512]{1,0:T(8,128)(2,1)S(1)} %collective-permute-done.6), kind=kLoop, calls=%fused_computation.3 | loop fusion | flops 229376 | bytes 393216 | tf_op jit(solution)/shard_map/convert_element_type | solution.py:267
  35.3 3.2 %collective-permute-start.9 = (bf16[64,2,64]{2,0,1:T(8,128)(2,1)S(1)}, bf16[64,2,64]{2,0,1:T(8,128)(2,1)S(1)}, u32[]{:S(2)}, u32[]{:S(2)}) collective-permute-start(bf16[64,2,64]{2,0,1:T(8,128)(2,1)S(1)} %bitcast.98), channel_id=1, source_target_pairs={{0,12},{4,0},{8,4},{12,8},{1,13},{5,1},{9,5},{13,9},{2,14},{6,2},{... | collective-permute-start | bytes 49160 | tf_op jit(solution)/shard_map/ppermute | solution.py:85
  38.5 0.6 %collective-permute-start.11 = (bf16[64,2,64]{2,0,1:T(8,128)(2,1)S(1)}, bf16[64,2,64]{2,0,1:T(8,128)(2,1)S(1)}, u32[]{:S(2)}, u32[]{:S(2)}) collective-permute-start(bf16[64,2,64]{2,0,1:T(8,128)(2,1)S(1)} %bitcast.96), channel_id=1, source_target_pairs={{0,4},{4,8},{8,12},{12,0},{1,5},{5,9},{9,13},{13,1},{2,6},{6,10},{... | collective-permute-start | bytes 49160 | tf_op jit(solution)/shard_map/ppermute | solution.py:85
  39.2 1.0 %collective-permute-done.9 = bf16[64,2,64]{2,0,1:T(8,128)(2,1)S(1)} collective-permute-done((bf16[64,2,64]{2,0,1:T(8,128)(2,1)S(1)}, bf16[64,2,64]{2,0,1:T(8,128)(2,1)S(1)}, u32[]{:S(2)}, u32[]{:S(2)}) %collective-permute-start.9) | collective-permute-done | bytes 16416 | tf_op jit(solution)/shard_map/ppermute | solution.py:85
  40.2 3.1 %collective-permute-done.10 = bf16[64,2,64]{2,0,1:T(8,128)(2,1)S(1)} collective-permute-done((bf16[64,2,64]{2,0,1:T(8,128)(2,1)S(1)}, bf16[64,2,64]{2,0,1:T(8,128)(2,1)S(1)}, u32[]{:S(2)}, u32[]{:S(2)}) %collective-permute-start.10) | collective-permute-done | bytes 16416 | tf_op jit(solution)/shard_map/ppermute | solution.py:85
  43.4 0.9 %collective-permute-done.11 = bf16[64,2,64]{2,0,1:T(8,128)(2,1)S(1)} collective-permute-done((bf16[64,2,64]{2,0,1:T(8,128)(2,1)S(1)}, bf16[64,2,64]{2,0,1:T(8,128)(2,1)S(1)}, u32[]{:S(2)}, u32[]{:S(2)}) %collective-permute-start.11) | collective-permute-done | bytes 16416 | tf_op jit(solution)/shard_map/ppermute | solution.py:85
  44.4 1.7 %multiply_subtract_fusion = f32[2,16,64,64]{3,2,1,0:T(8,128)} fusion(f32[2,16,64,64]{3,2,1,0:T(8,128)S(1)} %copy-done, f32[64,64]{1,0:T(8,128)S(1)} %get-tuple-element.14, f32[2,16]{1,0:T(2,128)S(1)} %bitcast.105, f32[64,64]{1,0:T(8,128)S(1)} %get-tuple-element.15, f32[2,16]{1,0:T(2,128)S(1)} %bitcast.106, f32[64,64]{1,0:T(8,128)S(1)} %get-tuple-element.16, ...), kind=kLoop, calls=%fused_computation.1 | loop fusion | flops 2228224 | bytes 1180672 | tf_op jit(solution)/shard_map/sub | solution.py:278
  (47 shorter events, 1.8 us)
Async XLA Ops:
  3.7 9.6 %collective-permute-start.2 = (bf16[2,64,64]{2,1,0:T(8,128)(2,1)S(1)}, bf16[2,64,64]{2,1,0:T(8,128)(2,1)S(1)}, u32[]{:S(2)}, u32[]{:S(2)}) collective-permute-start(bf16[2,64,64]{2,1,0:T(8,128)(2,1)S(1)} %get-tuple-element.25), channel_id=1, source_target_pairs={{0,4},{4,8},{8,12},{12,0},{1,5},{5,9},{9,13},{13,1},{2,6},{6,10},{... | collective-permute-start | bytes 49160 | tf_op jit(solution)/shard_map/ppermute | solution.py:85
  6.8 6.5 %collective-permute-start.1 = (bf16[2,64,64]{2,1,0:T(8,128)(2,1)S(1)}, bf16[2,64,64]{2,1,0:T(8,128)(2,1)S(1)}, u32[]{:S(2)}, u32[]{:S(2)}) collective-permute-start(bf16[2,64,64]{2,1,0:T(8,128)(2,1)S(1)} %get-tuple-element.26), channel_id=1, source_target_pairs={{0,8},{4,12},{8,0},{12,4},{1,9},{5,13},{9,1},{13,5},{2,10},{6,14},... | collective-permute-start | bytes 49160 | tf_op jit(solution)/shard_map/ppermute | solution.py:85
  9.4 3.9 %collective-permute-start = (bf16[2,64,64]{2,1,0:T(8,128)(2,1)S(1)}, bf16[2,64,64]{2,1,0:T(8,128)(2,1)S(1)}, u32[]{:S(2)}, u32[]{:S(2)}) collective-permute-start(bf16[2,64,64]{2,1,0:T(8,128)(2,1)S(1)} %get-tuple-element.27), channel_id=1, source_target_pairs={{0,12},{4,0},{8,4},{12,8},{1,13},{5,1},{9,5},{13,9},{2,14},{6,2},{... | collective-permute-start | bytes 49160 | tf_op jit(solution)/shard_map/ppermute | solution.py:85
  13.7 5.9 %copy-start.1 = (bf16[64,512]{1,0:T(8,128)(2,1)}, bf16[64,512]{1,0:T(8,128)(2,1)S(1)}, u32[]{:S(2)}) copy-start(bf16[64,512]{1,0:T(8,128)(2,1)S(1)} %reshape.49.refs_0_) | copy-start | bytes 196612
  13.7 2.0 %collective-permute-start.5 = (bf16[64,512]{1,0:T(8,128)(2,1)S(1)}, bf16[64,512]{1,0:T(8,128)(2,1)S(1)}, u32[]{:S(2)}, u32[]{:S(2)}) collective-permute-start(bf16[64,512]{1,0:T(8,128)(2,1)S(1)} %reshape.49.refs_0_), channel_id=1, source_target_pairs={{0,3},{1,0},{2,1},{3,2},{4,7},{5,4},{6,5},{7,6},{8,11},{9,8},{10,9... | collective-permute-start | bytes 196616 | tf_op jit(solution)/shard_map/ppermute | solution.py:255
  13.8 5.6 %collective-permute-start.4 = (bf16[64,512]{1,0:T(8,128)(2,1)S(1)}, bf16[64,512]{1,0:T(8,128)(2,1)S(1)}, u32[]{:S(2)}, u32[]{:S(2)}) collective-permute-start(bf16[64,512]{1,0:T(8,128)(2,1)S(1)} %reshape.49.refs_0_), channel_id=1, source_target_pairs={{0,2},{1,3},{2,0},{3,1},{4,6},{5,7},{6,4},{7,5},{8,10},{9,11},{10,... | collective-permute-start | bytes 196616 | tf_op jit(solution)/shard_map/ppermute | solution.py:255
  15.3 4.3 %collective-permute-start.3 = (bf16[64,512]{1,0:T(8,128)(2,1)S(1)}, bf16[64,512]{1,0:T(8,128)(2,1)S(1)}, u32[]{:S(2)}, u32[]{:S(2)}) collective-permute-start(bf16[64,512]{1,0:T(8,128)(2,1)S(1)} %reshape.49.refs_0_), channel_id=1, source_target_pairs={{0,1},{1,2},{2,3},{3,0},{4,5},{5,6},{6,7},{7,4},{8,9},{9,10},{10,1... | collective-permute-start | bytes 196616 | tf_op jit(solution)/shard_map/ppermute | solution.py:255
  15.7 3.9 %copy-start.2 = (bf16[64,512]{1,0:T(8,128)(2,1)}, bf16[64,512]{1,0:T(8,128)(2,1)S(1)}, u32[]{:S(2)}) copy-start(bf16[64,512]{1,0:T(8,128)(2,1)S(1)} %collective-permute-done.5.refs_3_) | copy-start | bytes 196612
  19.4 0.6 %copy-start.3 = (bf16[64,512]{1,0:T(8,128)(2,1)}, bf16[64,512]{1,0:T(8,128)(2,1)S(1)}, u32[]{:S(2)}) copy-start(bf16[64,512]{1,0:T(8,128)(2,1)S(1)} %collective-permute-done.4.refs_2_) | copy-start | bytes 196612
  19.6 0.6 %copy-start.4 = (bf16[64,512]{1,0:T(8,128)(2,1)}, bf16[64,512]{1,0:T(8,128)(2,1)S(1)}, u32[]{:S(2)}) copy-start(bf16[64,512]{1,0:T(8,128)(2,1)S(1)} %collective-permute-done.3.refs_1_) | copy-start | bytes 196612
  28.7 15.7 %copy-start = (f32[2,16,64,64]{3,2,1,0:T(8,128)S(1)}, f32[2,16,64,64]{3,2,1,0:T(8,128)}, u32[]{:S(2)}) copy-start(f32[2,16,64,64]{3,2,1,0:T(8,128)} %param.9) | copy-start | bytes 1572868
  28.7 4.0 %collective-permute-start.6 = (bf16[64,512]{1,0:T(8,128)(2,1)}, bf16[64,512]{1,0:T(8,128)(2,1)S(1)}, u32[]{:S(2)}, u32[]{:S(2)}) collective-permute-start(bf16[64,512]{1,0:T(8,128)(2,1)} %get-tuple-element.10), channel_id=1, source_target_pairs={{0,1},{1,2},{2,3},{3,0},{4,5},{5,6},{6,7},{7,4},{8,9},{9,10},{10,1... | collective-permute-start | bytes 196616 | tf_op jit(solution)/shard_map/ppermute | solution.py:264
  28.7 5.2 %collective-permute-start.7 = (bf16[64,512]{1,0:T(8,128)(2,1)}, bf16[64,512]{1,0:T(8,128)(2,1)S(1)}, u32[]{:S(2)}, u32[]{:S(2)}) collective-permute-start(bf16[64,512]{1,0:T(8,128)(2,1)} %get-tuple-element.11), channel_id=1, source_target_pairs={{0,2},{1,3},{2,0},{3,1},{4,6},{5,7},{6,4},{7,5},{8,10},{9,11},{10,... | collective-permute-start | bytes 196616 | tf_op jit(solution)/shard_map/ppermute | solution.py:264
  29.7 4.3 %collective-permute-start.8 = (bf16[64,512]{1,0:T(8,128)(2,1)}, bf16[64,512]{1,0:T(8,128)(2,1)S(1)}, u32[]{:S(2)}, u32[]{:S(2)}) collective-permute-start(bf16[64,512]{1,0:T(8,128)(2,1)} %get-tuple-element.12), channel_id=1, source_target_pairs={{0,3},{1,0},{2,1},{3,2},{4,7},{5,4},{6,5},{7,6},{8,11},{9,8},{10,9... | collective-permute-start | bytes 196616 | tf_op jit(solution)/shard_map/ppermute | solution.py:264
  35.3 4.9 %collective-permute-start.9 = (bf16[64,2,64]{2,0,1:T(8,128)(2,1)S(1)}, bf16[64,2,64]{2,0,1:T(8,128)(2,1)S(1)}, u32[]{:S(2)}, u32[]{:S(2)}) collective-permute-start(bf16[64,2,64]{2,0,1:T(8,128)(2,1)S(1)} %bitcast.98), channel_id=1, source_target_pairs={{0,12},{4,0},{8,4},{12,8},{1,13},{5,1},{9,5},{13,9},{2,14},{6,2},{... | collective-permute-start | bytes 49160 | tf_op jit(solution)/shard_map/ppermute | solution.py:85
  38.5 4.8 %collective-permute-start.10 = (bf16[64,2,64]{2,0,1:T(8,128)(2,1)S(1)}, bf16[64,2,64]{2,0,1:T(8,128)(2,1)S(1)}, u32[]{:S(2)}, u32[]{:S(2)}) collective-permute-start(bf16[64,2,64]{2,0,1:T(8,128)(2,1)S(1)} %bitcast.97), channel_id=1, source_target_pairs={{0,8},{4,12},{8,0},{12,4},{1,9},{5,13},{9,1},{13,5},{2,10},{6,14},... | collective-permute-start | bytes 49160 | tf_op jit(solution)/shard_map/ppermute | solution.py:85
  38.5 5.7 %collective-permute-start.11 = (bf16[64,2,64]{2,0,1:T(8,128)(2,1)S(1)}, bf16[64,2,64]{2,0,1:T(8,128)(2,1)S(1)}, u32[]{:S(2)}, u32[]{:S(2)}) collective-permute-start(bf16[64,2,64]{2,0,1:T(8,128)(2,1)S(1)} %bitcast.96), channel_id=1, source_target_pairs={{0,4},{4,8},{8,12},{12,0},{1,5},{5,9},{9,13},{13,1},{2,6},{6,10},{... | collective-permute-start | bytes 49160 | tf_op jit(solution)/shard_map/ppermute | solution.py:85

commit v21 on v20

--- a/solution.py
+++ b/solution.py
@@ -120,24 +120,32 @@
     ).astype(jnp.bfloat16)
     half_k = jnp.dot(coil.reshape(coils * height, width), forward_ref[...], preferred_element_type=jnp.float32)
     table = table_ref[...]
-    backs = []
+    turned = []
     for coil_index in range(coils):
         one = half_k[coil_index * height:(coil_index + 1) * height].astype(jnp.bfloat16).astype(jnp.float32)
-        turned = jnp.concatenate([one[:, :half_width].T, one[:, half_width:].T], axis=0).astype(jnp.bfloat16)
-        parts = jnp.dot(turned, table, preferred_element_type=jnp.float32)
+        turned.append(jnp.concatenate([one[:, :half_width].T, one[:, half_width:].T], axis=0).astype(jnp.bfloat16))
+    all_parts = jnp.dot(jnp.concatenate(turned, axis=0), table, preferred_element_type=jnp.float32)
+    residuals = []
+    for coil_index in range(coils):
+        parts = all_parts[coil_index * width:(coil_index + 1) * width]
         kspace_re = parts[:half_width, :height] - parts[half_width:, height:]
         kspace_im = parts[:half_width, height:] + parts[half_width:, :height]
         row = pl.program_id(0) * coils + coil_index
         sampled = sampled_ref[pl.ds(row, 1), :].astype(jnp.float32)
         measured = measured_ref[coil_index].astype(jnp.float32)
-        residual = jnp.concatenate(
-            [
-                (sampled * (kspace_re - measured[:, :half_width].T)).astype(jnp.bfloat16),
-                (sampled * (kspace_im - measured[:, half_width:].T)).astype(jnp.bfloat16),
-            ],
-            axis=0,
+        residuals.append(
+            jnp.concatenate(
+                [
+                    (sampled * (kspace_re - measured[:, :half_width].T)).astype(jnp.bfloat16),
+                    (sampled * (kspace_im - measured[:, half_width:].T)).astype(jnp.bfloat16),
+                ],
+                axis=0,
+            )
         )
-        parts = jnp.dot(residual, table, preferred_element_type=jnp.float32)
+    all_parts = jnp.dot(jnp.concatenate(residuals, axis=0), table, preferred_element_type=jnp.float32)
+    backs = []
+    for coil_index in range(coils):
+        parts = all_parts[coil_index * width:(coil_index + 1) * width]
         back_re = (parts[:half_width, :height] + parts[half_width:, height:]).astype(jnp.bfloat16)
         back_im = (parts[half_width:, :height] - parts[:half_width, height:]).astype(jnp.bfloat16)
         backs.append(

time: 46.4 us -> 47.1 us (1.015)
  Pallas kernels: 8.42 us -> 9.22 us
    pallas_call x1, Pallas kernels: 8.42 us -> 9.22 us  [coil_chain(): pl.pallas_call(coil_chain_kernel, out_shape=(jax.ShapeDtypeStruct((rows,...]
where the time goes in v21:
time: 47.1 us; the launch traced here: 46.9 us
  starting transfers between devices  15 us (32%)
  waiting for transfers between devices  13.2 us (28%)
  Pallas kernels  9.22 us (20%)
  other arithmetic  6.34 us (13%)
  local copies, waits for them, and re-layouts  2.92 us (6%)
    ppermute x6, starting transfers between devices, exchange_blocks(): pieces.append(lax.ppermute(outgoing, axis, shifted(count, step)))  10.9 us
    pallas_call x1, Pallas kernels, coil_chain(): pl.pallas_call(coil_chain_kernel, out_shape=(jax.ShapeDtypeStruct((rows,...  9.22 us
    ppermute x6, waiting for transfers between devices, exchange_blocks(): pieces.append(lax.ppermute(outgoing, axis, shifted(count, step)))  6.23 us
    ppermute x3, waiting for transfers between devices, on_device(): lax.ppermute(own_rows, 'coil', shifted(groups, step))  4.1 us
    ppermute x3, waiting for transfers between devices, on_device(): lax.ppermute(outgoing[step - 1], 'coil', shifted(groups, step))  2.86 us
    ppermute x3, starting transfers between devices, on_device(): lax.ppermute(outgoing[step - 1], 'coil', shifted(groups, step))  2.38 us
    reduce_sum x1, other arithmetic, on_device(): jnp.sum(mixing[:, :, :, :, None, None] * factors[None, :, None], axis=(1,...  2.23 us
    ppermute x3, starting transfers between devices, on_device(): lax.ppermute(own_rows, 'coil', shifted(groups, step))  1.78 us
  transfers between devices with their start and end apart: 12, of which 9 were waited for; matrix products, arithmetic and copies ran while one was open for 3% of the time, Pallas kernels for 0%

profile of v21, /device:TPU:0, one launch (start us, length us, event | category | flops | bytes accessed | tf_op | source)
XLA Modules:
  0.0 46.9 jit_solution(13011014751072216246)
XLA Ops:
  0.0 0.7 %reverse_bitcast_fusion = f32[1,2,4,16]{3,2,1,0:T(4,128)S(1)} fusion(f32[2,4,16]{2,1,0:T(4,128)} %param.10), kind=kLoop, calls=%fused_computation.53 | loop fusion | bytes 1024 | tf_op jit(solution)/shard_map/stack | solution.py:252
  0.7 0.8 %maximum_multiply_fusion = f32[2,2,4,16]{3,2,1,0:T(4,128)S(1)} fusion(f32[1,2,4,16]{3,2,1,0:T(4,128)S(1)} %reverse_bitcast_fusion, f32[1,2,4,16]{3,2,1,0:T(4,128)} %bitcast.95, f32[2,2]{1,0:T(2,128)} %constant.83.clone), kind=kLoop, calls=%fused_computation.50 | loop fusion | flops 512 | bytes 2064 | tf_op jit(solution)/shard_map/mul | solution.py:252
  1.5 2.2 %multiply_reduce_fusion = bf16[2,4,64,64]{3,2,1,0:T(8,128)(2,1)S(1)} fusion(f32[2,16,64,64]{3,2,1,0:T(8,128)} %param.9, f32[2,2,4,16]{3,2,1,0:T(4,128)S(1)} %maximum_multiply_fusion), kind=kLoop, calls=%fused_computation | loop fusion | flops 2064384 | bytes 590848 | tf_op jit(solution)/shard_map/reduce_sum | solution.py:253
  3.7 3.1 %collective-permute-start.2 = (bf16[2,64,64]{2,1,0:T(8,128)(2,1)S(1)}, bf16[2,64,64]{2,1,0:T(8,128)(2,1)S(1)}, u32[]{:S(2)}, u32[]{:S(2)}) collective-permute-start(bf16[2,64,64]{2,1,0:T(8,128)(2,1)S(1)} %get-tuple-element.25), channel_id=1, source_target_pairs={{0,4},{4,8},{8,12},{12,0},{1,5},{5,9},{9,13},{13,1},{2,6},{6,10},{... | collective-permute-start | bytes 49160 | tf_op jit(solution)/shard_map/ppermute | solution.py:85
  6.8 2.6 %collective-permute-start.1 = (bf16[2,64,64]{2,1,0:T(8,128)(2,1)S(1)}, bf16[2,64,64]{2,1,0:T(8,128)(2,1)S(1)}, u32[]{:S(2)}, u32[]{:S(2)}) collective-permute-start(bf16[2,64,64]{2,1,0:T(8,128)(2,1)S(1)} %get-tuple-element.26), channel_id=1, source_target_pairs={{0,8},{4,12},{8,0},{12,4},{1,9},{5,13},{9,1},{13,5},{2,10},{6,14},... | collective-permute-start | bytes 49160 | tf_op jit(solution)/shard_map/ppermute | solution.py:85
  9.4 1.3 %collective-permute-start = (bf16[2,64,64]{2,1,0:T(8,128)(2,1)S(1)}, bf16[2,64,64]{2,1,0:T(8,128)(2,1)S(1)}, u32[]{:S(2)}, u32[]{:S(2)}) collective-permute-start(bf16[2,64,64]{2,1,0:T(8,128)(2,1)S(1)} %get-tuple-element.27), channel_id=1, source_target_pairs={{0,12},{4,0},{8,4},{12,8},{1,13},{5,1},{9,5},{13,9},{2,14},{6,2},{... | collective-permute-start | bytes 49160 | tf_op jit(solution)/shard_map/ppermute | solution.py:85
  10.7 0.7 %fusion = f32[16,4,1]{0,1,2:T(4,128)S(1)} fusion(f32[2,4,16]{2,1,0:T(4,128)} %param.10), kind=kLoop, calls=%fused_computation.60 | loop fusion | flops 64 | bytes 512 | tf_op jit(solution)/shard_map/stack | solution.py:279
  11.4 0.7 %slice_bitcast_fusion.9 = (f32[16,4,1]{0,1,2:T(4,128)S(1)}, f32[16,4,1]{0,1,2:T(4,128)S(1)}) fusion(f32[2,4,16]{2,1,0:T(4,128)} %param.10), kind=kLoop, calls=%fused_computation.61 | loop fusion | bytes 1024 | tf_op jit(solution)/shard_map/stack | solution.py:279
  12.1 1.2 %collective-permute-done = bf16[2,64,64]{2,1,0:T(8,128)(2,1)S(1)} collective-permute-done((bf16[2,64,64]{2,1,0:T(8,128)(2,1)S(1)}, bf16[2,64,64]{2,1,0:T(8,128)(2,1)S(1)}, u32[]{:S(2)}, u32[]{:S(2)}) %collective-permute-start) | collective-permute-done | bytes 16416 | tf_op jit(solution)/shard_map/ppermute | solution.py:85
  13.8 1.6 %collective-permute-start.4 = (bf16[64,512]{1,0:T(8,128)(2,1)S(1)}, bf16[64,512]{1,0:T(8,128)(2,1)S(1)}, u32[]{:S(2)}, u32[]{:S(2)}) collective-permute-start(bf16[64,512]{1,0:T(8,128)(2,1)S(1)} %reshape.49.refs_0_), channel_id=1, source_target_pairs={{0,2},{1,3},{2,0},{3,1},{4,6},{5,7},{6,4},{7,5},{8,10},{9,11},{10,... | collective-permute-start | bytes 196616 | tf_op jit(solution)/shard_map/ppermute | solution.py:263
  15.7 3.7 %collective-permute-done.4.refs_2_ = bf16[64,512]{1,0:T(8,128)(2,1)S(1)} collective-permute-done((bf16[64,512]{1,0:T(8,128)(2,1)S(1)}, bf16[64,512]{1,0:T(8,128)(2,1)S(1)}, u32[]{:S(2)}, u32[]{:S(2)}) %collective-permute-start.4) | collective-permute-done | bytes 65568 | tf_op jit(solution)/shard_map/ppermute | solution.py:263
  19.6 0.4 copy-done.3
  20.2 9.2 %shard_map.91 = (f32[64,512]{1,0:T(8,128)}, bf16[64,512]{1,0:T(8,128)(2,1)}, bf16[64,512]{1,0:T(8,128)(2,1)}, bf16[64,512]{1,0:T(8,128)(2,1)}) custom-call(bf16[64,512]{1,0:T(8,128)(2,1)} %copy-done.1, bf16[64,512]{1,0:T(8,128)(2,1)} %copy-done.4, bf16[64,512]{1,0:T(8,128)(2,1)} %copy-done.3, bf16[64,512]{1,0:T(8,128)(2,1)} %copy-done.2, s32[1]{0:T(128)} %bitcast.23.refs_4_, ...), custom_call_target="tpu_custom_call" | custom-call | flops 4294967296 | bytes 4718592 | tf_op jit(solution)/shard_map/pallas_call | solution.py:216
  29.5 0.9 %collective-permute-start.7 = (bf16[64,512]{1,0:T(8,128)(2,1)}, bf16[64,512]{1,0:T(8,128)(2,1)S(1)}, u32[]{:S(2)}, u32[]{:S(2)}) collective-permute-start(bf16[64,512]{1,0:T(8,128)(2,1)} %get-tuple-element.11), channel_id=1, source_target_pairs={{0,2},{1,3},{2,0},{3,1},{4,6},{5,7},{6,4},{7,5},{8,10},{9,11},{10,... | collective-permute-start | bytes 196616 | tf_op jit(solution)/shard_map/ppermute | solution.py:272
  30.5 1.4 %collective-permute-start.8 = (bf16[64,512]{1,0:T(8,128)(2,1)}, bf16[64,512]{1,0:T(8,128)(2,1)S(1)}, u32[]{:S(2)}, u32[]{:S(2)}) collective-permute-start(bf16[64,512]{1,0:T(8,128)(2,1)} %get-tuple-element.12), channel_id=1, source_target_pairs={{0,3},{1,0},{2,1},{3,2},{4,7},{5,4},{6,5},{7,6},{8,11},{9,8},{10,9... | collective-permute-start | bytes 196616 | tf_op jit(solution)/shard_map/ppermute | solution.py:272
  31.9 1.6 %collective-permute-done.6 = bf16[64,512]{1,0:T(8,128)(2,1)S(1)} collective-permute-done((bf16[64,512]{1,0:T(8,128)(2,1)}, bf16[64,512]{1,0:T(8,128)(2,1)S(1)}, u32[]{:S(2)}, u32[]{:S(2)}) %collective-permute-start.6) | collective-permute-done | bytes 65568 | tf_op jit(solution)/shard_map/ppermute | solution.py:272
  33.5 1.2 %collective-permute-done.7 = bf16[64,512]{1,0:T(8,128)(2,1)S(1)} collective-permute-done((bf16[64,512]{1,0:T(8,128)(2,1)}, bf16[64,512]{1,0:T(8,128)(2,1)S(1)}, u32[]{:S(2)}, u32[]{:S(2)}) %collective-permute-start.7) | collective-permute-done | bytes 65568 | tf_op jit(solution)/shard_map/ppermute | solution.py:272
  34.7 0.9 %add_convert_fusion = bf16[64,512]{1,0:T(8,128)(2,1)S(1)} fusion(bf16[64,512]{1,0:T(8,128)(2,1)S(1)} %collective-permute-done.8, bf16[64,512]{1,0:T(8,128)(2,1)S(1)} %collective-permute-done.7, f32[64,512]{1,0:T(8,128)} %get-tuple-element.9, bf16[64,512]{1,0:T(8,128)(2,1)S(1)} %collective-permute-done.6), kind=kLoop, calls=%fused_computation.3 | loop fusion | flops 229376 | bytes 393216 | tf_op jit(solution)/shard_map/convert_element_type | solution.py:275
  36.1 3.2 %collective-permute-start.9 = (bf16[64,2,64]{2,0,1:T(8,128)(2,1)S(1)}, bf16[64,2,64]{2,0,1:T(8,128)(2,1)S(1)}, u32[]{:S(2)}, u32[]{:S(2)}) collective-permute-start(bf16[64,2,64]{2,0,1:T(8,128)(2,1)S(1)} %bitcast.98), channel_id=1, source_target_pairs={{0,12},{4,0},{8,4},{12,8},{1,13},{5,1},{9,5},{13,9},{2,14},{6,2},{... | collective-permute-start | bytes 49160 | tf_op jit(solution)/shard_map/ppermute | solution.py:85
  39.3 0.6 %collective-permute-start.11 = (bf16[64,2,64]{2,0,1:T(8,128)(2,1)S(1)}, bf16[64,2,64]{2,0,1:T(8,128)(2,1)S(1)}, u32[]{:S(2)}, u32[]{:S(2)}) collective-permute-start(bf16[64,2,64]{2,0,1:T(8,128)(2,1)S(1)} %bitcast.96), channel_id=1, source_target_pairs={{0,4},{4,8},{8,12},{12,0},{1,5},{5,9},{9,13},{13,1},{2,6},{6,10},{... | collective-permute-start | bytes 49160 | tf_op jit(solution)/shard_map/ppermute | solution.py:85
  40.0 1.0 %collective-permute-done.9 = bf16[64,2,64]{2,0,1:T(8,128)(2,1)S(1)} collective-permute-done((bf16[64,2,64]{2,0,1:T(8,128)(2,1)S(1)}, bf16[64,2,64]{2,0,1:T(8,128)(2,1)S(1)}, u32[]{:S(2)}, u32[]{:S(2)}) %collective-permute-start.9) | collective-permute-done | bytes 16416 | tf_op jit(solution)/shard_map/ppermute | solution.py:85
  41.0 3.1 %collective-permute-done.10 = bf16[64,2,64]{2,0,1:T(8,128)(2,1)S(1)} collective-permute-done((bf16[64,2,64]{2,0,1:T(8,128)(2,1)S(1)}, bf16[64,2,64]{2,0,1:T(8,128)(2,1)S(1)}, u32[]{:S(2)}, u32[]{:S(2)}) %collective-permute-start.10) | collective-permute-done | bytes 16416 | tf_op jit(solution)/shard_map/ppermute | solution.py:85
  44.2 0.9 %collective-permute-done.11 = bf16[64,2,64]{2,0,1:T(8,128)(2,1)S(1)} collective-permute-done((bf16[64,2,64]{2,0,1:T(8,128)(2,1)S(1)}, bf16[64,2,64]{2,0,1:T(8,128)(2,1)S(1)}, u32[]{:S(2)}, u32[]{:S(2)}) %collective-permute-start.11) | collective-permute-done | bytes 16416 | tf_op jit(solution)/shard_map/ppermute | solution.py:85
  45.2 1.7 %multiply_subtract_fusion = f32[2,16,64,64]{3,2,1,0:T(8,128)} fusion(f32[2,16,64,64]{3,2,1,0:T(8,128)S(1)} %copy-done, f32[64,64]{1,0:T(8,128)S(1)} %get-tuple-element.14, f32[2,16]{1,0:T(2,128)S(1)} %bitcast.105, f32[64,64]{1,0:T(8,128)S(1)} %get-tuple-element.15, f32[2,16]{1,0:T(2,128)S(1)} %bitcast.106, f32[64,64]{1,0:T(8,128)S(1)} %get-tuple-element.16, ...), kind=kLoop, calls=%fused_computation.1 | loop fusion | flops 2228224 | bytes 1180672 | tf_op jit(solution)/shard_map/sub | solution.py:286
  (47 shorter events, 1.8 us)
Async XLA Ops:
  3.7 9.6 %collective-permute-start.2 = (bf16[2,64,64]{2,1,0:T(8,128)(2,1)S(1)}, bf16[2,64,64]{2,1,0:T(8,128)(2,1)S(1)}, u32[]{:S(2)}, u32[]{:S(2)}) collective-permute-start(bf16[2,64,64]{2,1,0:T(8,128)(2,1)S(1)} %get-tuple-element.25), channel_id=1, source_target_pairs={{0,4},{4,8},{8,12},{12,0},{1,5},{5,9},{9,13},{13,1},{2,6},{6,10},{... | collective-permute-start | bytes 49160 | tf_op jit(solution)/shard_map/ppermute | solution.py:85
  6.8 6.5 %collective-permute-start.1 = (bf16[2,64,64]{2,1,0:T(8,128)(2,1)S(1)}, bf16[2,64,64]{2,1,0:T(8,128)(2,1)S(1)}, u32[]{:S(2)}, u32[]{:S(2)}) collective-permute-start(bf16[2,64,64]{2,1,0:T(8,128)(2,1)S(1)} %get-tuple-element.26), channel_id=1, source_target_pairs={{0,8},{4,12},{8,0},{12,4},{1,9},{5,13},{9,1},{13,5},{2,10},{6,14},... | collective-permute-start | bytes 49160 | tf_op jit(solution)/shard_map/ppermute | solution.py:85
  9.4 3.9 %collective-permute-start = (bf16[2,64,64]{2,1,0:T(8,128)(2,1)S(1)}, bf16[2,64,64]{2,1,0:T(8,128)(2,1)S(1)}, u32[]{:S(2)}, u32[]{:S(2)}) collective-permute-start(bf16[2,64,64]{2,1,0:T(8,128)(2,1)S(1)} %get-tuple-element.27), channel_id=1, source_target_pairs={{0,12},{4,0},{8,4},{12,8},{1,13},{5,1},{9,5},{13,9},{2,14},{6,2},{... | collective-permute-start | bytes 49160 | tf_op jit(solution)/shard_map/ppermute | solution.py:85
  13.7 5.9 %copy-start.1 = (bf16[64,512]{1,0:T(8,128)(2,1)}, bf16[64,512]{1,0:T(8,128)(2,1)S(1)}, u32[]{:S(2)}) copy-start(bf16[64,512]{1,0:T(8,128)(2,1)S(1)} %reshape.49.refs_0_) | copy-start | bytes 196612
  13.7 2.0 %collective-permute-start.5 = (bf16[64,512]{1,0:T(8,128)(2,1)S(1)}, bf16[64,512]{1,0:T(8,128)(2,1)S(1)}, u32[]{:S(2)}, u32[]{:S(2)}) collective-permute-start(bf16[64,512]{1,0:T(8,128)(2,1)S(1)} %reshape.49.refs_0_), channel_id=1, source_target_pairs={{0,3},{1,0},{2,1},{3,2},{4,7},{5,4},{6,5},{7,6},{8,11},{9,8},{10,9... | collective-permute-start | bytes 196616 | tf_op jit(solution)/shard_map/ppermute | solution.py:263
  13.8 5.6 %collective-permute-start.4 = (bf16[64,512]{1,0:T(8,128)(2,1)S(1)}, bf16[64,512]{1,0:T(8,128)(2,1)S(1)}, u32[]{:S(2)}, u32[]{:S(2)}) collective-permute-start(bf16[64,512]{1,0:T(8,128)(2,1)S(1)} %reshape.49.refs_0_), channel_id=1, source_target_pairs={{0,2},{1,3},{2,0},{3,1},{4,6},{5,7},{6,4},{7,5},{8,10},{9,11},{10,... | collective-permute-start | bytes 196616 | tf_op jit(solution)/shard_map/ppermute | solution.py:263
  15.3 4.3 %collective-permute-start.3 = (bf16[64,512]{1,0:T(8,128)(2,1)S(1)}, bf16[64,512]{1,0:T(8,128)(2,1)S(1)}, u32[]{:S(2)}, u32[]{:S(2)}) collective-permute-start(bf16[64,512]{1,0:T(8,128)(2,1)S(1)} %reshape.49.refs_0_), channel_id=1, source_target_pairs={{0,1},{1,2},{2,3},{3,0},{4,5},{5,6},{6,7},{7,4},{8,9},{9,10},{10,1... | collective-permute-start | bytes 196616 | tf_op jit(solution)/shard_map/ppermute | solution.py:263
  15.7 3.9 %copy-start.2 = (bf16[64,512]{1,0:T(8,128)(2,1)}, bf16[64,512]{1,0:T(8,128)(2,1)S(1)}, u32[]{:S(2)}) copy-start(bf16[64,512]{1,0:T(8,128)(2,1)S(1)} %collective-permute-done.5.refs_3_) | copy-start | bytes 196612
  19.4 0.6 %copy-start.3 = (bf16[64,512]{1,0:T(8,128)(2,1)}, bf16[64,512]{1,0:T(8,128)(2,1)S(1)}, u32[]{:S(2)}) copy-start(bf16[64,512]{1,0:T(8,128)(2,1)S(1)} %collective-permute-done.4.refs_2_) | copy-start | bytes 196612
  19.6 0.6 %copy-start.4 = (bf16[64,512]{1,0:T(8,128)(2,1)}, bf16[64,512]{1,0:T(8,128)(2,1)S(1)}, u32[]{:S(2)}) copy-start(bf16[64,512]{1,0:T(8,128)(2,1)S(1)} %collective-permute-done.3.refs_1_) | copy-start | bytes 196612
  29.4 15.7 %copy-start = (f32[2,16,64,64]{3,2,1,0:T(8,128)S(1)}, f32[2,16,64,64]{3,2,1,0:T(8,128)}, u32[]{:S(2)}) copy-start(f32[2,16,64,64]{3,2,1,0:T(8,128)} %param.9) | copy-start | bytes 1572868
  29.5 4.0 %collective-permute-start.6 = (bf16[64,512]{1,0:T(8,128)(2,1)}, bf16[64,512]{1,0:T(8,128)(2,1)S(1)}, u32[]{:S(2)}, u32[]{:S(2)}) collective-permute-start(bf16[64,512]{1,0:T(8,128)(2,1)} %get-tuple-element.10), channel_id=1, source_target_pairs={{0,1},{1,2},{2,3},{3,0},{4,5},{5,6},{6,7},{7,4},{8,9},{9,10},{10,1... | collective-permute-start | bytes 196616 | tf_op jit(solution)/shard_map/ppermute | solution.py:272
  29.5 5.2 %collective-permute-start.7 = (bf16[64,512]{1,0:T(8,128)(2,1)}, bf16[64,512]{1,0:T(8,128)(2,1)S(1)}, u32[]{:S(2)}, u32[]{:S(2)}) collective-permute-start(bf16[64,512]{1,0:T(8,128)(2,1)} %get-tuple-element.11), channel_id=1, source_target_pairs={{0,2},{1,3},{2,0},{3,1},{4,6},{5,7},{6,4},{7,5},{8,10},{9,11},{10,... | collective-permute-start | bytes 196616 | tf_op jit(solution)/shard_map/ppermute | solution.py:272
  30.5 4.3 %collective-permute-start.8 = (bf16[64,512]{1,0:T(8,128)(2,1)}, bf16[64,512]{1,0:T(8,128)(2,1)S(1)}, u32[]{:S(2)}, u32[]{:S(2)}) collective-permute-start(bf16[64,512]{1,0:T(8,128)(2,1)} %get-tuple-element.12), channel_id=1, source_target_pairs={{0,3},{1,0},{2,1},{3,2},{4,7},{5,4},{6,5},{7,6},{8,11},{9,8},{10,9... | collective-permute-start | bytes 196616 | tf_op jit(solution)/shard_map/ppermute | solution.py:272
  36.1 4.9 %collective-permute-start.9 = (bf16[64,2,64]{2,0,1:T(8,128)(2,1)S(1)}, bf16[64,2,64]{2,0,1:T(8,128)(2,1)S(1)}, u32[]{:S(2)}, u32[]{:S(2)}) collective-permute-start(bf16[64,2,64]{2,0,1:T(8,128)(2,1)S(1)} %bitcast.98), channel_id=1, source_target_pairs={{0,12},{4,0},{8,4},{12,8},{1,13},{5,1},{9,5},{13,9},{2,14},{6,2},{... | collective-permute-start | bytes 49160 | tf_op jit(solution)/shard_map/ppermute | solution.py:85
  39.3 4.8 %collective-permute-start.10 = (bf16[64,2,64]{2,0,1:T(8,128)(2,1)S(1)}, bf16[64,2,64]{2,0,1:T(8,128)(2,1)S(1)}, u32[]{:S(2)}, u32[]{:S(2)}) collective-permute-start(bf16[64,2,64]{2,0,1:T(8,128)(2,1)S(1)} %bitcast.97), channel_id=1, source_target_pairs={{0,8},{4,12},{8,0},{12,4},{1,9},{5,13},{9,1},{13,5},{2,10},{6,14},... | collective-permute-start | bytes 49160 | tf_op jit(solution)/shard_map/ppermute | solution.py:85
  39.3 5.7 %collective-permute-start.11 = (bf16[64,2,64]{2,0,1:T(8,128)(2,1)S(1)}, bf16[64,2,64]{2,0,1:T(8,128)(2,1)S(1)}, u32[]{:S(2)}, u32[]{:S(2)}) collective-permute-start(bf16[64,2,64]{2,0,1:T(8,128)(2,1)S(1)} %bitcast.96), channel_id=1, source_target_pairs={{0,4},{4,8},{8,12},{12,0},{1,5},{5,9},{9,13},{13,1},{2,6},{6,10},{... | collective-permute-start | bytes 49160 | tf_op jit(solution)/shard_map/ppermute | solution.py:85

commit v22 on v20

--- a/solution.py
+++ b/solution.py
@@ -203,7 +203,7 @@
     rows = pieces[0].shape[0]
     whole = lambda c: (0, 0)
     per_coil = lambda c: (c, 0, 0)
-    step_coils = 4 if coils % 4 == 0 else (2 if coils % 2 == 0 else 1)
+    step_coils = 2 if coils % 2 == 0 else 1
     flops = coils * 8 * height * width * width
     return pl.pallas_call(
         coil_chain_kernel,

time: 46.4 us -> 48.1 us (1.037)
  Pallas kernels: 8.42 us -> 10.2 us
    pallas_call x1, Pallas kernels: 8.42 us -> 10.2 us  [coil_chain(): pl.pallas_call(coil_chain_kernel, out_shape=(jax.ShapeDtypeStruct((rows,...]
where the time goes in v22:
time: 48.1 us; the launch traced here: 47.8 us
  starting transfers between devices  15 us (31%)
  waiting for transfers between devices  13.2 us (27%)
  Pallas kernels  10.2 us (21%)
  other arithmetic  6.34 us (13%)
  local copies, waits for them, and re-layouts  2.92 us (6%)
    ppermute x6, starting transfers between devices, exchange_blocks(): pieces.append(lax.ppermute(outgoing, axis, shifted(count, step)))  10.9 us
    pallas_call x1, Pallas kernels, coil_chain(): pl.pallas_call(coil_chain_kernel, out_shape=(jax.ShapeDtypeStruct((rows,...  10.2 us
    ppermute x6, waiting for transfers between devices, exchange_blocks(): pieces.append(lax.ppermute(outgoing, axis, shifted(count, step)))  6.23 us
    ppermute x3, waiting for transfers between devices, on_device(): lax.ppermute(own_rows, 'coil', shifted(groups, step))  4.1 us
    ppermute x3, waiting for transfers between devices, on_device(): lax.ppermute(outgoing[step - 1], 'coil', shifted(groups, step))  2.86 us
    ppermute x3, starting transfers between devices, on_device(): lax.ppermute(outgoing[step - 1], 'coil', shifted(groups, step))  2.37 us
    reduce_sum x1, other arithmetic, on_device(): jnp.sum(mixing[:, :, :, :, None, None] * factors[None, :, None], axis=(1,...  2.23 us
    ppermute x3, starting transfers between devices, on_device(): lax.ppermute(own_rows, 'coil', shifted(groups, step))  1.78 us
  transfers between devices with their start and end apart: 12, of which 9 were waited for; matrix products, arithmetic and copies ran while one was open for 3% of the time, Pallas kernels for 0%

profile of v22, /device:TPU:0, one launch (start us, length us, event | category | flops | bytes accessed | tf_op | source)
XLA Modules:
  0.0 47.8 jit_solution(18423331300632276088)
XLA Ops:
  0.0 0.7 %reverse_bitcast_fusion = f32[1,2,4,16]{3,2,1,0:T(4,128)S(1)} fusion(f32[2,4,16]{2,1,0:T(4,128)} %param.10), kind=kLoop, calls=%fused_computation.53 | loop fusion | bytes 1024 | tf_op jit(solution)/shard_map/stack | solution.py:244
  0.7 0.8 %maximum_multiply_fusion = f32[2,2,4,16]{3,2,1,0:T(4,128)S(1)} fusion(f32[1,2,4,16]{3,2,1,0:T(4,128)S(1)} %reverse_bitcast_fusion, f32[1,2,4,16]{3,2,1,0:T(4,128)} %bitcast.95, f32[2,2]{1,0:T(2,128)} %constant.83.clone), kind=kLoop, calls=%fused_computation.50 | loop fusion | flops 512 | bytes 2064 | tf_op jit(solution)/shard_map/mul | solution.py:244
  1.5 2.2 %multiply_reduce_fusion = bf16[2,4,64,64]{3,2,1,0:T(8,128)(2,1)S(1)} fusion(f32[2,16,64,64]{3,2,1,0:T(8,128)} %param.9, f32[2,2,4,16]{3,2,1,0:T(4,128)S(1)} %maximum_multiply_fusion), kind=kLoop, calls=%fused_computation | loop fusion | flops 2064384 | bytes 590848 | tf_op jit(solution)/shard_map/reduce_sum | solution.py:245
  3.7 3.1 %collective-permute-start.2 = (bf16[2,64,64]{2,1,0:T(8,128)(2,1)S(1)}, bf16[2,64,64]{2,1,0:T(8,128)(2,1)S(1)}, u32[]{:S(2)}, u32[]{:S(2)}) collective-permute-start(bf16[2,64,64]{2,1,0:T(8,128)(2,1)S(1)} %get-tuple-element.25), channel_id=1, source_target_pairs={{0,4},{4,8},{8,12},{12,0},{1,5},{5,9},{9,13},{13,1},{2,6},{6,10},{... | collective-permute-start | bytes 49160 | tf_op jit(solution)/shard_map/ppermute | solution.py:85
  6.8 2.6 %collective-permute-start.1 = (bf16[2,64,64]{2,1,0:T(8,128)(2,1)S(1)}, bf16[2,64,64]{2,1,0:T(8,128)(2,1)S(1)}, u32[]{:S(2)}, u32[]{:S(2)}) collective-permute-start(bf16[2,64,64]{2,1,0:T(8,128)(2,1)S(1)} %get-tuple-element.26), channel_id=1, source_target_pairs={{0,8},{4,12},{8,0},{12,4},{1,9},{5,13},{9,1},{13,5},{2,10},{6,14},... | collective-permute-start | bytes 49160 | tf_op jit(solution)/shard_map/ppermute | solution.py:85
  9.4 1.3 %collective-permute-start = (bf16[2,64,64]{2,1,0:T(8,128)(2,1)S(1)}, bf16[2,64,64]{2,1,0:T(8,128)(2,1)S(1)}, u32[]{:S(2)}, u32[]{:S(2)}) collective-permute-start(bf16[2,64,64]{2,1,0:T(8,128)(2,1)S(1)} %get-tuple-element.27), channel_id=1, source_target_pairs={{0,12},{4,0},{8,4},{12,8},{1,13},{5,1},{9,5},{13,9},{2,14},{6,2},{... | collective-permute-start | bytes 49160 | tf_op jit(solution)/shard_map/ppermute | solution.py:85
  10.7 0.7 %fusion = f32[16,4,1]{0,1,2:T(4,128)S(1)} fusion(f32[2,4,16]{2,1,0:T(4,128)} %param.10), kind=kLoop, calls=%fused_computation.60 | loop fusion | flops 64 | bytes 512 | tf_op jit(solution)/shard_map/stack | solution.py:271
  11.4 0.7 %slice_bitcast_fusion.9 = (f32[16,4,1]{0,1,2:T(4,128)S(1)}, f32[16,4,1]{0,1,2:T(4,128)S(1)}) fusion(f32[2,4,16]{2,1,0:T(4,128)} %param.10), kind=kLoop, calls=%fused_computation.61 | loop fusion | bytes 1024 | tf_op jit(solution)/shard_map/stack | solution.py:271
  12.1 1.2 %collective-permute-done = bf16[2,64,64]{2,1,0:T(8,128)(2,1)S(1)} collective-permute-done((bf16[2,64,64]{2,1,0:T(8,128)(2,1)S(1)}, bf16[2,64,64]{2,1,0:T(8,128)(2,1)S(1)}, u32[]{:S(2)}, u32[]{:S(2)}) %collective-permute-start) | collective-permute-done | bytes 16416 | tf_op jit(solution)/shard_map/ppermute | solution.py:85
  13.8 1.6 %collective-permute-start.4 = (bf16[64,512]{1,0:T(8,128)(2,1)S(1)}, bf16[64,512]{1,0:T(8,128)(2,1)S(1)}, u32[]{:S(2)}, u32[]{:S(2)}) collective-permute-start(bf16[64,512]{1,0:T(8,128)(2,1)S(1)} %reshape.49.refs_0_), channel_id=1, source_target_pairs={{0,2},{1,3},{2,0},{3,1},{4,6},{5,7},{6,4},{7,5},{8,10},{9,11},{10,... | collective-permute-start | bytes 196616 | tf_op jit(solution)/shard_map/ppermute | solution.py:255
  15.7 3.7 %collective-permute-done.4.refs_2_ = bf16[64,512]{1,0:T(8,128)(2,1)S(1)} collective-permute-done((bf16[64,512]{1,0:T(8,128)(2,1)S(1)}, bf16[64,512]{1,0:T(8,128)(2,1)S(1)}, u32[]{:S(2)}, u32[]{:S(2)}) %collective-permute-start.4) | collective-permute-done | bytes 65568 | tf_op jit(solution)/shard_map/ppermute | solution.py:255
  19.6 0.4 copy-done.3
  20.2 10.2 %shard_map.91 = (f32[64,512]{1,0:T(8,128)}, bf16[64,512]{1,0:T(8,128)(2,1)}, bf16[64,512]{1,0:T(8,128)(2,1)}, bf16[64,512]{1,0:T(8,128)(2,1)}) custom-call(bf16[64,512]{1,0:T(8,128)(2,1)} %copy-done.1, bf16[64,512]{1,0:T(8,128)(2,1)} %copy-done.4, bf16[64,512]{1,0:T(8,128)(2,1)} %copy-done.3, bf16[64,512]{1,0:T(8,128)(2,1)} %copy-done.2, s32[1]{0:T(128)} %bitcast.23.refs_4_, ...), custom_call_target="tpu_custom_call" | custom-call | flops 4294967296 | bytes 4718592 | tf_op jit(solution)/shard_map/pallas_call | solution.py:208
  30.5 0.9 %collective-permute-start.7 = (bf16[64,512]{1,0:T(8,128)(2,1)}, bf16[64,512]{1,0:T(8,128)(2,1)S(1)}, u32[]{:S(2)}, u32[]{:S(2)}) collective-permute-start(bf16[64,512]{1,0:T(8,128)(2,1)} %get-tuple-element.11), channel_id=1, source_target_pairs={{0,2},{1,3},{2,0},{3,1},{4,6},{5,7},{6,4},{7,5},{8,10},{9,11},{10,... | collective-permute-start | bytes 196616 | tf_op jit(solution)/shard_map/ppermute | solution.py:264
  31.4 1.4 %collective-permute-start.8 = (bf16[64,512]{1,0:T(8,128)(2,1)}, bf16[64,512]{1,0:T(8,128)(2,1)S(1)}, u32[]{:S(2)}, u32[]{:S(2)}) collective-permute-start(bf16[64,512]{1,0:T(8,128)(2,1)} %get-tuple-element.12), channel_id=1, source_target_pairs={{0,3},{1,0},{2,1},{3,2},{4,7},{5,4},{6,5},{7,6},{8,11},{9,8},{10,9... | collective-permute-start | bytes 196616 | tf_op jit(solution)/shard_map/ppermute | solution.py:264
  32.8 1.6 %collective-permute-done.6 = bf16[64,512]{1,0:T(8,128)(2,1)S(1)} collective-permute-done((bf16[64,512]{1,0:T(8,128)(2,1)}, bf16[64,512]{1,0:T(8,128)(2,1)S(1)}, u32[]{:S(2)}, u32[]{:S(2)}) %collective-permute-start.6) | collective-permute-done | bytes 65568 | tf_op jit(solution)/shard_map/ppermute | solution.py:264
  34.5 1.2 %collective-permute-done.7 = bf16[64,512]{1,0:T(8,128)(2,1)S(1)} collective-permute-done((bf16[64,512]{1,0:T(8,128)(2,1)}, bf16[64,512]{1,0:T(8,128)(2,1)S(1)}, u32[]{:S(2)}, u32[]{:S(2)}) %collective-permute-start.7) | collective-permute-done | bytes 65568 | tf_op jit(solution)/shard_map/ppermute | solution.py:264
  35.7 0.9 %add_convert_fusion = bf16[64,512]{1,0:T(8,128)(2,1)S(1)} fusion(bf16[64,512]{1,0:T(8,128)(2,1)S(1)} %collective-permute-done.8, bf16[64,512]{1,0:T(8,128)(2,1)S(1)} %collective-permute-done.7, f32[64,512]{1,0:T(8,128)} %get-tuple-element.9, bf16[64,512]{1,0:T(8,128)(2,1)S(1)} %collective-permute-done.6), kind=kLoop, calls=%fused_computation.3 | loop fusion | flops 229376 | bytes 393216 | tf_op jit(solution)/shard_map/convert_element_type | solution.py:267
  37.1 3.2 %collective-permute-start.9 = (bf16[64,2,64]{2,0,1:T(8,128)(2,1)S(1)}, bf16[64,2,64]{2,0,1:T(8,128)(2,1)S(1)}, u32[]{:S(2)}, u32[]{:S(2)}) collective-permute-start(bf16[64,2,64]{2,0,1:T(8,128)(2,1)S(1)} %bitcast.98), channel_id=1, source_target_pairs={{0,12},{4,0},{8,4},{12,8},{1,13},{5,1},{9,5},{13,9},{2,14},{6,2},{... | collective-permute-start | bytes 49160 | tf_op jit(solution)/shard_map/ppermute | solution.py:85
  40.3 0.6 %collective-permute-start.11 = (bf16[64,2,64]{2,0,1:T(8,128)(2,1)S(1)}, bf16[64,2,64]{2,0,1:T(8,128)(2,1)S(1)}, u32[]{:S(2)}, u32[]{:S(2)}) collective-permute-start(bf16[64,2,64]{2,0,1:T(8,128)(2,1)S(1)} %bitcast.96), channel_id=1, source_target_pairs={{0,4},{4,8},{8,12},{12,0},{1,5},{5,9},{9,13},{13,1},{2,6},{6,10},{... | collective-permute-start | bytes 49160 | tf_op jit(solution)/shard_map/ppermute | solution.py:85
  40.9 1.0 %collective-permute-done.9 = bf16[64,2,64]{2,0,1:T(8,128)(2,1)S(1)} collective-permute-done((bf16[64,2,64]{2,0,1:T(8,128)(2,1)S(1)}, bf16[64,2,64]{2,0,1:T(8,128)(2,1)S(1)}, u32[]{:S(2)}, u32[]{:S(2)}) %collective-permute-start.9) | collective-permute-done | bytes 16416 | tf_op jit(solution)/shard_map/ppermute | solution.py:85
  42.0 3.1 %collective-permute-done.10 = bf16[64,2,64]{2,0,1:T(8,128)(2,1)S(1)} collective-permute-done((bf16[64,2,64]{2,0,1:T(8,128)(2,1)S(1)}, bf16[64,2,64]{2,0,1:T(8,128)(2,1)S(1)}, u32[]{:S(2)}, u32[]{:S(2)}) %collective-permute-start.10) | collective-permute-done | bytes 16416 | tf_op jit(solution)/shard_map/ppermute | solution.py:85
  45.1 0.9 %collective-permute-done.11 = bf16[64,2,64]{2,0,1:T(8,128)(2,1)S(1)} collective-permute-done((bf16[64,2,64]{2,0,1:T(8,128)(2,1)S(1)}, bf16[64,2,64]{2,0,1:T(8,128)(2,1)S(1)}, u32[]{:S(2)}, u32[]{:S(2)}) %collective-permute-start.11) | collective-permute-done | bytes 16416 | tf_op jit(solution)/shard_map/ppermute | solution.py:85
  46.1 1.7 %multiply_subtract_fusion = f32[2,16,64,64]{3,2,1,0:T(8,128)} fusion(f32[2,16,64,64]{3,2,1,0:T(8,128)S(1)} %copy-done, f32[64,64]{1,0:T(8,128)S(1)} %get-tuple-element.14, f32[2,16]{1,0:T(2,128)S(1)} %bitcast.105, f32[64,64]{1,0:T(8,128)S(1)} %get-tuple-element.15, f32[2,16]{1,0:T(2,128)S(1)} %bitcast.106, f32[64,64]{1,0:T(8,128)S(1)} %get-tuple-element.16, ...), kind=kLoop, calls=%fused_computation.1 | loop fusion | flops 2228224 | bytes 1180672 | tf_op jit(solution)/shard_map/sub | solution.py:278
  (47 shorter events, 1.8 us)
Async XLA Ops:
  3.7 9.6 %collective-permute-start.2 = (bf16[2,64,64]{2,1,0:T(8,128)(2,1)S(1)}, bf16[2,64,64]{2,1,0:T(8,128)(2,1)S(1)}, u32[]{:S(2)}, u32[]{:S(2)}) collective-permute-start(bf16[2,64,64]{2,1,0:T(8,128)(2,1)S(1)} %get-tuple-element.25), channel_id=1, source_target_pairs={{0,4},{4,8},{8,12},{12,0},{1,5},{5,9},{9,13},{13,1},{2,6},{6,10},{... | collective-permute-start | bytes 49160 | tf_op jit(solution)/shard_map/ppermute | solution.py:85
  6.8 6.5 %collective-permute-start.1 = (bf16[2,64,64]{2,1,0:T(8,128)(2,1)S(1)}, bf16[2,64,64]{2,1,0:T(8,128)(2,1)S(1)}, u32[]{:S(2)}, u32[]{:S(2)}) collective-permute-start(bf16[2,64,64]{2,1,0:T(8,128)(2,1)S(1)} %get-tuple-element.26), channel_id=1, source_target_pairs={{0,8},{4,12},{8,0},{12,4},{1,9},{5,13},{9,1},{13,5},{2,10},{6,14},... | collective-permute-start | bytes 49160 | tf_op jit(solution)/shard_map/ppermute | solution.py:85
  9.4 3.9 %collective-permute-start = (bf16[2,64,64]{2,1,0:T(8,128)(2,1)S(1)}, bf16[2,64,64]{2,1,0:T(8,128)(2,1)S(1)}, u32[]{:S(2)}, u32[]{:S(2)}) collective-permute-start(bf16[2,64,64]{2,1,0:T(8,128)(2,1)S(1)} %get-tuple-element.27), channel_id=1, source_target_pairs={{0,12},{4,0},{8,4},{12,8},{1,13},{5,1},{9,5},{13,9},{2,14},{6,2},{... | collective-permute-start | bytes 49160 | tf_op jit(solution)/shard_map/ppermute | solution.py:85
  13.7 5.9 %copy-start.1 = (bf16[64,512]{1,0:T(8,128)(2,1)}, bf16[64,512]{1,0:T(8,128)(2,1)S(1)}, u32[]{:S(2)}) copy-start(bf16[64,512]{1,0:T(8,128)(2,1)S(1)} %reshape.49.refs_0_) | copy-start | bytes 196612
  13.7 2.0 %collective-permute-start.5 = (bf16[64,512]{1,0:T(8,128)(2,1)S(1)}, bf16[64,512]{1,0:T(8,128)(2,1)S(1)}, u32[]{:S(2)}, u32[]{:S(2)}) collective-permute-start(bf16[64,512]{1,0:T(8,128)(2,1)S(1)} %reshape.49.refs_0_), channel_id=1, source_target_pairs={{0,3},{1,0},{2,1},{3,2},{4,7},{5,4},{6,5},{7,6},{8,11},{9,8},{10,9... | collective-permute-start | bytes 196616 | tf_op jit(solution)/shard_map/ppermute | solution.py:255
  13.8 5.6 %collective-permute-start.4 = (bf16[64,512]{1,0:T(8,128)(2,1)S(1)}, bf16[64,512]{1,0:T(8,128)(2,1)S(1)}, u32[]{:S(2)}, u32[]{:S(2)}) collective-permute-start(bf16[64,512]{1,0:T(8,128)(2,1)S(1)} %reshape.49.refs_0_), channel_id=1, source_target_pairs={{0,2},{1,3},{2,0},{3,1},{4,6},{5,7},{6,4},{7,5},{8,10},{9,11},{10,... | collective-permute-start | bytes 196616 | tf_op jit(solution)/shard_map/ppermute | solution.py:255
  15.3 4.3 %collective-permute-start.3 = (bf16[64,512]{1,0:T(8,128)(2,1)S(1)}, bf16[64,512]{1,0:T(8,128)(2,1)S(1)}, u32[]{:S(2)}, u32[]{:S(2)}) collective-permute-start(bf16[64,512]{1,0:T(8,128)(2,1)S(1)} %reshape.49.refs_0_), channel_id=1, source_target_pairs={{0,1},{1,2},{2,3},{3,0},{4,5},{5,6},{6,7},{7,4},{8,9},{9,10},{10,1... | collective-permute-start | bytes 196616 | tf_op jit(solution)/shard_map/ppermute | solution.py:255
  15.7 3.9 %copy-start.2 = (bf16[64,512]{1,0:T(8,128)(2,1)}, bf16[64,512]{1,0:T(8,128)(2,1)S(1)}, u32[]{:S(2)}) copy-start(bf16[64,512]{1,0:T(8,128)(2,1)S(1)} %collective-permute-done.5.refs_3_) | copy-start | bytes 196612
  19.4 0.6 %copy-start.3 = (bf16[64,512]{1,0:T(8,128)(2,1)}, bf16[64,512]{1,0:T(8,128)(2,1)S(1)}, u32[]{:S(2)}) copy-start(bf16[64,512]{1,0:T(8,128)(2,1)S(1)} %collective-permute-done.4.refs_2_) | copy-start | bytes 196612
  19.6 0.6 %copy-start.4 = (bf16[64,512]{1,0:T(8,128)(2,1)}, bf16[64,512]{1,0:T(8,128)(2,1)S(1)}, u32[]{:S(2)}) copy-start(bf16[64,512]{1,0:T(8,128)(2,1)S(1)} %collective-permute-done.3.refs_1_) | copy-start | bytes 196612
  30.4 15.7 %copy-start = (f32[2,16,64,64]{3,2,1,0:T(8,128)S(1)}, f32[2,16,64,64]{3,2,1,0:T(8,128)}, u32[]{:S(2)}) copy-start(f32[2,16,64,64]{3,2,1,0:T(8,128)} %param.9) | copy-start | bytes 1572868
  30.4 4.0 %collective-permute-start.6 = (bf16[64,512]{1,0:T(8,128)(2,1)}, bf16[64,512]{1,0:T(8,128)(2,1)S(1)}, u32[]{:S(2)}, u32[]{:S(2)}) collective-permute-start(bf16[64,512]{1,0:T(8,128)(2,1)} %get-tuple-element.10), channel_id=1, source_target_pairs={{0,1},{1,2},{2,3},{3,0},{4,5},{5,6},{6,7},{7,4},{8,9},{9,10},{10,1... | collective-permute-start | bytes 196616 | tf_op jit(solution)/shard_map/ppermute | solution.py:264
  30.5 5.2 %collective-permute-start.7 = (bf16[64,512]{1,0:T(8,128)(2,1)}, bf16[64,512]{1,0:T(8,128)(2,1)S(1)}, u32[]{:S(2)}, u32[]{:S(2)}) collective-permute-start(bf16[64,512]{1,0:T(8,128)(2,1)} %get-tuple-element.11), channel_id=1, source_target_pairs={{0,2},{1,3},{2,0},{3,1},{4,6},{5,7},{6,4},{7,5},{8,10},{9,11},{10,... | collective-permute-start | bytes 196616 | tf_op jit(solution)/shard_map/ppermute | solution.py:264
  31.4 4.3 %collective-permute-start.8 = (bf16[64,512]{1,0:T(8,128)(2,1)}, bf16[64,512]{1,0:T(8,128)(2,1)S(1)}, u32[]{:S(2)}, u32[]{:S(2)}) collective-permute-start(bf16[64,512]{1,0:T(8,128)(2,1)} %get-tuple-element.12), channel_id=1, source_target_pairs={{0,3},{1,0},{2,1},{3,2},{4,7},{5,4},{6,5},{7,6},{8,11},{9,8},{10,9... | collective-permute-start | bytes 196616 | tf_op jit(solution)/shard_map/ppermute | solution.py:264
  37.1 4.9 %collective-permute-start.9 = (bf16[64,2,64]{2,0,1:T(8,128)(2,1)S(1)}, bf16[64,2,64]{2,0,1:T(8,128)(2,1)S(1)}, u32[]{:S(2)}, u32[]{:S(2)}) collective-permute-start(bf16[64,2,64]{2,0,1:T(8,128)(2,1)S(1)} %bitcast.98), channel_id=1, source_target_pairs={{0,12},{4,0},{8,4},{12,8},{1,13},{5,1},{9,5},{13,9},{2,14},{6,2},{... | collective-permute-start | bytes 49160 | tf_op jit(solution)/shard_map/ppermute | solution.py:85
  40.3 4.8 %collective-permute-start.10 = (bf16[64,2,64]{2,0,1:T(8,128)(2,1)S(1)}, bf16[64,2,64]{2,0,1:T(8,128)(2,1)S(1)}, u32[]{:S(2)}, u32[]{:S(2)}) collective-permute-start(bf16[64,2,64]{2,0,1:T(8,128)(2,1)S(1)} %bitcast.97), channel_id=1, source_target_pairs={{0,8},{4,12},{8,0},{12,4},{1,9},{5,13},{9,1},{13,5},{2,10},{6,14},... | collective-permute-start | bytes 49160 | tf_op jit(solution)/shard_map/ppermute | solution.py:85
  40.3 5.7 %collective-permute-start.11 = (bf16[64,2,64]{2,0,1:T(8,128)(2,1)S(1)}, bf16[64,2,64]{2,0,1:T(8,128)(2,1)S(1)}, u32[]{:S(2)}, u32[]{:S(2)}) collective-permute-start(bf16[64,2,64]{2,0,1:T(8,128)(2,1)S(1)} %bitcast.96), channel_id=1, source_target_pairs={{0,4},{4,8},{8,12},{12,0},{1,5},{5,9},{9,13},{13,1},{2,6},{6,10},{... | collective-permute-start | bytes 49160 | tf_op jit(solution)/shard_map/ppermute | solution.py:85

commit v23 on v20

--- a/solution.py
+++ b/solution.py
@@ -248,7 +248,7 @@
     images = jnp.transpose(images, (1, 0, 2, 3)).astype(jnp.bfloat16)
     frames_here = images.shape[0]
     width_own = images.shape[3]
-    pieces_x = exchange_blocks(images, "frame")
+    pieces_x = lax.all_to_all(images, "frame", 0, 0, tiled=True)
     own_rows = jnp.transpose(pieces_x, (2, 1, 0, 3)).reshape(rows_own, 2 * width_x)
     groups = lax.axis_size("coil")
     me_c = lax.axis_index("coil")

time: 46.4 us -> 49.3 us (1.062)
  waiting for transfers between devices: 13.2 us -> 16.6 us
  starting transfers between devices: 15 us -> 13.3 us
  local copies, waits for them, and re-layouts: 2.92 us -> 4.04 us
    ppermute x6 -> x3, starting transfers between devices: 10.9 us -> 2.83 us  [exchange_blocks(): pieces.append(lax.ppermute(outgoing, axis, shifted(count, step)))]
    all_to_all x0 -> x1, starting transfers between devices: none -> 6.32 us  [on_device(): pieces_x = lax.all_to_all(images, 'frame', 0, 0, tiled=True)]
    all_to_all x0 -> x1, waiting for transfers between devices: none -> 4.36 us  [on_device(): pieces_x = lax.all_to_all(images, 'frame', 0, 0, tiled=True)]
    ppermute x6 -> x3, waiting for transfers between devices: 6.23 us -> 5.29 us  [exchange_blocks(): pieces.append(lax.ppermute(outgoing, axis, shifted(count, step)))]
    unnamed x27 -> x22, local copies, waits for them, and re-layouts: 0.8 us -> 1.66 us
  transfers between devices with their start and end apart: 12 -> 10, of which waited for: 9 -> 9; matrix products, arithmetic and copies ran while one was open for 3% -> 3% of each run, Pallas kernels for 0% -> 0%
where the time goes in v23:
time: 49.3 us; the launch traced here: 48.9 us
  waiting for transfers between devices  16.6 us (34%)
  starting transfers between devices  13.3 us (27%)
  Pallas kernels  8.42 us (17%)
  other arithmetic  6.34 us (13%)
  local copies, waits for them, and re-layouts  4.04 us (8%)
    pallas_call x1, Pallas kernels, coil_chain(): pl.pallas_call(coil_chain_kernel, out_shape=(jax.ShapeDtypeStruct((rows,...  8.42 us
    all_to_all x1, starting transfers between devices, on_device(): pieces_x = lax.all_to_all(images, 'frame', 0, 0, tiled=True)  6.32 us
    ppermute x3, waiting for transfers between devices, exchange_blocks(): pieces.append(lax.ppermute(outgoing, axis, shifted(count, step)))  5.29 us
    all_to_all x1, waiting for transfers between devices, on_device(): pieces_x = lax.all_to_all(images, 'frame', 0, 0, tiled=True)  4.36 us
    ppermute x3, waiting for transfers between devices, on_device(): lax.ppermute(own_rows, 'coil', shifted(groups, step))  4.1 us
    ppermute x3, waiting for transfers between devices, on_device(): lax.ppermute(outgoing[step - 1], 'coil', shifted(groups, step))  2.86 us
    ppermute x3, starting transfers between devices, exchange_blocks(): pieces.append(lax.ppermute(outgoing, axis, shifted(count, step)))  2.83 us
    ppermute x3, starting transfers between devices, on_device(): lax.ppermute(outgoing[step - 1], 'coil', shifted(groups, step))  2.38 us
  transfers between devices with their start and end apart: 10, of which 9 were waited for; matrix products, arithmetic and copies ran while one was open for 3% of the time, Pallas kernels for 0%

profile of v23, /device:TPU:0, one launch (start us, length us, event | category | flops | bytes accessed | tf_op | source)
XLA Modules:
  0.0 48.9 jit_solution(1687522958367993171)
XLA Ops:
  0.0 0.7 %reverse_bitcast_fusion = f32[1,2,4,16]{3,2,1,0:T(4,128)S(1)} fusion(f32[2,4,16]{2,1,0:T(4,128)} %param.10), kind=kLoop, calls=%fused_computation.42 | loop fusion | bytes 1024 | tf_op jit(solution)/shard_map/stack | solution.py:244
  0.7 0.8 %maximum_multiply_fusion = f32[2,2,4,16]{3,2,1,0:T(4,128)S(1)} fusion(f32[1,2,4,16]{3,2,1,0:T(4,128)S(1)} %reverse_bitcast_fusion, f32[1,2,4,16]{3,2,1,0:T(4,128)} %bitcast.87, f32[2,2]{1,0:T(2,128)} %constant.65.clone), kind=kLoop, calls=%fused_computation.39 | loop fusion | flops 512 | bytes 2064 | tf_op jit(solution)/shard_map/mul | solution.py:244
  1.5 2.2 %multiply_reduce_fusion = bf16[2,4,64,64]{3,2,1,0:T(8,128)(2,1)S(1)} fusion(f32[2,16,64,64]{3,2,1,0:T(8,128)} %param.9, f32[2,2,4,16]{3,2,1,0:T(4,128)S(1)} %maximum_multiply_fusion), kind=kLoop, calls=%fused_computation | loop fusion | flops 2064384 | bytes 590848 | tf_op jit(solution)/shard_map/reduce_sum | solution.py:245
  3.8 0.8 %reshape.44 = bf16[4,2,4096]{2,1,0:T(2,128)(2,1)} reshape(bf16[4,64,2,64]{3,2,1,0:T(2,128)(2,1)S(1)} %bitcast.86) | data formatting | bytes 131072
  4.6 6.3 %all-to-all-start = ((bf16[4,2,4096]{2,1,0:T(2,128)(2,1)}), bf16[4,2,4096]{2,1,0:T(2,128)(2,1)S(1)}, u32[]{:S(2)}, u32[]{:S(2)}) async-start(bf16[4,2,4096]{2,1,0:T(2,128)(2,1)} %reshape.44), calls=%async_computation | async-start | bytes 131072 | tf_op jit(solution)/shard_map/all_to_all | solution.py:251
  11.0 0.7 %slice_bitcast_fusion.9 = (f32[16,4,1]{0,1,2:T(4,128)S(1)}, f32[16,4,1]{0,1,2:T(4,128)S(1)}) fusion(f32[2,4,16]{2,1,0:T(4,128)} %param.10), kind=kLoop, calls=%fused_computation.46 | loop fusion | bytes 1024 | tf_op jit(solution)/shard_map/stack | solution.py:271
  11.7 0.7 %fusion = f32[16,4,1]{0,1,2:T(4,128)S(1)} fusion(f32[2,4,16]{2,1,0:T(4,128)} %param.10), kind=kLoop, calls=%fused_computation.45 | loop fusion | flops 64 | bytes 512 | tf_op jit(solution)/shard_map/stack | solution.py:271
  12.3 4.4 %all-to-all-done = bf16[4,2,4096]{2,1,0:T(2,128)(2,1)S(1)} async-done(((bf16[4,2,4096]{2,1,0:T(2,128)(2,1)}), bf16[4,2,4096]{2,1,0:T(2,128)(2,1)S(1)}, u32[]{:S(2)}, u32[]{:S(2)}) %all-to-all-start) | async-done | bytes 65568 | tf_op jit(solution)/shard_map/all_to_all | solution.py:251
  17.4 1.6 %collective-permute-start.1 = (bf16[64,512]{1,0:T(8,128)(2,1)S(1)}, bf16[64,512]{1,0:T(8,128)(2,1)S(1)}, u32[]{:S(2)}, u32[]{:S(2)}) collective-permute-start(bf16[64,512]{1,0:T(8,128)(2,1)S(1)} %reshape.42.refs_0_), channel_id=1, source_target_pairs={{0,2},{1,3},{2,0},{3,1},{4,6},{5,7},{6,4},{7,5},{8,10},{9,11},{10,... | collective-permute-start | bytes 196616 | tf_op jit(solution)/shard_map/ppermute | solution.py:255
  19.3 3.7 %collective-permute-done.1.refs_2_ = bf16[64,512]{1,0:T(8,128)(2,1)S(1)} collective-permute-done((bf16[64,512]{1,0:T(8,128)(2,1)S(1)}, bf16[64,512]{1,0:T(8,128)(2,1)S(1)}, u32[]{:S(2)}, u32[]{:S(2)}) %collective-permute-start.1) | collective-permute-done | bytes 65568 | tf_op jit(solution)/shard_map/ppermute | solution.py:255
  23.2 0.4 copy-done.3
  23.8 8.4 %shard_map.91 = (f32[64,512]{1,0:T(8,128)}, bf16[64,512]{1,0:T(8,128)(2,1)}, bf16[64,512]{1,0:T(8,128)(2,1)}, bf16[64,512]{1,0:T(8,128)(2,1)}) custom-call(bf16[64,512]{1,0:T(8,128)(2,1)} %copy-done.1, bf16[64,512]{1,0:T(8,128)(2,1)} %copy-done.4, bf16[64,512]{1,0:T(8,128)(2,1)} %copy-done.3, bf16[64,512]{1,0:T(8,128)(2,1)} %copy-done.2, s32[1]{0:T(128)} %bitcast.17.refs_4_, ...), custom_call_target="tpu_custom_call" | custom-call | flops 4294967296 | bytes 4718592 | tf_op jit(solution)/shard_map/pallas_call | solution.py:208
  32.3 0.9 %collective-permute-start.4 = (bf16[64,512]{1,0:T(8,128)(2,1)}, bf16[64,512]{1,0:T(8,128)(2,1)S(1)}, u32[]{:S(2)}, u32[]{:S(2)}) collective-permute-start(bf16[64,512]{1,0:T(8,128)(2,1)} %get-tuple-element.11), channel_id=1, source_target_pairs={{0,2},{1,3},{2,0},{3,1},{4,6},{5,7},{6,4},{7,5},{8,10},{9,11},{10,... | collective-permute-start | bytes 196616 | tf_op jit(solution)/shard_map/ppermute | solution.py:264
  33.2 1.4 %collective-permute-start.5 = (bf16[64,512]{1,0:T(8,128)(2,1)}, bf16[64,512]{1,0:T(8,128)(2,1)S(1)}, u32[]{:S(2)}, u32[]{:S(2)}) collective-permute-start(bf16[64,512]{1,0:T(8,128)(2,1)} %get-tuple-element.12), channel_id=1, source_target_pairs={{0,3},{1,0},{2,1},{3,2},{4,7},{5,4},{6,5},{7,6},{8,11},{9,8},{10,9... | collective-permute-start | bytes 196616 | tf_op jit(solution)/shard_map/ppermute | solution.py:264
  34.6 1.6 %collective-permute-done.3 = bf16[64,512]{1,0:T(8,128)(2,1)S(1)} collective-permute-done((bf16[64,512]{1,0:T(8,128)(2,1)}, bf16[64,512]{1,0:T(8,128)(2,1)S(1)}, u32[]{:S(2)}, u32[]{:S(2)}) %collective-permute-start.3) | collective-permute-done | bytes 65568 | tf_op jit(solution)/shard_map/ppermute | solution.py:264
  36.3 1.2 %collective-permute-done.4 = bf16[64,512]{1,0:T(8,128)(2,1)S(1)} collective-permute-done((bf16[64,512]{1,0:T(8,128)(2,1)}, bf16[64,512]{1,0:T(8,128)(2,1)S(1)}, u32[]{:S(2)}, u32[]{:S(2)}) %collective-permute-start.4) | collective-permute-done | bytes 65568 | tf_op jit(solution)/shard_map/ppermute | solution.py:264
  37.5 0.9 %add_convert_fusion = bf16[64,512]{1,0:T(8,128)(2,1)S(1)} fusion(bf16[64,512]{1,0:T(8,128)(2,1)S(1)} %collective-permute-done.5, bf16[64,512]{1,0:T(8,128)(2,1)S(1)} %collective-permute-done.4, f32[64,512]{1,0:T(8,128)} %get-tuple-element.9, bf16[64,512]{1,0:T(8,128)(2,1)S(1)} %collective-permute-done.3), kind=kLoop, calls=%fused_computation.3 | loop fusion | flops 229376 | bytes 393216 | tf_op jit(solution)/shard_map/convert_element_type | solution.py:267
  38.9 0.8 %collective-permute-start.6 = (bf16[64,2,64]{2,0,1:T(8,128)(2,1)S(1)}, bf16[64,2,64]{2,0,1:T(8,128)(2,1)S(1)}, u32[]{:S(2)}, u32[]{:S(2)}) collective-permute-start(bf16[64,2,64]{2,0,1:T(8,128)(2,1)S(1)} %bitcast.90), channel_id=1, source_target_pairs={{0,12},{4,0},{8,4},{12,8},{1,13},{5,1},{9,5},{13,9},{2,14},{6,2},{... | collective-permute-start | bytes 49160 | tf_op jit(solution)/shard_map/ppermute | solution.py:85
  39.7 1.6 %collective-permute-start.7 = (bf16[64,2,64]{2,0,1:T(8,128)(2,1)S(1)}, bf16[64,2,64]{2,0,1:T(8,128)(2,1)S(1)}, u32[]{:S(2)}, u32[]{:S(2)}) collective-permute-start(bf16[64,2,64]{2,0,1:T(8,128)(2,1)S(1)} %bitcast.89), channel_id=1, source_target_pairs={{0,8},{4,12},{8,0},{12,4},{1,9},{5,13},{9,1},{13,5},{2,10},{6,14},... | collective-permute-start | bytes 49160 | tf_op jit(solution)/shard_map/ppermute | solution.py:85
  41.3 0.4 collective-permute-start.8
  41.7 1.1 %collective-permute-done.6 = bf16[64,2,64]{2,0,1:T(8,128)(2,1)S(1)} collective-permute-done((bf16[64,2,64]{2,0,1:T(8,128)(2,1)S(1)}, bf16[64,2,64]{2,0,1:T(8,128)(2,1)S(1)}, u32[]{:S(2)}, u32[]{:S(2)}) %collective-permute-start.6) | collective-permute-done | bytes 16416 | tf_op jit(solution)/shard_map/ppermute | solution.py:85
  42.9 2.0 %collective-permute-done.7 = bf16[64,2,64]{2,0,1:T(8,128)(2,1)S(1)} collective-permute-done((bf16[64,2,64]{2,0,1:T(8,128)(2,1)S(1)}, bf16[64,2,64]{2,0,1:T(8,128)(2,1)S(1)}, u32[]{:S(2)}, u32[]{:S(2)}) %collective-permute-start.7) | collective-permute-done | bytes 16416 | tf_op jit(solution)/shard_map/ppermute | solution.py:85
  44.9 2.2 %collective-permute-done.8 = bf16[64,2,64]{2,0,1:T(8,128)(2,1)S(1)} collective-permute-done((bf16[64,2,64]{2,0,1:T(8,128)(2,1)S(1)}, bf16[64,2,64]{2,0,1:T(8,128)(2,1)S(1)}, u32[]{:S(2)}, u32[]{:S(2)}) %collective-permute-start.8) | collective-permute-done | bytes 16416 | tf_op jit(solution)/shard_map/ppermute | solution.py:85
  47.2 1.7 %multiply_subtract_fusion = f32[2,16,64,64]{3,2,1,0:T(8,128)} fusion(f32[2,16,64,64]{3,2,1,0:T(8,128)S(1)} %copy-done, f32[64,64]{1,0:T(8,128)S(1)} %get-tuple-element.14, f32[2,16]{1,0:T(2,128)S(1)} %bitcast.97, f32[64,64]{1,0:T(8,128)S(1)} %get-tuple-element.15, f32[2,16]{1,0:T(2,128)S(1)} %bitcast.98, f32[64,64]{1,0:T(8,128)S(1)} %get-tuple-element.16, ...), kind=kLoop, calls=%fused_computation.1 | loop fusion | flops 2228224 | bytes 1180672 | tf_op jit(solution)/shard_map/sub | solution.py:278
  (37 shorter events, 2.1 us)
Async XLA Ops:
  4.6 12.1 %all-to-all-start = ((bf16[4,2,4096]{2,1,0:T(2,128)(2,1)}), bf16[4,2,4096]{2,1,0:T(2,128)(2,1)S(1)}, u32[]{:S(2)}, u32[]{:S(2)}) async-start(bf16[4,2,4096]{2,1,0:T(2,128)(2,1)} %reshape.44), calls=%async_computation | async-start | bytes 131072 | tf_op jit(solution)/shard_map/all_to_all | solution.py:251
  17.3 5.9 %copy-start.1 = (bf16[64,512]{1,0:T(8,128)(2,1)}, bf16[64,512]{1,0:T(8,128)(2,1)S(1)}, u32[]{:S(2)}) copy-start(bf16[64,512]{1,0:T(8,128)(2,1)S(1)} %reshape.42.refs_0_) | copy-start | bytes 196612
  17.3 2.0 %collective-permute-start.2 = (bf16[64,512]{1,0:T(8,128)(2,1)S(1)}, bf16[64,512]{1,0:T(8,128)(2,1)S(1)}, u32[]{:S(2)}, u32[]{:S(2)}) collective-permute-start(bf16[64,512]{1,0:T(8,128)(2,1)S(1)} %reshape.42.refs_0_), channel_id=1, source_target_pairs={{0,3},{1,0},{2,1},{3,2},{4,7},{5,4},{6,5},{7,6},{8,11},{9,8},{10,9... | collective-permute-start | bytes 196616 | tf_op jit(solution)/shard_map/ppermute | solution.py:255
  17.4 5.6 %collective-permute-start.1 = (bf16[64,512]{1,0:T(8,128)(2,1)S(1)}, bf16[64,512]{1,0:T(8,128)(2,1)S(1)}, u32[]{:S(2)}, u32[]{:S(2)}) collective-permute-start(bf16[64,512]{1,0:T(8,128)(2,1)S(1)} %reshape.42.refs_0_), channel_id=1, source_target_pairs={{0,2},{1,3},{2,0},{3,1},{4,6},{5,7},{6,4},{7,5},{8,10},{9,11},{10,... | collective-permute-start | bytes 196616 | tf_op jit(solution)/shard_map/ppermute | solution.py:255
  18.9 4.3 %collective-permute-start = (bf16[64,512]{1,0:T(8,128)(2,1)S(1)}, bf16[64,512]{1,0:T(8,128)(2,1)S(1)}, u32[]{:S(2)}, u32[]{:S(2)}) collective-permute-start(bf16[64,512]{1,0:T(8,128)(2,1)S(1)} %reshape.42.refs_0_), channel_id=1, source_target_pairs={{0,1},{1,2},{2,3},{3,0},{4,5},{5,6},{6,7},{7,4},{8,9},{9,10},{10,1... | collective-permute-start | bytes 196616 | tf_op jit(solution)/shard_map/ppermute | solution.py:255
  19.2 3.9 %copy-start.2 = (bf16[64,512]{1,0:T(8,128)(2,1)}, bf16[64,512]{1,0:T(8,128)(2,1)S(1)}, u32[]{:S(2)}) copy-start(bf16[64,512]{1,0:T(8,128)(2,1)S(1)} %collective-permute-done.2.refs_3_) | copy-start | bytes 196612
  23.0 0.6 %copy-start.3 = (bf16[64,512]{1,0:T(8,128)(2,1)}, bf16[64,512]{1,0:T(8,128)(2,1)S(1)}, u32[]{:S(2)}) copy-start(bf16[64,512]{1,0:T(8,128)(2,1)S(1)} %collective-permute-done.1.refs_2_) | copy-start | bytes 196612
  23.2 0.6 %copy-start.4 = (bf16[64,512]{1,0:T(8,128)(2,1)}, bf16[64,512]{1,0:T(8,128)(2,1)S(1)}, u32[]{:S(2)}) copy-start(bf16[64,512]{1,0:T(8,128)(2,1)S(1)} %collective-permute-done.refs_1_) | copy-start | bytes 196612
  32.2 15.0 %copy-start = (f32[2,16,64,64]{3,2,1,0:T(8,128)S(1)}, f32[2,16,64,64]{3,2,1,0:T(8,128)}, u32[]{:S(2)}) copy-start(f32[2,16,64,64]{3,2,1,0:T(8,128)} %param.9) | copy-start | bytes 1572868
  32.2 4.0 %collective-permute-start.3 = (bf16[64,512]{1,0:T(8,128)(2,1)}, bf16[64,512]{1,0:T(8,128)(2,1)S(1)}, u32[]{:S(2)}, u32[]{:S(2)}) collective-permute-start(bf16[64,512]{1,0:T(8,128)(2,1)} %get-tuple-element.10), channel_id=1, source_target_pairs={{0,1},{1,2},{2,3},{3,0},{4,5},{5,6},{6,7},{7,4},{8,9},{9,10},{10,1... | collective-permute-start | bytes 196616 | tf_op jit(solution)/shard_map/ppermute | solution.py:264
  32.3 5.2 %collective-permute-start.4 = (bf16[64,512]{1,0:T(8,128)(2,1)}, bf16[64,512]{1,0:T(8,128)(2,1)S(1)}, u32[]{:S(2)}, u32[]{:S(2)}) collective-permute-start(bf16[64,512]{1,0:T(8,128)(2,1)} %get-tuple-element.11), channel_id=1, source_target_pairs={{0,2},{1,3},{2,0},{3,1},{4,6},{5,7},{6,4},{7,5},{8,10},{9,11},{10,... | collective-permute-start | bytes 196616 | tf_op jit(solution)/shard_map/ppermute | solution.py:264
  33.2 4.3 %collective-permute-start.5 = (bf16[64,512]{1,0:T(8,128)(2,1)}, bf16[64,512]{1,0:T(8,128)(2,1)S(1)}, u32[]{:S(2)}, u32[]{:S(2)}) collective-permute-start(bf16[64,512]{1,0:T(8,128)(2,1)} %get-tuple-element.12), channel_id=1, source_target_pairs={{0,3},{1,0},{2,1},{3,2},{4,7},{5,4},{6,5},{7,6},{8,11},{9,8},{10,9... | collective-permute-start | bytes 196616 | tf_op jit(solution)/shard_map/ppermute | solution.py:264
  38.9 4.0 %collective-permute-start.6 = (bf16[64,2,64]{2,0,1:T(8,128)(2,1)S(1)}, bf16[64,2,64]{2,0,1:T(8,128)(2,1)S(1)}, u32[]{:S(2)}, u32[]{:S(2)}) collective-permute-start(bf16[64,2,64]{2,0,1:T(8,128)(2,1)S(1)} %bitcast.90), channel_id=1, source_target_pairs={{0,12},{4,0},{8,4},{12,8},{1,13},{5,1},{9,5},{13,9},{2,14},{6,2},{... | collective-permute-start | bytes 49160 | tf_op jit(solution)/shard_map/ppermute | solution.py:85
  39.7 5.2 %collective-permute-start.7 = (bf16[64,2,64]{2,0,1:T(8,128)(2,1)S(1)}, bf16[64,2,64]{2,0,1:T(8,128)(2,1)S(1)}, u32[]{:S(2)}, u32[]{:S(2)}) collective-permute-start(bf16[64,2,64]{2,0,1:T(8,128)(2,1)S(1)} %bitcast.89), channel_id=1, source_target_pairs={{0,8},{4,12},{8,0},{12,4},{1,9},{5,13},{9,1},{13,5},{2,10},{6,14},... | collective-permute-start | bytes 49160 | tf_op jit(solution)/shard_map/ppermute | solution.py:85
  41.3 5.7 %collective-permute-start.8 = (bf16[64,2,64]{2,0,1:T(8,128)(2,1)S(1)}, bf16[64,2,64]{2,0,1:T(8,128)(2,1)S(1)}, u32[]{:S(2)}, u32[]{:S(2)}) collective-permute-start(bf16[64,2,64]{2,0,1:T(8,128)(2,1)S(1)} %bitcast.88), channel_id=1, source_target_pairs={{0,4},{4,8},{8,12},{12,0},{1,5},{5,9},{9,13},{13,1},{2,6},{6,10},{... | collective-permute-start | bytes 49160 | tf_op jit(solution)/shard_map/ppermute | solution.py:85

commit v24 on v22

--- a/solution.py
+++ b/solution.py
@@ -203,7 +203,7 @@
     rows = pieces[0].shape[0]
     whole = lambda c: (0, 0)
     per_coil = lambda c: (c, 0, 0)
-    step_coils = 2 if coils % 2 == 0 else 1
+    step_coils = 8 if coils % 8 == 0 else (4 if coils % 4 == 0 else (2 if coils % 2 == 0 else 1))
     flops = coils * 8 * height * width * width
     return pl.pallas_call(
         coil_chain_kernel,

time: 48.1 us -> 46.8 us (0.973)
  Pallas kernels: 10.2 us -> 8.93 us
    pallas_call x1, Pallas kernels: 10.2 us -> 8.93 us  [coil_chain(): pl.pallas_call(coil_chain_kernel, out_shape=(jax.ShapeDtypeStruct((rows,...]
where the time goes in v24:
time: 46.8 us; the launch traced here: 46.6 us
  starting transfers between devices  15 us (32%)
  waiting for transfers between devices  13.2 us (28%)
  Pallas kernels  8.93 us (19%)
  other arithmetic  6.34 us (14%)
  local copies, waits for them, and re-layouts  2.92 us (6%)
    ppermute x6, starting transfers between devices, exchange_blocks(): pieces.append(lax.ppermute(outgoing, axis, shifted(count, step)))  10.9 us
    pallas_call x1, Pallas kernels, coil_chain(): pl.pallas_call(coil_chain_kernel, out_shape=(jax.ShapeDtypeStruct((rows,...  8.93 us
    ppermute x6, waiting for transfers between devices, exchange_blocks(): pieces.append(lax.ppermute(outgoing, axis, shifted(count, step)))  6.23 us
    ppermute x3, waiting for transfers between devices, on_device(): lax.ppermute(own_rows, 'coil', shifted(groups, step))  4.1 us
    ppermute x3, waiting for transfers between devices, on_device(): lax.ppermute(outgoing[step - 1], 'coil', shifted(groups, step))  2.86 us
    ppermute x3, starting transfers between devices, on_device(): lax.ppermute(outgoing[step - 1], 'coil', shifted(groups, step))  2.37 us
    reduce_sum x1, other arithmetic, on_device(): jnp.sum(mixing[:, :, :, :, None, None] * factors[None, :, None], axis=(1,...  2.23 us
    ppermute x3, starting transfers between devices, on_device(): lax.ppermute(own_rows, 'coil', shifted(groups, step))  1.78 us
  transfers between devices with their start and end apart: 12, of which 9 were waited for; matrix products, arithmetic and copies ran while one was open for 3% of the time, Pallas kernels for 0%

profile of v24, /device:TPU:0, one launch (start us, length us, event | category | flops | bytes accessed | tf_op | source)
XLA Modules:
  0.0 46.6 jit_solution(17094814363631779814)
XLA Ops:
  0.0 0.7 %reverse_bitcast_fusion = f32[1,2,4,16]{3,2,1,0:T(4,128)S(1)} fusion(f32[2,4,16]{2,1,0:T(4,128)} %param.10), kind=kLoop, calls=%fused_computation.53 | loop fusion | bytes 1024 | tf_op jit(solution)/shard_map/stack | solution.py:244
  0.7 0.8 %maximum_multiply_fusion = f32[2,2,4,16]{3,2,1,0:T(4,128)S(1)} fusion(f32[1,2,4,16]{3,2,1,0:T(4,128)S(1)} %reverse_bitcast_fusion, f32[1,2,4,16]{3,2,1,0:T(4,128)} %bitcast.95, f32[2,2]{1,0:T(2,128)} %constant.83.clone), kind=kLoop, calls=%fused_computation.50 | loop fusion | flops 512 | bytes 2064 | tf_op jit(solution)/shard_map/mul | solution.py:244
  1.5 2.2 %multiply_reduce_fusion = bf16[2,4,64,64]{3,2,1,0:T(8,128)(2,1)S(1)} fusion(f32[2,16,64,64]{3,2,1,0:T(8,128)} %param.9, f32[2,2,4,16]{3,2,1,0:T(4,128)S(1)} %maximum_multiply_fusion), kind=kLoop, calls=%fused_computation | loop fusion | flops 2064384 | bytes 590848 | tf_op jit(solution)/shard_map/reduce_sum | solution.py:245
  3.7 3.1 %collective-permute-start.2 = (bf16[2,64,64]{2,1,0:T(8,128)(2,1)S(1)}, bf16[2,64,64]{2,1,0:T(8,128)(2,1)S(1)}, u32[]{:S(2)}, u32[]{:S(2)}) collective-permute-start(bf16[2,64,64]{2,1,0:T(8,128)(2,1)S(1)} %get-tuple-element.25), channel_id=1, source_target_pairs={{0,4},{4,8},{8,12},{12,0},{1,5},{5,9},{9,13},{13,1},{2,6},{6,10},{... | collective-permute-start | bytes 49160 | tf_op jit(solution)/shard_map/ppermute | solution.py:85
  6.8 2.6 %collective-permute-start.1 = (bf16[2,64,64]{2,1,0:T(8,128)(2,1)S(1)}, bf16[2,64,64]{2,1,0:T(8,128)(2,1)S(1)}, u32[]{:S(2)}, u32[]{:S(2)}) collective-permute-start(bf16[2,64,64]{2,1,0:T(8,128)(2,1)S(1)} %get-tuple-element.26), channel_id=1, source_target_pairs={{0,8},{4,12},{8,0},{12,4},{1,9},{5,13},{9,1},{13,5},{2,10},{6,14},... | collective-permute-start | bytes 49160 | tf_op jit(solution)/shard_map/ppermute | solution.py:85
  9.4 1.3 %collective-permute-start = (bf16[2,64,64]{2,1,0:T(8,128)(2,1)S(1)}, bf16[2,64,64]{2,1,0:T(8,128)(2,1)S(1)}, u32[]{:S(2)}, u32[]{:S(2)}) collective-permute-start(bf16[2,64,64]{2,1,0:T(8,128)(2,1)S(1)} %get-tuple-element.27), channel_id=1, source_target_pairs={{0,12},{4,0},{8,4},{12,8},{1,13},{5,1},{9,5},{13,9},{2,14},{6,2},{... | collective-permute-start | bytes 49160 | tf_op jit(solution)/shard_map/ppermute | solution.py:85
  10.7 0.7 %fusion = f32[16,4,1]{0,1,2:T(4,128)S(1)} fusion(f32[2,4,16]{2,1,0:T(4,128)} %param.10), kind=kLoop, calls=%fused_computation.60 | loop fusion | flops 64 | bytes 512 | tf_op jit(solution)/shard_map/stack | solution.py:271
  11.4 0.7 %slice_bitcast_fusion.9 = (f32[16,4,1]{0,1,2:T(4,128)S(1)}, f32[16,4,1]{0,1,2:T(4,128)S(1)}) fusion(f32[2,4,16]{2,1,0:T(4,128)} %param.10), kind=kLoop, calls=%fused_computation.61 | loop fusion | bytes 1024 | tf_op jit(solution)/shard_map/stack | solution.py:271
  12.1 1.2 %collective-permute-done = bf16[2,64,64]{2,1,0:T(8,128)(2,1)S(1)} collective-permute-done((bf16[2,64,64]{2,1,0:T(8,128)(2,1)S(1)}, bf16[2,64,64]{2,1,0:T(8,128)(2,1)S(1)}, u32[]{:S(2)}, u32[]{:S(2)}) %collective-permute-start) | collective-permute-done | bytes 16416 | tf_op jit(solution)/shard_map/ppermute | solution.py:85
  13.8 1.6 %collective-permute-start.4 = (bf16[64,512]{1,0:T(8,128)(2,1)S(1)}, bf16[64,512]{1,0:T(8,128)(2,1)S(1)}, u32[]{:S(2)}, u32[]{:S(2)}) collective-permute-start(bf16[64,512]{1,0:T(8,128)(2,1)S(1)} %reshape.49.refs_0_), channel_id=1, source_target_pairs={{0,2},{1,3},{2,0},{3,1},{4,6},{5,7},{6,4},{7,5},{8,10},{9,11},{10,... | collective-permute-start | bytes 196616 | tf_op jit(solution)/shard_map/ppermute | solution.py:255
  15.7 3.7 %collective-permute-done.4.refs_2_ = bf16[64,512]{1,0:T(8,128)(2,1)S(1)} collective-permute-done((bf16[64,512]{1,0:T(8,128)(2,1)S(1)}, bf16[64,512]{1,0:T(8,128)(2,1)S(1)}, u32[]{:S(2)}, u32[]{:S(2)}) %collective-permute-start.4) | collective-permute-done | bytes 65568 | tf_op jit(solution)/shard_map/ppermute | solution.py:255
  19.6 0.4 copy-done.3
  20.2 8.9 %shard_map.91 = (f32[64,512]{1,0:T(8,128)}, bf16[64,512]{1,0:T(8,128)(2,1)}, bf16[64,512]{1,0:T(8,128)(2,1)}, bf16[64,512]{1,0:T(8,128)(2,1)}) custom-call(bf16[64,512]{1,0:T(8,128)(2,1)} %copy-done.1, bf16[64,512]{1,0:T(8,128)(2,1)} %copy-done.4, bf16[64,512]{1,0:T(8,128)(2,1)} %copy-done.3, bf16[64,512]{1,0:T(8,128)(2,1)} %copy-done.2, s32[1]{0:T(128)} %bitcast.23.refs_4_, ...), custom_call_target="tpu_custom_call" | custom-call | flops 4294967296 | bytes 4718592 | tf_op jit(solution)/shard_map/pallas_call | solution.py:208
  29.2 0.9 %collective-permute-start.7 = (bf16[64,512]{1,0:T(8,128)(2,1)}, bf16[64,512]{1,0:T(8,128)(2,1)S(1)}, u32[]{:S(2)}, u32[]{:S(2)}) collective-permute-start(bf16[64,512]{1,0:T(8,128)(2,1)} %get-tuple-element.11), channel_id=1, source_target_pairs={{0,2},{1,3},{2,0},{3,1},{4,6},{5,7},{6,4},{7,5},{8,10},{9,11},{10,... | collective-permute-start | bytes 196616 | tf_op jit(solution)/shard_map/ppermute | solution.py:264
  30.2 1.4 %collective-permute-start.8 = (bf16[64,512]{1,0:T(8,128)(2,1)}, bf16[64,512]{1,0:T(8,128)(2,1)S(1)}, u32[]{:S(2)}, u32[]{:S(2)}) collective-permute-start(bf16[64,512]{1,0:T(8,128)(2,1)} %get-tuple-element.12), channel_id=1, source_target_pairs={{0,3},{1,0},{2,1},{3,2},{4,7},{5,4},{6,5},{7,6},{8,11},{9,8},{10,9... | collective-permute-start | bytes 196616 | tf_op jit(solution)/shard_map/ppermute | solution.py:264
  31.6 1.6 %collective-permute-done.6 = bf16[64,512]{1,0:T(8,128)(2,1)S(1)} collective-permute-done((bf16[64,512]{1,0:T(8,128)(2,1)}, bf16[64,512]{1,0:T(8,128)(2,1)S(1)}, u32[]{:S(2)}, u32[]{:S(2)}) %collective-permute-start.6) | collective-permute-done | bytes 65568 | tf_op jit(solution)/shard_map/ppermute | solution.py:264
  33.2 1.2 %collective-permute-done.7 = bf16[64,512]{1,0:T(8,128)(2,1)S(1)} collective-permute-done((bf16[64,512]{1,0:T(8,128)(2,1)}, bf16[64,512]{1,0:T(8,128)(2,1)S(1)}, u32[]{:S(2)}, u32[]{:S(2)}) %collective-permute-start.7) | collective-permute-done | bytes 65568 | tf_op jit(solution)/shard_map/ppermute | solution.py:264
  34.4 0.9 %add_convert_fusion = bf16[64,512]{1,0:T(8,128)(2,1)S(1)} fusion(bf16[64,512]{1,0:T(8,128)(2,1)S(1)} %collective-permute-done.8, bf16[64,512]{1,0:T(8,128)(2,1)S(1)} %collective-permute-done.7, f32[64,512]{1,0:T(8,128)} %get-tuple-element.9, bf16[64,512]{1,0:T(8,128)(2,1)S(1)} %collective-permute-done.6), kind=kLoop, calls=%fused_computation.3 | loop fusion | flops 229376 | bytes 393216 | tf_op jit(solution)/shard_map/convert_element_type | solution.py:267
  35.8 3.2 %collective-permute-start.9 = (bf16[64,2,64]{2,0,1:T(8,128)(2,1)S(1)}, bf16[64,2,64]{2,0,1:T(8,128)(2,1)S(1)}, u32[]{:S(2)}, u32[]{:S(2)}) collective-permute-start(bf16[64,2,64]{2,0,1:T(8,128)(2,1)S(1)} %bitcast.98), channel_id=1, source_target_pairs={{0,12},{4,0},{8,4},{12,8},{1,13},{5,1},{9,5},{13,9},{2,14},{6,2},{... | collective-permute-start | bytes 49160 | tf_op jit(solution)/shard_map/ppermute | solution.py:85
  39.0 0.6 %collective-permute-start.11 = (bf16[64,2,64]{2,0,1:T(8,128)(2,1)S(1)}, bf16[64,2,64]{2,0,1:T(8,128)(2,1)S(1)}, u32[]{:S(2)}, u32[]{:S(2)}) collective-permute-start(bf16[64,2,64]{2,0,1:T(8,128)(2,1)S(1)} %bitcast.96), channel_id=1, source_target_pairs={{0,4},{4,8},{8,12},{12,0},{1,5},{5,9},{9,13},{13,1},{2,6},{6,10},{... | collective-permute-start | bytes 49160 | tf_op jit(solution)/shard_map/ppermute | solution.py:85
  39.7 1.0 %collective-permute-done.9 = bf16[64,2,64]{2,0,1:T(8,128)(2,1)S(1)} collective-permute-done((bf16[64,2,64]{2,0,1:T(8,128)(2,1)S(1)}, bf16[64,2,64]{2,0,1:T(8,128)(2,1)S(1)}, u32[]{:S(2)}, u32[]{:S(2)}) %collective-permute-start.9) | collective-permute-done | bytes 16416 | tf_op jit(solution)/shard_map/ppermute | solution.py:85
  40.7 3.1 %collective-permute-done.10 = bf16[64,2,64]{2,0,1:T(8,128)(2,1)S(1)} collective-permute-done((bf16[64,2,64]{2,0,1:T(8,128)(2,1)S(1)}, bf16[64,2,64]{2,0,1:T(8,128)(2,1)S(1)}, u32[]{:S(2)}, u32[]{:S(2)}) %collective-permute-start.10) | collective-permute-done | bytes 16416 | tf_op jit(solution)/shard_map/ppermute | solution.py:85
  43.9 0.9 %collective-permute-done.11 = bf16[64,2,64]{2,0,1:T(8,128)(2,1)S(1)} collective-permute-done((bf16[64,2,64]{2,0,1:T(8,128)(2,1)S(1)}, bf16[64,2,64]{2,0,1:T(8,128)(2,1)S(1)}, u32[]{:S(2)}, u32[]{:S(2)}) %collective-permute-start.11) | collective-permute-done | bytes 16416 | tf_op jit(solution)/shard_map/ppermute | solution.py:85
  44.9 1.7 %multiply_subtract_fusion = f32[2,16,64,64]{3,2,1,0:T(8,128)} fusion(f32[2,16,64,64]{3,2,1,0:T(8,128)S(1)} %copy-done, f32[64,64]{1,0:T(8,128)S(1)} %get-tuple-element.14, f32[2,16]{1,0:T(2,128)S(1)} %bitcast.105, f32[64,64]{1,0:T(8,128)S(1)} %get-tuple-element.15, f32[2,16]{1,0:T(2,128)S(1)} %bitcast.106, f32[64,64]{1,0:T(8,128)S(1)} %get-tuple-element.16, ...), kind=kLoop, calls=%fused_computation.1 | loop fusion | flops 2228224 | bytes 1180672 | tf_op jit(solution)/shard_map/sub | solution.py:278
  (47 shorter events, 1.8 us)
Async XLA Ops:
  3.7 9.6 %collective-permute-start.2 = (bf16[2,64,64]{2,1,0:T(8,128)(2,1)S(1)}, bf16[2,64,64]{2,1,0:T(8,128)(2,1)S(1)}, u32[]{:S(2)}, u32[]{:S(2)}) collective-permute-start(bf16[2,64,64]{2,1,0:T(8,128)(2,1)S(1)} %get-tuple-element.25), channel_id=1, source_target_pairs={{0,4},{4,8},{8,12},{12,0},{1,5},{5,9},{9,13},{13,1},{2,6},{6,10},{... | collective-permute-start | bytes 49160 | tf_op jit(solution)/shard_map/ppermute | solution.py:85
  6.8 6.5 %collective-permute-start.1 = (bf16[2,64,64]{2,1,0:T(8,128)(2,1)S(1)}, bf16[2,64,64]{2,1,0:T(8,128)(2,1)S(1)}, u32[]{:S(2)}, u32[]{:S(2)}) collective-permute-start(bf16[2,64,64]{2,1,0:T(8,128)(2,1)S(1)} %get-tuple-element.26), channel_id=1, source_target_pairs={{0,8},{4,12},{8,0},{12,4},{1,9},{5,13},{9,1},{13,5},{2,10},{6,14},... | collective-permute-start | bytes 49160 | tf_op jit(solution)/shard_map/ppermute | solution.py:85
  9.4 3.9 %collective-permute-start = (bf16[2,64,64]{2,1,0:T(8,128)(2,1)S(1)}, bf16[2,64,64]{2,1,0:T(8,128)(2,1)S(1)}, u32[]{:S(2)}, u32[]{:S(2)}) collective-permute-start(bf16[2,64,64]{2,1,0:T(8,128)(2,1)S(1)} %get-tuple-element.27), channel_id=1, source_target_pairs={{0,12},{4,0},{8,4},{12,8},{1,13},{5,1},{9,5},{13,9},{2,14},{6,2},{... | collective-permute-start | bytes 49160 | tf_op jit(solution)/shard_map/ppermute | solution.py:85
  13.7 5.9 %copy-start.1 = (bf16[64,512]{1,0:T(8,128)(2,1)}, bf16[64,512]{1,0:T(8,128)(2,1)S(1)}, u32[]{:S(2)}) copy-start(bf16[64,512]{1,0:T(8,128)(2,1)S(1)} %reshape.49.refs_0_) | copy-start | bytes 196612
  13.7 2.0 %collective-permute-start.5 = (bf16[64,512]{1,0:T(8,128)(2,1)S(1)}, bf16[64,512]{1,0:T(8,128)(2,1)S(1)}, u32[]{:S(2)}, u32[]{:S(2)}) collective-permute-start(bf16[64,512]{1,0:T(8,128)(2,1)S(1)} %reshape.49.refs_0_), channel_id=1, source_target_pairs={{0,3},{1,0},{2,1},{3,2},{4,7},{5,4},{6,5},{7,6},{8,11},{9,8},{10,9... | collective-permute-start | bytes 196616 | tf_op jit(solution)/shard_map/ppermute | solution.py:255
  13.8 5.6 %collective-permute-start.4 = (bf16[64,512]{1,0:T(8,128)(2,1)S(1)}, bf16[64,512]{1,0:T(8,128)(2,1)S(1)}, u32[]{:S(2)}, u32[]{:S(2)}) collective-permute-start(bf16[64,512]{1,0:T(8,128)(2,1)S(1)} %reshape.49.refs_0_), channel_id=1, source_target_pairs={{0,2},{1,3},{2,0},{3,1},{4,6},{5,7},{6,4},{7,5},{8,10},{9,11},{10,... | collective-permute-start | bytes 196616 | tf_op jit(solution)/shard_map/ppermute | solution.py:255
  15.3 4.3 %collective-permute-start.3 = (bf16[64,512]{1,0:T(8,128)(2,1)S(1)}, bf16[64,512]{1,0:T(8,128)(2,1)S(1)}, u32[]{:S(2)}, u32[]{:S(2)}) collective-permute-start(bf16[64,512]{1,0:T(8,128)(2,1)S(1)} %reshape.49.refs_0_), channel_id=1, source_target_pairs={{0,1},{1,2},{2,3},{3,0},{4,5},{5,6},{6,7},{7,4},{8,9},{9,10},{10,1... | collective-permute-start | bytes 196616 | tf_op jit(solution)/shard_map/ppermute | solution.py:255
  15.7 3.9 %copy-start.2 = (bf16[64,512]{1,0:T(8,128)(2,1)}, bf16[64,512]{1,0:T(8,128)(2,1)S(1)}, u32[]{:S(2)}) copy-start(bf16[64,512]{1,0:T(8,128)(2,1)S(1)} %collective-permute-done.5.refs_3_) | copy-start | bytes 196612
  19.4 0.6 %copy-start.3 = (bf16[64,512]{1,0:T(8,128)(2,1)}, bf16[64,512]{1,0:T(8,128)(2,1)S(1)}, u32[]{:S(2)}) copy-start(bf16[64,512]{1,0:T(8,128)(2,1)S(1)} %collective-permute-done.4.refs_2_) | copy-start | bytes 196612
  19.6 0.6 %copy-start.4 = (bf16[64,512]{1,0:T(8,128)(2,1)}, bf16[64,512]{1,0:T(8,128)(2,1)S(1)}, u32[]{:S(2)}) copy-start(bf16[64,512]{1,0:T(8,128)(2,1)S(1)} %collective-permute-done.3.refs_1_) | copy-start | bytes 196612
  29.2 15.7 %copy-start = (f32[2,16,64,64]{3,2,1,0:T(8,128)S(1)}, f32[2,16,64,64]{3,2,1,0:T(8,128)}, u32[]{:S(2)}) copy-start(f32[2,16,64,64]{3,2,1,0:T(8,128)} %param.9) | copy-start | bytes 1572868
  29.2 4.0 %collective-permute-start.6 = (bf16[64,512]{1,0:T(8,128)(2,1)}, bf16[64,512]{1,0:T(8,128)(2,1)S(1)}, u32[]{:S(2)}, u32[]{:S(2)}) collective-permute-start(bf16[64,512]{1,0:T(8,128)(2,1)} %get-tuple-element.10), channel_id=1, source_target_pairs={{0,1},{1,2},{2,3},{3,0},{4,5},{5,6},{6,7},{7,4},{8,9},{9,10},{10,1... | collective-permute-start | bytes 196616 | tf_op jit(solution)/shard_map/ppermute | solution.py:264
  29.2 5.2 %collective-permute-start.7 = (bf16[64,512]{1,0:T(8,128)(2,1)}, bf16[64,512]{1,0:T(8,128)(2,1)S(1)}, u32[]{:S(2)}, u32[]{:S(2)}) collective-permute-start(bf16[64,512]{1,0:T(8,128)(2,1)} %get-tuple-element.11), channel_id=1, source_target_pairs={{0,2},{1,3},{2,0},{3,1},{4,6},{5,7},{6,4},{7,5},{8,10},{9,11},{10,... | collective-permute-start | bytes 196616 | tf_op jit(solution)/shard_map/ppermute | solution.py:264
  30.2 4.3 %collective-permute-start.8 = (bf16[64,512]{1,0:T(8,128)(2,1)}, bf16[64,512]{1,0:T(8,128)(2,1)S(1)}, u32[]{:S(2)}, u32[]{:S(2)}) collective-permute-start(bf16[64,512]{1,0:T(8,128)(2,1)} %get-tuple-element.12), channel_id=1, source_target_pairs={{0,3},{1,0},{2,1},{3,2},{4,7},{5,4},{6,5},{7,6},{8,11},{9,8},{10,9... | collective-permute-start | bytes 196616 | tf_op jit(solution)/shard_map/ppermute | solution.py:264
  35.8 4.9 %collective-permute-start.9 = (bf16[64,2,64]{2,0,1:T(8,128)(2,1)S(1)}, bf16[64,2,64]{2,0,1:T(8,128)(2,1)S(1)}, u32[]{:S(2)}, u32[]{:S(2)}) collective-permute-start(bf16[64,2,64]{2,0,1:T(8,128)(2,1)S(1)} %bitcast.98), channel_id=1, source_target_pairs={{0,12},{4,0},{8,4},{12,8},{1,13},{5,1},{9,5},{13,9},{2,14},{6,2},{... | collective-permute-start | bytes 49160 | tf_op jit(solution)/shard_map/ppermute | solution.py:85
  39.0 4.8 %collective-permute-start.10 = (bf16[64,2,64]{2,0,1:T(8,128)(2,1)S(1)}, bf16[64,2,64]{2,0,1:T(8,128)(2,1)S(1)}, u32[]{:S(2)}, u32[]{:S(2)}) collective-permute-start(bf16[64,2,64]{2,0,1:T(8,128)(2,1)S(1)} %bitcast.97), channel_id=1, source_target_pairs={{0,8},{4,12},{8,0},{12,4},{1,9},{5,13},{9,1},{13,5},{2,10},{6,14},... | collective-permute-start | bytes 49160 | tf_op jit(solution)/shard_map/ppermute | solution.py:85
  39.0 5.7 %collective-permute-start.11 = (bf16[64,2,64]{2,0,1:T(8,128)(2,1)S(1)}, bf16[64,2,64]{2,0,1:T(8,128)(2,1)S(1)}, u32[]{:S(2)}, u32[]{:S(2)}) collective-permute-start(bf16[64,2,64]{2,0,1:T(8,128)(2,1)S(1)} %bitcast.96), channel_id=1, source_target_pairs={{0,4},{4,8},{8,12},{12,0},{1,5},{5,9},{9,13},{13,1},{2,6},{6,10},{... | collective-permute-start | bytes 49160 | tf_op jit(solution)/shard_map/ppermute | solution.py:85

commit v25 on v20

--- a/solution.py
+++ b/solution.py
@@ -240,10 +240,16 @@
     table_y = jnp.asarray(np.concatenate([table_y_re, table_y_im], axis=1))
     time_re = temporal[0]
     time_im = temporal[1]
-    sign = jnp.asarray(np.array([[1.0, -1.0], [1.0, 1.0]], np.float32))
-    mixing = jnp.stack([temporal, temporal[::-1]]) * sign[:, :, None, None]
+    parts, ranks = factors.shape[:2]
+    weights_in = jnp.stack(
+        [
+            jnp.concatenate([temporal[0], -temporal[1]], axis=-1),
+            jnp.concatenate([temporal[1], temporal[0]], axis=-1),
+        ]
+    )
     images = jnp.sum(
-        mixing[:, :, :, :, None, None] * factors[None, :, None], axis=(1, 3)
+        weights_in[:, :, :, None, None] * factors.reshape((parts * ranks,) + factors.shape[2:])[None, None],
+        axis=2,
     )
     images = jnp.transpose(images, (1, 0, 2, 3)).astype(jnp.bfloat16)
     frames_here = images.shape[0]

time: 46.4 us -> 46.4 us (level)
    mul x1 -> x0, other arithmetic: 0.77 us -> none  [on_device(): mixing = jnp.stack([temporal, temporal[::-1]]) * sign[:, :, None, None]]
    squeeze x0 -> x1, local copies, waits for them, and re-layouts: none -> 0.7 us  [on_device(): temporal[1]]
    another operation x2 -> x1, local copies, waits for them, and re-layouts: 0.97 us -> 0.28 us  [the longest x1 0.69 us: on_device(): mixing = jnp.stack([temporal, temporal[::-1]]) * sign[:, :, None, None]]
    neg x0 -> x1, other arithmetic: none -> 0.68 us  [on_device(): -temporal[1]]
where the time goes in v25:
time: 46.4 us; the launch traced here: 46.1 us
  starting transfers between devices  15 us (32%)
  waiting for transfers between devices  13.2 us (28%)
  Pallas kernels  8.42 us (18%)
  other arithmetic  6.39 us (14%)
  local copies, waits for them, and re-layouts  2.93 us (6%)
    ppermute x6, starting transfers between devices, exchange_blocks(): pieces.append(lax.ppermute(outgoing, axis, shifted(count, step)))  10.9 us
    pallas_call x1, Pallas kernels, coil_chain(): pl.pallas_call(coil_chain_kernel, out_shape=(jax.ShapeDtypeStruct((rows,...  8.42 us
    ppermute x6, waiting for transfers between devices, exchange_blocks(): pieces.append(lax.ppermute(outgoing, axis, shifted(count, step)))  6.23 us
    ppermute x3, waiting for transfers between devices, on_device(): lax.ppermute(own_rows, 'coil', shifted(groups, step))  4.1 us
    ppermute x3, waiting for transfers between devices, on_device(): lax.ppermute(outgoing[step - 1], 'coil', shifted(groups, step))  2.85 us
    ppermute x3, starting transfers between devices, on_device(): lax.ppermute(outgoing[step - 1], 'coil', shifted(groups, step))  2.38 us
    reduce_sum x1, other arithmetic, on_device(): jnp.sum(weights_in[:, :, :, None, None] * factors.reshape((parts * ranks,...  2.28 us
    ppermute x3, starting transfers between devices, on_device(): lax.ppermute(own_rows, 'coil', shifted(groups, step))  1.78 us
  transfers between devices with their start and end apart: 12, of which 9 were waited for; matrix products, arithmetic and copies ran while one was open for 3% of the time, Pallas kernels for 0%

profile of v25, /device:TPU:0, one launch (start us, length us, event | category | flops | bytes accessed | tf_op | source)
XLA Modules:
  0.0 46.1 jit_solution(5791088725787874887)
XLA Ops:
  0.0 0.7 %fusion.8 = f32[4,16]{1,0:T(4,128)S(1)} fusion(f32[2,4,16]{2,1,0:T(4,128)} %param.9), kind=kLoop, calls=%fused_computation.73 | loop fusion | flops 64 | bytes 512 | tf_op jit(solution)/shard_map/neg | solution.py:246
  0.7 0.7 %slice_bitcast_fusion.9 = (f32[4,16]{1,0:T(4,128)S(1)}, f32[4,16]{1,0:T(4,128)S(1)}) fusion(f32[2,4,16]{2,1,0:T(4,128)} %param.9), kind=kLoop, calls=%fused_computation.62 | loop fusion | bytes 1024 | tf_op jit(solution)/shard_map/squeeze | solution.py:246
  1.5 2.3 %multiply_reduce_fusion = bf16[2,4,64,64]{3,2,1,0:T(8,128)(2,1)S(1)} fusion(f32[32,64,64]{2,1,0:T(8,128)} %bitcast.103, f32[2,4,32]{2,1,0:T(4,128)S(1)} %pad_maximum_fusion), kind=kLoop, calls=%fused_computation | loop fusion | flops 2064384 | bytes 590848 | tf_op jit(solution)/shard_map/reduce_sum | solution.py:250
  3.8 3.1 %collective-permute-start.2 = (bf16[2,64,64]{2,1,0:T(8,128)(2,1)S(1)}, bf16[2,64,64]{2,1,0:T(8,128)(2,1)S(1)}, u32[]{:S(2)}, u32[]{:S(2)}) collective-permute-start(bf16[2,64,64]{2,1,0:T(8,128)(2,1)S(1)} %get-tuple-element.25), channel_id=1, source_target_pairs={{0,4},{4,8},{8,12},{12,0},{1,5},{5,9},{9,13},{13,1},{2,6},{6,10},{... | collective-permute-start | bytes 49160 | tf_op jit(solution)/shard_map/ppermute | solution.py:85
  6.9 2.6 %collective-permute-start.1 = (bf16[2,64,64]{2,1,0:T(8,128)(2,1)S(1)}, bf16[2,64,64]{2,1,0:T(8,128)(2,1)S(1)}, u32[]{:S(2)}, u32[]{:S(2)}) collective-permute-start(bf16[2,64,64]{2,1,0:T(8,128)(2,1)S(1)} %get-tuple-element.26), channel_id=1, source_target_pairs={{0,8},{4,12},{8,0},{12,4},{1,9},{5,13},{9,1},{13,5},{2,10},{6,14},... | collective-permute-start | bytes 49160 | tf_op jit(solution)/shard_map/ppermute | solution.py:85
  9.4 1.3 %collective-permute-start = (bf16[2,64,64]{2,1,0:T(8,128)(2,1)S(1)}, bf16[2,64,64]{2,1,0:T(8,128)(2,1)S(1)}, u32[]{:S(2)}, u32[]{:S(2)}) collective-permute-start(bf16[2,64,64]{2,1,0:T(8,128)(2,1)S(1)} %get-tuple-element.27), channel_id=1, source_target_pairs={{0,12},{4,0},{8,4},{12,8},{1,13},{5,1},{9,5},{13,9},{2,14},{6,2},{... | collective-permute-start | bytes 49160 | tf_op jit(solution)/shard_map/ppermute | solution.py:85
  10.8 0.7 %fusion = f32[16,4,1]{0,1,2:T(4,128)S(1)} fusion(f32[2,4,16]{2,1,0:T(4,128)} %param.9), kind=kLoop, calls=%fused_computation.61 | loop fusion | flops 64 | bytes 512 | tf_op jit(solution)/shard_map/stack | solution.py:277
  11.5 0.7 %slice_bitcast_fusion.11 = (f32[16,4,1]{0,1,2:T(4,128)S(1)}, f32[16,4,1]{0,1,2:T(4,128)S(1)}) fusion(f32[2,4,16]{2,1,0:T(4,128)} %param.9), kind=kLoop, calls=%fused_computation.64 | loop fusion | bytes 1024 | tf_op jit(solution)/shard_map/stack | solution.py:277
  12.2 1.2 %collective-permute-done = bf16[2,64,64]{2,1,0:T(8,128)(2,1)S(1)} collective-permute-done((bf16[2,64,64]{2,1,0:T(8,128)(2,1)S(1)}, bf16[2,64,64]{2,1,0:T(8,128)(2,1)S(1)}, u32[]{:S(2)}, u32[]{:S(2)}) %collective-permute-start) | collective-permute-done | bytes 16416 | tf_op jit(solution)/shard_map/ppermute | solution.py:85
  13.8 1.6 %collective-permute-start.4 = (bf16[64,512]{1,0:T(8,128)(2,1)S(1)}, bf16[64,512]{1,0:T(8,128)(2,1)S(1)}, u32[]{:S(2)}, u32[]{:S(2)}) collective-permute-start(bf16[64,512]{1,0:T(8,128)(2,1)S(1)} %reshape.32.refs_0_), channel_id=1, source_target_pairs={{0,2},{1,3},{2,0},{3,1},{4,6},{5,7},{6,4},{7,5},{8,10},{9,11},{10,... | collective-permute-start | bytes 196616 | tf_op jit(solution)/shard_map/ppermute | solution.py:261
  15.7 3.7 %collective-permute-done.4.refs_2_ = bf16[64,512]{1,0:T(8,128)(2,1)S(1)} collective-permute-done((bf16[64,512]{1,0:T(8,128)(2,1)S(1)}, bf16[64,512]{1,0:T(8,128)(2,1)S(1)}, u32[]{:S(2)}, u32[]{:S(2)}) %collective-permute-start.4) | collective-permute-done | bytes 65568 | tf_op jit(solution)/shard_map/ppermute | solution.py:261
  19.7 0.4 copy-done.3
  20.3 8.4 %shard_map.82 = (f32[64,512]{1,0:T(8,128)}, bf16[64,512]{1,0:T(8,128)(2,1)}, bf16[64,512]{1,0:T(8,128)(2,1)}, bf16[64,512]{1,0:T(8,128)(2,1)}) custom-call(bf16[64,512]{1,0:T(8,128)(2,1)} %copy-done.1, bf16[64,512]{1,0:T(8,128)(2,1)} %copy-done.4, bf16[64,512]{1,0:T(8,128)(2,1)} %copy-done.3, bf16[64,512]{1,0:T(8,128)(2,1)} %copy-done.2, s32[1]{0:T(128)} %bitcast.26.refs_4_, ...), custom_call_target="tpu_custom_call" | custom-call | flops 4294967296 | bytes 4718592 | tf_op jit(solution)/shard_map/pallas_call | solution.py:208
  28.8 0.9 %collective-permute-start.7 = (bf16[64,512]{1,0:T(8,128)(2,1)}, bf16[64,512]{1,0:T(8,128)(2,1)S(1)}, u32[]{:S(2)}, u32[]{:S(2)}) collective-permute-start(bf16[64,512]{1,0:T(8,128)(2,1)} %get-tuple-element.11), channel_id=1, source_target_pairs={{0,2},{1,3},{2,0},{3,1},{4,6},{5,7},{6,4},{7,5},{8,10},{9,11},{10,... | collective-permute-start | bytes 196616 | tf_op jit(solution)/shard_map/ppermute | solution.py:270
  29.7 1.4 %collective-permute-start.8 = (bf16[64,512]{1,0:T(8,128)(2,1)}, bf16[64,512]{1,0:T(8,128)(2,1)S(1)}, u32[]{:S(2)}, u32[]{:S(2)}) collective-permute-start(bf16[64,512]{1,0:T(8,128)(2,1)} %get-tuple-element.12), channel_id=1, source_target_pairs={{0,3},{1,0},{2,1},{3,2},{4,7},{5,4},{6,5},{7,6},{8,11},{9,8},{10,9... | collective-permute-start | bytes 196616 | tf_op jit(solution)/shard_map/ppermute | solution.py:270
  31.1 1.6 %collective-permute-done.6 = bf16[64,512]{1,0:T(8,128)(2,1)S(1)} collective-permute-done((bf16[64,512]{1,0:T(8,128)(2,1)}, bf16[64,512]{1,0:T(8,128)(2,1)S(1)}, u32[]{:S(2)}, u32[]{:S(2)}) %collective-permute-start.6) | collective-permute-done | bytes 65568 | tf_op jit(solution)/shard_map/ppermute | solution.py:270
  32.8 1.2 %collective-permute-done.7 = bf16[64,512]{1,0:T(8,128)(2,1)S(1)} collective-permute-done((bf16[64,512]{1,0:T(8,128)(2,1)}, bf16[64,512]{1,0:T(8,128)(2,1)S(1)}, u32[]{:S(2)}, u32[]{:S(2)}) %collective-permute-start.7) | collective-permute-done | bytes 65568 | tf_op jit(solution)/shard_map/ppermute | solution.py:270
  34.0 0.9 %add_convert_fusion = bf16[64,512]{1,0:T(8,128)(2,1)S(1)} fusion(bf16[64,512]{1,0:T(8,128)(2,1)S(1)} %collective-permute-done.8, bf16[64,512]{1,0:T(8,128)(2,1)S(1)} %collective-permute-done.7, f32[64,512]{1,0:T(8,128)} %get-tuple-element.9, bf16[64,512]{1,0:T(8,128)(2,1)S(1)} %collective-permute-done.6), kind=kLoop, calls=%fused_computation.3 | loop fusion | flops 229376 | bytes 393216 | tf_op jit(solution)/shard_map/convert_element_type | solution.py:273
  35.4 3.2 %collective-permute-start.9 = (bf16[64,2,64]{2,0,1:T(8,128)(2,1)S(1)}, bf16[64,2,64]{2,0,1:T(8,128)(2,1)S(1)}, u32[]{:S(2)}, u32[]{:S(2)}) collective-permute-start(bf16[64,2,64]{2,0,1:T(8,128)(2,1)S(1)} %bitcast.106), channel_id=1, source_target_pairs={{0,12},{4,0},{8,4},{12,8},{1,13},{5,1},{9,5},{13,9},{2,14},{6,2},{... | collective-permute-start | bytes 49160 | tf_op jit(solution)/shard_map/ppermute | solution.py:85
  38.6 0.6 %collective-permute-start.11 = (bf16[64,2,64]{2,0,1:T(8,128)(2,1)S(1)}, bf16[64,2,64]{2,0,1:T(8,128)(2,1)S(1)}, u32[]{:S(2)}, u32[]{:S(2)}) collective-permute-start(bf16[64,2,64]{2,0,1:T(8,128)(2,1)S(1)} %bitcast.104), channel_id=1, source_target_pairs={{0,4},{4,8},{8,12},{12,0},{1,5},{5,9},{9,13},{13,1},{2,6},{6,10},{... | collective-permute-start | bytes 49160 | tf_op jit(solution)/shard_map/ppermute | solution.py:85
  39.2 1.0 %collective-permute-done.9 = bf16[64,2,64]{2,0,1:T(8,128)(2,1)S(1)} collective-permute-done((bf16[64,2,64]{2,0,1:T(8,128)(2,1)S(1)}, bf16[64,2,64]{2,0,1:T(8,128)(2,1)S(1)}, u32[]{:S(2)}, u32[]{:S(2)}) %collective-permute-start.9) | collective-permute-done | bytes 16416 | tf_op jit(solution)/shard_map/ppermute | solution.py:85
  40.3 3.1 %collective-permute-done.10 = bf16[64,2,64]{2,0,1:T(8,128)(2,1)S(1)} collective-permute-done((bf16[64,2,64]{2,0,1:T(8,128)(2,1)S(1)}, bf16[64,2,64]{2,0,1:T(8,128)(2,1)S(1)}, u32[]{:S(2)}, u32[]{:S(2)}) %collective-permute-start.10) | collective-permute-done | bytes 16416 | tf_op jit(solution)/shard_map/ppermute | solution.py:85
  43.4 0.9 %collective-permute-done.11 = bf16[64,2,64]{2,0,1:T(8,128)(2,1)S(1)} collective-permute-done((bf16[64,2,64]{2,0,1:T(8,128)(2,1)S(1)}, bf16[64,2,64]{2,0,1:T(8,128)(2,1)S(1)}, u32[]{:S(2)}, u32[]{:S(2)}) %collective-permute-start.11) | collective-permute-done | bytes 16416 | tf_op jit(solution)/shard_map/ppermute | solution.py:85
  44.5 1.7 %multiply_subtract_fusion = f32[2,16,64,64]{3,2,1,0:T(8,128)} fusion(f32[2,16,64,64]{3,2,1,0:T(8,128)S(1)} %copy-done, f32[64,64]{1,0:T(8,128)S(1)} %get-tuple-element.14, f32[2,16]{1,0:T(2,128)S(1)} %bitcast.113, f32[64,64]{1,0:T(8,128)S(1)} %get-tuple-element.15, f32[2,16]{1,0:T(2,128)S(1)} %bitcast.114, f32[64,64]{1,0:T(8,128)S(1)} %get-tuple-element.16, ...), kind=kLoop, calls=%fused_computation.1 | loop fusion | flops 2228224 | bytes 1180672 | tf_op jit(solution)/shard_map/sub | solution.py:284
  (49 shorter events, 1.9 us)
Async XLA Ops:
  3.8 9.6 %collective-permute-start.2 = (bf16[2,64,64]{2,1,0:T(8,128)(2,1)S(1)}, bf16[2,64,64]{2,1,0:T(8,128)(2,1)S(1)}, u32[]{:S(2)}, u32[]{:S(2)}) collective-permute-start(bf16[2,64,64]{2,1,0:T(8,128)(2,1)S(1)} %get-tuple-element.25), channel_id=1, source_target_pairs={{0,4},{4,8},{8,12},{12,0},{1,5},{5,9},{9,13},{13,1},{2,6},{6,10},{... | collective-permute-start | bytes 49160 | tf_op jit(solution)/shard_map/ppermute | solution.py:85
  6.9 6.5 %collective-permute-start.1 = (bf16[2,64,64]{2,1,0:T(8,128)(2,1)S(1)}, bf16[2,64,64]{2,1,0:T(8,128)(2,1)S(1)}, u32[]{:S(2)}, u32[]{:S(2)}) collective-permute-start(bf16[2,64,64]{2,1,0:T(8,128)(2,1)S(1)} %get-tuple-element.26), channel_id=1, source_target_pairs={{0,8},{4,12},{8,0},{12,4},{1,9},{5,13},{9,1},{13,5},{2,10},{6,14},... | collective-permute-start | bytes 49160 | tf_op jit(solution)/shard_map/ppermute | solution.py:85
  9.4 3.9 %collective-permute-start = (bf16[2,64,64]{2,1,0:T(8,128)(2,1)S(1)}, bf16[2,64,64]{2,1,0:T(8,128)(2,1)S(1)}, u32[]{:S(2)}, u32[]{:S(2)}) collective-permute-start(bf16[2,64,64]{2,1,0:T(8,128)(2,1)S(1)} %get-tuple-element.27), channel_id=1, source_target_pairs={{0,12},{4,0},{8,4},{12,8},{1,13},{5,1},{9,5},{13,9},{2,14},{6,2},{... | collective-permute-start | bytes 49160 | tf_op jit(solution)/shard_map/ppermute | solution.py:85
  13.8 5.9 %copy-start.1 = (bf16[64,512]{1,0:T(8,128)(2,1)}, bf16[64,512]{1,0:T(8,128)(2,1)S(1)}, u32[]{:S(2)}) copy-start(bf16[64,512]{1,0:T(8,128)(2,1)S(1)} %reshape.32.refs_0_) | copy-start | bytes 196612
  13.8 2.0 %collective-permute-start.5 = (bf16[64,512]{1,0:T(8,128)(2,1)S(1)}, bf16[64,512]{1,0:T(8,128)(2,1)S(1)}, u32[]{:S(2)}, u32[]{:S(2)}) collective-permute-start(bf16[64,512]{1,0:T(8,128)(2,1)S(1)} %reshape.32.refs_0_), channel_id=1, source_target_pairs={{0,3},{1,0},{2,1},{3,2},{4,7},{5,4},{6,5},{7,6},{8,11},{9,8},{10,9... | collective-permute-start | bytes 196616 | tf_op jit(solution)/shard_map/ppermute | solution.py:261
  13.8 5.6 %collective-permute-start.4 = (bf16[64,512]{1,0:T(8,128)(2,1)S(1)}, bf16[64,512]{1,0:T(8,128)(2,1)S(1)}, u32[]{:S(2)}, u32[]{:S(2)}) collective-permute-start(bf16[64,512]{1,0:T(8,128)(2,1)S(1)} %reshape.32.refs_0_), channel_id=1, source_target_pairs={{0,2},{1,3},{2,0},{3,1},{4,6},{5,7},{6,4},{7,5},{8,10},{9,11},{10,... | collective-permute-start | bytes 196616 | tf_op jit(solution)/shard_map/ppermute | solution.py:261
  15.4 4.3 %collective-permute-start.3 = (bf16[64,512]{1,0:T(8,128)(2,1)S(1)}, bf16[64,512]{1,0:T(8,128)(2,1)S(1)}, u32[]{:S(2)}, u32[]{:S(2)}) collective-permute-start(bf16[64,512]{1,0:T(8,128)(2,1)S(1)} %reshape.32.refs_0_), channel_id=1, source_target_pairs={{0,1},{1,2},{2,3},{3,0},{4,5},{5,6},{6,7},{7,4},{8,9},{9,10},{10,1... | collective-permute-start | bytes 196616 | tf_op jit(solution)/shard_map/ppermute | solution.py:261
  15.7 3.9 %copy-start.2 = (bf16[64,512]{1,0:T(8,128)(2,1)}, bf16[64,512]{1,0:T(8,128)(2,1)S(1)}, u32[]{:S(2)}) copy-start(bf16[64,512]{1,0:T(8,128)(2,1)S(1)} %collective-permute-done.5.refs_3_) | copy-start | bytes 196612
  19.5 0.6 %copy-start.3 = (bf16[64,512]{1,0:T(8,128)(2,1)}, bf16[64,512]{1,0:T(8,128)(2,1)S(1)}, u32[]{:S(2)}) copy-start(bf16[64,512]{1,0:T(8,128)(2,1)S(1)} %collective-permute-done.4.refs_2_) | copy-start | bytes 196612
  19.7 0.6 %copy-start.4 = (bf16[64,512]{1,0:T(8,128)(2,1)}, bf16[64,512]{1,0:T(8,128)(2,1)S(1)}, u32[]{:S(2)}) copy-start(bf16[64,512]{1,0:T(8,128)(2,1)S(1)} %collective-permute-done.3.refs_1_) | copy-start | bytes 196612
  28.7 15.7 %copy-start = (f32[2,16,64,64]{3,2,1,0:T(8,128)S(1)}, f32[2,16,64,64]{3,2,1,0:T(8,128)}, u32[]{:S(2)}) copy-start(f32[2,16,64,64]{3,2,1,0:T(8,128)} %param.8) | copy-start | bytes 1572868
  28.7 4.0 %collective-permute-start.6 = (bf16[64,512]{1,0:T(8,128)(2,1)}, bf16[64,512]{1,0:T(8,128)(2,1)S(1)}, u32[]{:S(2)}, u32[]{:S(2)}) collective-permute-start(bf16[64,512]{1,0:T(8,128)(2,1)} %get-tuple-element.10), channel_id=1, source_target_pairs={{0,1},{1,2},{2,3},{3,0},{4,5},{5,6},{6,7},{7,4},{8,9},{9,10},{10,1... | collective-permute-start | bytes 196616 | tf_op jit(solution)/shard_map/ppermute | solution.py:270
  28.8 5.2 %collective-permute-start.7 = (bf16[64,512]{1,0:T(8,128)(2,1)}, bf16[64,512]{1,0:T(8,128)(2,1)S(1)}, u32[]{:S(2)}, u32[]{:S(2)}) collective-permute-start(bf16[64,512]{1,0:T(8,128)(2,1)} %get-tuple-element.11), channel_id=1, source_target_pairs={{0,2},{1,3},{2,0},{3,1},{4,6},{5,7},{6,4},{7,5},{8,10},{9,11},{10,... | collective-permute-start | bytes 196616 | tf_op jit(solution)/shard_map/ppermute | solution.py:270
  29.7 4.3 %collective-permute-start.8 = (bf16[64,512]{1,0:T(8,128)(2,1)}, bf16[64,512]{1,0:T(8,128)(2,1)S(1)}, u32[]{:S(2)}, u32[]{:S(2)}) collective-permute-start(bf16[64,512]{1,0:T(8,128)(2,1)} %get-tuple-element.12), channel_id=1, source_target_pairs={{0,3},{1,0},{2,1},{3,2},{4,7},{5,4},{6,5},{7,6},{8,11},{9,8},{10,9... | collective-permute-start | bytes 196616 | tf_op jit(solution)/shard_map/ppermute | solution.py:270
  35.4 4.9 %collective-permute-start.9 = (bf16[64,2,64]{2,0,1:T(8,128)(2,1)S(1)}, bf16[64,2,64]{2,0,1:T(8,128)(2,1)S(1)}, u32[]{:S(2)}, u32[]{:S(2)}) collective-permute-start(bf16[64,2,64]{2,0,1:T(8,128)(2,1)S(1)} %bitcast.106), channel_id=1, source_target_pairs={{0,12},{4,0},{8,4},{12,8},{1,13},{5,1},{9,5},{13,9},{2,14},{6,2},{... | collective-permute-start | bytes 49160 | tf_op jit(solution)/shard_map/ppermute | solution.py:85
  38.6 4.8 %collective-permute-start.10 = (bf16[64,2,64]{2,0,1:T(8,128)(2,1)S(1)}, bf16[64,2,64]{2,0,1:T(8,128)(2,1)S(1)}, u32[]{:S(2)}, u32[]{:S(2)}) collective-permute-start(bf16[64,2,64]{2,0,1:T(8,128)(2,1)S(1)} %bitcast.105), channel_id=1, source_target_pairs={{0,8},{4,12},{8,0},{12,4},{1,9},{5,13},{9,1},{13,5},{2,10},{6,14},... | collective-permute-start | bytes 49160 | tf_op jit(solution)/shard_map/ppermute | solution.py:85
  38.6 5.7 %collective-permute-start.11 = (bf16[64,2,64]{2,0,1:T(8,128)(2,1)S(1)}, bf16[64,2,64]{2,0,1:T(8,128)(2,1)S(1)}, u32[]{:S(2)}, u32[]{:S(2)}) collective-permute-start(bf16[64,2,64]{2,0,1:T(8,128)(2,1)S(1)} %bitcast.104), channel_id=1, source_target_pairs={{0,4},{4,8},{8,12},{12,0},{1,5},{5,9},{9,13},{13,1},{2,6},{6,10},{... | collective-permute-start | bytes 49160 | tf_op jit(solution)/shard_map/ppermute | solution.py:85

commit v26 on v25

--- a/solution.py
+++ b/solution.py
@@ -210,7 +210,7 @@
         out_shape=(jax.ShapeDtypeStruct((rows, width), jnp.float32),)
         + (jax.ShapeDtypeStruct((rows, width), jnp.bfloat16),) * (groups - 1),
         grid=(coils // step_coils,),
-        in_specs=[pl.BlockSpec((rows, width), whole)] * groups
+        in_specs=[pl.BlockSpec(memory_space=pltpu.VMEM)] * groups
         + [
             pl.BlockSpec(memory_space=pltpu.SMEM),
             pl.BlockSpec((step_coils, height, width), per_coil),

time: 46.4 us -> 46.4 us (level)
  no operation moved by 1% of the time
where the time goes in v26:
time: 46.4 us; the launch traced here: 46.1 us
  starting transfers between devices  15 us (32%)
  waiting for transfers between devices  13.2 us (28%)
  Pallas kernels  8.42 us (18%)
  other arithmetic  6.39 us (14%)
  local copies, waits for them, and re-layouts  2.93 us (6%)
    ppermute x6, starting transfers between devices, exchange_blocks(): pieces.append(lax.ppermute(outgoing, axis, shifted(count, step)))  10.9 us
    pallas_call x1, Pallas kernels, coil_chain(): pl.pallas_call(coil_chain_kernel, out_shape=(jax.ShapeDtypeStruct((rows,...  8.42 us
    ppermute x6, waiting for transfers between devices, exchange_blocks(): pieces.append(lax.ppermute(outgoing, axis, shifted(count, step)))  6.23 us
    ppermute x3, waiting for transfers between devices, on_device(): lax.ppermute(own_rows, 'coil', shifted(groups, step))  4.1 us
    ppermute x3, waiting for transfers between devices, on_device(): lax.ppermute(outgoing[step - 1], 'coil', shifted(groups, step))  2.85 us
    ppermute x3, starting transfers between devices, on_device(): lax.ppermute(outgoing[step - 1], 'coil', shifted(groups, step))  2.38 us
    reduce_sum x1, other arithmetic, on_device(): jnp.sum(weights_in[:, :, :, None, None] * factors.reshape((parts * ranks,...  2.28 us
    ppermute x3, starting transfers between devices, on_device(): lax.ppermute(own_rows, 'coil', shifted(groups, step))  1.78 us
  transfers between devices with their start and end apart: 12, of which 9 were waited for; matrix products, arithmetic and copies ran while one was open for 3% of the time, Pallas kernels for 0%

profile of v26, /device:TPU:0, one launch (start us, length us, event | category | flops | bytes accessed | tf_op | source)
XLA Modules:
  0.0 46.1 jit_solution(5791088725787874887)
XLA Ops:
  0.0 0.7 %fusion.8 = f32[4,16]{1,0:T(4,128)S(1)} fusion(f32[2,4,16]{2,1,0:T(4,128)} %param.9), kind=kLoop, calls=%fused_computation.73 | loop fusion | flops 64 | bytes 512 | tf_op jit(solution)/shard_map/neg | solution.py:246
  0.7 0.7 %slice_bitcast_fusion.9 = (f32[4,16]{1,0:T(4,128)S(1)}, f32[4,16]{1,0:T(4,128)S(1)}) fusion(f32[2,4,16]{2,1,0:T(4,128)} %param.9), kind=kLoop, calls=%fused_computation.62 | loop fusion | bytes 1024 | tf_op jit(solution)/shard_map/squeeze | solution.py:246
  1.5 2.3 %multiply_reduce_fusion = bf16[2,4,64,64]{3,2,1,0:T(8,128)(2,1)S(1)} fusion(f32[32,64,64]{2,1,0:T(8,128)} %bitcast.103, f32[2,4,32]{2,1,0:T(4,128)S(1)} %pad_maximum_fusion), kind=kLoop, calls=%fused_computation | loop fusion | flops 2064384 | bytes 590848 | tf_op jit(solution)/shard_map/reduce_sum | solution.py:250
  3.8 3.1 %collective-permute-start.2 = (bf16[2,64,64]{2,1,0:T(8,128)(2,1)S(1)}, bf16[2,64,64]{2,1,0:T(8,128)(2,1)S(1)}, u32[]{:S(2)}, u32[]{:S(2)}) collective-permute-start(bf16[2,64,64]{2,1,0:T(8,128)(2,1)S(1)} %get-tuple-element.25), channel_id=1, source_target_pairs={{0,4},{4,8},{8,12},{12,0},{1,5},{5,9},{9,13},{13,1},{2,6},{6,10},{... | collective-permute-start | bytes 49160 | tf_op jit(solution)/shard_map/ppermute | solution.py:85
  6.9 2.6 %collective-permute-start.1 = (bf16[2,64,64]{2,1,0:T(8,128)(2,1)S(1)}, bf16[2,64,64]{2,1,0:T(8,128)(2,1)S(1)}, u32[]{:S(2)}, u32[]{:S(2)}) collective-permute-start(bf16[2,64,64]{2,1,0:T(8,128)(2,1)S(1)} %get-tuple-element.26), channel_id=1, source_target_pairs={{0,8},{4,12},{8,0},{12,4},{1,9},{5,13},{9,1},{13,5},{2,10},{6,14},... | collective-permute-start | bytes 49160 | tf_op jit(solution)/shard_map/ppermute | solution.py:85
  9.4 1.3 %collective-permute-start = (bf16[2,64,64]{2,1,0:T(8,128)(2,1)S(1)}, bf16[2,64,64]{2,1,0:T(8,128)(2,1)S(1)}, u32[]{:S(2)}, u32[]{:S(2)}) collective-permute-start(bf16[2,64,64]{2,1,0:T(8,128)(2,1)S(1)} %get-tuple-element.27), channel_id=1, source_target_pairs={{0,12},{4,0},{8,4},{12,8},{1,13},{5,1},{9,5},{13,9},{2,14},{6,2},{... | collective-permute-start | bytes 49160 | tf_op jit(solution)/shard_map/ppermute | solution.py:85
  10.8 0.7 %fusion = f32[16,4,1]{0,1,2:T(4,128)S(1)} fusion(f32[2,4,16]{2,1,0:T(4,128)} %param.9), kind=kLoop, calls=%fused_computation.61 | loop fusion | flops 64 | bytes 512 | tf_op jit(solution)/shard_map/stack | solution.py:277
  11.5 0.7 %slice_bitcast_fusion.11 = (f32[16,4,1]{0,1,2:T(4,128)S(1)}, f32[16,4,1]{0,1,2:T(4,128)S(1)}) fusion(f32[2,4,16]{2,1,0:T(4,128)} %param.9), kind=kLoop, calls=%fused_computation.64 | loop fusion | bytes 1024 | tf_op jit(solution)/shard_map/stack | solution.py:277
  12.2 1.2 %collective-permute-done = bf16[2,64,64]{2,1,0:T(8,128)(2,1)S(1)} collective-permute-done((bf16[2,64,64]{2,1,0:T(8,128)(2,1)S(1)}, bf16[2,64,64]{2,1,0:T(8,128)(2,1)S(1)}, u32[]{:S(2)}, u32[]{:S(2)}) %collective-permute-start) | collective-permute-done | bytes 16416 | tf_op jit(solution)/shard_map/ppermute | solution.py:85
  13.8 1.6 %collective-permute-start.4 = (bf16[64,512]{1,0:T(8,128)(2,1)S(1)}, bf16[64,512]{1,0:T(8,128)(2,1)S(1)}, u32[]{:S(2)}, u32[]{:S(2)}) collective-permute-start(bf16[64,512]{1,0:T(8,128)(2,1)S(1)} %reshape.32.refs_0_), channel_id=1, source_target_pairs={{0,2},{1,3},{2,0},{3,1},{4,6},{5,7},{6,4},{7,5},{8,10},{9,11},{10,... | collective-permute-start | bytes 196616 | tf_op jit(solution)/shard_map/ppermute | solution.py:261
  15.7 3.7 %collective-permute-done.4.refs_2_ = bf16[64,512]{1,0:T(8,128)(2,1)S(1)} collective-permute-done((bf16[64,512]{1,0:T(8,128)(2,1)S(1)}, bf16[64,512]{1,0:T(8,128)(2,1)S(1)}, u32[]{:S(2)}, u32[]{:S(2)}) %collective-permute-start.4) | collective-permute-done | bytes 65568 | tf_op jit(solution)/shard_map/ppermute | solution.py:261
  19.7 0.4 copy-done.3
  20.3 8.4 %shard_map.82 = (f32[64,512]{1,0:T(8,128)}, bf16[64,512]{1,0:T(8,128)(2,1)}, bf16[64,512]{1,0:T(8,128)(2,1)}, bf16[64,512]{1,0:T(8,128)(2,1)}) custom-call(bf16[64,512]{1,0:T(8,128)(2,1)} %copy-done.1, bf16[64,512]{1,0:T(8,128)(2,1)} %copy-done.4, bf16[64,512]{1,0:T(8,128)(2,1)} %copy-done.3, bf16[64,512]{1,0:T(8,128)(2,1)} %copy-done.2, s32[1]{0:T(128)} %bitcast.26.refs_4_, ...), custom_call_target="tpu_custom_call" | custom-call | flops 4294967296 | bytes 4718592 | tf_op jit(solution)/shard_map/pallas_call | solution.py:208
  28.8 0.9 %collective-permute-start.7 = (bf16[64,512]{1,0:T(8,128)(2,1)}, bf16[64,512]{1,0:T(8,128)(2,1)S(1)}, u32[]{:S(2)}, u32[]{:S(2)}) collective-permute-start(bf16[64,512]{1,0:T(8,128)(2,1)} %get-tuple-element.11), channel_id=1, source_target_pairs={{0,2},{1,3},{2,0},{3,1},{4,6},{5,7},{6,4},{7,5},{8,10},{9,11},{10,... | collective-permute-start | bytes 196616 | tf_op jit(solution)/shard_map/ppermute | solution.py:270
  29.7 1.4 %collective-permute-start.8 = (bf16[64,512]{1,0:T(8,128)(2,1)}, bf16[64,512]{1,0:T(8,128)(2,1)S(1)}, u32[]{:S(2)}, u32[]{:S(2)}) collective-permute-start(bf16[64,512]{1,0:T(8,128)(2,1)} %get-tuple-element.12), channel_id=1, source_target_pairs={{0,3},{1,0},{2,1},{3,2},{4,7},{5,4},{6,5},{7,6},{8,11},{9,8},{10,9... | collective-permute-start | bytes 196616 | tf_op jit(solution)/shard_map/ppermute | solution.py:270
  31.1 1.6 %collective-permute-done.6 = bf16[64,512]{1,0:T(8,128)(2,1)S(1)} collective-permute-done((bf16[64,512]{1,0:T(8,128)(2,1)}, bf16[64,512]{1,0:T(8,128)(2,1)S(1)}, u32[]{:S(2)}, u32[]{:S(2)}) %collective-permute-start.6) | collective-permute-done | bytes 65568 | tf_op jit(solution)/shard_map/ppermute | solution.py:270
  32.8 1.2 %collective-permute-done.7 = bf16[64,512]{1,0:T(8,128)(2,1)S(1)} collective-permute-done((bf16[64,512]{1,0:T(8,128)(2,1)}, bf16[64,512]{1,0:T(8,128)(2,1)S(1)}, u32[]{:S(2)}, u32[]{:S(2)}) %collective-permute-start.7) | collective-permute-done | bytes 65568 | tf_op jit(solution)/shard_map/ppermute | solution.py:270
  34.0 0.9 %add_convert_fusion = bf16[64,512]{1,0:T(8,128)(2,1)S(1)} fusion(bf16[64,512]{1,0:T(8,128)(2,1)S(1)} %collective-permute-done.8, bf16[64,512]{1,0:T(8,128)(2,1)S(1)} %collective-permute-done.7, f32[64,512]{1,0:T(8,128)} %get-tuple-element.9, bf16[64,512]{1,0:T(8,128)(2,1)S(1)} %collective-permute-done.6), kind=kLoop, calls=%fused_computation.3 | loop fusion | flops 229376 | bytes 393216 | tf_op jit(solution)/shard_map/convert_element_type | solution.py:273
  35.4 3.2 %collective-permute-start.9 = (bf16[64,2,64]{2,0,1:T(8,128)(2,1)S(1)}, bf16[64,2,64]{2,0,1:T(8,128)(2,1)S(1)}, u32[]{:S(2)}, u32[]{:S(2)}) collective-permute-start(bf16[64,2,64]{2,0,1:T(8,128)(2,1)S(1)} %bitcast.106), channel_id=1, source_target_pairs={{0,12},{4,0},{8,4},{12,8},{1,13},{5,1},{9,5},{13,9},{2,14},{6,2},{... | collective-permute-start | bytes 49160 | tf_op jit(solution)/shard_map/ppermute | solution.py:85
  38.6 0.6 %collective-permute-start.11 = (bf16[64,2,64]{2,0,1:T(8,128)(2,1)S(1)}, bf16[64,2,64]{2,0,1:T(8,128)(2,1)S(1)}, u32[]{:S(2)}, u32[]{:S(2)}) collective-permute-start(bf16[64,2,64]{2,0,1:T(8,128)(2,1)S(1)} %bitcast.104), channel_id=1, source_target_pairs={{0,4},{4,8},{8,12},{12,0},{1,5},{5,9},{9,13},{13,1},{2,6},{6,10},{... | collective-permute-start | bytes 49160 | tf_op jit(solution)/shard_map/ppermute | solution.py:85
  39.2 1.0 %collective-permute-done.9 = bf16[64,2,64]{2,0,1:T(8,128)(2,1)S(1)} collective-permute-done((bf16[64,2,64]{2,0,1:T(8,128)(2,1)S(1)}, bf16[64,2,64]{2,0,1:T(8,128)(2,1)S(1)}, u32[]{:S(2)}, u32[]{:S(2)}) %collective-permute-start.9) | collective-permute-done | bytes 16416 | tf_op jit(solution)/shard_map/ppermute | solution.py:85
  40.3 3.1 %collective-permute-done.10 = bf16[64,2,64]{2,0,1:T(8,128)(2,1)S(1)} collective-permute-done((bf16[64,2,64]{2,0,1:T(8,128)(2,1)S(1)}, bf16[64,2,64]{2,0,1:T(8,128)(2,1)S(1)}, u32[]{:S(2)}, u32[]{:S(2)}) %collective-permute-start.10) | collective-permute-done | bytes 16416 | tf_op jit(solution)/shard_map/ppermute | solution.py:85
  43.4 0.9 %collective-permute-done.11 = bf16[64,2,64]{2,0,1:T(8,128)(2,1)S(1)} collective-permute-done((bf16[64,2,64]{2,0,1:T(8,128)(2,1)S(1)}, bf16[64,2,64]{2,0,1:T(8,128)(2,1)S(1)}, u32[]{:S(2)}, u32[]{:S(2)}) %collective-permute-start.11) | collective-permute-done | bytes 16416 | tf_op jit(solution)/shard_map/ppermute | solution.py:85
  44.5 1.7 %multiply_subtract_fusion = f32[2,16,64,64]{3,2,1,0:T(8,128)} fusion(f32[2,16,64,64]{3,2,1,0:T(8,128)S(1)} %copy-done, f32[64,64]{1,0:T(8,128)S(1)} %get-tuple-element.14, f32[2,16]{1,0:T(2,128)S(1)} %bitcast.113, f32[64,64]{1,0:T(8,128)S(1)} %get-tuple-element.15, f32[2,16]{1,0:T(2,128)S(1)} %bitcast.114, f32[64,64]{1,0:T(8,128)S(1)} %get-tuple-element.16, ...), kind=kLoop, calls=%fused_computation.1 | loop fusion | flops 2228224 | bytes 1180672 | tf_op jit(solution)/shard_map/sub | solution.py:284
  (49 shorter events, 1.9 us)
Async XLA Ops:
  3.8 9.6 %collective-permute-start.2 = (bf16[2,64,64]{2,1,0:T(8,128)(2,1)S(1)}, bf16[2,64,64]{2,1,0:T(8,128)(2,1)S(1)}, u32[]{:S(2)}, u32[]{:S(2)}) collective-permute-start(bf16[2,64,64]{2,1,0:T(8,128)(2,1)S(1)} %get-tuple-element.25), channel_id=1, source_target_pairs={{0,4},{4,8},{8,12},{12,0},{1,5},{5,9},{9,13},{13,1},{2,6},{6,10},{... | collective-permute-start | bytes 49160 | tf_op jit(solution)/shard_map/ppermute | solution.py:85
  6.9 6.5 %collective-permute-start.1 = (bf16[2,64,64]{2,1,0:T(8,128)(2,1)S(1)}, bf16[2,64,64]{2,1,0:T(8,128)(2,1)S(1)}, u32[]{:S(2)}, u32[]{:S(2)}) collective-permute-start(bf16[2,64,64]{2,1,0:T(8,128)(2,1)S(1)} %get-tuple-element.26), channel_id=1, source_target_pairs={{0,8},{4,12},{8,0},{12,4},{1,9},{5,13},{9,1},{13,5},{2,10},{6,14},... | collective-permute-start | bytes 49160 | tf_op jit(solution)/shard_map/ppermute | solution.py:85
  9.4 3.9 %collective-permute-start = (bf16[2,64,64]{2,1,0:T(8,128)(2,1)S(1)}, bf16[2,64,64]{2,1,0:T(8,128)(2,1)S(1)}, u32[]{:S(2)}, u32[]{:S(2)}) collective-permute-start(bf16[2,64,64]{2,1,0:T(8,128)(2,1)S(1)} %get-tuple-element.27), channel_id=1, source_target_pairs={{0,12},{4,0},{8,4},{12,8},{1,13},{5,1},{9,5},{13,9},{2,14},{6,2},{... | collective-permute-start | bytes 49160 | tf_op jit(solution)/shard_map/ppermute | solution.py:85
  13.8 5.9 %copy-start.1 = (bf16[64,512]{1,0:T(8,128)(2,1)}, bf16[64,512]{1,0:T(8,128)(2,1)S(1)}, u32[]{:S(2)}) copy-start(bf16[64,512]{1,0:T(8,128)(2,1)S(1)} %reshape.32.refs_0_) | copy-start | bytes 196612
  13.8 2.0 %collective-permute-start.5 = (bf16[64,512]{1,0:T(8,128)(2,1)S(1)}, bf16[64,512]{1,0:T(8,128)(2,1)S(1)}, u32[]{:S(2)}, u32[]{:S(2)}) collective-permute-start(bf16[64,512]{1,0:T(8,128)(2,1)S(1)} %reshape.32.refs_0_), channel_id=1, source_target_pairs={{0,3},{1,0},{2,1},{3,2},{4,7},{5,4},{6,5},{7,6},{8,11},{9,8},{10,9... | collective-permute-start | bytes 196616 | tf_op jit(solution)/shard_map/ppermute | solution.py:261
  13.8 5.6 %collective-permute-start.4 = (bf16[64,512]{1,0:T(8,128)(2,1)S(1)}, bf16[64,512]{1,0:T(8,128)(2,1)S(1)}, u32[]{:S(2)}, u32[]{:S(2)}) collective-permute-start(bf16[64,512]{1,0:T(8,128)(2,1)S(1)} %reshape.32.refs_0_), channel_id=1, source_target_pairs={{0,2},{1,3},{2,0},{3,1},{4,6},{5,7},{6,4},{7,5},{8,10},{9,11},{10,... | collective-permute-start | bytes 196616 | tf_op jit(solution)/shard_map/ppermute | solution.py:261
  15.4 4.3 %collective-permute-start.3 = (bf16[64,512]{1,0:T(8,128)(2,1)S(1)}, bf16[64,512]{1,0:T(8,128)(2,1)S(1)}, u32[]{:S(2)}, u32[]{:S(2)}) collective-permute-start(bf16[64,512]{1,0:T(8,128)(2,1)S(1)} %reshape.32.refs_0_), channel_id=1, source_target_pairs={{0,1},{1,2},{2,3},{3,0},{4,5},{5,6},{6,7},{7,4},{8,9},{9,10},{10,1... | collective-permute-start | bytes 196616 | tf_op jit(solution)/shard_map/ppermute | solution.py:261
  15.7 3.9 %copy-start.2 = (bf16[64,512]{1,0:T(8,128)(2,1)}, bf16[64,512]{1,0:T(8,128)(2,1)S(1)}, u32[]{:S(2)}) copy-start(bf16[64,512]{1,0:T(8,128)(2,1)S(1)} %collective-permute-done.5.refs_3_) | copy-start | bytes 196612
  19.5 0.6 %copy-start.3 = (bf16[64,512]{1,0:T(8,128)(2,1)}, bf16[64,512]{1,0:T(8,128)(2,1)S(1)}, u32[]{:S(2)}) copy-start(bf16[64,512]{1,0:T(8,128)(2,1)S(1)} %collective-permute-done.4.refs_2_) | copy-start | bytes 196612
  19.7 0.6 %copy-start.4 = (bf16[64,512]{1,0:T(8,128)(2,1)}, bf16[64,512]{1,0:T(8,128)(2,1)S(1)}, u32[]{:S(2)}) copy-start(bf16[64,512]{1,0:T(8,128)(2,1)S(1)} %collective-permute-done.3.refs_1_) | copy-start | bytes 196612
  28.7 15.7 %copy-start = (f32[2,16,64,64]{3,2,1,0:T(8,128)S(1)}, f32[2,16,64,64]{3,2,1,0:T(8,128)}, u32[]{:S(2)}) copy-start(f32[2,16,64,64]{3,2,1,0:T(8,128)} %param.8) | copy-start | bytes 1572868
  28.7 4.0 %collective-permute-start.6 = (bf16[64,512]{1,0:T(8,128)(2,1)}, bf16[64,512]{1,0:T(8,128)(2,1)S(1)}, u32[]{:S(2)}, u32[]{:S(2)}) collective-permute-start(bf16[64,512]{1,0:T(8,128)(2,1)} %get-tuple-element.10), channel_id=1, source_target_pairs={{0,1},{1,2},{2,3},{3,0},{4,5},{5,6},{6,7},{7,4},{8,9},{9,10},{10,1... | collective-permute-start | bytes 196616 | tf_op jit(solution)/shard_map/ppermute | solution.py:270
  28.8 5.2 %collective-permute-start.7 = (bf16[64,512]{1,0:T(8,128)(2,1)}, bf16[64,512]{1,0:T(8,128)(2,1)S(1)}, u32[]{:S(2)}, u32[]{:S(2)}) collective-permute-start(bf16[64,512]{1,0:T(8,128)(2,1)} %get-tuple-element.11), channel_id=1, source_target_pairs={{0,2},{1,3},{2,0},{3,1},{4,6},{5,7},{6,4},{7,5},{8,10},{9,11},{10,... | collective-permute-start | bytes 196616 | tf_op jit(solution)/shard_map/ppermute | solution.py:270
  29.7 4.3 %collective-permute-start.8 = (bf16[64,512]{1,0:T(8,128)(2,1)}, bf16[64,512]{1,0:T(8,128)(2,1)S(1)}, u32[]{:S(2)}, u32[]{:S(2)}) collective-permute-start(bf16[64,512]{1,0:T(8,128)(2,1)} %get-tuple-element.12), channel_id=1, source_target_pairs={{0,3},{1,0},{2,1},{3,2},{4,7},{5,4},{6,5},{7,6},{8,11},{9,8},{10,9... | collective-permute-start | bytes 196616 | tf_op jit(solution)/shard_map/ppermute | solution.py:270
  35.4 4.9 %collective-permute-start.9 = (bf16[64,2,64]{2,0,1:T(8,128)(2,1)S(1)}, bf16[64,2,64]{2,0,1:T(8,128)(2,1)S(1)}, u32[]{:S(2)}, u32[]{:S(2)}) collective-permute-start(bf16[64,2,64]{2,0,1:T(8,128)(2,1)S(1)} %bitcast.106), channel_id=1, source_target_pairs={{0,12},{4,0},{8,4},{12,8},{1,13},{5,1},{9,5},{13,9},{2,14},{6,2},{... | collective-permute-start | bytes 49160 | tf_op jit(solution)/shard_map/ppermute | solution.py:85
  38.6 4.8 %collective-permute-start.10 = (bf16[64,2,64]{2,0,1:T(8,128)(2,1)S(1)}, bf16[64,2,64]{2,0,1:T(8,128)(2,1)S(1)}, u32[]{:S(2)}, u32[]{:S(2)}) collective-permute-start(bf16[64,2,64]{2,0,1:T(8,128)(2,1)S(1)} %bitcast.105), channel_id=1, source_target_pairs={{0,8},{4,12},{8,0},{12,4},{1,9},{5,13},{9,1},{13,5},{2,10},{6,14},... | collective-permute-start | bytes 49160 | tf_op jit(solution)/shard_map/ppermute | solution.py:85
  38.6 5.7 %collective-permute-start.11 = (bf16[64,2,64]{2,0,1:T(8,128)(2,1)S(1)}, bf16[64,2,64]{2,0,1:T(8,128)(2,1)S(1)}, u32[]{:S(2)}, u32[]{:S(2)}) collective-permute-start(bf16[64,2,64]{2,0,1:T(8,128)(2,1)S(1)} %bitcast.104), channel_id=1, source_target_pairs={{0,4},{4,8},{8,12},{12,0},{1,5},{5,9},{9,13},{13,1},{2,6},{6,10},{... | collective-permute-start | bytes 49160 | tf_op jit(solution)/shard_map/ppermute | solution.py:85

commit v27 on v25

--- a/solution.py
+++ b/solution.py
@@ -276,12 +276,13 @@
     weights = jnp.stack(
         [jnp.stack([late[0].T, late[1].T], axis=2), jnp.stack([-late[1].T, late[0].T], axis=2)], axis=0
     )
+    step_weights = -0.5 * weights
     gradient = None
     for frame in range(returned.shape[0]):
         for part_in in range(2):
-            term = weights[:, :, frame, part_in, None, None] * returned[frame, :, part_in][None, None]
+            term = step_weights[:, :, frame, part_in, None, None] * returned[frame, :, part_in][None, None]
             gradient = term if gradient is None else gradient + term
-    return factors - 0.5 * gradient
+    return factors + gradient
 
 
 def solution(mesh):

time: 46.4 us -> 46.4 us (level)
    sub x1 -> x0, other arithmetic: 1.68 us -> none  [on_device(): return factors - 0.5 * gradient]
    add x0 -> x1, other arithmetic: none -> 1.65 us  [on_device(): return factors + gradient]
where the time goes in v27:
time: 46.4 us; the launch traced here: 46.1 us
  starting transfers between devices  15 us (32%)
  waiting for transfers between devices  13.2 us (28%)
  Pallas kernels  8.42 us (18%)
  other arithmetic  6.36 us (14%)
  local copies, waits for them, and re-layouts  2.94 us (6%)
    ppermute x6, starting transfers between devices, exchange_blocks(): pieces.append(lax.ppermute(outgoing, axis, shifted(count, step)))  10.9 us
    pallas_call x1, Pallas kernels, coil_chain(): pl.pallas_call(coil_chain_kernel, out_shape=(jax.ShapeDtypeStruct((rows,...  8.42 us
    ppermute x6, waiting for transfers between devices, exchange_blocks(): pieces.append(lax.ppermute(outgoing, axis, shifted(count, step)))  6.2 us
    ppermute x3, waiting for transfers between devices, on_device(): lax.ppermute(own_rows, 'coil', shifted(groups, step))  4.09 us
    ppermute x3, waiting for transfers between devices, on_device(): lax.ppermute(outgoing[step - 1], 'coil', shifted(groups, step))  2.86 us
    ppermute x3, starting transfers between devices, on_device(): lax.ppermute(outgoing[step - 1], 'coil', shifted(groups, step))  2.38 us
    reduce_sum x1, other arithmetic, on_device(): jnp.sum(weights_in[:, :, :, None, None] * factors.reshape((parts * ranks,...  2.28 us
    ppermute x3, starting transfers between devices, on_device(): lax.ppermute(own_rows, 'coil', shifted(groups, step))  1.78 us
  transfers between devices with their start and end apart: 12, of which 9 were waited for; matrix products, arithmetic and copies ran while one was open for 3% of the time, Pallas kernels for 0%

profile of v27, /device:TPU:0, one launch (start us, length us, event | category | flops | bytes accessed | tf_op | source)
XLA Modules:
  0.0 46.1 jit_solution(2340712973902437785)
XLA Ops:
  0.0 0.7 %fusion.1 = f32[4,16]{1,0:T(4,128)S(1)} fusion(f32[2,4,16]{2,1,0:T(4,128)} %param.9), kind=kLoop, calls=%fused_computation.52 | loop fusion | flops 64 | bytes 512 | tf_op jit(solution)/shard_map/neg | solution.py:246
  0.7 0.7 %slice_bitcast_fusion.9 = (f32[4,16]{1,0:T(4,128)S(1)}, f32[4,16]{1,0:T(4,128)S(1)}) fusion(f32[2,4,16]{2,1,0:T(4,128)} %param.9), kind=kLoop, calls=%fused_computation.49 | loop fusion | bytes 1024 | tf_op jit(solution)/shard_map/squeeze | solution.py:246
  1.5 2.3 %multiply_reduce_fusion = bf16[2,4,64,64]{3,2,1,0:T(8,128)(2,1)S(1)} fusion(f32[32,64,64]{2,1,0:T(8,128)} %bitcast.103, f32[2,4,32]{2,1,0:T(4,128)S(1)} %pad_maximum_fusion), kind=kLoop, calls=%fused_computation | loop fusion | flops 2064384 | bytes 590848 | tf_op jit(solution)/shard_map/reduce_sum | solution.py:250
  3.8 3.1 %collective-permute-start.2 = (bf16[2,64,64]{2,1,0:T(8,128)(2,1)S(1)}, bf16[2,64,64]{2,1,0:T(8,128)(2,1)S(1)}, u32[]{:S(2)}, u32[]{:S(2)}) collective-permute-start(bf16[2,64,64]{2,1,0:T(8,128)(2,1)S(1)} %get-tuple-element.25), channel_id=1, source_target_pairs={{0,4},{4,8},{8,12},{12,0},{1,5},{5,9},{9,13},{13,1},{2,6},{6,10},{... | collective-permute-start | bytes 49160 | tf_op jit(solution)/shard_map/ppermute | solution.py:85
  6.9 2.6 %collective-permute-start.1 = (bf16[2,64,64]{2,1,0:T(8,128)(2,1)S(1)}, bf16[2,64,64]{2,1,0:T(8,128)(2,1)S(1)}, u32[]{:S(2)}, u32[]{:S(2)}) collective-permute-start(bf16[2,64,64]{2,1,0:T(8,128)(2,1)S(1)} %get-tuple-element.26), channel_id=1, source_target_pairs={{0,8},{4,12},{8,0},{12,4},{1,9},{5,13},{9,1},{13,5},{2,10},{6,14},... | collective-permute-start | bytes 49160 | tf_op jit(solution)/shard_map/ppermute | solution.py:85
  9.4 1.3 %collective-permute-start = (bf16[2,64,64]{2,1,0:T(8,128)(2,1)S(1)}, bf16[2,64,64]{2,1,0:T(8,128)(2,1)S(1)}, u32[]{:S(2)}, u32[]{:S(2)}) collective-permute-start(bf16[2,64,64]{2,1,0:T(8,128)(2,1)S(1)} %get-tuple-element.27), channel_id=1, source_target_pairs={{0,12},{4,0},{8,4},{12,8},{1,13},{5,1},{9,5},{13,9},{2,14},{6,2},{... | collective-permute-start | bytes 49160 | tf_op jit(solution)/shard_map/ppermute | solution.py:85
  10.8 0.7 %fusion = f32[16,4,1]{0,1,2:T(4,128)S(1)} fusion(f32[2,4,16]{2,1,0:T(4,128)} %param.9), kind=kLoop, calls=%fused_computation.48 | loop fusion | flops 64 | bytes 512 | tf_op jit(solution)/shard_map/stack | solution.py:277
  11.5 0.7 %slice_bitcast_fusion.11 = (f32[16,4,1]{0,1,2:T(4,128)S(1)}, f32[16,4,1]{0,1,2:T(4,128)S(1)}) fusion(f32[2,4,16]{2,1,0:T(4,128)} %param.9), kind=kLoop, calls=%fused_computation.51 | loop fusion | bytes 1024 | tf_op jit(solution)/shard_map/stack | solution.py:277
  12.2 1.2 %collective-permute-done = bf16[2,64,64]{2,1,0:T(8,128)(2,1)S(1)} collective-permute-done((bf16[2,64,64]{2,1,0:T(8,128)(2,1)S(1)}, bf16[2,64,64]{2,1,0:T(8,128)(2,1)S(1)}, u32[]{:S(2)}, u32[]{:S(2)}) %collective-permute-start) | collective-permute-done | bytes 16416 | tf_op jit(solution)/shard_map/ppermute | solution.py:85
  13.8 1.6 %collective-permute-start.4 = (bf16[64,512]{1,0:T(8,128)(2,1)S(1)}, bf16[64,512]{1,0:T(8,128)(2,1)S(1)}, u32[]{:S(2)}, u32[]{:S(2)}) collective-permute-start(bf16[64,512]{1,0:T(8,128)(2,1)S(1)} %reshape.32.refs_0_), channel_id=1, source_target_pairs={{0,2},{1,3},{2,0},{3,1},{4,6},{5,7},{6,4},{7,5},{8,10},{9,11},{10,... | collective-permute-start | bytes 196616 | tf_op jit(solution)/shard_map/ppermute | solution.py:261
  15.7 3.7 %collective-permute-done.4.refs_2_ = bf16[64,512]{1,0:T(8,128)(2,1)S(1)} collective-permute-done((bf16[64,512]{1,0:T(8,128)(2,1)S(1)}, bf16[64,512]{1,0:T(8,128)(2,1)S(1)}, u32[]{:S(2)}, u32[]{:S(2)}) %collective-permute-start.4) | collective-permute-done | bytes 65568 | tf_op jit(solution)/shard_map/ppermute | solution.py:261
  19.7 0.4 copy-done.3
  20.3 8.4 %shard_map.82 = (f32[64,512]{1,0:T(8,128)}, bf16[64,512]{1,0:T(8,128)(2,1)}, bf16[64,512]{1,0:T(8,128)(2,1)}, bf16[64,512]{1,0:T(8,128)(2,1)}) custom-call(bf16[64,512]{1,0:T(8,128)(2,1)} %copy-done.1, bf16[64,512]{1,0:T(8,128)(2,1)} %copy-done.4, bf16[64,512]{1,0:T(8,128)(2,1)} %copy-done.3, bf16[64,512]{1,0:T(8,128)(2,1)} %copy-done.2, s32[1]{0:T(128)} %bitcast.26.refs_4_, ...), custom_call_target="tpu_custom_call" | custom-call | flops 4294967296 | bytes 4718592 | tf_op jit(solution)/shard_map/pallas_call | solution.py:208
  28.8 0.9 %collective-permute-start.7 = (bf16[64,512]{1,0:T(8,128)(2,1)}, bf16[64,512]{1,0:T(8,128)(2,1)S(1)}, u32[]{:S(2)}, u32[]{:S(2)}) collective-permute-start(bf16[64,512]{1,0:T(8,128)(2,1)} %get-tuple-element.11), channel_id=1, source_target_pairs={{0,2},{1,3},{2,0},{3,1},{4,6},{5,7},{6,4},{7,5},{8,10},{9,11},{10,... | collective-permute-start | bytes 196616 | tf_op jit(solution)/shard_map/ppermute | solution.py:270
  29.7 1.4 %collective-permute-start.8 = (bf16[64,512]{1,0:T(8,128)(2,1)}, bf16[64,512]{1,0:T(8,128)(2,1)S(1)}, u32[]{:S(2)}, u32[]{:S(2)}) collective-permute-start(bf16[64,512]{1,0:T(8,128)(2,1)} %get-tuple-element.12), channel_id=1, source_target_pairs={{0,3},{1,0},{2,1},{3,2},{4,7},{5,4},{6,5},{7,6},{8,11},{9,8},{10,9... | collective-permute-start | bytes 196616 | tf_op jit(solution)/shard_map/ppermute | solution.py:270
  31.1 1.6 %collective-permute-done.6 = bf16[64,512]{1,0:T(8,128)(2,1)S(1)} collective-permute-done((bf16[64,512]{1,0:T(8,128)(2,1)}, bf16[64,512]{1,0:T(8,128)(2,1)S(1)}, u32[]{:S(2)}, u32[]{:S(2)}) %collective-permute-start.6) | collective-permute-done | bytes 65568 | tf_op jit(solution)/shard_map/ppermute | solution.py:270
  32.8 1.2 %collective-permute-done.7 = bf16[64,512]{1,0:T(8,128)(2,1)S(1)} collective-permute-done((bf16[64,512]{1,0:T(8,128)(2,1)}, bf16[64,512]{1,0:T(8,128)(2,1)S(1)}, u32[]{:S(2)}, u32[]{:S(2)}) %collective-permute-start.7) | collective-permute-done | bytes 65568 | tf_op jit(solution)/shard_map/ppermute | solution.py:270
  34.0 0.9 %add_convert_fusion = bf16[64,512]{1,0:T(8,128)(2,1)S(1)} fusion(bf16[64,512]{1,0:T(8,128)(2,1)S(1)} %collective-permute-done.8, bf16[64,512]{1,0:T(8,128)(2,1)S(1)} %collective-permute-done.7, f32[64,512]{1,0:T(8,128)} %get-tuple-element.9, bf16[64,512]{1,0:T(8,128)(2,1)S(1)} %collective-permute-done.6), kind=kLoop, calls=%fused_computation.3 | loop fusion | flops 229376 | bytes 393216 | tf_op jit(solution)/shard_map/convert_element_type | solution.py:273
  35.4 3.2 %collective-permute-start.9 = (bf16[64,2,64]{2,0,1:T(8,128)(2,1)S(1)}, bf16[64,2,64]{2,0,1:T(8,128)(2,1)S(1)}, u32[]{:S(2)}, u32[]{:S(2)}) collective-permute-start(bf16[64,2,64]{2,0,1:T(8,128)(2,1)S(1)} %bitcast.106), channel_id=1, source_target_pairs={{0,12},{4,0},{8,4},{12,8},{1,13},{5,1},{9,5},{13,9},{2,14},{6,2},{... | collective-permute-start | bytes 49160 | tf_op jit(solution)/shard_map/ppermute | solution.py:85
  38.6 0.6 %collective-permute-start.11 = (bf16[64,2,64]{2,0,1:T(8,128)(2,1)S(1)}, bf16[64,2,64]{2,0,1:T(8,128)(2,1)S(1)}, u32[]{:S(2)}, u32[]{:S(2)}) collective-permute-start(bf16[64,2,64]{2,0,1:T(8,128)(2,1)S(1)} %bitcast.104), channel_id=1, source_target_pairs={{0,4},{4,8},{8,12},{12,0},{1,5},{5,9},{9,13},{13,1},{2,6},{6,10},{... | collective-permute-start | bytes 49160 | tf_op jit(solution)/shard_map/ppermute | solution.py:85
  39.2 1.0 %collective-permute-done.9 = bf16[64,2,64]{2,0,1:T(8,128)(2,1)S(1)} collective-permute-done((bf16[64,2,64]{2,0,1:T(8,128)(2,1)S(1)}, bf16[64,2,64]{2,0,1:T(8,128)(2,1)S(1)}, u32[]{:S(2)}, u32[]{:S(2)}) %collective-permute-start.9) | collective-permute-done | bytes 16416 | tf_op jit(solution)/shard_map/ppermute | solution.py:85
  40.3 3.1 %collective-permute-done.10 = bf16[64,2,64]{2,0,1:T(8,128)(2,1)S(1)} collective-permute-done((bf16[64,2,64]{2,0,1:T(8,128)(2,1)S(1)}, bf16[64,2,64]{2,0,1:T(8,128)(2,1)S(1)}, u32[]{:S(2)}, u32[]{:S(2)}) %collective-permute-start.10) | collective-permute-done | bytes 16416 | tf_op jit(solution)/shard_map/ppermute | solution.py:85
  43.4 0.9 %collective-permute-done.11 = bf16[64,2,64]{2,0,1:T(8,128)(2,1)S(1)} collective-permute-done((bf16[64,2,64]{2,0,1:T(8,128)(2,1)S(1)}, bf16[64,2,64]{2,0,1:T(8,128)(2,1)S(1)}, u32[]{:S(2)}, u32[]{:S(2)}) %collective-permute-start.11) | collective-permute-done | bytes 16416 | tf_op jit(solution)/shard_map/ppermute | solution.py:85
  44.5 1.6 %add_add_fusion = f32[2,16,64,64]{3,2,1,0:T(8,128)} fusion(f32[2,16,64,64]{3,2,1,0:T(8,128)S(1)} %copy-done, f32[64,64]{1,0:T(8,128)S(1)} %get-tuple-element.14, f32[2,16]{1,0:T(2,128)S(1)} %bitcast.108, f32[64,64]{1,0:T(8,128)S(1)} %get-tuple-element.15, f32[2,16]{1,0:T(2,128)S(1)} %bitcast.109, f32[64,64]{1,0:T(8,128)S(1)} %get-tuple-element.16, ...), kind=kLoop, calls=%fused_computation.1 | loop fusion | flops 2097152 | bytes 1180672 | tf_op jit(solution)/shard_map/add | solution.py:285
  (50 shorter events, 1.9 us)
Async XLA Ops:
  3.8 9.6 %collective-permute-start.2 = (bf16[2,64,64]{2,1,0:T(8,128)(2,1)S(1)}, bf16[2,64,64]{2,1,0:T(8,128)(2,1)S(1)}, u32[]{:S(2)}, u32[]{:S(2)}) collective-permute-start(bf16[2,64,64]{2,1,0:T(8,128)(2,1)S(1)} %get-tuple-element.25), channel_id=1, source_target_pairs={{0,4},{4,8},{8,12},{12,0},{1,5},{5,9},{9,13},{13,1},{2,6},{6,10},{... | collective-permute-start | bytes 49160 | tf_op jit(solution)/shard_map/ppermute | solution.py:85
  6.9 6.5 %collective-permute-start.1 = (bf16[2,64,64]{2,1,0:T(8,128)(2,1)S(1)}, bf16[2,64,64]{2,1,0:T(8,128)(2,1)S(1)}, u32[]{:S(2)}, u32[]{:S(2)}) collective-permute-start(bf16[2,64,64]{2,1,0:T(8,128)(2,1)S(1)} %get-tuple-element.26), channel_id=1, source_target_pairs={{0,8},{4,12},{8,0},{12,4},{1,9},{5,13},{9,1},{13,5},{2,10},{6,14},... | collective-permute-start | bytes 49160 | tf_op jit(solution)/shard_map/ppermute | solution.py:85
  9.4 3.9 %collective-permute-start = (bf16[2,64,64]{2,1,0:T(8,128)(2,1)S(1)}, bf16[2,64,64]{2,1,0:T(8,128)(2,1)S(1)}, u32[]{:S(2)}, u32[]{:S(2)}) collective-permute-start(bf16[2,64,64]{2,1,0:T(8,128)(2,1)S(1)} %get-tuple-element.27), channel_id=1, source_target_pairs={{0,12},{4,0},{8,4},{12,8},{1,13},{5,1},{9,5},{13,9},{2,14},{6,2},{... | collective-permute-start | bytes 49160 | tf_op jit(solution)/shard_map/ppermute | solution.py:85
  13.8 5.9 %copy-start.1 = (bf16[64,512]{1,0:T(8,128)(2,1)}, bf16[64,512]{1,0:T(8,128)(2,1)S(1)}, u32[]{:S(2)}) copy-start(bf16[64,512]{1,0:T(8,128)(2,1)S(1)} %reshape.32.refs_0_) | copy-start | bytes 196612
  13.8 2.0 %collective-permute-start.5 = (bf16[64,512]{1,0:T(8,128)(2,1)S(1)}, bf16[64,512]{1,0:T(8,128)(2,1)S(1)}, u32[]{:S(2)}, u32[]{:S(2)}) collective-permute-start(bf16[64,512]{1,0:T(8,128)(2,1)S(1)} %reshape.32.refs_0_), channel_id=1, source_target_pairs={{0,3},{1,0},{2,1},{3,2},{4,7},{5,4},{6,5},{7,6},{8,11},{9,8},{10,9... | collective-permute-start | bytes 196616 | tf_op jit(solution)/shard_map/ppermute | solution.py:261
  13.8 5.6 %collective-permute-start.4 = (bf16[64,512]{1,0:T(8,128)(2,1)S(1)}, bf16[64,512]{1,0:T(8,128)(2,1)S(1)}, u32[]{:S(2)}, u32[]{:S(2)}) collective-permute-start(bf16[64,512]{1,0:T(8,128)(2,1)S(1)} %reshape.32.refs_0_), channel_id=1, source_target_pairs={{0,2},{1,3},{2,0},{3,1},{4,6},{5,7},{6,4},{7,5},{8,10},{9,11},{10,... | collective-permute-start | bytes 196616 | tf_op jit(solution)/shard_map/ppermute | solution.py:261
  15.4 4.3 %collective-permute-start.3 = (bf16[64,512]{1,0:T(8,128)(2,1)S(1)}, bf16[64,512]{1,0:T(8,128)(2,1)S(1)}, u32[]{:S(2)}, u32[]{:S(2)}) collective-permute-start(bf16[64,512]{1,0:T(8,128)(2,1)S(1)} %reshape.32.refs_0_), channel_id=1, source_target_pairs={{0,1},{1,2},{2,3},{3,0},{4,5},{5,6},{6,7},{7,4},{8,9},{9,10},{10,1... | collective-permute-start | bytes 196616 | tf_op jit(solution)/shard_map/ppermute | solution.py:261
  15.7 3.9 %copy-start.2 = (bf16[64,512]{1,0:T(8,128)(2,1)}, bf16[64,512]{1,0:T(8,128)(2,1)S(1)}, u32[]{:S(2)}) copy-start(bf16[64,512]{1,0:T(8,128)(2,1)S(1)} %collective-permute-done.5.refs_3_) | copy-start | bytes 196612
  19.5 0.6 %copy-start.3 = (bf16[64,512]{1,0:T(8,128)(2,1)}, bf16[64,512]{1,0:T(8,128)(2,1)S(1)}, u32[]{:S(2)}) copy-start(bf16[64,512]{1,0:T(8,128)(2,1)S(1)} %collective-permute-done.4.refs_2_) | copy-start | bytes 196612
  19.7 0.6 %copy-start.4 = (bf16[64,512]{1,0:T(8,128)(2,1)}, bf16[64,512]{1,0:T(8,128)(2,1)S(1)}, u32[]{:S(2)}) copy-start(bf16[64,512]{1,0:T(8,128)(2,1)S(1)} %collective-permute-done.3.refs_1_) | copy-start | bytes 196612
  28.7 15.7 %copy-start = (f32[2,16,64,64]{3,2,1,0:T(8,128)S(1)}, f32[2,16,64,64]{3,2,1,0:T(8,128)}, u32[]{:S(2)}) copy-start(f32[2,16,64,64]{3,2,1,0:T(8,128)} %param.8) | copy-start | bytes 1572868
  28.7 4.0 %collective-permute-start.6 = (bf16[64,512]{1,0:T(8,128)(2,1)}, bf16[64,512]{1,0:T(8,128)(2,1)S(1)}, u32[]{:S(2)}, u32[]{:S(2)}) collective-permute-start(bf16[64,512]{1,0:T(8,128)(2,1)} %get-tuple-element.10), channel_id=1, source_target_pairs={{0,1},{1,2},{2,3},{3,0},{4,5},{5,6},{6,7},{7,4},{8,9},{9,10},{10,1... | collective-permute-start | bytes 196616 | tf_op jit(solution)/shard_map/ppermute | solution.py:270
  28.8 5.2 %collective-permute-start.7 = (bf16[64,512]{1,0:T(8,128)(2,1)}, bf16[64,512]{1,0:T(8,128)(2,1)S(1)}, u32[]{:S(2)}, u32[]{:S(2)}) collective-permute-start(bf16[64,512]{1,0:T(8,128)(2,1)} %get-tuple-element.11), channel_id=1, source_target_pairs={{0,2},{1,3},{2,0},{3,1},{4,6},{5,7},{6,4},{7,5},{8,10},{9,11},{10,... | collective-permute-start | bytes 196616 | tf_op jit(solution)/shard_map/ppermute | solution.py:270
  29.7 4.3 %collective-permute-start.8 = (bf16[64,512]{1,0:T(8,128)(2,1)}, bf16[64,512]{1,0:T(8,128)(2,1)S(1)}, u32[]{:S(2)}, u32[]{:S(2)}) collective-permute-start(bf16[64,512]{1,0:T(8,128)(2,1)} %get-tuple-element.12), channel_id=1, source_target_pairs={{0,3},{1,0},{2,1},{3,2},{4,7},{5,4},{6,5},{7,6},{8,11},{9,8},{10,9... | collective-permute-start | bytes 196616 | tf_op jit(solution)/shard_map/ppermute | solution.py:270
  35.4 4.9 %collective-permute-start.9 = (bf16[64,2,64]{2,0,1:T(8,128)(2,1)S(1)}, bf16[64,2,64]{2,0,1:T(8,128)(2,1)S(1)}, u32[]{:S(2)}, u32[]{:S(2)}) collective-permute-start(bf16[64,2,64]{2,0,1:T(8,128)(2,1)S(1)} %bitcast.106), channel_id=1, source_target_pairs={{0,12},{4,0},{8,4},{12,8},{1,13},{5,1},{9,5},{13,9},{2,14},{6,2},{... | collective-permute-start | bytes 49160 | tf_op jit(solution)/shard_map/ppermute | solution.py:85
  38.6 4.8 %collective-permute-start.10 = (bf16[64,2,64]{2,0,1:T(8,128)(2,1)S(1)}, bf16[64,2,64]{2,0,1:T(8,128)(2,1)S(1)}, u32[]{:S(2)}, u32[]{:S(2)}) collective-permute-start(bf16[64,2,64]{2,0,1:T(8,128)(2,1)S(1)} %bitcast.105), channel_id=1, source_target_pairs={{0,8},{4,12},{8,0},{12,4},{1,9},{5,13},{9,1},{13,5},{2,10},{6,14},... | collective-permute-start | bytes 49160 | tf_op jit(solution)/shard_map/ppermute | solution.py:85
  38.6 5.7 %collective-permute-start.11 = (bf16[64,2,64]{2,0,1:T(8,128)(2,1)S(1)}, bf16[64,2,64]{2,0,1:T(8,128)(2,1)S(1)}, u32[]{:S(2)}, u32[]{:S(2)}) collective-permute-start(bf16[64,2,64]{2,0,1:T(8,128)(2,1)S(1)} %bitcast.104), channel_id=1, source_target_pairs={{0,4},{4,8},{8,12},{12,0},{1,5},{5,9},{9,13},{13,1},{2,6},{6,10},{... | collective-permute-start | bytes 49160 | tf_op jit(solution)/shard_map/ppermute | solution.py:85

commit v28 on v27

--- a/solution.py
+++ b/solution.py
@@ -241,12 +241,16 @@
     time_re = temporal[0]
     time_im = temporal[1]
     parts, ranks = factors.shape[:2]
+    ranks_all = temporal.shape[2]
+    sign = jnp.asarray(np.concatenate([np.ones((1, 1, ranks_all)), -np.ones((1, 1, ranks_all))], axis=2)
+                       .astype(np.float32) * np.array([1.0, 0.0], np.float32)[:, None, None]
+                       + np.array([0.0, 1.0], np.float32)[:, None, None])
     weights_in = jnp.stack(
         [
-            jnp.concatenate([temporal[0], -temporal[1]], axis=-1),
+            jnp.concatenate([temporal[0], temporal[1]], axis=-1),
             jnp.concatenate([temporal[1], temporal[0]], axis=-1),
         ]
-    )
+    ) * sign
     images = jnp.sum(
         weights_in[:, :, :, None, None] * factors.reshape((parts * ranks,) + factors.shape[2:])[None, None],
         axis=2,

time: 46.4 us -> 46.4 us (level)
    mul x0 -> x1, other arithmetic: none -> 0.69 us  [on_device(): jnp.stack([jnp.concatenate([temporal[0], temporal[1]], axis=-1), jnp.conc...]
    neg x1 -> x0, other arithmetic: 0.68 us -> none  [on_device(): -temporal[1]]
where the time goes in v28:
time: 46.4 us; the launch traced here: 46.1 us
  starting transfers between devices  15 us (32%)
  waiting for transfers between devices  13.2 us (28%)
  Pallas kernels  8.42 us (18%)
  other arithmetic  6.35 us (14%)
  local copies, waits for them, and re-layouts  2.94 us (6%)
    ppermute x6, starting transfers between devices, exchange_blocks(): pieces.append(lax.ppermute(outgoing, axis, shifted(count, step)))  10.9 us
    pallas_call x1, Pallas kernels, coil_chain(): pl.pallas_call(coil_chain_kernel, out_shape=(jax.ShapeDtypeStruct((rows,...  8.42 us
    ppermute x6, waiting for transfers between devices, exchange_blocks(): pieces.append(lax.ppermute(outgoing, axis, shifted(count, step)))  6.2 us
    ppermute x3, waiting for transfers between devices, on_device(): lax.ppermute(own_rows, 'coil', shifted(groups, step))  4.09 us
    ppermute x3, waiting for transfers between devices, on_device(): lax.ppermute(outgoing[step - 1], 'coil', shifted(groups, step))  2.86 us
    ppermute x3, starting transfers between devices, on_device(): lax.ppermute(outgoing[step - 1], 'coil', shifted(groups, step))  2.38 us
    reduce_sum x1, other arithmetic, on_device(): jnp.sum(weights_in[:, :, :, None, None] * factors.reshape((parts * ranks,...  2.28 us
    ppermute x3, starting transfers between devices, on_device(): lax.ppermute(own_rows, 'coil', shifted(groups, step))  1.78 us
  transfers between devices with their start and end apart: 12, of which 9 were waited for; matrix products, arithmetic and copies ran while one was open for 3% of the time, Pallas kernels for 0%

profile of v28, /device:TPU:0, one launch (start us, length us, event | category | flops | bytes accessed | tf_op | source)
XLA Modules:
  0.0 46.1 jit_solution(11857347258703037176)
XLA Ops:
  0.0 0.7 %slice_bitcast_fusion.9 = (f32[4,16]{1,0:T(4,128)S(1)}, f32[4,16]{1,0:T(4,128)S(1)}) fusion(f32[2,4,16]{2,1,0:T(4,128)} %param.10), kind=kLoop, calls=%fused_computation.49 | loop fusion | bytes 1024 | tf_op jit(solution)/shard_map/squeeze | solution.py:250
  0.8 0.7 %maximum_multiply_fusion.1 = f32[2,4,32]{2,1,0:T(4,128)S(1)} fusion(f32[1,4,32]{2,1,0:T(4,128)S(1)} %get-tuple-element.39, f32[1,4,32]{2,1,0:T(4,128)S(1)} %get-tuple-element.38, f32[2,32]{1,0:T(2,128)} %constant.86), kind=kLoop, calls=%fused_computation.39 | loop fusion | flops 512 | bytes 2304 | tf_op jit(solution)/shard_map/mul | solution.py:248
  1.5 2.3 %multiply_reduce_fusion = bf16[2,4,64,64]{3,2,1,0:T(8,128)(2,1)S(1)} fusion(f32[32,64,64]{2,1,0:T(8,128)} %bitcast.101, f32[2,4,32]{2,1,0:T(4,128)S(1)} %maximum_multiply_fusion.1), kind=kLoop, calls=%fused_computation | loop fusion | flops 2064384 | bytes 590848 | tf_op jit(solution)/shard_map/reduce_sum | solution.py:254
  3.8 3.1 %collective-permute-start.2 = (bf16[2,64,64]{2,1,0:T(8,128)(2,1)S(1)}, bf16[2,64,64]{2,1,0:T(8,128)(2,1)S(1)}, u32[]{:S(2)}, u32[]{:S(2)}) collective-permute-start(bf16[2,64,64]{2,1,0:T(8,128)(2,1)S(1)} %get-tuple-element.25), channel_id=1, source_target_pairs={{0,4},{4,8},{8,12},{12,0},{1,5},{5,9},{9,13},{13,1},{2,6},{6,10},{... | collective-permute-start | bytes 49160 | tf_op jit(solution)/shard_map/ppermute | solution.py:85
  6.9 2.6 %collective-permute-start.1 = (bf16[2,64,64]{2,1,0:T(8,128)(2,1)S(1)}, bf16[2,64,64]{2,1,0:T(8,128)(2,1)S(1)}, u32[]{:S(2)}, u32[]{:S(2)}) collective-permute-start(bf16[2,64,64]{2,1,0:T(8,128)(2,1)S(1)} %get-tuple-element.26), channel_id=1, source_target_pairs={{0,8},{4,12},{8,0},{12,4},{1,9},{5,13},{9,1},{13,5},{2,10},{6,14},... | collective-permute-start | bytes 49160 | tf_op jit(solution)/shard_map/ppermute | solution.py:85
  9.4 1.3 %collective-permute-start = (bf16[2,64,64]{2,1,0:T(8,128)(2,1)S(1)}, bf16[2,64,64]{2,1,0:T(8,128)(2,1)S(1)}, u32[]{:S(2)}, u32[]{:S(2)}) collective-permute-start(bf16[2,64,64]{2,1,0:T(8,128)(2,1)S(1)} %get-tuple-element.27), channel_id=1, source_target_pairs={{0,12},{4,0},{8,4},{12,8},{1,13},{5,1},{9,5},{13,9},{2,14},{6,2},{... | collective-permute-start | bytes 49160 | tf_op jit(solution)/shard_map/ppermute | solution.py:85
  10.8 0.7 %fusion = f32[16,4,1]{0,1,2:T(4,128)S(1)} fusion(f32[2,4,16]{2,1,0:T(4,128)} %param.10), kind=kLoop, calls=%fused_computation.48 | loop fusion | flops 64 | bytes 512 | tf_op jit(solution)/shard_map/stack | solution.py:281
  11.5 0.7 %slice_bitcast_fusion.11 = (f32[16,4,1]{0,1,2:T(4,128)S(1)}, f32[16,4,1]{0,1,2:T(4,128)S(1)}) fusion(f32[2,4,16]{2,1,0:T(4,128)} %param.10), kind=kLoop, calls=%fused_computation.51 | loop fusion | bytes 1024 | tf_op jit(solution)/shard_map/stack | solution.py:281
  12.2 1.2 %collective-permute-done = bf16[2,64,64]{2,1,0:T(8,128)(2,1)S(1)} collective-permute-done((bf16[2,64,64]{2,1,0:T(8,128)(2,1)S(1)}, bf16[2,64,64]{2,1,0:T(8,128)(2,1)S(1)}, u32[]{:S(2)}, u32[]{:S(2)}) %collective-permute-start) | collective-permute-done | bytes 16416 | tf_op jit(solution)/shard_map/ppermute | solution.py:85
  13.8 1.6 %collective-permute-start.4 = (bf16[64,512]{1,0:T(8,128)(2,1)S(1)}, bf16[64,512]{1,0:T(8,128)(2,1)S(1)}, u32[]{:S(2)}, u32[]{:S(2)}) collective-permute-start(bf16[64,512]{1,0:T(8,128)(2,1)S(1)} %reshape.48.refs_0_), channel_id=1, source_target_pairs={{0,2},{1,3},{2,0},{3,1},{4,6},{5,7},{6,4},{7,5},{8,10},{9,11},{10,... | collective-permute-start | bytes 196616 | tf_op jit(solution)/shard_map/ppermute | solution.py:265
  15.7 3.7 %collective-permute-done.4.refs_2_ = bf16[64,512]{1,0:T(8,128)(2,1)S(1)} collective-permute-done((bf16[64,512]{1,0:T(8,128)(2,1)S(1)}, bf16[64,512]{1,0:T(8,128)(2,1)S(1)}, u32[]{:S(2)}, u32[]{:S(2)}) %collective-permute-start.4) | collective-permute-done | bytes 65568 | tf_op jit(solution)/shard_map/ppermute | solution.py:265
  19.7 0.4 copy-done.3
  20.3 8.4 %shard_map.91 = (f32[64,512]{1,0:T(8,128)}, bf16[64,512]{1,0:T(8,128)(2,1)}, bf16[64,512]{1,0:T(8,128)(2,1)}, bf16[64,512]{1,0:T(8,128)(2,1)}) custom-call(bf16[64,512]{1,0:T(8,128)(2,1)} %copy-done.1, bf16[64,512]{1,0:T(8,128)(2,1)} %copy-done.4, bf16[64,512]{1,0:T(8,128)(2,1)} %copy-done.3, bf16[64,512]{1,0:T(8,128)(2,1)} %copy-done.2, s32[1]{0:T(128)} %bitcast.26.refs_4_, ...), custom_call_target="tpu_custom_call" | custom-call | flops 4294967296 | bytes 4718592 | tf_op jit(solution)/shard_map/pallas_call | solution.py:208
  28.8 0.9 %collective-permute-start.7 = (bf16[64,512]{1,0:T(8,128)(2,1)}, bf16[64,512]{1,0:T(8,128)(2,1)S(1)}, u32[]{:S(2)}, u32[]{:S(2)}) collective-permute-start(bf16[64,512]{1,0:T(8,128)(2,1)} %get-tuple-element.11), channel_id=1, source_target_pairs={{0,2},{1,3},{2,0},{3,1},{4,6},{5,7},{6,4},{7,5},{8,10},{9,11},{10,... | collective-permute-start | bytes 196616 | tf_op jit(solution)/shard_map/ppermute | solution.py:274
  29.7 1.4 %collective-permute-start.8 = (bf16[64,512]{1,0:T(8,128)(2,1)}, bf16[64,512]{1,0:T(8,128)(2,1)S(1)}, u32[]{:S(2)}, u32[]{:S(2)}) collective-permute-start(bf16[64,512]{1,0:T(8,128)(2,1)} %get-tuple-element.12), channel_id=1, source_target_pairs={{0,3},{1,0},{2,1},{3,2},{4,7},{5,4},{6,5},{7,6},{8,11},{9,8},{10,9... | collective-permute-start | bytes 196616 | tf_op jit(solution)/shard_map/ppermute | solution.py:274
  31.1 1.6 %collective-permute-done.6 = bf16[64,512]{1,0:T(8,128)(2,1)S(1)} collective-permute-done((bf16[64,512]{1,0:T(8,128)(2,1)}, bf16[64,512]{1,0:T(8,128)(2,1)S(1)}, u32[]{:S(2)}, u32[]{:S(2)}) %collective-permute-start.6) | collective-permute-done | bytes 65568 | tf_op jit(solution)/shard_map/ppermute | solution.py:274
  32.7 1.2 %collective-permute-done.7 = bf16[64,512]{1,0:T(8,128)(2,1)S(1)} collective-permute-done((bf16[64,512]{1,0:T(8,128)(2,1)}, bf16[64,512]{1,0:T(8,128)(2,1)S(1)}, u32[]{:S(2)}, u32[]{:S(2)}) %collective-permute-start.7) | collective-permute-done | bytes 65568 | tf_op jit(solution)/shard_map/ppermute | solution.py:274
  34.0 0.9 %add_convert_fusion = bf16[64,512]{1,0:T(8,128)(2,1)S(1)} fusion(bf16[64,512]{1,0:T(8,128)(2,1)S(1)} %collective-permute-done.8, bf16[64,512]{1,0:T(8,128)(2,1)S(1)} %collective-permute-done.7, f32[64,512]{1,0:T(8,128)} %get-tuple-element.9, bf16[64,512]{1,0:T(8,128)(2,1)S(1)} %collective-permute-done.6), kind=kLoop, calls=%fused_computation.3 | loop fusion | flops 229376 | bytes 393216 | tf_op jit(solution)/shard_map/convert_element_type | solution.py:277
  35.4 3.2 %collective-permute-start.9 = (bf16[64,2,64]{2,0,1:T(8,128)(2,1)S(1)}, bf16[64,2,64]{2,0,1:T(8,128)(2,1)S(1)}, u32[]{:S(2)}, u32[]{:S(2)}) collective-permute-start(bf16[64,2,64]{2,0,1:T(8,128)(2,1)S(1)} %bitcast.104), channel_id=1, source_target_pairs={{0,12},{4,0},{8,4},{12,8},{1,13},{5,1},{9,5},{13,9},{2,14},{6,2},{... | collective-permute-start | bytes 49160 | tf_op jit(solution)/shard_map/ppermute | solution.py:85
  38.6 0.6 %collective-permute-start.11 = (bf16[64,2,64]{2,0,1:T(8,128)(2,1)S(1)}, bf16[64,2,64]{2,0,1:T(8,128)(2,1)S(1)}, u32[]{:S(2)}, u32[]{:S(2)}) collective-permute-start(bf16[64,2,64]{2,0,1:T(8,128)(2,1)S(1)} %bitcast.102), channel_id=1, source_target_pairs={{0,4},{4,8},{8,12},{12,0},{1,5},{5,9},{9,13},{13,1},{2,6},{6,10},{... | collective-permute-start | bytes 49160 | tf_op jit(solution)/shard_map/ppermute | solution.py:85
  39.2 1.0 %collective-permute-done.9 = bf16[64,2,64]{2,0,1:T(8,128)(2,1)S(1)} collective-permute-done((bf16[64,2,64]{2,0,1:T(8,128)(2,1)S(1)}, bf16[64,2,64]{2,0,1:T(8,128)(2,1)S(1)}, u32[]{:S(2)}, u32[]{:S(2)}) %collective-permute-start.9) | collective-permute-done | bytes 16416 | tf_op jit(solution)/shard_map/ppermute | solution.py:85
  40.3 3.1 %collective-permute-done.10 = bf16[64,2,64]{2,0,1:T(8,128)(2,1)S(1)} collective-permute-done((bf16[64,2,64]{2,0,1:T(8,128)(2,1)S(1)}, bf16[64,2,64]{2,0,1:T(8,128)(2,1)S(1)}, u32[]{:S(2)}, u32[]{:S(2)}) %collective-permute-start.10) | collective-permute-done | bytes 16416 | tf_op jit(solution)/shard_map/ppermute | solution.py:85
  43.4 0.9 %collective-permute-done.11 = bf16[64,2,64]{2,0,1:T(8,128)(2,1)S(1)} collective-permute-done((bf16[64,2,64]{2,0,1:T(8,128)(2,1)S(1)}, bf16[64,2,64]{2,0,1:T(8,128)(2,1)S(1)}, u32[]{:S(2)}, u32[]{:S(2)}) %collective-permute-start.11) | collective-permute-done | bytes 16416 | tf_op jit(solution)/shard_map/ppermute | solution.py:85
  44.4 1.6 %add_add_fusion = f32[2,16,64,64]{3,2,1,0:T(8,128)} fusion(f32[2,16,64,64]{3,2,1,0:T(8,128)S(1)} %copy-done, f32[64,64]{1,0:T(8,128)S(1)} %get-tuple-element.14, f32[2,16]{1,0:T(2,128)S(1)} %bitcast.106, f32[64,64]{1,0:T(8,128)S(1)} %get-tuple-element.15, f32[2,16]{1,0:T(2,128)S(1)} %bitcast.107, f32[64,64]{1,0:T(8,128)S(1)} %get-tuple-element.16, ...), kind=kLoop, calls=%fused_computation.1 | loop fusion | flops 2097152 | bytes 1180672 | tf_op jit(solution)/shard_map/add | solution.py:289
  (49 shorter events, 1.9 us)
Async XLA Ops:
  3.8 9.6 %collective-permute-start.2 = (bf16[2,64,64]{2,1,0:T(8,128)(2,1)S(1)}, bf16[2,64,64]{2,1,0:T(8,128)(2,1)S(1)}, u32[]{:S(2)}, u32[]{:S(2)}) collective-permute-start(bf16[2,64,64]{2,1,0:T(8,128)(2,1)S(1)} %get-tuple-element.25), channel_id=1, source_target_pairs={{0,4},{4,8},{8,12},{12,0},{1,5},{5,9},{9,13},{13,1},{2,6},{6,10},{... | collective-permute-start | bytes 49160 | tf_op jit(solution)/shard_map/ppermute | solution.py:85
  6.9 6.5 %collective-permute-start.1 = (bf16[2,64,64]{2,1,0:T(8,128)(2,1)S(1)}, bf16[2,64,64]{2,1,0:T(8,128)(2,1)S(1)}, u32[]{:S(2)}, u32[]{:S(2)}) collective-permute-start(bf16[2,64,64]{2,1,0:T(8,128)(2,1)S(1)} %get-tuple-element.26), channel_id=1, source_target_pairs={{0,8},{4,12},{8,0},{12,4},{1,9},{5,13},{9,1},{13,5},{2,10},{6,14},... | collective-permute-start | bytes 49160 | tf_op jit(solution)/shard_map/ppermute | solution.py:85
  9.4 3.9 %collective-permute-start = (bf16[2,64,64]{2,1,0:T(8,128)(2,1)S(1)}, bf16[2,64,64]{2,1,0:T(8,128)(2,1)S(1)}, u32[]{:S(2)}, u32[]{:S(2)}) collective-permute-start(bf16[2,64,64]{2,1,0:T(8,128)(2,1)S(1)} %get-tuple-element.27), channel_id=1, source_target_pairs={{0,12},{4,0},{8,4},{12,8},{1,13},{5,1},{9,5},{13,9},{2,14},{6,2},{... | collective-permute-start | bytes 49160 | tf_op jit(solution)/shard_map/ppermute | solution.py:85
  13.8 5.9 %copy-start.1 = (bf16[64,512]{1,0:T(8,128)(2,1)}, bf16[64,512]{1,0:T(8,128)(2,1)S(1)}, u32[]{:S(2)}) copy-start(bf16[64,512]{1,0:T(8,128)(2,1)S(1)} %reshape.48.refs_0_) | copy-start | bytes 196612
  13.8 2.0 %collective-permute-start.5 = (bf16[64,512]{1,0:T(8,128)(2,1)S(1)}, bf16[64,512]{1,0:T(8,128)(2,1)S(1)}, u32[]{:S(2)}, u32[]{:S(2)}) collective-permute-start(bf16[64,512]{1,0:T(8,128)(2,1)S(1)} %reshape.48.refs_0_), channel_id=1, source_target_pairs={{0,3},{1,0},{2,1},{3,2},{4,7},{5,4},{6,5},{7,6},{8,11},{9,8},{10,9... | collective-permute-start | bytes 196616 | tf_op jit(solution)/shard_map/ppermute | solution.py:265
  13.8 5.6 %collective-permute-start.4 = (bf16[64,512]{1,0:T(8,128)(2,1)S(1)}, bf16[64,512]{1,0:T(8,128)(2,1)S(1)}, u32[]{:S(2)}, u32[]{:S(2)}) collective-permute-start(bf16[64,512]{1,0:T(8,128)(2,1)S(1)} %reshape.48.refs_0_), channel_id=1, source_target_pairs={{0,2},{1,3},{2,0},{3,1},{4,6},{5,7},{6,4},{7,5},{8,10},{9,11},{10,... | collective-permute-start | bytes 196616 | tf_op jit(solution)/shard_map/ppermute | solution.py:265
  15.4 4.3 %collective-permute-start.3 = (bf16[64,512]{1,0:T(8,128)(2,1)S(1)}, bf16[64,512]{1,0:T(8,128)(2,1)S(1)}, u32[]{:S(2)}, u32[]{:S(2)}) collective-permute-start(bf16[64,512]{1,0:T(8,128)(2,1)S(1)} %reshape.48.refs_0_), channel_id=1, source_target_pairs={{0,1},{1,2},{2,3},{3,0},{4,5},{5,6},{6,7},{7,4},{8,9},{9,10},{10,1... | collective-permute-start | bytes 196616 | tf_op jit(solution)/shard_map/ppermute | solution.py:265
  15.7 3.9 %copy-start.2 = (bf16[64,512]{1,0:T(8,128)(2,1)}, bf16[64,512]{1,0:T(8,128)(2,1)S(1)}, u32[]{:S(2)}) copy-start(bf16[64,512]{1,0:T(8,128)(2,1)S(1)} %collective-permute-done.5.refs_3_) | copy-start | bytes 196612
  19.5 0.6 %copy-start.3 = (bf16[64,512]{1,0:T(8,128)(2,1)}, bf16[64,512]{1,0:T(8,128)(2,1)S(1)}, u32[]{:S(2)}) copy-start(bf16[64,512]{1,0:T(8,128)(2,1)S(1)} %collective-permute-done.4.refs_2_) | copy-start | bytes 196612
  19.7 0.6 %copy-start.4 = (bf16[64,512]{1,0:T(8,128)(2,1)}, bf16[64,512]{1,0:T(8,128)(2,1)S(1)}, u32[]{:S(2)}) copy-start(bf16[64,512]{1,0:T(8,128)(2,1)S(1)} %collective-permute-done.3.refs_1_) | copy-start | bytes 196612
  28.7 15.7 %copy-start = (f32[2,16,64,64]{3,2,1,0:T(8,128)S(1)}, f32[2,16,64,64]{3,2,1,0:T(8,128)}, u32[]{:S(2)}) copy-start(f32[2,16,64,64]{3,2,1,0:T(8,128)} %param.9) | copy-start | bytes 1572868
  28.7 4.0 %collective-permute-start.6 = (bf16[64,512]{1,0:T(8,128)(2,1)}, bf16[64,512]{1,0:T(8,128)(2,1)S(1)}, u32[]{:S(2)}, u32[]{:S(2)}) collective-permute-start(bf16[64,512]{1,0:T(8,128)(2,1)} %get-tuple-element.10), channel_id=1, source_target_pairs={{0,1},{1,2},{2,3},{3,0},{4,5},{5,6},{6,7},{7,4},{8,9},{9,10},{10,1... | collective-permute-start | bytes 196616 | tf_op jit(solution)/shard_map/ppermute | solution.py:274
  28.8 5.2 %collective-permute-start.7 = (bf16[64,512]{1,0:T(8,128)(2,1)}, bf16[64,512]{1,0:T(8,128)(2,1)S(1)}, u32[]{:S(2)}, u32[]{:S(2)}) collective-permute-start(bf16[64,512]{1,0:T(8,128)(2,1)} %get-tuple-element.11), channel_id=1, source_target_pairs={{0,2},{1,3},{2,0},{3,1},{4,6},{5,7},{6,4},{7,5},{8,10},{9,11},{10,... | collective-permute-start | bytes 196616 | tf_op jit(solution)/shard_map/ppermute | solution.py:274
  29.7 4.3 %collective-permute-start.8 = (bf16[64,512]{1,0:T(8,128)(2,1)}, bf16[64,512]{1,0:T(8,128)(2,1)S(1)}, u32[]{:S(2)}, u32[]{:S(2)}) collective-permute-start(bf16[64,512]{1,0:T(8,128)(2,1)} %get-tuple-element.12), channel_id=1, source_target_pairs={{0,3},{1,0},{2,1},{3,2},{4,7},{5,4},{6,5},{7,6},{8,11},{9,8},{10,9... | collective-permute-start | bytes 196616 | tf_op jit(solution)/shard_map/ppermute | solution.py:274
  35.4 4.9 %collective-permute-start.9 = (bf16[64,2,64]{2,0,1:T(8,128)(2,1)S(1)}, bf16[64,2,64]{2,0,1:T(8,128)(2,1)S(1)}, u32[]{:S(2)}, u32[]{:S(2)}) collective-permute-start(bf16[64,2,64]{2,0,1:T(8,128)(2,1)S(1)} %bitcast.104), channel_id=1, source_target_pairs={{0,12},{4,0},{8,4},{12,8},{1,13},{5,1},{9,5},{13,9},{2,14},{6,2},{... | collective-permute-start | bytes 49160 | tf_op jit(solution)/shard_map/ppermute | solution.py:85
  38.6 4.8 %collective-permute-start.10 = (bf16[64,2,64]{2,0,1:T(8,128)(2,1)S(1)}, bf16[64,2,64]{2,0,1:T(8,128)(2,1)S(1)}, u32[]{:S(2)}, u32[]{:S(2)}) collective-permute-start(bf16[64,2,64]{2,0,1:T(8,128)(2,1)S(1)} %bitcast.103), channel_id=1, source_target_pairs={{0,8},{4,12},{8,0},{12,4},{1,9},{5,13},{9,1},{13,5},{2,10},{6,14},... | collective-permute-start | bytes 49160 | tf_op jit(solution)/shard_map/ppermute | solution.py:85
  38.6 5.7 %collective-permute-start.11 = (bf16[64,2,64]{2,0,1:T(8,128)(2,1)S(1)}, bf16[64,2,64]{2,0,1:T(8,128)(2,1)S(1)}, u32[]{:S(2)}, u32[]{:S(2)}) collective-permute-start(bf16[64,2,64]{2,0,1:T(8,128)(2,1)S(1)} %bitcast.102), channel_id=1, source_target_pairs={{0,4},{4,8},{8,12},{12,0},{1,5},{5,9},{9,13},{13,1},{2,6},{6,10},{... | collective-permute-start | bytes 49160 | tf_op jit(solution)/shard_map/ppermute | solution.py:85

commit v29 on v27

--- a/solution.py
+++ b/solution.py
@@ -216,9 +216,9 @@
             pl.BlockSpec((step_coils, height, width), per_coil),
             pl.BlockSpec((step_coils, height, width), per_coil),
             pl.BlockSpec((coils, height), whole),
-            pl.BlockSpec((width, width), whole),
-            pl.BlockSpec((width, width), whole),
-            pl.BlockSpec((height, 2 * height), whole),
+            pl.BlockSpec((width, width), whole, pipeline_mode=pl.Buffered(1)),
+            pl.BlockSpec((width, width), whole, pipeline_mode=pl.Buffered(1)),
+            pl.BlockSpec((height, 2 * height), whole, pipeline_mode=pl.Buffered(1)),
         ],
         out_specs=(pl.BlockSpec((rows, width), whole),) * groups,
         scratch_shapes=[pltpu.VMEM((height, width), jnp.bfloat16), pltpu.VMEM((height, width), jnp.float32)],

time: 46.4 us -> 46.4 us (level)
  no operation moved by 1% of the time
where the time goes in v29:
time: 46.4 us; the launch traced here: 46.1 us
  starting transfers between devices  15 us (32%)
  waiting for transfers between devices  13.2 us (28%)
  Pallas kernels  8.42 us (18%)
  other arithmetic  6.36 us (14%)
  local copies, waits for them, and re-layouts  2.94 us (6%)
    ppermute x6, starting transfers between devices, exchange_blocks(): pieces.append(lax.ppermute(outgoing, axis, shifted(count, step)))  10.9 us
    pallas_call x1, Pallas kernels, coil_chain(): pl.pallas_call(coil_chain_kernel, out_shape=(jax.ShapeDtypeStruct((rows,...  8.42 us
    ppermute x6, waiting for transfers between devices, exchange_blocks(): pieces.append(lax.ppermute(outgoing, axis, shifted(count, step)))  6.2 us
    ppermute x3, waiting for transfers between devices, on_device(): lax.ppermute(own_rows, 'coil', shifted(groups, step))  4.09 us
    ppermute x3, waiting for transfers between devices, on_device(): lax.ppermute(outgoing[step - 1], 'coil', shifted(groups, step))  2.86 us
    ppermute x3, starting transfers between devices, on_device(): lax.ppermute(outgoing[step - 1], 'coil', shifted(groups, step))  2.38 us
    reduce_sum x1, other arithmetic, on_device(): jnp.sum(weights_in[:, :, :, None, None] * factors.reshape((parts * ranks,...  2.28 us
    ppermute x3, starting transfers between devices, on_device(): lax.ppermute(own_rows, 'coil', shifted(groups, step))  1.78 us
  transfers between devices with their start and end apart: 12, of which 9 were waited for; matrix products, arithmetic and copies ran while one was open for 3% of the time, Pallas kernels for 0%

profile of v29, /device:TPU:0, one launch (start us, length us, event | category | flops | bytes accessed | tf_op | source)
XLA Modules:
  0.0 46.1 jit_solution(2340712973902437785)
XLA Ops:
  0.0 0.7 %fusion.1 = f32[4,16]{1,0:T(4,128)S(1)} fusion(f32[2,4,16]{2,1,0:T(4,128)} %param.9), kind=kLoop, calls=%fused_computation.52 | loop fusion | flops 64 | bytes 512 | tf_op jit(solution)/shard_map/neg | solution.py:246
  0.7 0.7 %slice_bitcast_fusion.9 = (f32[4,16]{1,0:T(4,128)S(1)}, f32[4,16]{1,0:T(4,128)S(1)}) fusion(f32[2,4,16]{2,1,0:T(4,128)} %param.9), kind=kLoop, calls=%fused_computation.49 | loop fusion | bytes 1024 | tf_op jit(solution)/shard_map/squeeze | solution.py:246
  1.5 2.3 %multiply_reduce_fusion = bf16[2,4,64,64]{3,2,1,0:T(8,128)(2,1)S(1)} fusion(f32[32,64,64]{2,1,0:T(8,128)} %bitcast.103, f32[2,4,32]{2,1,0:T(4,128)S(1)} %pad_maximum_fusion), kind=kLoop, calls=%fused_computation | loop fusion | flops 2064384 | bytes 590848 | tf_op jit(solution)/shard_map/reduce_sum | solution.py:250
  3.8 3.1 %collective-permute-start.2 = (bf16[2,64,64]{2,1,0:T(8,128)(2,1)S(1)}, bf16[2,64,64]{2,1,0:T(8,128)(2,1)S(1)}, u32[]{:S(2)}, u32[]{:S(2)}) collective-permute-start(bf16[2,64,64]{2,1,0:T(8,128)(2,1)S(1)} %get-tuple-element.25), channel_id=1, source_target_pairs={{0,4},{4,8},{8,12},{12,0},{1,5},{5,9},{9,13},{13,1},{2,6},{6,10},{... | collective-permute-start | bytes 49160 | tf_op jit(solution)/shard_map/ppermute | solution.py:85
  6.9 2.6 %collective-permute-start.1 = (bf16[2,64,64]{2,1,0:T(8,128)(2,1)S(1)}, bf16[2,64,64]{2,1,0:T(8,128)(2,1)S(1)}, u32[]{:S(2)}, u32[]{:S(2)}) collective-permute-start(bf16[2,64,64]{2,1,0:T(8,128)(2,1)S(1)} %get-tuple-element.26), channel_id=1, source_target_pairs={{0,8},{4,12},{8,0},{12,4},{1,9},{5,13},{9,1},{13,5},{2,10},{6,14},... | collective-permute-start | bytes 49160 | tf_op jit(solution)/shard_map/ppermute | solution.py:85
  9.4 1.3 %collective-permute-start = (bf16[2,64,64]{2,1,0:T(8,128)(2,1)S(1)}, bf16[2,64,64]{2,1,0:T(8,128)(2,1)S(1)}, u32[]{:S(2)}, u32[]{:S(2)}) collective-permute-start(bf16[2,64,64]{2,1,0:T(8,128)(2,1)S(1)} %get-tuple-element.27), channel_id=1, source_target_pairs={{0,12},{4,0},{8,4},{12,8},{1,13},{5,1},{9,5},{13,9},{2,14},{6,2},{... | collective-permute-start | bytes 49160 | tf_op jit(solution)/shard_map/ppermute | solution.py:85
  10.8 0.7 %fusion = f32[16,4,1]{0,1,2:T(4,128)S(1)} fusion(f32[2,4,16]{2,1,0:T(4,128)} %param.9), kind=kLoop, calls=%fused_computation.48 | loop fusion | flops 64 | bytes 512 | tf_op jit(solution)/shard_map/stack | solution.py:277
  11.5 0.7 %slice_bitcast_fusion.11 = (f32[16,4,1]{0,1,2:T(4,128)S(1)}, f32[16,4,1]{0,1,2:T(4,128)S(1)}) fusion(f32[2,4,16]{2,1,0:T(4,128)} %param.9), kind=kLoop, calls=%fused_computation.51 | loop fusion | bytes 1024 | tf_op jit(solution)/shard_map/stack | solution.py:277
  12.2 1.2 %collective-permute-done = bf16[2,64,64]{2,1,0:T(8,128)(2,1)S(1)} collective-permute-done((bf16[2,64,64]{2,1,0:T(8,128)(2,1)S(1)}, bf16[2,64,64]{2,1,0:T(8,128)(2,1)S(1)}, u32[]{:S(2)}, u32[]{:S(2)}) %collective-permute-start) | collective-permute-done | bytes 16416 | tf_op jit(solution)/shard_map/ppermute | solution.py:85
  13.8 1.6 %collective-permute-start.4 = (bf16[64,512]{1,0:T(8,128)(2,1)S(1)}, bf16[64,512]{1,0:T(8,128)(2,1)S(1)}, u32[]{:S(2)}, u32[]{:S(2)}) collective-permute-start(bf16[64,512]{1,0:T(8,128)(2,1)S(1)} %reshape.32.refs_0_), channel_id=1, source_target_pairs={{0,2},{1,3},{2,0},{3,1},{4,6},{5,7},{6,4},{7,5},{8,10},{9,11},{10,... | collective-permute-start | bytes 196616 | tf_op jit(solution)/shard_map/ppermute | solution.py:261
  15.7 3.7 %collective-permute-done.4.refs_2_ = bf16[64,512]{1,0:T(8,128)(2,1)S(1)} collective-permute-done((bf16[64,512]{1,0:T(8,128)(2,1)S(1)}, bf16[64,512]{1,0:T(8,128)(2,1)S(1)}, u32[]{:S(2)}, u32[]{:S(2)}) %collective-permute-start.4) | collective-permute-done | bytes 65568 | tf_op jit(solution)/shard_map/ppermute | solution.py:261
  19.7 0.4 copy-done.3
  20.3 8.4 %shard_map.82 = (f32[64,512]{1,0:T(8,128)}, bf16[64,512]{1,0:T(8,128)(2,1)}, bf16[64,512]{1,0:T(8,128)(2,1)}, bf16[64,512]{1,0:T(8,128)(2,1)}) custom-call(bf16[64,512]{1,0:T(8,128)(2,1)} %copy-done.1, bf16[64,512]{1,0:T(8,128)(2,1)} %copy-done.4, bf16[64,512]{1,0:T(8,128)(2,1)} %copy-done.3, bf16[64,512]{1,0:T(8,128)(2,1)} %copy-done.2, s32[1]{0:T(128)} %bitcast.26.refs_4_, ...), custom_call_target="tpu_custom_call" | custom-call | flops 4294967296 | bytes 4718592 | tf_op jit(solution)/shard_map/pallas_call | solution.py:208
  28.8 0.9 %collective-permute-start.7 = (bf16[64,512]{1,0:T(8,128)(2,1)}, bf16[64,512]{1,0:T(8,128)(2,1)S(1)}, u32[]{:S(2)}, u32[]{:S(2)}) collective-permute-start(bf16[64,512]{1,0:T(8,128)(2,1)} %get-tuple-element.11), channel_id=1, source_target_pairs={{0,2},{1,3},{2,0},{3,1},{4,6},{5,7},{6,4},{7,5},{8,10},{9,11},{10,... | collective-permute-start | bytes 196616 | tf_op jit(solution)/shard_map/ppermute | solution.py:270
  29.7 1.4 %collective-permute-start.8 = (bf16[64,512]{1,0:T(8,128)(2,1)}, bf16[64,512]{1,0:T(8,128)(2,1)S(1)}, u32[]{:S(2)}, u32[]{:S(2)}) collective-permute-start(bf16[64,512]{1,0:T(8,128)(2,1)} %get-tuple-element.12), channel_id=1, source_target_pairs={{0,3},{1,0},{2,1},{3,2},{4,7},{5,4},{6,5},{7,6},{8,11},{9,8},{10,9... | collective-permute-start | bytes 196616 | tf_op jit(solution)/shard_map/ppermute | solution.py:270
  31.1 1.6 %collective-permute-done.6 = bf16[64,512]{1,0:T(8,128)(2,1)S(1)} collective-permute-done((bf16[64,512]{1,0:T(8,128)(2,1)}, bf16[64,512]{1,0:T(8,128)(2,1)S(1)}, u32[]{:S(2)}, u32[]{:S(2)}) %collective-permute-start.6) | collective-permute-done | bytes 65568 | tf_op jit(solution)/shard_map/ppermute | solution.py:270
  32.8 1.2 %collective-permute-done.7 = bf16[64,512]{1,0:T(8,128)(2,1)S(1)} collective-permute-done((bf16[64,512]{1,0:T(8,128)(2,1)}, bf16[64,512]{1,0:T(8,128)(2,1)S(1)}, u32[]{:S(2)}, u32[]{:S(2)}) %collective-permute-start.7) | collective-permute-done | bytes 65568 | tf_op jit(solution)/shard_map/ppermute | solution.py:270
  34.0 0.9 %add_convert_fusion = bf16[64,512]{1,0:T(8,128)(2,1)S(1)} fusion(bf16[64,512]{1,0:T(8,128)(2,1)S(1)} %collective-permute-done.8, bf16[64,512]{1,0:T(8,128)(2,1)S(1)} %collective-permute-done.7, f32[64,512]{1,0:T(8,128)} %get-tuple-element.9, bf16[64,512]{1,0:T(8,128)(2,1)S(1)} %collective-permute-done.6), kind=kLoop, calls=%fused_computation.3 | loop fusion | flops 229376 | bytes 393216 | tf_op jit(solution)/shard_map/convert_element_type | solution.py:273
  35.4 3.2 %collective-permute-start.9 = (bf16[64,2,64]{2,0,1:T(8,128)(2,1)S(1)}, bf16[64,2,64]{2,0,1:T(8,128)(2,1)S(1)}, u32[]{:S(2)}, u32[]{:S(2)}) collective-permute-start(bf16[64,2,64]{2,0,1:T(8,128)(2,1)S(1)} %bitcast.106), channel_id=1, source_target_pairs={{0,12},{4,0},{8,4},{12,8},{1,13},{5,1},{9,5},{13,9},{2,14},{6,2},{... | collective-permute-start | bytes 49160 | tf_op jit(solution)/shard_map/ppermute | solution.py:85
  38.6 0.6 %collective-permute-start.11 = (bf16[64,2,64]{2,0,1:T(8,128)(2,1)S(1)}, bf16[64,2,64]{2,0,1:T(8,128)(2,1)S(1)}, u32[]{:S(2)}, u32[]{:S(2)}) collective-permute-start(bf16[64,2,64]{2,0,1:T(8,128)(2,1)S(1)} %bitcast.104), channel_id=1, source_target_pairs={{0,4},{4,8},{8,12},{12,0},{1,5},{5,9},{9,13},{13,1},{2,6},{6,10},{... | collective-permute-start | bytes 49160 | tf_op jit(solution)/shard_map/ppermute | solution.py:85
  39.2 1.0 %collective-permute-done.9 = bf16[64,2,64]{2,0,1:T(8,128)(2,1)S(1)} collective-permute-done((bf16[64,2,64]{2,0,1:T(8,128)(2,1)S(1)}, bf16[64,2,64]{2,0,1:T(8,128)(2,1)S(1)}, u32[]{:S(2)}, u32[]{:S(2)}) %collective-permute-start.9) | collective-permute-done | bytes 16416 | tf_op jit(solution)/shard_map/ppermute | solution.py:85
  40.3 3.1 %collective-permute-done.10 = bf16[64,2,64]{2,0,1:T(8,128)(2,1)S(1)} collective-permute-done((bf16[64,2,64]{2,0,1:T(8,128)(2,1)S(1)}, bf16[64,2,64]{2,0,1:T(8,128)(2,1)S(1)}, u32[]{:S(2)}, u32[]{:S(2)}) %collective-permute-start.10) | collective-permute-done | bytes 16416 | tf_op jit(solution)/shard_map/ppermute | solution.py:85
  43.4 0.9 %collective-permute-done.11 = bf16[64,2,64]{2,0,1:T(8,128)(2,1)S(1)} collective-permute-done((bf16[64,2,64]{2,0,1:T(8,128)(2,1)S(1)}, bf16[64,2,64]{2,0,1:T(8,128)(2,1)S(1)}, u32[]{:S(2)}, u32[]{:S(2)}) %collective-permute-start.11) | collective-permute-done | bytes 16416 | tf_op jit(solution)/shard_map/ppermute | solution.py:85
  44.5 1.6 %add_add_fusion = f32[2,16,64,64]{3,2,1,0:T(8,128)} fusion(f32[2,16,64,64]{3,2,1,0:T(8,128)S(1)} %copy-done, f32[64,64]{1,0:T(8,128)S(1)} %get-tuple-element.14, f32[2,16]{1,0:T(2,128)S(1)} %bitcast.108, f32[64,64]{1,0:T(8,128)S(1)} %get-tuple-element.15, f32[2,16]{1,0:T(2,128)S(1)} %bitcast.109, f32[64,64]{1,0:T(8,128)S(1)} %get-tuple-element.16, ...), kind=kLoop, calls=%fused_computation.1 | loop fusion | flops 2097152 | bytes 1180672 | tf_op jit(solution)/shard_map/add | solution.py:285
  (50 shorter events, 1.9 us)
Async XLA Ops:
  3.8 9.6 %collective-permute-start.2 = (bf16[2,64,64]{2,1,0:T(8,128)(2,1)S(1)}, bf16[2,64,64]{2,1,0:T(8,128)(2,1)S(1)}, u32[]{:S(2)}, u32[]{:S(2)}) collective-permute-start(bf16[2,64,64]{2,1,0:T(8,128)(2,1)S(1)} %get-tuple-element.25), channel_id=1, source_target_pairs={{0,4},{4,8},{8,12},{12,0},{1,5},{5,9},{9,13},{13,1},{2,6},{6,10},{... | collective-permute-start | bytes 49160 | tf_op jit(solution)/shard_map/ppermute | solution.py:85
  6.9 6.5 %collective-permute-start.1 = (bf16[2,64,64]{2,1,0:T(8,128)(2,1)S(1)}, bf16[2,64,64]{2,1,0:T(8,128)(2,1)S(1)}, u32[]{:S(2)}, u32[]{:S(2)}) collective-permute-start(bf16[2,64,64]{2,1,0:T(8,128)(2,1)S(1)} %get-tuple-element.26), channel_id=1, source_target_pairs={{0,8},{4,12},{8,0},{12,4},{1,9},{5,13},{9,1},{13,5},{2,10},{6,14},... | collective-permute-start | bytes 49160 | tf_op jit(solution)/shard_map/ppermute | solution.py:85
  9.4 3.9 %collective-permute-start = (bf16[2,64,64]{2,1,0:T(8,128)(2,1)S(1)}, bf16[2,64,64]{2,1,0:T(8,128)(2,1)S(1)}, u32[]{:S(2)}, u32[]{:S(2)}) collective-permute-start(bf16[2,64,64]{2,1,0:T(8,128)(2,1)S(1)} %get-tuple-element.27), channel_id=1, source_target_pairs={{0,12},{4,0},{8,4},{12,8},{1,13},{5,1},{9,5},{13,9},{2,14},{6,2},{... | collective-permute-start | bytes 49160 | tf_op jit(solution)/shard_map/ppermute | solution.py:85
  13.8 5.9 %copy-start.1 = (bf16[64,512]{1,0:T(8,128)(2,1)}, bf16[64,512]{1,0:T(8,128)(2,1)S(1)}, u32[]{:S(2)}) copy-start(bf16[64,512]{1,0:T(8,128)(2,1)S(1)} %reshape.32.refs_0_) | copy-start | bytes 196612
  13.8 2.0 %collective-permute-start.5 = (bf16[64,512]{1,0:T(8,128)(2,1)S(1)}, bf16[64,512]{1,0:T(8,128)(2,1)S(1)}, u32[]{:S(2)}, u32[]{:S(2)}) collective-permute-start(bf16[64,512]{1,0:T(8,128)(2,1)S(1)} %reshape.32.refs_0_), channel_id=1, source_target_pairs={{0,3},{1,0},{2,1},{3,2},{4,7},{5,4},{6,5},{7,6},{8,11},{9,8},{10,9... | collective-permute-start | bytes 196616 | tf_op jit(solution)/shard_map/ppermute | solution.py:261
  13.8 5.6 %collective-permute-start.4 = (bf16[64,512]{1,0:T(8,128)(2,1)S(1)}, bf16[64,512]{1,0:T(8,128)(2,1)S(1)}, u32[]{:S(2)}, u32[]{:S(2)}) collective-permute-start(bf16[64,512]{1,0:T(8,128)(2,1)S(1)} %reshape.32.refs_0_), channel_id=1, source_target_pairs={{0,2},{1,3},{2,0},{3,1},{4,6},{5,7},{6,4},{7,5},{8,10},{9,11},{10,... | collective-permute-start | bytes 196616 | tf_op jit(solution)/shard_map/ppermute | solution.py:261
  15.4 4.3 %collective-permute-start.3 = (bf16[64,512]{1,0:T(8,128)(2,1)S(1)}, bf16[64,512]{1,0:T(8,128)(2,1)S(1)}, u32[]{:S(2)}, u32[]{:S(2)}) collective-permute-start(bf16[64,512]{1,0:T(8,128)(2,1)S(1)} %reshape.32.refs_0_), channel_id=1, source_target_pairs={{0,1},{1,2},{2,3},{3,0},{4,5},{5,6},{6,7},{7,4},{8,9},{9,10},{10,1... | collective-permute-start | bytes 196616 | tf_op jit(solution)/shard_map/ppermute | solution.py:261
  15.7 3.9 %copy-start.2 = (bf16[64,512]{1,0:T(8,128)(2,1)}, bf16[64,512]{1,0:T(8,128)(2,1)S(1)}, u32[]{:S(2)}) copy-start(bf16[64,512]{1,0:T(8,128)(2,1)S(1)} %collective-permute-done.5.refs_3_) | copy-start | bytes 196612
  19.5 0.6 %copy-start.3 = (bf16[64,512]{1,0:T(8,128)(2,1)}, bf16[64,512]{1,0:T(8,128)(2,1)S(1)}, u32[]{:S(2)}) copy-start(bf16[64,512]{1,0:T(8,128)(2,1)S(1)} %collective-permute-done.4.refs_2_) | copy-start | bytes 196612
  19.7 0.6 %copy-start.4 = (bf16[64,512]{1,0:T(8,128)(2,1)}, bf16[64,512]{1,0:T(8,128)(2,1)S(1)}, u32[]{:S(2)}) copy-start(bf16[64,512]{1,0:T(8,128)(2,1)S(1)} %collective-permute-done.3.refs_1_) | copy-start | bytes 196612
  28.7 15.7 %copy-start = (f32[2,16,64,64]{3,2,1,0:T(8,128)S(1)}, f32[2,16,64,64]{3,2,1,0:T(8,128)}, u32[]{:S(2)}) copy-start(f32[2,16,64,64]{3,2,1,0:T(8,128)} %param.8) | copy-start | bytes 1572868
  28.7 4.0 %collective-permute-start.6 = (bf16[64,512]{1,0:T(8,128)(2,1)}, bf16[64,512]{1,0:T(8,128)(2,1)S(1)}, u32[]{:S(2)}, u32[]{:S(2)}) collective-permute-start(bf16[64,512]{1,0:T(8,128)(2,1)} %get-tuple-element.10), channel_id=1, source_target_pairs={{0,1},{1,2},{2,3},{3,0},{4,5},{5,6},{6,7},{7,4},{8,9},{9,10},{10,1... | collective-permute-start | bytes 196616 | tf_op jit(solution)/shard_map/ppermute | solution.py:270
  28.8 5.2 %collective-permute-start.7 = (bf16[64,512]{1,0:T(8,128)(2,1)}, bf16[64,512]{1,0:T(8,128)(2,1)S(1)}, u32[]{:S(2)}, u32[]{:S(2)}) collective-permute-start(bf16[64,512]{1,0:T(8,128)(2,1)} %get-tuple-element.11), channel_id=1, source_target_pairs={{0,2},{1,3},{2,0},{3,1},{4,6},{5,7},{6,4},{7,5},{8,10},{9,11},{10,... | collective-permute-start | bytes 196616 | tf_op jit(solution)/shard_map/ppermute | solution.py:270
  29.7 4.3 %collective-permute-start.8 = (bf16[64,512]{1,0:T(8,128)(2,1)}, bf16[64,512]{1,0:T(8,128)(2,1)S(1)}, u32[]{:S(2)}, u32[]{:S(2)}) collective-permute-start(bf16[64,512]{1,0:T(8,128)(2,1)} %get-tuple-element.12), channel_id=1, source_target_pairs={{0,3},{1,0},{2,1},{3,2},{4,7},{5,4},{6,5},{7,6},{8,11},{9,8},{10,9... | collective-permute-start | bytes 196616 | tf_op jit(solution)/shard_map/ppermute | solution.py:270
  35.4 4.9 %collective-permute-start.9 = (bf16[64,2,64]{2,0,1:T(8,128)(2,1)S(1)}, bf16[64,2,64]{2,0,1:T(8,128)(2,1)S(1)}, u32[]{:S(2)}, u32[]{:S(2)}) collective-permute-start(bf16[64,2,64]{2,0,1:T(8,128)(2,1)S(1)} %bitcast.106), channel_id=1, source_target_pairs={{0,12},{4,0},{8,4},{12,8},{1,13},{5,1},{9,5},{13,9},{2,14},{6,2},{... | collective-permute-start | bytes 49160 | tf_op jit(solution)/shard_map/ppermute | solution.py:85
  38.6 4.8 %collective-permute-start.10 = (bf16[64,2,64]{2,0,1:T(8,128)(2,1)S(1)}, bf16[64,2,64]{2,0,1:T(8,128)(2,1)S(1)}, u32[]{:S(2)}, u32[]{:S(2)}) collective-permute-start(bf16[64,2,64]{2,0,1:T(8,128)(2,1)S(1)} %bitcast.105), channel_id=1, source_target_pairs={{0,8},{4,12},{8,0},{12,4},{1,9},{5,13},{9,1},{13,5},{2,10},{6,14},... | collective-permute-start | bytes 49160 | tf_op jit(solution)/shard_map/ppermute | solution.py:85
  38.6 5.7 %collective-permute-start.11 = (bf16[64,2,64]{2,0,1:T(8,128)(2,1)S(1)}, bf16[64,2,64]{2,0,1:T(8,128)(2,1)S(1)}, u32[]{:S(2)}, u32[]{:S(2)}) collective-permute-start(bf16[64,2,64]{2,0,1:T(8,128)(2,1)S(1)} %bitcast.104), channel_id=1, source_target_pairs={{0,4},{4,8},{8,12},{12,0},{1,5},{5,9},{9,13},{13,1},{2,6},{6,10},{... | collective-permute-start | bytes 49160 | tf_op jit(solution)/shard_map/ppermute | solution.py:85
